TPU v7x, 32 devices: a whole 2x2x4 slice. The times are simulated.
32 devices in a mesh: wide: 8 (over z, y), narrow: 4 (over x, core).
Axes of the slice: x: 2, y: 2, z: 4, core: 2. Of those that a mesh axis runs over, the one named last changes fastest.
Arguments:
- embeddings: bfloat16 [32768, 768], P(('wide', 'narrow')), may hold values from -6 to 6
- start: bfloat16 [32768, 64], P(('wide', 'narrow')), may hold values from -6 to 6
- neighbours: int32 [32, 3], replicated, may hold values from -1 to 31, as said below
Outputs:
- basis: float32 [32768, 64], P(('wide', 'narrow'))
- degrees: float32 [32768], P(('wide', 'narrow'))
Inputs may be any that keep to these rules, and one draw needn't show every extreme that they name: `neighbours`: row b lists distinct blocks c, then -1 in its unused slots; every listed c has c % 4 == b % 4 and (c // 4 - b // 4) mod 8 between 1 and 3, so no unordered pair is listed twice. Some row is full and some row is empty.
All inputs are finite; a program needn't handle non-finite values.
Results may differ from a plain program's by a relative error of at most 0.0034.
Values may be sent and summed in bfloat16 or wider, within the bound.
No kernel may reach another device: no remote copies, remote signals or barrier semaphores. Data moves between devices by JAX's collectives and lax.ppermute only.
A program may use at most 128 MiB of HBM per device.

v0:
```python
from functools import partial
import math

import jax
import jax.numpy as jnp
from jax import lax
from jax.sharding import PartitionSpec as P

ITERS = 2


kernel_width_factor = 0.05


def shifted(block, axis, distance):
    devices = range(lax.axis_size(axis))
    route = [((i - distance) % len(devices), i) for i in devices]
    return lax.ppermute(block, axis, route)


def normalize_rows(values):
    values_wide = values.astype(jnp.float32)
    scaling = lax.rsqrt(jnp.mean(values_wide * values_wide, axis=-1, keepdims=True) + 1e-06)
    return (values_wide * scaling / math.sqrt(values_wide.shape[-1])).astype(jnp.bfloat16)


def scores_tile(leftside_block, right_block):
    kernel_entries = lax.dot_general(
        leftside_block, right_block, (((1,), (1,)), ((), ())), preferred_element_type=jnp.float32
    )
    return jnp.exp(kernel_entries / kernel_width_factor).astype(jnp.bfloat16)


def apply_tile(affinity, near_weights, far_weights):
    row_part = jnp.dot(affinity, far_weights, preferred_element_type=jnp.float32)
    col_part = lax.dot_general(
        affinity, near_weights, (((0,), (0,)), ((), ())), preferred_element_type=jnp.float32
    )
    row_sum = jnp.sum(affinity, axis=1, dtype=jnp.float32)
    col_sum = jnp.sum(affinity, axis=0, dtype=jnp.float32)
    return (row_part, row_sum, col_part, col_sum)


def pass_terms(owned, build_submatrix, near_weights, far_weights):
    block_rows = near_weights.shape[0]
    vector_count = near_weights.shape[1]

    def compute_pair():
        affinity = build_submatrix()
        row_part, row_sum, col_part, col_sum = apply_tile(affinity, near_weights, far_weights)
        return (row_part, row_sum, col_part, col_sum, affinity)

    def skip_pair():
        zero_part = jnp.zeros((block_rows, vector_count), jnp.float32)
        zero_sum = jnp.zeros((block_rows,), jnp.float32)
        return (
            zero_part,
            zero_sum,
            zero_part,
            zero_sum,
            jnp.zeros((block_rows, block_rows), jnp.bfloat16),
        )

    return lax.cond(owned, compute_pair, skip_pair)


def fetch_pair(unit_block, weights, offset):
    return shifted((unit_block, weights), "wide", -offset)


def later_tile(offset_slot, unit_block, weights):
    offset = offset_slot + 1
    far_unit, far_weights = fetch_pair(unit_block, weights, offset)
    return (partial(scores_tile, unit_block, far_unit), far_weights)


def orthonormal(product, vertex_valence, device_count):
    column_sums, total_degree_sum = lax.psum(
        (jnp.sum(product, axis=0), jnp.sum(vertex_valence)), ("wide", "narrow")
    )
    displaced_entries = product / vertex_valence[:, None] - column_sums / total_degree_sum
    local_gram = jnp.dot(
        displaced_entries.T,
        displaced_entries,
        precision=lax.Precision.HIGHEST,
        preferred_element_type=jnp.float32,
    )
    gram_matrix = lax.psum(local_gram, ("wide", "narrow")) / (
        displaced_entries.shape[0] * device_count
    )
    normalizer_coefficient = jnp.linalg.cholesky(gram_matrix)
    return jax.scipy.linalg.solve_triangular(
        normalizer_coefficient, displaced_entries.T, lower=True
    ).T


def on_device(embeddings, start, neighbours):
    wide_count = lax.axis_size("wide")
    lane_count = lax.axis_size("narrow")
    broad_index = lax.axis_index("wide")
    vector_slot_number = lax.axis_index("narrow")
    my_block = broad_index * lane_count + vector_slot_number
    far_reach = wide_count // 2 - 1
    unit_block = normalize_rows(embeddings)
    block_rows = unit_block.shape[0]
    own_row = lax.dynamic_slice_in_dim(neighbours, my_block, 1, 0)[0]
    owned_list = []
    for offset_slot in range(far_reach):
        target = (broad_index + offset_slot + 1) % wide_count * lane_count + vector_slot_number
        owned_list.append(jnp.any(own_row == target))
    self_mask = lax.broadcasted_iota(
        jnp.int32, (block_rows, block_rows), 0
    ) == lax.broadcasted_iota(jnp.int32, (block_rows, block_rows), 1)
    near_tile = jnp.where(
        self_mask, jnp.zeros((), jnp.bfloat16), scores_tile(unit_block, unit_block)
    )
    near_sum = jnp.sum(near_tile, axis=1, dtype=jnp.float32)
    weights = start
    kept_units = []
    kept_tiles = []
    basis = None
    vertex_valence = None
    for iteration in range(ITERS):
        if iteration > 0:
            weights = basis.astype(jnp.bfloat16)
        product = jnp.dot(near_tile, weights, preferred_element_type=jnp.float32)
        vertex_valence = near_sum
        for offset_slot in range(far_reach):
            offset = offset_slot + 1
            if iteration == 0:
                far_unit, far_weights = fetch_pair(unit_block, weights, offset)
                build_submatrix = partial(scores_tile, unit_block, far_unit)
            else:
                build_submatrix, far_weights = later_tile(offset_slot, unit_block, weights)
            row_part, row_sum, col_part, col_sum, affinity = pass_terms(
                owned_list[offset_slot], build_submatrix, weights, far_weights
            )
            if iteration == 0:
                kept_units.append(far_unit)
                kept_tiles.append(affinity)
            returned, returned_sum = shifted((col_part, col_sum), "wide", offset)
            product = product + row_part + returned
            vertex_valence = vertex_valence + row_sum + returned_sum
        basis = orthonormal(product, vertex_valence, wide_count * lane_count)
    return (basis, vertex_valence / block_rows)


def solution(mesh):
    in_specs = (P(("wide", "narrow"), None), P(("wide", "narrow"), None), P())
    out_specs = (P(("wide", "narrow"), None), P(("wide", "narrow")))
    return jax.shard_map(
        on_device, mesh=mesh, in_specs=in_specs, out_specs=out_specs, check_vma=False
    )
```

profile of v0, /device:TPU:0, one launch (start us, length us, event | category | flops | bytes accessed | tf_op | source)
XLA Modules:
  0.0 454.2 jit_solution(4976166355017392789)
XLA Ops:
  0.6 1.9 fusion.1
  2.6 1.6 fusion.3
  4.2 5.0 %collective-permute-start.6 = (bf16[1024,768]{1,0:T(8,128)(2,1)}, bf16[1024,768]{1,0:T(8,128)(2,1)}, u32[]{:S(2)}, u32[]{:S(2)}) collective-permute-start(bf16[1024,768]{1,0:T(8,128)(2,1)} %fusion.3), channel_id=1, source_target_pairs={{12,0},{16,4},{20,8},{24,12},{28,16},{0,20},{4,24},{8,28},{13,1},{... | collective-permute-start | bytes 4718600 | tf_op jit(solution)/shard_map/ppermute | solution.py:18
  9.2 1.3 collective-permute-start.3
  11.0 0.8 copy.5
  11.9 2.6 collective-permute-start.7
  14.5 1.3 collective-permute-start.4
  15.9 0.7 compare_reduce_fusion.4
  17.3 100.1 %collective-permute-done.7 = bf16[1024,64]{1,0:T(8,128)(2,1)S(1)} collective-permute-done((bf16[1024,64]{1,0:T(8,128)(2,1)}, bf16[1024,64]{1,0:T(8,128)(2,1)S(1)}, u32[]{:S(2)}, u32[]{:S(2)}) %collective-permute-start.7) | collective-permute-done | bytes 131104 | tf_op jit(solution)/shard_map/ppermute | solution.py:18
  117.4 48.8 %collective-permute-start.1 = (bf16[1024,64]{1,0:T(8,128)(2,1)}, bf16[1024,64]{1,0:T(8,128)(2,1)S(1)}, u32[]{:S(2)}, u32[]{:S(2)}) collective-permute-start(bf16[1024,64]{1,0:T(8,128)(2,1)} %copy.5), channel_id=1, source_target_pairs={{4,0},{8,4},{12,8},{16,12},{20,16},{24,20},{28,24},{0,28},{5,1},{9... | collective-permute-start | bytes 393224 | tf_op jit(solution)/shard_map/ppermute | solution.py:18
  166.2 6.5 %conditional.8 = (f32[1024,64]{0,1:T(8,128)S(1)}, f32[1024]{0:T(1024)S(1)}, f32[1024,64]{0,1:T(8,128)}, f32[1024]{0:T(1024)}) conditional(s32[]{:T(128)} %convert_element_type.77, () %tuple.62, (bf16[1024,768]{1,0:T(8,128)(2,1)}, bf16[1024,768]{1,0:T(8,128)(2,1)}, bf16[1024,64]{1,0:T(8,128)(2,1)S(1)}, bf16[1024,64]{0,1:T(8,128)(2,1)S(1)}) %tuple.108), branch_computations={%region_12.13_spmd, %region_13.16_spmd} | conditional | flops 1884289024 | bytes 10231840 | solution.py:64
  166.2 4.5 %convert_reduce_fusion.4 = (f32[1024]{0:T(1024)}, f32[1024]{0:T(1024)S(1)}, bf16[1024,1024]{1,0:T(8,128)(2,1)S(1)}) fusion(bf16[1024,768]{1,0:T(8,128)(2,1)} %get-tuple-element.58, bf16[1024,768]{1,0:T(8,128)(2,1)} %get-tuple-element.59), kind=kOutput, calls=%fused_computation.6 | convolution fusion | flops 1615853568 | bytes 5251072 | tf_op jit(solution)/shard_map/cond/branch_1_fun/dot_general | solution.py:28
  170.7 0.8 fusion.23
  171.5 1.2 fusion.24
  172.7 3.8 convert_reduce_fusion.12
  177.8 6.5 %conditional.7 = (f32[1024,64]{0,1:T(8,128)S(1)}, f32[1024]{0:T(1024)S(1)}, f32[1024,64]{0,1:T(8,128)}, f32[1024]{0:T(1024)}) conditional(s32[]{:T(128)} %convert_element_type.76, () %tuple.60, (bf16[1024,768]{1,0:T(8,128)(2,1)}, bf16[1024,768]{1,0:T(8,128)(2,1)}, bf16[1024,64]{1,0:T(8,128)(2,1)S(1)}, bf16[1024,64]{0,1:T(8,128)(2,1)S(1)}) %tuple.109), branch_computations={%region_7.8_spmd, %region_8.0_spmd} | conditional | flops 1884289024 | bytes 10231840 | solution.py:64
  177.8 4.5 %convert_reduce_fusion.2 = (f32[1024]{0:T(1024)}, f32[1024]{0:T(1024)S(1)}, bf16[1024,1024]{1,0:T(8,128)(2,1)S(1)}) fusion(bf16[1024,768]{1,0:T(8,128)(2,1)} %get-tuple-element.54, bf16[1024,768]{1,0:T(8,128)(2,1)} %get-tuple-element.55), kind=kOutput, calls=%fused_computation.3 | convolution fusion | flops 1615853568 | bytes 5251072 | tf_op jit(solution)/shard_map/cond/branch_1_fun/dot_general | solution.py:28
  182.4 0.8 fusion.21
  183.1 1.2 fusion.22
  184.3 4.3 collective-permute-start.10
  188.7 5.2 %conditional.6 = (f32[1024,64]{0,1:T(8,128)S(1)}, f32[1024]{0:T(1024)S(1)}, f32[1024,64]{0,1:T(8,128)S(1)}, f32[1024]{0:T(1024)S(1)}) conditional(s32[]{:T(128)} %convert_element_type.75, () %tuple.58, (bf16[1024,768]{1,0:T(8,128)(2,1)}, bf16[1024,768]{1,0:T(8,128)(2,1)}, bf16[1024,64]{1,0:T(8,128)(2,1)S(1)}, bf16[1024,64]{0,1:T(8,128)(2,1)S(1)}) %tuple.110), branch_computations={%region_2.3_spmd, %region_3.0_spmd} | conditional | flops 1884289024 | bytes 10231840 | solution.py:64
  188.7 4.0 convert_reduce_fusion
  192.7 0.8 fusion.19
  194.6 0.9 collective-permute-start.2
  196.0 4.3 collective-permute-done.9
  200.3 1.3 fusion.17
  201.6 2.0 collective-permute-done.2
  203.6 1.2 fusion.18
  204.8 37.3 %all-reduce.1 = (f32[64]{0:T(128)S(1)}, f32[]{:T(128)}) all-reduce(f32[64]{0:T(128)S(1)} %get-tuple-element.173, f32[]{:T(128)} %get-tuple-element.171), channel_id=1, replica_groups=mesh['wide'=8,'narrow'=4] {'wide','narrow'}, use_global_device_ids=true, to_apply=%region_18.19 | all-reduce | flops 65 | bytes 520 | tf_op jit(solution)/shard_map/psum | solution.py:78
  242.1 0.6 broadcast_divide_fusion.1
  243.2 41.2 %psum.44 = f32[64,64]{0,1:T(8,128)S(1)} all-reduce(f32[64,64]{0,1:T(8,128)S(1)} %fusion.15), channel_id=1, replica_groups=mesh['wide'=8,'narrow'=4] {'wide','narrow'}, use_global_device_ids=true, to_apply=%region_21.22 | all-reduce | flops 4096 | bytes 32768 | tf_op jit(solution)/shard_map/psum | solution.py:88
  284.6 5.8 %cholesky.44 = f32[64,64]{1,0:T(8,128)S(1)} custom-call(f32[64,64]{1,0:T(8,128)S(1)} %fusion.11), custom_call_target="Cholesky" | custom-call | tf_op jit(solution)/shard_map/jit(cholesky)/cholesky | solution.py:91
  290.4 0.6 compare_reduce_fusion.1
  291.1 0.7 fusion.6
  291.8 4.9 %custom-call.6 = f32[1,64,64]{1,2,0:T(8,128)S(1)} custom-call(f32[1,64,64]{2,1,0:T(8,128)S(1)} %fusion.6), custom_call_target="InvertDiagBlocksLowerTriangular" | custom-call | tf_op jit(solution)/shard_map/jit(_solve_triangular)/triangular_solve | solution.py:92
  297.1 3.3 collective-permute-start.16
  300.4 1.5 collective-permute-start.14
  302.0 2.4 collective-permute-done.16
  304.4 5.9 %conditional.11 = (f32[1024,64]{0,1:T(8,128)S(1)}, f32[1024]{0:T(1024)S(1)}, f32[1024,64]{0,1:T(8,128)}, f32[1024]{0:T(1024)S(1)}) conditional(s32[]{:T(128)} %convert_element_type.77, () %tuple.68, (bf16[1024,768]{1,0:T(8,128)(2,1)}, bf16[1024,768]{1,0:T(8,128)(2,1)}, bf16[1024,64]{0,1:T(8,128)(2,1)S(1)}, bf16[1024,64]{0,1:T(8,128)(2,1)S(1)}) %tuple.111), branch_computations={%region_32.35_spmd, %region_33.0_spmd} | conditional | flops 1884289024 | bytes 10231840 | solution.py:64
  304.4 3.9 convert_reduce_fusion.10
  308.3 1.2 fusion.30
  309.5 0.8 fusion.29
  310.3 6.5 %conditional.10 = (f32[1024,64]{0,1:T(8,128)S(1)}, f32[1024]{0:T(1024)S(1)}, f32[1024,64]{0,1:T(8,128)}, f32[1024]{0:T(1024)}) conditional(s32[]{:T(128)} %convert_element_type.76, () %tuple.66, (bf16[1024,768]{1,0:T(8,128)(2,1)}, bf16[1024,768]{1,0:T(8,128)(2,1)}, bf16[1024,64]{0,1:T(8,128)(2,1)S(1)}, bf16[1024,64]{0,1:T(8,128)(2,1)S(1)}) %tuple.112), branch_computations={%region_28.31_spmd, %region_29.0_spmd} | conditional | flops 1884289024 | bytes 10231840 | solution.py:64
  310.4 4.5 %convert_reduce_fusion.8 = (f32[1024]{0:T(1024)}, f32[1024]{0:T(1024)S(1)}, bf16[1024,1024]{1,0:T(8,128)(2,1)S(1)}) fusion(bf16[1024,768]{1,0:T(8,128)(2,1)} %get-tuple-element.66, bf16[1024,768]{1,0:T(8,128)(2,1)} %get-tuple-element.67), kind=kOutput, calls=%fused_computation.12 | convolution fusion | flops 1615853568 | bytes 5251072 | tf_op jit(solution)/shard_map/cond/branch_1_fun/dot_general | solution.py:28
  314.9 1.2 fusion.28
  316.1 0.8 fusion.27
  316.9 7.0 %collective-permute-start.19 = (f32[1024]{0:T(1024)}, f32[1024]{0:T(1024)}, u32[]{:S(2)}, u32[]{:S(2)}) collective-permute-start(f32[1024]{0:T(1024)} %get-tuple-element.121), channel_id=1, source_target_pairs={{24,0},{28,4},{0,8},{4,12},{8,16},{12,20},{16,24},{20,28},{25,1},{... | collective-permute-start | bytes 12296 | tf_op jit(solution)/shard_map/ppermute | solution.py:18
  323.9 6.5 %conditional.9 = (f32[1024,64]{0,1:T(8,128)S(1)}, f32[1024]{0:T(1024)S(1)}, f32[1024,64]{0,1:T(8,128)}, f32[1024]{0:T(1024)}) conditional(s32[]{:T(128)} %convert_element_type.75, () %tuple.64, (bf16[1024,768]{1,0:T(8,128)(2,1)}, bf16[1024,768]{1,0:T(8,128)(2,1)}, bf16[1024,64]{0,1:T(8,128)(2,1)S(1)}, bf16[1024,64]{0,1:T(8,128)(2,1)S(1)}) %tuple.113), branch_computations={%region_24.27_spmd, %region_25.0_spmd} | conditional | flops 1884289024 | bytes 10231840 | solution.py:64
  323.9 4.5 %convert_reduce_fusion.6 = (f32[1024]{0:T(1024)}, f32[1024]{0:T(1024)S(1)}, bf16[1024,1024]{1,0:T(8,128)(2,1)S(1)}) fusion(bf16[1024,768]{1,0:T(8,128)(2,1)} %get-tuple-element.62, bf16[1024,768]{1,0:T(8,128)(2,1)} %get-tuple-element.63), kind=kOutput, calls=%fused_computation.9 | convolution fusion | flops 1615853568 | bytes 5251072 | tf_op jit(solution)/shard_map/cond/branch_1_fun/dot_general | solution.py:28
  328.4 1.2 fusion.26
  329.6 0.8 fusion.25
  330.4 1.5 collective-permute-start.13
  333.0 4.1 collective-permute-done.18
  337.1 1.3 broadcast_multiply_fusion.2
  339.0 3.7 collective-permute-done.13
  342.8 14.9 %collective-permute-done.17 = f32[1024,64]{0,1:T(8,128)} collective-permute-done((f32[1024,64]{0,1:T(8,128)}, f32[1024,64]{0,1:T(8,128)}, u32[]{:S(2)}, u32[]{:S(2)}) %collective-permute-start.17) | collective-permute-done | bytes 262176 | tf_op jit(solution)/shard_map/ppermute | solution.py:18
  357.7 1.2 fusion.16
  358.9 38.5 %all-reduce = (f32[64]{0:T(128)S(1)}, f32[]{:T(128)}) all-reduce(f32[64]{0:T(128)S(1)} %get-tuple-element.169, f32[]{:T(128)} %reduce_sum.167), channel_id=1, replica_groups=mesh['wide'=8,'narrow'=4] {'wide','narrow'}, use_global_device_ids=true, to_apply=%region_37.40 | all-reduce | flops 65 | bytes 520 | tf_op jit(solution)/shard_map/psum | solution.py:78
  397.4 0.6 broadcast_divide_fusion
  398.5 42.3 %psum.47 = f32[64,64]{0,1:T(8,128)S(1)} all-reduce(f32[64,64]{0,1:T(8,128)S(1)} %fusion.14), channel_id=1, replica_groups=mesh['wide'=8,'narrow'=4] {'wide','narrow'}, use_global_device_ids=true, to_apply=%region_40.43 | all-reduce | flops 4096 | bytes 32768 | tf_op jit(solution)/shard_map/psum | solution.py:88
  441.0 5.8 %cholesky.55 = f32[64,64]{1,0:T(8,128)S(1)} custom-call(f32[64,64]{1,0:T(8,128)S(1)} %fusion.9), custom_call_target="Cholesky" | custom-call | tf_op jit(solution)/shard_map/jit(cholesky)/cholesky | solution.py:91
  447.5 0.7 fusion.7
  448.2 4.9 %custom-call.7 = f32[1,64,64]{1,2,0:T(8,128)S(1)} custom-call(f32[1,64,64]{2,1,0:T(8,128)S(1)} %fusion.7), custom_call_target="InvertDiagBlocksLowerTriangular" | custom-call | tf_op jit(solution)/shard_map/jit(_solve_triangular)/triangular_solve | solution.py:92
  453.1 1.2 convolution_bitcast_fusion
  (51 shorter events, 6.2 us)
Async XLA Ops:
  0.6 2.0 copy-start
  0.6 10.4 %copy-start.1 = (bf16[1024,64]{0,1:T(8,128)(2,1)S(1)}, bf16[1024,64]{0,1:T(8,128)(2,1)}, u32[]{:S(2)}) copy-start(bf16[1024,64]{0,1:T(8,128)(2,1)} %param.19) | copy-start | bytes 393220
  2.6 13.3 %copy-start.4 = (s32[32,3]{0,1:T(4,128)S(1)}, s32[32,3]{0,1:T(4,128)}, u32[]{:S(2)}) copy-start(s32[32,3]{0,1:T(4,128)} %param.20) | copy-start | bytes 1156
  4.2 162.0 %collective-permute-start.6 = (bf16[1024,768]{1,0:T(8,128)(2,1)}, bf16[1024,768]{1,0:T(8,128)(2,1)}, u32[]{:S(2)}, u32[]{:S(2)}) collective-permute-start(bf16[1024,768]{1,0:T(8,128)(2,1)} %fusion.3), channel_id=1, source_target_pairs={{12,0},{16,4},{20,8},{24,12},{28,16},{0,20},{4,24},{8,28},{13,1},{... | collective-permute-start | bytes 4718600 | tf_op jit(solution)/shard_map/ppermute | solution.py:18
  9.2 168.6 %collective-permute-start.3 = (bf16[1024,768]{1,0:T(8,128)(2,1)}, bf16[1024,768]{1,0:T(8,128)(2,1)}, u32[]{:S(2)}, u32[]{:S(2)}) collective-permute-start(bf16[1024,768]{1,0:T(8,128)(2,1)} %fusion.3), channel_id=1, source_target_pairs={{8,0},{12,4},{16,8},{20,12},{24,16},{28,20},{0,24},{4,28},{9,1},{1... | collective-permute-start | bytes 4718600 | tf_op jit(solution)/shard_map/ppermute | solution.py:18
  10.5 178.2 %collective-permute-start = (bf16[1024,768]{1,0:T(8,128)(2,1)}, bf16[1024,768]{1,0:T(8,128)(2,1)}, u32[]{:S(2)}, u32[]{:S(2)}) collective-permute-start(bf16[1024,768]{1,0:T(8,128)(2,1)} %fusion.3), channel_id=1, source_target_pairs={{4,0},{8,4},{12,8},{16,12},{20,16},{24,20},{28,24},{0,28},{5,1},{9... | collective-permute-start | bytes 4718600 | tf_op jit(solution)/shard_map/ppermute | solution.py:18
  11.9 105.5 %collective-permute-start.7 = (bf16[1024,64]{1,0:T(8,128)(2,1)}, bf16[1024,64]{1,0:T(8,128)(2,1)S(1)}, u32[]{:S(2)}, u32[]{:S(2)}) collective-permute-start(bf16[1024,64]{1,0:T(8,128)(2,1)} %copy.5), channel_id=1, source_target_pairs={{12,0},{16,4},{20,8},{24,12},{28,16},{0,20},{4,24},{8,28},{13,1},{... | collective-permute-start | bytes 393224 | tf_op jit(solution)/shard_map/ppermute | solution.py:18
  14.5 163.2 %collective-permute-start.4 = (bf16[1024,64]{1,0:T(8,128)(2,1)}, bf16[1024,64]{1,0:T(8,128)(2,1)S(1)}, u32[]{:S(2)}, u32[]{:S(2)}) collective-permute-start(bf16[1024,64]{1,0:T(8,128)(2,1)} %copy.5), channel_id=1, source_target_pairs={{8,0},{12,4},{16,8},{20,12},{24,16},{28,20},{0,24},{4,28},{9,1},{1... | collective-permute-start | bytes 393224 | tf_op jit(solution)/shard_map/ppermute | solution.py:18
  117.4 71.3 %collective-permute-start.1 = (bf16[1024,64]{1,0:T(8,128)(2,1)}, bf16[1024,64]{1,0:T(8,128)(2,1)S(1)}, u32[]{:S(2)}, u32[]{:S(2)}) collective-permute-start(bf16[1024,64]{1,0:T(8,128)(2,1)} %copy.5), channel_id=1, source_target_pairs={{4,0},{8,4},{12,8},{16,12},{20,16},{24,20},{28,24},{0,28},{5,1},{9... | collective-permute-start | bytes 393224 | tf_op jit(solution)/shard_map/ppermute | solution.py:18
  172.7 21.9 %collective-permute-start.11 = (f32[1024]{0:T(1024)}, f32[1024]{0:T(1024)}, u32[]{:S(2)}, u32[]{:S(2)}) collective-permute-start(f32[1024]{0:T(1024)} %get-tuple-element.111), channel_id=1, source_target_pairs={{20,0},{24,4},{28,8},{0,12},{4,16},{8,20},{12,24},{16,28},{21,1},{... | collective-permute-start | bytes 12296 | tf_op jit(solution)/shard_map/ppermute | solution.py:18
  177.7 23.9 %collective-permute-start.8 = (f32[1024,64]{0,1:T(8,128)}, f32[1024,64]{0,1:T(8,128)S(1)}, u32[]{:S(2)}, u32[]{:S(2)}) collective-permute-start(f32[1024,64]{0,1:T(8,128)} %get-tuple-element.105), channel_id=1, source_target_pairs={{20,0},{24,4},{28,8},{0,12},{4,16},{8,20},{12,24},{16,28},{21,1},{... | collective-permute-start | bytes 786440 | tf_op jit(solution)/shard_map/ppermute | solution.py:18
  184.3 11.6 %collective-permute-start.10 = (f32[1024]{0:T(1024)}, f32[1024]{0:T(1024)}, u32[]{:S(2)}, u32[]{:S(2)}) collective-permute-start(f32[1024]{0:T(1024)} %get-tuple-element.109), channel_id=1, source_target_pairs={{24,0},{28,4},{0,8},{4,12},{8,16},{12,20},{16,24},{20,28},{25,1},{... | collective-permute-start | bytes 12296 | tf_op jit(solution)/shard_map/ppermute | solution.py:18
  188.7 12.9 %collective-permute-start.5 = (f32[1024,64]{0,1:T(8,128)}, f32[1024,64]{0,1:T(8,128)}, u32[]{:S(2)}, u32[]{:S(2)}) collective-permute-start(f32[1024,64]{0,1:T(8,128)} %get-tuple-element.103), channel_id=1, source_target_pairs={{24,0},{28,4},{0,8},{4,12},{8,16},{12,20},{16,24},{20,28},{25,1},{... | collective-permute-start | bytes 786440 | tf_op jit(solution)/shard_map/ppermute | solution.py:18
  193.9 6.4 %collective-permute-start.9 = (f32[1024]{0:T(1024)S(1)}, f32[1024]{0:T(1024)S(1)}, u32[]{:S(2)}, u32[]{:S(2)}) collective-permute-start(f32[1024]{0:T(1024)S(1)} %get-tuple-element.107), channel_id=1, source_target_pairs={{28,0},{0,4},{4,8},{8,12},{12,16},{16,20},{20,24},{24,28},{29,1},{... | collective-permute-start | bytes 12296 | tf_op jit(solution)/shard_map/ppermute | solution.py:18
  194.6 9.1 %collective-permute-start.2 = (f32[1024,64]{0,1:T(8,128)S(1)}, f32[1024,64]{0,1:T(8,128)S(1)}, u32[]{:S(2)}, u32[]{:S(2)}) collective-permute-start(f32[1024,64]{0,1:T(8,128)S(1)} %get-tuple-element.101), channel_id=1, source_target_pairs={{28,0},{0,4},{4,8},{8,12},{12,16},{16,20},{20,24},{24,28},{29,1},{... | collective-permute-start | bytes 786440 | tf_op jit(solution)/shard_map/ppermute | solution.py:18
  297.1 7.3 %collective-permute-start.16 = (bf16[1024,64]{0,1:T(8,128)(2,1)S(1)}, bf16[1024,64]{0,1:T(8,128)(2,1)S(1)}, u32[]{:S(2)}, u32[]{:S(2)}) collective-permute-start(bf16[1024,64]{0,1:T(8,128)(2,1)S(1)} %bitcast.69), channel_id=1, source_target_pairs={{12,0},{16,4},{20,8},{24,12},{28,16},{0,20},{4,24},{8,28},{13,1},{... | collective-permute-start | bytes 393224 | tf_op jit(solution)/shard_map/ppermute | solution.py:18
  300.4 9.9 %collective-permute-start.14 = (bf16[1024,64]{0,1:T(8,128)(2,1)S(1)}, bf16[1024,64]{0,1:T(8,128)(2,1)S(1)}, u32[]{:S(2)}, u32[]{:S(2)}) collective-permute-start(bf16[1024,64]{0,1:T(8,128)(2,1)S(1)} %bitcast.70), channel_id=1, source_target_pairs={{8,0},{12,4},{16,8},{20,12},{24,16},{28,20},{0,24},{4,28},{9,1},{1... | collective-permute-start | bytes 393224 | tf_op jit(solution)/shard_map/ppermute | solution.py:18
  302.0 21.9 %collective-permute-start.12 = (bf16[1024,64]{0,1:T(8,128)(2,1)S(1)}, bf16[1024,64]{0,1:T(8,128)(2,1)S(1)}, u32[]{:S(2)}, u32[]{:S(2)}) collective-permute-start(bf16[1024,64]{0,1:T(8,128)(2,1)S(1)} %bitcast.71), channel_id=1, source_target_pairs={{4,0},{8,4},{12,8},{16,12},{20,16},{24,20},{28,24},{0,28},{5,1},{9... | collective-permute-start | bytes 393224 | tf_op jit(solution)/shard_map/ppermute | solution.py:18
  310.3 21.7 %collective-permute-start.20 = (f32[1024]{0:T(1024)S(1)}, f32[1024]{0:T(1024)S(1)}, u32[]{:S(2)}, u32[]{:S(2)}) collective-permute-start(f32[1024]{0:T(1024)S(1)} %get-tuple-element.123), channel_id=1, source_target_pairs={{20,0},{24,4},{28,8},{0,12},{4,16},{8,20},{12,24},{16,28},{21,1},{... | collective-permute-start | bytes 12296 | tf_op jit(solution)/shard_map/ppermute | solution.py:18
  316.9 16.1 %collective-permute-start.19 = (f32[1024]{0:T(1024)}, f32[1024]{0:T(1024)}, u32[]{:S(2)}, u32[]{:S(2)}) collective-permute-start(f32[1024]{0:T(1024)} %get-tuple-element.121), channel_id=1, source_target_pairs={{24,0},{28,4},{0,8},{4,12},{8,16},{12,20},{16,24},{20,28},{25,1},{... | collective-permute-start | bytes 12296 | tf_op jit(solution)/shard_map/ppermute | solution.py:18
  330.4 6.8 %collective-permute-start.18 = (f32[1024]{0:T(1024)}, f32[1024]{0:T(1024)S(1)}, u32[]{:S(2)}, u32[]{:S(2)}) collective-permute-start(f32[1024]{0:T(1024)} %get-tuple-element.119), channel_id=1, source_target_pairs={{28,0},{0,4},{4,8},{8,12},{12,16},{16,20},{20,24},{24,28},{29,1},{... | collective-permute-start | bytes 12296 | tf_op jit(solution)/shard_map/ppermute | solution.py:18
  330.4 12.3 %collective-permute-start.13 = (f32[1024,64]{0,1:T(8,128)}, f32[1024,64]{0,1:T(8,128)S(1)}, u32[]{:S(2)}, u32[]{:S(2)}) collective-permute-start(f32[1024,64]{0,1:T(8,128)} %get-tuple-element.113), channel_id=1, source_target_pairs={{28,0},{0,4},{4,8},{8,12},{12,16},{16,20},{20,24},{24,28},{29,1},{... | collective-permute-start | bytes 786440 | tf_op jit(solution)/shard_map/ppermute | solution.py:18
  331.9 10.8 %collective-permute-start.15 = (f32[1024,64]{0,1:T(8,128)}, f32[1024,64]{0,1:T(8,128)}, u32[]{:S(2)}, u32[]{:S(2)}) collective-permute-start(f32[1024,64]{0,1:T(8,128)} %get-tuple-element.115), channel_id=1, source_target_pairs={{24,0},{28,4},{0,8},{4,12},{8,16},{12,20},{16,24},{20,28},{25,1},{... | collective-permute-start | bytes 786440 | tf_op jit(solution)/shard_map/ppermute | solution.py:18
  331.9 0.6 copy-start.2
  332.5 25.2 %collective-permute-start.17 = (f32[1024,64]{0,1:T(8,128)}, f32[1024,64]{0,1:T(8,128)}, u32[]{:S(2)}, u32[]{:S(2)}) collective-permute-start(f32[1024,64]{0,1:T(8,128)} %get-tuple-element.117), channel_id=1, source_target_pairs={{20,0},{24,4},{28,8},{0,12},{4,16},{8,20},{12,24},{16,28},{21,1},{... | collective-permute-start | bytes 786440 | tf_op jit(solution)/shard_map/ppermute | solution.py:18
  332.5 4.6 %copy-start.3 = (f32[1024]{0:T(1024)S(1)}, f32[1024]{0:T(1024)}, u32[]{:S(2)}) copy-start(f32[1024]{0:T(1024)} %copy-done.2) | copy-start | bytes 12292
where the time goes:
time: 454 us
  blocking collectives  159 us (35%)
  waiting for transfers between devices  132 us (29%)
  starting transfers between devices  79.1 us (17%)
  matrix products  44.4 us (10%)
  other arithmetic  35.3 us (8%)
    ppermute x21, waiting for transfers between devices, shifted(): return lax.ppermute(block, axis, route)  132 us
    psum x2, blocking collectives, orthonormal(): lax.psum(local_gram, ('wide', 'narrow'))  83.5 us
    ppermute x21, starting transfers between devices, shifted(): return lax.ppermute(block, axis, route)  79.1 us
    psum x2, blocking collectives, orthonormal(): lax.psum((jnp.sum(product, axis=0), jnp.sum(vertex_valence)), ('wide', 'n...  75.8 us
    dot_general x7, matrix products, scores_tile(): lax.dot_general(leftside_block, right_block, (((1,), (1,)), ((), ())), pr...  29.9 us
    another operation x6, other arithmetic, orthonormal(): normalizer_coefficient = jnp.linalg.cholesky(gram_matrix)  13 us
    another operation x4, other arithmetic, orthonormal(): jax.scipy.linalg.solve_triangular(normalizer_coefficient, displaced_entri...  11.1 us
  transfers between devices with their start and end apart: 21, of which 7 were waited for; matrix products, arithmetic and copies ran while one was open for 10% of the time, Pallas kernels for 0%

commit v1 on v0

v1 whole, which is shorter than its diff:
```python
from functools import partial
import itertools
import math

import jax
import jax.numpy as jnp
from jax import lax
from jax.sharding import PartitionSpec as P

ITERS = 2


kernel_width_factor = 0.05


def shifted(block, axis, distance):
    devices = range(lax.axis_size(axis))
    route = [((i - distance) % len(devices), i) for i in devices]
    return lax.ppermute(block, axis, route)


def ring_gap(offset, span):
    offset %= span
    return min(offset, span - offset)


def difference_plan(span, far_reach):
    candidates = sorted(range(1, span), key=lambda s: (ring_gap(s, span), s))
    for count in range(1, span):
        best = None
        for chosen in itertools.combinations(candidates, count):
            points = (0,) + chosen
            plan = {}
            for a, b in itertools.permutations(points, 2):
                gap = (b - a) % span
                if 1 <= gap <= far_reach and gap not in plan:
                    plan[gap] = (a, b)
            if len(plan) == far_reach:
                cost = sum(ring_gap(s, span) for s in chosen)
                if best is None or cost < best[0]:
                    best = (cost, chosen, plan)
        if best is not None:
            return list(best[1]), [best[2][gap] for gap in range(1, far_reach + 1)]
    raise ValueError("no plan")


def normalize_rows(values):
    values_wide = values.astype(jnp.float32)
    scaling = lax.rsqrt(jnp.mean(values_wide * values_wide, axis=-1, keepdims=True) + 1e-06)
    return (values_wide * scaling / math.sqrt(values_wide.shape[-1])).astype(jnp.bfloat16)


def scores_tile(leftside_block, right_block):
    kernel_entries = lax.dot_general(
        leftside_block, right_block, (((1,), (1,)), ((), ())), preferred_element_type=jnp.float32
    )
    return jnp.exp(kernel_entries / kernel_width_factor).astype(jnp.bfloat16)


def row_product(affinity, weights):
    return jnp.dot(affinity, weights, preferred_element_type=jnp.float32)


def col_product(affinity, weights):
    return lax.dot_general(
        affinity, weights, (((0,), (0,)), ((), ())), preferred_element_type=jnp.float32
    )


def first_pass(owned, left_unit, right_unit, left_weights, right_weights):
    block_rows = left_unit.shape[0]
    vector_count = left_weights.shape[1]

    def compute_pair():
        affinity = scores_tile(left_unit, right_unit)
        return (
            affinity,
            row_product(affinity, right_weights),
            jnp.sum(affinity, axis=1, dtype=jnp.float32),
            col_product(affinity, left_weights),
            jnp.sum(affinity, axis=0, dtype=jnp.float32),
        )

    def skip_pair():
        zero_part = jnp.zeros((block_rows, vector_count), jnp.float32)
        zero_sum = jnp.zeros((block_rows,), jnp.float32)
        return (
            jnp.zeros((block_rows, block_rows), jnp.bfloat16),
            zero_part,
            zero_sum,
            zero_part,
            zero_sum,
        )

    return lax.cond(owned, compute_pair, skip_pair)


def later_pass(owned, affinity, left_weights, right_weights):
    block_rows = affinity.shape[0]
    vector_count = left_weights.shape[1]

    def compute_pair():
        return (row_product(affinity, right_weights), col_product(affinity, left_weights))

    def skip_pair():
        zero_part = jnp.zeros((block_rows, vector_count), jnp.float32)
        return (zero_part, zero_part)

    return lax.cond(owned, compute_pair, skip_pair)


def butterfly(axis, summed, gathered):
    size = lax.axis_size(axis)
    if size & (size - 1):
        return (
            jax.tree.map(lambda v: lax.psum(v, axis), summed),
            lax.all_gather(gathered, axis, tiled=True),
        )
    index = lax.axis_index(axis)
    step = 1
    while step < size:
        route = [(i, i ^ step) for i in range(size)]
        other_summed, other_gathered = lax.ppermute((summed, gathered), axis, route)
        summed = jax.tree.map(jnp.add, summed, other_summed)
        upper = (index // step) % 2 == 1
        gathered = jnp.where(
            upper,
            jnp.concatenate([other_gathered, gathered]),
            jnp.concatenate([gathered, other_gathered]),
        )
        step *= 2
    return summed, gathered


def hdot(left, right):
    return jnp.dot(left, right, precision=lax.Precision.HIGHEST, preferred_element_type=jnp.float32)


def orthonormal(product, vertex_valence, total_rows):
    block_rows, vector_count = product.shape
    walk = product / vertex_valence[:, None]
    centre = jnp.mean(walk, axis=0)
    centred = walk - centre
    local_gram = hdot(centred.T, centred)
    local_drift = jnp.sum(centred, axis=0)
    summed = (local_gram, jnp.sum(product, axis=0), jnp.sum(vertex_valence))
    gathered = jnp.concatenate([centre, local_drift])[None, :]
    for axis in ("narrow", "wide"):
        summed, gathered = butterfly(axis, summed, gathered)
    gram_sum, column_sums, total_degree_sum = summed
    mean_walk = column_sums / total_degree_sum
    centres = gathered[:, :vector_count] - mean_walk
    drifts = gathered[:, vector_count:]
    cross = hdot(centres.T, drifts)
    gram_matrix = (gram_sum + cross + cross.T + block_rows * hdot(centres.T, centres)) / total_rows
    displaced_entries = walk - mean_walk
    normalizer_coefficient = jnp.linalg.cholesky(gram_matrix)
    return jax.scipy.linalg.solve_triangular(
        normalizer_coefficient, displaced_entries.T, lower=True
    ).T


def on_device(embeddings, start, neighbours):
    wide_count = lax.axis_size("wide")
    lane_count = lax.axis_size("narrow")
    broad_index = lax.axis_index("wide")
    lane_index = lax.axis_index("narrow")
    far_reach = wide_count // 2 - 1
    fetch_offsets, pair_plan = difference_plan(wide_count, far_reach)
    unit_block = normalize_rows(embeddings)
    block_rows = unit_block.shape[0]
    total_rows = block_rows * wide_count * lane_count

    def block_at(offset):
        return (broad_index + offset) % wide_count * lane_count + lane_index

    owned_list = []
    for left, right in pair_plan:
        own_row = lax.dynamic_slice_in_dim(neighbours, block_at(left), 1, 0)[0]
        owned_list.append(jnp.any(own_row == block_at(right)))

    units = {0: unit_block}
    weights = {0: start}
    for offset in fetch_offsets:
        units[offset], weights[offset] = shifted((unit_block, start), "wide", -offset)

    self_mask = lax.broadcasted_iota(
        jnp.int32, (block_rows, block_rows), 0
    ) == lax.broadcasted_iota(jnp.int32, (block_rows, block_rows), 1)
    near_tile = jnp.where(
        self_mask, jnp.zeros((), jnp.bfloat16), scores_tile(unit_block, unit_block)
    )

    vector_count = start.shape[1]
    zero_part = jnp.zeros((block_rows, vector_count), jnp.float32)
    zero_sum = jnp.zeros((block_rows,), jnp.float32)
    parts = {offset: zero_part for offset in units}
    sums = {offset: zero_sum for offset in units}
    tiles = []
    for (left, right), owned in zip(pair_plan, owned_list):
        affinity, row_part, row_sum, col_part, col_sum = first_pass(
            owned, units[left], units[right], weights[left], weights[right]
        )
        tiles.append(affinity)
        parts[left] = parts[left] + row_part
        sums[left] = sums[left] + row_sum
        parts[right] = parts[right] + col_part
        sums[right] = sums[right] + col_sum

    product = row_product(near_tile, start) + parts[0]
    vertex_valence = jnp.sum(near_tile, axis=1, dtype=jnp.float32) + sums[0]
    for offset in fetch_offsets:
        returned, returned_sum = shifted((parts[offset], sums[offset]), "wide", offset)
        product = product + returned
        vertex_valence = vertex_valence + returned_sum
    basis = orthonormal(product, vertex_valence, total_rows)

    for iteration in range(1, ITERS):
        current = basis.astype(jnp.bfloat16)
        weights = {0: current}
        for offset in fetch_offsets:
            weights[offset] = shifted(current, "wide", -offset)
        parts = {offset: zero_part for offset in units}
        for (left, right), owned, affinity in zip(pair_plan, owned_list, tiles):
            row_part, col_part = later_pass(owned, affinity, weights[left], weights[right])
            parts[left] = parts[left] + row_part
            parts[right] = parts[right] + col_part
        product = row_product(near_tile, current) + parts[0]
        for offset in fetch_offsets:
            product = product + shifted(parts[offset], "wide", offset)
        basis = orthonormal(product, vertex_valence, total_rows)
    return (basis, vertex_valence / block_rows)


def solution(mesh):
    in_specs = (P(("wide", "narrow"), None), P(("wide", "narrow"), None), P())
    out_specs = (P(("wide", "narrow"), None), P(("wide", "narrow")))
    return jax.shard_map(
        on_device, mesh=mesh, in_specs=in_specs, out_specs=out_specs, check_vma=False
    )
```

time: 454 us -> 283 us (0.62)
  blocking collectives: 159 us -> 0 us
  starting transfers between devices: 79.1 us -> 55.1 us
  matrix products: 44.4 us -> 51.6 us
    psum x4 -> x0, blocking collectives: 159 us -> none  [the longest x2 83.5 us: orthonormal(): lax.psum(local_gram, ('wide', 'narrow'))]
    ppermute x21 -> x12, starting transfers between devices: 79.1 us -> 15.7 us  [shifted(): return lax.ppermute(block, axis, route)]
    ppermute x0 -> x35, waiting for transfers between devices: none -> 49.6 us  [butterfly(): other_summed, other_gathered = lax.ppermute((summed, gathered), axis, route)]
    ppermute x21 -> x12, waiting for transfers between devices: 132 us -> 82.4 us  [shifted(): return lax.ppermute(block, axis, route)]
    ppermute x0 -> x35, starting transfers between devices: none -> 39.4 us  [butterfly(): other_summed, other_gathered = lax.ppermute((summed, gathered), axis, route)]
    dot_general x16 -> x20, matrix products: 12.9 us -> 29.4 us  [the longest x8 15 us: row_product(): return jnp.dot(affinity, weights, preferred_element_type=jnp.float32)]
    dot_general x7 -> x4, matrix products: 29.9 us -> 20.6 us  [scores_tile(): lax.dot_general(leftside_block, right_block, (((1,), (1,)), ((), ())), pr...]
  transfers between devices with their start and end apart: 21 -> 47, of which waited for: 7 -> 31; matrix products, arithmetic and copies ran while one was open for 10% -> 11% of each run, Pallas kernels for 0% -> 0%
where the time goes in v1:
time: 283 us; the launch traced here: 282 us
  waiting for transfers between devices  132 us (47%)
  starting transfers between devices  55.1 us (19%)
  matrix products  51.6 us (18%)
  other arithmetic  36.2 us (13%)
  between operations  6.76 us (2%)
    ppermute x12, waiting for transfers between devices, shifted(): return lax.ppermute(block, axis, route)  82.4 us
    ppermute x35, waiting for transfers between devices, butterfly(): other_summed, other_gathered = lax.ppermute((summed, gathered), axis, route)  49.6 us
    ppermute x35, starting transfers between devices, butterfly(): other_summed, other_gathered = lax.ppermute((summed, gathered), axis, route)  39.4 us
    dot_general x4, matrix products, scores_tile(): lax.dot_general(leftside_block, right_block, (((1,), (1,)), ((), ())), pr...  20.6 us
    ppermute x12, starting transfers between devices, shifted(): return lax.ppermute(block, axis, route)  15.7 us
    dot_general x8, matrix products, row_product(): return jnp.dot(affinity, weights, preferred_element_type=jnp.float32)  15 us
    another operation x6, other arithmetic, orthonormal(): normalizer_coefficient = jnp.linalg.cholesky(gram_matrix)  13 us
    dot_general x6, matrix products, col_product(): lax.dot_general(affinity, weights, (((0,), (0,)), ((), ())), preferred_el...  12.5 us
  transfers between devices with their start and end apart: 47, of which 31 were waited for; matrix products, arithmetic and copies ran while one was open for 11% of the time, Pallas kernels for 0%

profile of v1, /device:TPU:0, one launch (start us, length us, event | category | flops | bytes accessed | tf_op | source)
XLA Modules:
  0.0 282.2 jit_solution(15245356729804015650)
XLA Ops:
  0.6 1.9 fusion.1
  4.1 6.0 %collective-permute-start = (bf16[1024,768]{1,0:T(8,128)(2,1)}, bf16[1024,768]{1,0:T(8,128)(2,1)}, u32[]{:S(2)}, u32[]{:S(2)}) collective-permute-start(bf16[1024,768]{1,0:T(8,128)(2,1)} %fusion.3), channel_id=1, source_target_pairs={{4,0},{8,4},{12,8},{16,12},{20,16},{24,20},{28,24},{0,28},{5,1},{9... | collective-permute-start | bytes 4718600 | tf_op jit(solution)/shard_map/ppermute | solution.py:19
  10.9 4.4 %convert_reduce_fusion.6 = (f32[1024]{0:T(1024)}, bf16[1024,1024]{0,1:T(8,128)(2,1)S(1)}) fusion(bf16[1024,768]{1,0:T(8,128)(2,1)} %fusion.3), kind=kOutput, calls=%fused_computation.9 | convolution fusion | flops 1616903168 | bytes 3674112 | tf_op jit(solution)/shard_map/dot_general | solution.py:54
  18.0 66.5 %collective-permute-done.1 = bf16[1024,64]{1,0:T(8,128)(2,1)S(1)} collective-permute-done((bf16[1024,64]{1,0:T(8,128)(2,1)S(1)}, bf16[1024,64]{1,0:T(8,128)(2,1)S(1)}, u32[]{:S(2)}, u32[]{:S(2)}) %collective-permute-start.1) | collective-permute-done | bytes 131104 | tf_op jit(solution)/shard_map/ppermute | solution.py:19
  84.5 5.4 %collective-permute-done.3 = bf16[1024,64]{1,0:T(8,128)(2,1)S(1)} collective-permute-done((bf16[1024,64]{1,0:T(8,128)(2,1)S(1)}, bf16[1024,64]{1,0:T(8,128)(2,1)S(1)}, u32[]{:S(2)}, u32[]{:S(2)}) %collective-permute-start.3) | collective-permute-done | bytes 131104 | tf_op jit(solution)/shard_map/ppermute | solution.py:19
  89.9 9.7 %conditional.8 = (bf16[1024,1024]{1,0:T(8,128)(2,1)}, f32[1024,64]{0,1:T(8,128)S(1)}, f32[1024]{0:T(1024)S(1)}, f32[1024,64]{0,1:T(8,128)S(1)}, f32[1024]{0:T(1024)S(1)}) conditional(s32[]{:T(128)} %convert_element_type.56, () %tuple.62, (bf16[1024,768]{1,0:T(8,128)(2,1)}, bf16[1024,768]{1,0:T(8,128)(2,1)}, bf16[1024,64]{1,0:T(8,128)(2,1)S(1)}, ...), branch_computations={%region_12.13_spmd, %region_13.16_spmd} | conditional | flops 1884289024 | bytes 10231848 | solution.py:95
  89.9 5.2 %convert_reduce_fusion.4 = (f32[1024]{0:T(1024)S(1)}, f32[1024]{0:T(1024)S(1)}, bf16[1024,1024]{1,0:T(8,128)(2,1)}) fusion(bf16[1024,768]{1,0:T(8,128)(2,1)} %get-tuple-element.52, bf16[1024,768]{1,0:T(8,128)(2,1)} %get-tuple-element.53), kind=kOutput, calls=%fused_computation.6 | convolution fusion | flops 1615853568 | bytes 5251072 | tf_op jit(solution)/shard_map/cond/branch_1_fun/dot_general | solution.py:54
  95.1 2.3 fusion.49
  97.5 2.1 fusion.50
  99.6 9.6 %conditional.6 = (bf16[1024,1024]{1,0:T(8,128)(2,1)}, f32[1024,64]{0,1:T(8,128)S(1)}, f32[1024]{0:T(1024)S(1)}, f32[1024,64]{0,1:T(8,128)S(1)}, f32[1024]{0:T(1024)S(1)}) conditional(s32[]{:T(128)} %convert_element_type.54, () %tuple.58, (bf16[1024,768]{1,0:T(8,128)(2,1)}, bf16[1024,768]{1,0:T(8,128)(2,1)}, bf16[1024,64]{1,0:T(8,128)(2,1)S(1)}, ...), branch_computations={%region_2.3_spmd, %region_3.0_spmd} | conditional | flops 1884289024 | bytes 10231848 | solution.py:95
  99.6 5.2 %convert_reduce_fusion = (f32[1024]{0:T(1024)S(1)}, f32[1024]{0:T(1024)S(1)}, bf16[1024,1024]{1,0:T(8,128)(2,1)}) fusion(bf16[1024,768]{1,0:T(8,128)(2,1)} %get-tuple-element.36, bf16[1024,768]{1,0:T(8,128)(2,1)} %get-tuple-element.42), kind=kOutput, calls=%fused_computation | convolution fusion | flops 1615853568 | bytes 5251072 | tf_op jit(solution)/shard_map/cond/branch_1_fun/dot_general | solution.py:54
  104.8 2.3 fusion.45
  107.1 2.1 fusion.46
  110.0 10.3 %conditional.7 = (bf16[1024,1024]{1,0:T(8,128)(2,1)}, f32[1024,64]{0,1:T(8,128)S(1)}, f32[1024]{0:T(1024)}, f32[1024,64]{0,1:T(8,128)S(1)}, f32[1024]{0:T(1024)}) conditional(s32[]{:T(128)} %convert_element_type.55, () %tuple.60, (bf16[1024,768]{1,0:T(8,128)(2,1)}, bf16[1024,768]{1,0:T(8,128)(2,1)}, bf16[1024,64]{0,1:T(8,128)(2,1)S(1)}, ...), branch_computations={%region_7.8_spmd, %region_8.11_spmd} | conditional | flops 1884289024 | bytes 10231848 | solution.py:95
  110.0 5.8 %convert_reduce_fusion.2 = (f32[1024]{0:T(1024)}, f32[1024]{0:T(1024)}, bf16[1024,1024]{1,0:T(8,128)(2,1)}) fusion(bf16[1024,768]{1,0:T(8,128)(2,1)} %get-tuple-element.48, bf16[1024,768]{1,0:T(8,128)(2,1)} %get-tuple-element.49), kind=kOutput, calls=%fused_computation.3 | convolution fusion | flops 1615853568 | bytes 5251072 | tf_op jit(solution)/shard_map/cond/branch_1_fun/dot_general | solution.py:54
  115.8 2.3 fusion.47
  118.1 2.1 fusion.48
  121.0 5.3 %collective-permute-start.6 = (f32[1024]{0:T(1024)S(1)}, f32[1024]{0:T(1024)S(1)}, u32[]{:S(2)}, u32[]{:S(2)}) collective-permute-start(f32[1024]{0:T(1024)S(1)} %add.257), channel_id=1, source_target_pairs={{28,0},{0,4},{4,8},{8,12},{12,16},{16,20},{20,24},{24,28},{29,1},{... | collective-permute-start | bytes 12296 | tf_op jit(solution)/shard_map/ppermute | solution.py:19
  127.5 2.8 %collective-permute-done.6 = f32[1024]{0:T(1024)S(1)} collective-permute-done((f32[1024]{0:T(1024)S(1)}, f32[1024]{0:T(1024)S(1)}, u32[]{:S(2)}, u32[]{:S(2)}) %collective-permute-start.6) | collective-permute-done | bytes 4128 | tf_op jit(solution)/shard_map/ppermute | solution.py:19
  134.4 2.2 collective-permute-start.14
  138.9 2.9 %collective-permute-done.15 = f32[4,128]{1,0:T(4,128)S(1)} collective-permute-done((f32[4,128]{1,0:T(4,128)S(1)}, f32[4,128]{1,0:T(4,128)S(1)}, u32[]{:S(2)}, u32[]{:S(2)}) %collective-permute-start.15) | collective-permute-done | bytes 2080 | tf_op jit(solution)/shard_map/ppermute | solution.py:123
  141.8 1.8 collective-permute-start.16
  144.8 2.0 collective-permute-start.19
  151.4 2.3 collective-permute-done.24
  155.7 2.3 collective-permute-done.25
  160.4 1.7 collective-permute-start.21
  163.0 2.3 collective-permute-start.27
  165.4 2.3 collective-permute-done.27
  169.3 1.8 collective-permute-start.9
  171.5 1.8 collective-permute-done.9
  173.3 2.0 collective-permute-start.10
  175.3 1.9 collective-permute-done.10
  177.4 3.8 %collective-permute-done.11 = f32[64,64]{0,1:T(8,128)S(1)} collective-permute-done((f32[64,64]{0,1:T(8,128)S(1)}, f32[64,64]{0,1:T(8,128)S(1)}, u32[]{:S(2)}, u32[]{:S(2)}) %collective-permute-start.11) | collective-permute-done | bytes 16416 | tf_op jit(solution)/shard_map/ppermute | solution.py:123
  181.2 2.0 collective-permute-start.12
  183.5 2.5 collective-permute-done.12
  186.3 5.8 %cholesky.44 = f32[64,64]{1,0:T(8,128)S(1)} custom-call(f32[64,64]{1,0:T(8,128)S(1)} %fusion.23), custom_call_target="Cholesky" | custom-call | tf_op jit(solution)/shard_map/jit(cholesky)/cholesky | solution.py:157
  193.5 4.9 %custom-call.6 = f32[1,64,64]{1,2,0:T(8,128)S(1)} custom-call(f32[1,64,64]{2,1,0:T(8,128)S(1)} %fusion.16), custom_call_target="InvertDiagBlocksLowerTriangular" | custom-call | tf_op jit(solution)/shard_map/jit(_solve_triangular)/triangular_solve | solution.py:158
  200.2 2.2 collective-permute-start.29
  203.9 4.4 %conditional.9 = (f32[1024,64]{0,1:T(8,128)S(1)}, f32[1024,64]{0,1:T(8,128)S(1)}) conditional(s32[]{:T(128)} %convert_element_type.54, () %tuple.64, (bf16[1024,1024]{1,0:T(8,128)(2,1)}, bf16[1024,64]{0,1:T(8,128)(2,1)S(1)}, bf16[1024,64]{0,1:T(8,128)(2,1)S(1)}) %tuple.104), branch_computations={%region_23.26_spmd, %region_24.27_spmd} | conditional | flops 268435456 | bytes 4980752 | solution.py:109
  203.9 2.3 fusion.39
  206.2 2.1 fusion.40
  208.3 4.4 %conditional.11 = (f32[1024,64]{0,1:T(8,128)S(1)}, f32[1024,64]{0,1:T(8,128)S(1)}) conditional(s32[]{:T(128)} %convert_element_type.56, () %tuple.68, (bf16[1024,1024]{1,0:T(8,128)(2,1)}, bf16[1024,64]{0,1:T(8,128)(2,1)S(1)}, bf16[1024,64]{0,1:T(8,128)(2,1)S(1)}) %tuple.69), branch_computations={%region_27.30_spmd, %region_28.31_spmd} | conditional | flops 268435456 | bytes 4980752 | solution.py:109
  208.3 2.3 fusion.43
  210.7 2.1 fusion.44
  213.5 4.4 %conditional.10 = (f32[1024,64]{0,1:T(8,128)S(1)}, f32[1024,64]{0,1:T(8,128)S(1)}) conditional(s32[]{:T(128)} %convert_element_type.55, () %tuple.66, (bf16[1024,1024]{1,0:T(8,128)(2,1)}, bf16[1024,64]{0,1:T(8,128)(2,1)S(1)}, bf16[1024,64]{0,1:T(8,128)(2,1)S(1)}) %tuple.105), branch_computations={%region_25.28_spmd, %region_26.29_spmd} | conditional | flops 268435456 | bytes 4980752 | solution.py:109
  213.5 2.3 fusion.41
  215.9 2.1 fusion.42
  218.7 4.2 %collective-permute-done.30 = f32[1024,64]{0,1:T(8,128)} collective-permute-done((f32[1024,64]{0,1:T(8,128)}, f32[1024,64]{0,1:T(8,128)}, u32[]{:S(2)}, u32[]{:S(2)}) %collective-permute-start.30) | collective-permute-done | bytes 262176 | tf_op jit(solution)/shard_map/ppermute | solution.py:19
  222.9 1.7 collective-permute-done.31
  227.2 1.8 collective-permute-start.38
  228.9 1.9 collective-permute-done.38
  230.8 2.9 %collective-permute-start.39 = (f32[4,128]{1,0:T(4,128)S(1)}, f32[4,128]{1,0:T(4,128)S(1)}, u32[]{:S(2)}, u32[]{:S(2)}) collective-permute-start(f32[4,128]{1,0:T(4,128)S(1)} %maximum_select_fusion.7), channel_id=1, source_target_pairs={{0,4},{4,0},{8,12},{12,8},{16,20},{20,16},{24,28},{28,24},{1,5},{5... | collective-permute-start | bytes 6152 | tf_op jit(solution)/shard_map/ppermute | solution.py:123
  238.2 2.7 collective-permute-done.43
  242.1 2.4 collective-permute-done.44
  245.5 2.4 collective-permute-done.45
  248.0 3.9 %collective-permute-start.46 = (f32[64]{0:T(128)S(1)}, f32[64]{0:T(128)S(1)}, u32[]{:S(2)}, u32[]{:S(2)}) collective-permute-start(f32[64]{0:T(128)S(1)} %add.298), channel_id=1, source_target_pairs={{0,16},{4,20},{8,24},{12,28},{16,0},{20,4},{24,8},{28,12},{1,17},{... | collective-permute-start | bytes 776 | tf_op jit(solution)/shard_map/ppermute | solution.py:123
  251.9 1.8 collective-permute-start.33
  253.7 2.2 collective-permute-done.33
  255.9 2.0 collective-permute-start.34
  257.9 1.9 collective-permute-done.34
  259.9 3.8 %collective-permute-done.35 = f32[64,64]{0,1:T(8,128)S(1)} collective-permute-done((f32[64,64]{0,1:T(8,128)S(1)}, f32[64,64]{0,1:T(8,128)S(1)}, u32[]{:S(2)}, u32[]{:S(2)}) %collective-permute-start.35) | collective-permute-done | bytes 16416 | tf_op jit(solution)/shard_map/ppermute | solution.py:123
  264.9 3.7 %collective-permute-done.36 = f32[64,64]{0,1:T(8,128)S(1)} collective-permute-done((f32[64,64]{0,1:T(8,128)S(1)}, f32[64,64]{0,1:T(8,128)S(1)}, u32[]{:S(2)}, u32[]{:S(2)}) %collective-permute-start.36) | collective-permute-done | bytes 16416 | tf_op jit(solution)/shard_map/ppermute | solution.py:123
  268.9 5.8 %cholesky.55 = f32[64,64]{1,0:T(8,128)S(1)} custom-call(f32[64,64]{1,0:T(8,128)S(1)} %fusion.19), custom_call_target="Cholesky" | custom-call | tf_op jit(solution)/shard_map/jit(cholesky)/cholesky | solution.py:157
  276.1 4.9 %custom-call.7 = f32[1,64,64]{1,2,0:T(8,128)S(1)} custom-call(f32[1,64,64]{2,1,0:T(8,128)S(1)} %fusion.17), custom_call_target="InvertDiagBlocksLowerTriangular" | custom-call | tf_op jit(solution)/shard_map/jit(_solve_triangular)/triangular_solve | solution.py:158
  (137 shorter events, 41.6 us)
Async XLA Ops:
  0.6 1.9 copy-start
  0.6 9.5 %copy-start.1 = (bf16[1024,64]{0,1:T(8,128)(2,1)S(1)}, bf16[1024,64]{0,1:T(8,128)(2,1)}, u32[]{:S(2)}) copy-start(bf16[1024,64]{0,1:T(8,128)(2,1)} %param.19) | copy-start | bytes 393220
  4.1 85.8 %collective-permute-start = (bf16[1024,768]{1,0:T(8,128)(2,1)}, bf16[1024,768]{1,0:T(8,128)(2,1)}, u32[]{:S(2)}, u32[]{:S(2)}) collective-permute-start(bf16[1024,768]{1,0:T(8,128)(2,1)} %fusion.3), channel_id=1, source_target_pairs={{4,0},{8,4},{12,8},{16,12},{20,16},{24,20},{28,24},{0,28},{5,1},{9... | collective-permute-start | bytes 4718600 | tf_op jit(solution)/shard_map/ppermute | solution.py:19
  10.1 79.8 %collective-permute-start.2 = (bf16[1024,768]{1,0:T(8,128)(2,1)}, bf16[1024,768]{1,0:T(8,128)(2,1)}, u32[]{:S(2)}, u32[]{:S(2)}) collective-permute-start(bf16[1024,768]{1,0:T(8,128)(2,1)} %fusion.3), channel_id=1, source_target_pairs={{24,0},{28,4},{0,8},{4,12},{8,16},{12,20},{16,24},{20,28},{25,1},{... | collective-permute-start | bytes 4718600 | tf_op jit(solution)/shard_map/ppermute | solution.py:19
  10.3 5.0 %copy-start.4 = (s32[32,3]{0,1:T(4,128)S(1)}, s32[32,3]{0,1:T(4,128)}, u32[]{:S(2)}) copy-start(s32[32,3]{0,1:T(4,128)} %param.20) | copy-start | bytes 1156
  10.3 74.2 %collective-permute-start.1 = (bf16[1024,64]{1,0:T(8,128)(2,1)S(1)}, bf16[1024,64]{1,0:T(8,128)(2,1)S(1)}, u32[]{:S(2)}, u32[]{:S(2)}) collective-permute-start(bf16[1024,64]{1,0:T(8,128)(2,1)S(1)} %copy.5), channel_id=1, source_target_pairs={{4,0},{8,4},{12,8},{16,12},{20,16},{24,20},{28,24},{0,28},{5,1},{9... | collective-permute-start | bytes 393224 | tf_op jit(solution)/shard_map/ppermute | solution.py:19
  10.9 79.0 %collective-permute-start.3 = (bf16[1024,64]{1,0:T(8,128)(2,1)S(1)}, bf16[1024,64]{1,0:T(8,128)(2,1)S(1)}, u32[]{:S(2)}, u32[]{:S(2)}) collective-permute-start(bf16[1024,64]{1,0:T(8,128)(2,1)S(1)} %copy.5), channel_id=1, source_target_pairs={{24,0},{28,4},{0,8},{4,12},{8,16},{12,20},{16,24},{20,28},{25,1},{... | collective-permute-start | bytes 393224 | tf_op jit(solution)/shard_map/ppermute | solution.py:19
  109.2 0.8 copy-start.2
  110.0 21.9 %collective-permute-start.4 = (f32[1024,64]{0,1:T(8,128)}, f32[1024,64]{0,1:T(8,128)}, u32[]{:S(2)}, u32[]{:S(2)}) collective-permute-start(f32[1024,64]{0,1:T(8,128)} %add.251), channel_id=1, source_target_pairs={{28,0},{0,4},{4,8},{8,12},{12,16},{16,20},{20,24},{24,28},{29,1},{... | collective-permute-start | bytes 786440 | tf_op jit(solution)/shard_map/ppermute | solution.py:19
  120.3 11.6 %copy-start.3 = (f32[1024,64]{0,1:T(8,128)S(1)}, f32[1024,64]{0,1:T(8,128)}, u32[]{:S(2)}) copy-start(f32[1024,64]{0,1:T(8,128)} %copy-done.2) | copy-start | bytes 786436
  121.0 10.9 %collective-permute-start.5 = (f32[1024,64]{0,1:T(8,128)}, f32[1024,64]{0,1:T(8,128)S(1)}, u32[]{:S(2)}, u32[]{:S(2)}) collective-permute-start(f32[1024,64]{0,1:T(8,128)} %add.253), channel_id=1, source_target_pairs={{8,0},{12,4},{16,8},{20,12},{24,16},{28,20},{0,24},{4,28},{9,1},{1... | collective-permute-start | bytes 786440 | tf_op jit(solution)/shard_map/ppermute | solution.py:19
  121.0 9.3 %collective-permute-start.6 = (f32[1024]{0:T(1024)S(1)}, f32[1024]{0:T(1024)S(1)}, u32[]{:S(2)}, u32[]{:S(2)}) collective-permute-start(f32[1024]{0:T(1024)S(1)} %add.257), channel_id=1, source_target_pairs={{28,0},{0,4},{4,8},{8,12},{12,16},{16,20},{20,24},{24,28},{29,1},{... | collective-permute-start | bytes 12296 | tf_op jit(solution)/shard_map/ppermute | solution.py:19
  127.0 3.6 %collective-permute-start.7 = (f32[1024]{0:T(1024)S(1)}, f32[1024]{0:T(1024)S(1)}, u32[]{:S(2)}, u32[]{:S(2)}) collective-permute-start(f32[1024]{0:T(1024)S(1)} %add.259), channel_id=1, source_target_pairs={{8,0},{12,4},{16,8},{20,12},{24,16},{28,20},{0,24},{4,28},{9,1},{1... | collective-permute-start | bytes 12296 | tf_op jit(solution)/shard_map/ppermute | solution.py:19
  133.3 1.1 collective-permute-start.13
  134.4 3.7 %collective-permute-start.14 = (f32[2,128]{1,0:T(2,128)S(1)}, f32[2,128]{1,0:T(2,128)S(1)}, u32[]{:S(2)}, u32[]{:S(2)}) collective-permute-start(f32[2,128]{1,0:T(2,128)S(1)} %maximum_select_fusion.8), channel_id=1, source_target_pairs={{0,2},{1,3},{2,0},{3,1},{4,6},{5,7},{6,4},{7,5},{8,10},{9,11},{10,... | collective-permute-start | bytes 3080 | tf_op jit(solution)/shard_map/ppermute | solution.py:123
  138.2 3.6 %collective-permute-start.15 = (f32[4,128]{1,0:T(4,128)S(1)}, f32[4,128]{1,0:T(4,128)S(1)}, u32[]{:S(2)}, u32[]{:S(2)}) collective-permute-start(f32[4,128]{1,0:T(4,128)S(1)} %maximum_select_fusion.6), channel_id=1, source_target_pairs={{0,4},{4,0},{8,12},{12,8},{16,20},{20,16},{24,28},{28,24},{1,5},{5... | collective-permute-start | bytes 6152 | tf_op jit(solution)/shard_map/ppermute | solution.py:123
  138.8 30.5 %collective-permute-start.8 = (f32[64,64]{0,1:T(8,128)S(1)}, f32[64,64]{0,1:T(8,128)S(1)}, u32[]{:S(2)}, u32[]{:S(2)}) collective-permute-start(f32[64,64]{0,1:T(8,128)S(1)} %fusion.10), channel_id=1, source_target_pairs={{0,1},{1,0},{2,3},{3,2},{4,5},{5,4},{6,7},{7,6},{8,9},{9,8},{10,11... | collective-permute-start | bytes 49160 | tf_op jit(solution)/shard_map/ppermute | solution.py:123
  141.8 29.3 %collective-permute-start.16 = (f32[8,128]{1,0:T(8,128)S(1)}, f32[8,128]{1,0:T(8,128)S(1)}, u32[]{:S(2)}, u32[]{:S(2)}) collective-permute-start(f32[8,128]{1,0:T(8,128)S(1)} %maximum_select_fusion.4), channel_id=1, source_target_pairs={{0,8},{4,12},{8,0},{12,4},{16,24},{20,28},{24,16},{28,20},{1,9},{5... | collective-permute-start | bytes 12296 | tf_op jit(solution)/shard_map/ppermute | solution.py:123
  143.6 1.1 collective-permute-start.18
  144.8 6.6 %collective-permute-start.19 = (f32[64]{0:T(128)S(1)}, f32[64]{0:T(128)S(1)}, u32[]{:S(2)}, u32[]{:S(2)}) collective-permute-start(f32[64]{0:T(128)S(1)} %add.271), channel_id=1, source_target_pairs={{0,2},{1,3},{2,0},{3,1},{4,6},{5,7},{6,4},{7,5},{8,10},{9,11},{10,... | collective-permute-start | bytes 776 | tf_op jit(solution)/shard_map/ppermute | solution.py:123
  147.4 1.4 collective-permute-start.23
  150.0 3.7 %collective-permute-start.24 = (f32[]{:T(128)}, f32[]{:T(128)}, u32[]{:S(2)}, u32[]{:S(2)}) collective-permute-start(f32[]{:T(128)} %add.276), channel_id=1, source_target_pairs={{0,2},{1,3},{2,0},{3,1},{4,6},{5,7},{6,4},{7,5},{8,10},{9,11},{10,... | collective-permute-start | bytes 20 | tf_op jit(solution)/shard_map/ppermute | solution.py:123
  151.4 8.9 %collective-permute-start.20 = (f32[64]{0:T(128)S(1)}, f32[64]{0:T(128)S(1)}, u32[]{:S(2)}, u32[]{:S(2)}) collective-permute-start(f32[64]{0:T(128)S(1)} %add.272), channel_id=1, source_target_pairs={{0,4},{4,0},{8,12},{12,8},{16,20},{20,16},{24,28},{28,24},{1,5},{5... | collective-permute-start | bytes 776 | tf_op jit(solution)/shard_map/ppermute | solution.py:123
  154.4 3.7 %collective-permute-start.25 = (f32[]{:T(128)}, f32[]{:T(128)}, u32[]{:S(2)}, u32[]{:S(2)}) collective-permute-start(f32[]{:T(128)} %add.277), channel_id=1, source_target_pairs={{0,4},{4,0},{8,12},{12,8},{16,20},{20,16},{24,28},{28,24},{1,5},{5... | collective-permute-start | bytes 20 | tf_op jit(solution)/shard_map/ppermute | solution.py:123
  158.7 3.7 %collective-permute-start.26 = (f32[]{:T(128)}, f32[]{:T(128)}, u32[]{:S(2)}, u32[]{:S(2)}) collective-permute-start(f32[]{:T(128)} %add.278), channel_id=1, source_target_pairs={{0,8},{4,12},{8,0},{12,4},{16,24},{20,28},{24,16},{28,20},{1,9},{5... | collective-permute-start | bytes 20 | tf_op jit(solution)/shard_map/ppermute | solution.py:123
  160.4 7.9 %collective-permute-start.21 = (f32[64]{0:T(128)S(1)}, f32[64]{0:T(128)S(1)}, u32[]{:S(2)}, u32[]{:S(2)}) collective-permute-start(f32[64]{0:T(128)S(1)} %add.273), channel_id=1, source_target_pairs={{0,8},{4,12},{8,0},{12,4},{16,24},{20,28},{24,16},{28,20},{1,9},{5... | collective-permute-start | bytes 776 | tf_op jit(solution)/shard_map/ppermute | solution.py:123
  163.0 4.6 %collective-permute-start.27 = (f32[]{:T(128)}, f32[]{:T(128)}, u32[]{:S(2)}, u32[]{:S(2)}) collective-permute-start(f32[]{:T(128)} %add.279), channel_id=1, source_target_pairs={{0,16},{4,20},{8,24},{12,28},{16,0},{20,4},{24,8},{28,12},{1,17},{... | collective-permute-start | bytes 20 | tf_op jit(solution)/shard_map/ppermute | solution.py:123
  168.3 7.0 %collective-permute-start.22 = (f32[64]{0:T(128)S(1)}, f32[64]{0:T(128)S(1)}, u32[]{:S(2)}, u32[]{:S(2)}) collective-permute-start(f32[64]{0:T(128)S(1)} %add.274), channel_id=1, source_target_pairs={{0,16},{4,20},{8,24},{12,28},{16,0},{20,4},{24,8},{28,12},{1,17},{... | collective-permute-start | bytes 776 | tf_op jit(solution)/shard_map/ppermute | solution.py:123
  169.3 4.0 %collective-permute-start.9 = (f32[64,64]{0,1:T(8,128)S(1)}, f32[64,64]{0,1:T(8,128)S(1)}, u32[]{:S(2)}, u32[]{:S(2)}) collective-permute-start(f32[64,64]{0,1:T(8,128)S(1)} %add.261), channel_id=1, source_target_pairs={{0,2},{1,3},{2,0},{3,1},{4,6},{5,7},{6,4},{7,5},{8,10},{9,11},{10,... | collective-permute-start | bytes 49160 | tf_op jit(solution)/shard_map/ppermute | solution.py:123
  171.1 6.2 %collective-permute-start.17 = (f32[16,128]{1,0:T(8,128)S(1)}, f32[16,128]{1,0:T(8,128)S(1)}, u32[]{:S(2)}, u32[]{:S(2)}) collective-permute-start(f32[16,128]{1,0:T(8,128)S(1)} %maximum_select_fusion.2), channel_id=1, source_target_pairs={{0,16},{4,20},{8,24},{12,28},{16,0},{20,4},{24,8},{28,12},{1,17},{... | collective-permute-start | bytes 24584 | tf_op jit(solution)/shard_map/ppermute | solution.py:123
  173.3 3.9 %collective-permute-start.10 = (f32[64,64]{0,1:T(8,128)S(1)}, f32[64,64]{0,1:T(8,128)S(1)}, u32[]{:S(2)}, u32[]{:S(2)}) collective-permute-start(f32[64,64]{0,1:T(8,128)S(1)} %add.262), channel_id=1, source_target_pairs={{0,4},{4,0},{8,12},{12,8},{16,20},{20,16},{24,28},{28,24},{1,5},{5... | collective-permute-start | bytes 49160 | tf_op jit(solution)/shard_map/ppermute | solution.py:123
  177.2 3.9 %collective-permute-start.11 = (f32[64,64]{0,1:T(8,128)S(1)}, f32[64,64]{0,1:T(8,128)S(1)}, u32[]{:S(2)}, u32[]{:S(2)}) collective-permute-start(f32[64,64]{0,1:T(8,128)S(1)} %add.263), channel_id=1, source_target_pairs={{0,8},{4,12},{8,0},{12,4},{16,24},{20,28},{24,16},{28,20},{1,9},{5... | collective-permute-start | bytes 49160 | tf_op jit(solution)/shard_map/ppermute | solution.py:123
  181.2 4.8 %collective-permute-start.12 = (f32[64,64]{0,1:T(8,128)S(1)}, f32[64,64]{0,1:T(8,128)S(1)}, u32[]{:S(2)}, u32[]{:S(2)}) collective-permute-start(f32[64,64]{0,1:T(8,128)S(1)} %add.264), channel_id=1, source_target_pairs={{0,16},{4,20},{8,24},{12,28},{16,0},{20,4},{24,8},{28,12},{1,17},{... | collective-permute-start | bytes 49160 | tf_op jit(solution)/shard_map/ppermute | solution.py:123
  198.9 5.0 %collective-permute-start.28 = (bf16[1024,64]{0,1:T(8,128)(2,1)S(1)}, bf16[1024,64]{0,1:T(8,128)(2,1)S(1)}, u32[]{:S(2)}, u32[]{:S(2)}) collective-permute-start(bf16[1024,64]{0,1:T(8,128)(2,1)S(1)} %bitcast.79), channel_id=1, source_target_pairs={{4,0},{8,4},{12,8},{16,12},{20,16},{24,20},{28,24},{0,28},{5,1},{9... | collective-permute-start | bytes 393224 | tf_op jit(solution)/shard_map/ppermute | solution.py:19
  200.2 8.1 %collective-permute-start.29 = (bf16[1024,64]{0,1:T(8,128)(2,1)S(1)}, bf16[1024,64]{0,1:T(8,128)(2,1)S(1)}, u32[]{:S(2)}, u32[]{:S(2)}) collective-permute-start(bf16[1024,64]{0,1:T(8,128)(2,1)S(1)} %bitcast.80), channel_id=1, source_target_pairs={{24,0},{28,4},{0,8},{4,12},{8,16},{12,20},{16,24},{20,28},{25,1},{... | collective-permute-start | bytes 393224 | tf_op jit(solution)/shard_map/ppermute | solution.py:19
  213.5 9.4 %collective-permute-start.30 = (f32[1024,64]{0,1:T(8,128)}, f32[1024,64]{0,1:T(8,128)}, u32[]{:S(2)}, u32[]{:S(2)}) collective-permute-start(f32[1024,64]{0,1:T(8,128)} %add.286), channel_id=1, source_target_pairs={{28,0},{0,4},{4,8},{8,12},{12,16},{16,20},{20,24},{24,28},{29,1},{... | collective-permute-start | bytes 786440 | tf_op jit(solution)/shard_map/ppermute | solution.py:19
  218.0 6.6 %collective-permute-start.31 = (f32[1024,64]{0,1:T(8,128)S(1)}, f32[1024,64]{0,1:T(8,128)S(1)}, u32[]{:S(2)}, u32[]{:S(2)}) collective-permute-start(f32[1024,64]{0,1:T(8,128)S(1)} %add.288), channel_id=1, source_target_pairs={{8,0},{12,4},{16,8},{20,12},{24,16},{28,20},{0,24},{4,28},{9,1},{1... | collective-permute-start | bytes 786440 | tf_op jit(solution)/shard_map/ppermute | solution.py:19
  226.0 1.1 collective-permute-start.37
  227.2 3.6 %collective-permute-start.38 = (f32[2,128]{1,0:T(2,128)S(1)}, f32[2,128]{1,0:T(2,128)S(1)}, u32[]{:S(2)}, u32[]{:S(2)}) collective-permute-start(f32[2,128]{1,0:T(2,128)S(1)} %maximum_select_fusion.9), channel_id=1, source_target_pairs={{0,2},{1,3},{2,0},{3,1},{4,6},{5,7},{6,4},{7,5},{8,10},{9,11},{10,... | collective-permute-start | bytes 3080 | tf_op jit(solution)/shard_map/ppermute | solution.py:123
  230.8 4.4 %collective-permute-start.39 = (f32[4,128]{1,0:T(4,128)S(1)}, f32[4,128]{1,0:T(4,128)S(1)}, u32[]{:S(2)}, u32[]{:S(2)}) collective-permute-start(f32[4,128]{1,0:T(4,128)S(1)} %maximum_select_fusion.7), channel_id=1, source_target_pairs={{0,4},{4,0},{8,12},{12,8},{16,20},{20,16},{24,28},{28,24},{1,5},{5... | collective-permute-start | bytes 6152 | tf_op jit(solution)/shard_map/ppermute | solution.py:123
  234.1 17.8 %collective-permute-start.32 = (f32[64,64]{0,1:T(8,128)S(1)}, f32[64,64]{0,1:T(8,128)S(1)}, u32[]{:S(2)}, u32[]{:S(2)}) collective-permute-start(f32[64,64]{0,1:T(8,128)S(1)} %fusion.8), channel_id=1, source_target_pairs={{0,1},{1,0},{2,3},{3,2},{4,5},{5,4},{6,7},{7,6},{8,9},{9,8},{10,11... | collective-permute-start | bytes 49160 | tf_op jit(solution)/shard_map/ppermute | solution.py:123
  235.2 18.5 %collective-permute-start.40 = (f32[8,128]{1,0:T(8,128)S(1)}, f32[8,128]{1,0:T(8,128)S(1)}, u32[]{:S(2)}, u32[]{:S(2)}) collective-permute-start(f32[8,128]{1,0:T(8,128)S(1)} %maximum_select_fusion.5), channel_id=1, source_target_pairs={{0,8},{4,12},{8,0},{12,4},{16,24},{20,28},{24,16},{28,20},{1,9},{5... | collective-permute-start | bytes 12296 | tf_op jit(solution)/shard_map/ppermute | solution.py:123
  236.2 1.1 collective-permute-start.42
  237.4 3.5 %collective-permute-start.43 = (f32[64]{0:T(128)S(1)}, f32[64]{0:T(128)S(1)}, u32[]{:S(2)}, u32[]{:S(2)}) collective-permute-start(f32[64]{0:T(128)S(1)} %add.295), channel_id=1, source_target_pairs={{0,2},{1,3},{2,0},{3,1},{4,6},{5,7},{6,4},{7,5},{8,10},{9,11},{10,... | collective-permute-start | bytes 776 | tf_op jit(solution)/shard_map/ppermute | solution.py:123
  240.9 3.5 %collective-permute-start.44 = (f32[64]{0:T(128)S(1)}, f32[64]{0:T(128)S(1)}, u32[]{:S(2)}, u32[]{:S(2)}) collective-permute-start(f32[64]{0:T(128)S(1)} %add.296), channel_id=1, source_target_pairs={{0,4},{4,0},{8,12},{12,8},{16,20},{20,16},{24,28},{28,24},{1,5},{5... | collective-permute-start | bytes 776 | tf_op jit(solution)/shard_map/ppermute | solution.py:123
  244.5 3.5 %collective-permute-start.45 = (f32[64]{0:T(128)S(1)}, f32[64]{0:T(128)S(1)}, u32[]{:S(2)}, u32[]{:S(2)}) collective-permute-start(f32[64]{0:T(128)S(1)} %add.297), channel_id=1, source_target_pairs={{0,8},{4,12},{8,0},{12,4},{16,24},{20,28},{24,16},{28,20},{1,9},{5... | collective-permute-start | bytes 776 | tf_op jit(solution)/shard_map/ppermute | solution.py:123
  248.0 9.9 %collective-permute-start.46 = (f32[64]{0:T(128)S(1)}, f32[64]{0:T(128)S(1)}, u32[]{:S(2)}, u32[]{:S(2)}) collective-permute-start(f32[64]{0:T(128)S(1)} %add.298), channel_id=1, source_target_pairs={{0,16},{4,20},{8,24},{12,28},{16,0},{20,4},{24,8},{28,12},{1,17},{... | collective-permute-start | bytes 776 | tf_op jit(solution)/shard_map/ppermute | solution.py:123
  251.9 4.0 %collective-permute-start.33 = (f32[64,64]{0,1:T(8,128)S(1)}, f32[64,64]{0,1:T(8,128)S(1)}, u32[]{:S(2)}, u32[]{:S(2)}) collective-permute-start(f32[64,64]{0,1:T(8,128)S(1)} %add.290), channel_id=1, source_target_pairs={{0,2},{1,3},{2,0},{3,1},{4,6},{5,7},{6,4},{7,5},{8,10},{9,11},{10,... | collective-permute-start | bytes 49160 | tf_op jit(solution)/shard_map/ppermute | solution.py:123
  253.7 6.2 %collective-permute-start.41 = (f32[16,128]{1,0:T(8,128)S(1)}, f32[16,128]{1,0:T(8,128)S(1)}, u32[]{:S(2)}, u32[]{:S(2)}) collective-permute-start(f32[16,128]{1,0:T(8,128)S(1)} %maximum_select_fusion.3), channel_id=1, source_target_pairs={{0,16},{4,20},{8,24},{12,28},{16,0},{20,4},{24,8},{28,12},{1,17},{... | collective-permute-start | bytes 24584 | tf_op jit(solution)/shard_map/ppermute | solution.py:123
  255.9 3.9 %collective-permute-start.34 = (f32[64,64]{0,1:T(8,128)S(1)}, f32[64,64]{0,1:T(8,128)S(1)}, u32[]{:S(2)}, u32[]{:S(2)}) collective-permute-start(f32[64,64]{0,1:T(8,128)S(1)} %add.291), channel_id=1, source_target_pairs={{0,4},{4,0},{8,12},{12,8},{16,20},{20,16},{24,28},{28,24},{1,5},{5... | collective-permute-start | bytes 49160 | tf_op jit(solution)/shard_map/ppermute | solution.py:123
  259.8 3.9 %collective-permute-start.35 = (f32[64,64]{0,1:T(8,128)S(1)}, f32[64,64]{0,1:T(8,128)S(1)}, u32[]{:S(2)}, u32[]{:S(2)}) collective-permute-start(f32[64,64]{0,1:T(8,128)S(1)} %add.292), channel_id=1, source_target_pairs={{0,8},{4,12},{8,0},{12,4},{16,24},{20,28},{24,16},{28,20},{1,9},{5... | collective-permute-start | bytes 49160 | tf_op jit(solution)/shard_map/ppermute | solution.py:123
  263.7 4.8 %collective-permute-start.36 = (f32[64,64]{0,1:T(8,128)S(1)}, f32[64,64]{0,1:T(8,128)S(1)}, u32[]{:S(2)}, u32[]{:S(2)}) collective-permute-start(f32[64,64]{0,1:T(8,128)S(1)} %add.293), channel_id=1, source_target_pairs={{0,16},{4,20},{8,24},{12,28},{16,0},{20,4},{24,8},{28,12},{1,17},{... | collective-permute-start | bytes 49160 | tf_op jit(solution)/shard_map/ppermute | solution.py:123

commit v2 on v1

--- a/solution.py
+++ b/solution.py
@@ -109,27 +109,35 @@
     return lax.cond(owned, compute_pair, skip_pair)
 
 
-def butterfly(axis, summed, gathered):
+def butterfly(axis, summed_rows, block):
     size = lax.axis_size(axis)
     if size & (size - 1):
-        return (
-            jax.tree.map(lambda v: lax.psum(v, axis), summed),
-            lax.all_gather(gathered, axis, tiled=True),
+        return jnp.concatenate(
+            [
+                lax.psum(block[:summed_rows], axis),
+                lax.all_gather(block[summed_rows:], axis, tiled=True),
+            ]
         )
     index = lax.axis_index(axis)
     step = 1
     while step < size:
         route = [(i, i ^ step) for i in range(size)]
-        other_summed, other_gathered = lax.ppermute((summed, gathered), axis, route)
-        summed = jax.tree.map(jnp.add, summed, other_summed)
+        other = lax.ppermute(block, axis, route)
+        summed = block[:summed_rows] + other[:summed_rows]
+        mine = block[summed_rows:]
+        theirs = other[summed_rows:]
         upper = (index // step) % 2 == 1
         gathered = jnp.where(
-            upper,
-            jnp.concatenate([other_gathered, gathered]),
-            jnp.concatenate([gathered, other_gathered]),
-        )
+            upper, jnp.concatenate([theirs, mine]), jnp.concatenate([mine, theirs])
+        )
+        block = jnp.concatenate([summed, gathered])
         step *= 2
-    return summed, gathered
+    return block
+
+
+def as_rows(vector, lanes=128):
+    pad = (-vector.shape[0]) % lanes
+    return jnp.pad(vector, (0, pad)).reshape(-1, lanes)
 
 
 def hdot(left, right):
@@ -143,11 +151,22 @@
     centred = walk - centre
     local_gram = hdot(centred.T, centred)
     local_drift = jnp.sum(centred, axis=0)
-    summed = (local_gram, jnp.sum(product, axis=0), jnp.sum(vertex_valence))
-    gathered = jnp.concatenate([centre, local_drift])[None, :]
+    summed = jnp.concatenate(
+        [
+            as_rows(local_gram.reshape(-1)),
+            as_rows(jnp.concatenate([jnp.sum(product, axis=0), jnp.sum(vertex_valence)[None]])),
+        ]
+    )
+    summed_rows = summed.shape[0]
+    block = jnp.concatenate([summed, as_rows(jnp.concatenate([centre, local_drift]))])
+    gather_width = block.shape[0] - summed_rows
     for axis in ("narrow", "wide"):
-        summed, gathered = butterfly(axis, summed, gathered)
-    gram_sum, column_sums, total_degree_sum = summed
+        block = butterfly(axis, summed_rows, block)
+    totals = block[:summed_rows].reshape(-1)
+    gram_sum = totals[: vector_count * vector_count].reshape(vector_count, vector_count)
+    column_sums = totals[vector_count * vector_count : vector_count * vector_count + vector_count]
+    total_degree_sum = totals[vector_count * vector_count + vector_count]
+    gathered = block[summed_rows:].reshape(-1, gather_width * 128)
     mean_walk = column_sums / total_degree_sum
     centres = gathered[:, :vector_count] - mean_walk
     drifts = gathered[:, vector_count:]
@@ -181,8 +200,12 @@
 
     units = {0: unit_block}
     weights = {0: start}
+    unit_width = unit_block.shape[1]
+    packed = jnp.concatenate([unit_block, start], axis=1)
     for offset in fetch_offsets:
-        units[offset], weights[offset] = shifted((unit_block, start), "wide", -offset)
+        arrived = shifted(packed, "wide", -offset)
+        units[offset] = arrived[:, :unit_width]
+        weights[offset] = arrived[:, unit_width:]
 
     self_mask = lax.broadcasted_iota(
         jnp.int32, (block_rows, block_rows), 0
@@ -209,10 +232,12 @@
 
     product = row_product(near_tile, start) + parts[0]
     vertex_valence = jnp.sum(near_tile, axis=1, dtype=jnp.float32) + sums[0]
+    part_size = block_rows * vector_count
     for offset in fetch_offsets:
-        returned, returned_sum = shifted((parts[offset], sums[offset]), "wide", offset)
-        product = product + returned
-        vertex_valence = vertex_valence + returned_sum
+        sent = jnp.concatenate([as_rows(parts[offset].reshape(-1)), as_rows(sums[offset])])
+        returned = shifted(sent, "wide", offset).reshape(-1)
+        product = product + returned[:part_size].reshape(block_rows, vector_count)
+        vertex_valence = vertex_valence + returned[part_size : part_size + block_rows]
     basis = orthonormal(product, vertex_valence, total_rows)
 
     for iteration in range(1, ITERS):

time: 283 us -> 235 us (0.83)
  waiting for transfers between devices: 132 us -> 98.6 us
  local copies, waits for them, and re-layouts: 0.49 us -> 18.2 us
  starting transfers between devices: 55.1 us -> 39.1 us
  matrix products: 51.6 us -> 37.2 us
  between operations: 6.76 us -> 3.08 us
    ppermute x35 -> x10, waiting for transfers between devices: 49.6 us -> 19.5 us  [butterfly(): other = lax.ppermute(block, axis, route)]
    ppermute x35 -> x10, starting transfers between devices: 39.4 us -> 24 us  [butterfly(): other = lax.ppermute(block, axis, route)]
    slice x0 -> x20, local copies, waits for them, and re-layouts: none -> 9.52 us  [the longest x2 4.28 us: on_device(): units[offset] = arrived[:, :unit_width]]
    dot_general x4 -> x3, matrix products: 20.6 us -> 15 us  [scores_tile(): lax.dot_general(leftside_block, right_block, (((1,), (1,)), ((), ())), pr...]
    unnamed x11 -> x17, local copies, waits for them, and re-layouts: 0.19 us -> 5 us
    dot_general x8 -> x6, matrix products: 15 us -> 10.3 us  [row_product(): return jnp.dot(affinity, weights, preferred_element_type=jnp.float32)]
    dot_general x6 -> x4, matrix products: 12.5 us -> 8.28 us  [col_product(): lax.dot_general(affinity, weights, (((0,), (0,)), ((), ())), preferred_el...]
    concatenate x0 -> x15, other arithmetic: none -> 4.15 us  [the longest x2 1.44 us: on_device(): jnp.concatenate([as_rows(parts[offset].reshape(-1)), as_rows(sums[offset])])]
  transfers between devices with their start and end apart: 47 -> 18, of which waited for: 31 -> 16; matrix products, arithmetic and copies ran while one was open for 11% -> 11% of each run, Pallas kernels for 0% -> 0%
where the time goes in v2:
time: 235 us; the launch traced here: 234 us
  waiting for transfers between devices  98.6 us (42%)
  starting transfers between devices  39.1 us (17%)
  other arithmetic  37.8 us (16%)
  matrix products  37.2 us (16%)
  local copies, waits for them, and re-layouts  18.2 us (8%)
  between operations  3.08 us (1%)
    ppermute x8, waiting for transfers between devices, shifted(): return lax.ppermute(block, axis, route)  79.1 us
    ppermute x10, starting transfers between devices, butterfly(): other = lax.ppermute(block, axis, route)  24 us
    ppermute x10, waiting for transfers between devices, butterfly(): other = lax.ppermute(block, axis, route)  19.5 us
    ppermute x8, starting transfers between devices, shifted(): return lax.ppermute(block, axis, route)  15.1 us
    dot_general x3, matrix products, scores_tile(): lax.dot_general(leftside_block, right_block, (((1,), (1,)), ((), ())), pr...  15 us
    another operation x6, other arithmetic, orthonormal(): normalizer_coefficient = jnp.linalg.cholesky(gram_matrix)  13 us
    another operation x4, other arithmetic, orthonormal(): jax.scipy.linalg.solve_triangular(normalizer_coefficient, displaced_entri...  11.1 us
    dot_general x6, matrix products, row_product(): return jnp.dot(affinity, weights, preferred_element_type=jnp.float32)  10.3 us
  transfers between devices with their start and end apart: 18, of which 16 were waited for; matrix products, arithmetic and copies ran while one was open for 11% of the time, Pallas kernels for 0%

profile of v2, /device:TPU:0, one launch (start us, length us, event | category | flops | bytes accessed | tf_op | source)
XLA Modules:
  0.0 234.0 jit_solution(13597805401887399150)
XLA Ops:
  0.6 1.7 copy.41
  3.2 1.2 copy-done
  4.3 1.3 pad_maximum_fusion
  5.7 6.0 %collective-permute-start = (bf16[1024,832]{0,1:T(8,128)(2,1)}, bf16[1024,832]{0,1:T(8,128)(2,1)}, u32[]{:S(2)}, u32[]{:S(2)}) collective-permute-start(bf16[1024,832]{0,1:T(8,128)(2,1)} %pad_maximum_fusion), channel_id=1, source_target_pairs={{4,0},{8,4},{12,8},{16,12},{20,16},{24,20},{28,24},{0,28},{5,1},{9... | collective-permute-start | bytes 5111816 | tf_op jit(solution)/shard_map/ppermute | solution.py:19
  14.3 4.1 %convert_reduce_fusion.6 = (f32[1024]{0:T(1024)S(1)}, bf16[1024,1024]{0,1:T(8,128)(2,1)S(1)}) fusion(bf16[1024,768]{0,1:T(8,128)(2,1)} %copy-done), kind=kOutput, calls=%fused_computation.9 | convolution fusion | flops 1616903168 | bytes 3674112 | tf_op jit(solution)/shard_map/dot_general | solution.py:54
  18.4 31.3 %collective-permute-done = bf16[1024,832]{0,1:T(8,128)(2,1)} collective-permute-done((bf16[1024,832]{0,1:T(8,128)(2,1)}, bf16[1024,832]{0,1:T(8,128)(2,1)}, u32[]{:S(2)}, u32[]{:S(2)}) %collective-permute-start) | collective-permute-done | bytes 1703968 | tf_op jit(solution)/shard_map/ppermute | solution.py:19
  49.6 1.5 slice.172
  51.2 1.2 slice.173
  52.3 33.5 %collective-permute-done.1 = bf16[1024,832]{0,1:T(8,128)(2,1)} collective-permute-done((bf16[1024,832]{0,1:T(8,128)(2,1)}, bf16[1024,832]{0,1:T(8,128)(2,1)}, u32[]{:S(2)}, u32[]{:S(2)}) %collective-permute-start.1) | collective-permute-done | bytes 1703968 | tf_op jit(solution)/shard_map/ppermute | solution.py:19
  85.9 2.8 %slice.174 = bf16[1024,768]{0,1:T(8,128)(2,1)} slice(bf16[1024,832]{0,1:T(8,128)(2,1)} %collective-permute-done.1), slice={[0:1024], [0:768]} | slice | bytes 3145728 | tf_op jit(solution)/shard_map/slice | solution.py:207
  88.6 0.9 slice.175
  89.6 1.7 conditional.6
  89.6 1.6 broadcast.124
  91.9 9.9 %conditional.8 = (bf16[1024,1024]{1,0:T(8,128)(2,1)}, f32[1024,64]{0,1:T(8,128)S(1)}, f32[1024]{0:T(1024)S(1)}, f32[1024,64]{0,1:T(8,128)S(1)}, f32[1024]{0:T(1024)S(1)}) conditional(s32[]{:T(128)} %convert_element_type.59, () %tuple.62, (bf16[1024,768]{0,1:T(8,128)(2,1)}, bf16[1024,768]{0,1:T(8,128)(2,1)}, bf16[1024,64]{0,1:T(8,128)(2,1)S(1)}, ...), branch_computations={%region_12.13_spmd, %region_13.16_spmd} | conditional | flops 1884289024 | bytes 10231848 | solution.py:95
  91.9 5.5 %convert_reduce_fusion.4 = (f32[1024]{0:T(1024)S(1)}, f32[1024]{0:T(1024)S(1)}, bf16[1024,1024]{1,0:T(8,128)(2,1)}) fusion(bf16[1024,768]{0,1:T(8,128)(2,1)} %get-tuple-element.151, bf16[1024,768]{0,1:T(8,128)(2,1)} %get-tuple-element.152), kind=kOutput, calls=%fused_computation.6 | convolution fusion | flops 1615853568 | bytes 5251072 | tf_op jit(solution)/shard_map/cond/branch_1_fun/dot_general | solution.py:54
  97.4 2.3 %fusion.54 = f32[1024,64]{0,1:T(8,128)S(1)} fusion(bf16[1024,1024]{1,0:T(8,128)(2,1)} %get-tuple-element.205, bf16[1024,64]{0,1:T(8,128)(2,1)S(1)} %get-tuple-element.153), kind=kOutput, calls=%fused_computation.142 | convolution fusion | flops 134217728 | bytes 2490368 | tf_op jit(solution)/shard_map/cond/branch_1_fun/dot_general | solution.py:61
  99.8 2.1 fusion.55
  102.6 1.0 add.205
  104.6 9.9 %conditional.7 = (bf16[1024,1024]{1,0:T(8,128)(2,1)}, f32[1024,64]{0,1:T(8,128)S(1)}, f32[1024]{0:T(1024)S(1)}, f32[1024,64]{0,1:T(8,128)S(1)}, f32[1024]{0:T(1024)S(1)}) conditional(s32[]{:T(128)} %convert_element_type.58, () %tuple.60, (bf16[1024,768]{0,1:T(8,128)(2,1)}, bf16[1024,768]{0,1:T(8,128)(2,1)}, bf16[1024,64]{0,1:T(8,128)(2,1)S(1)}, ...), branch_computations={%region_7.8_spmd, %region_8.11_spmd} | conditional | flops 1884289024 | bytes 10231848 | solution.py:95
  104.6 5.5 %convert_reduce_fusion.2 = (f32[1024]{0:T(1024)S(1)}, f32[1024]{0:T(1024)S(1)}, bf16[1024,1024]{1,0:T(8,128)(2,1)}) fusion(bf16[1024,768]{0,1:T(8,128)(2,1)} %get-tuple-element.147, bf16[1024,768]{0,1:T(8,128)(2,1)} %get-tuple-element.148), kind=kOutput, calls=%fused_computation.3 | convolution fusion | flops 1615853568 | bytes 5251072 | tf_op jit(solution)/shard_map/cond/branch_1_fun/dot_general | solution.py:54
  110.1 2.3 %fusion.52 = f32[1024,64]{0,1:T(8,128)S(1)} fusion(bf16[1024,1024]{1,0:T(8,128)(2,1)} %get-tuple-element.195, bf16[1024,64]{0,1:T(8,128)(2,1)S(1)} %get-tuple-element.149), kind=kOutput, calls=%fused_computation.140 | convolution fusion | flops 134217728 | bytes 2490368 | tf_op jit(solution)/shard_map/cond/branch_1_fun/dot_general | solution.py:61
  112.4 2.1 fusion.53
  116.3 1.7 collective-permute-start.3
  118.6 1.0 slice.176
  119.9 3.2 %collective-permute-done.3 = f32[520,128]{1,0:T(8,128)} collective-permute-done((f32[520,128]{1,0:T(8,128)}, f32[520,128]{1,0:T(8,128)}, u32[]{:S(2)}, u32[]{:S(2)}) %collective-permute-start.3) | collective-permute-done | bytes 266272 | tf_op jit(solution)/shard_map/ppermute | solution.py:19
  123.1 1.0 slice.177
  124.4 1.3 broadcast_multiply_fusion
  125.7 1.2 fusion.39
  128.9 3.4 %collective-permute-start.4 = (f32[34,128]{1,0:T(8,128)S(1)}, f32[34,128]{1,0:T(8,128)S(1)}, u32[]{:S(2)}, u32[]{:S(2)}) collective-permute-start(f32[34,128]{1,0:T(8,128)S(1)} %pad_maximum_fusion.7), channel_id=1, source_target_pairs={{0,1},{1,0},{2,3},{3,2},{4,5},{5,4},{6,7},{7,6},{8,9},{9,8},{10,11... | collective-permute-start | bytes 52232 | tf_op jit(solution)/shard_map/ppermute | solution.py:125
  132.4 0.8 collective-permute-done.4
  133.3 4.4 %collective-permute-start.5 = (f32[35,128]{1,0:T(8,128)S(1)}, f32[35,128]{1,0:T(8,128)S(1)}, u32[]{:S(2)}, u32[]{:S(2)}) collective-permute-start(f32[35,128]{1,0:T(8,128)S(1)} %pad_maximum_fusion.8), channel_id=1, source_target_pairs={{0,2},{1,3},{2,0},{3,1},{4,6},{5,7},{6,4},{7,5},{8,10},{9,11},{10,... | collective-permute-start | bytes 53768 | tf_op jit(solution)/shard_map/ppermute | solution.py:125
  137.7 1.8 collective-permute-done.5
  139.5 3.6 %collective-permute-start.6 = (f32[37,128]{1,0:T(8,128)S(1)}, f32[37,128]{1,0:T(8,128)S(1)}, u32[]{:S(2)}, u32[]{:S(2)}) collective-permute-start(f32[37,128]{1,0:T(8,128)S(1)} %pad_maximum_fusion.9), channel_id=1, source_target_pairs={{0,4},{4,0},{8,12},{12,8},{16,20},{20,16},{24,28},{28,24},{1,5},{5... | collective-permute-start | bytes 56840 | tf_op jit(solution)/shard_map/ppermute | solution.py:125
  143.1 1.8 collective-permute-done.6
  145.5 3.3 %collective-permute-done.7 = f32[41,128]{1,0:T(8,128)S(1)} collective-permute-done((f32[41,128]{1,0:T(8,128)S(1)}, f32[41,128]{1,0:T(8,128)S(1)}, u32[]{:S(2)}, u32[]{:S(2)}) %collective-permute-start.7) | collective-permute-done | bytes 21024 | tf_op jit(solution)/shard_map/ppermute | solution.py:125
  148.8 2.6 %collective-permute-start.8 = (f32[49,128]{1,0:T(8,128)S(1)}, f32[49,128]{1,0:T(8,128)S(1)}, u32[]{:S(2)}, u32[]{:S(2)}) collective-permute-start(f32[49,128]{1,0:T(8,128)S(1)} %pad_maximum_fusion.3), channel_id=1, source_target_pairs={{0,16},{4,20},{8,24},{12,28},{16,0},{20,4},{24,8},{28,12},{1,17},{... | collective-permute-start | bytes 75272 | tf_op jit(solution)/shard_map/ppermute | solution.py:125
  151.4 2.2 collective-permute-done.8
  155.8 5.8 %cholesky.44 = f32[64,64]{1,0:T(8,128)S(1)} custom-call(f32[64,64]{1,0:T(8,128)S(1)} %fusion.25), custom_call_target="Cholesky" | custom-call | tf_op jit(solution)/shard_map/jit(cholesky)/cholesky | solution.py:176
  162.9 4.9 %custom-call.6 = f32[1,64,64]{1,2,0:T(8,128)S(1)} custom-call(f32[1,64,64]{2,1,0:T(8,128)S(1)} %fusion.20), custom_call_target="InvertDiagBlocksLowerTriangular" | custom-call | tf_op jit(solution)/shard_map/jit(_solve_triangular)/triangular_solve | solution.py:177
  168.3 5.5 %collective-permute-start.9 = (bf16[1024,64]{0,1:T(8,128)(2,1)S(1)}, bf16[1024,64]{0,1:T(8,128)(2,1)S(1)}, u32[]{:S(2)}, u32[]{:S(2)}) collective-permute-start(bf16[1024,64]{0,1:T(8,128)(2,1)S(1)} %bitcast.100), channel_id=1, source_target_pairs={{4,0},{8,4},{12,8},{16,12},{20,16},{24,20},{28,24},{0,28},{5,1},{9... | collective-permute-start | bytes 393224 | tf_op jit(solution)/shard_map/ppermute | solution.py:19
  173.8 2.5 %collective-permute-done.9 = bf16[1024,64]{0,1:T(8,128)(2,1)S(1)} collective-permute-done((bf16[1024,64]{0,1:T(8,128)(2,1)S(1)}, bf16[1024,64]{0,1:T(8,128)(2,1)S(1)}, u32[]{:S(2)}, u32[]{:S(2)}) %collective-permute-start.9) | collective-permute-done | bytes 131104 | tf_op jit(solution)/shard_map/ppermute | solution.py:19
  176.4 4.2 %collective-permute-done.10 = bf16[1024,64]{0,1:T(8,128)(2,1)S(1)} collective-permute-done((bf16[1024,64]{0,1:T(8,128)(2,1)S(1)}, bf16[1024,64]{0,1:T(8,128)(2,1)S(1)}, u32[]{:S(2)}, u32[]{:S(2)}) %collective-permute-start.10) | collective-permute-done | bytes 131104 | tf_op jit(solution)/shard_map/ppermute | solution.py:19
  180.6 4.4 %conditional.11 = (f32[1024,64]{0,1:T(8,128)S(1)}, f32[1024,64]{0,1:T(8,128)S(1)}) conditional(s32[]{:T(128)} %convert_element_type.59, () %tuple.68, (bf16[1024,1024]{1,0:T(8,128)(2,1)}, bf16[1024,64]{0,1:T(8,128)(2,1)S(1)}, bf16[1024,64]{0,1:T(8,128)(2,1)S(1)}) %tuple.69), branch_computations={%region_27.30_spmd, %region_28.31_spmd} | conditional | flops 268435456 | bytes 4980752 | solution.py:109
  180.6 2.3 %fusion.48 = f32[1024,64]{0,1:T(8,128)S(1)} fusion(bf16[1024,1024]{1,0:T(8,128)(2,1)} %get-tuple-element.62, bf16[1024,64]{0,1:T(8,128)(2,1)S(1)} %get-tuple-element.162), kind=kOutput, calls=%fused_computation.136 | convolution fusion | flops 134217728 | bytes 2490368 | tf_op jit(solution)/shard_map/cond/branch_1_fun/dot_general | solution.py:61
  182.9 2.1 fusion.49
  185.0 0.7 add.230
  185.7 4.4 %conditional.10 = (f32[1024,64]{0,1:T(8,128)S(1)}, f32[1024,64]{0,1:T(8,128)S(1)}) conditional(s32[]{:T(128)} %convert_element_type.58, () %tuple.66, (bf16[1024,1024]{1,0:T(8,128)(2,1)}, bf16[1024,64]{0,1:T(8,128)(2,1)S(1)}, bf16[1024,64]{0,1:T(8,128)(2,1)S(1)}) %tuple.120), branch_computations={%region_25.28_spmd, %region_26.29_spmd} | conditional | flops 268435456 | bytes 4980752 | solution.py:109
  185.7 2.3 %fusion.46 = f32[1024,64]{0,1:T(8,128)S(1)} fusion(bf16[1024,1024]{1,0:T(8,128)(2,1)} %get-tuple-element.59, bf16[1024,64]{0,1:T(8,128)(2,1)S(1)} %get-tuple-element.159), kind=kOutput, calls=%fused_computation.134 | convolution fusion | flops 134217728 | bytes 2490368 | tf_op jit(solution)/shard_map/cond/branch_1_fun/dot_general | solution.py:61
  188.1 2.1 fusion.47
  190.2 1.8 collective-permute-start.12
  192.5 4.4 %collective-permute-done.11 = f32[1024,64]{0,1:T(8,128)} collective-permute-done((f32[1024,64]{0,1:T(8,128)}, f32[1024,64]{0,1:T(8,128)}, u32[]{:S(2)}, u32[]{:S(2)}) %collective-permute-start.11) | collective-permute-done | bytes 262176 | tf_op jit(solution)/shard_map/ppermute | solution.py:19
  196.9 1.1 fusion.40
  199.5 1.2 collective-permute-done.13
  200.7 2.3 collective-permute-start.14
  203.0 1.8 collective-permute-done.14
  204.8 3.3 %collective-permute-start.15 = (f32[37,128]{1,0:T(8,128)S(1)}, f32[37,128]{1,0:T(8,128)S(1)}, u32[]{:S(2)}, u32[]{:S(2)}) collective-permute-start(f32[37,128]{1,0:T(8,128)S(1)} %pad_maximum_fusion.12), channel_id=1, source_target_pairs={{0,4},{4,0},{8,12},{12,8},{16,20},{20,16},{24,28},{28,24},{1,5},{5... | collective-permute-start | bytes 56840 | tf_op jit(solution)/shard_map/ppermute | solution.py:125
  208.1 1.8 collective-permute-done.15
  209.9 0.9 collective-permute-start.16
  210.8 3.0 %collective-permute-done.16 = f32[41,128]{1,0:T(8,128)S(1)} collective-permute-done((f32[41,128]{1,0:T(8,128)S(1)}, f32[41,128]{1,0:T(8,128)S(1)}, u32[]{:S(2)}, u32[]{:S(2)}) %collective-permute-start.16) | collective-permute-done | bytes 21024 | tf_op jit(solution)/shard_map/ppermute | solution.py:125
  213.8 2.9 %collective-permute-start.17 = (f32[49,128]{1,0:T(8,128)S(1)}, f32[49,128]{1,0:T(8,128)S(1)}, u32[]{:S(2)}, u32[]{:S(2)}) collective-permute-start(f32[49,128]{1,0:T(8,128)S(1)} %pad_maximum_fusion.4), channel_id=1, source_target_pairs={{0,16},{4,20},{8,24},{12,28},{16,0},{20,4},{24,8},{28,12},{1,17},{... | collective-permute-start | bytes 75272 | tf_op jit(solution)/shard_map/ppermute | solution.py:125
  216.7 1.9 collective-permute-done.17
  220.8 5.8 %cholesky.55 = f32[64,64]{1,0:T(8,128)S(1)} custom-call(f32[64,64]{1,0:T(8,128)S(1)} %fusion.23), custom_call_target="Cholesky" | custom-call | tf_op jit(solution)/shard_map/jit(cholesky)/cholesky | solution.py:176
  228.0 4.9 %custom-call.7 = f32[1,64,64]{1,2,0:T(8,128)S(1)} custom-call(f32[1,64,64]{2,1,0:T(8,128)S(1)} %fusion.21), custom_call_target="InvertDiagBlocksLowerTriangular" | custom-call | tf_op jit(solution)/shard_map/jit(_solve_triangular)/triangular_solve | solution.py:177
  232.9 1.2 convolution_bitcast_fusion
  (131 shorter events, 19.2 us)
Async XLA Ops:
  2.4 2.0 copy-start.2
  3.2 1.2 copy-start
  4.3 7.3 %copy-start.7 = (s32[32,3]{0,1:T(4,128)S(1)}, s32[32,3]{0,1:T(4,128)}, u32[]{:S(2)}) copy-start(s32[32,3]{0,1:T(4,128)} %param.20) | copy-start | bytes 1156
  5.7 43.9 %collective-permute-start = (bf16[1024,832]{0,1:T(8,128)(2,1)}, bf16[1024,832]{0,1:T(8,128)(2,1)}, u32[]{:S(2)}, u32[]{:S(2)}) collective-permute-start(bf16[1024,832]{0,1:T(8,128)(2,1)} %pad_maximum_fusion), channel_id=1, source_target_pairs={{4,0},{8,4},{12,8},{16,12},{20,16},{24,20},{28,24},{0,28},{5,1},{9... | collective-permute-start | bytes 5111816 | tf_op jit(solution)/shard_map/ppermute | solution.py:19
  11.7 74.2 %collective-permute-start.1 = (bf16[1024,832]{0,1:T(8,128)(2,1)}, bf16[1024,832]{0,1:T(8,128)(2,1)}, u32[]{:S(2)}, u32[]{:S(2)}) collective-permute-start(bf16[1024,832]{0,1:T(8,128)(2,1)} %pad_maximum_fusion), channel_id=1, source_target_pairs={{24,0},{28,4},{0,8},{4,12},{8,16},{12,20},{16,24},{20,28},{25,1},{... | collective-permute-start | bytes 5111816 | tf_op jit(solution)/shard_map/ppermute | solution.py:19
  51.1 38.4 %copy-start.3 = (bf16[1024,768]{0,1:T(8,128)(2,1)}, bf16[1024,768]{0,1:T(8,128)(2,1)S(1)}, u32[]{:S(2)}) copy-start(bf16[1024,768]{0,1:T(8,128)(2,1)S(1)} %slice.172) | copy-start | bytes 4718596
  51.1 38.4 %copy-start.1 = (bf16[1024,768]{0,1:T(8,128)(2,1)S(1)}, bf16[1024,768]{0,1:T(8,128)(2,1)}, u32[]{:S(2)}) copy-start(bf16[1024,768]{0,1:T(8,128)(2,1)} %copy-done) | copy-start | bytes 4718596
  91.2 0.7 copy-start.5
  101.9 0.7 copy-start.4
  104.6 13.9 %collective-permute-start.2 = (f32[520,128]{1,0:T(8,128)}, f32[520,128]{1,0:T(8,128)}, u32[]{:S(2)}, u32[]{:S(2)}) collective-permute-start(f32[520,128]{1,0:T(8,128)} %pad_maximum_fusion.1), channel_id=1, source_target_pairs={{28,0},{0,4},{4,8},{8,12},{12,16},{16,20},{20,24},{24,28},{29,1},{... | collective-permute-start | bytes 798728 | tf_op jit(solution)/shard_map/ppermute | solution.py:19
  114.5 0.7 copy-start.6
  116.3 6.7 %collective-permute-start.3 = (f32[520,128]{1,0:T(8,128)}, f32[520,128]{1,0:T(8,128)}, u32[]{:S(2)}, u32[]{:S(2)}) collective-permute-start(f32[520,128]{1,0:T(8,128)} %pad_maximum_fusion.2), channel_id=1, source_target_pairs={{8,0},{12,4},{16,8},{20,12},{24,16},{28,20},{0,24},{4,28},{9,1},{1... | collective-permute-start | bytes 798728 | tf_op jit(solution)/shard_map/ppermute | solution.py:19
  128.9 4.3 %collective-permute-start.4 = (f32[34,128]{1,0:T(8,128)S(1)}, f32[34,128]{1,0:T(8,128)S(1)}, u32[]{:S(2)}, u32[]{:S(2)}) collective-permute-start(f32[34,128]{1,0:T(8,128)S(1)} %pad_maximum_fusion.7), channel_id=1, source_target_pairs={{0,1},{1,0},{2,3},{3,2},{4,5},{5,4},{6,7},{7,6},{8,9},{9,8},{10,11... | collective-permute-start | bytes 52232 | tf_op jit(solution)/shard_map/ppermute | solution.py:125
  133.3 6.2 %collective-permute-start.5 = (f32[35,128]{1,0:T(8,128)S(1)}, f32[35,128]{1,0:T(8,128)S(1)}, u32[]{:S(2)}, u32[]{:S(2)}) collective-permute-start(f32[35,128]{1,0:T(8,128)S(1)} %pad_maximum_fusion.8), channel_id=1, source_target_pairs={{0,2},{1,3},{2,0},{3,1},{4,6},{5,7},{6,4},{7,5},{8,10},{9,11},{10,... | collective-permute-start | bytes 53768 | tf_op jit(solution)/shard_map/ppermute | solution.py:125
  139.5 5.3 %collective-permute-start.6 = (f32[37,128]{1,0:T(8,128)S(1)}, f32[37,128]{1,0:T(8,128)S(1)}, u32[]{:S(2)}, u32[]{:S(2)}) collective-permute-start(f32[37,128]{1,0:T(8,128)S(1)} %pad_maximum_fusion.9), channel_id=1, source_target_pairs={{0,4},{4,0},{8,12},{12,8},{16,20},{20,16},{24,28},{28,24},{1,5},{5... | collective-permute-start | bytes 56840 | tf_op jit(solution)/shard_map/ppermute | solution.py:125
  144.9 3.9 %collective-permute-start.7 = (f32[41,128]{1,0:T(8,128)S(1)}, f32[41,128]{1,0:T(8,128)S(1)}, u32[]{:S(2)}, u32[]{:S(2)}) collective-permute-start(f32[41,128]{1,0:T(8,128)S(1)} %pad_maximum_fusion.5), channel_id=1, source_target_pairs={{0,8},{4,12},{8,0},{12,4},{16,24},{20,28},{24,16},{28,20},{1,9},{5... | collective-permute-start | bytes 62984 | tf_op jit(solution)/shard_map/ppermute | solution.py:125
  148.8 4.8 %collective-permute-start.8 = (f32[49,128]{1,0:T(8,128)S(1)}, f32[49,128]{1,0:T(8,128)S(1)}, u32[]{:S(2)}, u32[]{:S(2)}) collective-permute-start(f32[49,128]{1,0:T(8,128)S(1)} %pad_maximum_fusion.3), channel_id=1, source_target_pairs={{0,16},{4,20},{8,24},{12,28},{16,0},{20,4},{24,8},{28,12},{1,17},{... | collective-permute-start | bytes 75272 | tf_op jit(solution)/shard_map/ppermute | solution.py:125
  168.3 8.0 %collective-permute-start.9 = (bf16[1024,64]{0,1:T(8,128)(2,1)S(1)}, bf16[1024,64]{0,1:T(8,128)(2,1)S(1)}, u32[]{:S(2)}, u32[]{:S(2)}) collective-permute-start(bf16[1024,64]{0,1:T(8,128)(2,1)S(1)} %bitcast.100), channel_id=1, source_target_pairs={{4,0},{8,4},{12,8},{16,12},{20,16},{24,20},{28,24},{0,28},{5,1},{9... | collective-permute-start | bytes 393224 | tf_op jit(solution)/shard_map/ppermute | solution.py:19
  173.8 6.8 %collective-permute-start.10 = (bf16[1024,64]{0,1:T(8,128)(2,1)S(1)}, bf16[1024,64]{0,1:T(8,128)(2,1)S(1)}, u32[]{:S(2)}, u32[]{:S(2)}) collective-permute-start(bf16[1024,64]{0,1:T(8,128)(2,1)S(1)} %bitcast.101), channel_id=1, source_target_pairs={{24,0},{28,4},{0,8},{4,12},{8,16},{12,20},{16,24},{20,28},{25,1},{... | collective-permute-start | bytes 393224 | tf_op jit(solution)/shard_map/ppermute | solution.py:19
  185.7 11.2 %collective-permute-start.11 = (f32[1024,64]{0,1:T(8,128)}, f32[1024,64]{0,1:T(8,128)}, u32[]{:S(2)}, u32[]{:S(2)}) collective-permute-start(f32[1024,64]{0,1:T(8,128)} %add.230), channel_id=1, source_target_pairs={{28,0},{0,4},{4,8},{8,12},{12,16},{16,20},{20,24},{24,28},{29,1},{... | collective-permute-start | bytes 786440 | tf_op jit(solution)/shard_map/ppermute | solution.py:19
  190.2 6.7 %collective-permute-start.12 = (f32[1024,64]{0,1:T(8,128)S(1)}, f32[1024,64]{0,1:T(8,128)S(1)}, u32[]{:S(2)}, u32[]{:S(2)}) collective-permute-start(f32[1024,64]{0,1:T(8,128)S(1)} %add.232), channel_id=1, source_target_pairs={{8,0},{12,4},{16,8},{20,12},{24,16},{28,20},{0,24},{4,28},{9,1},{1... | collective-permute-start | bytes 786440 | tf_op jit(solution)/shard_map/ppermute | solution.py:19
  199.5 1.2 collective-permute-start.13
  200.7 4.0 %collective-permute-start.14 = (f32[35,128]{1,0:T(8,128)S(1)}, f32[35,128]{1,0:T(8,128)S(1)}, u32[]{:S(2)}, u32[]{:S(2)}) collective-permute-start(f32[35,128]{1,0:T(8,128)S(1)} %pad_maximum_fusion.11), channel_id=1, source_target_pairs={{0,2},{1,3},{2,0},{3,1},{4,6},{5,7},{6,4},{7,5},{8,10},{9,11},{10,... | collective-permute-start | bytes 53768 | tf_op jit(solution)/shard_map/ppermute | solution.py:125
  204.8 5.1 %collective-permute-start.15 = (f32[37,128]{1,0:T(8,128)S(1)}, f32[37,128]{1,0:T(8,128)S(1)}, u32[]{:S(2)}, u32[]{:S(2)}) collective-permute-start(f32[37,128]{1,0:T(8,128)S(1)} %pad_maximum_fusion.12), channel_id=1, source_target_pairs={{0,4},{4,0},{8,12},{12,8},{16,20},{20,16},{24,28},{28,24},{1,5},{5... | collective-permute-start | bytes 56840 | tf_op jit(solution)/shard_map/ppermute | solution.py:125
  209.9 3.9 %collective-permute-start.16 = (f32[41,128]{1,0:T(8,128)S(1)}, f32[41,128]{1,0:T(8,128)S(1)}, u32[]{:S(2)}, u32[]{:S(2)}) collective-permute-start(f32[41,128]{1,0:T(8,128)S(1)} %pad_maximum_fusion.6), channel_id=1, source_target_pairs={{0,8},{4,12},{8,0},{12,4},{16,24},{20,28},{24,16},{28,20},{1,9},{5... | collective-permute-start | bytes 62984 | tf_op jit(solution)/shard_map/ppermute | solution.py:125
  213.8 4.8 %collective-permute-start.17 = (f32[49,128]{1,0:T(8,128)S(1)}, f32[49,128]{1,0:T(8,128)S(1)}, u32[]{:S(2)}, u32[]{:S(2)}) collective-permute-start(f32[49,128]{1,0:T(8,128)S(1)} %pad_maximum_fusion.4), channel_id=1, source_target_pairs={{0,16},{4,20},{8,24},{12,28},{16,0},{20,4},{24,8},{28,12},{1,17},{... | collective-permute-start | bytes 75272 | tf_op jit(solution)/shard_map/ppermute | solution.py:125

commit v3 on v2

--- a/solution.py
+++ b/solution.py
@@ -6,6 +6,7 @@
 import jax.numpy as jnp
 from jax import lax
 from jax.sharding import PartitionSpec as P
+from jax.experimental import pallas as pl
 
 ITERS = 2
 
@@ -67,18 +68,114 @@
     )
 
 
-def first_pass(owned, left_unit, right_unit, left_weights, right_weights):
-    block_rows = left_unit.shape[0]
+def pair_kernel(left_ref, right_ref, left_t_ref, right_w_ref, tile_ref, row_ref, col_ref):
+    step = pl.program_id(0)
+    entries = lax.dot_general(
+        left_ref[...], right_ref[...], (((1,), (1,)), ((), ())), preferred_element_type=jnp.float32
+    )
+    affinity = jnp.exp(entries / kernel_width_factor).astype(jnp.bfloat16)
+    tile_ref[...] = affinity
+    part = jnp.dot(affinity, right_w_ref[...], preferred_element_type=jnp.float32)
+
+    @pl.when(step == 0)
+    def _():
+        row_ref[...] = part
+
+    @pl.when(step > 0)
+    def _():
+        row_ref[...] += part
+
+    col_ref[...] = jnp.dot(left_t_ref[...], affinity, preferred_element_type=jnp.float32)
+
+
+def apply_kernel(tile_ref, left_t_ref, right_w_ref, row_ref, col_ref):
+    step = pl.program_id(0)
+    affinity = tile_ref[...]
+    part = jnp.dot(affinity, right_w_ref[...], preferred_element_type=jnp.float32)
+
+    @pl.when(step == 0)
+    def _():
+        row_ref[...] = part
+
+    @pl.when(step > 0)
+    def _():
+        row_ref[...] += part
+
+    col_ref[...] = jnp.dot(left_t_ref[...], affinity, preferred_element_type=jnp.float32)
+
+
+COLUMN_CHUNK = 256
+
+
+def pair_terms(left_packed, right_packed, left_t, right_w, block_rows):
+    unit_width = left_packed.shape[1]
+    width = right_w.shape[1]
+    chunk = min(COLUMN_CHUNK, block_rows)
+    return pl.pallas_call(
+        pair_kernel,
+        grid=(block_rows // chunk,),
+        in_specs=[
+            pl.BlockSpec((block_rows, unit_width), lambda j: (0, 0)),
+            pl.BlockSpec((chunk, unit_width), lambda j: (j, 0)),
+            pl.BlockSpec((width, block_rows), lambda j: (0, 0)),
+            pl.BlockSpec((chunk, width), lambda j: (j, 0)),
+        ],
+        out_specs=[
+            pl.BlockSpec((block_rows, chunk), lambda j: (0, j)),
+            pl.BlockSpec((block_rows, width), lambda j: (0, 0)),
+            pl.BlockSpec((width, chunk), lambda j: (0, j)),
+        ],
+        out_shape=[
+            jax.ShapeDtypeStruct((block_rows, block_rows), jnp.bfloat16),
+            jax.ShapeDtypeStruct((block_rows, width), jnp.float32),
+            jax.ShapeDtypeStruct((width, block_rows), jnp.float32),
+        ],
+    )(left_packed, right_packed, left_t, right_w)
+
+
+def apply_terms(affinity, left_t, right_w):
+    block_rows = affinity.shape[0]
+    width = right_w.shape[1]
+    chunk = min(COLUMN_CHUNK, block_rows)
+    return pl.pallas_call(
+        apply_kernel,
+        grid=(block_rows // chunk,),
+        in_specs=[
+            pl.BlockSpec((block_rows, chunk), lambda j: (0, j)),
+            pl.BlockSpec((width, block_rows), lambda j: (0, 0)),
+            pl.BlockSpec((chunk, width), lambda j: (j, 0)),
+        ],
+        out_specs=[
+            pl.BlockSpec((block_rows, width), lambda j: (0, 0)),
+            pl.BlockSpec((width, chunk), lambda j: (0, j)),
+        ],
+        out_shape=[
+            jax.ShapeDtypeStruct((block_rows, width), jnp.float32),
+            jax.ShapeDtypeStruct((width, block_rows), jnp.float32),
+        ],
+    )(affinity, left_t, right_w)
+
+
+def with_ones(weights):
+    rows, count = weights.shape
+    ones = jnp.ones((rows, 1), weights.dtype)
+    pad = (-(count + 1)) % 128
+    return jnp.concatenate([weights, ones, jnp.zeros((rows, pad), weights.dtype)], axis=1)
+
+
+def first_pass(owned, left_packed, right_packed, left_weights, right_weights, block_rows):
     vector_count = left_weights.shape[1]
 
     def compute_pair():
-        affinity = scores_tile(left_unit, right_unit)
+        affinity, row_wide, col_wide = pair_terms(
+            left_packed, right_packed, with_ones(left_weights).T, with_ones(right_weights), block_rows
+        )
         return (
             affinity,
-            row_product(affinity, right_weights),
-            jnp.sum(affinity, axis=1, dtype=jnp.float32),
-            col_product(affinity, left_weights),
-            jnp.sum(affinity, axis=0, dtype=jnp.float32),
+            row_wide[:, :vector_count],
+            row_wide[:, vector_count],
+            col_wide[:vector_count].T,
+            col_wide[vector_count],
         )
 
     def skip_pair():
@@ -100,7 +197,8 @@
     vector_count = left_weights.shape[1]
 
     def compute_pair():
-        return (row_product(affinity, right_weights), col_product(affinity, left_weights))
+        row_part, col_t = apply_terms(affinity, left_weights.T, right_weights)
+        return (row_part, col_t.T)
 
     def skip_pair():
         zero_part = jnp.zeros((block_rows, vector_count), jnp.float32)
@@ -198,14 +296,17 @@
         own_row = lax.dynamic_slice_in_dim(neighbours, block_at(left), 1, 0)[0]
         owned_list.append(jnp.any(own_row == block_at(right)))
 
-    units = {0: unit_block}
+    unit_width = unit_block.shape[1]
+    vector_count = start.shape[1]
+    packed = jnp.concatenate([unit_block, as_rows(start.reshape(-1), unit_width)])
+    units = {0: packed}
     weights = {0: start}
-    unit_width = unit_block.shape[1]
-    packed = jnp.concatenate([unit_block, start], axis=1)
     for offset in fetch_offsets:
         arrived = shifted(packed, "wide", -offset)
-        units[offset] = arrived[:, :unit_width]
-        weights[offset] = arrived[:, unit_width:]
+        units[offset] = arrived
+        weights[offset] = (
+            arrived[block_rows:].reshape(-1)[: block_rows * vector_count].reshape(block_rows, vector_count)
+        )
 
     self_mask = lax.broadcasted_iota(
         jnp.int32, (block_rows, block_rows), 0
@@ -214,7 +315,6 @@
         self_mask, jnp.zeros((), jnp.bfloat16), scores_tile(unit_block, unit_block)
     )
 
-    vector_count = start.shape[1]
     zero_part = jnp.zeros((block_rows, vector_count), jnp.float32)
     zero_sum = jnp.zeros((block_rows,), jnp.float32)
     parts = {offset: zero_part for offset in units}
@@ -222,7 +322,7 @@
     tiles = []
     for (left, right), owned in zip(pair_plan, owned_list):
         affinity, row_part, row_sum, col_part, col_sum = first_pass(
-            owned, units[left], units[right], weights[left], weights[right]
+            owned, units[left], units[right], weights[left], weights[right], block_rows
         )
         tiles.append(affinity)
         parts[left] = parts[left] + row_part

time: 235 us -> 271 us (1.15); the launches traced: 234 us -> 266 us
  Pallas kernels: 0 us -> 34.7 us
  matrix products: 37.2 us -> 10.2 us
  local copies, waits for them, and re-layouts: 18.2 us -> 42.8 us
  other arithmetic: 37.8 us -> 52.8 us
  starting transfers between devices: 39.1 us -> 28.9 us
  waiting for transfers between devices: 98.6 us -> 93.6 us
    pallas_call x0 -> x6, Pallas kernels: none -> 34.7 us  [the longest x3 21.6 us: pair_terms(): pl.pallas_call(pair_kernel, grid=(block_rows // chunk,), in_specs=[pl.Blo...]
    ppermute x10, starting transfers between devices: 24 us -> 11 us  [butterfly(): other = lax.ppermute(block, axis, route)]
    ppermute x8, waiting for transfers between devices: 79.1 us -> 67.1 us  [shifted(): return lax.ppermute(block, axis, route)]
    slice x4 -> x12, local copies, waits for them, and re-layouts: 6.37 us -> 16.9 us  [the longest x6 9.27 us: on_device(): arrived[block_rows:].reshape(-1)[:block_rows * vector_count]]
    dot_general x6 -> x2, matrix products: 10.3 us -> 0.95 us  [row_product(): return jnp.dot(affinity, weights, preferred_element_type=jnp.float32)]
    dot_general x3 -> x1, matrix products: 15 us -> 5.75 us  [scores_tile(): lax.dot_general(leftside_block, right_block, (((1,), (1,)), ((), ())), pr...]
    dot_general x4 -> x0, matrix products: 8.28 us -> none  [col_product(): lax.dot_general(affinity, weights, (((0,), (0,)), ((), ())), preferred_el...]
    another operation x7 -> x9, local copies, waits for them, and re-layouts: 1.65 us -> 8.7 us
  transfers between devices with their start and end apart: 18 -> 18, of which waited for: 16 -> 15; matrix products, arithmetic and copies ran while one was open for 11% -> 11% of each run, Pallas kernels for 0% -> 6%
where the time goes in v3:
time: 271 us; the launch traced here: 266 us
  waiting for transfers between devices  93.6 us (35%)
  other arithmetic  52.8 us (19%)
  local copies, waits for them, and re-layouts  42.8 us (16%)
  Pallas kernels  34.7 us (13%)
  starting transfers between devices  28.9 us (11%)
  matrix products  10.2 us (4%)
  between operations  3.23 us (1%)
    ppermute x8, waiting for transfers between devices, shifted(): return lax.ppermute(block, axis, route)  67.1 us
    ppermute x10, waiting for transfers between devices, butterfly(): other = lax.ppermute(block, axis, route)  26.6 us
    pallas_call x3, Pallas kernels, pair_terms(): pl.pallas_call(pair_kernel, grid=(block_rows // chunk,), in_specs=[pl.Blo...  21.6 us
    ppermute x8, starting transfers between devices, shifted(): return lax.ppermute(block, axis, route)  17.9 us
    pallas_call x3, Pallas kernels, apply_terms(): pl.pallas_call(apply_kernel, grid=(block_rows // chunk,), in_specs=[pl.Bl...  13.1 us
    another operation x6, other arithmetic, orthonormal(): normalizer_coefficient = jnp.linalg.cholesky(gram_matrix)  13 us
    another operation x4, other arithmetic, orthonormal(): jax.scipy.linalg.solve_triangular(normalizer_coefficient, displaced_entri...  11.1 us
    ppermute x10, starting transfers between devices, butterfly(): other = lax.ppermute(block, axis, route)  11 us
  transfers between devices with their start and end apart: 18, of which 15 were waited for; matrix products, arithmetic and copies ran while one was open for 11% of the time, Pallas kernels for 6%

profile of v3, /device:TPU:0, one launch (start us, length us, event | category | flops | bytes accessed | tf_op | source)
XLA Modules:
  0.0 266.3 jit_solution(5034967277461829339)
XLA Ops:
  2.2 1.8 fusion.1
  5.5 3.0 %collective-permute-start.1 = (bf16[1110,768]{1,0:T(8,128)(2,1)S(1)}, bf16[1110,768]{1,0:T(8,128)(2,1)}, u32[]{:S(2)}, u32[]{:S(2)}) collective-permute-start(bf16[1110,768]{1,0:T(8,128)(2,1)S(1)} %pad_maximum_fusion), channel_id=1, source_target_pairs={{24,0},{28,4},{0,8},{4,12},{8,16},{12,20},{16,24},{20,28},{25,1},{... | collective-permute-start | bytes 5114888 | tf_op jit(solution)/shard_map/ppermute | solution.py:20
  8.6 3.2 %collective-permute-start = (bf16[1110,768]{1,0:T(8,128)(2,1)S(1)}, bf16[1110,768]{1,0:T(8,128)(2,1)S(1)}, u32[]{:S(2)}, u32[]{:S(2)}) collective-permute-start(bf16[1110,768]{1,0:T(8,128)(2,1)S(1)} %pad_maximum_fusion), channel_id=1, source_target_pairs={{4,0},{8,4},{12,8},{16,12},{20,16},{24,20},{28,24},{0,28},{5,1},{9... | collective-permute-start | bytes 5114888 | tf_op jit(solution)/shard_map/ppermute | solution.py:20
  14.6 5.8 %convert_reduce_fusion = (f32[1024]{0:T(1024)}, bf16[1024,1024]{0,1:T(8,128)(2,1)}) fusion(bf16[1024,768]{1,0:T(8,128)(2,1)} %copy-done.2), kind=kOutput, calls=%fused_computation.12 | convolution fusion | flops 1616903168 | bytes 3674112 | tf_op jit(solution)/shard_map/dot_general | solution.py:55
  20.3 28.5 %collective-permute-done.1 = bf16[1110,768]{1,0:T(8,128)(2,1)} collective-permute-done((bf16[1110,768]{1,0:T(8,128)(2,1)S(1)}, bf16[1110,768]{1,0:T(8,128)(2,1)}, u32[]{:S(2)}, u32[]{:S(2)}) %collective-permute-start.1) | collective-permute-done | bytes 1704992 | tf_op jit(solution)/shard_map/ppermute | solution.py:20
  48.9 1.6 slice.218
  50.4 1.8 slice.178
  52.3 1.7 slice.219
  53.9 27.8 %collective-permute-done = bf16[1110,768]{1,0:T(8,128)(2,1)S(1)} collective-permute-done((bf16[1110,768]{1,0:T(8,128)(2,1)S(1)}, bf16[1110,768]{1,0:T(8,128)(2,1)S(1)}, u32[]{:S(2)}, u32[]{:S(2)}) %collective-permute-start) | collective-permute-done | bytes 1704992 | tf_op jit(solution)/shard_map/ppermute | solution.py:20
  82.4 1.8 slice.175
  84.3 1.7 slice.217
  86.0 17.4 %conditional.7 = (bf16[1024,1024]{1,0:T(8,128)(2,1)}, f32[1024,64]{1,0:T(8,128)}, f32[1024]{0:T(1024)S(1)}, f32[1024,64]{0,1:T(8,128)}, f32[1024]{0:T(1024)S(1)}) conditional(s32[]{:T(128)} %convert_element_type.39, () %tuple.60, (bf16[1024,64]{1,0:T(8,128)(2,1)}, bf16[1024,64]{0,1:T(8,128)(2,1)S(1)}, bf16[1110,768]{1,0:T(8,128)(2,1)}, ...), branch_computations={%region_5.6_spmd, %region_6.7_spmd} | conditional | flops 1572864 | bytes 2629690 | solution.py:192
  86.0 1.7 copy.45
  87.9 1.7 maximum_bitcast_fusion.1.left_t_ref
  90.5 1.7 maximum_maximum_fusion.1.right_w_ref
  92.2 7.3 %branch_1_fun.7 = (bf16[1024,1024]{1,0:T(8,128)(2,1)}, f32[1024,128]{1,0:T(8,128)}, f32[128,1024]{1,0:T(8,128)}) custom-call(bf16[1110,768]{1,0:T(8,128)(2,1)} %get-tuple-element.51.left_ref, bf16[1110,768]{1,0:T(8,128)(2,1)S(1)} %get-tuple-element.52.right_ref, bf16[128,1024]{1,0:T(8,128)(2,1)} %maximum_bitcast_fusion.1.left_t_ref, ...), custom_call_target="tpu_custom_call" | custom-call | tf_op jit(solution)/shard_map/cond/branch_1_fun/pallas_call | solution.py:114
  99.5 1.4 slice_reduce_fusion.1
  100.9 1.7 slice_bitcast_fusion.1
  103.4 17.7 %conditional.8 = (bf16[1024,1024]{1,0:T(8,128)(2,1)}, f32[1024,64]{1,0:T(8,128)}, f32[1024]{0:T(1024)}, f32[1024,64]{0,1:T(8,128)}, f32[1024]{0:T(1024)}) conditional(s32[]{:T(128)} %convert_element_type.40, () %tuple.62, (bf16[1024,64]{1,0:T(8,128)(2,1)}, bf16[1024,64]{1,0:T(8,128)(2,1)}, bf16[1110,768]{1,0:T(8,128)(2,1)}, ...), branch_computations={%region_8.9_spmd, %region_9.10_spmd} | conditional | flops 1572864 | bytes 2629690 | solution.py:192
  103.4 1.7 copy.48
  105.3 1.7 maximum_bitcast_fusion.2.left_t_ref
  107.0 1.7 maximum_maximum_fusion.2.right_w_ref
  108.7 7.3 %branch_1_fun.8 = (bf16[1024,1024]{1,0:T(8,128)(2,1)}, f32[1024,128]{1,0:T(8,128)}, f32[128,1024]{1,0:T(8,128)}) custom-call(bf16[1110,768]{1,0:T(8,128)(2,1)} %get-tuple-element.58.left_ref, bf16[1110,768]{1,0:T(8,128)(2,1)S(1)} %get-tuple-element.59.right_ref, bf16[128,1024]{1,0:T(8,128)(2,1)} %maximum_bitcast_fusion.2.left_t_ref, ...), custom_call_target="tpu_custom_call" | custom-call | tf_op jit(solution)/shard_map/cond/branch_1_fun/pallas_call | solution.py:114
  116.1 2.0 slice_reduce_fusion.2
  118.1 1.7 slice_bitcast_fusion.2
  119.8 1.3 slice.131
  121.1 2.1 add.210
  123.2 1.9 reshape.122
  125.7 1.7 pad_maximum_fusion.2
  127.4 12.8 %conditional.6 = (bf16[1024,1024]{1,0:T(8,128)(2,1)}, f32[1024,64]{1,0:T(8,128)}, f32[1024]{0:T(1024)S(1)}, f32[1024,64]{0,1:T(8,128)S(1)}, f32[1024]{0:T(1024)S(1)}) conditional(s32[]{:T(128)} %convert_element_type.38, () %tuple.58, (bf16[1024,64]{0,1:T(8,128)(2,1)S(1)}, bf16[1024,64]{1,0:T(8,128)(2,1)}, bf16[1110,768]{1,0:T(8,128)(2,1)S(1)}, ...), branch_computations={%region_2.3_spmd, %region_3.4_spmd} | conditional | flops 1572864 | bytes 2629690 | solution.py:192
  128.4 1.8 maximum_maximum_fusion.right_w_ref
  130.2 6.9 %branch_1_fun.6 = (bf16[1024,1024]{1,0:T(8,128)(2,1)}, f32[1024,128]{1,0:T(8,128)}, f32[128,1024]{1,0:T(8,128)}) custom-call(bf16[1110,768]{1,0:T(8,128)(2,1)S(1)} %get-tuple-element.36.left_ref, bf16[1110,768]{1,0:T(8,128)(2,1)S(1)} %get-tuple-element.42.right_ref, bf16[128,1024]{1,0:T(8,128)(2,1)} %maximum_bitcast_fusion.left_t_ref, ...), custom_call_target="tpu_custom_call" | custom-call | tf_op jit(solution)/shard_map/cond/branch_1_fun/pallas_call | solution.py:114
  137.1 1.4 slice_reduce_fusion
  143.6 5.9 %collective-permute-start.2 = (f32[520,128]{1,0:T(8,128)}, f32[520,128]{1,0:T(8,128)}, u32[]{:S(2)}, u32[]{:S(2)}) collective-permute-start(f32[520,128]{1,0:T(8,128)} %pad_maximum_fusion.1), channel_id=1, source_target_pairs={{28,0},{0,4},{4,8},{8,12},{12,16},{16,20},{20,24},{24,28},{29,1},{... | collective-permute-start | bytes 798728 | tf_op jit(solution)/shard_map/ppermute | solution.py:20
  155.0 1.3 broadcast_multiply_fusion
  160.9 2.8 %collective-permute-start.5 = (f32[35,128]{1,0:T(8,128)S(1)}, f32[35,128]{1,0:T(8,128)S(1)}, u32[]{:S(2)}, u32[]{:S(2)}) collective-permute-start(f32[35,128]{1,0:T(8,128)S(1)} %pad_maximum_fusion.8), channel_id=1, source_target_pairs={{0,2},{1,3},{2,0},{3,1},{4,6},{5,7},{6,4},{7,5},{8,10},{9,11},{10,... | collective-permute-start | bytes 53768 | tf_op jit(solution)/shard_map/ppermute | solution.py:223
  163.7 1.8 collective-permute-done.5
  165.5 1.9 collective-permute-start.6
  167.4 2.0 collective-permute-done.6
  169.4 1.3 collective-permute-start.7
  170.7 2.6 collective-permute-done.7
  173.3 4.6 %collective-permute-start.8 = (f32[49,128]{1,0:T(8,128)S(1)}, f32[49,128]{1,0:T(8,128)S(1)}, u32[]{:S(2)}, u32[]{:S(2)}) collective-permute-start(f32[49,128]{1,0:T(8,128)S(1)} %pad_maximum_fusion.3), channel_id=1, source_target_pairs={{0,16},{4,20},{8,24},{12,28},{16,0},{20,4},{24,8},{28,12},{1,17},{... | collective-permute-start | bytes 75272 | tf_op jit(solution)/shard_map/ppermute | solution.py:223
  177.9 1.9 collective-permute-done.8
  181.9 5.8 %cholesky.44 = f32[64,64]{1,0:T(8,128)S(1)} custom-call(f32[64,64]{1,0:T(8,128)S(1)} %fusion.25), custom_call_target="Cholesky" | custom-call | tf_op jit(solution)/shard_map/jit(cholesky)/cholesky | solution.py:274
  189.1 4.9 %custom-call.6 = f32[1,64,64]{1,2,0:T(8,128)S(1)} custom-call(f32[1,64,64]{2,1,0:T(8,128)S(1)} %fusion.20), custom_call_target="InvertDiagBlocksLowerTriangular" | custom-call | tf_op jit(solution)/shard_map/jit(_solve_triangular)/triangular_solve | solution.py:275
  194.4 2.0 collective-permute-start.10
  196.5 1.9 collective-permute-start.9
  198.4 3.5 %collective-permute-done.10 = bf16[1024,64]{0,1:T(8,128)(2,1)S(1)} collective-permute-done((bf16[1024,64]{0,1:T(8,128)(2,1)S(1)}, bf16[1024,64]{0,1:T(8,128)(2,1)S(1)}, u32[]{:S(2)}, u32[]{:S(2)}) %collective-permute-start.10) | collective-permute-done | bytes 131104 | tf_op jit(solution)/shard_map/ppermute | solution.py:20
  201.9 5.6 %conditional.10 = (f32[1024,64]{1,0:T(8,128)S(1)}, f32[1024,64]{0,1:T(8,128)}) conditional(s32[]{:T(128)} %convert_element_type.39, () %tuple.66, (bf16[1024,64]{0,1:T(8,128)(2,1)S(1)}, bf16[1024,1024]{1,0:T(8,128)(2,1)}, bf16[1024,64]{0,1:T(8,128)(2,1)S(1)}) %tuple.115), branch_computations={%region_19.22_spmd, %region_20.23_spmd} | conditional | bytes 524312 | solution.py:207
  202.7 4.8 %branch_1_fun.10 = (f32[1024,64]{1,0:T(8,128)S(1)}, f32[64,1024]{1,0:T(8,128)}) custom-call(bf16[1024,1024]{1,0:T(8,128)(2,1)} %get-tuple-element.70.tile_ref, bf16[64,1024]{1,0:T(8,128)(2,1)S(1)} %bitcast.108, bf16[1024,64]{1,0:T(8,128)(2,1)} %copy.57.right_w_ref), custom_call_target="tpu_custom_call" | custom-call | tf_op jit(solution)/shard_map/cond/branch_1_fun/pallas_call | solution.py:140
  207.7 5.9 %conditional.11 = (f32[1024,64]{1,0:T(8,128)S(1)}, f32[1024,64]{0,1:T(8,128)S(1)}) conditional(s32[]{:T(128)} %convert_element_type.40, () %tuple.68, (bf16[1024,64]{0,1:T(8,128)(2,1)S(1)}, bf16[1024,1024]{1,0:T(8,128)(2,1)}, bf16[1024,64]{0,1:T(8,128)(2,1)}) %tuple.69), branch_computations={%region_21.24_spmd, %region_22.25_spmd} | conditional | bytes 524312 | solution.py:207
  207.7 1.7 copy.59.right_w_ref
  209.5 4.2 %branch_1_fun.11 = (f32[1024,64]{1,0:T(8,128)S(1)}, f32[64,1024]{1,0:T(8,128)S(1)}) custom-call(bf16[1024,1024]{1,0:T(8,128)(2,1)} %get-tuple-element.75.tile_ref, bf16[64,1024]{1,0:T(8,128)(2,1)S(1)} %bitcast.109, bf16[1024,64]{1,0:T(8,128)(2,1)} %copy.59.right_w_ref), custom_call_target="tpu_custom_call" | custom-call | tf_op jit(solution)/shard_map/cond/branch_1_fun/pallas_call | solution.py:140
  214.6 5.9 %conditional.9 = (f32[1024,64]{1,0:T(8,128)S(1)}, f32[1024,64]{0,1:T(8,128)S(1)}) conditional(s32[]{:T(128)} %convert_element_type.38, () %tuple.64, (bf16[1024,64]{0,1:T(8,128)(2,1)S(1)}, bf16[1024,1024]{1,0:T(8,128)(2,1)}, bf16[1024,64]{0,1:T(8,128)(2,1)}) %tuple.116), branch_computations={%region_17.20_spmd, %region_18.21_spmd} | conditional | bytes 524312 | solution.py:207
  214.6 1.7 copy.56.right_w_ref
  216.3 4.2 %branch_1_fun.9 = (f32[1024,64]{1,0:T(8,128)S(1)}, f32[64,1024]{1,0:T(8,128)S(1)}) custom-call(bf16[1024,1024]{1,0:T(8,128)(2,1)} %get-tuple-element.65.tile_ref, bf16[64,1024]{1,0:T(8,128)(2,1)S(1)} %bitcast.104, bf16[1024,64]{1,0:T(8,128)(2,1)} %copy.56.right_w_ref), custom_call_target="tpu_custom_call" | custom-call | tf_op jit(solution)/shard_map/cond/branch_1_fun/pallas_call | solution.py:140
  221.2 1.9 collective-permute-start.11
  223.8 6.7 %collective-permute-done.11 = f32[1024,64]{0,1:T(8,128)S(1)} collective-permute-done((f32[1024,64]{0,1:T(8,128)}, f32[1024,64]{0,1:T(8,128)S(1)}, u32[]{:S(2)}, u32[]{:S(2)}) %collective-permute-start.11) | collective-permute-done | bytes 262176 | tf_op jit(solution)/shard_map/ppermute | solution.py:20
  234.5 3.8 %collective-permute-done.14 = f32[35,128]{1,0:T(8,128)S(1)} collective-permute-done((f32[35,128]{1,0:T(8,128)S(1)}, f32[35,128]{1,0:T(8,128)S(1)}, u32[]{:S(2)}, u32[]{:S(2)}) %collective-permute-start.14) | collective-permute-done | bytes 17952 | tf_op jit(solution)/shard_map/ppermute | solution.py:223
  238.4 3.8 %collective-permute-done.15 = f32[37,128]{1,0:T(8,128)S(1)} collective-permute-done((f32[37,128]{1,0:T(8,128)S(1)}, f32[37,128]{1,0:T(8,128)S(1)}, u32[]{:S(2)}, u32[]{:S(2)}) %collective-permute-start.15) | collective-permute-done | bytes 18976 | tf_op jit(solution)/shard_map/ppermute | solution.py:223
  242.3 3.8 %collective-permute-done.16 = f32[41,128]{1,0:T(8,128)S(1)} collective-permute-done((f32[41,128]{1,0:T(8,128)S(1)}, f32[41,128]{1,0:T(8,128)S(1)}, u32[]{:S(2)}, u32[]{:S(2)}) %collective-permute-start.16) | collective-permute-done | bytes 21024 | tf_op jit(solution)/shard_map/ppermute | solution.py:223
  246.3 4.7 %collective-permute-done.17 = f32[49,128]{1,0:T(8,128)S(1)} collective-permute-done((f32[49,128]{1,0:T(8,128)S(1)}, f32[49,128]{1,0:T(8,128)S(1)}, u32[]{:S(2)}, u32[]{:S(2)}) %collective-permute-start.17) | collective-permute-done | bytes 25120 | tf_op jit(solution)/shard_map/ppermute | solution.py:223
  253.1 5.8 %cholesky.55 = f32[64,64]{1,0:T(8,128)S(1)} custom-call(f32[64,64]{1,0:T(8,128)S(1)} %fusion.23), custom_call_target="Cholesky" | custom-call | tf_op jit(solution)/shard_map/jit(cholesky)/cholesky | solution.py:274
  260.3 4.9 %custom-call.7 = f32[1,64,64]{1,2,0:T(8,128)S(1)} custom-call(f32[1,64,64]{2,1,0:T(8,128)S(1)} %fusion.21), custom_call_target="InvertDiagBlocksLowerTriangular" | custom-call | tf_op jit(solution)/shard_map/jit(_solve_triangular)/triangular_solve | solution.py:275
  (158 shorter events, 39.4 us)
Async XLA Ops:
  0.6 3.3 %copy-start.1 = (bf16[1024,768]{1,0:T(8,128)(2,1)S(1)}, bf16[1024,768]{1,0:T(8,128)(2,1)}, u32[]{:S(2)}) copy-start(bf16[1024,768]{1,0:T(8,128)(2,1)} %param.18) | copy-start | bytes 4718596
  4.4 1.2 copy-start.2
  4.4 7.4 %copy-start.6 = (s32[32,3]{0,1:T(4,128)S(1)}, s32[32,3]{0,1:T(4,128)}, u32[]{:S(2)}) copy-start(s32[32,3]{0,1:T(4,128)} %param.20) | copy-start | bytes 1156
  5.5 43.3 %collective-permute-start.1 = (bf16[1110,768]{1,0:T(8,128)(2,1)S(1)}, bf16[1110,768]{1,0:T(8,128)(2,1)}, u32[]{:S(2)}, u32[]{:S(2)}) collective-permute-start(bf16[1110,768]{1,0:T(8,128)(2,1)S(1)} %pad_maximum_fusion), channel_id=1, source_target_pairs={{24,0},{28,4},{0,8},{4,12},{8,16},{12,20},{16,24},{20,28},{25,1},{... | collective-permute-start | bytes 5114888 | tf_op jit(solution)/shard_map/ppermute | solution.py:20
  8.6 73.2 %collective-permute-start = (bf16[1110,768]{1,0:T(8,128)(2,1)S(1)}, bf16[1110,768]{1,0:T(8,128)(2,1)S(1)}, u32[]{:S(2)}, u32[]{:S(2)}) collective-permute-start(bf16[1110,768]{1,0:T(8,128)(2,1)S(1)} %pad_maximum_fusion), channel_id=1, source_target_pairs={{4,0},{8,4},{12,8},{16,12},{20,16},{24,20},{28,24},{0,28},{5,1},{9... | collective-permute-start | bytes 5114888 | tf_op jit(solution)/shard_map/ppermute | solution.py:20
  20.3 65.6 %copy-start.3 = (bf16[1024,64]{0,1:T(8,128)(2,1)S(1)}, bf16[1024,64]{0,1:T(8,128)(2,1)}, u32[]{:S(2)}) copy-start(bf16[1024,64]{0,1:T(8,128)(2,1)} %param.19) | copy-start | bytes 393220
  127.4 23.8 %collective-permute-start.3 = (f32[520,128]{1,0:T(8,128)}, f32[520,128]{1,0:T(8,128)}, u32[]{:S(2)}, u32[]{:S(2)}) collective-permute-start(f32[520,128]{1,0:T(8,128)} %pad_maximum_fusion.2), channel_id=1, source_target_pairs={{8,0},{12,4},{16,8},{20,12},{24,16},{28,20},{0,24},{4,28},{9,1},{1... | collective-permute-start | bytes 798728 | tf_op jit(solution)/shard_map/ppermute | solution.py:20
  140.2 0.6 copy-start.5
  140.2 9.3 %copy-start = (bf16[1024,1024]{0,1:T(8,128)(2,1)S(1)}, bf16[1024,1024]{0,1:T(8,128)(2,1)}, u32[]{:S(2)}) copy-start(bf16[1024,1024]{0,1:T(8,128)(2,1)} %get-tuple-element.210) | copy-start | bytes 6291460
  143.6 10.1 %collective-permute-start.2 = (f32[520,128]{1,0:T(8,128)}, f32[520,128]{1,0:T(8,128)}, u32[]{:S(2)}, u32[]{:S(2)}) collective-permute-start(f32[520,128]{1,0:T(8,128)} %pad_maximum_fusion.1), channel_id=1, source_target_pairs={{28,0},{0,4},{4,8},{8,12},{12,16},{16,20},{20,24},{24,28},{29,1},{... | collective-permute-start | bytes 798728 | tf_op jit(solution)/shard_map/ppermute | solution.py:20
  151.2 3.9 %copy-start.7 = (f32[1024]{0:T(1024)S(1)}, f32[1024]{0:T(1024)}, u32[]{:S(2)}) copy-start(f32[1024]{0:T(1024)} %get-tuple-element.209) | copy-start | bytes 12292
  159.7 1.2 collective-permute-start.4
  160.9 4.5 %collective-permute-start.5 = (f32[35,128]{1,0:T(8,128)S(1)}, f32[35,128]{1,0:T(8,128)S(1)}, u32[]{:S(2)}, u32[]{:S(2)}) collective-permute-start(f32[35,128]{1,0:T(8,128)S(1)} %pad_maximum_fusion.8), channel_id=1, source_target_pairs={{0,2},{1,3},{2,0},{3,1},{4,6},{5,7},{6,4},{7,5},{8,10},{9,11},{10,... | collective-permute-start | bytes 53768 | tf_op jit(solution)/shard_map/ppermute | solution.py:223
  165.5 3.8 %collective-permute-start.6 = (f32[37,128]{1,0:T(8,128)S(1)}, f32[37,128]{1,0:T(8,128)S(1)}, u32[]{:S(2)}, u32[]{:S(2)}) collective-permute-start(f32[37,128]{1,0:T(8,128)S(1)} %pad_maximum_fusion.9), channel_id=1, source_target_pairs={{0,4},{4,0},{8,12},{12,8},{16,20},{20,16},{24,28},{28,24},{1,5},{5... | collective-permute-start | bytes 56840 | tf_op jit(solution)/shard_map/ppermute | solution.py:223
  169.4 3.9 %collective-permute-start.7 = (f32[41,128]{1,0:T(8,128)S(1)}, f32[41,128]{1,0:T(8,128)S(1)}, u32[]{:S(2)}, u32[]{:S(2)}) collective-permute-start(f32[41,128]{1,0:T(8,128)S(1)} %pad_maximum_fusion.5), channel_id=1, source_target_pairs={{0,8},{4,12},{8,0},{12,4},{16,24},{20,28},{24,16},{28,20},{1,9},{5... | collective-permute-start | bytes 62984 | tf_op jit(solution)/shard_map/ppermute | solution.py:223
  173.3 6.5 %collective-permute-start.8 = (f32[49,128]{1,0:T(8,128)S(1)}, f32[49,128]{1,0:T(8,128)S(1)}, u32[]{:S(2)}, u32[]{:S(2)}) collective-permute-start(f32[49,128]{1,0:T(8,128)S(1)} %pad_maximum_fusion.3), channel_id=1, source_target_pairs={{0,16},{4,20},{8,24},{12,28},{16,0},{20,4},{24,8},{28,12},{1,17},{... | collective-permute-start | bytes 75272 | tf_op jit(solution)/shard_map/ppermute | solution.py:223
  194.4 7.4 %collective-permute-start.10 = (bf16[1024,64]{0,1:T(8,128)(2,1)S(1)}, bf16[1024,64]{0,1:T(8,128)(2,1)S(1)}, u32[]{:S(2)}, u32[]{:S(2)}) collective-permute-start(bf16[1024,64]{0,1:T(8,128)(2,1)S(1)} %bitcast.100), channel_id=1, source_target_pairs={{24,0},{28,4},{0,8},{4,12},{8,16},{12,20},{16,24},{20,28},{25,1},{... | collective-permute-start | bytes 393224 | tf_op jit(solution)/shard_map/ppermute | solution.py:20
  196.5 11.2 %collective-permute-start.9 = (bf16[1024,64]{0,1:T(8,128)(2,1)S(1)}, bf16[1024,64]{0,1:T(8,128)(2,1)}, u32[]{:S(2)}, u32[]{:S(2)}) collective-permute-start(bf16[1024,64]{0,1:T(8,128)(2,1)S(1)} %bitcast.101), channel_id=1, source_target_pairs={{4,0},{8,4},{12,8},{16,12},{20,16},{24,20},{28,24},{0,28},{5,1},{9... | collective-permute-start | bytes 393224 | tf_op jit(solution)/shard_map/ppermute | solution.py:20
  214.6 9.3 %collective-permute-start.12 = (f32[1024,64]{0,1:T(8,128)}, f32[1024,64]{0,1:T(8,128)}, u32[]{:S(2)}, u32[]{:S(2)}) collective-permute-start(f32[1024,64]{0,1:T(8,128)} %add.234), channel_id=1, source_target_pairs={{8,0},{12,4},{16,8},{20,12},{24,16},{28,20},{0,24},{4,28},{9,1},{1... | collective-permute-start | bytes 786440 | tf_op jit(solution)/shard_map/ppermute | solution.py:20
  220.5 10.0 %copy-start.4 = (f32[1024,64]{0,1:T(8,128)S(1)}, f32[1024,64]{0,1:T(8,128)}, u32[]{:S(2)}) copy-start(f32[1024,64]{0,1:T(8,128)} %get-tuple-element.118) | copy-start | bytes 786436
  221.2 9.3 %collective-permute-start.11 = (f32[1024,64]{0,1:T(8,128)}, f32[1024,64]{0,1:T(8,128)S(1)}, u32[]{:S(2)}, u32[]{:S(2)}) collective-permute-start(f32[1024,64]{0,1:T(8,128)} %add.232), channel_id=1, source_target_pairs={{28,0},{0,4},{4,8},{8,12},{12,16},{16,20},{20,24},{24,28},{29,1},{... | collective-permute-start | bytes 786440 | tf_op jit(solution)/shard_map/ppermute | solution.py:20
  233.1 1.3 collective-permute-start.13
  234.4 3.8 %collective-permute-start.14 = (f32[35,128]{1,0:T(8,128)S(1)}, f32[35,128]{1,0:T(8,128)S(1)}, u32[]{:S(2)}, u32[]{:S(2)}) collective-permute-start(f32[35,128]{1,0:T(8,128)S(1)} %pad_maximum_fusion.11), channel_id=1, source_target_pairs={{0,2},{1,3},{2,0},{3,1},{4,6},{5,7},{6,4},{7,5},{8,10},{9,11},{10,... | collective-permute-start | bytes 53768 | tf_op jit(solution)/shard_map/ppermute | solution.py:223
  238.3 3.8 %collective-permute-start.15 = (f32[37,128]{1,0:T(8,128)S(1)}, f32[37,128]{1,0:T(8,128)S(1)}, u32[]{:S(2)}, u32[]{:S(2)}) collective-permute-start(f32[37,128]{1,0:T(8,128)S(1)} %pad_maximum_fusion.12), channel_id=1, source_target_pairs={{0,4},{4,0},{8,12},{12,8},{16,20},{20,16},{24,28},{28,24},{1,5},{5... | collective-permute-start | bytes 56840 | tf_op jit(solution)/shard_map/ppermute | solution.py:223
  242.2 3.9 %collective-permute-start.16 = (f32[41,128]{1,0:T(8,128)S(1)}, f32[41,128]{1,0:T(8,128)S(1)}, u32[]{:S(2)}, u32[]{:S(2)}) collective-permute-start(f32[41,128]{1,0:T(8,128)S(1)} %pad_maximum_fusion.6), channel_id=1, source_target_pairs={{0,8},{4,12},{8,0},{12,4},{16,24},{20,28},{24,16},{28,20},{1,9},{5... | collective-permute-start | bytes 62984 | tf_op jit(solution)/shard_map/ppermute | solution.py:223
  246.2 4.8 %collective-permute-start.17 = (f32[49,128]{1,0:T(8,128)S(1)}, f32[49,128]{1,0:T(8,128)S(1)}, u32[]{:S(2)}, u32[]{:S(2)}) collective-permute-start(f32[49,128]{1,0:T(8,128)S(1)} %pad_maximum_fusion.4), channel_id=1, source_target_pairs={{0,16},{4,20},{8,24},{12,28},{16,0},{20,4},{24,8},{28,12},{1,17},{... | collective-permute-start | bytes 75272 | tf_op jit(solution)/shard_map/ppermute | solution.py:223

commit v4 on v2

--- a/solution.py
+++ b/solution.py
@@ -201,11 +201,14 @@
     units = {0: unit_block}
     weights = {0: start}
     unit_width = unit_block.shape[1]
-    packed = jnp.concatenate([unit_block, start], axis=1)
+    vector_count = start.shape[1]
+    packed = jnp.concatenate([unit_block, as_rows(start.reshape(-1), unit_width)])
     for offset in fetch_offsets:
         arrived = shifted(packed, "wide", -offset)
-        units[offset] = arrived[:, :unit_width]
-        weights[offset] = arrived[:, unit_width:]
+        units[offset] = arrived[:block_rows]
+        weights[offset] = (
+            arrived[block_rows:].reshape(-1)[: block_rows * vector_count].reshape(block_rows, vector_count)
+        )
 
     self_mask = lax.broadcasted_iota(
         jnp.int32, (block_rows, block_rows), 0

time: 235 us -> 238 us (1.013)
  matrix products: 37.2 us -> 21.2 us
  waiting for transfers between devices: 98.6 us -> 110 us
  other arithmetic: 37.8 us -> 41 us
  starting transfers between devices: 39.1 us -> 41.9 us
    ppermute x8, starting transfers between devices: 15.1 us -> 27 us  [shifted(): return lax.ppermute(block, axis, route)]
    ppermute x10, starting transfers between devices: 24 us -> 14.9 us  [butterfly(): other = lax.ppermute(block, axis, route)]
    ppermute x8, waiting for transfers between devices: 79.1 us -> 87.2 us  [shifted(): return lax.ppermute(block, axis, route)]
    dot_general x3 -> x2, matrix products: 15 us -> 7.86 us  [scores_tile(): lax.dot_general(leftside_block, right_block, (((1,), (1,)), ((), ())), pr...]
    dot_general x6 -> x4, matrix products: 10.3 us -> 5.64 us  [row_product(): return jnp.dot(affinity, weights, preferred_element_type=jnp.float32)]
    dot_general x4 -> x2, matrix products: 8.28 us -> 4.14 us  [col_product(): lax.dot_general(affinity, weights, (((0,), (0,)), ((), ())), preferred_el...]
    ppermute x10, waiting for transfers between devices: 19.5 us -> 23.3 us  [butterfly(): other = lax.ppermute(block, axis, route)]
    unnamed x17 -> x23, local copies, waits for them, and re-layouts: 5 us -> 2.29 us
  transfers between devices with their start and end apart: 18 -> 18, of which waited for: 16 -> 16; matrix products, arithmetic and copies ran while one was open for 11% -> 6% of each run, Pallas kernels for 0% -> 0%
where the time goes in v4:
time: 238 us; the launch traced here: 235 us
  waiting for transfers between devices  110 us (46%)
  starting transfers between devices  41.9 us (18%)
  other arithmetic  41 us (17%)
  matrix products  21.2 us (9%)
  local copies, waits for them, and re-layouts  17.2 us (7%)
  between operations  3.28 us (1%)
    ppermute x8, waiting for transfers between devices, shifted(): return lax.ppermute(block, axis, route)  87.2 us
    ppermute x8, starting transfers between devices, shifted(): return lax.ppermute(block, axis, route)  27 us
    ppermute x10, waiting for transfers between devices, butterfly(): other = lax.ppermute(block, axis, route)  23.3 us
    ppermute x10, starting transfers between devices, butterfly(): other = lax.ppermute(block, axis, route)  14.9 us
    another operation x6, other arithmetic, orthonormal(): normalizer_coefficient = jnp.linalg.cholesky(gram_matrix)  13 us
    another operation x4, other arithmetic, orthonormal(): jax.scipy.linalg.solve_triangular(normalizer_coefficient, displaced_entri...  11.1 us
    dot_general x2, matrix products, scores_tile(): lax.dot_general(leftside_block, right_block, (((1,), (1,)), ((), ())), pr...  7.86 us
    dot_general x4, matrix products, row_product(): return jnp.dot(affinity, weights, preferred_element_type=jnp.float32)  5.64 us
  transfers between devices with their start and end apart: 18, of which 16 were waited for; matrix products, arithmetic and copies ran while one was open for 6% of the time, Pallas kernels for 0%

profile of v4, /device:TPU:0, one launch (start us, length us, event | category | flops | bytes accessed | tf_op | source)
XLA Modules:
  0.0 235.2 jit_solution(8162478282727145890)
XLA Ops:
  0.6 1.9 fusion.1
  2.6 1.6 fusion.3
  4.7 2.7 %pad_maximum_fusion = bf16[1110,768]{1,0:T(8,128)(2,1)} fusion(bf16[86,768]{1,0:T(8,128)(2,1)S(1)} %reshape.118, bf16[1024,768]{1,0:T(8,128)(2,1)} %fusion.3), kind=kLoop, calls=%fused_computation.18 | loop fusion | flops 3409920 | bytes 3409920 | tf_op jit(solution)/shard_map/concatenate | solution.py:205
  7.4 6.0 %collective-permute-start = (bf16[1110,768]{1,0:T(8,128)(2,1)}, bf16[1110,768]{1,0:T(8,128)(2,1)}, u32[]{:S(2)}, u32[]{:S(2)}) collective-permute-start(bf16[1110,768]{1,0:T(8,128)(2,1)} %pad_maximum_fusion), channel_id=1, source_target_pairs={{4,0},{8,4},{12,8},{16,12},{20,16},{24,20},{28,24},{0,28},{5,1},{9... | collective-permute-start | bytes 5114888 | tf_op jit(solution)/shard_map/ppermute | solution.py:19
  13.4 0.8 fusion.38
  16.1 4.5 %convert_reduce_fusion.6 = (f32[1024]{0:T(1024)}, bf16[1024,1024]{0,1:T(8,128)(2,1)S(1)}) fusion(bf16[1024,768]{1,0:T(8,128)(2,1)} %fusion.3), kind=kOutput, calls=%fused_computation.9 | convolution fusion | flops 1616903168 | bytes 3674112 | tf_op jit(solution)/shard_map/dot_general | solution.py:54
  20.5 30.9 %collective-permute-done = bf16[1110,768]{1,0:T(8,128)(2,1)} collective-permute-done((bf16[1110,768]{1,0:T(8,128)(2,1)}, bf16[1110,768]{1,0:T(8,128)(2,1)}, u32[]{:S(2)}, u32[]{:S(2)}) %collective-permute-start) | collective-permute-done | bytes 1704992 | tf_op jit(solution)/shard_map/ppermute | solution.py:19
  51.4 0.9 slice.189
  52.5 35.2 %collective-permute-done.1 = bf16[1110,768]{1,0:T(8,128)(2,1)} collective-permute-done((bf16[1110,768]{1,0:T(8,128)(2,1)}, bf16[1110,768]{1,0:T(8,128)(2,1)}, u32[]{:S(2)}, u32[]{:S(2)}) %collective-permute-start.1) | collective-permute-done | bytes 1704992 | tf_op jit(solution)/shard_map/ppermute | solution.py:19
  87.7 0.9 slice.192
  88.9 1.5 slice.188
  90.4 3.3 %slice.191 = bf16[1024,768]{1,0:T(8,128)(2,1)} slice(bf16[1110,768]{1,0:T(8,128)(2,1)} %collective-permute-done.1), slice={[0:1024], [0:768]} | slice | bytes 3145728 | tf_op jit(solution)/shard_map/slice | solution.py:208
  93.8 7.8 %conditional.6 = (bf16[1024,1024]{1,0:T(8,128)(2,1)}, f32[1024,64]{0,1:T(8,128)S(1)}, f32[1024]{0:T(1024)S(1)}, f32[1024,64]{0,1:T(8,128)S(1)}, f32[1024]{0:T(1024)S(1)}) conditional(s32[]{:T(128)} %convert_element_type.59, () %tuple.58, (bf16[1024,768]{1,0:T(8,128)(2,1)S(1)}, bf16[1024,768]{1,0:T(8,128)(2,1)S(1)}, bf16[1024,64]{1,0:T(8,128)(2,1)S(1)}, ...), branch_computations={%region_2.3_spmd, %region_3.0_spmd} | conditional | flops 1884289024 | bytes 10231848 | solution.py:95
  93.8 3.4 %convert_reduce_fusion = (f32[1024]{0:T(1024)S(1)}, f32[1024]{0:T(1024)S(1)}, bf16[1024,1024]{1,0:T(8,128)(2,1)}) fusion(bf16[1024,768]{1,0:T(8,128)(2,1)S(1)} %get-tuple-element.36, bf16[1024,768]{1,0:T(8,128)(2,1)S(1)} %get-tuple-element.42), kind=kOutput, calls=%fused_computation | convolution fusion | flops 1615853568 | bytes 5251072 | tf_op jit(solution)/shard_map/cond/branch_1_fun/dot_general | solution.py:54
  97.1 2.3 fusion.50
  99.5 2.1 fusion.51
  101.6 0.7 copy-done.4
  102.3 1.7 conditional.8
  102.3 1.6 broadcast.132
  104.3 0.7 pad_maximum_fusion.1
  105.1 1.6 conditional.7
  105.1 1.6 broadcast.128
  106.7 0.7 copy-done.5
  107.8 0.7 pad_maximum_fusion.2
  108.6 9.7 %collective-permute-start.3 = (f32[520,128]{1,0:T(8,128)}, f32[520,128]{1,0:T(8,128)}, u32[]{:S(2)}, u32[]{:S(2)}) collective-permute-start(f32[520,128]{1,0:T(8,128)} %pad_maximum_fusion.2), channel_id=1, source_target_pairs={{8,0},{12,4},{16,8},{20,12},{24,16},{28,20},{0,24},{4,28},{9,1},{1... | collective-permute-start | bytes 798728 | tf_op jit(solution)/shard_map/ppermute | solution.py:19
  118.8 0.7 copy-done.6
  119.9 12.2 %collective-permute-done.3 = f32[520,128]{1,0:T(8,128)} collective-permute-done((f32[520,128]{1,0:T(8,128)}, f32[520,128]{1,0:T(8,128)}, u32[]{:S(2)}, u32[]{:S(2)}) %collective-permute-start.3) | collective-permute-done | bytes 266272 | tf_op jit(solution)/shard_map/ppermute | solution.py:19
  132.1 1.0 slice.195
  133.4 1.3 broadcast_multiply_fusion
  134.7 1.2 fusion.39
  138.1 1.2 collective-permute-done.4
  139.4 3.7 %collective-permute-done.5 = f32[35,128]{1,0:T(8,128)S(1)} collective-permute-done((f32[35,128]{1,0:T(8,128)S(1)}, f32[35,128]{1,0:T(8,128)S(1)}, u32[]{:S(2)}, u32[]{:S(2)}) %collective-permute-start.5) | collective-permute-done | bytes 17952 | tf_op jit(solution)/shard_map/ppermute | solution.py:125
  143.2 2.9 %collective-permute-start.6 = (f32[37,128]{1,0:T(8,128)S(1)}, f32[37,128]{1,0:T(8,128)S(1)}, u32[]{:S(2)}, u32[]{:S(2)}) collective-permute-start(f32[37,128]{1,0:T(8,128)S(1)} %pad_maximum_fusion.9), channel_id=1, source_target_pairs={{0,4},{4,0},{8,12},{12,8},{16,20},{20,16},{24,28},{28,24},{1,5},{5... | collective-permute-start | bytes 56840 | tf_op jit(solution)/shard_map/ppermute | solution.py:125
  146.1 1.8 collective-permute-done.6
  147.9 0.9 collective-permute-start.7
  148.8 3.0 %collective-permute-done.7 = f32[41,128]{1,0:T(8,128)S(1)} collective-permute-done((f32[41,128]{1,0:T(8,128)S(1)}, f32[41,128]{1,0:T(8,128)S(1)}, u32[]{:S(2)}, u32[]{:S(2)}) %collective-permute-start.7) | collective-permute-done | bytes 21024 | tf_op jit(solution)/shard_map/ppermute | solution.py:125
  151.8 2.6 %collective-permute-start.8 = (f32[49,128]{1,0:T(8,128)S(1)}, f32[49,128]{1,0:T(8,128)S(1)}, u32[]{:S(2)}, u32[]{:S(2)}) collective-permute-start(f32[49,128]{1,0:T(8,128)S(1)} %pad_maximum_fusion.3), channel_id=1, source_target_pairs={{0,16},{4,20},{8,24},{12,28},{16,0},{20,4},{24,8},{28,12},{1,17},{... | collective-permute-start | bytes 75272 | tf_op jit(solution)/shard_map/ppermute | solution.py:125
  154.4 2.2 collective-permute-done.8
  158.8 5.8 %cholesky.44 = f32[64,64]{1,0:T(8,128)S(1)} custom-call(f32[64,64]{1,0:T(8,128)S(1)} %fusion.25), custom_call_target="Cholesky" | custom-call | tf_op jit(solution)/shard_map/jit(cholesky)/cholesky | solution.py:176
  165.3 0.7 fusion.20
  165.9 4.9 %custom-call.6 = f32[1,64,64]{1,2,0:T(8,128)S(1)} custom-call(f32[1,64,64]{2,1,0:T(8,128)S(1)} %fusion.20), custom_call_target="InvertDiagBlocksLowerTriangular" | custom-call | tf_op jit(solution)/shard_map/jit(_solve_triangular)/triangular_solve | solution.py:177
  171.3 5.5 %collective-permute-start.9 = (bf16[1024,64]{0,1:T(8,128)(2,1)S(1)}, bf16[1024,64]{0,1:T(8,128)(2,1)S(1)}, u32[]{:S(2)}, u32[]{:S(2)}) collective-permute-start(bf16[1024,64]{0,1:T(8,128)(2,1)S(1)} %bitcast.100), channel_id=1, source_target_pairs={{4,0},{8,4},{12,8},{16,12},{20,16},{24,20},{28,24},{0,28},{5,1},{9... | collective-permute-start | bytes 393224 | tf_op jit(solution)/shard_map/ppermute | solution.py:19
  176.8 2.5 %collective-permute-done.9 = bf16[1024,64]{0,1:T(8,128)(2,1)S(1)} collective-permute-done((bf16[1024,64]{0,1:T(8,128)(2,1)S(1)}, bf16[1024,64]{0,1:T(8,128)(2,1)S(1)}, u32[]{:S(2)}, u32[]{:S(2)}) %collective-permute-start.9) | collective-permute-done | bytes 131104 | tf_op jit(solution)/shard_map/ppermute | solution.py:19
  179.3 4.4 %conditional.9 = (f32[1024,64]{0,1:T(8,128)S(1)}, f32[1024,64]{0,1:T(8,128)S(1)}) conditional(s32[]{:T(128)} %convert_element_type.59, () %tuple.64, (bf16[1024,1024]{1,0:T(8,128)(2,1)}, bf16[1024,64]{0,1:T(8,128)(2,1)S(1)}, bf16[1024,64]{0,1:T(8,128)(2,1)S(1)}) %tuple.112), branch_computations={%region_23.26_spmd, %region_24.27_spmd} | conditional | flops 268435456 | bytes 4980752 | solution.py:109
  179.3 2.3 fusion.44
  181.7 2.1 fusion.45
  183.8 0.7 add.232
  184.6 5.7 %collective-permute-start.11 = (f32[1024,64]{0,1:T(8,128)}, f32[1024,64]{0,1:T(8,128)}, u32[]{:S(2)}, u32[]{:S(2)}) collective-permute-start(f32[1024,64]{0,1:T(8,128)} %add.232), channel_id=1, source_target_pairs={{28,0},{0,4},{4,8},{8,12},{12,16},{16,20},{20,24},{24,28},{29,1},{... | collective-permute-start | bytes 786440 | tf_op jit(solution)/shard_map/ppermute | solution.py:19
  190.9 5.2 %collective-permute-done.11 = f32[1024,64]{0,1:T(8,128)} collective-permute-done((f32[1024,64]{0,1:T(8,128)}, f32[1024,64]{0,1:T(8,128)}, u32[]{:S(2)}, u32[]{:S(2)}) %collective-permute-start.11) | collective-permute-done | bytes 262176 | tf_op jit(solution)/shard_map/ppermute | solution.py:19
  196.1 1.1 collective-permute-done.12
  197.2 1.1 fusion.40
  199.1 0.7 pad_maximum_fusion.14
  199.9 1.2 collective-permute-done.13
  201.1 2.9 %collective-permute-start.14 = (f32[35,128]{1,0:T(8,128)S(1)}, f32[35,128]{1,0:T(8,128)S(1)}, u32[]{:S(2)}, u32[]{:S(2)}) collective-permute-start(f32[35,128]{1,0:T(8,128)S(1)} %pad_maximum_fusion.11), channel_id=1, source_target_pairs={{0,2},{1,3},{2,0},{3,1},{4,6},{5,7},{6,4},{7,5},{8,10},{9,11},{10,... | collective-permute-start | bytes 53768 | tf_op jit(solution)/shard_map/ppermute | solution.py:125
  204.0 1.8 collective-permute-done.14
  205.8 3.2 %collective-permute-start.15 = (f32[37,128]{1,0:T(8,128)S(1)}, f32[37,128]{1,0:T(8,128)S(1)}, u32[]{:S(2)}, u32[]{:S(2)}) collective-permute-start(f32[37,128]{1,0:T(8,128)S(1)} %pad_maximum_fusion.12), channel_id=1, source_target_pairs={{0,4},{4,0},{8,12},{12,8},{16,20},{20,16},{24,28},{28,24},{1,5},{5... | collective-permute-start | bytes 56840 | tf_op jit(solution)/shard_map/ppermute | solution.py:125
  209.0 1.8 collective-permute-done.15
  211.3 3.4 %collective-permute-done.16 = f32[41,128]{1,0:T(8,128)S(1)} collective-permute-done((f32[41,128]{1,0:T(8,128)S(1)}, f32[41,128]{1,0:T(8,128)S(1)}, u32[]{:S(2)}, u32[]{:S(2)}) %collective-permute-start.16) | collective-permute-done | bytes 21024 | tf_op jit(solution)/shard_map/ppermute | solution.py:125
  214.7 1.7 collective-permute-start.17
  216.5 3.4 %collective-permute-done.17 = f32[49,128]{1,0:T(8,128)S(1)} collective-permute-done((f32[49,128]{1,0:T(8,128)S(1)}, f32[49,128]{1,0:T(8,128)S(1)}, u32[]{:S(2)}, u32[]{:S(2)}) %collective-permute-start.17) | collective-permute-done | bytes 25120 | tf_op jit(solution)/shard_map/ppermute | solution.py:125
  222.0 5.8 %cholesky.55 = f32[64,64]{1,0:T(8,128)S(1)} custom-call(f32[64,64]{1,0:T(8,128)S(1)} %fusion.23), custom_call_target="Cholesky" | custom-call | tf_op jit(solution)/shard_map/jit(cholesky)/cholesky | solution.py:176
  228.5 0.7 fusion.21
  229.2 4.9 %custom-call.7 = f32[1,64,64]{1,2,0:T(8,128)S(1)} custom-call(f32[1,64,64]{2,1,0:T(8,128)S(1)} %fusion.21), custom_call_target="InvertDiagBlocksLowerTriangular" | custom-call | tf_op jit(solution)/shard_map/jit(_solve_triangular)/triangular_solve | solution.py:177
  234.1 1.2 convolution_bitcast_fusion
  (146 shorter events, 13.4 us)
Async XLA Ops:
  0.6 1.9 copy-start
  0.6 3.5 %copy-start.2 = (bf16[1024,64]{0,1:T(8,128)(2,1)S(1)}, bf16[1024,64]{0,1:T(8,128)(2,1)}, u32[]{:S(2)}) copy-start(bf16[1024,64]{0,1:T(8,128)(2,1)} %param.19) | copy-start | bytes 393220
  4.5 8.9 %copy-start.9 = (s32[32,3]{0,1:T(4,128)S(1)}, s32[32,3]{0,1:T(4,128)}, u32[]{:S(2)}) copy-start(s32[32,3]{0,1:T(4,128)} %param.20) | copy-start | bytes 1156
  7.4 44.0 %collective-permute-start = (bf16[1110,768]{1,0:T(8,128)(2,1)}, bf16[1110,768]{1,0:T(8,128)(2,1)}, u32[]{:S(2)}, u32[]{:S(2)}) collective-permute-start(bf16[1110,768]{1,0:T(8,128)(2,1)} %pad_maximum_fusion), channel_id=1, source_target_pairs={{4,0},{8,4},{12,8},{16,12},{20,16},{24,20},{28,24},{0,28},{5,1},{9... | collective-permute-start | bytes 5114888 | tf_op jit(solution)/shard_map/ppermute | solution.py:19
  13.4 74.4 %collective-permute-start.1 = (bf16[1110,768]{1,0:T(8,128)(2,1)}, bf16[1110,768]{1,0:T(8,128)(2,1)}, u32[]{:S(2)}, u32[]{:S(2)}) collective-permute-start(bf16[1110,768]{1,0:T(8,128)(2,1)} %pad_maximum_fusion), channel_id=1, source_target_pairs={{24,0},{28,4},{0,8},{4,12},{8,16},{12,20},{16,24},{20,28},{25,1},{... | collective-permute-start | bytes 5114888 | tf_op jit(solution)/shard_map/ppermute | solution.py:19
  90.4 3.4 %copy-start.3 = (bf16[1024,768]{1,0:T(8,128)(2,1)}, bf16[1024,768]{1,0:T(8,128)(2,1)S(1)}, u32[]{:S(2)}) copy-start(bf16[1024,768]{1,0:T(8,128)(2,1)S(1)} %slice.188) | copy-start | bytes 4718596
  90.4 3.3 %copy-start.1 = (bf16[1024,768]{1,0:T(8,128)(2,1)S(1)}, bf16[1024,768]{1,0:T(8,128)(2,1)}, u32[]{:S(2)}) copy-start(bf16[1024,768]{1,0:T(8,128)(2,1)} %fusion.3) | copy-start | bytes 4718596
  101.6 0.7 copy-start.4
  105.1 13.7 %collective-permute-start.2 = (f32[520,128]{1,0:T(8,128)}, f32[520,128]{1,0:T(8,128)S(1)}, u32[]{:S(2)}, u32[]{:S(2)}) collective-permute-start(f32[520,128]{1,0:T(8,128)} %pad_maximum_fusion.1), channel_id=1, source_target_pairs={{28,0},{0,4},{4,8},{8,12},{12,16},{16,20},{20,24},{24,28},{29,1},{... | collective-permute-start | bytes 798728 | tf_op jit(solution)/shard_map/ppermute | solution.py:19
  106.7 0.7 copy-start.5
  106.7 0.7 copy-start.7
  108.6 23.6 %collective-permute-start.3 = (f32[520,128]{1,0:T(8,128)}, f32[520,128]{1,0:T(8,128)}, u32[]{:S(2)}, u32[]{:S(2)}) collective-permute-start(f32[520,128]{1,0:T(8,128)} %pad_maximum_fusion.2), channel_id=1, source_target_pairs={{8,0},{12,4},{16,8},{20,12},{24,16},{28,20},{0,24},{4,28},{9,1},{1... | collective-permute-start | bytes 798728 | tf_op jit(solution)/shard_map/ppermute | solution.py:19
  118.8 14.7 %copy-start.8 = (f32[1024]{0:T(1024)S(1)}, f32[1024]{0:T(1024)}, u32[]{:S(2)}) copy-start(f32[1024]{0:T(1024)} %copy-done.7) | copy-start | bytes 12292
  118.8 14.7 %copy-start.10 = (f32[1024]{0:T(1024)S(1)}, f32[1024]{0:T(1024)}, u32[]{:S(2)}) copy-start(f32[1024]{0:T(1024)} %get-tuple-element.165) | copy-start | bytes 12292
  118.8 0.7 copy-start.6
  138.0 1.2 collective-permute-start.4
  139.3 3.8 %collective-permute-start.5 = (f32[35,128]{1,0:T(8,128)S(1)}, f32[35,128]{1,0:T(8,128)S(1)}, u32[]{:S(2)}, u32[]{:S(2)}) collective-permute-start(f32[35,128]{1,0:T(8,128)S(1)} %pad_maximum_fusion.8), channel_id=1, source_target_pairs={{0,2},{1,3},{2,0},{3,1},{4,6},{5,7},{6,4},{7,5},{8,10},{9,11},{10,... | collective-permute-start | bytes 53768 | tf_op jit(solution)/shard_map/ppermute | solution.py:125
  143.2 4.7 %collective-permute-start.6 = (f32[37,128]{1,0:T(8,128)S(1)}, f32[37,128]{1,0:T(8,128)S(1)}, u32[]{:S(2)}, u32[]{:S(2)}) collective-permute-start(f32[37,128]{1,0:T(8,128)S(1)} %pad_maximum_fusion.9), channel_id=1, source_target_pairs={{0,4},{4,0},{8,12},{12,8},{16,20},{20,16},{24,28},{28,24},{1,5},{5... | collective-permute-start | bytes 56840 | tf_op jit(solution)/shard_map/ppermute | solution.py:125
  147.9 3.9 %collective-permute-start.7 = (f32[41,128]{1,0:T(8,128)S(1)}, f32[41,128]{1,0:T(8,128)S(1)}, u32[]{:S(2)}, u32[]{:S(2)}) collective-permute-start(f32[41,128]{1,0:T(8,128)S(1)} %pad_maximum_fusion.5), channel_id=1, source_target_pairs={{0,8},{4,12},{8,0},{12,4},{16,24},{20,28},{24,16},{28,20},{1,9},{5... | collective-permute-start | bytes 62984 | tf_op jit(solution)/shard_map/ppermute | solution.py:125
  151.8 4.8 %collective-permute-start.8 = (f32[49,128]{1,0:T(8,128)S(1)}, f32[49,128]{1,0:T(8,128)S(1)}, u32[]{:S(2)}, u32[]{:S(2)}) collective-permute-start(f32[49,128]{1,0:T(8,128)S(1)} %pad_maximum_fusion.3), channel_id=1, source_target_pairs={{0,16},{4,20},{8,24},{12,28},{16,0},{20,4},{24,8},{28,12},{1,17},{... | collective-permute-start | bytes 75272 | tf_op jit(solution)/shard_map/ppermute | solution.py:125
  171.3 8.0 %collective-permute-start.9 = (bf16[1024,64]{0,1:T(8,128)(2,1)S(1)}, bf16[1024,64]{0,1:T(8,128)(2,1)S(1)}, u32[]{:S(2)}, u32[]{:S(2)}) collective-permute-start(bf16[1024,64]{0,1:T(8,128)(2,1)S(1)} %bitcast.100), channel_id=1, source_target_pairs={{4,0},{8,4},{12,8},{16,12},{20,16},{24,20},{28,24},{0,28},{5,1},{9... | collective-permute-start | bytes 393224 | tf_op jit(solution)/shard_map/ppermute | solution.py:19
  176.8 6.9 %collective-permute-start.10 = (bf16[1024,64]{0,1:T(8,128)(2,1)S(1)}, bf16[1024,64]{0,1:T(8,128)(2,1)S(1)}, u32[]{:S(2)}, u32[]{:S(2)}) collective-permute-start(bf16[1024,64]{0,1:T(8,128)(2,1)S(1)} %bitcast.101), channel_id=1, source_target_pairs={{24,0},{28,4},{0,8},{4,12},{8,16},{12,20},{16,24},{20,28},{25,1},{... | collective-permute-start | bytes 393224 | tf_op jit(solution)/shard_map/ppermute | solution.py:19
  184.6 11.6 %collective-permute-start.11 = (f32[1024,64]{0,1:T(8,128)}, f32[1024,64]{0,1:T(8,128)}, u32[]{:S(2)}, u32[]{:S(2)}) collective-permute-start(f32[1024,64]{0,1:T(8,128)} %add.232), channel_id=1, source_target_pairs={{28,0},{0,4},{4,8},{8,12},{12,16},{16,20},{20,24},{24,28},{29,1},{... | collective-permute-start | bytes 786440 | tf_op jit(solution)/shard_map/ppermute | solution.py:19
  190.4 6.9 %collective-permute-start.12 = (f32[1024,64]{0,1:T(8,128)S(1)}, f32[1024,64]{0,1:T(8,128)S(1)}, u32[]{:S(2)}, u32[]{:S(2)}) collective-permute-start(f32[1024,64]{0,1:T(8,128)S(1)} %add.234), channel_id=1, source_target_pairs={{8,0},{12,4},{16,8},{20,12},{24,16},{28,20},{0,24},{4,28},{9,1},{1... | collective-permute-start | bytes 786440 | tf_op jit(solution)/shard_map/ppermute | solution.py:19
  199.8 1.2 collective-permute-start.13
  201.1 4.7 %collective-permute-start.14 = (f32[35,128]{1,0:T(8,128)S(1)}, f32[35,128]{1,0:T(8,128)S(1)}, u32[]{:S(2)}, u32[]{:S(2)}) collective-permute-start(f32[35,128]{1,0:T(8,128)S(1)} %pad_maximum_fusion.11), channel_id=1, source_target_pairs={{0,2},{1,3},{2,0},{3,1},{4,6},{5,7},{6,4},{7,5},{8,10},{9,11},{10,... | collective-permute-start | bytes 53768 | tf_op jit(solution)/shard_map/ppermute | solution.py:125
  205.8 5.0 %collective-permute-start.15 = (f32[37,128]{1,0:T(8,128)S(1)}, f32[37,128]{1,0:T(8,128)S(1)}, u32[]{:S(2)}, u32[]{:S(2)}) collective-permute-start(f32[37,128]{1,0:T(8,128)S(1)} %pad_maximum_fusion.12), channel_id=1, source_target_pairs={{0,4},{4,0},{8,12},{12,8},{16,20},{20,16},{24,28},{28,24},{1,5},{5... | collective-permute-start | bytes 56840 | tf_op jit(solution)/shard_map/ppermute | solution.py:125
  210.8 3.9 %collective-permute-start.16 = (f32[41,128]{1,0:T(8,128)S(1)}, f32[41,128]{1,0:T(8,128)S(1)}, u32[]{:S(2)}, u32[]{:S(2)}) collective-permute-start(f32[41,128]{1,0:T(8,128)S(1)} %pad_maximum_fusion.6), channel_id=1, source_target_pairs={{0,8},{4,12},{8,0},{12,4},{16,24},{20,28},{24,16},{28,20},{1,9},{5... | collective-permute-start | bytes 62984 | tf_op jit(solution)/shard_map/ppermute | solution.py:125
  214.7 5.1 %collective-permute-start.17 = (f32[49,128]{1,0:T(8,128)S(1)}, f32[49,128]{1,0:T(8,128)S(1)}, u32[]{:S(2)}, u32[]{:S(2)}) collective-permute-start(f32[49,128]{1,0:T(8,128)S(1)} %pad_maximum_fusion.4), channel_id=1, source_target_pairs={{0,16},{4,20},{8,24},{12,28},{16,0},{20,4},{24,8},{28,12},{1,17},{... | collective-permute-start | bytes 75272 | tf_op jit(solution)/shard_map/ppermute | solution.py:125

commit v5 on v4

--- a/solution.py
+++ b/solution.py
@@ -67,11 +67,16 @@
     )
 
 
-def first_pass(owned, left_unit, right_unit, left_weights, right_weights):
-    block_rows = left_unit.shape[0]
-    vector_count = left_weights.shape[1]
+def unpack(packed, block_rows, vector_count):
+    weights = packed[block_rows:].reshape(-1)[: block_rows * vector_count]
+    return packed[:block_rows], weights.reshape(block_rows, vector_count)
+
+
+def first_pass(owned, left_packed, right_packed, block_rows, vector_count):
 
     def compute_pair():
+        left_unit, left_weights = unpack(left_packed, block_rows, vector_count)
+        right_unit, right_weights = unpack(right_packed, block_rows, vector_count)
         affinity = scores_tile(left_unit, right_unit)
         return (
             affinity,
@@ -198,17 +203,12 @@
         own_row = lax.dynamic_slice_in_dim(neighbours, block_at(left), 1, 0)[0]
         owned_list.append(jnp.any(own_row == block_at(right)))
 
-    units = {0: unit_block}
-    weights = {0: start}
     unit_width = unit_block.shape[1]
     vector_count = start.shape[1]
     packed = jnp.concatenate([unit_block, as_rows(start.reshape(-1), unit_width)])
+    units = {0: packed}
     for offset in fetch_offsets:
-        arrived = shifted(packed, "wide", -offset)
-        units[offset] = arrived[:block_rows]
-        weights[offset] = (
-            arrived[block_rows:].reshape(-1)[: block_rows * vector_count].reshape(block_rows, vector_count)
-        )
+        units[offset] = shifted(packed, "wide", -offset)
 
     self_mask = lax.broadcasted_iota(
         jnp.int32, (block_rows, block_rows), 0
@@ -217,7 +217,6 @@
         self_mask, jnp.zeros((), jnp.bfloat16), scores_tile(unit_block, unit_block)
     )
 
-    vector_count = start.shape[1]
     zero_part = jnp.zeros((block_rows, vector_count), jnp.float32)
     zero_sum = jnp.zeros((block_rows,), jnp.float32)
     parts = {offset: zero_part for offset in units}
@@ -225,7 +224,7 @@
     tiles = []
     for (left, right), owned in zip(pair_plan, owned_list):
         affinity, row_part, row_sum, col_part, col_sum = first_pass(
-            owned, units[left], units[right], weights[left], weights[right]
+            owned, units[left], units[right], block_rows, vector_count
         )
         tiles.append(affinity)
         parts[left] = parts[left] + row_part

time: 238 us -> 239 us (level)
  matrix products: 21.2 us -> 37.1 us
  waiting for transfers between devices: 110 us -> 100 us
  local copies, waits for them, and re-layouts: 17.2 us -> 12.1 us
    ppermute x10, starting transfers between devices: 14.9 us -> 27.5 us  [butterfly(): other = lax.ppermute(block, axis, route)]
    ppermute x8, starting transfers between devices: 27 us -> 14.9 us  [shifted(): return lax.ppermute(block, axis, route)]
    dot_general x2 -> x3, matrix products: 7.86 us -> 14.8 us  [scores_tile(): lax.dot_general(leftside_block, right_block, (((1,), (1,)), ((), ())), pr...]
    ppermute x8, waiting for transfers between devices: 87.2 us -> 81.8 us  [shifted(): return lax.ppermute(block, axis, route)]
    dot_general x4 -> x6, matrix products: 5.64 us -> 10.3 us  [row_product(): return jnp.dot(affinity, weights, preferred_element_type=jnp.float32)]
    ppermute x10, waiting for transfers between devices: 23.3 us -> 18.7 us  [butterfly(): other = lax.ppermute(block, axis, route)]
    dot_general x2 -> x4, matrix products: 4.14 us -> 8.38 us  [col_product(): lax.dot_general(affinity, weights, (((0,), (0,)), ((), ())), preferred_el...]
    slice x8 -> x7, local copies, waits for them, and re-layouts: 7.08 us -> 3.32 us  [unpack(): weights = packed[block_rows:].reshape(-1)[:block_rows * vector_count]]
  transfers between devices with their start and end apart: 18 -> 18, of which waited for: 16 -> 17; matrix products, arithmetic and copies ran while one was open for 6% -> 10% of each run, Pallas kernels for 0% -> 0%
where the time goes in v5:
time: 239 us; the launch traced here: 237 us
  waiting for transfers between devices  100 us (42%)
  starting transfers between devices  42.4 us (18%)
  other arithmetic  41.8 us (17%)
  matrix products  37.1 us (16%)
  local copies, waits for them, and re-layouts  12.1 us (5%)
  between operations  3.17 us (1%)
    ppermute x8, waiting for transfers between devices, shifted(): return lax.ppermute(block, axis, route)  81.8 us
    ppermute x10, starting transfers between devices, butterfly(): other = lax.ppermute(block, axis, route)  27.5 us
    ppermute x10, waiting for transfers between devices, butterfly(): other = lax.ppermute(block, axis, route)  18.7 us
    ppermute x8, starting transfers between devices, shifted(): return lax.ppermute(block, axis, route)  14.9 us
    dot_general x3, matrix products, scores_tile(): lax.dot_general(leftside_block, right_block, (((1,), (1,)), ((), ())), pr...  14.8 us
    another operation x6, other arithmetic, orthonormal(): normalizer_coefficient = jnp.linalg.cholesky(gram_matrix)  13 us
    another operation x4, other arithmetic, orthonormal(): jax.scipy.linalg.solve_triangular(normalizer_coefficient, displaced_entri...  11.1 us
    dot_general x6, matrix products, row_product(): return jnp.dot(affinity, weights, preferred_element_type=jnp.float32)  10.3 us
  transfers between devices with their start and end apart: 18, of which 17 were waited for; matrix products, arithmetic and copies ran while one was open for 10% of the time, Pallas kernels for 0%

profile of v5, /device:TPU:0, one launch (start us, length us, event | category | flops | bytes accessed | tf_op | source)
XLA Modules:
  0.0 237.2 jit_solution(16133207269283166695)
XLA Ops:
  0.7 1.9 fusion.13
  2.6 1.7 fusion.15
  4.8 2.7 %pad_maximum_fusion = bf16[1110,768]{1,0:T(8,128)(2,1)} fusion(bf16[86,768]{1,0:T(8,128)(2,1)S(1)} %reshape.148, bf16[1024,768]{1,0:T(8,128)(2,1)} %fusion.15), kind=kLoop, calls=%fused_computation.30 | loop fusion | flops 3409920 | bytes 3409920 | tf_op jit(solution)/shard_map/concatenate | solution.py:208
  7.5 6.0 %collective-permute-start = (bf16[1110,768]{1,0:T(8,128)(2,1)}, bf16[1110,768]{1,0:T(8,128)(2,1)}, u32[]{:S(2)}, u32[]{:S(2)}) collective-permute-start(bf16[1110,768]{1,0:T(8,128)(2,1)} %pad_maximum_fusion), channel_id=1, source_target_pairs={{4,0},{8,4},{12,8},{16,12},{20,16},{24,20},{28,24},{0,28},{5,1},{9... | collective-permute-start | bytes 5114888 | tf_op jit(solution)/shard_map/ppermute | solution.py:19
  13.5 0.8 fusion.50
  16.3 4.5 %convert_reduce_fusion.6 = (f32[1024]{0:T(1024)}, bf16[1024,1024]{0,1:T(8,128)(2,1)S(1)}) fusion(bf16[1024,768]{1,0:T(8,128)(2,1)} %fusion.15), kind=kOutput, calls=%fused_computation.21 | convolution fusion | flops 1616903168 | bytes 3674112 | tf_op jit(solution)/shard_map/dot_general | solution.py:54
  20.7 30.7 %collective-permute-done = bf16[1110,768]{1,0:T(8,128)(2,1)} collective-permute-done((bf16[1110,768]{1,0:T(8,128)(2,1)}, bf16[1110,768]{1,0:T(8,128)(2,1)}, u32[]{:S(2)}, u32[]{:S(2)}) %collective-permute-start) | collective-permute-done | bytes 1704992 | tf_op jit(solution)/shard_map/ppermute | solution.py:19
  51.5 36.4 %collective-permute-done.1 = bf16[1110,768]{1,0:T(8,128)(2,1)} collective-permute-done((bf16[1110,768]{1,0:T(8,128)(2,1)}, bf16[1110,768]{1,0:T(8,128)(2,1)}, u32[]{:S(2)}, u32[]{:S(2)}) %collective-permute-start.1) | collective-permute-done | bytes 1704992 | tf_op jit(solution)/shard_map/ppermute | solution.py:19
  87.8 11.9 %conditional.8 = (bf16[1024,1024]{1,0:T(8,128)(2,1)}, f32[1024,64]{0,1:T(8,128)S(1)}, f32[1024]{0:T(1024)S(1)}, f32[1024,64]{0,1:T(8,128)S(1)}, f32[1024]{0:T(1024)S(1)}) conditional(s32[]{:T(128)} %convert_element_type.61, () %tuple.62, (bf16[1110,768]{1,0:T(8,128)(2,1)}, bf16[1110,768]{1,0:T(8,128)(2,1)}) %tuple.63), branch_computations={%region_12.13_spmd, %region_13.16_spmd} | conditional | flops 1884289024 | bytes 11550760 | solution.py:100
  87.8 5.2 %convert_reduce_fusion.4 = (f32[1024]{0:T(1024)S(1)}, f32[1024]{0:T(1024)S(1)}, bf16[1024,1024]{1,0:T(8,128)(2,1)}) fusion(bf16[1110,768]{1,0:T(8,128)(2,1)} %get-tuple-element.43, bf16[1110,768]{1,0:T(8,128)(2,1)} %get-tuple-element.42), kind=kOutput, calls=%fused_computation.12 | convolution fusion | flops 1615853568 | bytes 5251072 | tf_op jit(solution)/shard_map/cond/branch_1_fun/dot_general | solution.py:54
  93.0 0.9 slice.148
  94.1 2.4 fusion.10
  96.5 0.9 slice.151
  97.6 2.1 fusion.8
  99.7 3.0 %conditional.6 = (bf16[1024,1024]{1,0:T(8,128)(2,1)}, f32[1024,64]{0,1:T(8,128)}, f32[1024]{0:T(1024)S(1)}, f32[1024,64]{0,1:T(8,128)S(1)}, f32[1024]{0:T(1024)}) conditional(s32[]{:T(128)} %convert_element_type.59, () %tuple.58, (bf16[1110,768]{1,0:T(8,128)(2,1)}, bf16[1024,768]{1,0:T(8,128)(2,1)}, bf16[66048]{0:T(1024)(128)(2,1)S(1)}) %tuple.59), branch_computations={%region_2.3_spmd, %region_3.0_spmd} | conditional | flops 1884289024 | bytes 11415592 | solution.py:100
  99.8 1.6 broadcast.124
  104.5 10.9 %conditional.7 = (bf16[1024,1024]{1,0:T(8,128)(2,1)}, f32[1024,64]{0,1:T(8,128)S(1)}, f32[1024]{0:T(1024)S(1)}, f32[1024,64]{0,1:T(8,128)S(1)}, f32[1024]{0:T(1024)S(1)}) conditional(s32[]{:T(128)} %convert_element_type.60, () %tuple.60, (bf16[1110,768]{1,0:T(8,128)(2,1)}, bf16[1024,768]{1,0:T(8,128)(2,1)}, bf16[66048]{0:T(1024)(128)(2,1)S(1)}) %tuple.61), branch_computations={%region_7.8_spmd, %region_8.11_spmd} | conditional | flops 1884289024 | bytes 11415592 | solution.py:100
  104.5 5.2 %convert_reduce_fusion.2 = (f32[1024]{0:T(1024)S(1)}, f32[1024]{0:T(1024)S(1)}, bf16[1024,1024]{1,0:T(8,128)(2,1)}) fusion(bf16[1024,768]{1,0:T(8,128)(2,1)} %get-tuple-element.40, bf16[1110,768]{1,0:T(8,128)(2,1)} %get-tuple-element.39), kind=kOutput, calls=%fused_computation.6 | convolution fusion | flops 1615853568 | bytes 5251072 | tf_op jit(solution)/shard_map/cond/branch_1_fun/dot_general | solution.py:54
  109.7 0.9 slice.143
  110.8 2.1 fusion.4
  113.1 2.4 fusion.63
  116.6 1.8 collective-permute-start.3
  118.9 1.0 slice.230
  120.2 3.1 %collective-permute-done.3 = f32[520,128]{1,0:T(8,128)} collective-permute-done((f32[520,128]{1,0:T(8,128)}, f32[520,128]{1,0:T(8,128)}, u32[]{:S(2)}, u32[]{:S(2)}) %collective-permute-start.3) | collective-permute-done | bytes 266272 | tf_op jit(solution)/shard_map/ppermute | solution.py:19
  123.3 1.0 slice.231
  124.6 1.3 broadcast_multiply_fusion
  125.9 1.2 fusion.51
  129.2 7.2 %collective-permute-start.4 = (f32[34,128]{1,0:T(8,128)S(1)}, f32[34,128]{1,0:T(8,128)S(1)}, u32[]{:S(2)}, u32[]{:S(2)}) collective-permute-start(f32[34,128]{1,0:T(8,128)S(1)} %pad_maximum_fusion.7), channel_id=1, source_target_pairs={{0,1},{1,0},{2,3},{3,2},{4,5},{5,4},{6,7},{7,6},{8,9},{9,8},{10,11... | collective-permute-start | bytes 52232 | tf_op jit(solution)/shard_map/ppermute | solution.py:130
  136.4 0.8 collective-permute-done.4
  137.2 4.9 %collective-permute-start.5 = (f32[35,128]{1,0:T(8,128)S(1)}, f32[35,128]{1,0:T(8,128)S(1)}, u32[]{:S(2)}, u32[]{:S(2)}) collective-permute-start(f32[35,128]{1,0:T(8,128)S(1)} %pad_maximum_fusion.8), channel_id=1, source_target_pairs={{0,2},{1,3},{2,0},{3,1},{4,6},{5,7},{6,4},{7,5},{8,10},{9,11},{10,... | collective-permute-start | bytes 53768 | tf_op jit(solution)/shard_map/ppermute | solution.py:130
  142.1 1.8 collective-permute-done.5
  143.9 2.4 %collective-permute-start.6 = (f32[37,128]{1,0:T(8,128)S(1)}, f32[37,128]{1,0:T(8,128)S(1)}, u32[]{:S(2)}, u32[]{:S(2)}) collective-permute-start(f32[37,128]{1,0:T(8,128)S(1)} %pad_maximum_fusion.9), channel_id=1, source_target_pairs={{0,4},{4,0},{8,12},{12,8},{16,20},{20,16},{24,28},{28,24},{1,5},{5... | collective-permute-start | bytes 56840 | tf_op jit(solution)/shard_map/ppermute | solution.py:130
  146.3 1.8 collective-permute-done.6
  148.1 1.5 collective-permute-start.7
  149.6 2.4 collective-permute-done.7
  152.0 2.6 %collective-permute-start.8 = (f32[49,128]{1,0:T(8,128)S(1)}, f32[49,128]{1,0:T(8,128)S(1)}, u32[]{:S(2)}, u32[]{:S(2)}) collective-permute-start(f32[49,128]{1,0:T(8,128)S(1)} %pad_maximum_fusion.3), channel_id=1, source_target_pairs={{0,16},{4,20},{8,24},{12,28},{16,0},{20,4},{24,8},{28,12},{1,17},{... | collective-permute-start | bytes 75272 | tf_op jit(solution)/shard_map/ppermute | solution.py:130
  154.6 2.2 collective-permute-done.8
  159.0 5.8 %cholesky.44 = f32[64,64]{1,0:T(8,128)S(1)} custom-call(f32[64,64]{1,0:T(8,128)S(1)} %fusion.37), custom_call_target="Cholesky" | custom-call | tf_op jit(solution)/shard_map/jit(cholesky)/cholesky | solution.py:181
  166.2 4.9 %custom-call.6 = f32[1,64,64]{1,2,0:T(8,128)S(1)} custom-call(f32[1,64,64]{2,1,0:T(8,128)S(1)} %fusion.32), custom_call_target="InvertDiagBlocksLowerTriangular" | custom-call | tf_op jit(solution)/shard_map/jit(_solve_triangular)/triangular_solve | solution.py:182
  171.5 5.5 %collective-permute-start.9 = (bf16[1024,64]{0,1:T(8,128)(2,1)S(1)}, bf16[1024,64]{0,1:T(8,128)(2,1)S(1)}, u32[]{:S(2)}, u32[]{:S(2)}) collective-permute-start(bf16[1024,64]{0,1:T(8,128)(2,1)S(1)} %bitcast.92), channel_id=1, source_target_pairs={{4,0},{8,4},{12,8},{16,12},{20,16},{24,20},{28,24},{0,28},{5,1},{9... | collective-permute-start | bytes 393224 | tf_op jit(solution)/shard_map/ppermute | solution.py:19
  177.0 2.5 %collective-permute-done.9 = bf16[1024,64]{0,1:T(8,128)(2,1)S(1)} collective-permute-done((bf16[1024,64]{0,1:T(8,128)(2,1)S(1)}, bf16[1024,64]{0,1:T(8,128)(2,1)S(1)}, u32[]{:S(2)}, u32[]{:S(2)}) %collective-permute-start.9) | collective-permute-done | bytes 131104 | tf_op jit(solution)/shard_map/ppermute | solution.py:19
  179.6 4.2 %collective-permute-done.10 = bf16[1024,64]{0,1:T(8,128)(2,1)S(1)} collective-permute-done((bf16[1024,64]{0,1:T(8,128)(2,1)S(1)}, bf16[1024,64]{0,1:T(8,128)(2,1)S(1)}, u32[]{:S(2)}, u32[]{:S(2)}) %collective-permute-start.10) | collective-permute-done | bytes 131104 | tf_op jit(solution)/shard_map/ppermute | solution.py:19
  183.8 4.4 %conditional.11 = (f32[1024,64]{0,1:T(8,128)S(1)}, f32[1024,64]{0,1:T(8,128)S(1)}) conditional(s32[]{:T(128)} %convert_element_type.61, () %tuple.68, (bf16[1024,1024]{1,0:T(8,128)(2,1)}, bf16[1024,64]{0,1:T(8,128)(2,1)S(1)}, bf16[1024,64]{0,1:T(8,128)(2,1)S(1)}) %tuple.69), branch_computations={%region_27.30_spmd, %region_28.31_spmd} | conditional | flops 268435456 | bytes 4980752 | solution.py:114
  183.8 2.3 fusion.60
  186.1 2.1 fusion.61
  188.2 0.7 add.232
  188.9 4.4 %conditional.10 = (f32[1024,64]{0,1:T(8,128)S(1)}, f32[1024,64]{0,1:T(8,128)S(1)}) conditional(s32[]{:T(128)} %convert_element_type.60, () %tuple.66, (bf16[1024,1024]{1,0:T(8,128)(2,1)}, bf16[1024,64]{0,1:T(8,128)(2,1)S(1)}, bf16[1024,64]{0,1:T(8,128)(2,1)S(1)}) %tuple.105), branch_computations={%region_25.28_spmd, %region_26.29_spmd} | conditional | flops 268435456 | bytes 4980752 | solution.py:114
  188.9 2.3 fusion.58
  191.3 2.1 fusion.59
  193.4 1.6 collective-permute-start.12
  195.5 4.8 %collective-permute-done.11 = f32[1024,64]{0,1:T(8,128)} collective-permute-done((f32[1024,64]{0,1:T(8,128)}, f32[1024,64]{0,1:T(8,128)}, u32[]{:S(2)}, u32[]{:S(2)}) %collective-permute-start.11) | collective-permute-done | bytes 262176 | tf_op jit(solution)/shard_map/ppermute | solution.py:19
  200.3 1.1 fusion.52
  203.0 1.2 collective-permute-done.13
  204.2 3.1 %collective-permute-start.14 = (f32[35,128]{1,0:T(8,128)S(1)}, f32[35,128]{1,0:T(8,128)S(1)}, u32[]{:S(2)}, u32[]{:S(2)}) collective-permute-start(f32[35,128]{1,0:T(8,128)S(1)} %pad_maximum_fusion.11), channel_id=1, source_target_pairs={{0,2},{1,3},{2,0},{3,1},{4,6},{5,7},{6,4},{7,5},{8,10},{9,11},{10,... | collective-permute-start | bytes 53768 | tf_op jit(solution)/shard_map/ppermute | solution.py:130
  207.3 1.8 collective-permute-done.14
  209.1 2.0 collective-permute-start.15
  211.1 1.9 collective-permute-done.15
  213.0 1.1 collective-permute-start.16
  214.1 2.8 %collective-permute-done.16 = f32[41,128]{1,0:T(8,128)S(1)} collective-permute-done((f32[41,128]{1,0:T(8,128)S(1)}, f32[41,128]{1,0:T(8,128)S(1)}, u32[]{:S(2)}, u32[]{:S(2)}) %collective-permute-start.16) | collective-permute-done | bytes 21024 | tf_op jit(solution)/shard_map/ppermute | solution.py:130
  217.0 2.8 %collective-permute-start.17 = (f32[49,128]{1,0:T(8,128)S(1)}, f32[49,128]{1,0:T(8,128)S(1)}, u32[]{:S(2)}, u32[]{:S(2)}) collective-permute-start(f32[49,128]{1,0:T(8,128)S(1)} %pad_maximum_fusion.4), channel_id=1, source_target_pairs={{0,16},{4,20},{8,24},{12,28},{16,0},{20,4},{24,8},{28,12},{1,17},{... | collective-permute-start | bytes 75272 | tf_op jit(solution)/shard_map/ppermute | solution.py:130
  219.7 2.1 collective-permute-done.17
  223.9 5.8 %cholesky.55 = f32[64,64]{1,0:T(8,128)S(1)} custom-call(f32[64,64]{1,0:T(8,128)S(1)} %fusion.35), custom_call_target="Cholesky" | custom-call | tf_op jit(solution)/shard_map/jit(cholesky)/cholesky | solution.py:181
  231.1 4.9 %custom-call.7 = f32[1,64,64]{1,2,0:T(8,128)S(1)} custom-call(f32[1,64,64]{2,1,0:T(8,128)S(1)} %fusion.33), custom_call_target="InvertDiagBlocksLowerTriangular" | custom-call | tf_op jit(solution)/shard_map/jit(_solve_triangular)/triangular_solve | solution.py:182
  236.0 1.2 convolution_bitcast_fusion
  (134 shorter events, 18.2 us)
Async XLA Ops:
  0.6 1.9 copy-start
  0.6 3.6 %copy-start.2 = (bf16[1024,64]{0,1:T(8,128)(2,1)S(1)}, bf16[1024,64]{0,1:T(8,128)(2,1)}, u32[]{:S(2)}) copy-start(bf16[1024,64]{0,1:T(8,128)(2,1)} %param.19) | copy-start | bytes 393220
  4.6 8.9 %copy-start.4 = (s32[32,3]{0,1:T(4,128)S(1)}, s32[32,3]{0,1:T(4,128)}, u32[]{:S(2)}) copy-start(s32[32,3]{0,1:T(4,128)} %param.20) | copy-start | bytes 1156
  7.5 44.0 %collective-permute-start = (bf16[1110,768]{1,0:T(8,128)(2,1)}, bf16[1110,768]{1,0:T(8,128)(2,1)}, u32[]{:S(2)}, u32[]{:S(2)}) collective-permute-start(bf16[1110,768]{1,0:T(8,128)(2,1)} %pad_maximum_fusion), channel_id=1, source_target_pairs={{4,0},{8,4},{12,8},{16,12},{20,16},{24,20},{28,24},{0,28},{5,1},{9... | collective-permute-start | bytes 5114888 | tf_op jit(solution)/shard_map/ppermute | solution.py:19
  13.5 74.4 %collective-permute-start.1 = (bf16[1110,768]{1,0:T(8,128)(2,1)}, bf16[1110,768]{1,0:T(8,128)(2,1)}, u32[]{:S(2)}, u32[]{:S(2)}) collective-permute-start(bf16[1110,768]{1,0:T(8,128)(2,1)} %pad_maximum_fusion), channel_id=1, source_target_pairs={{24,0},{28,4},{0,8},{4,12},{8,16},{12,20},{16,24},{20,28},{25,1},{... | collective-permute-start | bytes 5114888 | tf_op jit(solution)/shard_map/ppermute | solution.py:19
  104.5 14.3 %collective-permute-start.2 = (f32[520,128]{1,0:T(8,128)}, f32[520,128]{1,0:T(8,128)}, u32[]{:S(2)}, u32[]{:S(2)}) collective-permute-start(f32[520,128]{1,0:T(8,128)} %pad_maximum_fusion.1), channel_id=1, source_target_pairs={{28,0},{0,4},{4,8},{8,12},{12,16},{16,20},{20,24},{24,28},{29,1},{... | collective-permute-start | bytes 798728 | tf_op jit(solution)/shard_map/ppermute | solution.py:19
  115.4 4.4 %copy-start.1 = (f32[1024,64]{0,1:T(8,128)}, f32[1024,64]{0,1:T(8,128)S(1)}, u32[]{:S(2)}) copy-start(f32[1024,64]{0,1:T(8,128)S(1)} %get-tuple-element.77) | copy-start | bytes 786436
  115.4 2.9 %copy-start.3 = (bf16[1024,64]{0,1:T(8,128)(2,1)S(1)}, bf16[1024,64]{0,1:T(8,128)(2,1)}, u32[]{:S(2)}) copy-start(bf16[1024,64]{0,1:T(8,128)(2,1)} %param.19) | copy-start | bytes 393220
  116.6 6.7 %collective-permute-start.3 = (f32[520,128]{1,0:T(8,128)}, f32[520,128]{1,0:T(8,128)}, u32[]{:S(2)}, u32[]{:S(2)}) collective-permute-start(f32[520,128]{1,0:T(8,128)} %pad_maximum_fusion.2), channel_id=1, source_target_pairs={{8,0},{12,4},{16,8},{20,12},{24,16},{28,20},{0,24},{4,28},{9,1},{1... | collective-permute-start | bytes 798728 | tf_op jit(solution)/shard_map/ppermute | solution.py:19
  118.9 5.8 %copy-start.5 = (f32[1024]{0:T(1024)S(1)}, f32[1024]{0:T(1024)}, u32[]{:S(2)}) copy-start(f32[1024]{0:T(1024)} %get-tuple-element.137) | copy-start | bytes 12292
  129.2 8.0 %collective-permute-start.4 = (f32[34,128]{1,0:T(8,128)S(1)}, f32[34,128]{1,0:T(8,128)S(1)}, u32[]{:S(2)}, u32[]{:S(2)}) collective-permute-start(f32[34,128]{1,0:T(8,128)S(1)} %pad_maximum_fusion.7), channel_id=1, source_target_pairs={{0,1},{1,0},{2,3},{3,2},{4,5},{5,4},{6,7},{7,6},{8,9},{9,8},{10,11... | collective-permute-start | bytes 52232 | tf_op jit(solution)/shard_map/ppermute | solution.py:130
  137.2 6.6 %collective-permute-start.5 = (f32[35,128]{1,0:T(8,128)S(1)}, f32[35,128]{1,0:T(8,128)S(1)}, u32[]{:S(2)}, u32[]{:S(2)}) collective-permute-start(f32[35,128]{1,0:T(8,128)S(1)} %pad_maximum_fusion.8), channel_id=1, source_target_pairs={{0,2},{1,3},{2,0},{3,1},{4,6},{5,7},{6,4},{7,5},{8,10},{9,11},{10,... | collective-permute-start | bytes 53768 | tf_op jit(solution)/shard_map/ppermute | solution.py:130
  143.9 4.1 %collective-permute-start.6 = (f32[37,128]{1,0:T(8,128)S(1)}, f32[37,128]{1,0:T(8,128)S(1)}, u32[]{:S(2)}, u32[]{:S(2)}) collective-permute-start(f32[37,128]{1,0:T(8,128)S(1)} %pad_maximum_fusion.9), channel_id=1, source_target_pairs={{0,4},{4,0},{8,12},{12,8},{16,20},{20,16},{24,28},{28,24},{1,5},{5... | collective-permute-start | bytes 56840 | tf_op jit(solution)/shard_map/ppermute | solution.py:130
  148.1 3.9 %collective-permute-start.7 = (f32[41,128]{1,0:T(8,128)S(1)}, f32[41,128]{1,0:T(8,128)S(1)}, u32[]{:S(2)}, u32[]{:S(2)}) collective-permute-start(f32[41,128]{1,0:T(8,128)S(1)} %pad_maximum_fusion.5), channel_id=1, source_target_pairs={{0,8},{4,12},{8,0},{12,4},{16,24},{20,28},{24,16},{28,20},{1,9},{5... | collective-permute-start | bytes 62984 | tf_op jit(solution)/shard_map/ppermute | solution.py:130
  152.0 4.8 %collective-permute-start.8 = (f32[49,128]{1,0:T(8,128)S(1)}, f32[49,128]{1,0:T(8,128)S(1)}, u32[]{:S(2)}, u32[]{:S(2)}) collective-permute-start(f32[49,128]{1,0:T(8,128)S(1)} %pad_maximum_fusion.3), channel_id=1, source_target_pairs={{0,16},{4,20},{8,24},{12,28},{16,0},{20,4},{24,8},{28,12},{1,17},{... | collective-permute-start | bytes 75272 | tf_op jit(solution)/shard_map/ppermute | solution.py:130
  171.5 8.0 %collective-permute-start.9 = (bf16[1024,64]{0,1:T(8,128)(2,1)S(1)}, bf16[1024,64]{0,1:T(8,128)(2,1)S(1)}, u32[]{:S(2)}, u32[]{:S(2)}) collective-permute-start(bf16[1024,64]{0,1:T(8,128)(2,1)S(1)} %bitcast.92), channel_id=1, source_target_pairs={{4,0},{8,4},{12,8},{16,12},{20,16},{24,20},{28,24},{0,28},{5,1},{9... | collective-permute-start | bytes 393224 | tf_op jit(solution)/shard_map/ppermute | solution.py:19
  177.0 6.8 %collective-permute-start.10 = (bf16[1024,64]{0,1:T(8,128)(2,1)S(1)}, bf16[1024,64]{0,1:T(8,128)(2,1)S(1)}, u32[]{:S(2)}, u32[]{:S(2)}) collective-permute-start(bf16[1024,64]{0,1:T(8,128)(2,1)S(1)} %bitcast.93), channel_id=1, source_target_pairs={{24,0},{28,4},{0,8},{4,12},{8,16},{12,20},{16,24},{20,28},{25,1},{... | collective-permute-start | bytes 393224 | tf_op jit(solution)/shard_map/ppermute | solution.py:19
  188.9 11.3 %collective-permute-start.11 = (f32[1024,64]{0,1:T(8,128)}, f32[1024,64]{0,1:T(8,128)}, u32[]{:S(2)}, u32[]{:S(2)}) collective-permute-start(f32[1024,64]{0,1:T(8,128)} %add.232), channel_id=1, source_target_pairs={{28,0},{0,4},{4,8},{8,12},{12,16},{16,20},{20,24},{24,28},{29,1},{... | collective-permute-start | bytes 786440 | tf_op jit(solution)/shard_map/ppermute | solution.py:19
  193.4 6.9 %collective-permute-start.12 = (f32[1024,64]{0,1:T(8,128)S(1)}, f32[1024,64]{0,1:T(8,128)S(1)}, u32[]{:S(2)}, u32[]{:S(2)}) collective-permute-start(f32[1024,64]{0,1:T(8,128)S(1)} %add.234), channel_id=1, source_target_pairs={{8,0},{12,4},{16,8},{20,12},{24,16},{28,20},{0,24},{4,28},{9,1},{1... | collective-permute-start | bytes 786440 | tf_op jit(solution)/shard_map/ppermute | solution.py:19
  202.9 1.2 collective-permute-start.13
  204.2 4.9 %collective-permute-start.14 = (f32[35,128]{1,0:T(8,128)S(1)}, f32[35,128]{1,0:T(8,128)S(1)}, u32[]{:S(2)}, u32[]{:S(2)}) collective-permute-start(f32[35,128]{1,0:T(8,128)S(1)} %pad_maximum_fusion.11), channel_id=1, source_target_pairs={{0,2},{1,3},{2,0},{3,1},{4,6},{5,7},{6,4},{7,5},{8,10},{9,11},{10,... | collective-permute-start | bytes 53768 | tf_op jit(solution)/shard_map/ppermute | solution.py:130
  209.1 3.8 %collective-permute-start.15 = (f32[37,128]{1,0:T(8,128)S(1)}, f32[37,128]{1,0:T(8,128)S(1)}, u32[]{:S(2)}, u32[]{:S(2)}) collective-permute-start(f32[37,128]{1,0:T(8,128)S(1)} %pad_maximum_fusion.12), channel_id=1, source_target_pairs={{0,4},{4,0},{8,12},{12,8},{16,20},{20,16},{24,28},{28,24},{1,5},{5... | collective-permute-start | bytes 56840 | tf_op jit(solution)/shard_map/ppermute | solution.py:130
  213.0 3.9 %collective-permute-start.16 = (f32[41,128]{1,0:T(8,128)S(1)}, f32[41,128]{1,0:T(8,128)S(1)}, u32[]{:S(2)}, u32[]{:S(2)}) collective-permute-start(f32[41,128]{1,0:T(8,128)S(1)} %pad_maximum_fusion.6), channel_id=1, source_target_pairs={{0,8},{4,12},{8,0},{12,4},{16,24},{20,28},{24,16},{28,20},{1,9},{5... | collective-permute-start | bytes 62984 | tf_op jit(solution)/shard_map/ppermute | solution.py:130
  217.0 4.8 %collective-permute-start.17 = (f32[49,128]{1,0:T(8,128)S(1)}, f32[49,128]{1,0:T(8,128)S(1)}, u32[]{:S(2)}, u32[]{:S(2)}) collective-permute-start(f32[49,128]{1,0:T(8,128)S(1)} %pad_maximum_fusion.4), channel_id=1, source_target_pairs={{0,16},{4,20},{8,24},{12,28},{16,0},{20,4},{24,8},{28,12},{1,17},{... | collective-permute-start | bytes 75272 | tf_op jit(solution)/shard_map/ppermute | solution.py:130

commit v6 on v5

--- a/solution.py
+++ b/solution.py
@@ -149,9 +149,10 @@
     return jnp.dot(left, right, precision=lax.Precision.HIGHEST, preferred_element_type=jnp.float32)
 
 
-def orthonormal(product, vertex_valence, total_rows):
+def orthonormal(product, vertex_valence, total_rows, fetch_offsets=()):
     block_rows, vector_count = product.shape
     walk = product / vertex_valence[:, None]
+    partner_walks = [shifted(walk, "wide", -offset) for offset in fetch_offsets]
     centre = jnp.mean(walk, axis=0)
     centred = walk - centre
     local_gram = hdot(centred.T, centred)
@@ -177,11 +178,12 @@
     drifts = gathered[:, vector_count:]
     cross = hdot(centres.T, drifts)
     gram_matrix = (gram_sum + cross + cross.T + block_rows * hdot(centres.T, centres)) / total_rows
-    displaced_entries = walk - mean_walk
+    displaced_entries = jnp.concatenate([walk] + partner_walks) - mean_walk
     normalizer_coefficient = jnp.linalg.cholesky(gram_matrix)
-    return jax.scipy.linalg.solve_triangular(
+    bases = jax.scipy.linalg.solve_triangular(
         normalizer_coefficient, displaced_entries.T, lower=True
     ).T
+    return [bases[i * block_rows : (i + 1) * block_rows] for i in range(1 + len(partner_walks))]
 
 
 def on_device(embeddings, start, neighbours):
@@ -240,13 +242,13 @@
         returned = shifted(sent, "wide", offset).reshape(-1)
         product = product + returned[:part_size].reshape(block_rows, vector_count)
         vertex_valence = vertex_valence + returned[part_size : part_size + block_rows]
-    basis = orthonormal(product, vertex_valence, total_rows)
+    bases = orthonormal(product, vertex_valence, total_rows, fetch_offsets if ITERS > 1 else ())
 
     for iteration in range(1, ITERS):
-        current = basis.astype(jnp.bfloat16)
-        weights = {0: current}
-        for offset in fetch_offsets:
-            weights[offset] = shifted(current, "wide", -offset)
+        weights = {0: bases[0].astype(jnp.bfloat16)}
+        for position, offset in enumerate(fetch_offsets):
+            weights[offset] = bases[position + 1].astype(jnp.bfloat16)
+        current = weights[0]
         parts = {offset: zero_part for offset in units}
         for (left, right), owned, affinity in zip(pair_plan, owned_list, tiles):
             row_part, col_part = later_pass(owned, affinity, weights[left], weights[right])
@@ -255,8 +257,9 @@
         product = row_product(near_tile, current) + parts[0]
         for offset in fetch_offsets:
             product = product + shifted(parts[offset], "wide", offset)
-        basis = orthonormal(product, vertex_valence, total_rows)
-    return (basis, vertex_valence / block_rows)
+        last = iteration == ITERS - 1
+        bases = orthonormal(product, vertex_valence, total_rows, () if last else fetch_offsets)
+    return (bases[0], vertex_valence / block_rows)
 
 
 def solution(mesh):

time: 239 us -> 233 us (0.975); the launches traced: 237 us -> 235 us
  waiting for transfers between devices: 100 us -> 87.9 us
  starting transfers between devices: 42.4 us -> 52.8 us
  other arithmetic: 41.8 us -> 37.6 us
  local copies, waits for them, and re-layouts: 12.1 us -> 15.3 us
    ppermute x8, waiting for transfers between devices: 81.8 us -> 60.6 us  [shifted(): return lax.ppermute(block, axis, route)]
    ppermute x8, starting transfers between devices: 14.9 us -> 30 us  [shifted(): return lax.ppermute(block, axis, route)]
    ppermute x10, waiting for transfers between devices: 18.7 us -> 27.3 us  [butterfly(): other = lax.ppermute(block, axis, route)]
    ppermute x10, starting transfers between devices: 27.5 us -> 22.8 us  [butterfly(): other = lax.ppermute(block, axis, route)]
    unnamed x13 -> x21, local copies, waits for them, and re-layouts: 0.2 us -> 4.58 us
  transfers between devices with their start and end apart: 18 -> 18, of which waited for: 17 -> 15; matrix products, arithmetic and copies ran while one was open for 10% -> 14% of each run, Pallas kernels for 0% -> 0%
where the time goes in v6:
time: 233 us; the launch traced here: 235 us
  waiting for transfers between devices  87.9 us (38%)
  starting transfers between devices  52.8 us (23%)
  matrix products  37.8 us (16%)
  other arithmetic  37.6 us (16%)
  local copies, waits for them, and re-layouts  15.3 us (7%)
  between operations  3.26 us (1%)
    ppermute x8, waiting for transfers between devices, shifted(): return lax.ppermute(block, axis, route)  60.6 us
    ppermute x8, starting transfers between devices, shifted(): return lax.ppermute(block, axis, route)  30 us
    ppermute x10, waiting for transfers between devices, butterfly(): other = lax.ppermute(block, axis, route)  27.3 us
    ppermute x10, starting transfers between devices, butterfly(): other = lax.ppermute(block, axis, route)  22.8 us
    dot_general x3, matrix products, scores_tile(): lax.dot_general(leftside_block, right_block, (((1,), (1,)), ((), ())), pr...  13.9 us
    another operation x6, other arithmetic, orthonormal(): normalizer_coefficient = jnp.linalg.cholesky(gram_matrix)  13 us
    dot_general x6, matrix products, row_product(): return jnp.dot(affinity, weights, preferred_element_type=jnp.float32)  11.5 us
    another operation x4, other arithmetic, orthonormal(): jax.scipy.linalg.solve_triangular(normalizer_coefficient, displaced_entri...  11.1 us
  transfers between devices with their start and end apart: 18, of which 15 were waited for; matrix products, arithmetic and copies ran while one was open for 14% of the time, Pallas kernels for 0%

profile of v6, /device:TPU:0, one launch (start us, length us, event | category | flops | bytes accessed | tf_op | source)
XLA Modules:
  0.0 235.0 jit_solution(15808536991261630976)
XLA Ops:
  0.6 1.2 copy.17
  2.2 1.8 fusion.13
  4.4 1.2 copy-done.1
  5.6 1.3 pad_maximum_fusion
  7.0 3.0 %collective-permute-start.1 = (bf16[1110,768]{1,0:T(8,128)(2,1)}, bf16[1110,768]{1,0:T(8,128)(2,1)}, u32[]{:S(2)}, u32[]{:S(2)}) collective-permute-start(bf16[1110,768]{1,0:T(8,128)(2,1)} %pad_maximum_fusion), channel_id=1, source_target_pairs={{24,0},{28,4},{0,8},{4,12},{8,16},{12,20},{16,24},{20,28},{25,1},{... | collective-permute-start | bytes 5114888 | tf_op jit(solution)/shard_map/ppermute | solution.py:19
  10.0 3.2 %collective-permute-start = (bf16[1110,768]{1,0:T(8,128)(2,1)}, bf16[1110,768]{1,0:T(8,128)(2,1)}, u32[]{:S(2)}, u32[]{:S(2)}) collective-permute-start(bf16[1110,768]{1,0:T(8,128)(2,1)} %pad_maximum_fusion), channel_id=1, source_target_pairs={{4,0},{8,4},{12,8},{16,12},{20,16},{24,20},{28,24},{0,28},{5,1},{9... | collective-permute-start | bytes 5114888 | tf_op jit(solution)/shard_map/ppermute | solution.py:19
  13.2 0.7 fusion.52
  15.8 4.0 %convert_reduce_fusion.6 = (f32[1024]{0:T(1024)S(1)}, bf16[1024,1024]{0,1:T(8,128)(2,1)S(1)}) fusion(bf16[1024,768]{1,0:T(8,128)(2,1)} %copy-done.1), kind=kOutput, calls=%fused_computation.21 | convolution fusion | flops 1616903168 | bytes 3674112 | tf_op jit(solution)/shard_map/dot_general | solution.py:54
  19.8 30.6 %collective-permute-done.1 = bf16[1110,768]{1,0:T(8,128)(2,1)} collective-permute-done((bf16[1110,768]{1,0:T(8,128)(2,1)}, bf16[1110,768]{1,0:T(8,128)(2,1)}, u32[]{:S(2)}, u32[]{:S(2)}) %collective-permute-start.1) | collective-permute-done | bytes 1704992 | tf_op jit(solution)/shard_map/ppermute | solution.py:19
  50.5 10.4 %conditional.7 = (bf16[1024,1024]{1,0:T(8,128)(2,1)}, f32[1024,64]{0,1:T(8,128)S(1)}, f32[1024]{0:T(1024)S(1)}, f32[1024,64]{0,1:T(8,128)S(1)}, f32[1024]{0:T(1024)S(1)}) conditional(s32[]{:T(128)} %convert_element_type.57, () %tuple.59, (bf16[1110,768]{1,0:T(8,128)(2,1)}, bf16[1024,768]{1,0:T(8,128)(2,1)S(1)}, bf16[66048]{0:T(1024)(128)(2,1)S(1)}) %tuple.106), branch_computations={%region_7.8_spmd, %region_8.11_spmd} | conditional | flops 1884289024 | bytes 11415592 | solution.py:100
  50.5 4.7 %convert_reduce_fusion.2 = (f32[1024]{0:T(1024)S(1)}, f32[1024]{0:T(1024)S(1)}, bf16[1024,1024]{1,0:T(8,128)(2,1)}) fusion(bf16[1024,768]{1,0:T(8,128)(2,1)S(1)} %get-tuple-element.39, bf16[1110,768]{1,0:T(8,128)(2,1)} %get-tuple-element.38), kind=kOutput, calls=%fused_computation.6 | convolution fusion | flops 1615853568 | bytes 5251072 | tf_op jit(solution)/shard_map/cond/branch_1_fun/dot_general | solution.py:54
  55.3 2.4 %fusion.68 = f32[1024,64]{0,1:T(8,128)S(1)} fusion(bf16[1024,1024]{1,0:T(8,128)(2,1)} %get-tuple-element.148, bf16[1024,64]{1,0:T(8,128)(2,1)S(1)} %reshape.133), kind=kOutput, calls=%fused_computation.157 | convolution fusion | flops 134217728 | bytes 2490368 | tf_op jit(solution)/shard_map/cond/branch_1_fun/dot_general | solution.py:61
  57.7 0.9 slice.160
  58.8 2.1 fusion.4
  60.9 22.6 %collective-permute-done = bf16[1110,768]{1,0:T(8,128)(2,1)} collective-permute-done((bf16[1110,768]{1,0:T(8,128)(2,1)}, bf16[1110,768]{1,0:T(8,128)(2,1)}, u32[]{:S(2)}, u32[]{:S(2)}) %collective-permute-start) | collective-permute-done | bytes 1704992 | tf_op jit(solution)/shard_map/ppermute | solution.py:19
  83.5 11.9 %conditional.8 = (bf16[1024,1024]{1,0:T(8,128)(2,1)}, f32[1024,64]{0,1:T(8,128)S(1)}, f32[1024]{0:T(1024)S(1)}, f32[1024,64]{0,1:T(8,128)S(1)}, f32[1024]{0:T(1024)S(1)}) conditional(s32[]{:T(128)} %convert_element_type.58, () %tuple.61, (bf16[1110,768]{1,0:T(8,128)(2,1)}, bf16[1110,768]{1,0:T(8,128)(2,1)}) %tuple.62), branch_computations={%region_12.13_spmd, %region_13.16_spmd} | conditional | flops 1884289024 | bytes 11550760 | solution.py:100
  83.5 5.2 %convert_reduce_fusion.4 = (f32[1024]{0:T(1024)S(1)}, f32[1024]{0:T(1024)S(1)}, bf16[1024,1024]{1,0:T(8,128)(2,1)}) fusion(bf16[1110,768]{1,0:T(8,128)(2,1)} %get-tuple-element.42, bf16[1110,768]{1,0:T(8,128)(2,1)} %get-tuple-element.41), kind=kOutput, calls=%fused_computation.12 | convolution fusion | flops 1615853568 | bytes 5251072 | tf_op jit(solution)/shard_map/cond/branch_1_fun/dot_general | solution.py:54
  88.7 0.9 slice.165
  89.8 2.4 %fusion.10 = f32[1024,64]{0,1:T(8,128)S(1)} fusion(bf16[1024,1024]{1,0:T(8,128)(2,1)} %get-tuple-element.158, bf16[1032,64]{1,0:T(8,128)(2,1)S(1)} %slice.166), kind=kOutput, calls=%fused_computation.19 | convolution fusion | flops 134217728 | bytes 2621440 | tf_op jit(solution)/shard_map/cond/branch_1_fun/dot_general | solution.py:61
  92.2 0.9 slice.168
  93.3 2.1 fusion.8
  96.5 0.7 pad_maximum_fusion.2
  97.2 1.9 conditional.6
  97.2 1.6 broadcast.148
  100.9 15.2 %collective-permute-start.2 = (f32[520,128]{1,0:T(8,128)}, f32[520,128]{1,0:T(8,128)}, u32[]{:S(2)}, u32[]{:S(2)}) collective-permute-start(f32[520,128]{1,0:T(8,128)} %pad_maximum_fusion.1), channel_id=1, source_target_pairs={{28,0},{0,4},{4,8},{8,12},{12,16},{16,20},{20,24},{24,28},{29,1},{... | collective-permute-start | bytes 798728 | tf_op jit(solution)/shard_map/ppermute | solution.py:19
  116.6 1.0 slice.254
  117.9 3.3 %collective-permute-done.2 = f32[520,128]{1,0:T(8,128)} collective-permute-done((f32[520,128]{1,0:T(8,128)}, f32[520,128]{1,0:T(8,128)}, u32[]{:S(2)}, u32[]{:S(2)}) %collective-permute-start.2) | collective-permute-done | bytes 266272 | tf_op jit(solution)/shard_map/ppermute | solution.py:19
  121.3 1.0 slice.253
  122.6 1.2 fusion.58
  123.8 1.3 broadcast_multiply_fusion
  126.6 0.8 pad_maximum_fusion.13
  127.6 1.2 collective-permute-done.6
  128.8 15.6 %collective-permute-start.7 = (f32[35,128]{1,0:T(8,128)S(1)}, f32[35,128]{1,0:T(8,128)S(1)}, u32[]{:S(2)}, u32[]{:S(2)}) collective-permute-start(f32[35,128]{1,0:T(8,128)S(1)} %pad_maximum_fusion.8), channel_id=1, source_target_pairs={{0,2},{1,3},{2,0},{3,1},{4,6},{5,7},{6,4},{7,5},{8,10},{9,11},{10,... | collective-permute-start | bytes 53768 | tf_op jit(solution)/shard_map/ppermute | solution.py:130
  144.3 1.8 collective-permute-done.7
  146.2 3.8 %collective-permute-done.8 = f32[37,128]{1,0:T(8,128)S(1)} collective-permute-done((f32[37,128]{1,0:T(8,128)S(1)}, f32[37,128]{1,0:T(8,128)S(1)}, u32[]{:S(2)}, u32[]{:S(2)}) %collective-permute-start.8) | collective-permute-done | bytes 18976 | tf_op jit(solution)/shard_map/ppermute | solution.py:130
  150.1 3.8 %collective-permute-done.9 = f32[41,128]{1,0:T(8,128)S(1)} collective-permute-done((f32[41,128]{1,0:T(8,128)S(1)}, f32[41,128]{1,0:T(8,128)S(1)}, u32[]{:S(2)}, u32[]{:S(2)}) %collective-permute-start.9) | collective-permute-done | bytes 21024 | tf_op jit(solution)/shard_map/ppermute | solution.py:130
  154.2 3.2 %collective-permute-start.4 = (f32[1024,64]{0,1:T(8,128)S(1)}, f32[1024,64]{0,1:T(8,128)S(1)}, u32[]{:S(2)}, u32[]{:S(2)}) collective-permute-start(f32[1024,64]{0,1:T(8,128)S(1)} %get-tuple-element.130), channel_id=1, source_target_pairs={{4,0},{8,4},{12,8},{16,12},{20,16},{24,20},{28,24},{0,28},{5,1},{9... | collective-permute-start | bytes 786440 | tf_op jit(solution)/shard_map/ppermute | solution.py:19
  157.4 1.9 collective-permute-done.10
  161.4 5.8 %cholesky.44 = f32[64,64]{1,0:T(8,128)S(1)} custom-call(f32[64,64]{1,0:T(8,128)S(1)} %fusion.41), custom_call_target="Cholesky" | custom-call | tf_op jit(solution)/shard_map/jit(cholesky)/cholesky | solution.py:182
  168.6 4.9 %custom-call.10 = f32[1,64,64]{1,2,0:T(8,128)S(1)} custom-call(f32[1,64,64]{2,1,0:T(8,128)S(1)} %fusion.36), custom_call_target="InvertDiagBlocksLowerTriangular" | custom-call | tf_op jit(solution)/shard_map/jit(_solve_triangular)/triangular_solve | solution.py:183
  173.6 0.9 convolution_convert_fusion
  174.6 0.7 copy-done.7
  175.3 4.4 %conditional.10 = (f32[1024,64]{0,1:T(8,128)S(1)}, f32[1024,64]{0,1:T(8,128)S(1)}) conditional(s32[]{:T(128)} %convert_element_type.57, () %tuple.65, (bf16[1024,1024]{1,0:T(8,128)(2,1)}, bf16[1024,64]{0,1:T(8,128)(2,1)S(1)}, bf16[1024,64]{0,1:T(8,128)(2,1)S(1)}) %tuple.66), branch_computations={%region_25.27_spmd, %region_26.28_spmd} | conditional | flops 268435456 | bytes 4980752 | solution.py:114
  175.3 2.3 fusion.63
  177.6 2.1 fusion.64
  179.7 4.4 %conditional.11 = (f32[1024,64]{0,1:T(8,128)S(1)}, f32[1024,64]{0,1:T(8,128)S(1)}) conditional(s32[]{:T(128)} %convert_element_type.58, () %tuple.67, (bf16[1024,1024]{1,0:T(8,128)(2,1)}, bf16[1024,64]{0,1:T(8,128)(2,1)S(1)}, bf16[1024,64]{0,1:T(8,128)(2,1)S(1)}) %tuple.68), branch_computations={%region_27.29_spmd, %region_28.30_spmd} | conditional | flops 268435456 | bytes 4980752 | solution.py:114
  179.7 2.3 fusion.65
  182.1 2.1 fusion.66
  184.2 0.7 add.238
  185.0 5.3 %collective-permute-start.11 = (f32[1024,64]{0,1:T(8,128)S(1)}, f32[1024,64]{0,1:T(8,128)S(1)}, u32[]{:S(2)}, u32[]{:S(2)}) collective-permute-start(f32[1024,64]{0,1:T(8,128)S(1)} %add.236), channel_id=1, source_target_pairs={{28,0},{0,4},{4,8},{8,12},{12,16},{16,20},{20,24},{24,28},{29,1},{... | collective-permute-start | bytes 786440 | tf_op jit(solution)/shard_map/ppermute | solution.py:19
  190.3 1.3 collective-permute-done.12
  191.6 2.8 %collective-permute-done.11 = f32[1024,64]{0,1:T(8,128)S(1)} collective-permute-done((f32[1024,64]{0,1:T(8,128)S(1)}, f32[1024,64]{0,1:T(8,128)S(1)}, u32[]{:S(2)}, u32[]{:S(2)}) %collective-permute-start.11) | collective-permute-done | bytes 262176 | tf_op jit(solution)/shard_map/ppermute | solution.py:19
  194.3 1.6 fusion.55
  196.7 0.8 pad_maximum_fusion.14
  197.6 1.2 collective-permute-done.13
  198.8 6.0 %collective-permute-start.14 = (f32[35,128]{1,0:T(8,128)S(1)}, f32[35,128]{1,0:T(8,128)S(1)}, u32[]{:S(2)}, u32[]{:S(2)}) collective-permute-start(f32[35,128]{1,0:T(8,128)S(1)} %pad_maximum_fusion.11), channel_id=1, source_target_pairs={{0,2},{1,3},{2,0},{3,1},{4,6},{5,7},{6,4},{7,5},{8,10},{9,11},{10,... | collective-permute-start | bytes 53768 | tf_op jit(solution)/shard_map/ppermute | solution.py:130
  204.8 1.8 collective-permute-done.14
  206.7 3.8 %collective-permute-done.15 = f32[37,128]{1,0:T(8,128)S(1)} collective-permute-done((f32[37,128]{1,0:T(8,128)S(1)}, f32[37,128]{1,0:T(8,128)S(1)}, u32[]{:S(2)}, u32[]{:S(2)}) %collective-permute-start.15) | collective-permute-done | bytes 18976 | tf_op jit(solution)/shard_map/ppermute | solution.py:130
  210.5 0.8 collective-permute-start.16
  211.3 3.1 %collective-permute-done.16 = f32[41,128]{1,0:T(8,128)S(1)} collective-permute-done((f32[41,128]{1,0:T(8,128)S(1)}, f32[41,128]{1,0:T(8,128)S(1)}, u32[]{:S(2)}, u32[]{:S(2)}) %collective-permute-start.16) | collective-permute-done | bytes 21024 | tf_op jit(solution)/shard_map/ppermute | solution.py:130
  214.5 5.1 %collective-permute-done.17 = f32[49,128]{1,0:T(8,128)S(1)} collective-permute-done((f32[49,128]{1,0:T(8,128)S(1)}, f32[49,128]{1,0:T(8,128)S(1)}, u32[]{:S(2)}, u32[]{:S(2)}) %collective-permute-start.17) | collective-permute-done | bytes 25120 | tf_op jit(solution)/shard_map/ppermute | solution.py:130
  221.7 5.8 %cholesky.55 = f32[64,64]{1,0:T(8,128)S(1)} custom-call(f32[64,64]{1,0:T(8,128)S(1)} %fusion.39), custom_call_target="Cholesky" | custom-call | tf_op jit(solution)/shard_map/jit(cholesky)/cholesky | solution.py:182
  228.9 4.9 %custom-call.11 = f32[1,64,64]{1,2,0:T(8,128)S(1)} custom-call(f32[1,64,64]{2,1,0:T(8,128)S(1)} %fusion.37), custom_call_target="InvertDiagBlocksLowerTriangular" | custom-call | tf_op jit(solution)/shard_map/jit(_solve_triangular)/triangular_solve | solution.py:183
  233.8 1.2 fusion.27
  (143 shorter events, 15.6 us)
Async XLA Ops:
  0.6 3.3 %copy-start = (bf16[1024,768]{1,0:T(8,128)(2,1)S(1)}, bf16[1024,768]{1,0:T(8,128)(2,1)}, u32[]{:S(2)}) copy-start(bf16[1024,768]{1,0:T(8,128)(2,1)} %param.16) | copy-start | bytes 4718596
  4.4 1.2 copy-start.1
  5.6 7.6 %copy-start.9 = (s32[32,3]{0,1:T(4,128)S(1)}, s32[32,3]{0,1:T(4,128)}, u32[]{:S(2)}) copy-start(s32[32,3]{0,1:T(4,128)} %param.18) | copy-start | bytes 1156
  7.0 43.5 %collective-permute-start.1 = (bf16[1110,768]{1,0:T(8,128)(2,1)}, bf16[1110,768]{1,0:T(8,128)(2,1)}, u32[]{:S(2)}, u32[]{:S(2)}) collective-permute-start(bf16[1110,768]{1,0:T(8,128)(2,1)} %pad_maximum_fusion), channel_id=1, source_target_pairs={{24,0},{28,4},{0,8},{4,12},{8,16},{12,20},{16,24},{20,28},{25,1},{... | collective-permute-start | bytes 5114888 | tf_op jit(solution)/shard_map/ppermute | solution.py:19
  10.0 73.5 %collective-permute-start = (bf16[1110,768]{1,0:T(8,128)(2,1)}, bf16[1110,768]{1,0:T(8,128)(2,1)}, u32[]{:S(2)}, u32[]{:S(2)}) collective-permute-start(bf16[1110,768]{1,0:T(8,128)(2,1)} %pad_maximum_fusion), channel_id=1, source_target_pairs={{4,0},{8,4},{12,8},{16,12},{20,16},{24,20},{28,24},{0,28},{5,1},{9... | collective-permute-start | bytes 5114888 | tf_op jit(solution)/shard_map/ppermute | solution.py:19
  15.8 34.7 %copy-start.2 = (bf16[1024,768]{1,0:T(8,128)(2,1)S(1)}, bf16[1024,768]{1,0:T(8,128)(2,1)}, u32[]{:S(2)}) copy-start(bf16[1024,768]{1,0:T(8,128)(2,1)} %copy-done.1) | copy-start | bytes 4718596
  60.9 22.6 %copy-start.5 = (f32[1024,64]{0,1:T(8,128)}, f32[1024,64]{0,1:T(8,128)S(1)}, u32[]{:S(2)}) copy-start(f32[1024,64]{0,1:T(8,128)S(1)} %get-tuple-element.76) | copy-start | bytes 786436
  95.4 0.7 copy-start.3
  97.2 19.4 %collective-permute-start.3 = (f32[520,128]{1,0:T(8,128)}, f32[520,128]{1,0:T(8,128)}, u32[]{:S(2)}, u32[]{:S(2)}) collective-permute-start(f32[520,128]{1,0:T(8,128)} %pad_maximum_fusion.2), channel_id=1, source_target_pairs={{8,0},{12,4},{16,8},{20,12},{24,16},{28,20},{0,24},{4,28},{9,1},{1... | collective-permute-start | bytes 798728 | tf_op jit(solution)/shard_map/ppermute | solution.py:19
  97.2 2.6 %copy-start.4 = (f32[1024,64]{0,1:T(8,128)S(1)}, f32[1024,64]{0,1:T(8,128)}, u32[]{:S(2)}) copy-start(f32[1024,64]{0,1:T(8,128)} %copy-done.3) | copy-start | bytes 786436
  99.1 0.7 copy-start.6
  99.1 17.0 %copy-start.8 = (bf16[1024,64]{0,1:T(8,128)(2,1)S(1)}, bf16[1024,64]{0,1:T(8,128)(2,1)}, u32[]{:S(2)}) copy-start(bf16[1024,64]{0,1:T(8,128)(2,1)} %param.17) | copy-start | bytes 393220
  100.9 20.3 %collective-permute-start.2 = (f32[520,128]{1,0:T(8,128)}, f32[520,128]{1,0:T(8,128)}, u32[]{:S(2)}, u32[]{:S(2)}) collective-permute-start(f32[520,128]{1,0:T(8,128)} %pad_maximum_fusion.1), channel_id=1, source_target_pairs={{28,0},{0,4},{4,8},{8,12},{12,16},{16,20},{20,24},{24,28},{29,1},{... | collective-permute-start | bytes 798728 | tf_op jit(solution)/shard_map/ppermute | solution.py:19
  127.5 1.3 collective-permute-start.6
  128.8 17.3 %collective-permute-start.7 = (f32[35,128]{1,0:T(8,128)S(1)}, f32[35,128]{1,0:T(8,128)S(1)}, u32[]{:S(2)}, u32[]{:S(2)}) collective-permute-start(f32[35,128]{1,0:T(8,128)S(1)} %pad_maximum_fusion.8), channel_id=1, source_target_pairs={{0,2},{1,3},{2,0},{3,1},{4,6},{5,7},{6,4},{7,5},{8,10},{9,11},{10,... | collective-permute-start | bytes 53768 | tf_op jit(solution)/shard_map/ppermute | solution.py:130
  146.1 3.8 %collective-permute-start.8 = (f32[37,128]{1,0:T(8,128)S(1)}, f32[37,128]{1,0:T(8,128)S(1)}, u32[]{:S(2)}, u32[]{:S(2)}) collective-permute-start(f32[37,128]{1,0:T(8,128)S(1)} %pad_maximum_fusion.9), channel_id=1, source_target_pairs={{0,4},{4,0},{8,12},{12,8},{16,20},{20,16},{24,28},{28,24},{1,5},{5... | collective-permute-start | bytes 56840 | tf_op jit(solution)/shard_map/ppermute | solution.py:130
  150.0 3.9 %collective-permute-start.9 = (f32[41,128]{1,0:T(8,128)S(1)}, f32[41,128]{1,0:T(8,128)S(1)}, u32[]{:S(2)}, u32[]{:S(2)}) collective-permute-start(f32[41,128]{1,0:T(8,128)S(1)} %pad_maximum_fusion.5), channel_id=1, source_target_pairs={{0,8},{4,12},{8,0},{12,4},{16,24},{20,28},{24,16},{28,20},{1,9},{5... | collective-permute-start | bytes 62984 | tf_op jit(solution)/shard_map/ppermute | solution.py:130
  154.0 5.4 %collective-permute-start.10 = (f32[49,128]{1,0:T(8,128)S(1)}, f32[49,128]{1,0:T(8,128)S(1)}, u32[]{:S(2)}, u32[]{:S(2)}) collective-permute-start(f32[49,128]{1,0:T(8,128)S(1)} %pad_maximum_fusion.3), channel_id=1, source_target_pairs={{0,16},{4,20},{8,24},{12,28},{16,0},{20,4},{24,8},{28,12},{1,17},{... | collective-permute-start | bytes 75272 | tf_op jit(solution)/shard_map/ppermute | solution.py:130
  154.1 19.5 %collective-permute-start.5 = (f32[1024,64]{0,1:T(8,128)S(1)}, f32[1024,64]{0,1:T(8,128)S(1)}, u32[]{:S(2)}, u32[]{:S(2)}) collective-permute-start(f32[1024,64]{0,1:T(8,128)S(1)} %get-tuple-element.130), channel_id=1, source_target_pairs={{24,0},{28,4},{0,8},{4,12},{8,16},{12,20},{16,24},{20,28},{25,1},{... | collective-permute-start | bytes 786440 | tf_op jit(solution)/shard_map/ppermute | solution.py:19
  154.2 19.4 %collective-permute-start.4 = (f32[1024,64]{0,1:T(8,128)S(1)}, f32[1024,64]{0,1:T(8,128)S(1)}, u32[]{:S(2)}, u32[]{:S(2)}) collective-permute-start(f32[1024,64]{0,1:T(8,128)S(1)} %get-tuple-element.130), channel_id=1, source_target_pairs={{4,0},{8,4},{12,8},{16,12},{20,16},{24,20},{28,24},{0,28},{5,1},{9... | collective-permute-start | bytes 786440 | tf_op jit(solution)/shard_map/ppermute | solution.py:19
  174.5 0.8 copy-start.7
  184.9 6.7 %collective-permute-start.12 = (f32[1024,64]{0,1:T(8,128)}, f32[1024,64]{0,1:T(8,128)}, u32[]{:S(2)}, u32[]{:S(2)}) collective-permute-start(f32[1024,64]{0,1:T(8,128)} %add.238), channel_id=1, source_target_pairs={{8,0},{12,4},{16,8},{20,12},{24,16},{28,20},{0,24},{4,28},{9,1},{1... | collective-permute-start | bytes 786440 | tf_op jit(solution)/shard_map/ppermute | solution.py:19
  185.0 9.3 %collective-permute-start.11 = (f32[1024,64]{0,1:T(8,128)S(1)}, f32[1024,64]{0,1:T(8,128)S(1)}, u32[]{:S(2)}, u32[]{:S(2)}) collective-permute-start(f32[1024,64]{0,1:T(8,128)S(1)} %add.236), channel_id=1, source_target_pairs={{28,0},{0,4},{4,8},{8,12},{12,16},{16,20},{20,24},{24,28},{29,1},{... | collective-permute-start | bytes 786440 | tf_op jit(solution)/shard_map/ppermute | solution.py:19
  197.6 1.2 collective-permute-start.13
  198.8 7.7 %collective-permute-start.14 = (f32[35,128]{1,0:T(8,128)S(1)}, f32[35,128]{1,0:T(8,128)S(1)}, u32[]{:S(2)}, u32[]{:S(2)}) collective-permute-start(f32[35,128]{1,0:T(8,128)S(1)} %pad_maximum_fusion.11), channel_id=1, source_target_pairs={{0,2},{1,3},{2,0},{3,1},{4,6},{5,7},{6,4},{7,5},{8,10},{9,11},{10,... | collective-permute-start | bytes 53768 | tf_op jit(solution)/shard_map/ppermute | solution.py:130
  206.6 3.8 %collective-permute-start.15 = (f32[37,128]{1,0:T(8,128)S(1)}, f32[37,128]{1,0:T(8,128)S(1)}, u32[]{:S(2)}, u32[]{:S(2)}) collective-permute-start(f32[37,128]{1,0:T(8,128)S(1)} %pad_maximum_fusion.12), channel_id=1, source_target_pairs={{0,4},{4,0},{8,12},{12,8},{16,20},{20,16},{24,28},{28,24},{1,5},{5... | collective-permute-start | bytes 56840 | tf_op jit(solution)/shard_map/ppermute | solution.py:130
  210.5 3.9 %collective-permute-start.16 = (f32[41,128]{1,0:T(8,128)S(1)}, f32[41,128]{1,0:T(8,128)S(1)}, u32[]{:S(2)}, u32[]{:S(2)}) collective-permute-start(f32[41,128]{1,0:T(8,128)S(1)} %pad_maximum_fusion.6), channel_id=1, source_target_pairs={{0,8},{4,12},{8,0},{12,4},{16,24},{20,28},{24,16},{28,20},{1,9},{5... | collective-permute-start | bytes 62984 | tf_op jit(solution)/shard_map/ppermute | solution.py:130
  214.4 5.1 %collective-permute-start.17 = (f32[49,128]{1,0:T(8,128)S(1)}, f32[49,128]{1,0:T(8,128)S(1)}, u32[]{:S(2)}, u32[]{:S(2)}) collective-permute-start(f32[49,128]{1,0:T(8,128)S(1)} %pad_maximum_fusion.4), channel_id=1, source_target_pairs={{0,16},{4,20},{8,24},{12,28},{16,0},{20,4},{24,8},{28,12},{1,17},{... | collective-permute-start | bytes 75272 | tf_op jit(solution)/shard_map/ppermute | solution.py:130

commit v7 on v6

--- a/solution.py
+++ b/solution.py
@@ -6,6 +6,7 @@
 import jax.numpy as jnp
 from jax import lax
 from jax.sharding import PartitionSpec as P
+from jax.experimental import pallas as pl
 
 ITERS = 2
 
@@ -149,6 +150,37 @@
     return jnp.dot(left, right, precision=lax.Precision.HIGHEST, preferred_element_type=jnp.float32)
 
 
+def factor_kernel(gram_ref, inverse_ref):
+    size = gram_ref.shape[0]
+    rows = lax.broadcasted_iota(jnp.int32, (size, size), 0)
+    cols = lax.broadcasted_iota(jnp.int32, (size, size), 1)
+    eye = jnp.where(rows == cols, 1.0, 0.0).astype(jnp.float32)
+
+    def step(j, carry):
+        remaining, inverse = carry
+        column = jnp.sum(jnp.where(cols == j, remaining, 0.0), axis=1, keepdims=True)
+        pivot = jnp.sum(jnp.where(rows[:, :1] == j, column, 0.0), axis=0, keepdims=True)
+        scale = lax.rsqrt(pivot)
+        factor_column = jnp.where(rows[:, :1] >= j, column * scale, 0.0)
+        factor_row = jnp.sum(jnp.where(rows == j, remaining, 0.0), axis=0, keepdims=True)
+        factor_row = jnp.where(cols[:1] >= j, factor_row * scale, 0.0)
+        remaining = remaining - factor_column * factor_row
+        inverse_row = jnp.sum(jnp.where(rows == j, inverse, 0.0), axis=0, keepdims=True) * scale
+        inverse = jnp.where(rows == j, inverse_row, inverse)
+        below = jnp.where(rows[:, :1] > j, factor_column, 0.0)
+        inverse = inverse - below * inverse_row
+        return remaining, inverse
+
+    _, inverse = lax.fori_loop(0, size, step, (gram_ref[...], eye))
+    inverse_ref[...] = inverse
+
+
+def factor_inverse(gram_matrix):
+    return pl.pallas_call(
+        factor_kernel, out_shape=jax.ShapeDtypeStruct(gram_matrix.shape, jnp.float32)
+    )(gram_matrix)
+
+
 def orthonormal(product, vertex_valence, total_rows, fetch_offsets=()):
     block_rows, vector_count = product.shape
     walk = product / vertex_valence[:, None]
@@ -179,10 +211,8 @@
     cross = hdot(centres.T, drifts)
     gram_matrix = (gram_sum + cross + cross.T + block_rows * hdot(centres.T, centres)) / total_rows
     displaced_entries = jnp.concatenate([walk] + partner_walks) - mean_walk
-    normalizer_coefficient = jnp.linalg.cholesky(gram_matrix)
-    bases = jax.scipy.linalg.solve_triangular(
-        normalizer_coefficient, displaced_entries.T, lower=True
-    ).T
+    inverse_factor = factor_inverse(gram_matrix)
+    bases = hdot(displaced_entries, inverse_factor.T)
     return [bases[i * block_rows : (i + 1) * block_rows] for i in range(1 + len(partner_walks))]
 
 

time: 233 us -> 229 us (0.983)
  other arithmetic: 37.6 us -> 13.4 us
  Pallas kernels: 0 us -> 16.8 us
  waiting for transfers between devices: 87.9 us -> 101 us
  starting transfers between devices: 52.8 us -> 40.7 us
  matrix products: 37.8 us -> 40.7 us
    another operation x10 -> x0, other arithmetic: 24.1 us -> none  [the longest x6 13 us: orthonormal(): normalizer_coefficient = jnp.linalg.cholesky(gram_matrix)]
    ppermute x10, starting transfers between devices: 22.8 us -> 1.37 us  [butterfly(): other = lax.ppermute(block, axis, route)]
    pallas_call x0 -> x2, Pallas kernels: none -> 16.8 us  [factor_inverse(): pl.pallas_call(factor_kernel, out_shape=jax.ShapeDtypeStruct(gram_matrix....]
    ppermute x8, starting transfers between devices: 30 us -> 39.4 us  [shifted(): return lax.ppermute(block, axis, route)]
    ppermute x8, waiting for transfers between devices: 60.6 us -> 69.9 us  [shifted(): return lax.ppermute(block, axis, route)]
    dot_general x6 -> x8, matrix products: 1.92 us -> 6.78 us  [hdot(): jnp.dot(left, right, precision=lax.Precision.HIGHEST, preferred_element_t...]
    ppermute x10, waiting for transfers between devices: 27.3 us -> 31 us  [butterfly(): other = lax.ppermute(block, axis, route)]
  transfers between devices with their start and end apart: 18 -> 18, of which waited for: 15 -> 15; matrix products, arithmetic and copies ran while one was open for 14% -> 16% of each run, Pallas kernels for 0% -> 4%
where the time goes in v7:
time: 229 us; the launch traced here: 230 us
  waiting for transfers between devices  101 us (44%)
  starting transfers between devices  40.7 us (18%)
  matrix products  40.7 us (18%)
  Pallas kernels  16.8 us (7%)
  local copies, waits for them, and re-layouts  14 us (6%)
  other arithmetic  13.4 us (6%)
  between operations  3.23 us (1%)
    ppermute x8, waiting for transfers between devices, shifted(): return lax.ppermute(block, axis, route)  69.9 us
    ppermute x8, starting transfers between devices, shifted(): return lax.ppermute(block, axis, route)  39.4 us
    ppermute x10, waiting for transfers between devices, butterfly(): other = lax.ppermute(block, axis, route)  31 us
    pallas_call x2, Pallas kernels, factor_inverse(): pl.pallas_call(factor_kernel, out_shape=jax.ShapeDtypeStruct(gram_matrix....  16.8 us
    dot_general x3, matrix products, scores_tile(): lax.dot_general(leftside_block, right_block, (((1,), (1,)), ((), ())), pr...  14 us
    dot_general x6, matrix products, row_product(): return jnp.dot(affinity, weights, preferred_element_type=jnp.float32)  11.5 us
    dot_general x4, matrix products, col_product(): lax.dot_general(affinity, weights, (((0,), (0,)), ((), ())), preferred_el...  8.39 us
    dot_general x8, matrix products, hdot(): jnp.dot(left, right, precision=lax.Precision.HIGHEST, preferred_element_t...  6.78 us
  transfers between devices with their start and end apart: 18, of which 15 were waited for; matrix products, arithmetic and copies ran while one was open for 16% of the time, Pallas kernels for 4%

profile of v7, /device:TPU:0, one launch (start us, length us, event | category | flops | bytes accessed | tf_op | source)
XLA Modules:
  0.0 230.0 jit_solution(3122850625735994075)
XLA Ops:
  0.6 1.2 copy.13
  2.2 1.8 fusion.13
  4.4 1.2 copy-done.1
  5.6 1.3 pad_maximum_fusion
  7.0 3.0 %collective-permute-start.1 = (bf16[1110,768]{1,0:T(8,128)(2,1)}, bf16[1110,768]{1,0:T(8,128)(2,1)}, u32[]{:S(2)}, u32[]{:S(2)}) collective-permute-start(bf16[1110,768]{1,0:T(8,128)(2,1)} %pad_maximum_fusion), channel_id=1, source_target_pairs={{24,0},{28,4},{0,8},{4,12},{8,16},{12,20},{16,24},{20,28},{25,1},{... | collective-permute-start | bytes 5114888 | tf_op jit(solution)/shard_map/ppermute | solution.py:20
  10.0 3.2 %collective-permute-start = (bf16[1110,768]{1,0:T(8,128)(2,1)}, bf16[1110,768]{1,0:T(8,128)(2,1)}, u32[]{:S(2)}, u32[]{:S(2)}) collective-permute-start(bf16[1110,768]{1,0:T(8,128)(2,1)} %pad_maximum_fusion), channel_id=1, source_target_pairs={{4,0},{8,4},{12,8},{16,12},{20,16},{24,20},{28,24},{0,28},{5,1},{9... | collective-permute-start | bytes 5114888 | tf_op jit(solution)/shard_map/ppermute | solution.py:20
  13.2 0.7 fusion.46
  15.8 4.0 %convert_reduce_fusion.6 = (f32[1024]{0:T(1024)S(1)}, bf16[1024,1024]{0,1:T(8,128)(2,1)S(1)}) fusion(bf16[1024,768]{1,0:T(8,128)(2,1)} %copy-done.1), kind=kOutput, calls=%fused_computation.21 | convolution fusion | flops 1616903168 | bytes 3674112 | tf_op jit(solution)/shard_map/dot_general | solution.py:55
  19.8 30.6 %collective-permute-done.1 = bf16[1110,768]{1,0:T(8,128)(2,1)} collective-permute-done((bf16[1110,768]{1,0:T(8,128)(2,1)}, bf16[1110,768]{1,0:T(8,128)(2,1)}, u32[]{:S(2)}, u32[]{:S(2)}) %collective-permute-start.1) | collective-permute-done | bytes 1704992 | tf_op jit(solution)/shard_map/ppermute | solution.py:20
  50.5 10.4 %conditional.7 = (bf16[1024,1024]{1,0:T(8,128)(2,1)}, f32[1024,64]{0,1:T(8,128)S(1)}, f32[1024]{0:T(1024)S(1)}, f32[1024,64]{0,1:T(8,128)S(1)}, f32[1024]{0:T(1024)S(1)}) conditional(s32[]{:T(128)} %convert_element_type.57, () %tuple.58, (bf16[1110,768]{1,0:T(8,128)(2,1)}, bf16[1024,768]{1,0:T(8,128)(2,1)S(1)}, bf16[66048]{0:T(1024)(128)(2,1)S(1)}) %tuple.105), branch_computations={%region_7.8_spmd, %region_8.11_spmd} | conditional | flops 1884289024 | bytes 11415592 | solution.py:101
  50.5 4.7 %convert_reduce_fusion.2 = (f32[1024]{0:T(1024)S(1)}, f32[1024]{0:T(1024)S(1)}, bf16[1024,1024]{1,0:T(8,128)(2,1)}) fusion(bf16[1024,768]{1,0:T(8,128)(2,1)S(1)} %get-tuple-element.38, bf16[1110,768]{1,0:T(8,128)(2,1)} %get-tuple-element.37), kind=kOutput, calls=%fused_computation.6 | convolution fusion | flops 1615853568 | bytes 5251072 | tf_op jit(solution)/shard_map/cond/branch_1_fun/dot_general | solution.py:55
  55.3 2.4 %fusion.62 = f32[1024,64]{0,1:T(8,128)S(1)} fusion(bf16[1024,1024]{1,0:T(8,128)(2,1)} %get-tuple-element.147, bf16[1024,64]{1,0:T(8,128)(2,1)S(1)} %reshape.120), kind=kOutput, calls=%fused_computation.141 | convolution fusion | flops 134217728 | bytes 2490368 | tf_op jit(solution)/shard_map/cond/branch_1_fun/dot_general | solution.py:62
  57.7 0.9 slice.144
  58.8 2.1 fusion.4
  60.9 22.6 %collective-permute-done = bf16[1110,768]{1,0:T(8,128)(2,1)} collective-permute-done((bf16[1110,768]{1,0:T(8,128)(2,1)}, bf16[1110,768]{1,0:T(8,128)(2,1)}, u32[]{:S(2)}, u32[]{:S(2)}) %collective-permute-start) | collective-permute-done | bytes 1704992 | tf_op jit(solution)/shard_map/ppermute | solution.py:20
  83.5 1.7 conditional.8
  83.5 1.6 broadcast.96
  85.2 0.7 copy-done.3
  86.3 0.7 pad_maximum_fusion.2
  87.0 25.8 %collective-permute-start.3 = (f32[520,128]{1,0:T(8,128)}, f32[520,128]{1,0:T(8,128)}, u32[]{:S(2)}, u32[]{:S(2)}) collective-permute-start(f32[520,128]{1,0:T(8,128)} %pad_maximum_fusion.2), channel_id=1, source_target_pairs={{8,0},{12,4},{16,8},{20,12},{24,16},{28,20},{0,24},{4,28},{9,1},{1... | collective-permute-start | bytes 798728 | tf_op jit(solution)/shard_map/ppermute | solution.py:20
  112.8 11.2 %conditional.6 = (bf16[1024,1024]{1,0:T(8,128)(2,1)}, f32[1024,64]{0,1:T(8,128)S(1)}, f32[1024]{0:T(1024)S(1)}, f32[1024,64]{0,1:T(8,128)S(1)}, f32[1024]{0:T(1024)S(1)}) conditional(s32[]{:T(128)} %convert_element_type.56, () %tuple.56, (bf16[1110,768]{1,0:T(8,128)(2,1)}, bf16[1024,768]{1,0:T(8,128)(2,1)}, bf16[66048]{0:T(1024)(128)(2,1)S(1)}) %tuple.104), branch_computations={%region_2.3_spmd, %region_3.0_spmd} | conditional | flops 1884289024 | bytes 11415592 | solution.py:101
  112.8 5.3 %convert_reduce_fusion = (f32[1024]{0:T(1024)S(1)}, f32[1024]{0:T(1024)S(1)}, bf16[1024,1024]{1,0:T(8,128)(2,1)}) fusion(bf16[1024,768]{1,0:T(8,128)(2,1)} %get-tuple-element.34, bf16[1110,768]{1,0:T(8,128)(2,1)} %get-tuple-element.35), kind=kOutput, calls=%fused_computation | convolution fusion | flops 1615853568 | bytes 5251072 | tf_op jit(solution)/shard_map/cond/branch_1_fun/dot_general | solution.py:55
  118.1 0.9 slice.138
  119.2 2.4 %fusion.1 = f32[1024,64]{0,1:T(8,128)S(1)} fusion(bf16[1024,1024]{1,0:T(8,128)(2,1)} %get-tuple-element.167, bf16[1032,64]{1,0:T(8,128)(2,1)S(1)} %slice.139), kind=kOutput, calls=%fused_computation.4 | convolution fusion | flops 134217728 | bytes 2621440 | tf_op jit(solution)/shard_map/cond/branch_1_fun/dot_general | solution.py:62
  121.7 2.1 fusion.61
  124.0 0.7 copy-done.6
  125.1 0.7 pad_maximum_fusion.1
  126.4 1.0 slice.238
  127.7 7.6 %collective-permute-done.2 = f32[520,128]{1,0:T(8,128)} collective-permute-done((f32[520,128]{1,0:T(8,128)}, f32[520,128]{1,0:T(8,128)}, u32[]{:S(2)}, u32[]{:S(2)}) %collective-permute-start.2) | collective-permute-done | bytes 266272 | tf_op jit(solution)/shard_map/ppermute | solution.py:20
  135.3 1.0 slice.237
  136.6 1.2 fusion.52
  137.8 1.3 broadcast_multiply_fusion
  140.0 0.7 reduce_sum.143
  140.6 0.8 pad_maximum_fusion.13
  141.6 1.2 collective-permute-done.6
  142.9 3.7 %collective-permute-done.7 = f32[35,128]{1,0:T(8,128)S(1)} collective-permute-done((f32[35,128]{1,0:T(8,128)S(1)}, f32[35,128]{1,0:T(8,128)S(1)}, u32[]{:S(2)}, u32[]{:S(2)}) %collective-permute-start.7) | collective-permute-done | bytes 17952 | tf_op jit(solution)/shard_map/ppermute | solution.py:131
  146.8 3.8 %collective-permute-done.8 = f32[37,128]{1,0:T(8,128)S(1)} collective-permute-done((f32[37,128]{1,0:T(8,128)S(1)}, f32[37,128]{1,0:T(8,128)S(1)}, u32[]{:S(2)}, u32[]{:S(2)}) %collective-permute-start.8) | collective-permute-done | bytes 18976 | tf_op jit(solution)/shard_map/ppermute | solution.py:131
  150.7 3.8 %collective-permute-done.9 = f32[41,128]{1,0:T(8,128)S(1)} collective-permute-done((f32[41,128]{1,0:T(8,128)S(1)}, f32[41,128]{1,0:T(8,128)S(1)}, u32[]{:S(2)}, u32[]{:S(2)}) %collective-permute-start.9) | collective-permute-done | bytes 21024 | tf_op jit(solution)/shard_map/ppermute | solution.py:131
  154.9 3.0 %collective-permute-start.4 = (f32[1024,64]{0,1:T(8,128)S(1)}, f32[1024,64]{0,1:T(8,128)S(1)}, u32[]{:S(2)}, u32[]{:S(2)}) collective-permute-start(f32[1024,64]{0,1:T(8,128)S(1)} %get-tuple-element.129), channel_id=1, source_target_pairs={{4,0},{8,4},{12,8},{16,12},{20,16},{24,20},{28,24},{0,28},{5,1},{9... | collective-permute-start | bytes 786440 | tf_op jit(solution)/shard_map/ppermute | solution.py:20
  157.9 1.9 collective-permute-done.10
  161.5 0.9 fusion.21.gram_ref
  162.4 8.4 %shard_map.50 = f32[64,64]{1,0:T(8,128)} custom-call(f32[64,64]{1,0:T(8,128)} %fusion.21.gram_ref), custom_call_target="tpu_custom_call" | custom-call | tf_op jit(solution)/shard_map/pallas_call | solution.py:179
  170.8 1.7 convolution_convert_fusion
  172.6 0.7 copy-done.7
  173.3 4.4 %conditional.10 = (f32[1024,64]{0,1:T(8,128)S(1)}, f32[1024,64]{0,1:T(8,128)S(1)}) conditional(s32[]{:T(128)} %convert_element_type.57, () %tuple.64, (bf16[1024,1024]{1,0:T(8,128)(2,1)}, bf16[1024,64]{0,1:T(8,128)(2,1)S(1)}, bf16[1024,64]{0,1:T(8,128)(2,1)S(1)}) %tuple.65), branch_computations={%region_23.24_spmd, %region_24.25_spmd} | conditional | flops 268435456 | bytes 4980752 | solution.py:115
  173.3 2.3 %fusion.57 = f32[1024,64]{0,1:T(8,128)S(1)} fusion(bf16[1024,1024]{1,0:T(8,128)(2,1)} %get-tuple-element.45, bf16[1024,64]{0,1:T(8,128)(2,1)S(1)} %get-tuple-element.108), kind=kOutput, calls=%fused_computation.136 | convolution fusion | flops 134217728 | bytes 2490368 | tf_op jit(solution)/shard_map/cond/branch_1_fun/dot_general | solution.py:62
  175.6 2.1 fusion.58
  177.8 0.7 add.225
  178.5 3.9 %collective-permute-start.12 = (f32[1024,64]{0,1:T(8,128)}, f32[1024,64]{0,1:T(8,128)}, u32[]{:S(2)}, u32[]{:S(2)}) collective-permute-start(f32[1024,64]{0,1:T(8,128)} %add.225), channel_id=1, source_target_pairs={{8,0},{12,4},{16,8},{20,12},{24,16},{28,20},{0,24},{4,28},{9,1},{1... | collective-permute-start | bytes 786440 | tf_op jit(solution)/shard_map/ppermute | solution.py:20
  182.5 4.4 %conditional.9 = (f32[1024,64]{0,1:T(8,128)S(1)}, f32[1024,64]{0,1:T(8,128)S(1)}) conditional(s32[]{:T(128)} %convert_element_type.56, () %tuple.62, (bf16[1024,1024]{1,0:T(8,128)(2,1)}, bf16[1024,64]{0,1:T(8,128)(2,1)S(1)}, bf16[1024,64]{0,1:T(8,128)(2,1)S(1)}) %tuple.63), branch_computations={%region_21.22_spmd, %region_22.23_spmd} | conditional | flops 268435456 | bytes 4980752 | solution.py:115
  182.5 2.3 %fusion.55 = f32[1024,64]{0,1:T(8,128)S(1)} fusion(bf16[1024,1024]{1,0:T(8,128)(2,1)} %get-tuple-element.42, bf16[1024,64]{0,1:T(8,128)(2,1)S(1)} %get-tuple-element.105), kind=kOutput, calls=%fused_computation.134 | convolution fusion | flops 134217728 | bytes 2490368 | tf_op jit(solution)/shard_map/cond/branch_1_fun/dot_general | solution.py:62
  184.8 2.1 fusion.56
  187.0 0.7 collective-permute-done.12
  187.7 8.4 %collective-permute-done.11 = f32[1024,64]{0,1:T(8,128)S(1)} collective-permute-done((f32[1024,64]{0,1:T(8,128)S(1)}, f32[1024,64]{0,1:T(8,128)S(1)}, u32[]{:S(2)}, u32[]{:S(2)}) %collective-permute-start.11) | collective-permute-done | bytes 262176 | tf_op jit(solution)/shard_map/ppermute | solution.py:20
  196.1 1.7 fusion.49
  198.4 0.8 pad_maximum_fusion.14
  199.3 1.2 collective-permute-done.13
  201.1 3.3 %collective-permute-done.14 = f32[35,128]{1,0:T(8,128)S(1)} collective-permute-done((f32[35,128]{1,0:T(8,128)S(1)}, f32[35,128]{1,0:T(8,128)S(1)}, u32[]{:S(2)}, u32[]{:S(2)}) %collective-permute-start.14) | collective-permute-done | bytes 17952 | tf_op jit(solution)/shard_map/ppermute | solution.py:131
  204.5 3.8 %collective-permute-done.15 = f32[37,128]{1,0:T(8,128)S(1)} collective-permute-done((f32[37,128]{1,0:T(8,128)S(1)}, f32[37,128]{1,0:T(8,128)S(1)}, u32[]{:S(2)}, u32[]{:S(2)}) %collective-permute-start.15) | collective-permute-done | bytes 18976 | tf_op jit(solution)/shard_map/ppermute | solution.py:131
  208.4 3.8 %collective-permute-done.16 = f32[41,128]{1,0:T(8,128)S(1)} collective-permute-done((f32[41,128]{1,0:T(8,128)S(1)}, f32[41,128]{1,0:T(8,128)S(1)}, u32[]{:S(2)}, u32[]{:S(2)}) %collective-permute-start.16) | collective-permute-done | bytes 21024 | tf_op jit(solution)/shard_map/ppermute | solution.py:131
  212.6 4.5 %collective-permute-done.17 = f32[49,128]{1,0:T(8,128)S(1)} collective-permute-done((f32[49,128]{1,0:T(8,128)S(1)}, f32[49,128]{1,0:T(8,128)S(1)}, u32[]{:S(2)}, u32[]{:S(2)}) %collective-permute-start.17) | collective-permute-done | bytes 25120 | tf_op jit(solution)/shard_map/ppermute | solution.py:131
  218.8 0.9 fusion.19.gram_ref
  219.7 8.4 %shard_map.51 = f32[64,64]{1,0:T(8,128)} custom-call(f32[64,64]{1,0:T(8,128)} %fusion.19.gram_ref), custom_call_target="tpu_custom_call" | custom-call | tf_op jit(solution)/shard_map/pallas_call | solution.py:179
  228.1 1.9 fusion.27
  (129 shorter events, 10.5 us)
Async XLA Ops:
  0.6 3.3 %copy-start = (bf16[1024,768]{1,0:T(8,128)(2,1)S(1)}, bf16[1024,768]{1,0:T(8,128)(2,1)}, u32[]{:S(2)}) copy-start(bf16[1024,768]{1,0:T(8,128)(2,1)} %param.15) | copy-start | bytes 4718596
  4.4 1.2 copy-start.1
  5.6 7.6 %copy-start.9 = (s32[32,3]{0,1:T(4,128)S(1)}, s32[32,3]{0,1:T(4,128)}, u32[]{:S(2)}) copy-start(s32[32,3]{0,1:T(4,128)} %param.17) | copy-start | bytes 1156
  7.0 43.5 %collective-permute-start.1 = (bf16[1110,768]{1,0:T(8,128)(2,1)}, bf16[1110,768]{1,0:T(8,128)(2,1)}, u32[]{:S(2)}, u32[]{:S(2)}) collective-permute-start(bf16[1110,768]{1,0:T(8,128)(2,1)} %pad_maximum_fusion), channel_id=1, source_target_pairs={{24,0},{28,4},{0,8},{4,12},{8,16},{12,20},{16,24},{20,28},{25,1},{... | collective-permute-start | bytes 5114888 | tf_op jit(solution)/shard_map/ppermute | solution.py:20
  10.0 73.5 %collective-permute-start = (bf16[1110,768]{1,0:T(8,128)(2,1)}, bf16[1110,768]{1,0:T(8,128)(2,1)}, u32[]{:S(2)}, u32[]{:S(2)}) collective-permute-start(bf16[1110,768]{1,0:T(8,128)(2,1)} %pad_maximum_fusion), channel_id=1, source_target_pairs={{4,0},{8,4},{12,8},{16,12},{20,16},{24,20},{28,24},{0,28},{5,1},{9... | collective-permute-start | bytes 5114888 | tf_op jit(solution)/shard_map/ppermute | solution.py:20
  15.8 34.7 %copy-start.2 = (bf16[1024,768]{1,0:T(8,128)(2,1)S(1)}, bf16[1024,768]{1,0:T(8,128)(2,1)}, u32[]{:S(2)}) copy-start(bf16[1024,768]{1,0:T(8,128)(2,1)} %copy-done.1) | copy-start | bytes 4718596
  60.9 22.6 %copy-start.5 = (f32[1024,64]{0,1:T(8,128)}, f32[1024,64]{0,1:T(8,128)S(1)}, u32[]{:S(2)}) copy-start(f32[1024,64]{0,1:T(8,128)S(1)} %get-tuple-element.75) | copy-start | bytes 786436
  85.2 0.7 copy-start.3
  87.0 39.4 %collective-permute-start.3 = (f32[520,128]{1,0:T(8,128)}, f32[520,128]{1,0:T(8,128)}, u32[]{:S(2)}, u32[]{:S(2)}) collective-permute-start(f32[520,128]{1,0:T(8,128)} %pad_maximum_fusion.2), channel_id=1, source_target_pairs={{8,0},{12,4},{16,8},{20,12},{24,16},{28,20},{0,24},{4,28},{9,1},{1... | collective-permute-start | bytes 798728 | tf_op jit(solution)/shard_map/ppermute | solution.py:20
  112.8 11.9 %copy-start.4 = (f32[1024,64]{0,1:T(8,128)S(1)}, f32[1024,64]{0,1:T(8,128)}, u32[]{:S(2)}) copy-start(f32[1024,64]{0,1:T(8,128)} %copy-done.3) | copy-start | bytes 786436
  124.0 0.7 copy-start.6
  124.0 1.8 copy-start.8
  125.9 9.4 %collective-permute-start.2 = (f32[520,128]{1,0:T(8,128)}, f32[520,128]{1,0:T(8,128)}, u32[]{:S(2)}, u32[]{:S(2)}) collective-permute-start(f32[520,128]{1,0:T(8,128)} %pad_maximum_fusion.1), channel_id=1, source_target_pairs={{28,0},{0,4},{4,8},{8,12},{12,16},{16,20},{20,24},{24,28},{29,1},{... | collective-permute-start | bytes 798728 | tf_op jit(solution)/shard_map/ppermute | solution.py:20
  141.5 1.3 collective-permute-start.6
  142.8 3.8 %collective-permute-start.7 = (f32[35,128]{1,0:T(8,128)S(1)}, f32[35,128]{1,0:T(8,128)S(1)}, u32[]{:S(2)}, u32[]{:S(2)}) collective-permute-start(f32[35,128]{1,0:T(8,128)S(1)} %pad_maximum_fusion.8), channel_id=1, source_target_pairs={{0,2},{1,3},{2,0},{3,1},{4,6},{5,7},{6,4},{7,5},{8,10},{9,11},{10,... | collective-permute-start | bytes 53768 | tf_op jit(solution)/shard_map/ppermute | solution.py:131
  146.7 3.8 %collective-permute-start.8 = (f32[37,128]{1,0:T(8,128)S(1)}, f32[37,128]{1,0:T(8,128)S(1)}, u32[]{:S(2)}, u32[]{:S(2)}) collective-permute-start(f32[37,128]{1,0:T(8,128)S(1)} %pad_maximum_fusion.9), channel_id=1, source_target_pairs={{0,4},{4,0},{8,12},{12,8},{16,20},{20,16},{24,28},{28,24},{1,5},{5... | collective-permute-start | bytes 56840 | tf_op jit(solution)/shard_map/ppermute | solution.py:131
  150.6 3.9 %collective-permute-start.9 = (f32[41,128]{1,0:T(8,128)S(1)}, f32[41,128]{1,0:T(8,128)S(1)}, u32[]{:S(2)}, u32[]{:S(2)}) collective-permute-start(f32[41,128]{1,0:T(8,128)S(1)} %pad_maximum_fusion.5), channel_id=1, source_target_pairs={{0,8},{4,12},{8,0},{12,4},{16,24},{20,28},{24,16},{28,20},{1,9},{5... | collective-permute-start | bytes 62984 | tf_op jit(solution)/shard_map/ppermute | solution.py:131
  154.5 5.3 %collective-permute-start.10 = (f32[49,128]{1,0:T(8,128)S(1)}, f32[49,128]{1,0:T(8,128)S(1)}, u32[]{:S(2)}, u32[]{:S(2)}) collective-permute-start(f32[49,128]{1,0:T(8,128)S(1)} %pad_maximum_fusion.3), channel_id=1, source_target_pairs={{0,16},{4,20},{8,24},{12,28},{16,0},{20,4},{24,8},{28,12},{1,17},{... | collective-permute-start | bytes 75272 | tf_op jit(solution)/shard_map/ppermute | solution.py:131
  154.6 16.2 %collective-permute-start.5 = (f32[1024,64]{0,1:T(8,128)S(1)}, f32[1024,64]{0,1:T(8,128)S(1)}, u32[]{:S(2)}, u32[]{:S(2)}) collective-permute-start(f32[1024,64]{0,1:T(8,128)S(1)} %get-tuple-element.129), channel_id=1, source_target_pairs={{24,0},{28,4},{0,8},{4,12},{8,16},{12,20},{16,24},{20,28},{25,1},{... | collective-permute-start | bytes 786440 | tf_op jit(solution)/shard_map/ppermute | solution.py:20
  154.9 15.9 %collective-permute-start.4 = (f32[1024,64]{0,1:T(8,128)S(1)}, f32[1024,64]{0,1:T(8,128)S(1)}, u32[]{:S(2)}, u32[]{:S(2)}) collective-permute-start(f32[1024,64]{0,1:T(8,128)S(1)} %get-tuple-element.129), channel_id=1, source_target_pairs={{4,0},{8,4},{12,8},{16,12},{20,16},{24,20},{28,24},{0,28},{5,1},{9... | collective-permute-start | bytes 786440 | tf_op jit(solution)/shard_map/ppermute | solution.py:20
  172.5 0.8 copy-start.7
  178.5 9.2 %collective-permute-start.12 = (f32[1024,64]{0,1:T(8,128)}, f32[1024,64]{0,1:T(8,128)}, u32[]{:S(2)}, u32[]{:S(2)}) collective-permute-start(f32[1024,64]{0,1:T(8,128)} %add.225), channel_id=1, source_target_pairs={{8,0},{12,4},{16,8},{20,12},{24,16},{28,20},{0,24},{4,28},{9,1},{1... | collective-permute-start | bytes 786440 | tf_op jit(solution)/shard_map/ppermute | solution.py:20
  186.9 9.1 %collective-permute-start.11 = (f32[1024,64]{0,1:T(8,128)S(1)}, f32[1024,64]{0,1:T(8,128)S(1)}, u32[]{:S(2)}, u32[]{:S(2)}) collective-permute-start(f32[1024,64]{0,1:T(8,128)S(1)} %add.223), channel_id=1, source_target_pairs={{28,0},{0,4},{4,8},{8,12},{12,16},{16,20},{20,24},{24,28},{29,1},{... | collective-permute-start | bytes 786440 | tf_op jit(solution)/shard_map/ppermute | solution.py:20
  199.3 1.2 collective-permute-start.13
  200.6 3.8 %collective-permute-start.14 = (f32[35,128]{1,0:T(8,128)S(1)}, f32[35,128]{1,0:T(8,128)S(1)}, u32[]{:S(2)}, u32[]{:S(2)}) collective-permute-start(f32[35,128]{1,0:T(8,128)S(1)} %pad_maximum_fusion.11), channel_id=1, source_target_pairs={{0,2},{1,3},{2,0},{3,1},{4,6},{5,7},{6,4},{7,5},{8,10},{9,11},{10,... | collective-permute-start | bytes 53768 | tf_op jit(solution)/shard_map/ppermute | solution.py:131
  204.5 3.8 %collective-permute-start.15 = (f32[37,128]{1,0:T(8,128)S(1)}, f32[37,128]{1,0:T(8,128)S(1)}, u32[]{:S(2)}, u32[]{:S(2)}) collective-permute-start(f32[37,128]{1,0:T(8,128)S(1)} %pad_maximum_fusion.12), channel_id=1, source_target_pairs={{0,4},{4,0},{8,12},{12,8},{16,20},{20,16},{24,28},{28,24},{1,5},{5... | collective-permute-start | bytes 56840 | tf_op jit(solution)/shard_map/ppermute | solution.py:131
  208.3 3.9 %collective-permute-start.16 = (f32[41,128]{1,0:T(8,128)S(1)}, f32[41,128]{1,0:T(8,128)S(1)}, u32[]{:S(2)}, u32[]{:S(2)}) collective-permute-start(f32[41,128]{1,0:T(8,128)S(1)} %pad_maximum_fusion.6), channel_id=1, source_target_pairs={{0,8},{4,12},{8,0},{12,4},{16,24},{20,28},{24,16},{28,20},{1,9},{5... | collective-permute-start | bytes 62984 | tf_op jit(solution)/shard_map/ppermute | solution.py:131
  212.3 4.8 %collective-permute-start.17 = (f32[49,128]{1,0:T(8,128)S(1)}, f32[49,128]{1,0:T(8,128)S(1)}, u32[]{:S(2)}, u32[]{:S(2)}) collective-permute-start(f32[49,128]{1,0:T(8,128)S(1)} %pad_maximum_fusion.4), channel_id=1, source_target_pairs={{0,16},{4,20},{8,24},{12,28},{16,0},{20,4},{24,8},{28,12},{1,17},{... | collective-permute-start | bytes 75272 | tf_op jit(solution)/shard_map/ppermute | solution.py:131

commit v8 on v7

--- a/solution.py
+++ b/solution.py
@@ -68,16 +68,11 @@
     )
 
 
-def unpack(packed, block_rows, vector_count):
-    weights = packed[block_rows:].reshape(-1)[: block_rows * vector_count]
-    return packed[:block_rows], weights.reshape(block_rows, vector_count)
-
-
-def first_pass(owned, left_packed, right_packed, block_rows, vector_count):
+def first_pass(owned, left_unit, right_unit, left_weights, right_weights):
+    block_rows = left_unit.shape[0]
+    vector_count = left_weights.shape[1]
 
     def compute_pair():
-        left_unit, left_weights = unpack(left_packed, block_rows, vector_count)
-        right_unit, right_weights = unpack(right_packed, block_rows, vector_count)
         affinity = scores_tile(left_unit, right_unit)
         return (
             affinity,
@@ -235,12 +230,12 @@
         own_row = lax.dynamic_slice_in_dim(neighbours, block_at(left), 1, 0)[0]
         owned_list.append(jnp.any(own_row == block_at(right)))
 
-    unit_width = unit_block.shape[1]
     vector_count = start.shape[1]
-    packed = jnp.concatenate([unit_block, as_rows(start.reshape(-1), unit_width)])
-    units = {0: packed}
+    units = {0: unit_block}
+    weights = {0: start}
     for offset in fetch_offsets:
-        units[offset] = shifted(packed, "wide", -offset)
+        units[offset] = normalize_rows(shifted(embeddings, "wide", -offset))
+        weights[offset] = shifted(start, "wide", -offset)
 
     self_mask = lax.broadcasted_iota(
         jnp.int32, (block_rows, block_rows), 0
@@ -256,7 +251,7 @@
     tiles = []
     for (left, right), owned in zip(pair_plan, owned_list):
         affinity, row_part, row_sum, col_part, col_sum = first_pass(
-            owned, units[left], units[right], block_rows, vector_count
+            owned, units[left], units[right], weights[left], weights[right]
         )
         tiles.append(affinity)
         parts[left] = parts[left] + row_part

time: 229 us -> 223 us (0.974)
  matrix products: 40.7 us -> 25.5 us
  other arithmetic: 13.4 us -> 21.2 us
  starting transfers between devices: 40.7 us -> 46.3 us
  waiting for transfers between devices: 101 us -> 96.9 us
    dot_general x3 -> x2, matrix products: 14 us -> 7.79 us  [scores_tile(): lax.dot_general(leftside_block, right_block, (((1,), (1,)), ((), ())), pr...]
    convert_element_type x1 -> x3, other arithmetic: 0.42 us -> 5.9 us  [normalize_rows(): (values_wide * scaling / math.sqrt(values_wide.shape[-1])).astype(jnp.bfl...]
    dot_general x6 -> x4, matrix products: 11.5 us -> 6.82 us  [row_product(): return jnp.dot(affinity, weights, preferred_element_type=jnp.float32)]
    dot_general x4 -> x2, matrix products: 8.39 us -> 4.14 us  [col_product(): lax.dot_general(affinity, weights, (((0,), (0,)), ((), ())), preferred_el...]
    reduce_sum x1 -> x3, other arithmetic: 1.78 us -> 5.35 us  [normalize_rows(): jnp.mean(values_wide * values_wide, axis=-1, keepdims=True) + 1e-06]
    ppermute x10, starting transfers between devices: 1.37 us -> 4.44 us  [butterfly(): other = lax.ppermute(block, axis, route)]
    ppermute x10, waiting for transfers between devices: 31 us -> 28.1 us  [butterfly(): other = lax.ppermute(block, axis, route)]
    ppermute x8 -> x10, starting transfers between devices: 39.4 us -> 41.9 us  [shifted(): return lax.ppermute(block, axis, route)]
  transfers between devices with their start and end apart: 18 -> 20, of which waited for: 15 -> 16; matrix products, arithmetic and copies ran while one was open for 16% -> 17% of each run, Pallas kernels for 4% -> 4%
where the time goes in v8:
time: 223 us; the launch traced here: 222 us
  waiting for transfers between devices  96.9 us (43%)
  starting transfers between devices  46.3 us (21%)
  matrix products  25.5 us (11%)
  other arithmetic  21.2 us (10%)
  Pallas kernels  16.8 us (8%)
  local copies, waits for them, and re-layouts  11.9 us (5%)
  between operations  3.23 us (1%)
    ppermute x10, waiting for transfers between devices, shifted(): return lax.ppermute(block, axis, route)  68.9 us
    ppermute x10, starting transfers between devices, shifted(): return lax.ppermute(block, axis, route)  41.9 us
    ppermute x10, waiting for transfers between devices, butterfly(): other = lax.ppermute(block, axis, route)  28.1 us
    pallas_call x2, Pallas kernels, factor_inverse(): pl.pallas_call(factor_kernel, out_shape=jax.ShapeDtypeStruct(gram_matrix....  16.8 us
    dot_general x2, matrix products, scores_tile(): lax.dot_general(leftside_block, right_block, (((1,), (1,)), ((), ())), pr...  7.79 us
    dot_general x4, matrix products, row_product(): return jnp.dot(affinity, weights, preferred_element_type=jnp.float32)  6.82 us
    dot_general x8, matrix products, hdot(): jnp.dot(left, right, precision=lax.Precision.HIGHEST, preferred_element_t...  6.78 us
    convert_element_type x3, other arithmetic, normalize_rows(): (values_wide * scaling / math.sqrt(values_wide.shape[-1])).astype(jnp.bfl...  5.9 us
  transfers between devices with their start and end apart: 20, of which 16 were waited for; matrix products, arithmetic and copies ran while one was open for 17% of the time, Pallas kernels for 4%

profile of v8, /device:TPU:0, one launch (start us, length us, event | category | flops | bytes accessed | tf_op | source)
XLA Modules:
  0.0 222.0 jit_solution(11868271466939780860)
XLA Ops:
  0.6 3.1 %collective-permute-start.2 = (bf16[1024,768]{1,0:T(8,128)(2,1)}, bf16[1024,768]{1,0:T(8,128)(2,1)}, u32[]{:S(2)}, u32[]{:S(2)}) collective-permute-start(bf16[1024,768]{1,0:T(8,128)(2,1)} %param.15), channel_id=1, source_target_pairs={{24,0},{28,4},{0,8},{4,12},{8,16},{12,20},{16,24},{20,28},{25,1},{... | collective-permute-start | bytes 4718600 | tf_op jit(solution)/shard_map/ppermute | solution.py:20
  3.7 3.2 %collective-permute-start = (bf16[1024,768]{1,0:T(8,128)(2,1)}, bf16[1024,768]{1,0:T(8,128)(2,1)}, u32[]{:S(2)}, u32[]{:S(2)}) collective-permute-start(bf16[1024,768]{1,0:T(8,128)(2,1)} %param.15), channel_id=1, source_target_pairs={{4,0},{8,4},{12,8},{16,12},{20,16},{24,20},{28,24},{0,28},{5,1},{9... | collective-permute-start | bytes 4718600 | tf_op jit(solution)/shard_map/ppermute | solution.py:20
  6.9 1.1 copy.17
  8.1 2.1 collective-permute-start.1
  10.1 1.8 fusion.1
  12.0 1.5 fusion.40
  15.7 2.5 %convert_reduce_fusion.6 = (f32[1024]{0:T(1024)}, bf16[1024,1024]{0,1:T(8,128)(2,1)S(1)}) fusion(bf16[1024,768]{1,0:T(8,128)(2,1)S(1)} %fusion.3), kind=kOutput, calls=%fused_computation.9 | convolution fusion | flops 1616903168 | bytes 3674112 | tf_op jit(solution)/shard_map/dot_general | solution.py:55
  18.3 23.1 %collective-permute-done.2 = bf16[1024,768]{1,0:T(8,128)(2,1)} collective-permute-done((bf16[1024,768]{1,0:T(8,128)(2,1)}, bf16[1024,768]{1,0:T(8,128)(2,1)}, u32[]{:S(2)}, u32[]{:S(2)}) %collective-permute-start.2) | collective-permute-done | bytes 1572896 | tf_op jit(solution)/shard_map/ppermute | solution.py:20
  41.3 1.8 fusion.7
  43.1 29.5 %collective-permute-done = bf16[1024,768]{1,0:T(8,128)(2,1)} collective-permute-done((bf16[1024,768]{1,0:T(8,128)(2,1)}, bf16[1024,768]{1,0:T(8,128)(2,1)}, u32[]{:S(2)}, u32[]{:S(2)}) %collective-permute-start) | collective-permute-done | bytes 1572896 | tf_op jit(solution)/shard_map/ppermute | solution.py:20
  72.6 1.8 fusion.4
  74.4 1.8 fusion.9
  76.2 3.6 %fusion.6 = bf16[1024,768]{1,0:T(8,128)(2,1)} fusion(bf16[1024,768]{1,0:T(8,128)(2,1)} %collective-permute-done, f32[1024]{0:T(1024)S(1)} %add_rsqrt_fusion.1), kind=kLoop, calls=%fused_computation.25 | loop fusion | flops 3145728 | bytes 3149824 | tf_op jit(solution)/shard_map/convert_element_type | solution.py:51
  79.9 0.7 collective-permute-done.3
  80.6 1.6 conditional.7
  80.6 1.6 broadcast.122
  83.0 1.7 conditional.8
  83.0 1.6 broadcast.126
  84.7 0.7 copy-done.4
  85.8 0.7 pad_maximum_fusion.1
  86.5 20.6 %collective-permute-start.5 = (f32[520,128]{1,0:T(8,128)}, f32[520,128]{1,0:T(8,128)}, u32[]{:S(2)}, u32[]{:S(2)}) collective-permute-start(f32[520,128]{1,0:T(8,128)} %pad_maximum_fusion.1), channel_id=1, source_target_pairs={{8,0},{12,4},{16,8},{20,12},{24,16},{28,20},{0,24},{4,28},{9,1},{1... | collective-permute-start | bytes 798728 | tf_op jit(solution)/shard_map/ppermute | solution.py:20
  107.1 9.7 %conditional.6 = (bf16[1024,1024]{1,0:T(8,128)(2,1)}, f32[1024,64]{0,1:T(8,128)S(1)}, f32[1024]{0:T(1024)S(1)}, f32[1024,64]{0,1:T(8,128)S(1)}, f32[1024]{0:T(1024)S(1)}) conditional(s32[]{:T(128)} %convert_element_type.66, () %tuple.56, (bf16[1024,768]{1,0:T(8,128)(2,1)}, bf16[1024,768]{1,0:T(8,128)(2,1)}, bf16[1024,64]{1,0:T(8,128)(2,1)S(1)}, ...), branch_computations={%region_3.4_spmd, %region_4.0_spmd} | conditional | flops 1884289024 | bytes 10231848 | solution.py:96
  107.1 5.3 %convert_reduce_fusion = (f32[1024]{0:T(1024)S(1)}, f32[1024]{0:T(1024)S(1)}, bf16[1024,1024]{1,0:T(8,128)(2,1)}) fusion(bf16[1024,768]{1,0:T(8,128)(2,1)} %get-tuple-element.42, bf16[1024,768]{1,0:T(8,128)(2,1)} %get-tuple-element.43), kind=kOutput, calls=%fused_computation | convolution fusion | flops 1615853568 | bytes 5251072 | tf_op jit(solution)/shard_map/cond/branch_1_fun/dot_general | solution.py:55
  112.4 2.3 %fusion.55 = f32[1024,64]{0,1:T(8,128)S(1)} fusion(bf16[1024,1024]{1,0:T(8,128)(2,1)} %get-tuple-element.195, bf16[1024,64]{1,0:T(8,128)(2,1)S(1)} %get-tuple-element.44), kind=kOutput, calls=%fused_computation.139 | convolution fusion | flops 134217728 | bytes 2490368 | tf_op jit(solution)/shard_map/cond/branch_1_fun/dot_general | solution.py:62
  114.7 2.1 fusion.56
  116.8 0.7 copy-done.7
  118.5 1.0 slice.164
  119.8 7.4 %collective-permute-done.4 = f32[520,128]{1,0:T(8,128)} collective-permute-done((f32[520,128]{1,0:T(8,128)S(1)}, f32[520,128]{1,0:T(8,128)}, u32[]{:S(2)}, u32[]{:S(2)}) %collective-permute-start.4) | collective-permute-done | bytes 266272 | tf_op jit(solution)/shard_map/ppermute | solution.py:20
  127.2 1.0 slice.163
  128.5 1.2 fusion.46
  129.7 1.3 broadcast_multiply_fusion
  131.8 0.7 reduce_sum.163
  132.5 0.8 pad_maximum_fusion.12
  133.5 1.2 collective-permute-done.8
  134.7 1.6 collective-permute-start.9
  136.2 2.3 %collective-permute-done.9 = f32[35,128]{1,0:T(8,128)S(1)} collective-permute-done((f32[35,128]{1,0:T(8,128)S(1)}, f32[35,128]{1,0:T(8,128)S(1)}, u32[]{:S(2)}, u32[]{:S(2)}) %collective-permute-start.9) | collective-permute-done | bytes 17952 | tf_op jit(solution)/shard_map/ppermute | solution.py:126
  138.7 3.8 %collective-permute-done.10 = f32[37,128]{1,0:T(8,128)S(1)} collective-permute-done((f32[37,128]{1,0:T(8,128)S(1)}, f32[37,128]{1,0:T(8,128)S(1)}, u32[]{:S(2)}, u32[]{:S(2)}) %collective-permute-start.10) | collective-permute-done | bytes 18976 | tf_op jit(solution)/shard_map/ppermute | solution.py:126
  142.6 3.8 %collective-permute-done.11 = f32[41,128]{1,0:T(8,128)S(1)} collective-permute-done((f32[41,128]{1,0:T(8,128)S(1)}, f32[41,128]{1,0:T(8,128)S(1)}, u32[]{:S(2)}, u32[]{:S(2)}) %collective-permute-start.11) | collective-permute-done | bytes 21024 | tf_op jit(solution)/shard_map/ppermute | solution.py:126
  146.8 3.0 %collective-permute-start.6 = (f32[1024,64]{0,1:T(8,128)S(1)}, f32[1024,64]{0,1:T(8,128)S(1)}, u32[]{:S(2)}, u32[]{:S(2)}) collective-permute-start(f32[1024,64]{0,1:T(8,128)S(1)} %get-tuple-element.157), channel_id=1, source_target_pairs={{4,0},{8,4},{12,8},{16,12},{20,16},{24,20},{28,24},{0,28},{5,1},{9... | collective-permute-start | bytes 786440 | tf_op jit(solution)/shard_map/ppermute | solution.py:20
  149.8 1.9 collective-permute-done.12
  152.3 0.6 slice_divide_fusion.1
  153.4 0.9 fusion.15.gram_ref
  154.3 8.4 %shard_map.50 = f32[64,64]{1,0:T(8,128)} custom-call(f32[64,64]{1,0:T(8,128)} %fusion.15.gram_ref), custom_call_target="tpu_custom_call" | custom-call | tf_op jit(solution)/shard_map/pallas_call | solution.py:174
  162.7 1.7 convolution_convert_fusion
  164.5 0.7 copy-done.8
  165.3 0.7 add.237
  166.1 8.3 %collective-permute-start.14 = (f32[1024,64]{0,1:T(8,128)}, f32[1024,64]{0,1:T(8,128)}, u32[]{:S(2)}, u32[]{:S(2)}) collective-permute-start(f32[1024,64]{0,1:T(8,128)} %add.237), channel_id=1, source_target_pairs={{8,0},{12,4},{16,8},{20,12},{24,16},{28,20},{0,24},{4,28},{9,1},{1... | collective-permute-start | bytes 786440 | tf_op jit(solution)/shard_map/ppermute | solution.py:20
  174.4 4.4 %conditional.9 = (f32[1024,64]{0,1:T(8,128)S(1)}, f32[1024,64]{0,1:T(8,128)S(1)}) conditional(s32[]{:T(128)} %convert_element_type.66, () %tuple.62, (bf16[1024,1024]{1,0:T(8,128)(2,1)}, bf16[1024,64]{0,1:T(8,128)(2,1)S(1)}, bf16[1024,64]{0,1:T(8,128)(2,1)S(1)}) %tuple.63), branch_computations={%region_23.24_spmd, %region_24.25_spmd} | conditional | flops 268435456 | bytes 4980752 | solution.py:110
  174.4 2.3 %fusion.49 = f32[1024,64]{0,1:T(8,128)S(1)} fusion(bf16[1024,1024]{1,0:T(8,128)(2,1)} %get-tuple-element.54, bf16[1024,64]{0,1:T(8,128)(2,1)S(1)} %get-tuple-element.133), kind=kOutput, calls=%fused_computation.133 | convolution fusion | flops 134217728 | bytes 2490368 | tf_op jit(solution)/shard_map/cond/branch_1_fun/dot_general | solution.py:62
  176.7 2.1 fusion.50
  178.8 1.2 collective-permute-start.13
  180.0 8.0 %collective-permute-done.13 = f32[1024,64]{0,1:T(8,128)S(1)} collective-permute-done((f32[1024,64]{0,1:T(8,128)S(1)}, f32[1024,64]{0,1:T(8,128)S(1)}, u32[]{:S(2)}, u32[]{:S(2)}) %collective-permute-start.13) | collective-permute-done | bytes 262176 | tf_op jit(solution)/shard_map/ppermute | solution.py:20
  187.9 1.7 fusion.43
  190.3 0.8 pad_maximum_fusion.13
  191.2 1.2 collective-permute-done.15
  192.4 2.0 collective-permute-start.16
  194.4 1.9 collective-permute-done.16
  196.4 3.8 %collective-permute-done.17 = f32[37,128]{1,0:T(8,128)S(1)} collective-permute-done((f32[37,128]{1,0:T(8,128)S(1)}, f32[37,128]{1,0:T(8,128)S(1)}, u32[]{:S(2)}, u32[]{:S(2)}) %collective-permute-start.17) | collective-permute-done | bytes 18976 | tf_op jit(solution)/shard_map/ppermute | solution.py:126
  200.4 3.7 %collective-permute-done.18 = f32[41,128]{1,0:T(8,128)S(1)} collective-permute-done((f32[41,128]{1,0:T(8,128)S(1)}, f32[41,128]{1,0:T(8,128)S(1)}, u32[]{:S(2)}, u32[]{:S(2)}) %collective-permute-start.18) | collective-permute-done | bytes 21024 | tf_op jit(solution)/shard_map/ppermute | solution.py:126
  204.5 4.7 %collective-permute-done.19 = f32[49,128]{1,0:T(8,128)S(1)} collective-permute-done((f32[49,128]{1,0:T(8,128)S(1)}, f32[49,128]{1,0:T(8,128)S(1)}, u32[]{:S(2)}, u32[]{:S(2)}) %collective-permute-start.19) | collective-permute-done | bytes 25120 | tf_op jit(solution)/shard_map/ppermute | solution.py:126
  209.7 0.6 slice_divide_fusion
  210.8 0.9 fusion.13.gram_ref
  211.7 8.4 %shard_map.51 = f32[64,64]{1,0:T(8,128)} custom-call(f32[64,64]{1,0:T(8,128)} %fusion.13.gram_ref), custom_call_target="tpu_custom_call" | custom-call | tf_op jit(solution)/shard_map/pallas_call | solution.py:174
  220.1 1.9 fusion.21
  (129 shorter events, 8.7 us)
Async XLA Ops:
  0.6 14.7 %copy-start = (bf16[1024,768]{1,0:T(8,128)(2,1)S(1)}, bf16[1024,768]{1,0:T(8,128)(2,1)}, u32[]{:S(2)}) copy-start(bf16[1024,768]{1,0:T(8,128)(2,1)} %param.15) | copy-start | bytes 4718596
  0.6 40.7 %collective-permute-start.2 = (bf16[1024,768]{1,0:T(8,128)(2,1)}, bf16[1024,768]{1,0:T(8,128)(2,1)}, u32[]{:S(2)}, u32[]{:S(2)}) collective-permute-start(bf16[1024,768]{1,0:T(8,128)(2,1)} %param.15), channel_id=1, source_target_pairs={{24,0},{28,4},{0,8},{4,12},{8,16},{12,20},{16,24},{20,28},{25,1},{... | collective-permute-start | bytes 4718600 | tf_op jit(solution)/shard_map/ppermute | solution.py:20
  3.7 68.9 %collective-permute-start = (bf16[1024,768]{1,0:T(8,128)(2,1)}, bf16[1024,768]{1,0:T(8,128)(2,1)}, u32[]{:S(2)}, u32[]{:S(2)}) collective-permute-start(bf16[1024,768]{1,0:T(8,128)(2,1)} %param.15), channel_id=1, source_target_pairs={{4,0},{8,4},{12,8},{16,12},{20,16},{24,20},{28,24},{0,28},{5,1},{9... | collective-permute-start | bytes 4718600 | tf_op jit(solution)/shard_map/ppermute | solution.py:20
  8.0 72.6 %collective-permute-start.3 = (bf16[1024,64]{1,0:T(8,128)(2,1)S(1)}, bf16[1024,64]{1,0:T(8,128)(2,1)S(1)}, u32[]{:S(2)}, u32[]{:S(2)}) collective-permute-start(bf16[1024,64]{1,0:T(8,128)(2,1)S(1)} %copy.17), channel_id=1, source_target_pairs={{24,0},{28,4},{0,8},{4,12},{8,16},{12,20},{16,24},{20,28},{25,1},{... | collective-permute-start | bytes 393224 | tf_op jit(solution)/shard_map/ppermute | solution.py:20
  8.1 74.5 %collective-permute-start.1 = (bf16[1024,64]{1,0:T(8,128)(2,1)S(1)}, bf16[1024,64]{1,0:T(8,128)(2,1)S(1)}, u32[]{:S(2)}, u32[]{:S(2)}) collective-permute-start(bf16[1024,64]{1,0:T(8,128)(2,1)S(1)} %copy.17), channel_id=1, source_target_pairs={{4,0},{8,4},{12,8},{16,12},{20,16},{24,20},{28,24},{0,28},{5,1},{9... | collective-permute-start | bytes 393224 | tf_op jit(solution)/shard_map/ppermute | solution.py:20
  15.7 64.9 %copy-start.2 = (bf16[1024,768]{1,0:T(8,128)(2,1)}, bf16[1024,768]{1,0:T(8,128)(2,1)S(1)}, u32[]{:S(2)}) copy-start(bf16[1024,768]{1,0:T(8,128)(2,1)S(1)} %fusion.3) | copy-start | bytes 4718596
  76.2 4.4 %copy-start.3 = (bf16[1024,768]{1,0:T(8,128)(2,1)}, bf16[1024,768]{1,0:T(8,128)(2,1)S(1)}, u32[]{:S(2)}) copy-start(bf16[1024,768]{1,0:T(8,128)(2,1)S(1)} %fusion.9) | copy-start | bytes 4718596
  76.2 4.4 %copy-start.1 = (bf16[1024,64]{0,1:T(8,128)(2,1)S(1)}, bf16[1024,64]{0,1:T(8,128)(2,1)}, u32[]{:S(2)}) copy-start(bf16[1024,64]{0,1:T(8,128)(2,1)} %param.16) | copy-start | bytes 393220
  82.3 0.7 copy-start.6
  84.7 0.7 copy-start.4
  86.5 32.0 %collective-permute-start.5 = (f32[520,128]{1,0:T(8,128)}, f32[520,128]{1,0:T(8,128)}, u32[]{:S(2)}, u32[]{:S(2)}) collective-permute-start(f32[520,128]{1,0:T(8,128)} %pad_maximum_fusion.1), channel_id=1, source_target_pairs={{8,0},{12,4},{16,8},{20,12},{24,16},{28,20},{0,24},{4,28},{9,1},{1... | collective-permute-start | bytes 798728 | tf_op jit(solution)/shard_map/ppermute | solution.py:20
  107.1 10.4 %copy-start.5 = (f32[1024,64]{0,1:T(8,128)S(1)}, f32[1024,64]{0,1:T(8,128)}, u32[]{:S(2)}) copy-start(f32[1024,64]{0,1:T(8,128)} %copy-done.4) | copy-start | bytes 786436
  116.8 0.7 copy-start.7
  117.9 9.3 %collective-permute-start.4 = (f32[520,128]{1,0:T(8,128)S(1)}, f32[520,128]{1,0:T(8,128)}, u32[]{:S(2)}, u32[]{:S(2)}) collective-permute-start(f32[520,128]{1,0:T(8,128)S(1)} %pad_maximum_fusion), channel_id=1, source_target_pairs={{28,0},{0,4},{4,8},{8,12},{12,16},{16,20},{20,24},{24,28},{29,1},{... | collective-permute-start | bytes 798728 | tf_op jit(solution)/shard_map/ppermute | solution.py:20
  119.6 10.1 %copy-start.9 = (f32[1024]{0:T(1024)S(1)}, f32[1024]{0:T(1024)}, u32[]{:S(2)}) copy-start(f32[1024]{0:T(1024)} %get-tuple-element.164) | copy-start | bytes 12292
  133.4 1.3 collective-permute-start.8
  134.7 3.8 %collective-permute-start.9 = (f32[35,128]{1,0:T(8,128)S(1)}, f32[35,128]{1,0:T(8,128)S(1)}, u32[]{:S(2)}, u32[]{:S(2)}) collective-permute-start(f32[35,128]{1,0:T(8,128)S(1)} %pad_maximum_fusion.7), channel_id=1, source_target_pairs={{0,2},{1,3},{2,0},{3,1},{4,6},{5,7},{6,4},{7,5},{8,10},{9,11},{10,... | collective-permute-start | bytes 53768 | tf_op jit(solution)/shard_map/ppermute | solution.py:126
  138.6 3.8 %collective-permute-start.10 = (f32[37,128]{1,0:T(8,128)S(1)}, f32[37,128]{1,0:T(8,128)S(1)}, u32[]{:S(2)}, u32[]{:S(2)}) collective-permute-start(f32[37,128]{1,0:T(8,128)S(1)} %pad_maximum_fusion.8), channel_id=1, source_target_pairs={{0,4},{4,0},{8,12},{12,8},{16,20},{20,16},{24,28},{28,24},{1,5},{5... | collective-permute-start | bytes 56840 | tf_op jit(solution)/shard_map/ppermute | solution.py:126
  142.5 3.9 %collective-permute-start.11 = (f32[41,128]{1,0:T(8,128)S(1)}, f32[41,128]{1,0:T(8,128)S(1)}, u32[]{:S(2)}, u32[]{:S(2)}) collective-permute-start(f32[41,128]{1,0:T(8,128)S(1)} %pad_maximum_fusion.4), channel_id=1, source_target_pairs={{0,8},{4,12},{8,0},{12,4},{16,24},{20,28},{24,16},{28,20},{1,9},{5... | collective-permute-start | bytes 62984 | tf_op jit(solution)/shard_map/ppermute | solution.py:126
  146.4 5.3 %collective-permute-start.12 = (f32[49,128]{1,0:T(8,128)S(1)}, f32[49,128]{1,0:T(8,128)S(1)}, u32[]{:S(2)}, u32[]{:S(2)}) collective-permute-start(f32[49,128]{1,0:T(8,128)S(1)} %pad_maximum_fusion.2), channel_id=1, source_target_pairs={{0,16},{4,20},{8,24},{12,28},{16,0},{20,4},{24,8},{28,12},{1,17},{... | collective-permute-start | bytes 75272 | tf_op jit(solution)/shard_map/ppermute | solution.py:126
  146.5 16.2 %collective-permute-start.7 = (f32[1024,64]{0,1:T(8,128)S(1)}, f32[1024,64]{0,1:T(8,128)S(1)}, u32[]{:S(2)}, u32[]{:S(2)}) collective-permute-start(f32[1024,64]{0,1:T(8,128)S(1)} %get-tuple-element.157), channel_id=1, source_target_pairs={{24,0},{28,4},{0,8},{4,12},{8,16},{12,20},{16,24},{20,28},{25,1},{... | collective-permute-start | bytes 786440 | tf_op jit(solution)/shard_map/ppermute | solution.py:20
  146.8 15.9 %collective-permute-start.6 = (f32[1024,64]{0,1:T(8,128)S(1)}, f32[1024,64]{0,1:T(8,128)S(1)}, u32[]{:S(2)}, u32[]{:S(2)}) collective-permute-start(f32[1024,64]{0,1:T(8,128)S(1)} %get-tuple-element.157), channel_id=1, source_target_pairs={{4,0},{8,4},{12,8},{16,12},{20,16},{24,20},{28,24},{0,28},{5,1},{9... | collective-permute-start | bytes 786440 | tf_op jit(solution)/shard_map/ppermute | solution.py:20
  164.4 0.8 copy-start.8
  166.1 13.9 %collective-permute-start.14 = (f32[1024,64]{0,1:T(8,128)}, f32[1024,64]{0,1:T(8,128)}, u32[]{:S(2)}, u32[]{:S(2)}) collective-permute-start(f32[1024,64]{0,1:T(8,128)} %add.237), channel_id=1, source_target_pairs={{8,0},{12,4},{16,8},{20,12},{24,16},{28,20},{0,24},{4,28},{9,1},{1... | collective-permute-start | bytes 786440 | tf_op jit(solution)/shard_map/ppermute | solution.py:20
  178.8 9.1 %collective-permute-start.13 = (f32[1024,64]{0,1:T(8,128)S(1)}, f32[1024,64]{0,1:T(8,128)S(1)}, u32[]{:S(2)}, u32[]{:S(2)}) collective-permute-start(f32[1024,64]{0,1:T(8,128)S(1)} %add.235), channel_id=1, source_target_pairs={{28,0},{0,4},{4,8},{8,12},{12,16},{16,20},{20,24},{24,28},{29,1},{... | collective-permute-start | bytes 786440 | tf_op jit(solution)/shard_map/ppermute | solution.py:20
  191.2 1.2 collective-permute-start.15
  192.4 3.8 %collective-permute-start.16 = (f32[35,128]{1,0:T(8,128)S(1)}, f32[35,128]{1,0:T(8,128)S(1)}, u32[]{:S(2)}, u32[]{:S(2)}) collective-permute-start(f32[35,128]{1,0:T(8,128)S(1)} %pad_maximum_fusion.10), channel_id=1, source_target_pairs={{0,2},{1,3},{2,0},{3,1},{4,6},{5,7},{6,4},{7,5},{8,10},{9,11},{10,... | collective-permute-start | bytes 53768 | tf_op jit(solution)/shard_map/ppermute | solution.py:126
  196.3 3.8 %collective-permute-start.17 = (f32[37,128]{1,0:T(8,128)S(1)}, f32[37,128]{1,0:T(8,128)S(1)}, u32[]{:S(2)}, u32[]{:S(2)}) collective-permute-start(f32[37,128]{1,0:T(8,128)S(1)} %pad_maximum_fusion.11), channel_id=1, source_target_pairs={{0,4},{4,0},{8,12},{12,8},{16,20},{20,16},{24,28},{28,24},{1,5},{5... | collective-permute-start | bytes 56840 | tf_op jit(solution)/shard_map/ppermute | solution.py:126
  200.2 3.9 %collective-permute-start.18 = (f32[41,128]{1,0:T(8,128)S(1)}, f32[41,128]{1,0:T(8,128)S(1)}, u32[]{:S(2)}, u32[]{:S(2)}) collective-permute-start(f32[41,128]{1,0:T(8,128)S(1)} %pad_maximum_fusion.5), channel_id=1, source_target_pairs={{0,8},{4,12},{8,0},{12,4},{16,24},{20,28},{24,16},{28,20},{1,9},{5... | collective-permute-start | bytes 62984 | tf_op jit(solution)/shard_map/ppermute | solution.py:126
  204.2 5.0 %collective-permute-start.19 = (f32[49,128]{1,0:T(8,128)S(1)}, f32[49,128]{1,0:T(8,128)S(1)}, u32[]{:S(2)}, u32[]{:S(2)}) collective-permute-start(f32[49,128]{1,0:T(8,128)S(1)} %pad_maximum_fusion.3), channel_id=1, source_target_pairs={{0,16},{4,20},{8,24},{12,28},{16,0},{20,4},{24,8},{28,12},{1,17},{... | collective-permute-start | bytes 75272 | tf_op jit(solution)/shard_map/ppermute | solution.py:126

commit v9 on v8

--- a/solution.py
+++ b/solution.py
@@ -234,7 +234,7 @@
     units = {0: unit_block}
     weights = {0: start}
     for offset in fetch_offsets:
-        units[offset] = normalize_rows(shifted(embeddings, "wide", -offset))
+        units[offset] = shifted(unit_block, "wide", -offset)
         weights[offset] = shifted(start, "wide", -offset)
 
     self_mask = lax.broadcasted_iota(

time: 223 us -> 230 us (1.031)
  matrix products: 25.5 us -> 42.2 us
  waiting for transfers between devices: 96.9 us -> 113 us
  starting transfers between devices: 46.3 us -> 31.1 us
  other arithmetic: 21.2 us -> 13.4 us
  local copies, waits for them, and re-layouts: 11.9 us -> 9.13 us
    ppermute x10, waiting for transfers between devices: 68.9 us -> 81.2 us  [shifted(): return lax.ppermute(block, axis, route)]
    ppermute x10, starting transfers between devices: 41.9 us -> 30.2 us  [shifted(): return lax.ppermute(block, axis, route)]
    dot_general x2 -> x3, matrix products: 7.79 us -> 14.9 us  [scores_tile(): lax.dot_general(leftside_block, right_block, (((1,), (1,)), ((), ())), pr...]
    dot_general x4 -> x6, matrix products: 6.82 us -> 12.2 us  [row_product(): return jnp.dot(affinity, weights, preferred_element_type=jnp.float32)]
    convert_element_type x3 -> x1, other arithmetic: 5.9 us -> 1.57 us  [normalize_rows(): (values_wide * scaling / math.sqrt(values_wide.shape[-1])).astype(jnp.bfl...]
    dot_general x2 -> x4, matrix products: 4.14 us -> 8.32 us  [col_product(): lax.dot_general(affinity, weights, (((0,), (0,)), ((), ())), preferred_el...]
    ppermute x10, starting transfers between devices: 4.44 us -> 0.9 us  [butterfly(): other = lax.ppermute(block, axis, route)]
    reduce_sum x3 -> x1, other arithmetic: 5.35 us -> 1.91 us  [normalize_rows(): jnp.mean(values_wide * values_wide, axis=-1, keepdims=True) + 1e-06]
  transfers between devices with their start and end apart: 20 -> 20, of which waited for: 16 -> 15; matrix products, arithmetic and copies ran while one was open for 17% -> 12% of each run, Pallas kernels for 4% -> 4%
where the time goes in v9:
time: 230 us; the launch traced here: 229 us
  waiting for transfers between devices  113 us (49%)
  matrix products  42.2 us (18%)
  starting transfers between devices  31.1 us (14%)
  Pallas kernels  16.8 us (7%)
  other arithmetic  13.4 us (6%)
  local copies, waits for them, and re-layouts  9.13 us (4%)
  between operations  3.27 us (1%)
    ppermute x10, waiting for transfers between devices, shifted(): return lax.ppermute(block, axis, route)  81.2 us
    ppermute x10, waiting for transfers between devices, butterfly(): other = lax.ppermute(block, axis, route)  31.4 us
    ppermute x10, starting transfers between devices, shifted(): return lax.ppermute(block, axis, route)  30.2 us
    pallas_call x2, Pallas kernels, factor_inverse(): pl.pallas_call(factor_kernel, out_shape=jax.ShapeDtypeStruct(gram_matrix....  16.8 us
    dot_general x3, matrix products, scores_tile(): lax.dot_general(leftside_block, right_block, (((1,), (1,)), ((), ())), pr...  14.9 us
    dot_general x6, matrix products, row_product(): return jnp.dot(affinity, weights, preferred_element_type=jnp.float32)  12.2 us
    dot_general x4, matrix products, col_product(): lax.dot_general(affinity, weights, (((0,), (0,)), ((), ())), preferred_el...  8.32 us
    dot_general x8, matrix products, hdot(): jnp.dot(left, right, precision=lax.Precision.HIGHEST, preferred_element_t...  6.78 us
  transfers between devices with their start and end apart: 20, of which 15 were waited for; matrix products, arithmetic and copies ran while one was open for 12% of the time, Pallas kernels for 4%

profile of v9, /device:TPU:0, one launch (start us, length us, event | category | flops | bytes accessed | tf_op | source)
XLA Modules:
  0.0 228.6 jit_solution(110986331725442660)
XLA Ops:
  0.6 1.9 fusion.1
  2.6 1.6 fusion.3
  4.2 3.0 %collective-permute-start.2 = (bf16[1024,768]{1,0:T(8,128)(2,1)}, bf16[1024,768]{1,0:T(8,128)(2,1)}, u32[]{:S(2)}, u32[]{:S(2)}) collective-permute-start(bf16[1024,768]{1,0:T(8,128)(2,1)} %fusion.3), channel_id=1, source_target_pairs={{24,0},{28,4},{0,8},{4,12},{8,16},{12,20},{16,24},{20,28},{25,1},{... | collective-permute-start | bytes 4718600 | tf_op jit(solution)/shard_map/ppermute | solution.py:20
  7.2 3.2 %collective-permute-start = (bf16[1024,768]{1,0:T(8,128)(2,1)}, bf16[1024,768]{1,0:T(8,128)(2,1)}, u32[]{:S(2)}, u32[]{:S(2)}) collective-permute-start(bf16[1024,768]{1,0:T(8,128)(2,1)} %fusion.3), channel_id=1, source_target_pairs={{4,0},{8,4},{12,8},{16,12},{20,16},{24,20},{28,24},{0,28},{5,1},{9... | collective-permute-start | bytes 4718600 | tf_op jit(solution)/shard_map/ppermute | solution.py:20
  10.6 2.1 collective-permute-start.1
  12.7 4.5 %convert_reduce_fusion.6 = (f32[1024]{0:T(1024)}, bf16[1024,1024]{0,1:T(8,128)(2,1)S(1)}) fusion(bf16[1024,768]{1,0:T(8,128)(2,1)} %fusion.3), kind=kOutput, calls=%fused_computation.9 | convolution fusion | flops 1616903168 | bytes 3674112 | tf_op jit(solution)/shard_map/dot_general | solution.py:55
  17.2 0.8 fusion.34
  19.8 64.2 %collective-permute-done.3 = bf16[1024,64]{1,0:T(8,128)(2,1)S(1)} collective-permute-done((bf16[1024,64]{1,0:T(8,128)(2,1)S(1)}, bf16[1024,64]{1,0:T(8,128)(2,1)S(1)}, u32[]{:S(2)}, u32[]{:S(2)}) %collective-permute-start.3) | collective-permute-done | bytes 131104 | tf_op jit(solution)/shard_map/ppermute | solution.py:20
  84.0 1.6 conditional.7
  84.0 1.6 broadcast.92
  86.4 9.7 %conditional.8 = (bf16[1024,1024]{1,0:T(8,128)(2,1)}, f32[1024,64]{0,1:T(8,128)S(1)}, f32[1024]{0:T(1024)S(1)}, f32[1024,64]{0,1:T(8,128)S(1)}, f32[1024]{0:T(1024)S(1)}) conditional(s32[]{:T(128)} %convert_element_type.56, () %tuple.60, (bf16[1024,768]{1,0:T(8,128)(2,1)}, bf16[1024,768]{1,0:T(8,128)(2,1)}, bf16[1024,64]{1,0:T(8,128)(2,1)S(1)}, ...), branch_computations={%region_12.13_spmd, %region_13.16_spmd} | conditional | flops 1884289024 | bytes 10231848 | solution.py:96
  86.4 5.2 %convert_reduce_fusion.4 = (f32[1024]{0:T(1024)S(1)}, f32[1024]{0:T(1024)S(1)}, bf16[1024,1024]{1,0:T(8,128)(2,1)}) fusion(bf16[1024,768]{1,0:T(8,128)(2,1)} %get-tuple-element.50, bf16[1024,768]{1,0:T(8,128)(2,1)} %get-tuple-element.51), kind=kOutput, calls=%fused_computation.6 | convolution fusion | flops 1615853568 | bytes 5251072 | tf_op jit(solution)/shard_map/cond/branch_1_fun/dot_general | solution.py:55
  91.6 2.3 %fusion.53 = f32[1024,64]{0,1:T(8,128)S(1)} fusion(bf16[1024,1024]{1,0:T(8,128)(2,1)} %get-tuple-element.185, bf16[1024,64]{1,0:T(8,128)(2,1)S(1)} %get-tuple-element.52), kind=kOutput, calls=%fused_computation.131 | convolution fusion | flops 134217728 | bytes 2490368 | tf_op jit(solution)/shard_map/cond/branch_1_fun/dot_general | solution.py:62
  93.9 2.1 fusion.54
  96.1 0.7 copy-done.2
  97.2 14.5 %collective-permute-start.5 = (f32[520,128]{1,0:T(8,128)S(1)}, f32[520,128]{1,0:T(8,128)}, u32[]{:S(2)}, u32[]{:S(2)}) collective-permute-start(f32[520,128]{1,0:T(8,128)S(1)} %pad_maximum_fusion.1), channel_id=1, source_target_pairs={{8,0},{12,4},{16,8},{20,12},{24,16},{28,20},{0,24},{4,28},{9,1},{1... | collective-permute-start | bytes 798728 | tf_op jit(solution)/shard_map/ppermute | solution.py:20
  111.7 10.4 %conditional.6 = (bf16[1024,1024]{1,0:T(8,128)(2,1)}, f32[1024,64]{0,1:T(8,128)}, f32[1024]{0:T(1024)S(1)}, f32[1024,64]{0,1:T(8,128)S(1)}, f32[1024]{0:T(1024)S(1)}) conditional(s32[]{:T(128)} %convert_element_type.54, () %tuple.56, (bf16[1024,768]{1,0:T(8,128)(2,1)}, bf16[1024,768]{1,0:T(8,128)(2,1)}, bf16[1024,64]{1,0:T(8,128)(2,1)S(1)}, ...), branch_computations={%region_2.3_spmd, %region_3.0_spmd} | conditional | flops 1884289024 | bytes 10231848 | solution.py:96
  111.7 5.3 %convert_reduce_fusion = (f32[1024]{0:T(1024)S(1)}, f32[1024]{0:T(1024)S(1)}, bf16[1024,1024]{1,0:T(8,128)(2,1)}) fusion(bf16[1024,768]{1,0:T(8,128)(2,1)} %get-tuple-element.42, bf16[1024,768]{1,0:T(8,128)(2,1)} %get-tuple-element.43), kind=kOutput, calls=%fused_computation | convolution fusion | flops 1615853568 | bytes 5251072 | tf_op jit(solution)/shard_map/cond/branch_1_fun/dot_general | solution.py:55
  117.0 3.1 %fusion.49 = f32[1024,64]{0,1:T(8,128)} fusion(bf16[1024,1024]{1,0:T(8,128)(2,1)} %get-tuple-element.195, bf16[1024,64]{1,0:T(8,128)(2,1)S(1)} %get-tuple-element.44), kind=kOutput, calls=%fused_computation.127 | convolution fusion | flops 134217728 | bytes 2490368 | tf_op jit(solution)/shard_map/cond/branch_1_fun/dot_general | solution.py:62
  120.0 2.1 fusion.50
  122.1 0.6 copy-done.6
  123.1 0.7 add_bitcast_fusion.1
  123.8 0.7 pad_maximum_fusion
  125.0 1.0 slice.164
  126.3 7.6 %collective-permute-done.4 = f32[520,128]{1,0:T(8,128)} collective-permute-done((f32[520,128]{1,0:T(8,128)}, f32[520,128]{1,0:T(8,128)}, u32[]{:S(2)}, u32[]{:S(2)}) %collective-permute-start.4) | collective-permute-done | bytes 266272 | tf_op jit(solution)/shard_map/ppermute | solution.py:20
  133.9 1.0 slice.163
  135.2 1.2 fusion.40
  136.4 1.3 broadcast_multiply_fusion
  138.6 0.7 reduce_sum.143
  139.3 0.8 pad_maximum_fusion.12
  140.2 1.2 collective-permute-done.8
  141.5 3.7 %collective-permute-done.9 = f32[35,128]{1,0:T(8,128)S(1)} collective-permute-done((f32[35,128]{1,0:T(8,128)S(1)}, f32[35,128]{1,0:T(8,128)S(1)}, u32[]{:S(2)}, u32[]{:S(2)}) %collective-permute-start.9) | collective-permute-done | bytes 17952 | tf_op jit(solution)/shard_map/ppermute | solution.py:126
  145.4 3.8 %collective-permute-done.10 = f32[37,128]{1,0:T(8,128)S(1)} collective-permute-done((f32[37,128]{1,0:T(8,128)S(1)}, f32[37,128]{1,0:T(8,128)S(1)}, u32[]{:S(2)}, u32[]{:S(2)}) %collective-permute-start.10) | collective-permute-done | bytes 18976 | tf_op jit(solution)/shard_map/ppermute | solution.py:126
  149.3 3.8 %collective-permute-done.11 = f32[41,128]{1,0:T(8,128)S(1)} collective-permute-done((f32[41,128]{1,0:T(8,128)S(1)}, f32[41,128]{1,0:T(8,128)S(1)}, u32[]{:S(2)}, u32[]{:S(2)}) %collective-permute-start.11) | collective-permute-done | bytes 21024 | tf_op jit(solution)/shard_map/ppermute | solution.py:126
  153.5 3.0 %collective-permute-start.6 = (f32[1024,64]{0,1:T(8,128)S(1)}, f32[1024,64]{0,1:T(8,128)S(1)}, u32[]{:S(2)}, u32[]{:S(2)}) collective-permute-start(f32[1024,64]{0,1:T(8,128)S(1)} %get-tuple-element.157), channel_id=1, source_target_pairs={{4,0},{8,4},{12,8},{16,12},{20,16},{24,20},{28,24},{0,28},{5,1},{9... | collective-permute-start | bytes 786440 | tf_op jit(solution)/shard_map/ppermute | solution.py:20
  156.5 1.9 collective-permute-done.12
  158.5 0.6 slice.177
  159.0 0.6 slice_divide_fusion.1
  160.1 0.9 fusion.9.gram_ref
  161.0 8.4 %shard_map.50 = f32[64,64]{1,0:T(8,128)} custom-call(f32[64,64]{1,0:T(8,128)} %fusion.9.gram_ref), custom_call_target="tpu_custom_call" | custom-call | tf_op jit(solution)/shard_map/pallas_call | solution.py:174
  169.4 1.7 convolution_convert_fusion
  171.2 0.7 copy-done.5
  172.0 4.4 %conditional.11 = (f32[1024,64]{0,1:T(8,128)S(1)}, f32[1024,64]{0,1:T(8,128)S(1)}) conditional(s32[]{:T(128)} %convert_element_type.56, () %tuple.66, (bf16[1024,1024]{1,0:T(8,128)(2,1)}, bf16[1024,64]{0,1:T(8,128)(2,1)S(1)}, bf16[1024,64]{0,1:T(8,128)(2,1)S(1)}) %tuple.67), branch_computations={%region_25.26_spmd, %region_26.27_spmd} | conditional | flops 268435456 | bytes 4980752 | solution.py:110
  172.0 2.3 %fusion.47 = f32[1024,64]{0,1:T(8,128)S(1)} fusion(bf16[1024,1024]{1,0:T(8,128)(2,1)} %get-tuple-element.60, bf16[1024,64]{0,1:T(8,128)(2,1)S(1)} %get-tuple-element.139), kind=kOutput, calls=%fused_computation.125 | convolution fusion | flops 134217728 | bytes 2490368 | tf_op jit(solution)/shard_map/cond/branch_1_fun/dot_general | solution.py:62
  174.3 2.1 fusion.48
  176.4 0.7 add.223
  177.2 3.9 %collective-permute-start.14 = (f32[1024,64]{0,1:T(8,128)}, f32[1024,64]{0,1:T(8,128)}, u32[]{:S(2)}, u32[]{:S(2)}) collective-permute-start(f32[1024,64]{0,1:T(8,128)} %add.223), channel_id=1, source_target_pairs={{8,0},{12,4},{16,8},{20,12},{24,16},{28,20},{0,24},{4,28},{9,1},{1... | collective-permute-start | bytes 786440 | tf_op jit(solution)/shard_map/ppermute | solution.py:20
  181.1 4.4 %conditional.9 = (f32[1024,64]{0,1:T(8,128)S(1)}, f32[1024,64]{0,1:T(8,128)S(1)}) conditional(s32[]{:T(128)} %convert_element_type.54, () %tuple.62, (bf16[1024,1024]{1,0:T(8,128)(2,1)}, bf16[1024,64]{0,1:T(8,128)(2,1)S(1)}, bf16[1024,64]{0,1:T(8,128)(2,1)S(1)}) %tuple.63), branch_computations={%region_21.22_spmd, %region_22.23_spmd} | conditional | flops 268435456 | bytes 4980752 | solution.py:110
  181.1 2.3 %fusion.43 = f32[1024,64]{0,1:T(8,128)S(1)} fusion(bf16[1024,1024]{1,0:T(8,128)(2,1)} %get-tuple-element.54, bf16[1024,64]{0,1:T(8,128)(2,1)S(1)} %get-tuple-element.133), kind=kOutput, calls=%fused_computation.121 | convolution fusion | flops 134217728 | bytes 2490368 | tf_op jit(solution)/shard_map/cond/branch_1_fun/dot_general | solution.py:62
  183.4 2.1 fusion.44
  185.6 0.7 collective-permute-done.14
  186.3 8.3 %collective-permute-done.13 = f32[1024,64]{0,1:T(8,128)S(1)} collective-permute-done((f32[1024,64]{0,1:T(8,128)S(1)}, f32[1024,64]{0,1:T(8,128)S(1)}, u32[]{:S(2)}, u32[]{:S(2)}) %collective-permute-start.13) | collective-permute-done | bytes 262176 | tf_op jit(solution)/shard_map/ppermute | solution.py:20
  194.7 1.7 fusion.37
  197.0 0.8 pad_maximum_fusion.13
  198.0 1.2 collective-permute-done.15
  199.3 3.8 %collective-permute-done.16 = f32[35,128]{1,0:T(8,128)S(1)} collective-permute-done((f32[35,128]{1,0:T(8,128)S(1)}, f32[35,128]{1,0:T(8,128)S(1)}, u32[]{:S(2)}, u32[]{:S(2)}) %collective-permute-start.16) | collective-permute-done | bytes 17952 | tf_op jit(solution)/shard_map/ppermute | solution.py:126
  203.1 3.8 %collective-permute-done.17 = f32[37,128]{1,0:T(8,128)S(1)} collective-permute-done((f32[37,128]{1,0:T(8,128)S(1)}, f32[37,128]{1,0:T(8,128)S(1)}, u32[]{:S(2)}, u32[]{:S(2)}) %collective-permute-start.17) | collective-permute-done | bytes 18976 | tf_op jit(solution)/shard_map/ppermute | solution.py:126
  207.0 3.8 %collective-permute-done.18 = f32[41,128]{1,0:T(8,128)S(1)} collective-permute-done((f32[41,128]{1,0:T(8,128)S(1)}, f32[41,128]{1,0:T(8,128)S(1)}, u32[]{:S(2)}, u32[]{:S(2)}) %collective-permute-start.18) | collective-permute-done | bytes 21024 | tf_op jit(solution)/shard_map/ppermute | solution.py:126
  211.2 4.5 %collective-permute-done.19 = f32[49,128]{1,0:T(8,128)S(1)} collective-permute-done((f32[49,128]{1,0:T(8,128)S(1)}, f32[49,128]{1,0:T(8,128)S(1)}, u32[]{:S(2)}, u32[]{:S(2)}) %collective-permute-start.19) | collective-permute-done | bytes 25120 | tf_op jit(solution)/shard_map/ppermute | solution.py:126
  215.8 0.6 slice.195
  216.3 0.6 slice_divide_fusion
  217.4 0.9 fusion.7.gram_ref
  218.3 8.4 %shard_map.51 = f32[64,64]{1,0:T(8,128)} custom-call(f32[64,64]{1,0:T(8,128)} %fusion.7.gram_ref), custom_call_target="tpu_custom_call" | custom-call | tf_op jit(solution)/shard_map/pallas_call | solution.py:174
  226.7 1.9 fusion.15
  (119 shorter events, 7.1 us)
Async XLA Ops:
  0.6 1.9 copy-start
  0.6 9.7 %copy-start.1 = (bf16[1024,64]{0,1:T(8,128)(2,1)S(1)}, bf16[1024,64]{0,1:T(8,128)(2,1)}, u32[]{:S(2)}) copy-start(bf16[1024,64]{0,1:T(8,128)(2,1)} %param.16) | copy-start | bytes 393220
  4.2 79.9 %collective-permute-start.2 = (bf16[1024,768]{1,0:T(8,128)(2,1)}, bf16[1024,768]{1,0:T(8,128)(2,1)}, u32[]{:S(2)}, u32[]{:S(2)}) collective-permute-start(bf16[1024,768]{1,0:T(8,128)(2,1)} %fusion.3), channel_id=1, source_target_pairs={{24,0},{28,4},{0,8},{4,12},{8,16},{12,20},{16,24},{20,28},{25,1},{... | collective-permute-start | bytes 4718600 | tf_op jit(solution)/shard_map/ppermute | solution.py:20
  7.2 78.9 %collective-permute-start = (bf16[1024,768]{1,0:T(8,128)(2,1)}, bf16[1024,768]{1,0:T(8,128)(2,1)}, u32[]{:S(2)}, u32[]{:S(2)}) collective-permute-start(bf16[1024,768]{1,0:T(8,128)(2,1)} %fusion.3), channel_id=1, source_target_pairs={{4,0},{8,4},{12,8},{16,12},{20,16},{24,20},{28,24},{0,28},{5,1},{9... | collective-permute-start | bytes 4718600 | tf_op jit(solution)/shard_map/ppermute | solution.py:20
  10.6 6.6 %copy-start.7 = (s32[32,3]{0,1:T(4,128)S(1)}, s32[32,3]{0,1:T(4,128)}, u32[]{:S(2)}) copy-start(s32[32,3]{0,1:T(4,128)} %param.17) | copy-start | bytes 1156
  10.6 73.5 %collective-permute-start.3 = (bf16[1024,64]{1,0:T(8,128)(2,1)S(1)}, bf16[1024,64]{1,0:T(8,128)(2,1)S(1)}, u32[]{:S(2)}, u32[]{:S(2)}) collective-permute-start(bf16[1024,64]{1,0:T(8,128)(2,1)S(1)} %copy.17), channel_id=1, source_target_pairs={{24,0},{28,4},{0,8},{4,12},{8,16},{12,20},{16,24},{20,28},{25,1},{... | collective-permute-start | bytes 393224 | tf_op jit(solution)/shard_map/ppermute | solution.py:20
  10.6 75.4 %collective-permute-start.1 = (bf16[1024,64]{1,0:T(8,128)(2,1)S(1)}, bf16[1024,64]{1,0:T(8,128)(2,1)S(1)}, u32[]{:S(2)}, u32[]{:S(2)}) collective-permute-start(bf16[1024,64]{1,0:T(8,128)(2,1)S(1)} %copy.17), channel_id=1, source_target_pairs={{4,0},{8,4},{12,8},{16,12},{20,16},{24,20},{28,24},{0,28},{5,1},{9... | collective-permute-start | bytes 393224 | tf_op jit(solution)/shard_map/ppermute | solution.py:20
  85.7 0.7 copy-start.4
  96.1 0.7 copy-start.2
  97.2 27.8 %collective-permute-start.5 = (f32[520,128]{1,0:T(8,128)S(1)}, f32[520,128]{1,0:T(8,128)}, u32[]{:S(2)}, u32[]{:S(2)}) collective-permute-start(f32[520,128]{1,0:T(8,128)S(1)} %pad_maximum_fusion.1), channel_id=1, source_target_pairs={{8,0},{12,4},{16,8},{20,12},{24,16},{28,20},{0,24},{4,28},{9,1},{1... | collective-permute-start | bytes 798728 | tf_op jit(solution)/shard_map/ppermute | solution.py:20
  111.7 11.0 %copy-start.3 = (f32[1024,64]{0,1:T(8,128)S(1)}, f32[1024,64]{0,1:T(8,128)}, u32[]{:S(2)}) copy-start(f32[1024,64]{0,1:T(8,128)} %copy-done.2) | copy-start | bytes 786436
  122.1 0.6 copy-start.6
  124.5 9.4 %collective-permute-start.4 = (f32[520,128]{1,0:T(8,128)}, f32[520,128]{1,0:T(8,128)}, u32[]{:S(2)}, u32[]{:S(2)}) collective-permute-start(f32[520,128]{1,0:T(8,128)} %pad_maximum_fusion), channel_id=1, source_target_pairs={{28,0},{0,4},{4,8},{8,12},{12,16},{16,20},{20,24},{24,28},{29,1},{... | collective-permute-start | bytes 798728 | tf_op jit(solution)/shard_map/ppermute | solution.py:20
  126.1 10.3 %copy-start.8 = (f32[1024]{0:T(1024)S(1)}, f32[1024]{0:T(1024)}, u32[]{:S(2)}) copy-start(f32[1024]{0:T(1024)} %get-tuple-element.164) | copy-start | bytes 12292
  140.1 1.3 collective-permute-start.8
  141.4 3.8 %collective-permute-start.9 = (f32[35,128]{1,0:T(8,128)S(1)}, f32[35,128]{1,0:T(8,128)S(1)}, u32[]{:S(2)}, u32[]{:S(2)}) collective-permute-start(f32[35,128]{1,0:T(8,128)S(1)} %pad_maximum_fusion.7), channel_id=1, source_target_pairs={{0,2},{1,3},{2,0},{3,1},{4,6},{5,7},{6,4},{7,5},{8,10},{9,11},{10,... | collective-permute-start | bytes 53768 | tf_op jit(solution)/shard_map/ppermute | solution.py:126
  145.3 3.8 %collective-permute-start.10 = (f32[37,128]{1,0:T(8,128)S(1)}, f32[37,128]{1,0:T(8,128)S(1)}, u32[]{:S(2)}, u32[]{:S(2)}) collective-permute-start(f32[37,128]{1,0:T(8,128)S(1)} %pad_maximum_fusion.8), channel_id=1, source_target_pairs={{0,4},{4,0},{8,12},{12,8},{16,20},{20,16},{24,28},{28,24},{1,5},{5... | collective-permute-start | bytes 56840 | tf_op jit(solution)/shard_map/ppermute | solution.py:126
  149.2 3.9 %collective-permute-start.11 = (f32[41,128]{1,0:T(8,128)S(1)}, f32[41,128]{1,0:T(8,128)S(1)}, u32[]{:S(2)}, u32[]{:S(2)}) collective-permute-start(f32[41,128]{1,0:T(8,128)S(1)} %pad_maximum_fusion.4), channel_id=1, source_target_pairs={{0,8},{4,12},{8,0},{12,4},{16,24},{20,28},{24,16},{28,20},{1,9},{5... | collective-permute-start | bytes 62984 | tf_op jit(solution)/shard_map/ppermute | solution.py:126
  153.1 5.3 %collective-permute-start.12 = (f32[49,128]{1,0:T(8,128)S(1)}, f32[49,128]{1,0:T(8,128)S(1)}, u32[]{:S(2)}, u32[]{:S(2)}) collective-permute-start(f32[49,128]{1,0:T(8,128)S(1)} %pad_maximum_fusion.2), channel_id=1, source_target_pairs={{0,16},{4,20},{8,24},{12,28},{16,0},{20,4},{24,8},{28,12},{1,17},{... | collective-permute-start | bytes 75272 | tf_op jit(solution)/shard_map/ppermute | solution.py:126
  153.2 16.2 %collective-permute-start.7 = (f32[1024,64]{0,1:T(8,128)S(1)}, f32[1024,64]{0,1:T(8,128)S(1)}, u32[]{:S(2)}, u32[]{:S(2)}) collective-permute-start(f32[1024,64]{0,1:T(8,128)S(1)} %get-tuple-element.157), channel_id=1, source_target_pairs={{24,0},{28,4},{0,8},{4,12},{8,16},{12,20},{16,24},{20,28},{25,1},{... | collective-permute-start | bytes 786440 | tf_op jit(solution)/shard_map/ppermute | solution.py:20
  153.5 15.9 %collective-permute-start.6 = (f32[1024,64]{0,1:T(8,128)S(1)}, f32[1024,64]{0,1:T(8,128)S(1)}, u32[]{:S(2)}, u32[]{:S(2)}) collective-permute-start(f32[1024,64]{0,1:T(8,128)S(1)} %get-tuple-element.157), channel_id=1, source_target_pairs={{4,0},{8,4},{12,8},{16,12},{20,16},{24,20},{28,24},{0,28},{5,1},{9... | collective-permute-start | bytes 786440 | tf_op jit(solution)/shard_map/ppermute | solution.py:20
  171.1 0.8 copy-start.5
  177.2 9.2 %collective-permute-start.14 = (f32[1024,64]{0,1:T(8,128)}, f32[1024,64]{0,1:T(8,128)}, u32[]{:S(2)}, u32[]{:S(2)}) collective-permute-start(f32[1024,64]{0,1:T(8,128)} %add.223), channel_id=1, source_target_pairs={{8,0},{12,4},{16,8},{20,12},{24,16},{28,20},{0,24},{4,28},{9,1},{1... | collective-permute-start | bytes 786440 | tf_op jit(solution)/shard_map/ppermute | solution.py:20
  185.6 9.1 %collective-permute-start.13 = (f32[1024,64]{0,1:T(8,128)S(1)}, f32[1024,64]{0,1:T(8,128)S(1)}, u32[]{:S(2)}, u32[]{:S(2)}) collective-permute-start(f32[1024,64]{0,1:T(8,128)S(1)} %add.221), channel_id=1, source_target_pairs={{28,0},{0,4},{4,8},{8,12},{12,16},{16,20},{20,24},{24,28},{29,1},{... | collective-permute-start | bytes 786440 | tf_op jit(solution)/shard_map/ppermute | solution.py:20
  197.9 1.2 collective-permute-start.15
  199.2 3.8 %collective-permute-start.16 = (f32[35,128]{1,0:T(8,128)S(1)}, f32[35,128]{1,0:T(8,128)S(1)}, u32[]{:S(2)}, u32[]{:S(2)}) collective-permute-start(f32[35,128]{1,0:T(8,128)S(1)} %pad_maximum_fusion.10), channel_id=1, source_target_pairs={{0,2},{1,3},{2,0},{3,1},{4,6},{5,7},{6,4},{7,5},{8,10},{9,11},{10,... | collective-permute-start | bytes 53768 | tf_op jit(solution)/shard_map/ppermute | solution.py:126
  203.1 3.8 %collective-permute-start.17 = (f32[37,128]{1,0:T(8,128)S(1)}, f32[37,128]{1,0:T(8,128)S(1)}, u32[]{:S(2)}, u32[]{:S(2)}) collective-permute-start(f32[37,128]{1,0:T(8,128)S(1)} %pad_maximum_fusion.11), channel_id=1, source_target_pairs={{0,4},{4,0},{8,12},{12,8},{16,20},{20,16},{24,28},{28,24},{1,5},{5... | collective-permute-start | bytes 56840 | tf_op jit(solution)/shard_map/ppermute | solution.py:126
  207.0 3.9 %collective-permute-start.18 = (f32[41,128]{1,0:T(8,128)S(1)}, f32[41,128]{1,0:T(8,128)S(1)}, u32[]{:S(2)}, u32[]{:S(2)}) collective-permute-start(f32[41,128]{1,0:T(8,128)S(1)} %pad_maximum_fusion.5), channel_id=1, source_target_pairs={{0,8},{4,12},{8,0},{12,4},{16,24},{20,28},{24,16},{28,20},{1,9},{5... | collective-permute-start | bytes 62984 | tf_op jit(solution)/shard_map/ppermute | solution.py:126
  210.9 4.8 %collective-permute-start.19 = (f32[49,128]{1,0:T(8,128)S(1)}, f32[49,128]{1,0:T(8,128)S(1)}, u32[]{:S(2)}, u32[]{:S(2)}) collective-permute-start(f32[49,128]{1,0:T(8,128)S(1)} %pad_maximum_fusion.3), channel_id=1, source_target_pairs={{0,16},{4,20},{8,24},{12,28},{16,0},{20,4},{24,8},{28,12},{1,17},{... | collective-permute-start | bytes 75272 | tf_op jit(solution)/shard_map/ppermute | solution.py:126

commit v10 on v9

--- a/solution.py
+++ b/solution.py
@@ -234,7 +234,10 @@
     units = {0: unit_block}
     weights = {0: start}
     for offset in fetch_offsets:
-        units[offset] = shifted(unit_block, "wide", -offset)
+        if offset == fetch_offsets[-1]:
+            units[offset] = normalize_rows(shifted(embeddings, "wide", -offset))
+        else:
+            units[offset] = shifted(unit_block, "wide", -offset)
         weights[offset] = shifted(start, "wide", -offset)
 
     self_mask = lax.broadcasted_iota(

time: 230 us -> 224 us (0.974)
  matrix products: 42.2 us -> 13.4 us
  starting transfers between devices: 31.1 us -> 58 us
  waiting for transfers between devices: 113 us -> 98.3 us
  other arithmetic: 13.4 us -> 18.1 us
  local copies, waits for them, and re-layouts: 9.13 us -> 13.2 us
    ppermute x10, starting transfers between devices: 30.2 us -> 48.9 us  [shifted(): return lax.ppermute(block, axis, route)]
    ppermute x10, waiting for transfers between devices: 81.2 us -> 70.4 us  [shifted(): return lax.ppermute(block, axis, route)]
    dot_general x3 -> x1, matrix products: 14.9 us -> 4.46 us  [scores_tile(): lax.dot_general(leftside_block, right_block, (((1,), (1,)), ((), ())), pr...]
    dot_general x6 -> x2, matrix products: 12.2 us -> 2.12 us  [row_product(): return jnp.dot(affinity, weights, preferred_element_type=jnp.float32)]
    dot_general x4 -> x0, matrix products: 8.32 us -> none  [col_product(): lax.dot_general(affinity, weights, (((0,), (0,)), ((), ())), preferred_el...]
    ppermute x10, starting transfers between devices: 0.9 us -> 9.11 us  [butterfly(): other = lax.ppermute(block, axis, route)]
    another operation x7 -> x21, local copies, waits for them, and re-layouts: 1.64 us -> 5.71 us
    ppermute x10, waiting for transfers between devices: 31.4 us -> 27.9 us  [butterfly(): other = lax.ppermute(block, axis, route)]
  transfers between devices with their start and end apart: 20 -> 20, of which waited for: 15 -> 16; matrix products, arithmetic and copies ran while one was open for 12% -> 11% of each run, Pallas kernels for 4% -> 4%
where the time goes in v10:
time: 224 us; the launch traced here: 221 us
  waiting for transfers between devices  98.3 us (44%)
  starting transfers between devices  58 us (26%)
  other arithmetic  18.1 us (8%)
  Pallas kernels  16.8 us (8%)
  matrix products  13.4 us (6%)
  local copies, waits for them, and re-layouts  13.2 us (6%)
  between operations  3.2 us (1%)
    ppermute x10, waiting for transfers between devices, shifted(): return lax.ppermute(block, axis, route)  70.4 us
    ppermute x10, starting transfers between devices, shifted(): return lax.ppermute(block, axis, route)  48.9 us
    ppermute x10, waiting for transfers between devices, butterfly(): other = lax.ppermute(block, axis, route)  27.9 us
    pallas_call x2, Pallas kernels, factor_inverse(): pl.pallas_call(factor_kernel, out_shape=jax.ShapeDtypeStruct(gram_matrix....  16.8 us
    ppermute x10, starting transfers between devices, butterfly(): other = lax.ppermute(block, axis, route)  9.11 us
    dot_general x8, matrix products, hdot(): jnp.dot(left, right, precision=lax.Precision.HIGHEST, preferred_element_t...  6.77 us
    another operation x21, local copies, waits for them, and re-layouts  5.71 us
    convert_element_type x2, other arithmetic, normalize_rows(): (values_wide * scaling / math.sqrt(values_wide.shape[-1])).astype(jnp.bfl...  4.55 us
  transfers between devices with their start and end apart: 20, of which 16 were waited for; matrix products, arithmetic and copies ran while one was open for 11% of the time, Pallas kernels for 4%

profile of v10, /device:TPU:0, one launch (start us, length us, event | category | flops | bytes accessed | tf_op | source)
XLA Modules:
  0.0 221.1 jit_solution(5344980481608671439)
XLA Ops:
  0.6 3.1 %collective-permute-start.2 = (bf16[1024,768]{1,0:T(8,128)(2,1)}, bf16[1024,768]{1,0:T(8,128)(2,1)}, u32[]{:S(2)}, u32[]{:S(2)}) collective-permute-start(bf16[1024,768]{1,0:T(8,128)(2,1)} %param.15), channel_id=1, source_target_pairs={{24,0},{28,4},{0,8},{4,12},{8,16},{12,20},{16,24},{20,28},{25,1},{... | collective-permute-start | bytes 4718600 | tf_op jit(solution)/shard_map/ppermute | solution.py:20
  3.7 1.8 fusion.1
  5.6 1.6 fusion.3
  7.1 3.3 %collective-permute-start = (bf16[1024,768]{1,0:T(8,128)(2,1)}, bf16[1024,768]{1,0:T(8,128)(2,1)}, u32[]{:S(2)}, u32[]{:S(2)}) collective-permute-start(bf16[1024,768]{1,0:T(8,128)(2,1)} %fusion.3), channel_id=1, source_target_pairs={{4,0},{8,4},{12,8},{16,12},{20,16},{24,20},{28,24},{0,28},{5,1},{9... | collective-permute-start | bytes 4718600 | tf_op jit(solution)/shard_map/ppermute | solution.py:20
  10.7 2.0 collective-permute-start.1
  12.7 0.8 fusion.37
  15.4 4.5 %convert_reduce_fusion.6 = (f32[1024]{0:T(1024)}, bf16[1024,1024]{0,1:T(8,128)(2,1)S(1)}) fusion(bf16[1024,768]{1,0:T(8,128)(2,1)} %fusion.3), kind=kOutput, calls=%fused_computation.9 | convolution fusion | flops 1616903168 | bytes 3674112 | tf_op jit(solution)/shard_map/dot_general | solution.py:55
  19.8 21.5 %collective-permute-done.2 = bf16[1024,768]{1,0:T(8,128)(2,1)} collective-permute-done((bf16[1024,768]{1,0:T(8,128)(2,1)}, bf16[1024,768]{1,0:T(8,128)(2,1)}, u32[]{:S(2)}, u32[]{:S(2)}) %collective-permute-start.2) | collective-permute-done | bytes 1572896 | tf_op jit(solution)/shard_map/ppermute | solution.py:20
  41.3 1.8 fusion.4
  43.1 3.0 %fusion.6 = bf16[1024,768]{1,0:T(8,128)(2,1)} fusion(bf16[1024,768]{1,0:T(8,128)(2,1)} %collective-permute-done.2, f32[1024]{0:T(1024)S(1)} %add_rsqrt_fusion), kind=kLoop, calls=%fused_computation.23 | loop fusion | flops 3145728 | bytes 3149824 | tf_op jit(solution)/shard_map/convert_element_type | solution.py:51
  46.1 34.5 %collective-permute-done.3 = bf16[1024,64]{1,0:T(8,128)(2,1)S(1)} collective-permute-done((bf16[1024,64]{1,0:T(8,128)(2,1)S(1)}, bf16[1024,64]{1,0:T(8,128)(2,1)S(1)}, u32[]{:S(2)}, u32[]{:S(2)}) %collective-permute-start.3) | collective-permute-done | bytes 131104 | tf_op jit(solution)/shard_map/ppermute | solution.py:20
  80.6 1.6 conditional.7
  80.6 1.6 broadcast.110
  82.9 1.7 conditional.8
  82.9 1.6 broadcast.114
  84.6 0.7 copy-done.2
  85.7 22.5 %collective-permute-start.5 = (f32[520,128]{1,0:T(8,128)S(1)}, f32[520,128]{1,0:T(8,128)}, u32[]{:S(2)}, u32[]{:S(2)}) collective-permute-start(f32[520,128]{1,0:T(8,128)S(1)} %pad_maximum_fusion.1), channel_id=1, source_target_pairs={{8,0},{12,4},{16,8},{20,12},{24,16},{28,20},{0,24},{4,28},{9,1},{1... | collective-permute-start | bytes 798728 | tf_op jit(solution)/shard_map/ppermute | solution.py:20
  108.2 2.4 %conditional.6 = (bf16[1024,1024]{1,0:T(8,128)(2,1)}, f32[1024,64]{0,1:T(8,128)}, f32[1024]{0:T(1024)S(1)}, f32[1024,64]{0,1:T(8,128)S(1)}, f32[1024]{0:T(1024)S(1)}) conditional(s32[]{:T(128)} %convert_element_type.60, () %tuple.56, (bf16[1024,768]{1,0:T(8,128)(2,1)}, bf16[1024,768]{1,0:T(8,128)(2,1)}, bf16[1024,64]{1,0:T(8,128)(2,1)S(1)}, ...), branch_computations={%region_2.3_spmd, %region_3.0_spmd} | conditional | flops 1884289024 | bytes 10231848 | solution.py:96
  108.2 1.6 broadcast.106
  109.9 0.7 broadcast.107
  110.6 0.6 copy-done.6
  111.6 0.7 add_bitcast_fusion.1
  112.3 0.7 pad_maximum_fusion
  113.0 0.5 fusion.58
  113.5 1.0 slice.164
  114.8 7.6 %collective-permute-done.4 = f32[520,128]{1,0:T(8,128)} collective-permute-done((f32[520,128]{1,0:T(8,128)}, f32[520,128]{1,0:T(8,128)}, u32[]{:S(2)}, u32[]{:S(2)}) %collective-permute-start.4) | collective-permute-done | bytes 266272 | tf_op jit(solution)/shard_map/ppermute | solution.py:20
  122.4 1.0 slice.163
  123.8 1.2 fusion.43
  125.0 1.3 broadcast_multiply_fusion
  127.1 0.7 reduce_sum.153
  127.8 0.8 pad_maximum_fusion.12
  128.7 1.2 collective-permute-done.8
  129.9 4.1 %collective-permute-start.9 = (f32[35,128]{1,0:T(8,128)S(1)}, f32[35,128]{1,0:T(8,128)S(1)}, u32[]{:S(2)}, u32[]{:S(2)}) collective-permute-start(f32[35,128]{1,0:T(8,128)S(1)} %pad_maximum_fusion.7), channel_id=1, source_target_pairs={{0,2},{1,3},{2,0},{3,1},{4,6},{5,7},{6,4},{7,5},{8,10},{9,11},{10,... | collective-permute-start | bytes 53768 | tf_op jit(solution)/shard_map/ppermute | solution.py:126
  134.1 1.8 collective-permute-done.9
  136.0 3.8 %collective-permute-done.10 = f32[37,128]{1,0:T(8,128)S(1)} collective-permute-done((f32[37,128]{1,0:T(8,128)S(1)}, f32[37,128]{1,0:T(8,128)S(1)}, u32[]{:S(2)}, u32[]{:S(2)}) %collective-permute-start.10) | collective-permute-done | bytes 18976 | tf_op jit(solution)/shard_map/ppermute | solution.py:126
  139.9 3.8 %collective-permute-done.11 = f32[41,128]{1,0:T(8,128)S(1)} collective-permute-done((f32[41,128]{1,0:T(8,128)S(1)}, f32[41,128]{1,0:T(8,128)S(1)}, u32[]{:S(2)}, u32[]{:S(2)}) %collective-permute-start.11) | collective-permute-done | bytes 21024 | tf_op jit(solution)/shard_map/ppermute | solution.py:126
  143.7 3.1 %collective-permute-start.12 = (f32[49,128]{1,0:T(8,128)S(1)}, f32[49,128]{1,0:T(8,128)S(1)}, u32[]{:S(2)}, u32[]{:S(2)}) collective-permute-start(f32[49,128]{1,0:T(8,128)S(1)} %pad_maximum_fusion.2), channel_id=1, source_target_pairs={{0,16},{4,20},{8,24},{12,28},{16,0},{20,4},{24,8},{28,12},{1,17},{... | collective-permute-start | bytes 75272 | tf_op jit(solution)/shard_map/ppermute | solution.py:126
  146.8 2.0 collective-permute-start.7
  148.8 1.2 collective-permute-start.6
  150.0 1.5 collective-permute-done.12
  151.5 0.6 slice.177
  152.1 0.6 slice_divide_fusion.1
  153.2 0.9 fusion.12.gram_ref
  154.1 8.4 %shard_map.50 = f32[64,64]{1,0:T(8,128)} custom-call(f32[64,64]{1,0:T(8,128)} %fusion.12.gram_ref), custom_call_target="tpu_custom_call" | custom-call | tf_op jit(solution)/shard_map/pallas_call | solution.py:174
  162.5 1.7 convolution_convert_fusion
  164.2 0.7 copy-done.5
  165.1 0.7 add.228
  165.8 12.1 %collective-permute-start.14 = (f32[1024,64]{0,1:T(8,128)}, f32[1024,64]{0,1:T(8,128)}, u32[]{:S(2)}, u32[]{:S(2)}) collective-permute-start(f32[1024,64]{0,1:T(8,128)} %add.228), channel_id=1, source_target_pairs={{8,0},{12,4},{16,8},{20,12},{24,16},{28,20},{0,24},{4,28},{9,1},{1... | collective-permute-start | bytes 786440 | tf_op jit(solution)/shard_map/ppermute | solution.py:20
  178.0 2.7 %collective-permute-start.13 = (f32[1024,64]{0,1:T(8,128)S(1)}, f32[1024,64]{0,1:T(8,128)S(1)}, u32[]{:S(2)}, u32[]{:S(2)}) collective-permute-start(f32[1024,64]{0,1:T(8,128)S(1)} %add.226), channel_id=1, source_target_pairs={{28,0},{0,4},{4,8},{8,12},{12,16},{16,20},{20,24},{24,28},{29,1},{... | collective-permute-start | bytes 786440 | tf_op jit(solution)/shard_map/ppermute | solution.py:20
  180.7 1.4 collective-permute-done.14
  182.2 5.0 %collective-permute-done.13 = f32[1024,64]{0,1:T(8,128)S(1)} collective-permute-done((f32[1024,64]{0,1:T(8,128)S(1)}, f32[1024,64]{0,1:T(8,128)S(1)}, u32[]{:S(2)}, u32[]{:S(2)}) %collective-permute-start.13) | collective-permute-done | bytes 262176 | tf_op jit(solution)/shard_map/ppermute | solution.py:20
  187.2 1.6 fusion.40
  189.5 0.8 pad_maximum_fusion.13
  190.4 1.2 collective-permute-done.15
  191.7 3.8 %collective-permute-done.16 = f32[35,128]{1,0:T(8,128)S(1)} collective-permute-done((f32[35,128]{1,0:T(8,128)S(1)}, f32[35,128]{1,0:T(8,128)S(1)}, u32[]{:S(2)}, u32[]{:S(2)}) %collective-permute-start.16) | collective-permute-done | bytes 17952 | tf_op jit(solution)/shard_map/ppermute | solution.py:126
  195.6 3.8 %collective-permute-done.17 = f32[37,128]{1,0:T(8,128)S(1)} collective-permute-done((f32[37,128]{1,0:T(8,128)S(1)}, f32[37,128]{1,0:T(8,128)S(1)}, u32[]{:S(2)}, u32[]{:S(2)}) %collective-permute-start.17) | collective-permute-done | bytes 18976 | tf_op jit(solution)/shard_map/ppermute | solution.py:126
  199.5 3.8 %collective-permute-done.18 = f32[41,128]{1,0:T(8,128)S(1)} collective-permute-done((f32[41,128]{1,0:T(8,128)S(1)}, f32[41,128]{1,0:T(8,128)S(1)}, u32[]{:S(2)}, u32[]{:S(2)}) %collective-permute-start.18) | collective-permute-done | bytes 21024 | tf_op jit(solution)/shard_map/ppermute | solution.py:126
  203.4 1.4 collective-permute-start.19
  204.8 3.4 %collective-permute-done.19 = f32[49,128]{1,0:T(8,128)S(1)} collective-permute-done((f32[49,128]{1,0:T(8,128)S(1)}, f32[49,128]{1,0:T(8,128)S(1)}, u32[]{:S(2)}, u32[]{:S(2)}) %collective-permute-start.19) | collective-permute-done | bytes 25120 | tf_op jit(solution)/shard_map/ppermute | solution.py:126
  208.2 0.6 slice.195
  208.8 0.6 slice_divide_fusion
  209.9 0.9 fusion.10.gram_ref
  210.8 8.4 %shard_map.51 = f32[64,64]{1,0:T(8,128)} custom-call(f32[64,64]{1,0:T(8,128)} %fusion.10.gram_ref), custom_call_target="tpu_custom_call" | custom-call | tf_op jit(solution)/shard_map/pallas_call | solution.py:174
  219.2 1.9 fusion.18
  (126 shorter events, 6.1 us)
Async XLA Ops:
  0.6 4.9 %copy-start = (bf16[1024,768]{1,0:T(8,128)(2,1)S(1)}, bf16[1024,768]{1,0:T(8,128)(2,1)}, u32[]{:S(2)}) copy-start(bf16[1024,768]{1,0:T(8,128)(2,1)} %param.15) | copy-start | bytes 4718596
  0.6 9.8 %copy-start.1 = (bf16[1024,64]{0,1:T(8,128)(2,1)S(1)}, bf16[1024,64]{0,1:T(8,128)(2,1)}, u32[]{:S(2)}) copy-start(bf16[1024,64]{0,1:T(8,128)(2,1)} %param.16) | copy-start | bytes 393220
  0.6 40.7 %collective-permute-start.2 = (bf16[1024,768]{1,0:T(8,128)(2,1)}, bf16[1024,768]{1,0:T(8,128)(2,1)}, u32[]{:S(2)}, u32[]{:S(2)}) collective-permute-start(bf16[1024,768]{1,0:T(8,128)(2,1)} %param.15), channel_id=1, source_target_pairs={{24,0},{28,4},{0,8},{4,12},{8,16},{12,20},{16,24},{20,28},{25,1},{... | collective-permute-start | bytes 4718600 | tf_op jit(solution)/shard_map/ppermute | solution.py:20
  5.5 7.1 %copy-start.7 = (s32[32,3]{0,1:T(4,128)S(1)}, s32[32,3]{0,1:T(4,128)}, u32[]{:S(2)}) copy-start(s32[32,3]{0,1:T(4,128)} %param.17) | copy-start | bytes 1156
  7.1 75.4 %collective-permute-start = (bf16[1024,768]{1,0:T(8,128)(2,1)}, bf16[1024,768]{1,0:T(8,128)(2,1)}, u32[]{:S(2)}, u32[]{:S(2)}) collective-permute-start(bf16[1024,768]{1,0:T(8,128)(2,1)} %fusion.3), channel_id=1, source_target_pairs={{4,0},{8,4},{12,8},{16,12},{20,16},{24,20},{28,24},{0,28},{5,1},{9... | collective-permute-start | bytes 4718600 | tf_op jit(solution)/shard_map/ppermute | solution.py:20
  10.6 70.0 %collective-permute-start.3 = (bf16[1024,64]{1,0:T(8,128)(2,1)S(1)}, bf16[1024,64]{1,0:T(8,128)(2,1)S(1)}, u32[]{:S(2)}, u32[]{:S(2)}) collective-permute-start(bf16[1024,64]{1,0:T(8,128)(2,1)S(1)} %copy.17), channel_id=1, source_target_pairs={{24,0},{28,4},{0,8},{4,12},{8,16},{12,20},{16,24},{20,28},{25,1},{... | collective-permute-start | bytes 393224 | tf_op jit(solution)/shard_map/ppermute | solution.py:20
  10.7 71.9 %collective-permute-start.1 = (bf16[1024,64]{1,0:T(8,128)(2,1)S(1)}, bf16[1024,64]{1,0:T(8,128)(2,1)S(1)}, u32[]{:S(2)}, u32[]{:S(2)}) collective-permute-start(bf16[1024,64]{1,0:T(8,128)(2,1)S(1)} %copy.17), channel_id=1, source_target_pairs={{4,0},{8,4},{12,8},{16,12},{20,16},{24,20},{28,24},{0,28},{5,1},{9... | collective-permute-start | bytes 393224 | tf_op jit(solution)/shard_map/ppermute | solution.py:20
  82.2 0.7 copy-start.4
  84.6 0.7 copy-start.2
  85.7 27.8 %collective-permute-start.5 = (f32[520,128]{1,0:T(8,128)S(1)}, f32[520,128]{1,0:T(8,128)}, u32[]{:S(2)}, u32[]{:S(2)}) collective-permute-start(f32[520,128]{1,0:T(8,128)S(1)} %pad_maximum_fusion.1), channel_id=1, source_target_pairs={{8,0},{12,4},{16,8},{20,12},{24,16},{28,20},{0,24},{4,28},{9,1},{1... | collective-permute-start | bytes 798728 | tf_op jit(solution)/shard_map/ppermute | solution.py:20
  108.2 3.0 %copy-start.3 = (f32[1024,64]{0,1:T(8,128)S(1)}, f32[1024,64]{0,1:T(8,128)}, u32[]{:S(2)}) copy-start(f32[1024,64]{0,1:T(8,128)} %copy-done.2) | copy-start | bytes 786436
  110.6 0.6 copy-start.6
  113.0 9.4 %collective-permute-start.4 = (f32[520,128]{1,0:T(8,128)}, f32[520,128]{1,0:T(8,128)}, u32[]{:S(2)}, u32[]{:S(2)}) collective-permute-start(f32[520,128]{1,0:T(8,128)} %pad_maximum_fusion), channel_id=1, source_target_pairs={{28,0},{0,4},{4,8},{8,12},{12,16},{16,20},{20,24},{24,28},{29,1},{... | collective-permute-start | bytes 798728 | tf_op jit(solution)/shard_map/ppermute | solution.py:20
  114.6 10.3 %copy-start.8 = (f32[1024]{0:T(1024)S(1)}, f32[1024]{0:T(1024)}, u32[]{:S(2)}) copy-start(f32[1024]{0:T(1024)} %get-tuple-element.164) | copy-start | bytes 12292
  128.6 1.3 collective-permute-start.8
  129.9 5.9 %collective-permute-start.9 = (f32[35,128]{1,0:T(8,128)S(1)}, f32[35,128]{1,0:T(8,128)S(1)}, u32[]{:S(2)}, u32[]{:S(2)}) collective-permute-start(f32[35,128]{1,0:T(8,128)S(1)} %pad_maximum_fusion.7), channel_id=1, source_target_pairs={{0,2},{1,3},{2,0},{3,1},{4,6},{5,7},{6,4},{7,5},{8,10},{9,11},{10,... | collective-permute-start | bytes 53768 | tf_op jit(solution)/shard_map/ppermute | solution.py:126
  135.9 3.8 %collective-permute-start.10 = (f32[37,128]{1,0:T(8,128)S(1)}, f32[37,128]{1,0:T(8,128)S(1)}, u32[]{:S(2)}, u32[]{:S(2)}) collective-permute-start(f32[37,128]{1,0:T(8,128)S(1)} %pad_maximum_fusion.8), channel_id=1, source_target_pairs={{0,4},{4,0},{8,12},{12,8},{16,20},{20,16},{24,28},{28,24},{1,5},{5... | collective-permute-start | bytes 56840 | tf_op jit(solution)/shard_map/ppermute | solution.py:126
  139.8 3.9 %collective-permute-start.11 = (f32[41,128]{1,0:T(8,128)S(1)}, f32[41,128]{1,0:T(8,128)S(1)}, u32[]{:S(2)}, u32[]{:S(2)}) collective-permute-start(f32[41,128]{1,0:T(8,128)S(1)} %pad_maximum_fusion.4), channel_id=1, source_target_pairs={{0,8},{4,12},{8,0},{12,4},{16,24},{20,28},{24,16},{28,20},{1,9},{5... | collective-permute-start | bytes 62984 | tf_op jit(solution)/shard_map/ppermute | solution.py:126
  143.7 7.8 %collective-permute-start.12 = (f32[49,128]{1,0:T(8,128)S(1)}, f32[49,128]{1,0:T(8,128)S(1)}, u32[]{:S(2)}, u32[]{:S(2)}) collective-permute-start(f32[49,128]{1,0:T(8,128)S(1)} %pad_maximum_fusion.2), channel_id=1, source_target_pairs={{0,16},{4,20},{8,24},{12,28},{16,0},{20,4},{24,8},{28,12},{1,17},{... | collective-permute-start | bytes 75272 | tf_op jit(solution)/shard_map/ppermute | solution.py:126
  146.8 15.7 %collective-permute-start.7 = (f32[1024,64]{0,1:T(8,128)S(1)}, f32[1024,64]{0,1:T(8,128)S(1)}, u32[]{:S(2)}, u32[]{:S(2)}) collective-permute-start(f32[1024,64]{0,1:T(8,128)S(1)} %get-tuple-element.157), channel_id=1, source_target_pairs={{24,0},{28,4},{0,8},{4,12},{8,16},{12,20},{16,24},{20,28},{25,1},{... | collective-permute-start | bytes 786440 | tf_op jit(solution)/shard_map/ppermute | solution.py:20
  148.8 13.7 %collective-permute-start.6 = (f32[1024,64]{0,1:T(8,128)S(1)}, f32[1024,64]{0,1:T(8,128)S(1)}, u32[]{:S(2)}, u32[]{:S(2)}) collective-permute-start(f32[1024,64]{0,1:T(8,128)S(1)} %get-tuple-element.157), channel_id=1, source_target_pairs={{4,0},{8,4},{12,8},{16,12},{20,16},{24,20},{28,24},{0,28},{5,1},{9... | collective-permute-start | bytes 786440 | tf_op jit(solution)/shard_map/ppermute | solution.py:20
  164.2 0.8 copy-start.5
  165.8 16.3 %collective-permute-start.14 = (f32[1024,64]{0,1:T(8,128)}, f32[1024,64]{0,1:T(8,128)}, u32[]{:S(2)}, u32[]{:S(2)}) collective-permute-start(f32[1024,64]{0,1:T(8,128)} %add.228), channel_id=1, source_target_pairs={{8,0},{12,4},{16,8},{20,12},{24,16},{28,20},{0,24},{4,28},{9,1},{1... | collective-permute-start | bytes 786440 | tf_op jit(solution)/shard_map/ppermute | solution.py:20
  178.0 9.1 %collective-permute-start.13 = (f32[1024,64]{0,1:T(8,128)S(1)}, f32[1024,64]{0,1:T(8,128)S(1)}, u32[]{:S(2)}, u32[]{:S(2)}) collective-permute-start(f32[1024,64]{0,1:T(8,128)S(1)} %add.226), channel_id=1, source_target_pairs={{28,0},{0,4},{4,8},{8,12},{12,16},{16,20},{20,24},{24,28},{29,1},{... | collective-permute-start | bytes 786440 | tf_op jit(solution)/shard_map/ppermute | solution.py:20
  190.4 1.2 collective-permute-start.15
  191.7 3.8 %collective-permute-start.16 = (f32[35,128]{1,0:T(8,128)S(1)}, f32[35,128]{1,0:T(8,128)S(1)}, u32[]{:S(2)}, u32[]{:S(2)}) collective-permute-start(f32[35,128]{1,0:T(8,128)S(1)} %pad_maximum_fusion.10), channel_id=1, source_target_pairs={{0,2},{1,3},{2,0},{3,1},{4,6},{5,7},{6,4},{7,5},{8,10},{9,11},{10,... | collective-permute-start | bytes 53768 | tf_op jit(solution)/shard_map/ppermute | solution.py:126
  195.6 3.8 %collective-permute-start.17 = (f32[37,128]{1,0:T(8,128)S(1)}, f32[37,128]{1,0:T(8,128)S(1)}, u32[]{:S(2)}, u32[]{:S(2)}) collective-permute-start(f32[37,128]{1,0:T(8,128)S(1)} %pad_maximum_fusion.11), channel_id=1, source_target_pairs={{0,4},{4,0},{8,12},{12,8},{16,20},{20,16},{24,28},{28,24},{1,5},{5... | collective-permute-start | bytes 56840 | tf_op jit(solution)/shard_map/ppermute | solution.py:126
  199.4 3.9 %collective-permute-start.18 = (f32[41,128]{1,0:T(8,128)S(1)}, f32[41,128]{1,0:T(8,128)S(1)}, u32[]{:S(2)}, u32[]{:S(2)}) collective-permute-start(f32[41,128]{1,0:T(8,128)S(1)} %pad_maximum_fusion.5), channel_id=1, source_target_pairs={{0,8},{4,12},{8,0},{12,4},{16,24},{20,28},{24,16},{28,20},{1,9},{5... | collective-permute-start | bytes 62984 | tf_op jit(solution)/shard_map/ppermute | solution.py:126
  203.4 4.8 %collective-permute-start.19 = (f32[49,128]{1,0:T(8,128)S(1)}, f32[49,128]{1,0:T(8,128)S(1)}, u32[]{:S(2)}, u32[]{:S(2)}) collective-permute-start(f32[49,128]{1,0:T(8,128)S(1)} %pad_maximum_fusion.3), channel_id=1, source_target_pairs={{0,16},{4,20},{8,24},{12,28},{16,0},{20,4},{24,8},{28,12},{1,17},{... | collective-permute-start | bytes 75272 | tf_op jit(solution)/shard_map/ppermute | solution.py:126

commit v11 on v9

--- a/solution.py
+++ b/solution.py
@@ -233,9 +233,16 @@
     vector_count = start.shape[1]
     units = {0: unit_block}
     weights = {0: start}
+    unit_width = unit_block.shape[1]
+    weight_rows = as_rows(start.reshape(-1), unit_width)
     for offset in fetch_offsets:
-        units[offset] = shifted(unit_block, "wide", -offset)
-        weights[offset] = shifted(start, "wide", -offset)
+        raw = offset == fetch_offsets[-1]
+        rows = embeddings if raw else unit_block
+        arrived = shifted(jnp.concatenate([rows, weight_rows]), "wide", -offset)
+        units[offset] = normalize_rows(arrived[:block_rows]) if raw else arrived[:block_rows]
+        weights[offset] = (
+            arrived[block_rows:].reshape(-1)[: block_rows * vector_count].reshape(block_rows, vector_count)
+        )
 
     self_mask = lax.broadcasted_iota(
         jnp.int32, (block_rows, block_rows), 0

time: 230 us -> 231 us (level)
  waiting for transfers between devices: 113 us -> 91.7 us
  starting transfers between devices: 31.1 us -> 42.2 us
  local copies, waits for them, and re-layouts: 9.13 us -> 16.5 us
  other arithmetic: 13.4 us -> 17.6 us
  matrix products: 42.2 us -> 39.7 us
    ppermute x10, starting transfers between devices: 0.9 us -> 13.4 us  [butterfly(): other = lax.ppermute(block, axis, route)]
    ppermute x10 -> x8, waiting for transfers between devices: 81.2 us -> 70.1 us  [shifted(): return lax.ppermute(block, axis, route)]
    ppermute x10, waiting for transfers between devices: 31.4 us -> 21.5 us  [butterfly(): other = lax.ppermute(block, axis, route)]
    slice x0 -> x7, local copies, waits for them, and re-layouts: none -> 5.57 us  [the longest x1 3.33 us: on_device(): arrived[:block_rows]]
    ppermute x10 -> x8, starting transfers between devices: 30.2 us -> 28.8 us  [shifted(): return lax.ppermute(block, axis, route)]
  transfers between devices with their start and end apart: 20 -> 18, of which waited for: 15 -> 15; matrix products, arithmetic and copies ran while one was open for 12% -> 7% of each run, Pallas kernels for 4% -> 4%
where the time goes in v11:
time: 231 us; the launch traced here: 228 us
  waiting for transfers between devices  91.7 us (40%)
  starting transfers between devices  42.2 us (18%)
  matrix products  39.7 us (17%)
  other arithmetic  17.6 us (8%)
  Pallas kernels  16.8 us (7%)
  local copies, waits for them, and re-layouts  16.5 us (7%)
  between operations  3.29 us (1%)
    ppermute x8, waiting for transfers between devices, shifted(): return lax.ppermute(block, axis, route)  70.1 us
    ppermute x8, starting transfers between devices, shifted(): return lax.ppermute(block, axis, route)  28.8 us
    ppermute x10, waiting for transfers between devices, butterfly(): other = lax.ppermute(block, axis, route)  21.5 us
    pallas_call x2, Pallas kernels, factor_inverse(): pl.pallas_call(factor_kernel, out_shape=jax.ShapeDtypeStruct(gram_matrix....  16.8 us
    ppermute x10, starting transfers between devices, butterfly(): other = lax.ppermute(block, axis, route)  13.4 us
    dot_general x3, matrix products, scores_tile(): lax.dot_general(leftside_block, right_block, (((1,), (1,)), ((), ())), pr...  13 us
    dot_general x6, matrix products, row_product(): return jnp.dot(affinity, weights, preferred_element_type=jnp.float32)  11.5 us
    dot_general x4, matrix products, col_product(): lax.dot_general(affinity, weights, (((0,), (0,)), ((), ())), preferred_el...  8.37 us
  transfers between devices with their start and end apart: 18, of which 15 were waited for; matrix products, arithmetic and copies ran while one was open for 7% of the time, Pallas kernels for 4%

profile of v11, /device:TPU:0, one launch (start us, length us, event | category | flops | bytes accessed | tf_op | source)
XLA Modules:
  0.0 228.0 jit_solution(10169695026761613509)
XLA Ops:
  0.6 1.2 copy.15
  2.2 1.8 fusion.1
  4.4 2.2 pad_maximum_fusion.1
  6.7 3.0 %collective-permute-start.1 = (bf16[1110,768]{1,0:T(8,128)(2,1)}, bf16[1110,768]{1,0:T(8,128)(2,1)}, u32[]{:S(2)}, u32[]{:S(2)}) collective-permute-start(bf16[1110,768]{1,0:T(8,128)(2,1)} %get-tuple-element.165), channel_id=1, source_target_pairs={{24,0},{28,4},{0,8},{4,12},{8,16},{12,20},{16,24},{20,28},{25,1},{... | collective-permute-start | bytes 5114888 | tf_op jit(solution)/shard_map/ppermute | solution.py:20
  9.7 3.2 %collective-permute-start = (bf16[1110,768]{1,0:T(8,128)(2,1)}, bf16[1110,768]{1,0:T(8,128)(2,1)}, u32[]{:S(2)}, u32[]{:S(2)}) collective-permute-start(bf16[1110,768]{1,0:T(8,128)(2,1)} %get-tuple-element.164), channel_id=1, source_target_pairs={{4,0},{8,4},{12,8},{16,12},{20,16},{24,20},{28,24},{0,28},{5,1},{9... | collective-permute-start | bytes 5114888 | tf_op jit(solution)/shard_map/ppermute | solution.py:20
  15.7 4.4 %convert_reduce_fusion.6 = (f32[1024]{0:T(1024)}, bf16[1024,1024]{0,1:T(8,128)(2,1)S(1)}) fusion(bf16[1024,768]{1,0:T(8,128)(2,1)} %copy-done.1), kind=kOutput, calls=%fused_computation.9 | convolution fusion | flops 1616903168 | bytes 3674112 | tf_op jit(solution)/shard_map/dot_general | solution.py:55
  20.1 30.1 %collective-permute-done.1 = bf16[1110,768]{1,0:T(8,128)(2,1)} collective-permute-done((bf16[1110,768]{1,0:T(8,128)(2,1)}, bf16[1110,768]{1,0:T(8,128)(2,1)}, u32[]{:S(2)}, u32[]{:S(2)}) %collective-permute-start.1) | collective-permute-done | bytes 1704992 | tf_op jit(solution)/shard_map/ppermute | solution.py:20
  50.2 0.9 slice.199
  51.3 1.8 fusion.4
  53.1 30.1 %collective-permute-done = bf16[1110,768]{1,0:T(8,128)(2,1)} collective-permute-done((bf16[1110,768]{1,0:T(8,128)(2,1)}, bf16[1110,768]{1,0:T(8,128)(2,1)}, u32[]{:S(2)}, u32[]{:S(2)}) %collective-permute-start) | collective-permute-done | bytes 1704992 | tf_op jit(solution)/shard_map/ppermute | solution.py:20
  83.2 0.9 slice.196
  84.4 1.8 fusion.6
  86.2 3.3 %slice.195 = bf16[1024,768]{1,0:T(8,128)(2,1)} slice(bf16[1110,768]{1,0:T(8,128)(2,1)} %collective-permute-done), slice={[0:1024], [0:768]} | slice | bytes 3145728 | tf_op jit(solution)/shard_map/slice | solution.py:242
  89.6 7.8 %conditional.7 = (bf16[1024,1024]{1,0:T(8,128)(2,1)}, f32[1024,64]{0,1:T(8,128)S(1)}, f32[1024]{0:T(1024)S(1)}, f32[1024,64]{0,1:T(8,128)S(1)}, f32[1024]{0:T(1024)S(1)}) conditional(s32[]{:T(128)} %convert_element_type.63, () %tuple.58, (bf16[1024,768]{1,0:T(8,128)(2,1)S(1)}, bf16[1024,768]{1,0:T(8,128)(2,1)S(1)}, bf16[1024,64]{0,1:T(8,128)(2,1)S(1)}, ...), branch_computations={%region_8.9_spmd, %region_9.12_spmd} | conditional | flops 1884289024 | bytes 10231848 | solution.py:96
  89.6 3.4 %convert_reduce_fusion.2 = (f32[1024]{0:T(1024)S(1)}, f32[1024]{0:T(1024)S(1)}, bf16[1024,1024]{1,0:T(8,128)(2,1)}) fusion(bf16[1024,768]{1,0:T(8,128)(2,1)S(1)} %get-tuple-element.46, bf16[1024,768]{1,0:T(8,128)(2,1)S(1)} %get-tuple-element.47), kind=kOutput, calls=%fused_computation.3 | convolution fusion | flops 1615853568 | bytes 5251072 | tf_op jit(solution)/shard_map/cond/branch_1_fun/dot_general | solution.py:55
  93.0 2.3 %fusion.54 = f32[1024,64]{0,1:T(8,128)S(1)} fusion(bf16[1024,1024]{1,0:T(8,128)(2,1)} %get-tuple-element.177, bf16[1024,64]{0,1:T(8,128)(2,1)S(1)} %get-tuple-element.130), kind=kOutput, calls=%fused_computation.137 | convolution fusion | flops 134217728 | bytes 2490368 | tf_op jit(solution)/shard_map/cond/branch_1_fun/dot_general | solution.py:62
  95.3 2.1 fusion.55
  98.1 9.7 %conditional.8 = (bf16[1024,1024]{1,0:T(8,128)(2,1)}, f32[1024,64]{0,1:T(8,128)S(1)}, f32[1024]{0:T(1024)S(1)}, f32[1024,64]{0,1:T(8,128)S(1)}, f32[1024]{0:T(1024)S(1)}) conditional(s32[]{:T(128)} %convert_element_type.66, () %tuple.60, (bf16[1024,768]{1,0:T(8,128)(2,1)}, bf16[1024,768]{1,0:T(8,128)(2,1)}, bf16[1024,64]{1,0:T(8,128)(2,1)S(1)}, ...), branch_computations={%region_13.14_spmd, %region_14.17_spmd} | conditional | flops 1884289024 | bytes 10231848 | solution.py:96
  98.1 5.2 %convert_reduce_fusion.4 = (f32[1024]{0:T(1024)S(1)}, f32[1024]{0:T(1024)S(1)}, bf16[1024,1024]{1,0:T(8,128)(2,1)}) fusion(bf16[1024,768]{1,0:T(8,128)(2,1)} %get-tuple-element.50, bf16[1024,768]{1,0:T(8,128)(2,1)} %get-tuple-element.51), kind=kOutput, calls=%fused_computation.6 | convolution fusion | flops 1615853568 | bytes 5251072 | tf_op jit(solution)/shard_map/cond/branch_1_fun/dot_general | solution.py:55
  103.3 2.3 %fusion.56 = f32[1024,64]{0,1:T(8,128)S(1)} fusion(bf16[1024,1024]{1,0:T(8,128)(2,1)} %get-tuple-element.187, bf16[1024,64]{1,0:T(8,128)(2,1)S(1)} %get-tuple-element.52), kind=kOutput, calls=%fused_computation.139 | convolution fusion | flops 134217728 | bytes 2490368 | tf_op jit(solution)/shard_map/cond/branch_1_fun/dot_general | solution.py:62
  105.7 2.1 fusion.57
  108.9 7.4 %collective-permute-start.3 = (f32[520,128]{1,0:T(8,128)S(1)}, f32[520,128]{1,0:T(8,128)}, u32[]{:S(2)}, u32[]{:S(2)}) collective-permute-start(f32[520,128]{1,0:T(8,128)S(1)} %pad_maximum_fusion.3), channel_id=1, source_target_pairs={{8,0},{12,4},{16,8},{20,12},{24,16},{28,20},{0,24},{4,28},{9,1},{1... | collective-permute-start | bytes 798728 | tf_op jit(solution)/shard_map/ppermute | solution.py:20
  116.4 1.8 conditional.6
  116.4 1.6 broadcast.106
  120.7 6.2 %collective-permute-start.2 = (f32[520,128]{1,0:T(8,128)}, f32[520,128]{1,0:T(8,128)}, u32[]{:S(2)}, u32[]{:S(2)}) collective-permute-start(f32[520,128]{1,0:T(8,128)} %pad_maximum_fusion.2), channel_id=1, source_target_pairs={{28,0},{0,4},{4,8},{8,12},{12,16},{16,20},{20,24},{24,28},{29,1},{... | collective-permute-start | bytes 798728 | tf_op jit(solution)/shard_map/ppermute | solution.py:20
  127.5 1.0 slice.202
  128.8 3.6 %collective-permute-done.2 = f32[520,128]{1,0:T(8,128)} collective-permute-done((f32[520,128]{1,0:T(8,128)}, f32[520,128]{1,0:T(8,128)}, u32[]{:S(2)}, u32[]{:S(2)}) %collective-permute-start.2) | collective-permute-done | bytes 266272 | tf_op jit(solution)/shard_map/ppermute | solution.py:20
  132.3 1.0 slice.201
  133.7 1.2 fusion.43
  134.9 1.3 broadcast_multiply_fusion
  138.4 1.2 collective-permute-done.6
  139.6 1.6 collective-permute-start.7
  141.2 2.2 collective-permute-done.7
  143.5 1.9 collective-permute-start.8
  145.3 2.0 collective-permute-done.8
  147.4 1.6 collective-permute-start.9
  149.0 2.3 %collective-permute-done.9 = f32[41,128]{1,0:T(8,128)S(1)} collective-permute-done((f32[41,128]{1,0:T(8,128)S(1)}, f32[41,128]{1,0:T(8,128)S(1)}, u32[]{:S(2)}, u32[]{:S(2)}) %collective-permute-start.9) | collective-permute-done | bytes 21024 | tf_op jit(solution)/shard_map/ppermute | solution.py:126
  151.3 3.1 %collective-permute-start.10 = (f32[49,128]{1,0:T(8,128)S(1)}, f32[49,128]{1,0:T(8,128)S(1)}, u32[]{:S(2)}, u32[]{:S(2)}) collective-permute-start(f32[49,128]{1,0:T(8,128)S(1)} %pad_maximum_fusion.4), channel_id=1, source_target_pairs={{0,16},{4,20},{8,24},{12,28},{16,0},{20,4},{24,8},{28,12},{1,17},{... | collective-permute-start | bytes 75272 | tf_op jit(solution)/shard_map/ppermute | solution.py:126
  154.4 1.5 collective-permute-start.5
  155.9 1.8 collective-permute-start.4
  157.7 1.4 collective-permute-done.10
  161.6 8.4 %shard_map.50 = f32[64,64]{1,0:T(8,128)} custom-call(f32[64,64]{1,0:T(8,128)} %fusion.12.gram_ref), custom_call_target="tpu_custom_call" | custom-call | tf_op jit(solution)/shard_map/pallas_call | solution.py:174
  170.1 1.7 convolution_convert_fusion
  172.5 4.4 %conditional.10 = (f32[1024,64]{0,1:T(8,128)S(1)}, f32[1024,64]{0,1:T(8,128)S(1)}) conditional(s32[]{:T(128)} %convert_element_type.63, () %tuple.64, (bf16[1024,1024]{1,0:T(8,128)(2,1)}, bf16[1024,64]{0,1:T(8,128)(2,1)S(1)}, bf16[1024,64]{0,1:T(8,128)(2,1)S(1)}) %tuple.65), branch_computations={%region_24.25_spmd, %region_25.26_spmd} | conditional | flops 268435456 | bytes 4980752 | solution.py:110
  172.5 2.3 %fusion.48 = f32[1024,64]{0,1:T(8,128)S(1)} fusion(bf16[1024,1024]{1,0:T(8,128)(2,1)} %get-tuple-element.57, bf16[1024,64]{0,1:T(8,128)(2,1)S(1)} %get-tuple-element.136), kind=kOutput, calls=%fused_computation.131 | convolution fusion | flops 134217728 | bytes 2490368 | tf_op jit(solution)/shard_map/cond/branch_1_fun/dot_general | solution.py:62
  174.9 2.1 fusion.49
  176.9 4.4 %conditional.11 = (f32[1024,64]{0,1:T(8,128)S(1)}, f32[1024,64]{0,1:T(8,128)S(1)}) conditional(s32[]{:T(128)} %convert_element_type.66, () %tuple.66, (bf16[1024,1024]{1,0:T(8,128)(2,1)}, bf16[1024,64]{0,1:T(8,128)(2,1)S(1)}, bf16[1024,64]{0,1:T(8,128)(2,1)S(1)}) %tuple.67), branch_computations={%region_26.27_spmd, %region_27.28_spmd} | conditional | flops 268435456 | bytes 4980752 | solution.py:110
  177.0 2.3 %fusion.50 = f32[1024,64]{0,1:T(8,128)S(1)} fusion(bf16[1024,1024]{1,0:T(8,128)(2,1)} %get-tuple-element.60, bf16[1024,64]{0,1:T(8,128)(2,1)S(1)} %get-tuple-element.139), kind=kOutput, calls=%fused_computation.133 | convolution fusion | flops 134217728 | bytes 2490368 | tf_op jit(solution)/shard_map/cond/branch_1_fun/dot_general | solution.py:62
  179.3 2.1 fusion.51
  182.1 2.9 %collective-permute-start.12 = (f32[1024,64]{0,1:T(8,128)}, f32[1024,64]{0,1:T(8,128)}, u32[]{:S(2)}, u32[]{:S(2)}) collective-permute-start(f32[1024,64]{0,1:T(8,128)} %add.230), channel_id=1, source_target_pairs={{8,0},{12,4},{16,8},{20,12},{24,16},{28,20},{0,24},{4,28},{9,1},{1... | collective-permute-start | bytes 786440 | tf_op jit(solution)/shard_map/ppermute | solution.py:20
  185.1 2.7 %collective-permute-start.11 = (f32[1024,64]{0,1:T(8,128)S(1)}, f32[1024,64]{0,1:T(8,128)S(1)}, u32[]{:S(2)}, u32[]{:S(2)}) collective-permute-start(f32[1024,64]{0,1:T(8,128)S(1)} %add.228), channel_id=1, source_target_pairs={{28,0},{0,4},{4,8},{8,12},{12,16},{16,20},{20,24},{24,28},{29,1},{... | collective-permute-start | bytes 786440 | tf_op jit(solution)/shard_map/ppermute | solution.py:20
  187.8 1.4 collective-permute-done.12
  189.2 5.0 %collective-permute-done.11 = f32[1024,64]{0,1:T(8,128)S(1)} collective-permute-done((f32[1024,64]{0,1:T(8,128)S(1)}, f32[1024,64]{0,1:T(8,128)S(1)}, u32[]{:S(2)}, u32[]{:S(2)}) %collective-permute-start.11) | collective-permute-done | bytes 262176 | tf_op jit(solution)/shard_map/ppermute | solution.py:20
  194.2 1.7 fusion.40
  197.3 1.2 collective-permute-done.13
  198.6 2.1 collective-permute-start.14
  200.7 1.8 collective-permute-done.14
  202.6 3.8 %collective-permute-done.15 = f32[37,128]{1,0:T(8,128)S(1)} collective-permute-done((f32[37,128]{1,0:T(8,128)S(1)}, f32[37,128]{1,0:T(8,128)S(1)}, u32[]{:S(2)}, u32[]{:S(2)}) %collective-permute-start.15) | collective-permute-done | bytes 18976 | tf_op jit(solution)/shard_map/ppermute | solution.py:126
  206.4 1.8 collective-permute-start.16
  208.2 2.1 collective-permute-done.16
  210.3 1.2 collective-permute-start.17
  211.5 3.6 %collective-permute-done.17 = f32[49,128]{1,0:T(8,128)S(1)} collective-permute-done((f32[49,128]{1,0:T(8,128)S(1)}, f32[49,128]{1,0:T(8,128)S(1)}, u32[]{:S(2)}, u32[]{:S(2)}) %collective-permute-start.17) | collective-permute-done | bytes 25120 | tf_op jit(solution)/shard_map/ppermute | solution.py:126
  217.7 8.4 %shard_map.51 = f32[64,64]{1,0:T(8,128)} custom-call(f32[64,64]{1,0:T(8,128)} %fusion.10.gram_ref), custom_call_target="tpu_custom_call" | custom-call | tf_op jit(solution)/shard_map/pallas_call | solution.py:174
  226.1 1.9 fusion.18
  (137 shorter events, 18.0 us)
Async XLA Ops:
  0.6 3.3 %copy-start = (bf16[1024,768]{1,0:T(8,128)(2,1)S(1)}, bf16[1024,768]{1,0:T(8,128)(2,1)}, u32[]{:S(2)}) copy-start(bf16[1024,768]{1,0:T(8,128)(2,1)} %param.15) | copy-start | bytes 4718596
  4.4 2.3 %copy-start.1 = (bf16[1024,768]{1,0:T(8,128)(2,1)}, bf16[1024,768]{1,0:T(8,128)(2,1)S(1)}, u32[]{:S(2)}) copy-start(bf16[1024,768]{1,0:T(8,128)(2,1)S(1)} %fusion.3) | copy-start | bytes 4718596
  4.4 8.5 %copy-start.11 = (s32[32,3]{0,1:T(4,128)S(1)}, s32[32,3]{0,1:T(4,128)}, u32[]{:S(2)}) copy-start(s32[32,3]{0,1:T(4,128)} %param.17) | copy-start | bytes 1156
  6.7 43.5 %collective-permute-start.1 = (bf16[1110,768]{1,0:T(8,128)(2,1)}, bf16[1110,768]{1,0:T(8,128)(2,1)}, u32[]{:S(2)}, u32[]{:S(2)}) collective-permute-start(bf16[1110,768]{1,0:T(8,128)(2,1)} %get-tuple-element.165), channel_id=1, source_target_pairs={{24,0},{28,4},{0,8},{4,12},{8,16},{12,20},{16,24},{20,28},{25,1},{... | collective-permute-start | bytes 5114888 | tf_op jit(solution)/shard_map/ppermute | solution.py:20
  9.7 73.5 %collective-permute-start = (bf16[1110,768]{1,0:T(8,128)(2,1)}, bf16[1110,768]{1,0:T(8,128)(2,1)}, u32[]{:S(2)}, u32[]{:S(2)}) collective-permute-start(bf16[1110,768]{1,0:T(8,128)(2,1)} %get-tuple-element.164), channel_id=1, source_target_pairs={{4,0},{8,4},{12,8},{16,12},{20,16},{24,20},{28,24},{0,28},{5,1},{9... | collective-permute-start | bytes 5114888 | tf_op jit(solution)/shard_map/ppermute | solution.py:20
  86.2 3.4 %copy-start.4 = (bf16[1024,768]{1,0:T(8,128)(2,1)}, bf16[1024,768]{1,0:T(8,128)(2,1)S(1)}, u32[]{:S(2)}) copy-start(bf16[1024,768]{1,0:T(8,128)(2,1)S(1)} %fusion.6) | copy-start | bytes 4718596
  86.2 3.4 %copy-start.2 = (bf16[1024,768]{1,0:T(8,128)(2,1)S(1)}, bf16[1024,768]{1,0:T(8,128)(2,1)}, u32[]{:S(2)}) copy-start(bf16[1024,768]{1,0:T(8,128)(2,1)} %copy-done.1) | copy-start | bytes 4718596
  86.2 3.3 %copy-start.3 = (bf16[1024,64]{0,1:T(8,128)(2,1)S(1)}, bf16[1024,64]{0,1:T(8,128)(2,1)}, u32[]{:S(2)}) copy-start(bf16[1024,64]{0,1:T(8,128)(2,1)} %param.16) | copy-start | bytes 393220
  97.4 0.7 copy-start.7
  107.8 0.7 copy-start.5
  108.9 10.0 %copy-start.6 = (f32[1024,64]{0,1:T(8,128)S(1)}, f32[1024,64]{0,1:T(8,128)}, u32[]{:S(2)}) copy-start(f32[1024,64]{0,1:T(8,128)} %copy-done.5) | copy-start | bytes 786436
  108.9 18.5 %collective-permute-start.3 = (f32[520,128]{1,0:T(8,128)S(1)}, f32[520,128]{1,0:T(8,128)}, u32[]{:S(2)}, u32[]{:S(2)}) collective-permute-start(f32[520,128]{1,0:T(8,128)S(1)} %pad_maximum_fusion.3), channel_id=1, source_target_pairs={{8,0},{12,4},{16,8},{20,12},{24,16},{28,20},{0,24},{4,28},{9,1},{1... | collective-permute-start | bytes 798728 | tf_op jit(solution)/shard_map/ppermute | solution.py:20
  118.2 0.7 copy-start.8
  118.2 0.7 copy-start.10
  120.7 11.6 %collective-permute-start.2 = (f32[520,128]{1,0:T(8,128)}, f32[520,128]{1,0:T(8,128)}, u32[]{:S(2)}, u32[]{:S(2)}) collective-permute-start(f32[520,128]{1,0:T(8,128)} %pad_maximum_fusion.2), channel_id=1, source_target_pairs={{28,0},{0,4},{4,8},{8,12},{12,16},{16,20},{20,24},{24,28},{29,1},{... | collective-permute-start | bytes 798728 | tf_op jit(solution)/shard_map/ppermute | solution.py:20
  128.6 6.3 %copy-start.12 = (f32[1024]{0:T(1024)S(1)}, f32[1024]{0:T(1024)}, u32[]{:S(2)}) copy-start(f32[1024]{0:T(1024)} %get-tuple-element.166) | copy-start | bytes 12292
  138.3 1.3 collective-permute-start.6
  139.6 3.8 %collective-permute-start.7 = (f32[35,128]{1,0:T(8,128)S(1)}, f32[35,128]{1,0:T(8,128)S(1)}, u32[]{:S(2)}, u32[]{:S(2)}) collective-permute-start(f32[35,128]{1,0:T(8,128)S(1)} %pad_maximum_fusion.9), channel_id=1, source_target_pairs={{0,2},{1,3},{2,0},{3,1},{4,6},{5,7},{6,4},{7,5},{8,10},{9,11},{10,... | collective-permute-start | bytes 53768 | tf_op jit(solution)/shard_map/ppermute | solution.py:126
  143.5 3.8 %collective-permute-start.8 = (f32[37,128]{1,0:T(8,128)S(1)}, f32[37,128]{1,0:T(8,128)S(1)}, u32[]{:S(2)}, u32[]{:S(2)}) collective-permute-start(f32[37,128]{1,0:T(8,128)S(1)} %pad_maximum_fusion.10), channel_id=1, source_target_pairs={{0,4},{4,0},{8,12},{12,8},{16,20},{20,16},{24,28},{28,24},{1,5},{5... | collective-permute-start | bytes 56840 | tf_op jit(solution)/shard_map/ppermute | solution.py:126
  147.4 3.9 %collective-permute-start.9 = (f32[41,128]{1,0:T(8,128)S(1)}, f32[41,128]{1,0:T(8,128)S(1)}, u32[]{:S(2)}, u32[]{:S(2)}) collective-permute-start(f32[41,128]{1,0:T(8,128)S(1)} %pad_maximum_fusion.6), channel_id=1, source_target_pairs={{0,8},{4,12},{8,0},{12,4},{16,24},{20,28},{24,16},{28,20},{1,9},{5... | collective-permute-start | bytes 62984 | tf_op jit(solution)/shard_map/ppermute | solution.py:126
  151.3 7.8 %collective-permute-start.10 = (f32[49,128]{1,0:T(8,128)S(1)}, f32[49,128]{1,0:T(8,128)S(1)}, u32[]{:S(2)}, u32[]{:S(2)}) collective-permute-start(f32[49,128]{1,0:T(8,128)S(1)} %pad_maximum_fusion.4), channel_id=1, source_target_pairs={{0,16},{4,20},{8,24},{12,28},{16,0},{20,4},{24,8},{28,12},{1,17},{... | collective-permute-start | bytes 75272 | tf_op jit(solution)/shard_map/ppermute | solution.py:126
  154.4 15.7 %collective-permute-start.5 = (f32[1024,64]{0,1:T(8,128)S(1)}, f32[1024,64]{0,1:T(8,128)S(1)}, u32[]{:S(2)}, u32[]{:S(2)}) collective-permute-start(f32[1024,64]{0,1:T(8,128)S(1)} %get-tuple-element.157), channel_id=1, source_target_pairs={{24,0},{28,4},{0,8},{4,12},{8,16},{12,20},{16,24},{20,28},{25,1},{... | collective-permute-start | bytes 786440 | tf_op jit(solution)/shard_map/ppermute | solution.py:20
  155.9 14.2 %collective-permute-start.4 = (f32[1024,64]{0,1:T(8,128)S(1)}, f32[1024,64]{0,1:T(8,128)S(1)}, u32[]{:S(2)}, u32[]{:S(2)}) collective-permute-start(f32[1024,64]{0,1:T(8,128)S(1)} %get-tuple-element.157), channel_id=1, source_target_pairs={{4,0},{8,4},{12,8},{16,12},{20,16},{24,20},{28,24},{0,28},{5,1},{9... | collective-permute-start | bytes 786440 | tf_op jit(solution)/shard_map/ppermute | solution.py:20
  171.8 0.7 copy-start.9
  182.1 7.1 %collective-permute-start.12 = (f32[1024,64]{0,1:T(8,128)}, f32[1024,64]{0,1:T(8,128)}, u32[]{:S(2)}, u32[]{:S(2)}) collective-permute-start(f32[1024,64]{0,1:T(8,128)} %add.230), channel_id=1, source_target_pairs={{8,0},{12,4},{16,8},{20,12},{24,16},{28,20},{0,24},{4,28},{9,1},{1... | collective-permute-start | bytes 786440 | tf_op jit(solution)/shard_map/ppermute | solution.py:20
  185.1 9.1 %collective-permute-start.11 = (f32[1024,64]{0,1:T(8,128)S(1)}, f32[1024,64]{0,1:T(8,128)S(1)}, u32[]{:S(2)}, u32[]{:S(2)}) collective-permute-start(f32[1024,64]{0,1:T(8,128)S(1)} %add.228), channel_id=1, source_target_pairs={{28,0},{0,4},{4,8},{8,12},{12,16},{16,20},{20,24},{24,28},{29,1},{... | collective-permute-start | bytes 786440 | tf_op jit(solution)/shard_map/ppermute | solution.py:20
  197.3 1.2 collective-permute-start.13
  198.6 3.9 %collective-permute-start.14 = (f32[35,128]{1,0:T(8,128)S(1)}, f32[35,128]{1,0:T(8,128)S(1)}, u32[]{:S(2)}, u32[]{:S(2)}) collective-permute-start(f32[35,128]{1,0:T(8,128)S(1)} %pad_maximum_fusion.12), channel_id=1, source_target_pairs={{0,2},{1,3},{2,0},{3,1},{4,6},{5,7},{6,4},{7,5},{8,10},{9,11},{10,... | collective-permute-start | bytes 53768 | tf_op jit(solution)/shard_map/ppermute | solution.py:126
  202.5 3.8 %collective-permute-start.15 = (f32[37,128]{1,0:T(8,128)S(1)}, f32[37,128]{1,0:T(8,128)S(1)}, u32[]{:S(2)}, u32[]{:S(2)}) collective-permute-start(f32[37,128]{1,0:T(8,128)S(1)} %pad_maximum_fusion.13), channel_id=1, source_target_pairs={{0,4},{4,0},{8,12},{12,8},{16,20},{20,16},{24,28},{28,24},{1,5},{5... | collective-permute-start | bytes 56840 | tf_op jit(solution)/shard_map/ppermute | solution.py:126
  206.4 3.9 %collective-permute-start.16 = (f32[41,128]{1,0:T(8,128)S(1)}, f32[41,128]{1,0:T(8,128)S(1)}, u32[]{:S(2)}, u32[]{:S(2)}) collective-permute-start(f32[41,128]{1,0:T(8,128)S(1)} %pad_maximum_fusion.7), channel_id=1, source_target_pairs={{0,8},{4,12},{8,0},{12,4},{16,24},{20,28},{24,16},{28,20},{1,9},{5... | collective-permute-start | bytes 62984 | tf_op jit(solution)/shard_map/ppermute | solution.py:126
  210.3 4.8 %collective-permute-start.17 = (f32[49,128]{1,0:T(8,128)S(1)}, f32[49,128]{1,0:T(8,128)S(1)}, u32[]{:S(2)}, u32[]{:S(2)}) collective-permute-start(f32[49,128]{1,0:T(8,128)S(1)} %pad_maximum_fusion.5), channel_id=1, source_target_pairs={{0,16},{4,20},{8,24},{12,28},{16,0},{20,4},{24,8},{28,12},{1,17},{... | collective-permute-start | bytes 75272 | tf_op jit(solution)/shard_map/ppermute | solution.py:126

commit v12 on v10

--- a/solution.py
+++ b/solution.py
@@ -94,6 +94,49 @@
         )
 
     return lax.cond(owned, compute_pair, skip_pair)
+
+
+def early_pass(owned, left_unit, right_unit, near_weights, near_is_right):
+    block_rows = left_unit.shape[0]
+    vector_count = near_weights.shape[1]
+
+    def compute_pair():
+        affinity = scores_tile(left_unit, right_unit)
+        if near_is_right:
+            part = row_product(affinity, near_weights)
+        else:
+            part = col_product(affinity, near_weights)
+        return (
+            affinity,
+            part,
+            jnp.sum(affinity, axis=1, dtype=jnp.float32),
+            jnp.sum(affinity, axis=0, dtype=jnp.float32),
+        )
+
+    def skip_pair():
+        zero_sum = jnp.zeros((block_rows,), jnp.float32)
+        return (
+            jnp.zeros((block_rows, block_rows), jnp.bfloat16),
+            jnp.zeros((block_rows, vector_count), jnp.float32),
+            zero_sum,
+            zero_sum,
+        )
+
+    return lax.cond(owned, compute_pair, skip_pair)
+
+
+def deferred_pass(owned, affinity, far_weights, far_is_right):
+    block_rows = affinity.shape[0]
+    vector_count = far_weights.shape[1]
+
+    def compute_pair():
+        if far_is_right:
+            return row_product(affinity, far_weights)
+        return col_product(affinity, far_weights)
+
+    return lax.cond(
+        owned, compute_pair, lambda: jnp.zeros((block_rows, vector_count), jnp.float32)
+    )
 
 
 def later_pass(owned, affinity, left_weights, right_weights):
@@ -251,12 +294,46 @@
     zero_sum = jnp.zeros((block_rows,), jnp.float32)
     parts = {offset: zero_part for offset in units}
     sums = {offset: zero_sum for offset in units}
-    tiles = []
-    for (left, right), owned in zip(pair_plan, owned_list):
+    early = fetch_offsets[-1]
+    early_ids = [i for i, pair in enumerate(pair_plan) if set(pair) <= {0, early}]
+    tiles = [None] * len(pair_plan)
+    early_results = []
+    for i in early_ids:
+        left, right = pair_plan[i]
+        near_is_right = right == 0
+        near_weights = weights[0]
+        early_results.append(
+            early_pass(owned_list[i], units[left], units[right], near_weights, near_is_right)
+        )
+    if early_ids:
+        late_offsets = [offset for offset in fetch_offsets if offset != early]
+        late_units, late_weights, early_results = lax.optimization_barrier(
+            ([units[o] for o in late_offsets], [weights[o] for o in late_offsets], early_results)
+        )
+        for position, offset in enumerate(late_offsets):
+            units[offset] = late_units[position]
+            weights[offset] = late_weights[position]
+    for i, (affinity, part, row_sum, col_sum) in zip(early_ids, early_results):
+        left, right = pair_plan[i]
+        near_is_right = right == 0
+        tiles[i] = affinity
+        far = left if near_is_right else right
+        far_part = deferred_pass(owned_list[i], affinity, weights[far], not near_is_right)
+        if near_is_right:
+            row_part, col_part = part, far_part
+        else:
+            row_part, col_part = far_part, part
+        parts[left] = parts[left] + row_part
+        sums[left] = sums[left] + row_sum
+        parts[right] = parts[right] + col_part
+        sums[right] = sums[right] + col_sum
+    for i, ((left, right), owned) in enumerate(zip(pair_plan, owned_list)):
+        if i in early_ids:
+            continue
         affinity, row_part, row_sum, col_part, col_sum = first_pass(
             owned, units[left], units[right], weights[left], weights[right]
         )
-        tiles.append(affinity)
+        tiles[i] = affinity
         parts[left] = parts[left] + row_part
         sums[left] = sums[left] + row_sum
         parts[right] = parts[right] + col_part

time: 224 us -> 219 us (0.978); the launches traced: 221 us -> 219 us
  matrix products: 13.4 us -> 41.5 us
  starting transfers between devices: 58 us -> 36.8 us
  waiting for transfers between devices: 98.3 us -> 92.6 us
  local copies, waits for them, and re-layouts: 13.2 us -> 9.59 us
    ppermute x10, starting transfers between devices: 48.9 us -> 24.5 us  [shifted(): return lax.ppermute(block, axis, route)]
    dot_general x1 -> x3, matrix products: 4.46 us -> 14.9 us  [scores_tile(): lax.dot_general(leftside_block, right_block, (((1,), (1,)), ((), ())), pr...]
    dot_general x2 -> x6, matrix products: 2.12 us -> 11.5 us  [row_product(): return jnp.dot(affinity, weights, preferred_element_type=jnp.float32)]
    dot_general x0 -> x4, matrix products: none -> 8.36 us  [col_product(): lax.dot_general(affinity, weights, (((0,), (0,)), ((), ())), preferred_el...]
    another operation x21 -> x7, local copies, waits for them, and re-layouts: 5.71 us -> 1.64 us
    ppermute x10, starting transfers between devices: 9.11 us -> 12.3 us  [butterfly(): other = lax.ppermute(block, axis, route)]
    ppermute x10, waiting for transfers between devices: 70.4 us -> 67.4 us  [shifted(): return lax.ppermute(block, axis, route)]
    ppermute x10, waiting for transfers between devices: 27.9 us -> 25.2 us  [butterfly(): other = lax.ppermute(block, axis, route)]
  transfers between devices with their start and end apart: 20 -> 20, of which waited for: 16 -> 16; matrix products, arithmetic and copies ran while one was open for 11% -> 14% of each run, Pallas kernels for 4% -> 4%
where the time goes in v12:
time: 219 us
  waiting for transfers between devices  92.6 us (42%)
  matrix products  41.5 us (19%)
  starting transfers between devices  36.8 us (17%)
  other arithmetic  18.4 us (8%)
  Pallas kernels  16.8 us (8%)
  local copies, waits for them, and re-layouts  9.59 us (4%)
  between operations  3.18 us (1%)
    ppermute x10, waiting for transfers between devices, shifted(): return lax.ppermute(block, axis, route)  67.4 us
    ppermute x10, waiting for transfers between devices, butterfly(): other = lax.ppermute(block, axis, route)  25.2 us
    ppermute x10, starting transfers between devices, shifted(): return lax.ppermute(block, axis, route)  24.5 us
    pallas_call x2, Pallas kernels, factor_inverse(): pl.pallas_call(factor_kernel, out_shape=jax.ShapeDtypeStruct(gram_matrix....  16.8 us
    dot_general x3, matrix products, scores_tile(): lax.dot_general(leftside_block, right_block, (((1,), (1,)), ((), ())), pr...  14.9 us
    ppermute x10, starting transfers between devices, butterfly(): other = lax.ppermute(block, axis, route)  12.3 us
    dot_general x6, matrix products, row_product(): return jnp.dot(affinity, weights, preferred_element_type=jnp.float32)  11.5 us
    dot_general x4, matrix products, col_product(): lax.dot_general(affinity, weights, (((0,), (0,)), ((), ())), preferred_el...  8.36 us
  transfers between devices with their start and end apart: 20, of which 16 were waited for; matrix products, arithmetic and copies ran while one was open for 14% of the time, Pallas kernels for 4%

profile of v12, /device:TPU:0, one launch (start us, length us, event | category | flops | bytes accessed | tf_op | source)
XLA Modules:
  0.0 219.2 jit_solution(11813137567584482755)
XLA Ops:
  0.6 3.1 %collective-permute-start.2 = (bf16[1024,768]{1,0:T(8,128)(2,1)}, bf16[1024,768]{1,0:T(8,128)(2,1)}, u32[]{:S(2)}, u32[]{:S(2)}) collective-permute-start(bf16[1024,768]{1,0:T(8,128)(2,1)} %param.17), channel_id=1, source_target_pairs={{24,0},{28,4},{0,8},{4,12},{8,16},{12,20},{16,24},{20,28},{25,1},{... | collective-permute-start | bytes 4718600 | tf_op jit(solution)/shard_map/ppermute | solution.py:20
  3.7 1.8 fusion.1
  5.6 1.6 fusion.3
  7.1 3.3 %collective-permute-start = (bf16[1024,768]{1,0:T(8,128)(2,1)}, bf16[1024,768]{1,0:T(8,128)(2,1)}, u32[]{:S(2)}, u32[]{:S(2)}) collective-permute-start(bf16[1024,768]{1,0:T(8,128)(2,1)} %fusion.3), channel_id=1, source_target_pairs={{4,0},{8,4},{12,8},{16,12},{20,16},{24,20},{28,24},{0,28},{5,1},{9... | collective-permute-start | bytes 4718600 | tf_op jit(solution)/shard_map/ppermute | solution.py:20
  11.0 0.8 fusion.37
  13.7 4.5 %convert_reduce_fusion.6 = (f32[1024]{0:T(1024)}, bf16[1024,1024]{0,1:T(8,128)(2,1)S(1)}) fusion(bf16[1024,768]{1,0:T(8,128)(2,1)} %fusion.3), kind=kOutput, calls=%fused_computation.9 | convolution fusion | flops 1616903168 | bytes 3674112 | tf_op jit(solution)/shard_map/dot_general | solution.py:55
  18.2 23.2 %collective-permute-done.2 = bf16[1024,768]{1,0:T(8,128)(2,1)} collective-permute-done((bf16[1024,768]{1,0:T(8,128)(2,1)}, bf16[1024,768]{1,0:T(8,128)(2,1)}, u32[]{:S(2)}, u32[]{:S(2)}) %collective-permute-start.2) | collective-permute-done | bytes 1572896 | tf_op jit(solution)/shard_map/ppermute | solution.py:20
  41.3 1.8 fusion.4
  43.1 3.0 %fusion.6 = bf16[1024,768]{1,0:T(8,128)(2,1)} fusion(bf16[1024,768]{1,0:T(8,128)(2,1)} %collective-permute-done.2, f32[1024]{0:T(1024)S(1)} %add_rsqrt_fusion), kind=kLoop, calls=%fused_computation.23 | loop fusion | flops 3145728 | bytes 3149824 | tf_op jit(solution)/shard_map/convert_element_type | solution.py:51
  46.1 7.6 %conditional.7 = (bf16[1024,1024]{1,0:T(8,128)(2,1)}, f32[1024,64]{0,1:T(8,128)S(1)}, f32[1024]{0:T(1024)S(1)}, f32[1024]{0:T(1024)S(1)}) conditional(s32[]{:T(128)} %convert_element_type.61, () %tuple.64, (bf16[1024,768]{1,0:T(8,128)(2,1)}, bf16[1024,768]{1,0:T(8,128)(2,1)}, bf16[1024,64]{0,1:T(8,128)(2,1)S(1)}) %tuple.120), branch_computations={%region_3.4_spmd, %region_4.0_spmd} | conditional | flops 1750071296 | bytes 7741472 | solution.py:125
  46.1 5.2 %convert_reduce_fusion = (f32[1024]{0:T(1024)S(1)}, f32[1024]{0:T(1024)S(1)}, bf16[1024,1024]{1,0:T(8,128)(2,1)}) fusion(bf16[1024,768]{1,0:T(8,128)(2,1)} %get-tuple-element.44, bf16[1024,768]{1,0:T(8,128)(2,1)} %get-tuple-element.48), kind=kOutput, calls=%fused_computation | convolution fusion | flops 1615853568 | bytes 5251072 | tf_op jit(solution)/shard_map/cond/branch_1_fun/dot_general | solution.py:55
  51.3 2.3 %fusion.53 = f32[1024,64]{0,1:T(8,128)S(1)} fusion(bf16[1024,1024]{1,0:T(8,128)(2,1)} %get-tuple-element.188, bf16[1024,64]{0,1:T(8,128)(2,1)S(1)} %get-tuple-element.141), kind=kOutput, calls=%fused_computation.134 | convolution fusion | flops 134217728 | bytes 2490368 | tf_op jit(solution)/shard_map/cond/branch_1_fun/dot_general | solution.py:62
  53.7 24.4 %collective-permute-done.1 = bf16[1024,64]{1,0:T(8,128)(2,1)S(1)} collective-permute-done((bf16[1024,64]{1,0:T(8,128)(2,1)S(1)}, bf16[1024,64]{1,0:T(8,128)(2,1)S(1)}, u32[]{:S(2)}, u32[]{:S(2)}) %collective-permute-start.1) | collective-permute-done | bytes 131104 | tf_op jit(solution)/shard_map/ppermute | solution.py:20
  78.1 7.2 %collective-permute-done.3 = bf16[1024,64]{1,0:T(8,128)(2,1)S(1)} collective-permute-done((bf16[1024,64]{1,0:T(8,128)(2,1)S(1)}, bf16[1024,64]{1,0:T(8,128)(2,1)S(1)}, u32[]{:S(2)}, u32[]{:S(2)}) %collective-permute-start.3) | collective-permute-done | bytes 131104 | tf_op jit(solution)/shard_map/ppermute | solution.py:20
  85.3 9.7 %conditional.10 = (bf16[1024,1024]{1,0:T(8,128)(2,1)}, f32[1024,64]{0,1:T(8,128)S(1)}, f32[1024]{0:T(1024)S(1)}, f32[1024,64]{0,1:T(8,128)S(1)}, f32[1024]{0:T(1024)S(1)}) conditional(s32[]{:T(128)} %convert_element_type.65, () %tuple.70, (bf16[1024,768]{1,0:T(8,128)(2,1)}, bf16[1024,768]{1,0:T(8,128)(2,1)}, bf16[1024,64]{1,0:T(8,128)(2,1)S(1)}, ...), branch_computations={%region_15.16_spmd, %region_16.19_spmd} | conditional | flops 1884289024 | bytes 10231848 | solution.py:96
  85.3 5.2 %convert_reduce_fusion.4 = (f32[1024]{0:T(1024)S(1)}, f32[1024]{0:T(1024)S(1)}, bf16[1024,1024]{1,0:T(8,128)(2,1)}) fusion(bf16[1024,768]{1,0:T(8,128)(2,1)} %get-tuple-element.56, bf16[1024,768]{1,0:T(8,128)(2,1)} %get-tuple-element.57), kind=kOutput, calls=%fused_computation.6 | convolution fusion | flops 1615853568 | bytes 5251072 | tf_op jit(solution)/shard_map/cond/branch_1_fun/dot_general | solution.py:55
  90.5 2.3 %fusion.56 = f32[1024,64]{0,1:T(8,128)S(1)} fusion(bf16[1024,1024]{1,0:T(8,128)(2,1)} %get-tuple-element.197, bf16[1024,64]{1,0:T(8,128)(2,1)S(1)} %get-tuple-element.58), kind=kOutput, calls=%fused_computation.137 | convolution fusion | flops 134217728 | bytes 2490368 | tf_op jit(solution)/shard_map/cond/branch_1_fun/dot_general | solution.py:62
  92.9 2.1 fusion.57
  95.7 1.0 add.204
  97.8 10.4 %collective-permute-start.5 = (f32[520,128]{1,0:T(8,128)}, f32[520,128]{1,0:T(8,128)}, u32[]{:S(2)}, u32[]{:S(2)}) collective-permute-start(f32[520,128]{1,0:T(8,128)} %pad_maximum_fusion.1), channel_id=1, source_target_pairs={{8,0},{12,4},{16,8},{20,12},{24,16},{28,20},{0,24},{4,28},{9,1},{1... | collective-permute-start | bytes 798728 | tf_op jit(solution)/shard_map/ppermute | solution.py:20
  108.2 1.6 conditional.9
  108.2 1.6 broadcast.113
  111.5 2.3 %conditional.8 = (f32[1024,64]{0,1:T(8,128)S(1)}) conditional(s32[]{:T(128)} %convert_element_type.61, () %tuple.63, (bf16[1024,1024]{1,0:T(8,128)(2,1)}, bf16[1024,64]{1,0:T(8,128)(2,1)S(1)}) %tuple.67), branch_computations={%region_7.8_spmd, %region_8.9_spmd} | conditional | flops 134217728 | bytes 2490376 | solution.py:137
  111.7 2.1 fusion.46
  114.5 1.0 slice.164
  115.9 4.4 %collective-permute-done.4 = f32[520,128]{1,0:T(8,128)} collective-permute-done((f32[520,128]{1,0:T(8,128)S(1)}, f32[520,128]{1,0:T(8,128)}, u32[]{:S(2)}, u32[]{:S(2)}) %collective-permute-start.4) | collective-permute-done | bytes 266272 | tf_op jit(solution)/shard_map/ppermute | solution.py:20
  120.2 1.0 slice.163
  121.5 1.2 fusion.43
  122.8 1.3 broadcast_multiply_fusion
  126.5 1.2 collective-permute-done.8
  127.8 3.7 %collective-permute-done.9 = f32[35,128]{1,0:T(8,128)S(1)} collective-permute-done((f32[35,128]{1,0:T(8,128)S(1)}, f32[35,128]{1,0:T(8,128)S(1)}, u32[]{:S(2)}, u32[]{:S(2)}) %collective-permute-start.9) | collective-permute-done | bytes 17952 | tf_op jit(solution)/shard_map/ppermute | solution.py:169
  131.6 1.8 collective-permute-start.10
  133.4 2.1 collective-permute-done.10
  135.5 2.9 %collective-permute-start.11 = (f32[41,128]{1,0:T(8,128)S(1)}, f32[41,128]{1,0:T(8,128)S(1)}, u32[]{:S(2)}, u32[]{:S(2)}) collective-permute-start(f32[41,128]{1,0:T(8,128)S(1)} %pad_maximum_fusion.4), channel_id=1, source_target_pairs={{0,8},{4,12},{8,0},{12,4},{16,24},{20,28},{24,16},{28,20},{1,9},{5... | collective-permute-start | bytes 62984 | tf_op jit(solution)/shard_map/ppermute | solution.py:169
  138.4 1.8 collective-permute-done.11
  140.3 4.7 %collective-permute-start.12 = (f32[49,128]{1,0:T(8,128)S(1)}, f32[49,128]{1,0:T(8,128)S(1)}, u32[]{:S(2)}, u32[]{:S(2)}) collective-permute-start(f32[49,128]{1,0:T(8,128)S(1)} %pad_maximum_fusion.2), channel_id=1, source_target_pairs={{0,16},{4,20},{8,24},{12,28},{16,0},{20,4},{24,8},{28,12},{1,17},{... | collective-permute-start | bytes 75272 | tf_op jit(solution)/shard_map/ppermute | solution.py:169
  144.9 2.0 collective-permute-start.7
  146.9 1.1 collective-permute-start.6
  148.0 1.6 collective-permute-done.12
  151.3 0.9 fusion.12.gram_ref
  152.2 8.4 %shard_map.50 = f32[64,64]{1,0:T(8,128)} custom-call(f32[64,64]{1,0:T(8,128)} %fusion.12.gram_ref), custom_call_target="tpu_custom_call" | custom-call | tf_op jit(solution)/shard_map/pallas_call | solution.py:217
  160.6 1.7 convolution_convert_fusion
  163.1 4.4 %conditional.12 = (f32[1024,64]{0,1:T(8,128)S(1)}, f32[1024,64]{0,1:T(8,128)S(1)}) conditional(s32[]{:T(128)} %convert_element_type.61, () %tuple.74, (bf16[1024,1024]{1,0:T(8,128)(2,1)}, bf16[1024,64]{0,1:T(8,128)(2,1)S(1)}, bf16[1024,64]{0,1:T(8,128)(2,1)S(1)}) %tuple.75), branch_computations={%region_26.27_spmd, %region_27.28_spmd} | conditional | flops 268435456 | bytes 4980752 | solution.py:153
  163.1 2.3 %fusion.49 = f32[1024,64]{0,1:T(8,128)S(1)} fusion(bf16[1024,1024]{1,0:T(8,128)(2,1)} %get-tuple-element.63, bf16[1024,64]{0,1:T(8,128)(2,1)S(1)} %get-tuple-element.150), kind=kOutput, calls=%fused_computation.130 | convolution fusion | flops 134217728 | bytes 2490368 | tf_op jit(solution)/shard_map/cond/branch_1_fun/dot_general | solution.py:62
  165.5 2.1 fusion.50
  167.5 4.4 %conditional.13 = (f32[1024,64]{0,1:T(8,128)S(1)}, f32[1024,64]{0,1:T(8,128)S(1)}) conditional(s32[]{:T(128)} %convert_element_type.65, () %tuple.76, (bf16[1024,1024]{1,0:T(8,128)(2,1)}, bf16[1024,64]{0,1:T(8,128)(2,1)S(1)}, bf16[1024,64]{0,1:T(8,128)(2,1)S(1)}) %tuple.77), branch_computations={%region_28.29_spmd, %region_29.30_spmd} | conditional | flops 268435456 | bytes 4980752 | solution.py:153
  167.6 2.3 %fusion.51 = f32[1024,64]{0,1:T(8,128)S(1)} fusion(bf16[1024,1024]{1,0:T(8,128)(2,1)} %get-tuple-element.66, bf16[1024,64]{0,1:T(8,128)(2,1)S(1)} %get-tuple-element.153), kind=kOutput, calls=%fused_computation.132 | convolution fusion | flops 134217728 | bytes 2490368 | tf_op jit(solution)/shard_map/cond/branch_1_fun/dot_general | solution.py:62
  169.9 2.1 fusion.52
  172.7 3.4 %collective-permute-start.14 = (f32[1024,64]{0,1:T(8,128)}, f32[1024,64]{0,1:T(8,128)}, u32[]{:S(2)}, u32[]{:S(2)}) collective-permute-start(f32[1024,64]{0,1:T(8,128)} %add.228), channel_id=1, source_target_pairs={{8,0},{12,4},{16,8},{20,12},{24,16},{28,20},{0,24},{4,28},{9,1},{1... | collective-permute-start | bytes 786440 | tf_op jit(solution)/shard_map/ppermute | solution.py:20
  176.2 0.9 collective-permute-start.13
  177.1 3.2 %collective-permute-done.14 = f32[1024,64]{0,1:T(8,128)} collective-permute-done((f32[1024,64]{0,1:T(8,128)}, f32[1024,64]{0,1:T(8,128)}, u32[]{:S(2)}, u32[]{:S(2)}) %collective-permute-start.14) | collective-permute-done | bytes 262176 | tf_op jit(solution)/shard_map/ppermute | solution.py:20
  180.3 5.0 %collective-permute-done.13 = f32[1024,64]{0,1:T(8,128)S(1)} collective-permute-done((f32[1024,64]{0,1:T(8,128)S(1)}, f32[1024,64]{0,1:T(8,128)S(1)}, u32[]{:S(2)}, u32[]{:S(2)}) %collective-permute-start.13) | collective-permute-done | bytes 262176 | tf_op jit(solution)/shard_map/ppermute | solution.py:20
  185.3 1.7 fusion.40
  187.6 0.8 pad_maximum_fusion.13
  188.6 1.2 collective-permute-done.15
  190.1 3.6 %collective-permute-done.16 = f32[35,128]{1,0:T(8,128)S(1)} collective-permute-done((f32[35,128]{1,0:T(8,128)S(1)}, f32[35,128]{1,0:T(8,128)S(1)}, u32[]{:S(2)}, u32[]{:S(2)}) %collective-permute-start.16) | collective-permute-done | bytes 17952 | tf_op jit(solution)/shard_map/ppermute | solution.py:169
  193.8 3.8 %collective-permute-done.17 = f32[37,128]{1,0:T(8,128)S(1)} collective-permute-done((f32[37,128]{1,0:T(8,128)S(1)}, f32[37,128]{1,0:T(8,128)S(1)}, u32[]{:S(2)}, u32[]{:S(2)}) %collective-permute-start.17) | collective-permute-done | bytes 18976 | tf_op jit(solution)/shard_map/ppermute | solution.py:169
  197.6 1.3 collective-permute-start.18
  198.9 2.6 %collective-permute-done.18 = f32[41,128]{1,0:T(8,128)S(1)} collective-permute-done((f32[41,128]{1,0:T(8,128)S(1)}, f32[41,128]{1,0:T(8,128)S(1)}, u32[]{:S(2)}, u32[]{:S(2)}) %collective-permute-start.18) | collective-permute-done | bytes 21024 | tf_op jit(solution)/shard_map/ppermute | solution.py:169
  201.5 1.2 collective-permute-start.19
  202.7 3.7 %collective-permute-done.19 = f32[49,128]{1,0:T(8,128)S(1)} collective-permute-done((f32[49,128]{1,0:T(8,128)S(1)}, f32[49,128]{1,0:T(8,128)S(1)}, u32[]{:S(2)}, u32[]{:S(2)}) %collective-permute-start.19) | collective-permute-done | bytes 25120 | tf_op jit(solution)/shard_map/ppermute | solution.py:169
  208.0 0.9 fusion.10.gram_ref
  208.9 8.4 %shard_map.51 = f32[64,64]{1,0:T(8,128)} custom-call(f32[64,64]{1,0:T(8,128)} %fusion.10.gram_ref), custom_call_target="tpu_custom_call" | custom-call | tf_op jit(solution)/shard_map/pallas_call | solution.py:217
  217.3 1.9 fusion.18
  (125 shorter events, 14.1 us)
Async XLA Ops:
  0.6 4.9 %copy-start = (bf16[1024,768]{1,0:T(8,128)(2,1)S(1)}, bf16[1024,768]{1,0:T(8,128)(2,1)}, u32[]{:S(2)}) copy-start(bf16[1024,768]{1,0:T(8,128)(2,1)} %param.17) | copy-start | bytes 4718596
  0.6 9.8 %copy-start.1 = (bf16[1024,64]{0,1:T(8,128)(2,1)S(1)}, bf16[1024,64]{0,1:T(8,128)(2,1)}, u32[]{:S(2)}) copy-start(bf16[1024,64]{0,1:T(8,128)(2,1)} %param.18) | copy-start | bytes 393220
  0.6 40.7 %collective-permute-start.2 = (bf16[1024,768]{1,0:T(8,128)(2,1)}, bf16[1024,768]{1,0:T(8,128)(2,1)}, u32[]{:S(2)}, u32[]{:S(2)}) collective-permute-start(bf16[1024,768]{1,0:T(8,128)(2,1)} %param.17), channel_id=1, source_target_pairs={{24,0},{28,4},{0,8},{4,12},{8,16},{12,20},{16,24},{20,28},{25,1},{... | collective-permute-start | bytes 4718600 | tf_op jit(solution)/shard_map/ppermute | solution.py:20
  5.5 5.4 %copy-start.8 = (s32[32,3]{0,1:T(4,128)S(1)}, s32[32,3]{0,1:T(4,128)}, u32[]{:S(2)}) copy-start(s32[32,3]{0,1:T(4,128)} %param.19) | copy-start | bytes 1156
  7.1 71.0 %collective-permute-start = (bf16[1024,768]{1,0:T(8,128)(2,1)}, bf16[1024,768]{1,0:T(8,128)(2,1)}, u32[]{:S(2)}, u32[]{:S(2)}) collective-permute-start(bf16[1024,768]{1,0:T(8,128)(2,1)} %fusion.3), channel_id=1, source_target_pairs={{4,0},{8,4},{12,8},{16,12},{20,16},{24,20},{28,24},{0,28},{5,1},{9... | collective-permute-start | bytes 4718600 | tf_op jit(solution)/shard_map/ppermute | solution.py:20
  10.6 67.5 %collective-permute-start.1 = (bf16[1024,64]{1,0:T(8,128)(2,1)S(1)}, bf16[1024,64]{1,0:T(8,128)(2,1)S(1)}, u32[]{:S(2)}, u32[]{:S(2)}) collective-permute-start(bf16[1024,64]{1,0:T(8,128)(2,1)S(1)} %copy.17), channel_id=1, source_target_pairs={{4,0},{8,4},{12,8},{16,12},{20,16},{24,20},{28,24},{0,28},{5,1},{9... | collective-permute-start | bytes 393224 | tf_op jit(solution)/shard_map/ppermute | solution.py:20
  11.0 74.4 %collective-permute-start.3 = (bf16[1024,64]{1,0:T(8,128)(2,1)S(1)}, bf16[1024,64]{1,0:T(8,128)(2,1)S(1)}, u32[]{:S(2)}, u32[]{:S(2)}) collective-permute-start(bf16[1024,64]{1,0:T(8,128)(2,1)S(1)} %copy.17), channel_id=1, source_target_pairs={{24,0},{28,4},{0,8},{4,12},{8,16},{12,20},{16,24},{20,28},{25,1},{... | collective-permute-start | bytes 393224 | tf_op jit(solution)/shard_map/ppermute | solution.py:20
  53.7 31.7 %copy-start.4 = (f32[1024,64]{0,1:T(8,128)}, f32[1024,64]{0,1:T(8,128)S(1)}, u32[]{:S(2)}) copy-start(f32[1024,64]{0,1:T(8,128)S(1)} %get-tuple-element.109) | copy-start | bytes 786436
  95.0 0.7 copy-start.2
  97.8 12.7 %copy-start.3 = (f32[1024,64]{0,1:T(8,128)S(1)}, f32[1024,64]{0,1:T(8,128)}, u32[]{:S(2)}) copy-start(f32[1024,64]{0,1:T(8,128)} %copy-done.2) | copy-start | bytes 786436
  97.8 16.0 %collective-permute-start.5 = (f32[520,128]{1,0:T(8,128)}, f32[520,128]{1,0:T(8,128)}, u32[]{:S(2)}, u32[]{:S(2)}) collective-permute-start(f32[520,128]{1,0:T(8,128)} %pad_maximum_fusion.1), channel_id=1, source_target_pairs={{8,0},{12,4},{16,8},{20,12},{24,16},{28,20},{0,24},{4,28},{9,1},{1... | collective-permute-start | bytes 798728 | tf_op jit(solution)/shard_map/ppermute | solution.py:20
  109.8 0.7 copy-start.5
  111.0 9.3 %collective-permute-start.4 = (f32[520,128]{1,0:T(8,128)S(1)}, f32[520,128]{1,0:T(8,128)}, u32[]{:S(2)}, u32[]{:S(2)}) collective-permute-start(f32[520,128]{1,0:T(8,128)S(1)} %pad_maximum_fusion), channel_id=1, source_target_pairs={{28,0},{0,4},{4,8},{8,12},{12,16},{16,20},{20,24},{24,28},{29,1},{... | collective-permute-start | bytes 798728 | tf_op jit(solution)/shard_map/ppermute | solution.py:20
  113.8 0.7 copy-start.6
  115.7 7.1 %copy-start.9 = (f32[1024]{0:T(1024)S(1)}, f32[1024]{0:T(1024)}, u32[]{:S(2)}) copy-start(f32[1024]{0:T(1024)} %get-tuple-element.178) | copy-start | bytes 12292
  126.4 1.3 collective-permute-start.8
  127.7 3.8 %collective-permute-start.9 = (f32[35,128]{1,0:T(8,128)S(1)}, f32[35,128]{1,0:T(8,128)S(1)}, u32[]{:S(2)}, u32[]{:S(2)}) collective-permute-start(f32[35,128]{1,0:T(8,128)S(1)} %pad_maximum_fusion.7), channel_id=1, source_target_pairs={{0,2},{1,3},{2,0},{3,1},{4,6},{5,7},{6,4},{7,5},{8,10},{9,11},{10,... | collective-permute-start | bytes 53768 | tf_op jit(solution)/shard_map/ppermute | solution.py:169
  131.6 3.8 %collective-permute-start.10 = (f32[37,128]{1,0:T(8,128)S(1)}, f32[37,128]{1,0:T(8,128)S(1)}, u32[]{:S(2)}, u32[]{:S(2)}) collective-permute-start(f32[37,128]{1,0:T(8,128)S(1)} %pad_maximum_fusion.8), channel_id=1, source_target_pairs={{0,4},{4,0},{8,12},{12,8},{16,20},{20,16},{24,28},{28,24},{1,5},{5... | collective-permute-start | bytes 56840 | tf_op jit(solution)/shard_map/ppermute | solution.py:169
  135.5 4.7 %collective-permute-start.11 = (f32[41,128]{1,0:T(8,128)S(1)}, f32[41,128]{1,0:T(8,128)S(1)}, u32[]{:S(2)}, u32[]{:S(2)}) collective-permute-start(f32[41,128]{1,0:T(8,128)S(1)} %pad_maximum_fusion.4), channel_id=1, source_target_pairs={{0,8},{4,12},{8,0},{12,4},{16,24},{20,28},{24,16},{28,20},{1,9},{5... | collective-permute-start | bytes 62984 | tf_op jit(solution)/shard_map/ppermute | solution.py:169
  140.3 9.4 %collective-permute-start.12 = (f32[49,128]{1,0:T(8,128)S(1)}, f32[49,128]{1,0:T(8,128)S(1)}, u32[]{:S(2)}, u32[]{:S(2)}) collective-permute-start(f32[49,128]{1,0:T(8,128)S(1)} %pad_maximum_fusion.2), channel_id=1, source_target_pairs={{0,16},{4,20},{8,24},{12,28},{16,0},{20,4},{24,8},{28,12},{1,17},{... | collective-permute-start | bytes 75272 | tf_op jit(solution)/shard_map/ppermute | solution.py:169
  144.9 15.7 %collective-permute-start.7 = (f32[1024,64]{0,1:T(8,128)S(1)}, f32[1024,64]{0,1:T(8,128)S(1)}, u32[]{:S(2)}, u32[]{:S(2)}) collective-permute-start(f32[1024,64]{0,1:T(8,128)S(1)} %get-tuple-element.171), channel_id=1, source_target_pairs={{24,0},{28,4},{0,8},{4,12},{8,16},{12,20},{16,24},{20,28},{25,1},{... | collective-permute-start | bytes 786440 | tf_op jit(solution)/shard_map/ppermute | solution.py:20
  146.9 13.7 %collective-permute-start.6 = (f32[1024,64]{0,1:T(8,128)S(1)}, f32[1024,64]{0,1:T(8,128)S(1)}, u32[]{:S(2)}, u32[]{:S(2)}) collective-permute-start(f32[1024,64]{0,1:T(8,128)S(1)} %get-tuple-element.171), channel_id=1, source_target_pairs={{4,0},{8,4},{12,8},{16,12},{20,16},{24,20},{28,24},{0,28},{5,1},{9... | collective-permute-start | bytes 786440 | tf_op jit(solution)/shard_map/ppermute | solution.py:20
  162.3 0.8 copy-start.7
  172.7 7.6 %collective-permute-start.14 = (f32[1024,64]{0,1:T(8,128)}, f32[1024,64]{0,1:T(8,128)}, u32[]{:S(2)}, u32[]{:S(2)}) collective-permute-start(f32[1024,64]{0,1:T(8,128)} %add.228), channel_id=1, source_target_pairs={{8,0},{12,4},{16,8},{20,12},{24,16},{28,20},{0,24},{4,28},{9,1},{1... | collective-permute-start | bytes 786440 | tf_op jit(solution)/shard_map/ppermute | solution.py:20
  176.2 9.1 %collective-permute-start.13 = (f32[1024,64]{0,1:T(8,128)S(1)}, f32[1024,64]{0,1:T(8,128)S(1)}, u32[]{:S(2)}, u32[]{:S(2)}) collective-permute-start(f32[1024,64]{0,1:T(8,128)S(1)} %add.226), channel_id=1, source_target_pairs={{28,0},{0,4},{4,8},{8,12},{12,16},{16,20},{20,24},{24,28},{29,1},{... | collective-permute-start | bytes 786440 | tf_op jit(solution)/shard_map/ppermute | solution.py:20
  188.5 1.2 collective-permute-start.15
  189.8 3.8 %collective-permute-start.16 = (f32[35,128]{1,0:T(8,128)S(1)}, f32[35,128]{1,0:T(8,128)S(1)}, u32[]{:S(2)}, u32[]{:S(2)}) collective-permute-start(f32[35,128]{1,0:T(8,128)S(1)} %pad_maximum_fusion.10), channel_id=1, source_target_pairs={{0,2},{1,3},{2,0},{3,1},{4,6},{5,7},{6,4},{7,5},{8,10},{9,11},{10,... | collective-permute-start | bytes 53768 | tf_op jit(solution)/shard_map/ppermute | solution.py:169
  193.7 3.8 %collective-permute-start.17 = (f32[37,128]{1,0:T(8,128)S(1)}, f32[37,128]{1,0:T(8,128)S(1)}, u32[]{:S(2)}, u32[]{:S(2)}) collective-permute-start(f32[37,128]{1,0:T(8,128)S(1)} %pad_maximum_fusion.11), channel_id=1, source_target_pairs={{0,4},{4,0},{8,12},{12,8},{16,20},{20,16},{24,28},{28,24},{1,5},{5... | collective-permute-start | bytes 56840 | tf_op jit(solution)/shard_map/ppermute | solution.py:169
  197.6 3.9 %collective-permute-start.18 = (f32[41,128]{1,0:T(8,128)S(1)}, f32[41,128]{1,0:T(8,128)S(1)}, u32[]{:S(2)}, u32[]{:S(2)}) collective-permute-start(f32[41,128]{1,0:T(8,128)S(1)} %pad_maximum_fusion.5), channel_id=1, source_target_pairs={{0,8},{4,12},{8,0},{12,4},{16,24},{20,28},{24,16},{28,20},{1,9},{5... | collective-permute-start | bytes 62984 | tf_op jit(solution)/shard_map/ppermute | solution.py:169
  201.5 4.8 %collective-permute-start.19 = (f32[49,128]{1,0:T(8,128)S(1)}, f32[49,128]{1,0:T(8,128)S(1)}, u32[]{:S(2)}, u32[]{:S(2)}) collective-permute-start(f32[49,128]{1,0:T(8,128)S(1)} %pad_maximum_fusion.3), channel_id=1, source_target_pairs={{0,16},{4,20},{8,24},{12,28},{16,0},{20,4},{24,8},{28,12},{1,17},{... | collective-permute-start | bytes 75272 | tf_op jit(solution)/shard_map/ppermute | solution.py:169

commit v13 on v12

--- a/solution.py
+++ b/solution.py
@@ -137,6 +137,33 @@
     return lax.cond(
         owned, compute_pair, lambda: jnp.zeros((block_rows, vector_count), jnp.float32)
     )
+
+
+def column_chunk(owned, left_unit, right_chunk, left_weights, right_weights_chunk):
+    block_rows = left_unit.shape[0]
+    chunk_rows = right_chunk.shape[0]
+    vector_count = left_weights.shape[1]
+
+    def compute_pair():
+        affinity = scores_tile(left_unit, right_chunk)
+        return (
+            affinity,
+            row_product(affinity, right_weights_chunk),
+            jnp.sum(affinity, axis=1, dtype=jnp.float32),
+            col_product(affinity, left_weights),
+            jnp.sum(affinity, axis=0, dtype=jnp.float32),
+        )
+
+    def skip_pair():
+        return (
+            jnp.zeros((block_rows, chunk_rows), jnp.bfloat16),
+            jnp.zeros((block_rows, vector_count), jnp.float32),
+            jnp.zeros((block_rows,), jnp.float32),
+            jnp.zeros((chunk_rows, vector_count), jnp.float32),
+            jnp.zeros((chunk_rows,), jnp.float32),
+        )
+
+    return lax.cond(owned, compute_pair, skip_pair)
 
 
 def later_pass(owned, affinity, left_weights, right_weights):
@@ -276,11 +303,17 @@
     vector_count = start.shape[1]
     units = {0: unit_block}
     weights = {0: start}
+    halves = {}
+    half_rows = block_rows // 2
     for offset in fetch_offsets:
         if offset == fetch_offsets[-1]:
             units[offset] = normalize_rows(shifted(embeddings, "wide", -offset))
         else:
-            units[offset] = shifted(unit_block, "wide", -offset)
+            halves[offset] = [
+                shifted(unit_block[:half_rows], "wide", -offset),
+                shifted(unit_block[half_rows:], "wide", -offset),
+            ]
+            units[offset] = None
         weights[offset] = shifted(start, "wide", -offset)
 
     self_mask = lax.broadcasted_iota(
@@ -305,14 +338,49 @@
         early_results.append(
             early_pass(owned_list[i], units[left], units[right], near_weights, near_is_right)
         )
-    if early_ids:
-        late_offsets = [offset for offset in fetch_offsets if offset != early]
-        late_units, late_weights, early_results = lax.optimization_barrier(
-            ([units[o] for o in late_offsets], [weights[o] for o in late_offsets], early_results)
-        )
+    late_offsets = [offset for offset in fetch_offsets if offset != early]
+    split_ids = [
+        i
+        for i, (left, right) in enumerate(pair_plan)
+        if i not in early_ids and right in halves and left not in halves
+    ]
+    chunk_results = {}
+
+    def run_chunk(i, h):
+        left, right = pair_plan[i]
+        rows = slice(h * half_rows, (h + 1) * half_rows)
+        return column_chunk(
+            owned_list[i], units[left], halves[right][h], weights[left], weights[right][rows]
+        )
+
+    for i in split_ids:
+        chunk_results[(i, 0)] = run_chunk(i, 0)
+    if early_ids or split_ids:
+        late_halves, late_weights, early_results, first_chunks = lax.optimization_barrier(
+            (
+                [halves[o][1] for o in late_offsets if o in halves],
+                [weights[o] for o in late_offsets],
+                early_results,
+                [chunk_results[(i, 0)] for i in split_ids],
+            )
+        )
+        for position, offset in enumerate([o for o in late_offsets if o in halves]):
+            halves[offset][1] = late_halves[position]
         for position, offset in enumerate(late_offsets):
-            units[offset] = late_units[position]
             weights[offset] = late_weights[position]
+        for position, i in enumerate(split_ids):
+            chunk_results[(i, 0)] = first_chunks[position]
+    for offset in halves:
+        units[offset] = jnp.concatenate(halves[offset])
+    for i in split_ids:
+        chunk_results[(i, 1)] = run_chunk(i, 1)
+        left, right = pair_plan[i]
+        first, second = chunk_results[(i, 0)], chunk_results[(i, 1)]
+        tiles[i] = jnp.concatenate([first[0], second[0]], axis=1)
+        parts[left] = parts[left] + first[1] + second[1]
+        sums[left] = sums[left] + first[2] + second[2]
+        parts[right] = parts[right] + jnp.concatenate([first[3], second[3]])
+        sums[right] = sums[right] + jnp.concatenate([first[4], second[4]])
     for i, (affinity, part, row_sum, col_sum) in zip(early_ids, early_results):
         left, right = pair_plan[i]
         near_is_right = right == 0
@@ -328,7 +396,7 @@
         parts[right] = parts[right] + col_part
         sums[right] = sums[right] + col_sum
     for i, ((left, right), owned) in enumerate(zip(pair_plan, owned_list)):
-        if i in early_ids:
+        if i in early_ids or i in split_ids:
             continue
         affinity, row_part, row_sum, col_part, col_sum = first_pass(
             owned, units[left], units[right], weights[left], weights[right]

time: 219 us -> 220 us (level)
  waiting for transfers between devices: 92.6 us -> 80.9 us
  matrix products: 41.5 us -> 30.8 us
  local copies, waits for them, and re-layouts: 9.59 us -> 17.7 us
  starting transfers between devices: 36.8 us -> 44.7 us
  other arithmetic: 18.4 us -> 23.9 us
    ppermute x10 -> x11, waiting for transfers between devices: 67.4 us -> 58.7 us  [shifted(): return lax.ppermute(block, axis, route)]
    ppermute x10 -> x11, starting transfers between devices: 24.5 us -> 31.3 us  [shifted(): return lax.ppermute(block, axis, route)]
    dot_general x4 -> x3, matrix products: 8.36 us -> 3.62 us  [col_product(): lax.dot_general(affinity, weights, (((0,), (0,)), ((), ())), preferred_el...]
    concatenate x0 -> x1, other arithmetic: none -> 4.08 us  [on_device(): tiles[i] = jnp.concatenate([first[0], second[0]], axis=1)]
    another operation x7 -> x18, local copies, waits for them, and re-layouts: 1.64 us -> 5.21 us
    dot_general x3, matrix products: 14.9 us -> 11.9 us  [scores_tile(): lax.dot_general(leftside_block, right_block, (((1,), (1,)), ((), ())), pr...]
    dot_general x6 -> x5, matrix products: 11.5 us -> 8.54 us  [row_product(): return jnp.dot(affinity, weights, preferred_element_type=jnp.float32)]
    ppermute x10, waiting for transfers between devices: 25.2 us -> 22.2 us  [butterfly(): other = lax.ppermute(block, axis, route)]
  transfers between devices with their start and end apart: 20 -> 21, of which waited for: 16 -> 14; matrix products, arithmetic and copies ran while one was open for 14% -> 18% of each run, Pallas kernels for 4% -> 4%
where the time goes in v13:
time: 220 us; the launch traced here: 218 us
  waiting for transfers between devices  80.9 us (37%)
  starting transfers between devices  44.7 us (20%)
  matrix products  30.8 us (14%)
  other arithmetic  23.9 us (11%)
  local copies, waits for them, and re-layouts  17.7 us (8%)
  Pallas kernels  16.8 us (8%)
  between operations  3.11 us (1%)
    ppermute x11, waiting for transfers between devices, shifted(): return lax.ppermute(block, axis, route)  58.7 us
    ppermute x11, starting transfers between devices, shifted(): return lax.ppermute(block, axis, route)  31.3 us
    ppermute x10, waiting for transfers between devices, butterfly(): other = lax.ppermute(block, axis, route)  22.2 us
    pallas_call x2, Pallas kernels, factor_inverse(): pl.pallas_call(factor_kernel, out_shape=jax.ShapeDtypeStruct(gram_matrix....  16.8 us
    ppermute x10, starting transfers between devices, butterfly(): other = lax.ppermute(block, axis, route)  13.4 us
    dot_general x3, matrix products, scores_tile(): lax.dot_general(leftside_block, right_block, (((1,), (1,)), ((), ())), pr...  11.9 us
    dot_general x5, matrix products, row_product(): return jnp.dot(affinity, weights, preferred_element_type=jnp.float32)  8.54 us
    dot_general x8, matrix products, hdot(): jnp.dot(left, right, precision=lax.Precision.HIGHEST, preferred_element_t...  6.78 us
  transfers between devices with their start and end apart: 21, of which 14 were waited for; matrix products, arithmetic and copies ran while one was open for 18% of the time, Pallas kernels for 4%

profile of v13, /device:TPU:0, one launch (start us, length us, event | category | flops | bytes accessed | tf_op | source)
XLA Modules:
  0.0 218.0 jit_solution(787816166527679673)
XLA Ops:
  0.6 3.1 %collective-permute-start.2 = (bf16[1024,768]{1,0:T(8,128)(2,1)}, bf16[1024,768]{1,0:T(8,128)(2,1)}, u32[]{:S(2)}, u32[]{:S(2)}) collective-permute-start(bf16[1024,768]{1,0:T(8,128)(2,1)} %param.21), channel_id=1, source_target_pairs={{24,0},{28,4},{0,8},{4,12},{8,16},{12,20},{16,24},{20,28},{25,1},{... | collective-permute-start | bytes 4718600 | tf_op jit(solution)/shard_map/ppermute | solution.py:20
  3.7 1.8 fusion.1
  6.0 1.1 copy-done.3
  7.1 1.1 fusion.45
  8.2 3.3 %collective-permute-start.3 = (bf16[512,768]{1,0:T(8,128)(2,1)S(1)}, bf16[512,768]{1,0:T(8,128)(2,1)}, u32[]{:S(2)}, u32[]{:S(2)}) collective-permute-start(bf16[512,768]{1,0:T(8,128)(2,1)S(1)} %get-tuple-element.255), channel_id=1, source_target_pairs={{4,0},{8,4},{12,8},{16,12},{20,16},{24,20},{28,24},{0,28},{5,1},{9... | collective-permute-start | bytes 2359304 | tf_op jit(solution)/shard_map/ppermute | solution.py:20
  12.7 5.0 %collective-permute-start = (bf16[512,768]{1,0:T(8,128)(2,1)}, bf16[512,768]{1,0:T(8,128)(2,1)}, u32[]{:S(2)}, u32[]{:S(2)}) collective-permute-start(bf16[512,768]{1,0:T(8,128)(2,1)} %get-tuple-element.256), channel_id=1, source_target_pairs={{4,0},{8,4},{12,8},{16,12},{20,16},{24,20},{28,24},{0,28},{5,1},{9... | collective-permute-start | bytes 2359304 | tf_op jit(solution)/shard_map/ppermute | solution.py:20
  17.7 4.4 %convert_reduce_fusion.10 = (f32[1024]{0:T(1024)}, bf16[1024,1024]{0,1:T(8,128)(2,1)S(1)}) fusion(bf16[1024,768]{1,0:T(8,128)(2,1)} %copy-done.3), kind=kOutput, calls=%fused_computation.15 | convolution fusion | flops 1616903168 | bytes 3674112 | tf_op jit(solution)/shard_map/dot_general | solution.py:55
  22.1 1.0 compare_reduce_fusion
  24.8 36.5 %collective-permute-done.1 = bf16[1024,64]{1,0:T(8,128)(2,1)} collective-permute-done((bf16[1024,64]{1,0:T(8,128)(2,1)}, bf16[1024,64]{1,0:T(8,128)(2,1)}, u32[]{:S(2)}, u32[]{:S(2)}) %collective-permute-start.1) | collective-permute-done | bytes 131104 | tf_op jit(solution)/shard_map/ppermute | solution.py:20
  61.3 0.9 slice.183
  62.3 2.5 %conditional.10 = (bf16[1024,512]{1,0:T(8,128)(2,1)}, f32[1024,64]{0,1:T(8,128)}, f32[1024]{0:T(1024)S(1)}, f32[512,64]{0,1:T(8,128)}, f32[512]{0:T(512)S(1)}) conditional(s32[]{:T(128)} %convert_element_type.80, () %tuple.85, (bf16[1024,768]{1,0:T(8,128)(2,1)}, bf16[512,768]{1,0:T(8,128)(2,1)}, bf16[512,64]{1,0:T(8,128)(2,1)S(1)}, ...), branch_computations={%region_8.9_spmd, %region_9.12_spmd} | conditional | flops 942144000 | bytes 6101032 | solution.py:166
  62.3 1.1 broadcast.148
  64.7 1.9 fusion.4
  66.7 3.0 %fusion.6 = bf16[1024,768]{1,0:T(8,128)(2,1)} fusion(bf16[1024,768]{1,0:T(8,128)(2,1)} %collective-permute-done.2, f32[1024]{0:T(1024)S(1)} %add_rsqrt_fusion), kind=kLoop, calls=%fused_computation.29 | loop fusion | flops 3145728 | bytes 3149824 | tf_op jit(solution)/shard_map/convert_element_type | solution.py:51
  69.7 1.6 conditional.9
  69.7 1.6 broadcast.144
  72.0 6.9 %conditional.11 = (bf16[1024,512]{1,0:T(8,128)(2,1)}, f32[1024,64]{0,1:T(8,128)S(1)}, f32[1024]{0:T(1024)S(1)}, f32[512,64]{0,1:T(8,128)S(1)}, f32[512]{0:T(512)S(1)}) conditional(s32[]{:T(128)} %convert_element_type.81, () %tuple.87, (bf16[1024,768]{1,0:T(8,128)(2,1)}, bf16[512,768]{1,0:T(8,128)(2,1)}, bf16[512,64]{1,0:T(8,128)(2,1)S(1)}, ...), branch_computations={%region_13.14_spmd, %region_14.17_spmd} | conditional | flops 942144000 | bytes 6101032 | solution.py:166
  72.0 3.7 %convert_reduce_fusion.4 = (f32[512]{0:T(512)S(1)}, f32[1024]{0:T(1024)S(1)}, bf16[1024,512]{1,0:T(8,128)(2,1)}) fusion(bf16[1024,768]{1,0:T(8,128)(2,1)} %get-tuple-element.72, bf16[512,768]{1,0:T(8,128)(2,1)} %get-tuple-element.73), kind=kOutput, calls=%fused_computation.6 | convolution fusion | flops 807926272 | bytes 3414016 | tf_op jit(solution)/shard_map/cond/branch_1_fun/dot_general | solution.py:55
  75.7 1.7 fusion.57
  77.4 1.6 fusion.58
  78.9 3.7 %collective-permute-done = bf16[512,768]{1,0:T(8,128)(2,1)} collective-permute-done((bf16[512,768]{1,0:T(8,128)(2,1)}, bf16[512,768]{1,0:T(8,128)(2,1)}, u32[]{:S(2)}, u32[]{:S(2)}) %collective-permute-start) | collective-permute-done | bytes 786464 | tf_op jit(solution)/shard_map/ppermute | solution.py:20
  82.7 0.9 slice.141
  83.6 7.0 %conditional.14 = (bf16[1024,512]{1,0:T(8,128)(2,1)}, f32[1024,64]{0,1:T(8,128)S(1)}, f32[1024]{0:T(1024)S(1)}, f32[512,64]{0,1:T(8,128)S(1)}, f32[4,128]{1,0:T(4,128)S(1)}) conditional(s32[]{:T(128)} %convert_element_type.81, () %tuple.94, (bf16[1024,768]{1,0:T(8,128)(2,1)}, bf16[512,768]{1,0:T(8,128)(2,1)}, bf16[512,64]{1,0:T(8,128)(2,1)S(1)}, ...), branch_computations={%region_23.24_spmd, %region_24.0_spmd} | conditional | flops 942144000 | bytes 6101032 | solution.py:166
  83.6 3.8 %convert_reduce_fusion.8 = (f32[512]{0:T(512)S(1)}, f32[1024]{0:T(1024)S(1)}, bf16[1024,512]{1,0:T(8,128)(2,1)}) fusion(bf16[1024,768]{1,0:T(8,128)(2,1)} %get-tuple-element.82, bf16[512,768]{1,0:T(8,128)(2,1)} %get-tuple-element.83), kind=kOutput, calls=%fused_computation.12 | convolution fusion | flops 807926272 | bytes 3414016 | tf_op jit(solution)/shard_map/cond/branch_1_fun/dot_general | solution.py:55
  87.4 1.7 fusion.61
  89.1 1.6 fusion.62
  91.3 1.0 add_add_fusion
  93.4 11.4 %collective-permute-start.6 = (f32[520,128]{1,0:T(8,128)}, f32[520,128]{1,0:T(8,128)}, u32[]{:S(2)}, u32[]{:S(2)}) collective-permute-start(f32[520,128]{1,0:T(8,128)} %pad_maximum_fusion.3), channel_id=1, source_target_pairs={{8,0},{12,4},{16,8},{20,12},{24,16},{28,20},{0,24},{4,28},{9,1},{1... | collective-permute-start | bytes 798728 | tf_op jit(solution)/shard_map/ppermute | solution.py:20
  104.8 1.1 conditional.12
  104.8 1.0 broadcast.160
  106.4 0.9 maximum_add_fusion
  109.7 1.0 slice.185
  111.0 9.2 %collective-permute-done.5 = f32[520,128]{1,0:T(8,128)} collective-permute-done((f32[520,128]{1,0:T(8,128)}, f32[520,128]{1,0:T(8,128)}, u32[]{:S(2)}, u32[]{:S(2)}) %collective-permute-start.5) | collective-permute-done | bytes 266272 | tf_op jit(solution)/shard_map/ppermute | solution.py:20
  120.2 1.0 slice.184
  121.5 1.1 fusion.43
  122.6 1.3 broadcast_multiply_fusion
  126.3 1.1 collective-permute-start.9
  127.4 0.8 collective-permute-done.9
  128.3 5.0 %collective-permute-start.10 = (f32[35,128]{1,0:T(8,128)S(1)}, f32[35,128]{1,0:T(8,128)S(1)}, u32[]{:S(2)}, u32[]{:S(2)}) collective-permute-start(f32[35,128]{1,0:T(8,128)S(1)} %pad_maximum_fusion.9), channel_id=1, source_target_pairs={{0,2},{1,3},{2,0},{3,1},{4,6},{5,7},{6,4},{7,5},{8,10},{9,11},{10,... | collective-permute-start | bytes 53768 | tf_op jit(solution)/shard_map/ppermute | solution.py:196
  133.3 1.8 collective-permute-done.10
  135.2 3.8 %collective-permute-done.11 = f32[37,128]{1,0:T(8,128)S(1)} collective-permute-done((f32[37,128]{1,0:T(8,128)S(1)}, f32[37,128]{1,0:T(8,128)S(1)}, u32[]{:S(2)}, u32[]{:S(2)}) %collective-permute-start.11) | collective-permute-done | bytes 18976 | tf_op jit(solution)/shard_map/ppermute | solution.py:196
  139.1 3.8 %collective-permute-done.12 = f32[41,128]{1,0:T(8,128)S(1)} collective-permute-done((f32[41,128]{1,0:T(8,128)S(1)}, f32[41,128]{1,0:T(8,128)S(1)}, u32[]{:S(2)}, u32[]{:S(2)}) %collective-permute-start.12) | collective-permute-done | bytes 21024 | tf_op jit(solution)/shard_map/ppermute | solution.py:196
  143.0 4.1 %pad_maximum_fusion = (bf16[1024,1024]{1,0:T(8,128)(2,1)S(1)}, bf16[1024,1024]{1,0:T(8,128)(2,1)}) fusion(bf16[1024,512]{1,0:T(8,128)(2,1)} %get-tuple-element.180, bf16[1024,512]{1,0:T(8,128)(2,1)} %get-tuple-element.179, bf16[1024,512]{1,0:T(8,128)(2,1)} %get-tuple-element.185, bf16[1024,512]{1,0:T(8,128)(2,1)} %get-tuple-element.184), kind=kLoop, calls=%fused_computation.30 | loop fusion | flops 8388608 | bytes 8388608 | tf_op jit(solution)/shard_map/concatenate | solution.py:379
  147.1 3.2 %collective-permute-start.7 = (f32[1024,64]{0,1:T(8,128)S(1)}, f32[1024,64]{0,1:T(8,128)S(1)}, u32[]{:S(2)}, u32[]{:S(2)}) collective-permute-start(f32[1024,64]{0,1:T(8,128)S(1)} %get-tuple-element.249), channel_id=1, source_target_pairs={{4,0},{8,4},{12,8},{16,12},{20,16},{24,20},{28,24},{0,28},{5,1},{9... | collective-permute-start | bytes 786440 | tf_op jit(solution)/shard_map/ppermute | solution.py:20
  152.1 0.9 fusion.12.gram_ref
  152.9 8.4 %shard_map.50 = f32[64,64]{1,0:T(8,128)} custom-call(f32[64,64]{1,0:T(8,128)} %fusion.12.gram_ref), custom_call_target="tpu_custom_call" | custom-call | tf_op jit(solution)/shard_map/pallas_call | solution.py:244
  161.3 1.7 convolution_convert_fusion
  163.9 3.0 %conditional.17 = (f32[1024,64]{0,1:T(8,128)S(1)}, f32[1024,64]{0,1:T(8,128)S(1)}) conditional(s32[]{:T(128)} %convert_element_type.81, () %tuple.100, (bf16[1024,1024]{1,0:T(8,128)(2,1)}, bf16[1024,64]{0,1:T(8,128)(2,1)S(1)}, bf16[1024,64]{0,1:T(8,128)(2,1)S(1)}) %tuple.101), branch_computations={%region_36.37_spmd, %region_37.38_spmd} | conditional | flops 268435456 | bytes 13369388 | solution.py:180
  163.9 2.5 %fusion.52 = f32[1024,64]{0,1:T(8,128)S(1)} fusion(bf16[1024,1024]{1,0:T(8,128)(2,1)} %get-tuple-element.92, bf16[1024,64]{0,1:T(8,128)(2,1)S(1)} %get-tuple-element.227), kind=kOutput, calls=%fused_computation.143 | convolution fusion | flops 134217728 | bytes 2490368 | tf_op jit(solution)/shard_map/cond/branch_1_fun/dot_general | solution.py:62
  167.6 4.9 %collective-permute-start.15 = (f32[1024,64]{0,1:T(8,128)}, f32[1024,64]{0,1:T(8,128)}, u32[]{:S(2)}, u32[]{:S(2)}) collective-permute-start(f32[1024,64]{0,1:T(8,128)} %add.250), channel_id=1, source_target_pairs={{8,0},{12,4},{16,8},{20,12},{24,16},{28,20},{0,24},{4,28},{9,1},{1... | collective-permute-start | bytes 786440 | tf_op jit(solution)/shard_map/ppermute | solution.py:20
  172.7 4.0 %collective-permute-done.15 = f32[1024,64]{0,1:T(8,128)} collective-permute-done((f32[1024,64]{0,1:T(8,128)}, f32[1024,64]{0,1:T(8,128)}, u32[]{:S(2)}, u32[]{:S(2)}) %collective-permute-start.15) | collective-permute-done | bytes 262176 | tf_op jit(solution)/shard_map/ppermute | solution.py:20
  176.8 5.2 %collective-permute-done.14 = f32[1024,64]{0,1:T(8,128)S(1)} collective-permute-done((f32[1024,64]{0,1:T(8,128)S(1)}, f32[1024,64]{0,1:T(8,128)S(1)}, u32[]{:S(2)}, u32[]{:S(2)}) %collective-permute-start.14) | collective-permute-done | bytes 262176 | tf_op jit(solution)/shard_map/ppermute | solution.py:20
  182.0 2.2 %fusion.40 = (f32[64]{0:T(128)S(1)}, f32[1024,64]{0,1:T(8,128)S(1)}) fusion(f32[1024]{0:T(1024)S(1)} %get-tuple-element.245, f32[1024,64]{0,1:T(8,128)} %collective-permute-done.15, f32[1024,64]{0,1:T(8,128)S(1)} %collective-permute-done.14, f32[1024,64]{0,1:T(8,128)S(1)} %get-tuple-element.181, f32[1024,64]{0,1:T(8,128)S(1)} %get-tuple-element.182, ...), kind=kOutput, calls=%fused_computation.132 | convolution fusion | flops 134610880 | bytes 3543296 | tf_op jit(solution)/shard_map/dot_general | solution.py:62
  185.9 1.2 collective-permute-done.16
  187.1 3.2 %collective-permute-start.17 = (f32[35,128]{1,0:T(8,128)S(1)}, f32[35,128]{1,0:T(8,128)S(1)}, u32[]{:S(2)}, u32[]{:S(2)}) collective-permute-start(f32[35,128]{1,0:T(8,128)S(1)} %pad_maximum_fusion.12), channel_id=1, source_target_pairs={{0,2},{1,3},{2,0},{3,1},{4,6},{5,7},{6,4},{7,5},{8,10},{9,11},{10,... | collective-permute-start | bytes 53768 | tf_op jit(solution)/shard_map/ppermute | solution.py:196
  190.4 1.8 collective-permute-done.17
  192.2 1.4 collective-permute-start.18
  193.6 2.4 %collective-permute-done.18 = f32[37,128]{1,0:T(8,128)S(1)} collective-permute-done((f32[37,128]{1,0:T(8,128)S(1)}, f32[37,128]{1,0:T(8,128)S(1)}, u32[]{:S(2)}, u32[]{:S(2)}) %collective-permute-start.18) | collective-permute-done | bytes 18976 | tf_op jit(solution)/shard_map/ppermute | solution.py:196
  196.8 3.1 %collective-permute-done.19 = f32[41,128]{1,0:T(8,128)S(1)} collective-permute-done((f32[41,128]{1,0:T(8,128)S(1)}, f32[41,128]{1,0:T(8,128)S(1)}, u32[]{:S(2)}, u32[]{:S(2)}) %collective-permute-start.19) | collective-permute-done | bytes 21024 | tf_op jit(solution)/shard_map/ppermute | solution.py:196
  200.0 1.5 collective-permute-start.20
  201.5 3.6 %collective-permute-done.20 = f32[49,128]{1,0:T(8,128)S(1)} collective-permute-done((f32[49,128]{1,0:T(8,128)S(1)}, f32[49,128]{1,0:T(8,128)S(1)}, u32[]{:S(2)}, u32[]{:S(2)}) %collective-permute-start.20) | collective-permute-done | bytes 25120 | tf_op jit(solution)/shard_map/ppermute | solution.py:196
  206.8 0.9 fusion.10.gram_ref
  207.7 8.4 %shard_map.51 = f32[64,64]{1,0:T(8,128)} custom-call(f32[64,64]{1,0:T(8,128)} %fusion.10.gram_ref), custom_call_target="tpu_custom_call" | custom-call | tf_op jit(solution)/shard_map/pallas_call | solution.py:244
  216.1 1.9 fusion.18
  (158 shorter events, 19.7 us)
Async XLA Ops:
  0.6 4.9 %copy-start.2 = (bf16[1024,768]{1,0:T(8,128)(2,1)S(1)}, bf16[1024,768]{1,0:T(8,128)(2,1)}, u32[]{:S(2)}) copy-start(bf16[1024,768]{1,0:T(8,128)(2,1)} %param.21) | copy-start | bytes 4718596
  0.6 64.1 %collective-permute-start.2 = (bf16[1024,768]{1,0:T(8,128)(2,1)}, bf16[1024,768]{1,0:T(8,128)(2,1)}, u32[]{:S(2)}, u32[]{:S(2)}) collective-permute-start(bf16[1024,768]{1,0:T(8,128)(2,1)} %param.21), channel_id=1, source_target_pairs={{24,0},{28,4},{0,8},{4,12},{8,16},{12,20},{16,24},{20,28},{25,1},{... | collective-permute-start | bytes 4718600 | tf_op jit(solution)/shard_map/ppermute | solution.py:20
  6.0 1.2 copy-start.3
  7.1 4.4 %copy-start.5 = (bf16[1024,64]{0,1:T(8,128)(2,1)S(1)}, bf16[1024,64]{0,1:T(8,128)(2,1)}, u32[]{:S(2)}) copy-start(bf16[1024,64]{0,1:T(8,128)(2,1)} %param.22) | copy-start | bytes 393220
  8.2 54.0 %collective-permute-start.3 = (bf16[512,768]{1,0:T(8,128)(2,1)S(1)}, bf16[512,768]{1,0:T(8,128)(2,1)}, u32[]{:S(2)}, u32[]{:S(2)}) collective-permute-start(bf16[512,768]{1,0:T(8,128)(2,1)S(1)} %get-tuple-element.255), channel_id=1, source_target_pairs={{4,0},{8,4},{12,8},{16,12},{20,16},{24,20},{28,24},{0,28},{5,1},{9... | collective-permute-start | bytes 2359304 | tf_op jit(solution)/shard_map/ppermute | solution.py:20
  12.4 49.0 %collective-permute-start.1 = (bf16[1024,64]{1,0:T(8,128)(2,1)}, bf16[1024,64]{1,0:T(8,128)(2,1)}, u32[]{:S(2)}, u32[]{:S(2)}) collective-permute-start(bf16[1024,64]{1,0:T(8,128)(2,1)} %copy.18), channel_id=1, source_target_pairs={{4,0},{8,4},{12,8},{16,12},{20,16},{24,20},{28,24},{0,28},{5,1},{9... | collective-permute-start | bytes 393224 | tf_op jit(solution)/shard_map/ppermute | solution.py:20
  12.7 58.7 %collective-permute-start.4 = (bf16[1024,64]{1,0:T(8,128)(2,1)}, bf16[1024,64]{1,0:T(8,128)(2,1)S(1)}, u32[]{:S(2)}, u32[]{:S(2)}) collective-permute-start(bf16[1024,64]{1,0:T(8,128)(2,1)} %copy.18), channel_id=1, source_target_pairs={{24,0},{28,4},{0,8},{4,12},{8,16},{12,20},{16,24},{20,28},{25,1},{... | collective-permute-start | bytes 393224 | tf_op jit(solution)/shard_map/ppermute | solution.py:20
  12.7 9.4 %copy-start.15 = (s32[32,3]{0,1:T(4,128)S(1)}, s32[32,3]{0,1:T(4,128)}, u32[]{:S(2)}) copy-start(s32[32,3]{0,1:T(4,128)} %param.23) | copy-start | bytes 1156
  12.7 70.0 %collective-permute-start = (bf16[512,768]{1,0:T(8,128)(2,1)}, bf16[512,768]{1,0:T(8,128)(2,1)}, u32[]{:S(2)}, u32[]{:S(2)}) collective-permute-start(bf16[512,768]{1,0:T(8,128)(2,1)} %get-tuple-element.256), channel_id=1, source_target_pairs={{4,0},{8,4},{12,8},{16,12},{20,16},{24,20},{28,24},{0,28},{5,1},{9... | collective-permute-start | bytes 2359304 | tf_op jit(solution)/shard_map/ppermute | solution.py:20
  22.1 87.0 %copy-start.1 = (bf16[1024,1024]{0,1:T(8,128)(2,1)}, bf16[1024,1024]{0,1:T(8,128)(2,1)S(1)}, u32[]{:S(2)}) copy-start(bf16[1024,1024]{0,1:T(8,128)(2,1)S(1)} %get-tuple-element.261) | copy-start | bytes 6291460
  64.7 4.9 %copy-start.4 = (bf16[1024,768]{1,0:T(8,128)(2,1)S(1)}, bf16[1024,768]{1,0:T(8,128)(2,1)}, u32[]{:S(2)}) copy-start(bf16[1024,768]{1,0:T(8,128)(2,1)} %copy-done.3) | copy-start | bytes 4718596
  71.3 0.7 copy-start.6
  78.9 4.7 %copy-start.8 = (f32[512,64]{0,1:T(8,128)}, f32[512,64]{0,1:T(8,128)S(1)}, u32[]{:S(2)}) copy-start(f32[512,64]{0,1:T(8,128)S(1)} %get-tuple-element.164) | copy-start | bytes 393220
  78.9 4.7 %copy-start.12 = (f32[512]{0:T(512)}, f32[512]{0:T(512)S(1)}, u32[]{:S(2)}) copy-start(f32[512]{0:T(512)S(1)} %get-tuple-element.168) | copy-start | bytes 6148
  90.7 0.7 copy-start.10
  90.7 14.1 %copy-start.13 = (f32[4,128]{1,0:T(4,128)}, f32[4,128]{1,0:T(4,128)S(1)}, u32[]{:S(2)}) copy-start(f32[4,128]{1,0:T(4,128)S(1)} %get-tuple-element.169) | copy-start | bytes 6148
  93.4 13.0 %copy-start.9 = (f32[512,64]{0,1:T(8,128)S(1)}, f32[512,64]{0,1:T(8,128)}, u32[]{:S(2)}) copy-start(f32[512,64]{0,1:T(8,128)} %copy-done.8) | copy-start | bytes 393220
  93.4 13.0 %copy-start.11 = (f32[512,64]{0,1:T(8,128)S(1)}, f32[512,64]{0,1:T(8,128)}, u32[]{:S(2)}) copy-start(f32[512,64]{0,1:T(8,128)} %copy-done.10) | copy-start | bytes 393220
  93.4 16.3 %collective-permute-start.6 = (f32[520,128]{1,0:T(8,128)}, f32[520,128]{1,0:T(8,128)}, u32[]{:S(2)}, u32[]{:S(2)}) collective-permute-start(f32[520,128]{1,0:T(8,128)} %pad_maximum_fusion.3), channel_id=1, source_target_pairs={{8,0},{12,4},{16,8},{20,12},{24,16},{28,20},{0,24},{4,28},{9,1},{1... | collective-permute-start | bytes 798728 | tf_op jit(solution)/shard_map/ppermute | solution.py:20
  105.9 0.5 copy-start.14
  109.1 11.1 %collective-permute-start.5 = (f32[520,128]{1,0:T(8,128)}, f32[520,128]{1,0:T(8,128)}, u32[]{:S(2)}, u32[]{:S(2)}) collective-permute-start(f32[520,128]{1,0:T(8,128)} %pad_maximum_fusion.2), channel_id=1, source_target_pairs={{28,0},{0,4},{4,8},{8,12},{12,16},{16,20},{20,24},{24,28},{29,1},{... | collective-permute-start | bytes 798728 | tf_op jit(solution)/shard_map/ppermute | solution.py:20
  111.0 11.7 %copy-start.16 = (f32[1024]{0:T(1024)S(1)}, f32[1024]{0:T(1024)}, u32[]{:S(2)}) copy-start(f32[1024]{0:T(1024)} %get-tuple-element.260) | copy-start | bytes 12292
  126.3 2.0 collective-permute-start.9
  128.3 6.8 %collective-permute-start.10 = (f32[35,128]{1,0:T(8,128)S(1)}, f32[35,128]{1,0:T(8,128)S(1)}, u32[]{:S(2)}, u32[]{:S(2)}) collective-permute-start(f32[35,128]{1,0:T(8,128)S(1)} %pad_maximum_fusion.9), channel_id=1, source_target_pairs={{0,2},{1,3},{2,0},{3,1},{4,6},{5,7},{6,4},{7,5},{8,10},{9,11},{10,... | collective-permute-start | bytes 53768 | tf_op jit(solution)/shard_map/ppermute | solution.py:196
  135.1 3.8 %collective-permute-start.11 = (f32[37,128]{1,0:T(8,128)S(1)}, f32[37,128]{1,0:T(8,128)S(1)}, u32[]{:S(2)}, u32[]{:S(2)}) collective-permute-start(f32[37,128]{1,0:T(8,128)S(1)} %pad_maximum_fusion.10), channel_id=1, source_target_pairs={{0,4},{4,0},{8,12},{12,8},{16,20},{20,16},{24,28},{28,24},{1,5},{5... | collective-permute-start | bytes 56840 | tf_op jit(solution)/shard_map/ppermute | solution.py:196
  139.0 3.9 %collective-permute-start.12 = (f32[41,128]{1,0:T(8,128)S(1)}, f32[41,128]{1,0:T(8,128)S(1)}, u32[]{:S(2)}, u32[]{:S(2)}) collective-permute-start(f32[41,128]{1,0:T(8,128)S(1)} %pad_maximum_fusion.6), channel_id=1, source_target_pairs={{0,8},{4,12},{8,0},{12,4},{16,24},{20,28},{24,16},{28,20},{1,9},{5... | collective-permute-start | bytes 62984 | tf_op jit(solution)/shard_map/ppermute | solution.py:196
  142.9 7.4 %collective-permute-start.13 = (f32[49,128]{1,0:T(8,128)S(1)}, f32[49,128]{1,0:T(8,128)S(1)}, u32[]{:S(2)}, u32[]{:S(2)}) collective-permute-start(f32[49,128]{1,0:T(8,128)S(1)} %pad_maximum_fusion.4), channel_id=1, source_target_pairs={{0,16},{4,20},{8,24},{12,28},{16,0},{20,4},{24,8},{28,12},{1,17},{... | collective-permute-start | bytes 75272 | tf_op jit(solution)/shard_map/ppermute | solution.py:196
  147.1 14.2 %collective-permute-start.8 = (f32[1024,64]{0,1:T(8,128)S(1)}, f32[1024,64]{0,1:T(8,128)S(1)}, u32[]{:S(2)}, u32[]{:S(2)}) collective-permute-start(f32[1024,64]{0,1:T(8,128)S(1)} %get-tuple-element.249), channel_id=1, source_target_pairs={{24,0},{28,4},{0,8},{4,12},{8,16},{12,20},{16,24},{20,28},{25,1},{... | collective-permute-start | bytes 786440 | tf_op jit(solution)/shard_map/ppermute | solution.py:20
  147.1 14.2 %collective-permute-start.7 = (f32[1024,64]{0,1:T(8,128)S(1)}, f32[1024,64]{0,1:T(8,128)S(1)}, u32[]{:S(2)}, u32[]{:S(2)}) collective-permute-start(f32[1024,64]{0,1:T(8,128)S(1)} %get-tuple-element.249), channel_id=1, source_target_pairs={{4,0},{8,4},{12,8},{16,12},{20,16},{24,20},{28,24},{0,28},{5,1},{9... | collective-permute-start | bytes 786440 | tf_op jit(solution)/shard_map/ppermute | solution.py:20
  163.1 0.8 copy-start.7
  163.9 2.5 %copy-start = (bf16[1024,1024]{1,0:T(8,128)(2,1)S(1)}, bf16[1024,1024]{1,0:T(8,128)(2,1)}, u32[]{:S(2)}) copy-start(bf16[1024,1024]{1,0:T(8,128)(2,1)} %get-tuple-element.92) | copy-start | bytes 6291460 | tf_op jit(solution)/shard_map/cond
  167.6 9.2 %collective-permute-start.15 = (f32[1024,64]{0,1:T(8,128)}, f32[1024,64]{0,1:T(8,128)}, u32[]{:S(2)}, u32[]{:S(2)}) collective-permute-start(f32[1024,64]{0,1:T(8,128)} %add.250), channel_id=1, source_target_pairs={{8,0},{12,4},{16,8},{20,12},{24,16},{28,20},{0,24},{4,28},{9,1},{1... | collective-permute-start | bytes 786440 | tf_op jit(solution)/shard_map/ppermute | solution.py:20
  172.7 9.3 %collective-permute-start.14 = (f32[1024,64]{0,1:T(8,128)S(1)}, f32[1024,64]{0,1:T(8,128)S(1)}, u32[]{:S(2)}, u32[]{:S(2)}) collective-permute-start(f32[1024,64]{0,1:T(8,128)S(1)} %add.248), channel_id=1, source_target_pairs={{28,0},{0,4},{4,8},{8,12},{12,16},{16,20},{20,24},{24,28},{29,1},{... | collective-permute-start | bytes 786440 | tf_op jit(solution)/shard_map/ppermute | solution.py:20
  185.8 1.3 collective-permute-start.16
  187.1 5.0 %collective-permute-start.17 = (f32[35,128]{1,0:T(8,128)S(1)}, f32[35,128]{1,0:T(8,128)S(1)}, u32[]{:S(2)}, u32[]{:S(2)}) collective-permute-start(f32[35,128]{1,0:T(8,128)S(1)} %pad_maximum_fusion.12), channel_id=1, source_target_pairs={{0,2},{1,3},{2,0},{3,1},{4,6},{5,7},{6,4},{7,5},{8,10},{9,11},{10,... | collective-permute-start | bytes 53768 | tf_op jit(solution)/shard_map/ppermute | solution.py:196
  192.2 3.8 %collective-permute-start.18 = (f32[37,128]{1,0:T(8,128)S(1)}, f32[37,128]{1,0:T(8,128)S(1)}, u32[]{:S(2)}, u32[]{:S(2)}) collective-permute-start(f32[37,128]{1,0:T(8,128)S(1)} %pad_maximum_fusion.13), channel_id=1, source_target_pairs={{0,4},{4,0},{8,12},{12,8},{16,20},{20,16},{24,28},{28,24},{1,5},{5... | collective-permute-start | bytes 56840 | tf_op jit(solution)/shard_map/ppermute | solution.py:196
  196.1 3.9 %collective-permute-start.19 = (f32[41,128]{1,0:T(8,128)S(1)}, f32[41,128]{1,0:T(8,128)S(1)}, u32[]{:S(2)}, u32[]{:S(2)}) collective-permute-start(f32[41,128]{1,0:T(8,128)S(1)} %pad_maximum_fusion.7), channel_id=1, source_target_pairs={{0,8},{4,12},{8,0},{12,4},{16,24},{20,28},{24,16},{28,20},{1,9},{5... | collective-permute-start | bytes 62984 | tf_op jit(solution)/shard_map/ppermute | solution.py:196
  200.0 5.1 %collective-permute-start.20 = (f32[49,128]{1,0:T(8,128)S(1)}, f32[49,128]{1,0:T(8,128)S(1)}, u32[]{:S(2)}, u32[]{:S(2)}) collective-permute-start(f32[49,128]{1,0:T(8,128)S(1)} %pad_maximum_fusion.5), channel_id=1, source_target_pairs={{0,16},{4,20},{8,24},{12,28},{16,0},{20,4},{24,8},{28,12},{1,17},{... | collective-permute-start | bytes 75272 | tf_op jit(solution)/shard_map/ppermute | solution.py:196

commit v14 on v12

--- a/solution.py
+++ b/solution.py
@@ -9,6 +9,7 @@
 from jax.experimental import pallas as pl
 
 ITERS = 2
+FETCH_PIECES = 2
 
 
 kernel_width_factor = 0.05
@@ -276,11 +277,15 @@
     vector_count = start.shape[1]
     units = {0: unit_block}
     weights = {0: start}
+    piece_rows = block_rows // FETCH_PIECES
     for offset in fetch_offsets:
-        if offset == fetch_offsets[-1]:
-            units[offset] = normalize_rows(shifted(embeddings, "wide", -offset))
-        else:
-            units[offset] = shifted(unit_block, "wide", -offset)
+        rows = embeddings if offset == fetch_offsets[-1] else unit_block
+        pieces = [
+            shifted(rows[i * piece_rows : (i + 1) * piece_rows], "wide", -offset)
+            for i in range(FETCH_PIECES)
+        ]
+        arrived = jnp.concatenate(pieces)
+        units[offset] = normalize_rows(arrived) if offset == fetch_offsets[-1] else arrived
         weights[offset] = shifted(start, "wide", -offset)
 
     self_mask = lax.broadcasted_iota(

time: 219 us -> 227 us (1.037); the launches traced: 219 us -> 224 us
  waiting for transfers between devices: 92.6 us -> 87.1 us
  starting transfers between devices: 36.8 us -> 42.2 us
  local copies, waits for them, and re-layouts: 9.59 us -> 14.8 us
    ppermute x10 -> x12, waiting for transfers between devices: 67.4 us -> 60.8 us  [shifted(): return lax.ppermute(block, axis, route)]
    ppermute x10 -> x12, starting transfers between devices: 24.5 us -> 30.9 us  [shifted(): return lax.ppermute(block, axis, route)]
    slice x0 -> x2, local copies, waits for them, and re-layouts: none -> 4.1 us  [on_device(): rows[i * piece_rows:(i + 1) * piece_rows]]
    concatenate x0 -> x1, other arithmetic: none -> 2.7 us  [on_device(): arrived = jnp.concatenate(pieces)]
  transfers between devices with their start and end apart: 20 -> 22, of which waited for: 16 -> 19; matrix products, arithmetic and copies ran while one was open for 14% -> 15% of each run, Pallas kernels for 4% -> 4%
where the time goes in v14:
time: 227 us; the launch traced here: 224 us
  waiting for transfers between devices  87.1 us (38%)
  starting transfers between devices  42.2 us (19%)
  matrix products  41.7 us (18%)
  other arithmetic  18.4 us (8%)
  Pallas kernels  16.8 us (7%)
  local copies, waits for them, and re-layouts  14.8 us (7%)
  between operations  3.14 us (1%)
    ppermute x12, waiting for transfers between devices, shifted(): return lax.ppermute(block, axis, route)  60.8 us
    ppermute x12, starting transfers between devices, shifted(): return lax.ppermute(block, axis, route)  30.9 us
    ppermute x10, waiting for transfers between devices, butterfly(): other = lax.ppermute(block, axis, route)  26.3 us
    pallas_call x2, Pallas kernels, factor_inverse(): pl.pallas_call(factor_kernel, out_shape=jax.ShapeDtypeStruct(gram_matrix....  16.8 us
    dot_general x3, matrix products, scores_tile(): lax.dot_general(leftside_block, right_block, (((1,), (1,)), ((), ())), pr...  14.4 us
    dot_general x6, matrix products, row_product(): return jnp.dot(affinity, weights, preferred_element_type=jnp.float32)  11.5 us
    ppermute x10, starting transfers between devices, butterfly(): other = lax.ppermute(block, axis, route)  11.3 us
    dot_general x4, matrix products, col_product(): lax.dot_general(affinity, weights, (((0,), (0,)), ((), ())), preferred_el...  9.07 us
  transfers between devices with their start and end apart: 22, of which 19 were waited for; matrix products, arithmetic and copies ran while one was open for 15% of the time, Pallas kernels for 4%

profile of v14, /device:TPU:0, one launch (start us, length us, event | category | flops | bytes accessed | tf_op | source)
XLA Modules:
  0.0 224.2 jit_solution(12631142093562219975)
XLA Ops:
  0.6 2.8 %fusion.45 = (bf16[512,768]{1,0:T(8,128)(2,1)}, bf16[512,768]{1,0:T(8,128)(2,1)}) fusion(bf16[1024,768]{1,0:T(8,128)(2,1)} %param.17), kind=kLoop, calls=%fused_computation.128 | loop fusion | bytes 3145728 | tf_op jit(solution)/shard_map/slice | solution.py:284
  3.4 3.0 %collective-permute-start.4 = (bf16[512,768]{1,0:T(8,128)(2,1)}, bf16[512,768]{1,0:T(8,128)(2,1)S(1)}, u32[]{:S(2)}, u32[]{:S(2)}) collective-permute-start(bf16[512,768]{1,0:T(8,128)(2,1)} %get-tuple-element.176), channel_id=1, source_target_pairs={{24,0},{28,4},{0,8},{4,12},{8,16},{12,20},{16,24},{20,28},{25,1},{... | collective-permute-start | bytes 2359304 | tf_op jit(solution)/shard_map/ppermute | solution.py:21
  6.4 1.6 collective-permute-start.3
  8.8 1.1 copy-done.1
  10.0 1.3 fusion.46
  11.3 3.2 %collective-permute-start.1 = (bf16[512,768]{1,0:T(8,128)(2,1)}, bf16[512,768]{1,0:T(8,128)(2,1)}, u32[]{:S(2)}, u32[]{:S(2)}) collective-permute-start(bf16[512,768]{1,0:T(8,128)(2,1)} %get-tuple-element.178), channel_id=1, source_target_pairs={{4,0},{8,4},{12,8},{16,12},{20,16},{24,20},{28,24},{0,28},{5,1},{9... | collective-permute-start | bytes 2359304 | tf_op jit(solution)/shard_map/ppermute | solution.py:21
  15.9 1.4 collective-permute-start.2
  17.3 4.5 %convert_reduce_fusion.6 = (f32[1024]{0:T(1024)}, bf16[1024,1024]{0,1:T(8,128)(2,1)S(1)}) fusion(bf16[1024,768]{1,0:T(8,128)(2,1)} %copy-done.1), kind=kOutput, calls=%fused_computation.9 | convolution fusion | flops 1616903168 | bytes 3674112 | tf_op jit(solution)/shard_map/dot_general | solution.py:56
  24.5 2.6 %collective-permute-done.4 = bf16[512,768]{1,0:T(8,128)(2,1)S(1)} collective-permute-done((bf16[512,768]{1,0:T(8,128)(2,1)}, bf16[512,768]{1,0:T(8,128)(2,1)S(1)}, u32[]{:S(2)}, u32[]{:S(2)}) %collective-permute-start.4) | collective-permute-done | bytes 786464 | tf_op jit(solution)/shard_map/ppermute | solution.py:21
  27.1 16.9 %collective-permute-done.3 = bf16[512,768]{1,0:T(8,128)(2,1)} collective-permute-done((bf16[512,768]{1,0:T(8,128)(2,1)}, bf16[512,768]{1,0:T(8,128)(2,1)}, u32[]{:S(2)}, u32[]{:S(2)}) %collective-permute-start.3) | collective-permute-done | bytes 786464 | tf_op jit(solution)/shard_map/ppermute | solution.py:21
  44.0 1.5 fusion.4
  45.6 2.7 %fusion.6 = bf16[1024,768]{1,0:T(8,128)(2,1)} fusion(f32[1024]{0:T(1024)S(1)} %add_rsqrt_fusion, bf16[512,768]{1,0:T(8,128)(2,1)S(1)} %collective-permute-done.4, bf16[512,768]{1,0:T(8,128)(2,1)} %collective-permute-done.3), kind=kLoop, calls=%fused_computation.23 | loop fusion | flops 5505024 | bytes 3149824 | tf_op jit(solution)/shard_map/convert_element_type | solution.py:52
  48.3 7.1 %conditional.7 = (bf16[1024,1024]{1,0:T(8,128)(2,1)}, f32[1024,64]{0,1:T(8,128)S(1)}, f32[1024]{0:T(1024)S(1)}, f32[1024]{0:T(1024)S(1)}) conditional(s32[]{:T(128)} %convert_element_type.61, () %tuple.64, (bf16[1024,768]{1,0:T(8,128)(2,1)}, bf16[1024,768]{1,0:T(8,128)(2,1)S(1)}, bf16[1024,64]{0,1:T(8,128)(2,1)S(1)}) %tuple.124), branch_computations={%region_3.4_spmd, %region_4.0_spmd} | conditional | flops 1750071296 | bytes 7741472 | solution.py:126
  48.3 4.7 %convert_reduce_fusion = (f32[1024]{0:T(1024)S(1)}, f32[1024]{0:T(1024)S(1)}, bf16[1024,1024]{1,0:T(8,128)(2,1)}) fusion(bf16[1024,768]{1,0:T(8,128)(2,1)} %get-tuple-element.44, bf16[1024,768]{1,0:T(8,128)(2,1)S(1)} %get-tuple-element.48), kind=kOutput, calls=%fused_computation | convolution fusion | flops 1615853568 | bytes 5251072 | tf_op jit(solution)/shard_map/cond/branch_1_fun/dot_general | solution.py:56
  53.0 2.3 %fusion.55 = f32[1024,64]{0,1:T(8,128)S(1)} fusion(bf16[1024,1024]{1,0:T(8,128)(2,1)} %get-tuple-element.192, bf16[1024,64]{0,1:T(8,128)(2,1)S(1)} %get-tuple-element.141), kind=kOutput, calls=%fused_computation.138 | convolution fusion | flops 134217728 | bytes 2490368 | tf_op jit(solution)/shard_map/cond/branch_1_fun/dot_general | solution.py:63
  55.4 3.1 %collective-permute-done.1 = bf16[512,768]{1,0:T(8,128)(2,1)} collective-permute-done((bf16[512,768]{1,0:T(8,128)(2,1)}, bf16[512,768]{1,0:T(8,128)(2,1)}, u32[]{:S(2)}, u32[]{:S(2)}) %collective-permute-start.1) | collective-permute-done | bytes 786464 | tf_op jit(solution)/shard_map/ppermute | solution.py:21
  58.4 16.9 %collective-permute-done = bf16[512,768]{1,0:T(8,128)(2,1)} collective-permute-done((bf16[512,768]{1,0:T(8,128)(2,1)}, bf16[512,768]{1,0:T(8,128)(2,1)}, u32[]{:S(2)}, u32[]{:S(2)}) %collective-permute-start) | collective-permute-done | bytes 786464 | tf_op jit(solution)/shard_map/ppermute | solution.py:21
  75.3 2.7 %pad_maximum_fusion = bf16[1024,768]{1,0:T(8,128)(2,1)} fusion(bf16[512,768]{1,0:T(8,128)(2,1)} %collective-permute-done.1, bf16[512,768]{1,0:T(8,128)(2,1)} %collective-permute-done), kind=kLoop, calls=%fused_computation.24 | loop fusion | flops 3145728 | bytes 3145728 | tf_op jit(solution)/shard_map/concatenate | solution.py:287
  78.0 2.9 %collective-permute-done.2 = bf16[1024,64]{1,0:T(8,128)(2,1)S(1)} collective-permute-done((bf16[1024,64]{1,0:T(8,128)(2,1)}, bf16[1024,64]{1,0:T(8,128)(2,1)S(1)}, u32[]{:S(2)}, u32[]{:S(2)}) %collective-permute-start.2) | collective-permute-done | bytes 131104 | tf_op jit(solution)/shard_map/ppermute | solution.py:21
  80.9 7.1 %collective-permute-done.5 = bf16[1024,64]{1,0:T(8,128)(2,1)S(1)} collective-permute-done((bf16[1024,64]{1,0:T(8,128)(2,1)}, bf16[1024,64]{1,0:T(8,128)(2,1)S(1)}, u32[]{:S(2)}, u32[]{:S(2)}) %collective-permute-start.5) | collective-permute-done | bytes 131104 | tf_op jit(solution)/shard_map/ppermute | solution.py:21
  88.0 9.6 %conditional.10 = (bf16[1024,1024]{1,0:T(8,128)(2,1)}, f32[1024,64]{0,1:T(8,128)S(1)}, f32[1024]{0:T(1024)S(1)}, f32[1024,64]{0,1:T(8,128)S(1)}, f32[1024]{0:T(1024)S(1)}) conditional(s32[]{:T(128)} %convert_element_type.65, () %tuple.70, (bf16[1024,768]{1,0:T(8,128)(2,1)}, bf16[1024,768]{1,0:T(8,128)(2,1)}, bf16[1024,64]{1,0:T(8,128)(2,1)S(1)}, ...), branch_computations={%region_15.16_spmd, %region_16.19_spmd} | conditional | flops 1884289024 | bytes 10231848 | solution.py:97
  88.0 5.2 %convert_reduce_fusion.4 = (f32[1024]{0:T(1024)S(1)}, f32[1024]{0:T(1024)S(1)}, bf16[1024,1024]{1,0:T(8,128)(2,1)}) fusion(bf16[1024,768]{1,0:T(8,128)(2,1)} %get-tuple-element.56, bf16[1024,768]{1,0:T(8,128)(2,1)} %get-tuple-element.57), kind=kOutput, calls=%fused_computation.6 | convolution fusion | flops 1615853568 | bytes 5251072 | tf_op jit(solution)/shard_map/cond/branch_1_fun/dot_general | solution.py:56
  93.2 2.3 %fusion.58 = f32[1024,64]{0,1:T(8,128)S(1)} fusion(bf16[1024,1024]{1,0:T(8,128)(2,1)} %get-tuple-element.201, bf16[1024,64]{1,0:T(8,128)(2,1)S(1)} %get-tuple-element.58), kind=kOutput, calls=%fused_computation.141 | convolution fusion | flops 134217728 | bytes 2490368 | tf_op jit(solution)/shard_map/cond/branch_1_fun/dot_general | solution.py:63
  95.6 2.1 fusion.59
  98.4 1.0 add.204
  100.4 11.5 %collective-permute-start.7 = (f32[520,128]{1,0:T(8,128)}, f32[520,128]{1,0:T(8,128)}, u32[]{:S(2)}, u32[]{:S(2)}) collective-permute-start(f32[520,128]{1,0:T(8,128)} %pad_maximum_fusion.3), channel_id=1, source_target_pairs={{8,0},{12,4},{16,8},{20,12},{24,16},{28,20},{0,24},{4,28},{9,1},{1... | collective-permute-start | bytes 798728 | tf_op jit(solution)/shard_map/ppermute | solution.py:21
  111.9 2.3 %conditional.9 = (bf16[1024,1024]{1,0:T(8,128)(2,1)}, f32[1024,64]{0,1:T(8,128)}, f32[1024]{0:T(1024)S(1)}, f32[1024,64]{0,1:T(8,128)S(1)}, f32[1024]{0:T(1024)S(1)}) conditional(s32[]{:T(128)} %convert_element_type.64, () %tuple.68, (bf16[1024,768]{1,0:T(8,128)(2,1)}, bf16[1024,768]{1,0:T(8,128)(2,1)}, bf16[1024,64]{1,0:T(8,128)(2,1)S(1)}, ...), branch_computations={%region_10.11_spmd, %region_11.14_spmd} | conditional | flops 1884289024 | bytes 10231848 | solution.py:97
  112.0 1.6 broadcast.113
  115.9 2.8 %conditional.8 = (f32[1024,64]{0,1:T(8,128)}) conditional(s32[]{:T(128)} %convert_element_type.61, () %tuple.63, (bf16[1024,1024]{1,0:T(8,128)(2,1)}, bf16[1024,64]{1,0:T(8,128)(2,1)S(1)}) %tuple.67), branch_computations={%region_7.8_spmd, %region_8.9_spmd} | conditional | flops 134217728 | bytes 2490376 | solution.py:138
  115.9 2.8 %fusion.48 = f32[1024,64]{0,1:T(8,128)} fusion(bf16[1024,1024]{1,0:T(8,128)(2,1)} %get-tuple-element.50, bf16[1024,64]{1,0:T(8,128)(2,1)S(1)} %get-tuple-element.51), kind=kOutput, calls=%fused_computation.131 | convolution fusion | flops 134217728 | bytes 2490368 | tf_op jit(solution)/shard_map/cond/branch_1_fun/dot_general | solution.py:67
  118.8 1.0 slice.182
  120.1 4.8 %collective-permute-done.6 = f32[520,128]{1,0:T(8,128)} collective-permute-done((f32[520,128]{1,0:T(8,128)}, f32[520,128]{1,0:T(8,128)}, u32[]{:S(2)}, u32[]{:S(2)}) %collective-permute-start.6) | collective-permute-done | bytes 266272 | tf_op jit(solution)/shard_map/ppermute | solution.py:21
  126.2 1.2 fusion.43
  127.4 1.3 broadcast_multiply_fusion
  131.0 1.2 collective-permute-done.10
  132.2 4.1 %collective-permute-start.11 = (f32[35,128]{1,0:T(8,128)S(1)}, f32[35,128]{1,0:T(8,128)S(1)}, u32[]{:S(2)}, u32[]{:S(2)}) collective-permute-start(f32[35,128]{1,0:T(8,128)S(1)} %pad_maximum_fusion.9), channel_id=1, source_target_pairs={{0,2},{1,3},{2,0},{3,1},{4,6},{5,7},{6,4},{7,5},{8,10},{9,11},{10,... | collective-permute-start | bytes 53768 | tf_op jit(solution)/shard_map/ppermute | solution.py:170
  136.3 1.8 collective-permute-done.11
  138.2 3.8 %collective-permute-done.12 = f32[37,128]{1,0:T(8,128)S(1)} collective-permute-done((f32[37,128]{1,0:T(8,128)S(1)}, f32[37,128]{1,0:T(8,128)S(1)}, u32[]{:S(2)}, u32[]{:S(2)}) %collective-permute-start.12) | collective-permute-done | bytes 18976 | tf_op jit(solution)/shard_map/ppermute | solution.py:170
  142.3 3.5 %collective-permute-done.13 = f32[41,128]{1,0:T(8,128)S(1)} collective-permute-done((f32[41,128]{1,0:T(8,128)S(1)}, f32[41,128]{1,0:T(8,128)S(1)}, u32[]{:S(2)}, u32[]{:S(2)}) %collective-permute-start.13) | collective-permute-done | bytes 21024 | tf_op jit(solution)/shard_map/ppermute | solution.py:170
  145.9 3.0 %collective-permute-start.14 = (f32[49,128]{1,0:T(8,128)S(1)}, f32[49,128]{1,0:T(8,128)S(1)}, u32[]{:S(2)}, u32[]{:S(2)}) collective-permute-start(f32[49,128]{1,0:T(8,128)S(1)} %pad_maximum_fusion.4), channel_id=1, source_target_pairs={{0,16},{4,20},{8,24},{12,28},{16,0},{20,4},{24,8},{28,12},{1,17},{... | collective-permute-start | bytes 75272 | tf_op jit(solution)/shard_map/ppermute | solution.py:170
  148.9 2.1 collective-permute-start.9
  151.0 1.7 collective-permute-start.8
  152.7 1.2 collective-permute-done.14
  156.4 8.4 %shard_map.50 = f32[64,64]{1,0:T(8,128)} custom-call(f32[64,64]{1,0:T(8,128)} %fusion.12.gram_ref), custom_call_target="tpu_custom_call" | custom-call | tf_op jit(solution)/shard_map/pallas_call | solution.py:218
  164.8 1.7 convolution_convert_fusion
  167.3 4.4 %conditional.12 = (f32[1024,64]{0,1:T(8,128)S(1)}, f32[1024,64]{0,1:T(8,128)S(1)}) conditional(s32[]{:T(128)} %convert_element_type.61, () %tuple.74, (bf16[1024,1024]{1,0:T(8,128)(2,1)}, bf16[1024,64]{0,1:T(8,128)(2,1)S(1)}, bf16[1024,64]{0,1:T(8,128)(2,1)S(1)}) %tuple.75), branch_computations={%region_26.27_spmd, %region_27.28_spmd} | conditional | flops 268435456 | bytes 4980752 | solution.py:154
  167.3 2.3 %fusion.51 = f32[1024,64]{0,1:T(8,128)S(1)} fusion(bf16[1024,1024]{1,0:T(8,128)(2,1)} %get-tuple-element.63, bf16[1024,64]{0,1:T(8,128)(2,1)S(1)} %get-tuple-element.150), kind=kOutput, calls=%fused_computation.134 | convolution fusion | flops 134217728 | bytes 2490368 | tf_op jit(solution)/shard_map/cond/branch_1_fun/dot_general | solution.py:63
  169.6 2.1 fusion.52
  171.7 4.4 %conditional.13 = (f32[1024,64]{0,1:T(8,128)S(1)}, f32[1024,64]{0,1:T(8,128)S(1)}) conditional(s32[]{:T(128)} %convert_element_type.65, () %tuple.76, (bf16[1024,1024]{1,0:T(8,128)(2,1)}, bf16[1024,64]{0,1:T(8,128)(2,1)S(1)}, bf16[1024,64]{0,1:T(8,128)(2,1)S(1)}) %tuple.77), branch_computations={%region_28.29_spmd, %region_29.30_spmd} | conditional | flops 268435456 | bytes 4980752 | solution.py:154
  171.7 2.3 %fusion.53 = f32[1024,64]{0,1:T(8,128)S(1)} fusion(bf16[1024,1024]{1,0:T(8,128)(2,1)} %get-tuple-element.66, bf16[1024,64]{0,1:T(8,128)(2,1)S(1)} %get-tuple-element.153), kind=kOutput, calls=%fused_computation.136 | convolution fusion | flops 134217728 | bytes 2490368 | tf_op jit(solution)/shard_map/cond/branch_1_fun/dot_general | solution.py:63
  174.1 2.1 fusion.54
  176.9 3.3 %collective-permute-start.16 = (f32[1024,64]{0,1:T(8,128)}, f32[1024,64]{0,1:T(8,128)}, u32[]{:S(2)}, u32[]{:S(2)}) collective-permute-start(f32[1024,64]{0,1:T(8,128)} %add.228), channel_id=1, source_target_pairs={{8,0},{12,4},{16,8},{20,12},{24,16},{28,20},{0,24},{4,28},{9,1},{1... | collective-permute-start | bytes 786440 | tf_op jit(solution)/shard_map/ppermute | solution.py:21
  180.3 2.6 %collective-permute-start.15 = (f32[1024,64]{0,1:T(8,128)S(1)}, f32[1024,64]{0,1:T(8,128)S(1)}, u32[]{:S(2)}, u32[]{:S(2)}) collective-permute-start(f32[1024,64]{0,1:T(8,128)S(1)} %add.226), channel_id=1, source_target_pairs={{28,0},{0,4},{4,8},{8,12},{12,16},{16,20},{20,24},{24,28},{29,1},{... | collective-permute-start | bytes 786440 | tf_op jit(solution)/shard_map/ppermute | solution.py:21
  182.9 1.5 collective-permute-done.16
  184.4 5.0 %collective-permute-done.15 = f32[1024,64]{0,1:T(8,128)S(1)} collective-permute-done((f32[1024,64]{0,1:T(8,128)S(1)}, f32[1024,64]{0,1:T(8,128)S(1)}, u32[]{:S(2)}, u32[]{:S(2)}) %collective-permute-start.15) | collective-permute-done | bytes 262176 | tf_op jit(solution)/shard_map/ppermute | solution.py:21
  189.4 1.6 fusion.40
  192.6 1.2 collective-permute-done.17
  193.8 2.9 %collective-permute-start.18 = (f32[35,128]{1,0:T(8,128)S(1)}, f32[35,128]{1,0:T(8,128)S(1)}, u32[]{:S(2)}, u32[]{:S(2)}) collective-permute-start(f32[35,128]{1,0:T(8,128)S(1)} %pad_maximum_fusion.12), channel_id=1, source_target_pairs={{0,2},{1,3},{2,0},{3,1},{4,6},{5,7},{6,4},{7,5},{8,10},{9,11},{10,... | collective-permute-start | bytes 53768 | tf_op jit(solution)/shard_map/ppermute | solution.py:170
  196.7 1.8 collective-permute-done.18
  198.6 3.8 %collective-permute-done.19 = f32[37,128]{1,0:T(8,128)S(1)} collective-permute-done((f32[37,128]{1,0:T(8,128)S(1)}, f32[37,128]{1,0:T(8,128)S(1)}, u32[]{:S(2)}, u32[]{:S(2)}) %collective-permute-start.19) | collective-permute-done | bytes 18976 | tf_op jit(solution)/shard_map/ppermute | solution.py:170
  202.7 3.6 %collective-permute-done.20 = f32[41,128]{1,0:T(8,128)S(1)} collective-permute-done((f32[41,128]{1,0:T(8,128)S(1)}, f32[41,128]{1,0:T(8,128)S(1)}, u32[]{:S(2)}, u32[]{:S(2)}) %collective-permute-start.20) | collective-permute-done | bytes 21024 | tf_op jit(solution)/shard_map/ppermute | solution.py:170
  206.7 4.6 %collective-permute-done.21 = f32[49,128]{1,0:T(8,128)S(1)} collective-permute-done((f32[49,128]{1,0:T(8,128)S(1)}, f32[49,128]{1,0:T(8,128)S(1)}, u32[]{:S(2)}, u32[]{:S(2)}) %collective-permute-start.21) | collective-permute-done | bytes 25120 | tf_op jit(solution)/shard_map/ppermute | solution.py:170
  213.9 8.4 %shard_map.51 = f32[64,64]{1,0:T(8,128)} custom-call(f32[64,64]{1,0:T(8,128)} %fusion.10.gram_ref), custom_call_target="tpu_custom_call" | custom-call | tf_op jit(solution)/shard_map/pallas_call | solution.py:218
  222.3 1.9 fusion.18
  (132 shorter events, 20.5 us)
Async XLA Ops:
  0.6 7.4 %copy-start = (bf16[1024,768]{1,0:T(8,128)(2,1)S(1)}, bf16[1024,768]{1,0:T(8,128)(2,1)}, u32[]{:S(2)}) copy-start(bf16[1024,768]{1,0:T(8,128)(2,1)} %param.17) | copy-start | bytes 4718596
  3.4 23.7 %collective-permute-start.4 = (bf16[512,768]{1,0:T(8,128)(2,1)}, bf16[512,768]{1,0:T(8,128)(2,1)S(1)}, u32[]{:S(2)}, u32[]{:S(2)}) collective-permute-start(bf16[512,768]{1,0:T(8,128)(2,1)} %get-tuple-element.176), channel_id=1, source_target_pairs={{24,0},{28,4},{0,8},{4,12},{8,16},{12,20},{16,24},{20,28},{25,1},{... | collective-permute-start | bytes 2359304 | tf_op jit(solution)/shard_map/ppermute | solution.py:21
  6.4 37.6 %collective-permute-start.3 = (bf16[512,768]{1,0:T(8,128)(2,1)}, bf16[512,768]{1,0:T(8,128)(2,1)}, u32[]{:S(2)}, u32[]{:S(2)}) collective-permute-start(bf16[512,768]{1,0:T(8,128)(2,1)} %get-tuple-element.175), channel_id=1, source_target_pairs={{24,0},{28,4},{0,8},{4,12},{8,16},{12,20},{16,24},{20,28},{25,1},{... | collective-permute-start | bytes 2359304 | tf_op jit(solution)/shard_map/ppermute | solution.py:21
  8.8 1.1 copy-start.1
  10.0 5.1 %copy-start.3 = (bf16[1024,64]{0,1:T(8,128)(2,1)S(1)}, bf16[1024,64]{0,1:T(8,128)(2,1)}, u32[]{:S(2)}) copy-start(bf16[1024,64]{0,1:T(8,128)(2,1)} %param.18) | copy-start | bytes 393220
  11.3 47.1 %collective-permute-start.1 = (bf16[512,768]{1,0:T(8,128)(2,1)}, bf16[512,768]{1,0:T(8,128)(2,1)}, u32[]{:S(2)}, u32[]{:S(2)}) collective-permute-start(bf16[512,768]{1,0:T(8,128)(2,1)} %get-tuple-element.178), channel_id=1, source_target_pairs={{4,0},{8,4},{12,8},{16,12},{20,16},{24,20},{28,24},{0,28},{5,1},{9... | collective-permute-start | bytes 2359304 | tf_op jit(solution)/shard_map/ppermute | solution.py:21
  14.5 60.8 %collective-permute-start = (bf16[512,768]{1,0:T(8,128)(2,1)}, bf16[512,768]{1,0:T(8,128)(2,1)}, u32[]{:S(2)}, u32[]{:S(2)}) collective-permute-start(bf16[512,768]{1,0:T(8,128)(2,1)} %get-tuple-element.177), channel_id=1, source_target_pairs={{4,0},{8,4},{12,8},{16,12},{20,16},{24,20},{28,24},{0,28},{5,1},{9... | collective-permute-start | bytes 2359304 | tf_op jit(solution)/shard_map/ppermute | solution.py:21
  15.9 5.9 %copy-start.8 = (s32[32,3]{0,1:T(4,128)S(1)}, s32[32,3]{0,1:T(4,128)}, u32[]{:S(2)}) copy-start(s32[32,3]{0,1:T(4,128)} %param.19) | copy-start | bytes 1156
  15.9 65.0 %collective-permute-start.2 = (bf16[1024,64]{1,0:T(8,128)(2,1)}, bf16[1024,64]{1,0:T(8,128)(2,1)S(1)}, u32[]{:S(2)}, u32[]{:S(2)}) collective-permute-start(bf16[1024,64]{1,0:T(8,128)(2,1)} %copy.17), channel_id=1, source_target_pairs={{4,0},{8,4},{12,8},{16,12},{20,16},{24,20},{28,24},{0,28},{5,1},{9... | collective-permute-start | bytes 393224 | tf_op jit(solution)/shard_map/ppermute | solution.py:21
  24.5 23.8 %copy-start.2 = (bf16[1024,768]{1,0:T(8,128)(2,1)S(1)}, bf16[1024,768]{1,0:T(8,128)(2,1)}, u32[]{:S(2)}) copy-start(bf16[1024,768]{1,0:T(8,128)(2,1)} %copy-done.1) | copy-start | bytes 4718596
  27.1 60.9 %collective-permute-start.5 = (bf16[1024,64]{1,0:T(8,128)(2,1)}, bf16[1024,64]{1,0:T(8,128)(2,1)S(1)}, u32[]{:S(2)}, u32[]{:S(2)}) collective-permute-start(bf16[1024,64]{1,0:T(8,128)(2,1)} %copy.17), channel_id=1, source_target_pairs={{24,0},{28,4},{0,8},{4,12},{8,16},{12,20},{16,24},{20,28},{25,1},{... | collective-permute-start | bytes 393224 | tf_op jit(solution)/shard_map/ppermute | solution.py:21
  55.3 32.7 %copy-start.6 = (f32[1024,64]{0,1:T(8,128)}, f32[1024,64]{0,1:T(8,128)S(1)}, u32[]{:S(2)}) copy-start(f32[1024,64]{0,1:T(8,128)S(1)} %get-tuple-element.109) | copy-start | bytes 786436
  97.7 0.7 copy-start.4
  100.4 13.8 %copy-start.5 = (f32[1024,64]{0,1:T(8,128)S(1)}, f32[1024,64]{0,1:T(8,128)}, u32[]{:S(2)}) copy-start(f32[1024,64]{0,1:T(8,128)} %copy-done.4) | copy-start | bytes 786436
  100.4 18.3 %collective-permute-start.7 = (f32[520,128]{1,0:T(8,128)}, f32[520,128]{1,0:T(8,128)}, u32[]{:S(2)}, u32[]{:S(2)}) collective-permute-start(f32[520,128]{1,0:T(8,128)} %pad_maximum_fusion.3), channel_id=1, source_target_pairs={{8,0},{12,4},{16,8},{20,12},{24,16},{28,20},{0,24},{4,28},{9,1},{1... | collective-permute-start | bytes 798728 | tf_op jit(solution)/shard_map/ppermute | solution.py:21
  115.4 9.4 %collective-permute-start.6 = (f32[520,128]{1,0:T(8,128)}, f32[520,128]{1,0:T(8,128)}, u32[]{:S(2)}, u32[]{:S(2)}) collective-permute-start(f32[520,128]{1,0:T(8,128)} %pad_maximum_fusion.2), channel_id=1, source_target_pairs={{28,0},{0,4},{4,8},{8,12},{12,16},{16,20},{20,24},{24,28},{29,1},{... | collective-permute-start | bytes 798728 | tf_op jit(solution)/shard_map/ppermute | solution.py:21
  119.9 7.5 %copy-start.9 = (f32[1024]{0:T(1024)S(1)}, f32[1024]{0:T(1024)}, u32[]{:S(2)}) copy-start(f32[1024]{0:T(1024)} %get-tuple-element.182) | copy-start | bytes 12292
  130.9 1.3 collective-permute-start.10
  132.2 5.8 %collective-permute-start.11 = (f32[35,128]{1,0:T(8,128)S(1)}, f32[35,128]{1,0:T(8,128)S(1)}, u32[]{:S(2)}, u32[]{:S(2)}) collective-permute-start(f32[35,128]{1,0:T(8,128)S(1)} %pad_maximum_fusion.9), channel_id=1, source_target_pairs={{0,2},{1,3},{2,0},{3,1},{4,6},{5,7},{6,4},{7,5},{8,10},{9,11},{10,... | collective-permute-start | bytes 53768 | tf_op jit(solution)/shard_map/ppermute | solution.py:170
  138.1 3.8 %collective-permute-start.12 = (f32[37,128]{1,0:T(8,128)S(1)}, f32[37,128]{1,0:T(8,128)S(1)}, u32[]{:S(2)}, u32[]{:S(2)}) collective-permute-start(f32[37,128]{1,0:T(8,128)S(1)} %pad_maximum_fusion.10), channel_id=1, source_target_pairs={{0,4},{4,0},{8,12},{12,8},{16,20},{20,16},{24,28},{28,24},{1,5},{5... | collective-permute-start | bytes 56840 | tf_op jit(solution)/shard_map/ppermute | solution.py:170
  142.0 3.9 %collective-permute-start.13 = (f32[41,128]{1,0:T(8,128)S(1)}, f32[41,128]{1,0:T(8,128)S(1)}, u32[]{:S(2)}, u32[]{:S(2)}) collective-permute-start(f32[41,128]{1,0:T(8,128)S(1)} %pad_maximum_fusion.6), channel_id=1, source_target_pairs={{0,8},{4,12},{8,0},{12,4},{16,24},{20,28},{24,16},{28,20},{1,9},{5... | collective-permute-start | bytes 62984 | tf_op jit(solution)/shard_map/ppermute | solution.py:170
  145.9 8.0 %collective-permute-start.14 = (f32[49,128]{1,0:T(8,128)S(1)}, f32[49,128]{1,0:T(8,128)S(1)}, u32[]{:S(2)}, u32[]{:S(2)}) collective-permute-start(f32[49,128]{1,0:T(8,128)S(1)} %pad_maximum_fusion.4), channel_id=1, source_target_pairs={{0,16},{4,20},{8,24},{12,28},{16,0},{20,4},{24,8},{28,12},{1,17},{... | collective-permute-start | bytes 75272 | tf_op jit(solution)/shard_map/ppermute | solution.py:170
  148.9 15.9 %collective-permute-start.9 = (f32[1024,64]{0,1:T(8,128)S(1)}, f32[1024,64]{0,1:T(8,128)S(1)}, u32[]{:S(2)}, u32[]{:S(2)}) collective-permute-start(f32[1024,64]{0,1:T(8,128)S(1)} %get-tuple-element.171), channel_id=1, source_target_pairs={{24,0},{28,4},{0,8},{4,12},{8,16},{12,20},{16,24},{20,28},{25,1},{... | collective-permute-start | bytes 786440 | tf_op jit(solution)/shard_map/ppermute | solution.py:21
  151.0 13.8 %collective-permute-start.8 = (f32[1024,64]{0,1:T(8,128)S(1)}, f32[1024,64]{0,1:T(8,128)S(1)}, u32[]{:S(2)}, u32[]{:S(2)}) collective-permute-start(f32[1024,64]{0,1:T(8,128)S(1)} %get-tuple-element.171), channel_id=1, source_target_pairs={{4,0},{8,4},{12,8},{16,12},{20,16},{24,20},{28,24},{0,28},{5,1},{9... | collective-permute-start | bytes 786440 | tf_op jit(solution)/shard_map/ppermute | solution.py:21
  166.5 0.7 copy-start.7
  176.9 7.5 %collective-permute-start.16 = (f32[1024,64]{0,1:T(8,128)}, f32[1024,64]{0,1:T(8,128)}, u32[]{:S(2)}, u32[]{:S(2)}) collective-permute-start(f32[1024,64]{0,1:T(8,128)} %add.228), channel_id=1, source_target_pairs={{8,0},{12,4},{16,8},{20,12},{24,16},{28,20},{0,24},{4,28},{9,1},{1... | collective-permute-start | bytes 786440 | tf_op jit(solution)/shard_map/ppermute | solution.py:21
  180.3 9.1 %collective-permute-start.15 = (f32[1024,64]{0,1:T(8,128)S(1)}, f32[1024,64]{0,1:T(8,128)S(1)}, u32[]{:S(2)}, u32[]{:S(2)}) collective-permute-start(f32[1024,64]{0,1:T(8,128)S(1)} %add.226), channel_id=1, source_target_pairs={{28,0},{0,4},{4,8},{8,12},{12,16},{16,20},{20,24},{24,28},{29,1},{... | collective-permute-start | bytes 786440 | tf_op jit(solution)/shard_map/ppermute | solution.py:21
  192.5 1.2 collective-permute-start.17
  193.8 4.6 %collective-permute-start.18 = (f32[35,128]{1,0:T(8,128)S(1)}, f32[35,128]{1,0:T(8,128)S(1)}, u32[]{:S(2)}, u32[]{:S(2)}) collective-permute-start(f32[35,128]{1,0:T(8,128)S(1)} %pad_maximum_fusion.12), channel_id=1, source_target_pairs={{0,2},{1,3},{2,0},{3,1},{4,6},{5,7},{6,4},{7,5},{8,10},{9,11},{10,... | collective-permute-start | bytes 53768 | tf_op jit(solution)/shard_map/ppermute | solution.py:170
  198.5 3.8 %collective-permute-start.19 = (f32[37,128]{1,0:T(8,128)S(1)}, f32[37,128]{1,0:T(8,128)S(1)}, u32[]{:S(2)}, u32[]{:S(2)}) collective-permute-start(f32[37,128]{1,0:T(8,128)S(1)} %pad_maximum_fusion.13), channel_id=1, source_target_pairs={{0,4},{4,0},{8,12},{12,8},{16,20},{20,16},{24,28},{28,24},{1,5},{5... | collective-permute-start | bytes 56840 | tf_op jit(solution)/shard_map/ppermute | solution.py:170
  202.4 3.9 %collective-permute-start.20 = (f32[41,128]{1,0:T(8,128)S(1)}, f32[41,128]{1,0:T(8,128)S(1)}, u32[]{:S(2)}, u32[]{:S(2)}) collective-permute-start(f32[41,128]{1,0:T(8,128)S(1)} %pad_maximum_fusion.7), channel_id=1, source_target_pairs={{0,8},{4,12},{8,0},{12,4},{16,24},{20,28},{24,16},{28,20},{1,9},{5... | collective-permute-start | bytes 62984 | tf_op jit(solution)/shard_map/ppermute | solution.py:170
  206.3 5.0 %collective-permute-start.21 = (f32[49,128]{1,0:T(8,128)S(1)}, f32[49,128]{1,0:T(8,128)S(1)}, u32[]{:S(2)}, u32[]{:S(2)}) collective-permute-start(f32[49,128]{1,0:T(8,128)S(1)} %pad_maximum_fusion.5), channel_id=1, source_target_pairs={{0,16},{4,20},{8,24},{12,28},{16,0},{20,4},{24,8},{28,12},{1,17},{... | collective-permute-start | bytes 75272 | tf_op jit(solution)/shard_map/ppermute | solution.py:170

commit v15 on v13

--- a/solution.py
+++ b/solution.py
@@ -307,7 +307,12 @@
     half_rows = block_rows // 2
     for offset in fetch_offsets:
         if offset == fetch_offsets[-1]:
-            units[offset] = normalize_rows(shifted(embeddings, "wide", -offset))
+            units[offset] = jnp.concatenate(
+                [
+                    normalize_rows(shifted(embeddings[:half_rows], "wide", -offset)),
+                    normalize_rows(shifted(embeddings[half_rows:], "wide", -offset)),
+                ]
+            )
         else:
             halves[offset] = [
                 shifted(unit_block[:half_rows], "wide", -offset),

time: 220 us -> 229 us (1.041)
  matrix products: 30.8 us -> 58.9 us
  starting transfers between devices: 44.7 us -> 22.2 us
  waiting for transfers between devices: 80.9 us -> 90.8 us
  other arithmetic: 23.9 us -> 20 us
  local copies, waits for them, and re-layouts: 17.7 us -> 15 us
    ppermute x11 -> x12, starting transfers between devices: 31.3 us -> 16.1 us  [shifted(): return lax.ppermute(block, axis, route)]
    dot_general x3 -> x6, matrix products: 11.9 us -> 22.8 us  [scores_tile(): lax.dot_general(leftside_block, right_block, (((1,), (1,)), ((), ())), pr...]
    dot_general x5 -> x10, matrix products: 8.54 us -> 18 us  [row_product(): return jnp.dot(affinity, weights, preferred_element_type=jnp.float32)]
    ppermute x11 -> x12, waiting for transfers between devices: 58.7 us -> 66.4 us  [shifted(): return lax.ppermute(block, axis, route)]
    dot_general x3 -> x8, matrix products: 3.62 us -> 11.3 us  [col_product(): lax.dot_general(affinity, weights, (((0,), (0,)), ((), ())), preferred_el...]
    ppermute x10, starting transfers between devices: 13.4 us -> 6.13 us  [butterfly(): other = lax.ppermute(block, axis, route)]
    another operation x18 -> x0, local copies, waits for them, and re-layouts: 5.21 us -> none
    slice x0 -> x1, local copies, waits for them, and re-layouts: none -> 2.69 us  [on_device(): embeddings[:half_rows]]
  transfers between devices with their start and end apart: 21 -> 22, of which waited for: 14 -> 15; matrix products, arithmetic and copies ran while one was open for 18% -> 25% of each run, Pallas kernels for 4% -> 4%
where the time goes in v15:
time: 229 us; the launch traced here: 227 us
  waiting for transfers between devices  90.8 us (40%)
  matrix products  58.9 us (26%)
  starting transfers between devices  22.2 us (10%)
  other arithmetic  20 us (9%)
  Pallas kernels  16.8 us (7%)
  local copies, waits for them, and re-layouts  15 us (7%)
  between operations  3.37 us (1%)
    ppermute x12, waiting for transfers between devices, shifted(): return lax.ppermute(block, axis, route)  66.4 us
    ppermute x10, waiting for transfers between devices, butterfly(): other = lax.ppermute(block, axis, route)  24.4 us
    dot_general x6, matrix products, scores_tile(): lax.dot_general(leftside_block, right_block, (((1,), (1,)), ((), ())), pr...  22.8 us
    dot_general x10, matrix products, row_product(): return jnp.dot(affinity, weights, preferred_element_type=jnp.float32)  18 us
    pallas_call x2, Pallas kernels, factor_inverse(): pl.pallas_call(factor_kernel, out_shape=jax.ShapeDtypeStruct(gram_matrix....  16.8 us
    ppermute x12, starting transfers between devices, shifted(): return lax.ppermute(block, axis, route)  16.1 us
    dot_general x8, matrix products, col_product(): lax.dot_general(affinity, weights, (((0,), (0,)), ((), ())), preferred_el...  11.3 us
    dot_general x8, matrix products, hdot(): jnp.dot(left, right, precision=lax.Precision.HIGHEST, preferred_element_t...  6.78 us
  transfers between devices with their start and end apart: 22, of which 15 were waited for; matrix products, arithmetic and copies ran while one was open for 25% of the time, Pallas kernels for 4%

profile of v15, /device:TPU:0, one launch (start us, length us, event | category | flops | bytes accessed | tf_op | source)
XLA Modules:
  0.0 227.4 jit_solution(13507169196477056907)
XLA Ops:
  0.6 1.9 copy.18
  2.5 6.0 %collective-permute-start.1 = (bf16[1024,64]{1,0:T(8,128)(2,1)}, bf16[1024,64]{1,0:T(8,128)(2,1)S(1)}, u32[]{:S(2)}, u32[]{:S(2)}) collective-permute-start(bf16[1024,64]{1,0:T(8,128)(2,1)} %copy.18), channel_id=1, source_target_pairs={{4,0},{8,4},{12,8},{16,12},{20,16},{24,20},{28,24},{0,28},{5,1},{9... | collective-permute-start | bytes 393224 | tf_op jit(solution)/shard_map/ppermute | solution.py:20
  8.5 2.7 %fusion.49 = (bf16[512,768]{1,0:T(8,128)(2,1)}, bf16[512,768]{1,0:T(8,128)(2,1)}) fusion(bf16[1024,768]{1,0:T(8,128)(2,1)} %param.21), kind=kLoop, calls=%fused_computation.144 | loop fusion | bytes 3145728 | tf_op jit(solution)/shard_map/slice | solution.py:312
  12.1 1.4 fusion.48
  13.4 2.3 %collective-permute-start = (bf16[512,768]{1,0:T(8,128)(2,1)}, bf16[512,768]{1,0:T(8,128)(2,1)}, u32[]{:S(2)}, u32[]{:S(2)}) collective-permute-start(bf16[512,768]{1,0:T(8,128)(2,1)} %get-tuple-element.256), channel_id=1, source_target_pairs={{4,0},{8,4},{12,8},{16,12},{20,16},{24,20},{28,24},{0,28},{5,1},{9... | collective-permute-start | bytes 2359304 | tf_op jit(solution)/shard_map/ppermute | solution.py:20
  15.8 2.5 %convert_reduce_fusion.10 = (f32[1024]{0:T(1024)}, bf16[1024,1024]{0,1:T(8,128)(2,1)S(1)}) fusion(bf16[1024,768]{1,0:T(8,128)(2,1)S(1)} %fusion.3), kind=kOutput, calls=%fused_computation.15 | convolution fusion | flops 1616903168 | bytes 3674112 | tf_op jit(solution)/shard_map/dot_general | solution.py:55
  21.2 3.0 %collective-permute-start.4 = (bf16[512,768]{1,0:T(8,128)(2,1)}, bf16[512,768]{1,0:T(8,128)(2,1)}, u32[]{:S(2)}, u32[]{:S(2)}) collective-permute-start(bf16[512,768]{1,0:T(8,128)(2,1)} %get-tuple-element.255), channel_id=1, source_target_pairs={{4,0},{8,4},{12,8},{16,12},{20,16},{24,20},{28,24},{0,28},{5,1},{9... | collective-permute-start | bytes 2359304 | tf_op jit(solution)/shard_map/ppermute | solution.py:20
  24.3 14.6 %collective-permute-done.3 = bf16[512,768]{1,0:T(8,128)(2,1)S(1)} collective-permute-done((bf16[512,768]{1,0:T(8,128)(2,1)}, bf16[512,768]{1,0:T(8,128)(2,1)S(1)}, u32[]{:S(2)}, u32[]{:S(2)}) %collective-permute-start.3) | collective-permute-done | bytes 786464 | tf_op jit(solution)/shard_map/ppermute | solution.py:20
  39.1 33.6 %collective-permute-done.2 = bf16[512,768]{1,0:T(8,128)(2,1)} collective-permute-done((bf16[512,768]{1,0:T(8,128)(2,1)}, bf16[512,768]{1,0:T(8,128)(2,1)}, u32[]{:S(2)}, u32[]{:S(2)}) %collective-permute-start.2) | collective-permute-done | bytes 786464 | tf_op jit(solution)/shard_map/ppermute | solution.py:20
  72.8 1.4 fusion.4
  74.4 1.5 fusion.6
  75.9 1.3 pad_maximum_fusion.2
  77.2 7.8 %conditional.9 = (bf16[1024,1024]{1,0:T(8,128)(2,1)}, f32[1024,64]{0,1:T(8,128)}, f32[1024]{0:T(1024)S(1)}, f32[1024]{0:T(1024)S(1)}) conditional(s32[]{:T(128)} %convert_element_type.83, () %tuple.83, (bf16[1024,768]{1,0:T(8,128)(2,1)}, bf16[1024,768]{1,0:T(8,128)(2,1)S(1)}, bf16[1024,64]{0,1:T(8,128)(2,1)S(1)}) %tuple.159), branch_computations={%region_4.5_spmd, %region_5.0_spmd} | conditional | flops 1750071296 | bytes 7741472 | solution.py:125
  77.2 4.7 %convert_reduce_fusion = (f32[1024]{0:T(1024)S(1)}, f32[1024]{0:T(1024)S(1)}, bf16[1024,1024]{1,0:T(8,128)(2,1)}) fusion(bf16[1024,768]{1,0:T(8,128)(2,1)} %get-tuple-element.65, bf16[1024,768]{1,0:T(8,128)(2,1)S(1)} %get-tuple-element.66), kind=kOutput, calls=%fused_computation | convolution fusion | flops 1615853568 | bytes 5251072 | tf_op jit(solution)/shard_map/cond/branch_1_fun/dot_general | solution.py:55
  81.9 3.1 %fusion.58 = f32[1024,64]{0,1:T(8,128)} fusion(bf16[1024,1024]{1,0:T(8,128)(2,1)} %get-tuple-element.272, bf16[1024,64]{0,1:T(8,128)(2,1)S(1)} %get-tuple-element.211), kind=kOutput, calls=%fused_computation.153 | convolution fusion | flops 134217728 | bytes 2490368 | tf_op jit(solution)/shard_map/cond/branch_1_fun/dot_general | solution.py:62
  85.0 2.5 %collective-permute-done.4 = bf16[512,768]{1,0:T(8,128)(2,1)} collective-permute-done((bf16[512,768]{1,0:T(8,128)(2,1)}, bf16[512,768]{1,0:T(8,128)(2,1)}, u32[]{:S(2)}, u32[]{:S(2)}) %collective-permute-start.4) | collective-permute-done | bytes 786464 | tf_op jit(solution)/shard_map/ppermute | solution.py:20
  87.5 7.0 %conditional.10 = (bf16[1024,512]{1,0:T(8,128)(2,1)}, f32[1024,64]{0,1:T(8,128)S(1)}, f32[1024]{0:T(1024)S(1)}, f32[512,64]{0,1:T(8,128)S(1)}, f32[512]{0:T(512)S(1)}) conditional(s32[]{:T(128)} %convert_element_type.88, () %tuple.85, (bf16[1024,768]{1,0:T(8,128)(2,1)}, bf16[512,768]{1,0:T(8,128)(2,1)}, bf16[512,64]{1,0:T(8,128)(2,1)S(1)}, ...), branch_computations={%region_9.10_spmd, %region_10.13_spmd} | conditional | flops 942144000 | bytes 6101032 | solution.py:166
  87.5 3.8 %convert_reduce_fusion.2 = (f32[512]{0:T(512)S(1)}, f32[1024]{0:T(1024)S(1)}, bf16[1024,512]{1,0:T(8,128)(2,1)}) fusion(bf16[1024,768]{1,0:T(8,128)(2,1)} %get-tuple-element.68, bf16[512,768]{1,0:T(8,128)(2,1)} %get-tuple-element.69), kind=kOutput, calls=%fused_computation.3 | convolution fusion | flops 807926272 | bytes 3414016 | tf_op jit(solution)/shard_map/cond/branch_1_fun/dot_general | solution.py:55
  91.3 1.7 fusion.59
  93.0 1.5 fusion.60
  95.2 6.9 %conditional.11 = (bf16[1024,512]{1,0:T(8,128)(2,1)}, f32[1024,64]{0,1:T(8,128)S(1)}, f32[1024]{0:T(1024)S(1)}, f32[512,64]{0,1:T(8,128)S(1)}, f32[512]{0:T(512)S(1)}) conditional(s32[]{:T(128)} %convert_element_type.89, () %tuple.87, (bf16[1024,768]{1,0:T(8,128)(2,1)}, bf16[512,768]{1,0:T(8,128)(2,1)}, bf16[512,64]{1,0:T(8,128)(2,1)S(1)}, ...), branch_computations={%region_14.15_spmd, %region_15.18_spmd} | conditional | flops 942144000 | bytes 6101032 | solution.py:166
  95.2 3.7 %convert_reduce_fusion.4 = (f32[512]{0:T(512)S(1)}, f32[1024]{0:T(1024)S(1)}, bf16[1024,512]{1,0:T(8,128)(2,1)}) fusion(bf16[1024,768]{1,0:T(8,128)(2,1)} %get-tuple-element.72, bf16[512,768]{1,0:T(8,128)(2,1)} %get-tuple-element.73), kind=kOutput, calls=%fused_computation.6 | convolution fusion | flops 807926272 | bytes 3414016 | tf_op jit(solution)/shard_map/cond/branch_1_fun/dot_general | solution.py:55
  98.9 1.7 fusion.61
  100.6 1.6 fusion.62
  103.7 7.0 %conditional.14 = (bf16[1024,512]{1,0:T(8,128)(2,1)}, f32[1024,64]{0,1:T(8,128)S(1)}, f32[1024]{0:T(1024)S(1)}, f32[512,64]{0,1:T(8,128)S(1)}, f32[4,128]{1,0:T(4,128)S(1)}) conditional(s32[]{:T(128)} %convert_element_type.89, () %tuple.94, (bf16[1024,768]{1,0:T(8,128)(2,1)}, bf16[512,768]{1,0:T(8,128)(2,1)}, bf16[512,64]{1,0:T(8,128)(2,1)S(1)}, ...), branch_computations={%region_24.25_spmd, %region_25.0_spmd} | conditional | flops 942144000 | bytes 6101032 | solution.py:166
  103.8 3.7 %convert_reduce_fusion.8 = (f32[512]{0:T(512)S(1)}, f32[1024]{0:T(1024)S(1)}, bf16[1024,512]{1,0:T(8,128)(2,1)}) fusion(bf16[1024,768]{1,0:T(8,128)(2,1)} %get-tuple-element.82, bf16[512,768]{1,0:T(8,128)(2,1)} %get-tuple-element.83), kind=kOutput, calls=%fused_computation.12 | convolution fusion | flops 807926272 | bytes 3414016 | tf_op jit(solution)/shard_map/cond/branch_1_fun/dot_general | solution.py:55
  107.5 1.7 fusion.65
  109.1 1.6 fusion.66
  114.0 7.7 %conditional.12 = (bf16[1024,512]{1,0:T(8,128)(2,1)}, f32[1024,64]{0,1:T(8,128)S(1)}, f32[1024]{0:T(1024)S(1)}, f32[512,64]{0,1:T(8,128)S(1)}, f32[4,128]{1,0:T(4,128)}) conditional(s32[]{:T(128)} %convert_element_type.88, () %tuple.90, (bf16[1024,768]{1,0:T(8,128)(2,1)}, bf16[512,768]{1,0:T(8,128)(2,1)}, bf16[512,64]{1,0:T(8,128)(2,1)S(1)}, ...), branch_computations={%region_18.19_spmd, %region_19.22_spmd} | conditional | flops 942144000 | bytes 6101032 | solution.py:166
  114.0 4.3 %convert_reduce_fusion.6 = (f32[512]{0:T(512)}, f32[1024]{0:T(1024)S(1)}, bf16[1024,512]{1,0:T(8,128)(2,1)}) fusion(bf16[1024,768]{1,0:T(8,128)(2,1)} %get-tuple-element.76, bf16[512,768]{1,0:T(8,128)(2,1)} %get-tuple-element.77), kind=kOutput, calls=%fused_computation.9 | convolution fusion | flops 807926272 | bytes 3414016 | tf_op jit(solution)/shard_map/cond/branch_1_fun/dot_general | solution.py:55
  118.3 1.7 fusion.63
  120.0 1.5 fusion.64
  125.0 2.1 conditional.13
  125.0 2.1 fusion.51
  128.6 6.7 %collective-permute-done.6 = f32[520,128]{1,0:T(8,128)S(1)} collective-permute-done((f32[520,128]{1,0:T(8,128)S(1)}, f32[520,128]{1,0:T(8,128)S(1)}, u32[]{:S(2)}, u32[]{:S(2)}) %collective-permute-start.6) | collective-permute-done | bytes 266272 | tf_op jit(solution)/shard_map/ppermute | solution.py:20
  135.8 1.3 broadcast_multiply_fusion
  139.3 1.2 collective-permute-done.10
  140.5 1.6 collective-permute-start.11
  142.1 2.3 %collective-permute-done.11 = f32[35,128]{1,0:T(8,128)S(1)} collective-permute-done((f32[35,128]{1,0:T(8,128)S(1)}, f32[35,128]{1,0:T(8,128)S(1)}, u32[]{:S(2)}, u32[]{:S(2)}) %collective-permute-start.11) | collective-permute-done | bytes 17952 | tf_op jit(solution)/shard_map/ppermute | solution.py:196
  144.5 3.8 %collective-permute-done.12 = f32[37,128]{1,0:T(8,128)S(1)} collective-permute-done((f32[37,128]{1,0:T(8,128)S(1)}, f32[37,128]{1,0:T(8,128)S(1)}, u32[]{:S(2)}, u32[]{:S(2)}) %collective-permute-start.12) | collective-permute-done | bytes 18976 | tf_op jit(solution)/shard_map/ppermute | solution.py:196
  148.3 1.2 collective-permute-start.13
  149.5 2.7 %collective-permute-done.13 = f32[41,128]{1,0:T(8,128)S(1)} collective-permute-done((f32[41,128]{1,0:T(8,128)S(1)}, f32[41,128]{1,0:T(8,128)S(1)}, u32[]{:S(2)}, u32[]{:S(2)}) %collective-permute-start.13) | collective-permute-done | bytes 21024 | tf_op jit(solution)/shard_map/ppermute | solution.py:196
  152.3 4.1 %pad_maximum_fusion = (bf16[1024,1024]{1,0:T(8,128)(2,1)S(1)}, bf16[1024,1024]{1,0:T(8,128)(2,1)}) fusion(bf16[1024,512]{1,0:T(8,128)(2,1)} %get-tuple-element.180, bf16[1024,512]{1,0:T(8,128)(2,1)} %get-tuple-element.179, bf16[1024,512]{1,0:T(8,128)(2,1)} %get-tuple-element.185, bf16[1024,512]{1,0:T(8,128)(2,1)} %get-tuple-element.184), kind=kLoop, calls=%fused_computation.25 | loop fusion | flops 8388608 | bytes 8388608 | tf_op jit(solution)/shard_map/concatenate | solution.py:384
  157.5 2.5 %collective-permute-start.8 = (f32[1024,64]{0,1:T(8,128)S(1)}, f32[1024,64]{0,1:T(8,128)S(1)}, u32[]{:S(2)}, u32[]{:S(2)}) collective-permute-start(f32[1024,64]{0,1:T(8,128)S(1)} %get-tuple-element.249), channel_id=1, source_target_pairs={{4,0},{8,4},{12,8},{16,12},{20,16},{24,20},{28,24},{0,28},{5,1},{9... | collective-permute-start | bytes 786440 | tf_op jit(solution)/shard_map/ppermute | solution.py:20
  162.5 8.4 %shard_map.50 = f32[64,64]{1,0:T(8,128)} custom-call(f32[64,64]{1,0:T(8,128)} %fusion.15.gram_ref), custom_call_target="tpu_custom_call" | custom-call | tf_op jit(solution)/shard_map/pallas_call | solution.py:244
  170.9 1.7 convolution_convert_fusion
  173.4 4.4 %conditional.16 = (f32[1024,64]{0,1:T(8,128)S(1)}, f32[1024,64]{0,1:T(8,128)S(1)}) conditional(s32[]{:T(128)} %convert_element_type.83, () %tuple.98, (bf16[1024,1024]{1,0:T(8,128)(2,1)}, bf16[1024,64]{0,1:T(8,128)(2,1)S(1)}, bf16[1024,64]{0,1:T(8,128)(2,1)S(1)}) %tuple.99), branch_computations={%region_35.36_spmd, %region_36.37_spmd} | conditional | flops 268435456 | bytes 4980752 | solution.py:180
  173.4 2.3 %fusion.54 = f32[1024,64]{0,1:T(8,128)S(1)} fusion(bf16[1024,1024]{1,0:T(8,128)(2,1)} %get-tuple-element.89, bf16[1024,64]{0,1:T(8,128)(2,1)S(1)} %get-tuple-element.224), kind=kOutput, calls=%fused_computation.149 | convolution fusion | flops 134217728 | bytes 2490368 | tf_op jit(solution)/shard_map/cond/branch_1_fun/dot_general | solution.py:62
  175.7 2.1 fusion.55
  177.8 3.0 %conditional.17 = (f32[1024,64]{0,1:T(8,128)S(1)}, f32[1024,64]{0,1:T(8,128)S(1)}) conditional(s32[]{:T(128)} %convert_element_type.89, () %tuple.100, (bf16[1024,1024]{1,0:T(8,128)(2,1)}, bf16[1024,64]{0,1:T(8,128)(2,1)S(1)}, bf16[1024,64]{0,1:T(8,128)(2,1)S(1)}) %tuple.101), branch_computations={%region_37.38_spmd, %region_38.39_spmd} | conditional | flops 268435456 | bytes 13369388 | solution.py:180
  177.8 2.5 %fusion.56 = f32[1024,64]{0,1:T(8,128)S(1)} fusion(bf16[1024,1024]{1,0:T(8,128)(2,1)} %get-tuple-element.92, bf16[1024,64]{0,1:T(8,128)(2,1)S(1)} %get-tuple-element.227), kind=kOutput, calls=%fused_computation.151 | convolution fusion | flops 134217728 | bytes 2490368 | tf_op jit(solution)/shard_map/cond/branch_1_fun/dot_general | solution.py:62
  181.6 1.2 conditional.15
  182.9 1.1 collective-permute-start.15
  184.0 4.3 %collective-permute-done.16 = f32[1024,64]{0,1:T(8,128)} collective-permute-done((f32[1024,64]{0,1:T(8,128)}, f32[1024,64]{0,1:T(8,128)}, u32[]{:S(2)}, u32[]{:S(2)}) %collective-permute-start.16) | collective-permute-done | bytes 262176 | tf_op jit(solution)/shard_map/ppermute | solution.py:20
  188.3 4.7 %collective-permute-done.15 = f32[1024,64]{0,1:T(8,128)S(1)} collective-permute-done((f32[1024,64]{0,1:T(8,128)S(1)}, f32[1024,64]{0,1:T(8,128)S(1)}, u32[]{:S(2)}, u32[]{:S(2)}) %collective-permute-start.15) | collective-permute-done | bytes 262176 | tf_op jit(solution)/shard_map/ppermute | solution.py:20
  192.9 2.2 fusion.43
  196.7 1.2 collective-permute-done.17
  197.9 2.0 collective-permute-start.18
  200.0 1.8 collective-permute-done.18
  201.9 3.8 %collective-permute-done.19 = f32[37,128]{1,0:T(8,128)S(1)} collective-permute-done((f32[37,128]{1,0:T(8,128)S(1)}, f32[37,128]{1,0:T(8,128)S(1)}, u32[]{:S(2)}, u32[]{:S(2)}) %collective-permute-start.19) | collective-permute-done | bytes 18976 | tf_op jit(solution)/shard_map/ppermute | solution.py:196
  205.9 3.7 %collective-permute-done.20 = f32[41,128]{1,0:T(8,128)S(1)} collective-permute-done((f32[41,128]{1,0:T(8,128)S(1)}, f32[41,128]{1,0:T(8,128)S(1)}, u32[]{:S(2)}, u32[]{:S(2)}) %collective-permute-start.20) | collective-permute-done | bytes 21024 | tf_op jit(solution)/shard_map/ppermute | solution.py:196
  210.5 4.0 %collective-permute-done.21 = f32[49,128]{1,0:T(8,128)S(1)} collective-permute-done((f32[49,128]{1,0:T(8,128)S(1)}, f32[49,128]{1,0:T(8,128)S(1)}, u32[]{:S(2)}, u32[]{:S(2)}) %collective-permute-start.21) | collective-permute-done | bytes 25120 | tf_op jit(solution)/shard_map/ppermute | solution.py:196
  217.0 8.4 %shard_map.51 = f32[64,64]{1,0:T(8,128)} custom-call(f32[64,64]{1,0:T(8,128)} %fusion.13.gram_ref), custom_call_target="tpu_custom_call" | custom-call | tf_op jit(solution)/shard_map/pallas_call | solution.py:244
  225.4 1.9 fusion.21
  (179 shorter events, 27.4 us)
Async XLA Ops:
  0.6 10.6 %copy-start.1 = (bf16[1024,768]{1,0:T(8,128)(2,1)S(1)}, bf16[1024,768]{1,0:T(8,128)(2,1)}, u32[]{:S(2)}) copy-start(bf16[1024,768]{1,0:T(8,128)(2,1)} %param.21) | copy-start | bytes 4718596
  2.5 18.7 %collective-permute-start.1 = (bf16[1024,64]{1,0:T(8,128)(2,1)}, bf16[1024,64]{1,0:T(8,128)(2,1)S(1)}, u32[]{:S(2)}, u32[]{:S(2)}) collective-permute-start(bf16[1024,64]{1,0:T(8,128)(2,1)} %copy.18), channel_id=1, source_target_pairs={{4,0},{8,4},{12,8},{16,12},{20,16},{24,20},{28,24},{0,28},{5,1},{9... | collective-permute-start | bytes 393224 | tf_op jit(solution)/shard_map/ppermute | solution.py:20
  8.5 86.0 %collective-permute-start.5 = (bf16[1024,64]{1,0:T(8,128)(2,1)}, bf16[1024,64]{1,0:T(8,128)(2,1)S(1)}, u32[]{:S(2)}, u32[]{:S(2)}) collective-permute-start(bf16[1024,64]{1,0:T(8,128)(2,1)} %copy.18), channel_id=1, source_target_pairs={{24,0},{28,4},{0,8},{4,12},{8,16},{12,20},{16,24},{20,28},{25,1},{... | collective-permute-start | bytes 393224 | tf_op jit(solution)/shard_map/ppermute | solution.py:20
  11.2 27.7 %collective-permute-start.3 = (bf16[512,768]{1,0:T(8,128)(2,1)}, bf16[512,768]{1,0:T(8,128)(2,1)S(1)}, u32[]{:S(2)}, u32[]{:S(2)}) collective-permute-start(bf16[512,768]{1,0:T(8,128)(2,1)} %get-tuple-element.258), channel_id=1, source_target_pairs={{24,0},{28,4},{0,8},{4,12},{8,16},{12,20},{16,24},{20,28},{25,1},{... | collective-permute-start | bytes 2359304 | tf_op jit(solution)/shard_map/ppermute | solution.py:20
  12.0 6.2 %copy-start.3 = (bf16[1024,768]{1,0:T(8,128)(2,1)}, bf16[1024,768]{1,0:T(8,128)(2,1)S(1)}, u32[]{:S(2)}) copy-start(bf16[1024,768]{1,0:T(8,128)(2,1)S(1)} %fusion.3) | copy-start | bytes 4718596
  13.4 88.7 %collective-permute-start = (bf16[512,768]{1,0:T(8,128)(2,1)}, bf16[512,768]{1,0:T(8,128)(2,1)}, u32[]{:S(2)}, u32[]{:S(2)}) collective-permute-start(bf16[512,768]{1,0:T(8,128)(2,1)} %get-tuple-element.256), channel_id=1, source_target_pairs={{4,0},{8,4},{12,8},{16,12},{20,16},{24,20},{28,24},{0,28},{5,1},{9... | collective-permute-start | bytes 2359304 | tf_op jit(solution)/shard_map/ppermute | solution.py:20
  15.7 2.5 %copy-start.25 = (s32[32,3]{0,1:T(4,128)S(1)}, s32[32,3]{0,1:T(4,128)}, u32[]{:S(2)}) copy-start(s32[32,3]{0,1:T(4,128)} %param.23) | copy-start | bytes 1156
  15.8 57.0 %collective-permute-start.2 = (bf16[512,768]{1,0:T(8,128)(2,1)}, bf16[512,768]{1,0:T(8,128)(2,1)}, u32[]{:S(2)}, u32[]{:S(2)}) collective-permute-start(bf16[512,768]{1,0:T(8,128)(2,1)} %get-tuple-element.257), channel_id=1, source_target_pairs={{24,0},{28,4},{0,8},{4,12},{8,16},{12,20},{16,24},{20,28},{25,1},{... | collective-permute-start | bytes 2359304 | tf_op jit(solution)/shard_map/ppermute | solution.py:20
  18.3 106.2 %copy-start.2 = (bf16[1024,1024]{0,1:T(8,128)(2,1)}, bf16[1024,1024]{0,1:T(8,128)(2,1)S(1)}, u32[]{:S(2)}) copy-start(bf16[1024,1024]{0,1:T(8,128)(2,1)S(1)} %get-tuple-element.263) | copy-start | bytes 6291460
  21.2 54.7 %copy-start.16 = (bf16[1024,64]{1,0:T(8,128)(2,1)}, bf16[1024,64]{1,0:T(8,128)(2,1)S(1)}, u32[]{:S(2)}) copy-start(bf16[1024,64]{1,0:T(8,128)(2,1)S(1)} %collective-permute-done.1) | copy-start | bytes 393220
  21.2 66.3 %collective-permute-start.4 = (bf16[512,768]{1,0:T(8,128)(2,1)}, bf16[512,768]{1,0:T(8,128)(2,1)}, u32[]{:S(2)}, u32[]{:S(2)}) collective-permute-start(bf16[512,768]{1,0:T(8,128)(2,1)} %get-tuple-element.255), channel_id=1, source_target_pairs={{4,0},{8,4},{12,8},{16,12},{20,16},{24,20},{28,24},{0,28},{5,1},{9... | collective-permute-start | bytes 2359304 | tf_op jit(solution)/shard_map/ppermute | solution.py:20
  74.4 2.8 %copy-start.4 = (bf16[1024,768]{1,0:T(8,128)(2,1)S(1)}, bf16[1024,768]{1,0:T(8,128)(2,1)}, u32[]{:S(2)}) copy-start(bf16[1024,768]{1,0:T(8,128)(2,1)} %copy-done.3) | copy-start | bytes 4718596
  74.4 2.8 %copy-start.5 = (bf16[1024,64]{0,1:T(8,128)(2,1)S(1)}, bf16[1024,64]{0,1:T(8,128)(2,1)}, u32[]{:S(2)}) copy-start(bf16[1024,64]{0,1:T(8,128)(2,1)} %param.22) | copy-start | bytes 393220
  85.0 2.5 %copy-start.17 = (f32[1024]{0:T(1024)}, f32[1024]{0:T(1024)S(1)}, u32[]{:S(2)}) copy-start(f32[1024]{0:T(1024)S(1)} %get-tuple-element.178) | copy-start | bytes 12292
  94.5 0.6 copy-start.19
  94.5 0.7 copy-start.6
  102.2 0.7 copy-start.11
  102.2 1.6 copy-start.21
  110.7 0.7 copy-start.13
  111.4 0.6 copy-start.23
  114.0 8.4 %copy-start.12 = (f32[512,64]{0,1:T(8,128)S(1)}, f32[512,64]{0,1:T(8,128)}, u32[]{:S(2)}) copy-start(f32[512,64]{0,1:T(8,128)} %copy-done.11) | copy-start | bytes 393220
  114.0 8.4 %copy-start.14 = (f32[512,64]{0,1:T(8,128)S(1)}, f32[512,64]{0,1:T(8,128)}, u32[]{:S(2)}) copy-start(f32[512,64]{0,1:T(8,128)} %copy-done.13) | copy-start | bytes 393220
  114.0 13.2 %collective-permute-start.7 = (f32[520,128]{1,0:T(8,128)}, f32[520,128]{1,0:T(8,128)}, u32[]{:S(2)}, u32[]{:S(2)}) collective-permute-start(f32[520,128]{1,0:T(8,128)} %pad_maximum_fusion.4), channel_id=1, source_target_pairs={{8,0},{12,4},{16,8},{20,12},{24,16},{28,20},{0,24},{4,28},{9,1},{1... | collective-permute-start | bytes 798728 | tf_op jit(solution)/shard_map/ppermute | solution.py:20
  121.7 0.7 copy-start.15
  121.7 0.7 copy-start.8
  121.7 2.0 copy-start.20
  121.7 2.0 copy-start.22
  121.7 2.0 copy-start.24
  124.4 10.8 %collective-permute-start.6 = (f32[520,128]{1,0:T(8,128)S(1)}, f32[520,128]{1,0:T(8,128)S(1)}, u32[]{:S(2)}, u32[]{:S(2)}) collective-permute-start(f32[520,128]{1,0:T(8,128)S(1)} %pad_maximum_fusion.3), channel_id=1, source_target_pairs={{28,0},{0,4},{4,8},{8,12},{12,16},{16,20},{20,24},{24,28},{29,1},{... | collective-permute-start | bytes 798728 | tf_op jit(solution)/shard_map/ppermute | solution.py:20
  127.1 8.5 %copy-start.7 = (f32[1024,64]{0,1:T(8,128)S(1)}, f32[1024,64]{0,1:T(8,128)}, u32[]{:S(2)}) copy-start(f32[1024,64]{0,1:T(8,128)} %copy-done.6) | copy-start | bytes 786436
  127.2 8.5 %copy-start.9 = (f32[1024,64]{0,1:T(8,128)S(1)}, f32[1024,64]{0,1:T(8,128)}, u32[]{:S(2)}) copy-start(f32[1024,64]{0,1:T(8,128)} %copy-done.8) | copy-start | bytes 786436
  128.5 7.3 %copy-start.18 = (f32[1024]{0:T(1024)S(1)}, f32[1024]{0:T(1024)}, u32[]{:S(2)}) copy-start(f32[1024]{0:T(1024)} %copy-done.17) | copy-start | bytes 12292
  128.6 7.2 %copy-start.26 = (f32[1024]{0:T(1024)S(1)}, f32[1024]{0:T(1024)}, u32[]{:S(2)}) copy-start(f32[1024]{0:T(1024)} %get-tuple-element.262) | copy-start | bytes 12292
  139.2 1.3 collective-permute-start.10
  140.5 3.8 %collective-permute-start.11 = (f32[35,128]{1,0:T(8,128)S(1)}, f32[35,128]{1,0:T(8,128)S(1)}, u32[]{:S(2)}, u32[]{:S(2)}) collective-permute-start(f32[35,128]{1,0:T(8,128)S(1)} %pad_maximum_fusion.10), channel_id=1, source_target_pairs={{0,2},{1,3},{2,0},{3,1},{4,6},{5,7},{6,4},{7,5},{8,10},{9,11},{10,... | collective-permute-start | bytes 53768 | tf_op jit(solution)/shard_map/ppermute | solution.py:196
  144.4 3.8 %collective-permute-start.12 = (f32[37,128]{1,0:T(8,128)S(1)}, f32[37,128]{1,0:T(8,128)S(1)}, u32[]{:S(2)}, u32[]{:S(2)}) collective-permute-start(f32[37,128]{1,0:T(8,128)S(1)} %pad_maximum_fusion.11), channel_id=1, source_target_pairs={{0,4},{4,0},{8,12},{12,8},{16,20},{20,16},{24,28},{28,24},{1,5},{5... | collective-permute-start | bytes 56840 | tf_op jit(solution)/shard_map/ppermute | solution.py:196
  148.3 3.9 %collective-permute-start.13 = (f32[41,128]{1,0:T(8,128)S(1)}, f32[41,128]{1,0:T(8,128)S(1)}, u32[]{:S(2)}, u32[]{:S(2)}) collective-permute-start(f32[41,128]{1,0:T(8,128)S(1)} %pad_maximum_fusion.7), channel_id=1, source_target_pairs={{0,8},{4,12},{8,0},{12,4},{16,24},{20,28},{24,16},{28,20},{1,9},{5... | collective-permute-start | bytes 62984 | tf_op jit(solution)/shard_map/ppermute | solution.py:196
  152.2 7.7 %collective-permute-start.14 = (f32[49,128]{1,0:T(8,128)S(1)}, f32[49,128]{1,0:T(8,128)S(1)}, u32[]{:S(2)}, u32[]{:S(2)}) collective-permute-start(f32[49,128]{1,0:T(8,128)S(1)} %pad_maximum_fusion.5), channel_id=1, source_target_pairs={{0,16},{4,20},{8,24},{12,28},{16,0},{20,4},{24,8},{28,12},{1,17},{... | collective-permute-start | bytes 75272 | tf_op jit(solution)/shard_map/ppermute | solution.py:196
  156.4 14.5 %collective-permute-start.9 = (f32[1024,64]{0,1:T(8,128)S(1)}, f32[1024,64]{0,1:T(8,128)S(1)}, u32[]{:S(2)}, u32[]{:S(2)}) collective-permute-start(f32[1024,64]{0,1:T(8,128)S(1)} %get-tuple-element.249), channel_id=1, source_target_pairs={{24,0},{28,4},{0,8},{4,12},{8,16},{12,20},{16,24},{20,28},{25,1},{... | collective-permute-start | bytes 786440 | tf_op jit(solution)/shard_map/ppermute | solution.py:20
  157.5 13.4 %collective-permute-start.8 = (f32[1024,64]{0,1:T(8,128)S(1)}, f32[1024,64]{0,1:T(8,128)S(1)}, u32[]{:S(2)}, u32[]{:S(2)}) collective-permute-start(f32[1024,64]{0,1:T(8,128)S(1)} %get-tuple-element.249), channel_id=1, source_target_pairs={{4,0},{8,4},{12,8},{16,12},{20,16},{24,20},{28,24},{0,28},{5,1},{9... | collective-permute-start | bytes 786440 | tf_op jit(solution)/shard_map/ppermute | solution.py:20
  172.6 0.8 copy-start.10
  177.8 2.5 %copy-start = (bf16[1024,1024]{1,0:T(8,128)(2,1)S(1)}, bf16[1024,1024]{1,0:T(8,128)(2,1)}, u32[]{:S(2)}) copy-start(bf16[1024,1024]{1,0:T(8,128)(2,1)} %get-tuple-element.92) | copy-start | bytes 6291460 | tf_op jit(solution)/shard_map/cond
  181.6 6.7 %collective-permute-start.16 = (f32[1024,64]{0,1:T(8,128)}, f32[1024,64]{0,1:T(8,128)}, u32[]{:S(2)}, u32[]{:S(2)}) collective-permute-start(f32[1024,64]{0,1:T(8,128)} %add.263), channel_id=1, source_target_pairs={{8,0},{12,4},{16,8},{20,12},{24,16},{28,20},{0,24},{4,28},{9,1},{1... | collective-permute-start | bytes 786440 | tf_op jit(solution)/shard_map/ppermute | solution.py:20
  182.9 10.1 %collective-permute-start.15 = (f32[1024,64]{0,1:T(8,128)S(1)}, f32[1024,64]{0,1:T(8,128)S(1)}, u32[]{:S(2)}, u32[]{:S(2)}) collective-permute-start(f32[1024,64]{0,1:T(8,128)S(1)} %add.261), channel_id=1, source_target_pairs={{28,0},{0,4},{4,8},{8,12},{12,16},{16,20},{20,24},{24,28},{29,1},{... | collective-permute-start | bytes 786440 | tf_op jit(solution)/shard_map/ppermute | solution.py:20
  196.6 1.3 collective-permute-start.17
  197.9 3.8 %collective-permute-start.18 = (f32[35,128]{1,0:T(8,128)S(1)}, f32[35,128]{1,0:T(8,128)S(1)}, u32[]{:S(2)}, u32[]{:S(2)}) collective-permute-start(f32[35,128]{1,0:T(8,128)S(1)} %pad_maximum_fusion.13), channel_id=1, source_target_pairs={{0,2},{1,3},{2,0},{3,1},{4,6},{5,7},{6,4},{7,5},{8,10},{9,11},{10,... | collective-permute-start | bytes 53768 | tf_op jit(solution)/shard_map/ppermute | solution.py:196
  201.8 3.8 %collective-permute-start.19 = (f32[37,128]{1,0:T(8,128)S(1)}, f32[37,128]{1,0:T(8,128)S(1)}, u32[]{:S(2)}, u32[]{:S(2)}) collective-permute-start(f32[37,128]{1,0:T(8,128)S(1)} %pad_maximum_fusion.14), channel_id=1, source_target_pairs={{0,4},{4,0},{8,12},{12,8},{16,20},{20,16},{24,28},{28,24},{1,5},{5... | collective-permute-start | bytes 56840 | tf_op jit(solution)/shard_map/ppermute | solution.py:196
  205.7 3.9 %collective-permute-start.20 = (f32[41,128]{1,0:T(8,128)S(1)}, f32[41,128]{1,0:T(8,128)S(1)}, u32[]{:S(2)}, u32[]{:S(2)}) collective-permute-start(f32[41,128]{1,0:T(8,128)S(1)} %pad_maximum_fusion.8), channel_id=1, source_target_pairs={{0,8},{4,12},{8,0},{12,4},{16,24},{20,28},{24,16},{28,20},{1,9},{5... | collective-permute-start | bytes 62984 | tf_op jit(solution)/shard_map/ppermute | solution.py:196
  209.6 4.8 %collective-permute-start.21 = (f32[49,128]{1,0:T(8,128)S(1)}, f32[49,128]{1,0:T(8,128)S(1)}, u32[]{:S(2)}, u32[]{:S(2)}) collective-permute-start(f32[49,128]{1,0:T(8,128)S(1)} %pad_maximum_fusion.6), channel_id=1, source_target_pairs={{0,16},{4,20},{8,24},{12,28},{16,0},{20,4},{24,8},{28,12},{1,17},{... | collective-permute-start | bytes 75272 | tf_op jit(solution)/shard_map/ppermute | solution.py:196

commit v16 on v13

--- a/solution.py
+++ b/solution.py
@@ -263,7 +263,7 @@
     summed_rows = summed.shape[0]
     block = jnp.concatenate([summed, as_rows(jnp.concatenate([centre, local_drift]))])
     gather_width = block.shape[0] - summed_rows
-    for axis in ("narrow", "wide"):
+    for axis in ("wide", "narrow"):
         block = butterfly(axis, summed_rows, block)
     totals = block[:summed_rows].reshape(-1)
     gram_sum = totals[: vector_count * vector_count].reshape(vector_count, vector_count)

time: 220 us -> 223 us (1.014); the launches traced: 218 us -> 225 us
  matrix products: 30.8 us -> 44.4 us
  waiting for transfers between devices: 80.9 us -> 74.9 us
    ppermute x11, waiting for transfers between devices: 58.7 us -> 47.9 us  [shifted(): return lax.ppermute(block, axis, route)]
    ppermute x11, starting transfers between devices: 31.3 us -> 36.5 us  [shifted(): return lax.ppermute(block, axis, route)]
    ppermute x10, waiting for transfers between devices: 22.2 us -> 27 us  [butterfly(): other = lax.ppermute(block, axis, route)]
    dot_general x3 -> x4, matrix products: 11.9 us -> 16.6 us  [scores_tile(): lax.dot_general(leftside_block, right_block, (((1,), (1,)), ((), ())), pr...]
    dot_general x5 -> x7, matrix products: 8.54 us -> 13.2 us  [row_product(): return jnp.dot(affinity, weights, preferred_element_type=jnp.float32)]
    ppermute x10, starting transfers between devices: 13.4 us -> 9.02 us  [butterfly(): other = lax.ppermute(block, axis, route)]
    dot_general x3 -> x5, matrix products: 3.62 us -> 7.8 us  [col_product(): lax.dot_general(affinity, weights, (((0,), (0,)), ((), ())), preferred_el...]
    another operation x18 -> x11, local copies, waits for them, and re-layouts: 5.21 us -> 3.56 us
  transfers between devices with their start and end apart: 21 -> 21, of which waited for: 14 -> 13; matrix products, arithmetic and copies ran while one was open for 18% -> 20% of each run, Pallas kernels for 4% -> 4%
where the time goes in v16:
time: 223 us; the launch traced here: 225 us
  waiting for transfers between devices  74.9 us (34%)
  starting transfers between devices  45.5 us (20%)
  matrix products  44.4 us (20%)
  other arithmetic  23.9 us (11%)
  Pallas kernels  16.8 us (8%)
  local copies, waits for them, and re-layouts  16.1 us (7%)
  between operations  3.12 us (1%)
    ppermute x11, waiting for transfers between devices, shifted(): return lax.ppermute(block, axis, route)  47.9 us
    ppermute x11, starting transfers between devices, shifted(): return lax.ppermute(block, axis, route)  36.5 us
    ppermute x10, waiting for transfers between devices, butterfly(): other = lax.ppermute(block, axis, route)  27 us
    pallas_call x2, Pallas kernels, factor_inverse(): pl.pallas_call(factor_kernel, out_shape=jax.ShapeDtypeStruct(gram_matrix....  16.8 us
    dot_general x4, matrix products, scores_tile(): lax.dot_general(leftside_block, right_block, (((1,), (1,)), ((), ())), pr...  16.6 us
    dot_general x7, matrix products, row_product(): return jnp.dot(affinity, weights, preferred_element_type=jnp.float32)  13.2 us
    ppermute x10, starting transfers between devices, butterfly(): other = lax.ppermute(block, axis, route)  9.02 us
    dot_general x5, matrix products, col_product(): lax.dot_general(affinity, weights, (((0,), (0,)), ((), ())), preferred_el...  7.8 us
  transfers between devices with their start and end apart: 21, of which 13 were waited for; matrix products, arithmetic and copies ran while one was open for 20% of the time, Pallas kernels for 4%

profile of v16, /device:TPU:0, one launch (start us, length us, event | category | flops | bytes accessed | tf_op | source)
XLA Modules:
  0.0 224.9 jit_solution(13126229936392674169)
XLA Ops:
  0.6 3.1 %collective-permute-start.2 = (bf16[1024,768]{1,0:T(8,128)(2,1)}, bf16[1024,768]{1,0:T(8,128)(2,1)}, u32[]{:S(2)}, u32[]{:S(2)}) collective-permute-start(bf16[1024,768]{1,0:T(8,128)(2,1)} %param.21), channel_id=1, source_target_pairs={{24,0},{28,4},{0,8},{4,12},{8,16},{12,20},{16,24},{20,28},{25,1},{... | collective-permute-start | bytes 4718600 | tf_op jit(solution)/shard_map/ppermute | solution.py:20
  3.7 1.8 fusion.1
  6.0 1.1 copy-done.3
  7.1 1.1 fusion.45
  8.2 3.3 %collective-permute-start.3 = (bf16[512,768]{1,0:T(8,128)(2,1)S(1)}, bf16[512,768]{1,0:T(8,128)(2,1)}, u32[]{:S(2)}, u32[]{:S(2)}) collective-permute-start(bf16[512,768]{1,0:T(8,128)(2,1)S(1)} %get-tuple-element.255), channel_id=1, source_target_pairs={{4,0},{8,4},{12,8},{16,12},{20,16},{24,20},{28,24},{0,28},{5,1},{9... | collective-permute-start | bytes 2359304 | tf_op jit(solution)/shard_map/ppermute | solution.py:20
  12.7 5.0 %collective-permute-start = (bf16[512,768]{1,0:T(8,128)(2,1)}, bf16[512,768]{1,0:T(8,128)(2,1)}, u32[]{:S(2)}, u32[]{:S(2)}) collective-permute-start(bf16[512,768]{1,0:T(8,128)(2,1)} %get-tuple-element.256), channel_id=1, source_target_pairs={{4,0},{8,4},{12,8},{16,12},{20,16},{24,20},{28,24},{0,28},{5,1},{9... | collective-permute-start | bytes 2359304 | tf_op jit(solution)/shard_map/ppermute | solution.py:20
  17.7 4.4 %convert_reduce_fusion.10 = (f32[1024]{0:T(1024)}, bf16[1024,1024]{0,1:T(8,128)(2,1)S(1)}) fusion(bf16[1024,768]{1,0:T(8,128)(2,1)} %copy-done.3), kind=kOutput, calls=%fused_computation.15 | convolution fusion | flops 1616903168 | bytes 3674112 | tf_op jit(solution)/shard_map/dot_general | solution.py:55
  22.1 1.0 compare_reduce_fusion
  24.8 36.5 %collective-permute-done.1 = bf16[1024,64]{1,0:T(8,128)(2,1)} collective-permute-done((bf16[1024,64]{1,0:T(8,128)(2,1)}, bf16[1024,64]{1,0:T(8,128)(2,1)}, u32[]{:S(2)}, u32[]{:S(2)}) %collective-permute-start.1) | collective-permute-done | bytes 131104 | tf_op jit(solution)/shard_map/ppermute | solution.py:20
  62.3 2.5 %conditional.10 = (bf16[1024,512]{1,0:T(8,128)(2,1)}, f32[1024,64]{0,1:T(8,128)}, f32[1024]{0:T(1024)S(1)}, f32[512,64]{0,1:T(8,128)}, f32[512]{0:T(512)S(1)}) conditional(s32[]{:T(128)} %convert_element_type.80, () %tuple.85, (bf16[1024,768]{1,0:T(8,128)(2,1)}, bf16[512,768]{1,0:T(8,128)(2,1)}, bf16[512,64]{1,0:T(8,128)(2,1)S(1)}, ...), branch_computations={%region_8.9_spmd, %region_9.12_spmd} | conditional | flops 942144000 | bytes 6101032 | solution.py:166
  62.3 1.1 broadcast.148
  64.7 1.9 fusion.4
  66.7 3.0 %fusion.6 = bf16[1024,768]{1,0:T(8,128)(2,1)} fusion(bf16[1024,768]{1,0:T(8,128)(2,1)} %collective-permute-done.2, f32[1024]{0:T(1024)S(1)} %add_rsqrt_fusion), kind=kLoop, calls=%fused_computation.29 | loop fusion | flops 3145728 | bytes 3149824 | tf_op jit(solution)/shard_map/convert_element_type | solution.py:51
  69.7 7.1 %conditional.9 = (bf16[1024,1024]{1,0:T(8,128)(2,1)}, f32[1024,64]{0,1:T(8,128)S(1)}, f32[1024]{0:T(1024)S(1)}, f32[1024]{0:T(1024)S(1)}) conditional(s32[]{:T(128)} %convert_element_type.77, () %tuple.83, (bf16[1024,768]{1,0:T(8,128)(2,1)}, bf16[1024,768]{1,0:T(8,128)(2,1)S(1)}, bf16[1024,64]{0,1:T(8,128)(2,1)S(1)}) %tuple.159), branch_computations={%region_3.4_spmd, %region_4.0_spmd} | conditional | flops 1750071296 | bytes 7741472 | solution.py:125
  69.7 4.7 %convert_reduce_fusion = (f32[1024]{0:T(1024)S(1)}, f32[1024]{0:T(1024)S(1)}, bf16[1024,1024]{1,0:T(8,128)(2,1)}) fusion(bf16[1024,768]{1,0:T(8,128)(2,1)} %get-tuple-element.65, bf16[1024,768]{1,0:T(8,128)(2,1)S(1)} %get-tuple-element.66), kind=kOutput, calls=%fused_computation | convolution fusion | flops 1615853568 | bytes 5251072 | tf_op jit(solution)/shard_map/cond/branch_1_fun/dot_general | solution.py:55
  74.4 2.3 %fusion.54 = f32[1024,64]{0,1:T(8,128)S(1)} fusion(bf16[1024,1024]{1,0:T(8,128)(2,1)} %get-tuple-element.270, bf16[1024,64]{0,1:T(8,128)(2,1)S(1)} %get-tuple-element.211), kind=kOutput, calls=%fused_computation.145 | convolution fusion | flops 134217728 | bytes 2490368 | tf_op jit(solution)/shard_map/cond/branch_1_fun/dot_general | solution.py:62
  77.4 6.9 %conditional.11 = (bf16[1024,512]{1,0:T(8,128)(2,1)}, f32[1024,64]{0,1:T(8,128)S(1)}, f32[1024]{0:T(1024)S(1)}, f32[512,64]{0,1:T(8,128)S(1)}, f32[512]{0:T(512)S(1)}) conditional(s32[]{:T(128)} %convert_element_type.81, () %tuple.87, (bf16[1024,768]{1,0:T(8,128)(2,1)}, bf16[512,768]{1,0:T(8,128)(2,1)}, bf16[512,64]{1,0:T(8,128)(2,1)S(1)}, ...), branch_computations={%region_13.14_spmd, %region_14.17_spmd} | conditional | flops 942144000 | bytes 6101032 | solution.py:166
  77.4 3.7 %convert_reduce_fusion.4 = (f32[512]{0:T(512)S(1)}, f32[1024]{0:T(1024)S(1)}, bf16[1024,512]{1,0:T(8,128)(2,1)}) fusion(bf16[1024,768]{1,0:T(8,128)(2,1)} %get-tuple-element.72, bf16[512,768]{1,0:T(8,128)(2,1)} %get-tuple-element.73), kind=kOutput, calls=%fused_computation.6 | convolution fusion | flops 807926272 | bytes 3414016 | tf_op jit(solution)/shard_map/cond/branch_1_fun/dot_general | solution.py:55
  81.1 1.7 fusion.57
  82.8 1.6 fusion.58
  84.4 1.0 slice.141
  85.4 7.0 %conditional.14 = (bf16[1024,512]{1,0:T(8,128)(2,1)}, f32[1024,64]{0,1:T(8,128)S(1)}, f32[1024]{0:T(1024)S(1)}, f32[512,64]{0,1:T(8,128)S(1)}, f32[4,128]{1,0:T(4,128)S(1)}) conditional(s32[]{:T(128)} %convert_element_type.81, () %tuple.94, (bf16[1024,768]{1,0:T(8,128)(2,1)}, bf16[512,768]{1,0:T(8,128)(2,1)}, bf16[512,64]{1,0:T(8,128)(2,1)S(1)}, ...), branch_computations={%region_23.24_spmd, %region_24.0_spmd} | conditional | flops 942144000 | bytes 6101032 | solution.py:166
  85.4 3.8 %convert_reduce_fusion.8 = (f32[512]{0:T(512)S(1)}, f32[1024]{0:T(1024)S(1)}, bf16[1024,512]{1,0:T(8,128)(2,1)}) fusion(bf16[1024,768]{1,0:T(8,128)(2,1)} %get-tuple-element.82, bf16[512,768]{1,0:T(8,128)(2,1)} %get-tuple-element.83), kind=kOutput, calls=%fused_computation.12 | convolution fusion | flops 807926272 | bytes 3414016 | tf_op jit(solution)/shard_map/cond/branch_1_fun/dot_general | solution.py:55
  89.2 1.7 fusion.61
  90.8 1.6 fusion.62
  93.1 1.0 add_add_fusion
  95.2 9.6 %collective-permute-start.6 = (f32[520,128]{1,0:T(8,128)}, f32[520,128]{1,0:T(8,128)}, u32[]{:S(2)}, u32[]{:S(2)}) collective-permute-start(f32[520,128]{1,0:T(8,128)} %pad_maximum_fusion.3), channel_id=1, source_target_pairs={{8,0},{12,4},{16,8},{20,12},{24,16},{28,20},{0,24},{4,28},{9,1},{1... | collective-permute-start | bytes 798728 | tf_op jit(solution)/shard_map/ppermute | solution.py:20
  104.8 1.1 conditional.12
  104.8 1.0 broadcast.160
  106.4 0.9 maximum_add_fusion
  109.1 7.7 %collective-permute-start.5 = (f32[520,128]{1,0:T(8,128)}, f32[520,128]{1,0:T(8,128)}, u32[]{:S(2)}, u32[]{:S(2)}) collective-permute-start(f32[520,128]{1,0:T(8,128)} %pad_maximum_fusion.2), channel_id=1, source_target_pairs={{28,0},{0,4},{4,8},{8,12},{12,16},{16,20},{20,24},{24,28},{29,1},{... | collective-permute-start | bytes 798728 | tf_op jit(solution)/shard_map/ppermute | solution.py:20
  117.3 2.1 conditional.13
  117.4 2.1 fusion.47
  119.5 1.0 slice.185
  121.2 1.0 slice.184
  122.5 1.1 fusion.43
  123.7 1.3 broadcast_multiply_fusion
  127.3 2.5 %collective-permute-start.9 = (f32[34,128]{1,0:T(8,128)S(1)}, f32[34,128]{1,0:T(8,128)S(1)}, u32[]{:S(2)}, u32[]{:S(2)}) collective-permute-start(f32[34,128]{1,0:T(8,128)S(1)} %pad_maximum_fusion.8), channel_id=1, source_target_pairs={{0,4},{4,0},{8,12},{12,8},{16,20},{20,16},{24,28},{28,24},{1,5},{5... | collective-permute-start | bytes 52232 | tf_op jit(solution)/shard_map/ppermute | solution.py:196
  129.8 1.8 collective-permute-done.9
  131.6 1.8 collective-permute-start.10
  133.4 2.1 collective-permute-done.10
  135.6 4.6 %collective-permute-done.11 = f32[37,128]{1,0:T(8,128)S(1)} collective-permute-done((f32[37,128]{1,0:T(8,128)S(1)}, f32[37,128]{1,0:T(8,128)S(1)}, u32[]{:S(2)}, u32[]{:S(2)}) %collective-permute-start.11) | collective-permute-done | bytes 18976 | tf_op jit(solution)/shard_map/ppermute | solution.py:196
  140.4 1.1 collective-permute-done.12
  141.6 4.3 %collective-permute-start.13 = (f32[49,128]{1,0:T(8,128)S(1)}, f32[49,128]{1,0:T(8,128)S(1)}, u32[]{:S(2)}, u32[]{:S(2)}) collective-permute-start(f32[49,128]{1,0:T(8,128)S(1)} %pad_maximum_fusion.4), channel_id=1, source_target_pairs={{0,2},{1,3},{2,0},{3,1},{4,6},{5,7},{6,4},{7,5},{8,10},{9,11},{10,... | collective-permute-start | bytes 75272 | tf_op jit(solution)/shard_map/ppermute | solution.py:196
  145.9 4.1 %pad_maximum_fusion = (bf16[1024,1024]{1,0:T(8,128)(2,1)S(1)}, bf16[1024,1024]{1,0:T(8,128)(2,1)}) fusion(bf16[1024,512]{1,0:T(8,128)(2,1)} %get-tuple-element.180, bf16[1024,512]{1,0:T(8,128)(2,1)} %get-tuple-element.179, bf16[1024,512]{1,0:T(8,128)(2,1)} %get-tuple-element.185, bf16[1024,512]{1,0:T(8,128)(2,1)} %get-tuple-element.184), kind=kLoop, calls=%fused_computation.30 | loop fusion | flops 8388608 | bytes 8388608 | tf_op jit(solution)/shard_map/concatenate | solution.py:379
  150.0 3.2 %collective-permute-start.7 = (f32[1024,64]{0,1:T(8,128)S(1)}, f32[1024,64]{0,1:T(8,128)S(1)}, u32[]{:S(2)}, u32[]{:S(2)}) collective-permute-start(f32[1024,64]{0,1:T(8,128)S(1)} %get-tuple-element.249), channel_id=1, source_target_pairs={{4,0},{8,4},{12,8},{16,12},{20,16},{24,20},{28,24},{0,28},{5,1},{9... | collective-permute-start | bytes 786440 | tf_op jit(solution)/shard_map/ppermute | solution.py:20
  155.8 8.4 %shard_map.50 = f32[64,64]{1,0:T(8,128)} custom-call(f32[64,64]{1,0:T(8,128)} %fusion.12.gram_ref), custom_call_target="tpu_custom_call" | custom-call | tf_op jit(solution)/shard_map/pallas_call | solution.py:244
  164.2 1.7 convolution_convert_fusion
  166.7 4.4 %conditional.16 = (f32[1024,64]{0,1:T(8,128)S(1)}, f32[1024,64]{0,1:T(8,128)S(1)}) conditional(s32[]{:T(128)} %convert_element_type.77, () %tuple.98, (bf16[1024,1024]{1,0:T(8,128)(2,1)}, bf16[1024,64]{0,1:T(8,128)(2,1)S(1)}, bf16[1024,64]{0,1:T(8,128)(2,1)S(1)}) %tuple.99), branch_computations={%region_34.35_spmd, %region_35.36_spmd} | conditional | flops 268435456 | bytes 4980752 | solution.py:180
  166.7 2.3 %fusion.50 = f32[1024,64]{0,1:T(8,128)S(1)} fusion(bf16[1024,1024]{1,0:T(8,128)(2,1)} %get-tuple-element.89, bf16[1024,64]{0,1:T(8,128)(2,1)S(1)} %get-tuple-element.224), kind=kOutput, calls=%fused_computation.141 | convolution fusion | flops 134217728 | bytes 2490368 | tf_op jit(solution)/shard_map/cond/branch_1_fun/dot_general | solution.py:62
  169.0 2.1 fusion.51
  171.1 3.0 %conditional.17 = (f32[1024,64]{0,1:T(8,128)S(1)}, f32[1024,64]{0,1:T(8,128)S(1)}) conditional(s32[]{:T(128)} %convert_element_type.81, () %tuple.100, (bf16[1024,1024]{1,0:T(8,128)(2,1)}, bf16[1024,64]{0,1:T(8,128)(2,1)S(1)}, bf16[1024,64]{0,1:T(8,128)(2,1)S(1)}) %tuple.101), branch_computations={%region_36.37_spmd, %region_37.38_spmd} | conditional | flops 268435456 | bytes 13369388 | solution.py:180
  171.1 2.5 %fusion.52 = f32[1024,64]{0,1:T(8,128)S(1)} fusion(bf16[1024,1024]{1,0:T(8,128)(2,1)} %get-tuple-element.92, bf16[1024,64]{0,1:T(8,128)(2,1)S(1)} %get-tuple-element.227), kind=kOutput, calls=%fused_computation.143 | convolution fusion | flops 134217728 | bytes 2490368 | tf_op jit(solution)/shard_map/cond/branch_1_fun/dot_general | solution.py:62
  175.8 3.4 %collective-permute-start.14 = (f32[1024,64]{0,1:T(8,128)S(1)}, f32[1024,64]{0,1:T(8,128)S(1)}, u32[]{:S(2)}, u32[]{:S(2)}) collective-permute-start(f32[1024,64]{0,1:T(8,128)S(1)} %add.248), channel_id=1, source_target_pairs={{28,0},{0,4},{4,8},{8,12},{12,16},{16,20},{20,24},{24,28},{29,1},{... | collective-permute-start | bytes 786440 | tf_op jit(solution)/shard_map/ppermute | solution.py:20
  179.2 2.3 %collective-permute-done.15 = f32[1024,64]{0,1:T(8,128)} collective-permute-done((f32[1024,64]{0,1:T(8,128)}, f32[1024,64]{0,1:T(8,128)}, u32[]{:S(2)}, u32[]{:S(2)}) %collective-permute-start.15) | collective-permute-done | bytes 262176 | tf_op jit(solution)/shard_map/ppermute | solution.py:20
  181.6 8.6 %collective-permute-done.14 = f32[1024,64]{0,1:T(8,128)S(1)} collective-permute-done((f32[1024,64]{0,1:T(8,128)S(1)}, f32[1024,64]{0,1:T(8,128)S(1)}, u32[]{:S(2)}, u32[]{:S(2)}) %collective-permute-start.14) | collective-permute-done | bytes 262176 | tf_op jit(solution)/shard_map/ppermute | solution.py:20
  190.2 2.2 %fusion.40 = (f32[64]{0:T(128)S(1)}, f32[1024,64]{0,1:T(8,128)S(1)}) fusion(f32[1024]{0:T(1024)S(1)} %get-tuple-element.245, f32[1024,64]{0,1:T(8,128)} %collective-permute-done.15, f32[1024,64]{0,1:T(8,128)S(1)} %collective-permute-done.14, f32[1024,64]{0,1:T(8,128)S(1)} %get-tuple-element.181, f32[1024,64]{0,1:T(8,128)S(1)} %get-tuple-element.182, ...), kind=kOutput, calls=%fused_computation.132 | convolution fusion | flops 134610880 | bytes 3543296 | tf_op jit(solution)/shard_map/dot_general | solution.py:62
  194.1 3.8 %collective-permute-done.16 = f32[34,128]{1,0:T(8,128)S(1)} collective-permute-done((f32[34,128]{1,0:T(8,128)S(1)}, f32[34,128]{1,0:T(8,128)S(1)}, u32[]{:S(2)}, u32[]{:S(2)}) %collective-permute-start.16) | collective-permute-done | bytes 17440 | tf_op jit(solution)/shard_map/ppermute | solution.py:196
  198.0 3.9 %collective-permute-done.17 = f32[35,128]{1,0:T(8,128)S(1)} collective-permute-done((f32[35,128]{1,0:T(8,128)S(1)}, f32[35,128]{1,0:T(8,128)S(1)}, u32[]{:S(2)}, u32[]{:S(2)}) %collective-permute-start.17) | collective-permute-done | bytes 17952 | tf_op jit(solution)/shard_map/ppermute | solution.py:196
  202.1 4.7 %collective-permute-done.18 = f32[37,128]{1,0:T(8,128)S(1)} collective-permute-done((f32[37,128]{1,0:T(8,128)S(1)}, f32[37,128]{1,0:T(8,128)S(1)}, u32[]{:S(2)}, u32[]{:S(2)}) %collective-permute-start.18) | collective-permute-done | bytes 18976 | tf_op jit(solution)/shard_map/ppermute | solution.py:196
  206.8 1.2 collective-permute-done.19
  208.1 3.9 %collective-permute-done.20 = f32[49,128]{1,0:T(8,128)S(1)} collective-permute-done((f32[49,128]{1,0:T(8,128)S(1)}, f32[49,128]{1,0:T(8,128)S(1)}, u32[]{:S(2)}, u32[]{:S(2)}) %collective-permute-start.20) | collective-permute-done | bytes 25120 | tf_op jit(solution)/shard_map/ppermute | solution.py:196
  214.5 8.4 %shard_map.51 = f32[64,64]{1,0:T(8,128)} custom-call(f32[64,64]{1,0:T(8,128)} %fusion.10.gram_ref), custom_call_target="tpu_custom_call" | custom-call | tf_op jit(solution)/shard_map/pallas_call | solution.py:244
  223.0 1.9 fusion.18
  (156 shorter events, 22.8 us)
Async XLA Ops:
  0.6 4.9 %copy-start.2 = (bf16[1024,768]{1,0:T(8,128)(2,1)S(1)}, bf16[1024,768]{1,0:T(8,128)(2,1)}, u32[]{:S(2)}) copy-start(bf16[1024,768]{1,0:T(8,128)(2,1)} %param.21) | copy-start | bytes 4718596
  0.6 64.1 %collective-permute-start.2 = (bf16[1024,768]{1,0:T(8,128)(2,1)}, bf16[1024,768]{1,0:T(8,128)(2,1)}, u32[]{:S(2)}, u32[]{:S(2)}) collective-permute-start(bf16[1024,768]{1,0:T(8,128)(2,1)} %param.21), channel_id=1, source_target_pairs={{24,0},{28,4},{0,8},{4,12},{8,16},{12,20},{16,24},{20,28},{25,1},{... | collective-permute-start | bytes 4718600 | tf_op jit(solution)/shard_map/ppermute | solution.py:20
  6.0 1.2 copy-start.3
  7.1 4.4 %copy-start.5 = (bf16[1024,64]{0,1:T(8,128)(2,1)S(1)}, bf16[1024,64]{0,1:T(8,128)(2,1)}, u32[]{:S(2)}) copy-start(bf16[1024,64]{0,1:T(8,128)(2,1)} %param.22) | copy-start | bytes 393220
  8.2 54.0 %collective-permute-start.3 = (bf16[512,768]{1,0:T(8,128)(2,1)S(1)}, bf16[512,768]{1,0:T(8,128)(2,1)}, u32[]{:S(2)}, u32[]{:S(2)}) collective-permute-start(bf16[512,768]{1,0:T(8,128)(2,1)S(1)} %get-tuple-element.255), channel_id=1, source_target_pairs={{4,0},{8,4},{12,8},{16,12},{20,16},{24,20},{28,24},{0,28},{5,1},{9... | collective-permute-start | bytes 2359304 | tf_op jit(solution)/shard_map/ppermute | solution.py:20
  12.4 49.0 %collective-permute-start.1 = (bf16[1024,64]{1,0:T(8,128)(2,1)}, bf16[1024,64]{1,0:T(8,128)(2,1)}, u32[]{:S(2)}, u32[]{:S(2)}) collective-permute-start(bf16[1024,64]{1,0:T(8,128)(2,1)} %copy.18), channel_id=1, source_target_pairs={{4,0},{8,4},{12,8},{16,12},{20,16},{24,20},{28,24},{0,28},{5,1},{9... | collective-permute-start | bytes 393224 | tf_op jit(solution)/shard_map/ppermute | solution.py:20
  12.7 64.1 %collective-permute-start.4 = (bf16[1024,64]{1,0:T(8,128)(2,1)}, bf16[1024,64]{1,0:T(8,128)(2,1)S(1)}, u32[]{:S(2)}, u32[]{:S(2)}) collective-permute-start(bf16[1024,64]{1,0:T(8,128)(2,1)} %copy.18), channel_id=1, source_target_pairs={{24,0},{28,4},{0,8},{4,12},{8,16},{12,20},{16,24},{20,28},{25,1},{... | collective-permute-start | bytes 393224 | tf_op jit(solution)/shard_map/ppermute | solution.py:20
  12.7 9.4 %copy-start.15 = (s32[32,3]{0,1:T(4,128)S(1)}, s32[32,3]{0,1:T(4,128)}, u32[]{:S(2)}) copy-start(s32[32,3]{0,1:T(4,128)} %param.23) | copy-start | bytes 1156
  12.7 71.7 %collective-permute-start = (bf16[512,768]{1,0:T(8,128)(2,1)}, bf16[512,768]{1,0:T(8,128)(2,1)}, u32[]{:S(2)}, u32[]{:S(2)}) collective-permute-start(bf16[512,768]{1,0:T(8,128)(2,1)} %get-tuple-element.256), channel_id=1, source_target_pairs={{4,0},{8,4},{12,8},{16,12},{20,16},{24,20},{28,24},{0,28},{5,1},{9... | collective-permute-start | bytes 2359304 | tf_op jit(solution)/shard_map/ppermute | solution.py:20
  22.1 94.8 %copy-start.1 = (bf16[1024,1024]{0,1:T(8,128)(2,1)}, bf16[1024,1024]{0,1:T(8,128)(2,1)S(1)}, u32[]{:S(2)}) copy-start(bf16[1024,1024]{0,1:T(8,128)(2,1)S(1)} %get-tuple-element.261) | copy-start | bytes 6291460
  64.7 4.9 %copy-start.4 = (bf16[1024,768]{1,0:T(8,128)(2,1)S(1)}, bf16[1024,768]{1,0:T(8,128)(2,1)}, u32[]{:S(2)}) copy-start(bf16[1024,768]{1,0:T(8,128)(2,1)} %copy-done.3) | copy-start | bytes 4718596
  76.7 0.7 copy-start.6
  84.4 1.0 copy-start.8
  84.4 1.0 copy-start.12
  92.4 0.7 copy-start.10
  92.4 12.3 %copy-start.13 = (f32[4,128]{1,0:T(4,128)}, f32[4,128]{1,0:T(4,128)S(1)}, u32[]{:S(2)}) copy-start(f32[4,128]{1,0:T(4,128)S(1)} %get-tuple-element.169) | copy-start | bytes 6148
  95.2 11.3 %copy-start.9 = (f32[512,64]{0,1:T(8,128)S(1)}, f32[512,64]{0,1:T(8,128)}, u32[]{:S(2)}) copy-start(f32[512,64]{0,1:T(8,128)} %copy-done.8) | copy-start | bytes 393220
  95.2 11.3 %copy-start.11 = (f32[512,64]{0,1:T(8,128)S(1)}, f32[512,64]{0,1:T(8,128)}, u32[]{:S(2)}) copy-start(f32[512,64]{0,1:T(8,128)} %copy-done.10) | copy-start | bytes 393220
  95.2 24.3 %collective-permute-start.6 = (f32[520,128]{1,0:T(8,128)}, f32[520,128]{1,0:T(8,128)}, u32[]{:S(2)}, u32[]{:S(2)}) collective-permute-start(f32[520,128]{1,0:T(8,128)} %pad_maximum_fusion.3), channel_id=1, source_target_pairs={{8,0},{12,4},{16,8},{20,12},{24,16},{28,20},{0,24},{4,28},{9,1},{1... | collective-permute-start | bytes 798728 | tf_op jit(solution)/shard_map/ppermute | solution.py:20
  105.9 0.5 copy-start.14
  109.1 12.1 %collective-permute-start.5 = (f32[520,128]{1,0:T(8,128)}, f32[520,128]{1,0:T(8,128)}, u32[]{:S(2)}, u32[]{:S(2)}) collective-permute-start(f32[520,128]{1,0:T(8,128)} %pad_maximum_fusion.2), channel_id=1, source_target_pairs={{28,0},{0,4},{4,8},{8,12},{12,16},{16,20},{20,24},{24,28},{29,1},{... | collective-permute-start | bytes 798728 | tf_op jit(solution)/shard_map/ppermute | solution.py:20
  120.8 2.9 %copy-start.16 = (f32[1024]{0:T(1024)S(1)}, f32[1024]{0:T(1024)}, u32[]{:S(2)}) copy-start(f32[1024]{0:T(1024)} %get-tuple-element.260) | copy-start | bytes 12292
  127.3 4.2 %collective-permute-start.9 = (f32[34,128]{1,0:T(8,128)S(1)}, f32[34,128]{1,0:T(8,128)S(1)}, u32[]{:S(2)}, u32[]{:S(2)}) collective-permute-start(f32[34,128]{1,0:T(8,128)S(1)} %pad_maximum_fusion.8), channel_id=1, source_target_pairs={{0,4},{4,0},{8,12},{12,8},{16,20},{20,16},{24,28},{28,24},{1,5},{5... | collective-permute-start | bytes 52232 | tf_op jit(solution)/shard_map/ppermute | solution.py:196
  131.6 3.8 %collective-permute-start.10 = (f32[35,128]{1,0:T(8,128)S(1)}, f32[35,128]{1,0:T(8,128)S(1)}, u32[]{:S(2)}, u32[]{:S(2)}) collective-permute-start(f32[35,128]{1,0:T(8,128)S(1)} %pad_maximum_fusion.9), channel_id=1, source_target_pairs={{0,8},{4,12},{8,0},{12,4},{16,24},{20,28},{24,16},{28,20},{1,9},{5... | collective-permute-start | bytes 53768 | tf_op jit(solution)/shard_map/ppermute | solution.py:196
  135.5 4.7 %collective-permute-start.11 = (f32[37,128]{1,0:T(8,128)S(1)}, f32[37,128]{1,0:T(8,128)S(1)}, u32[]{:S(2)}, u32[]{:S(2)}) collective-permute-start(f32[37,128]{1,0:T(8,128)S(1)} %pad_maximum_fusion.10), channel_id=1, source_target_pairs={{0,16},{4,20},{8,24},{12,28},{16,0},{20,4},{24,8},{28,12},{1,17},{... | collective-permute-start | bytes 56840 | tf_op jit(solution)/shard_map/ppermute | solution.py:196
  140.3 1.3 collective-permute-start.12
  141.6 11.7 %collective-permute-start.13 = (f32[49,128]{1,0:T(8,128)S(1)}, f32[49,128]{1,0:T(8,128)S(1)}, u32[]{:S(2)}, u32[]{:S(2)}) collective-permute-start(f32[49,128]{1,0:T(8,128)S(1)} %pad_maximum_fusion.4), channel_id=1, source_target_pairs={{0,2},{1,3},{2,0},{3,1},{4,6},{5,7},{6,4},{7,5},{8,10},{9,11},{10,... | collective-permute-start | bytes 75272 | tf_op jit(solution)/shard_map/ppermute | solution.py:196
  150.0 14.2 %collective-permute-start.8 = (f32[1024,64]{0,1:T(8,128)S(1)}, f32[1024,64]{0,1:T(8,128)S(1)}, u32[]{:S(2)}, u32[]{:S(2)}) collective-permute-start(f32[1024,64]{0,1:T(8,128)S(1)} %get-tuple-element.249), channel_id=1, source_target_pairs={{24,0},{28,4},{0,8},{4,12},{8,16},{12,20},{16,24},{20,28},{25,1},{... | collective-permute-start | bytes 786440 | tf_op jit(solution)/shard_map/ppermute | solution.py:20
  150.0 14.2 %collective-permute-start.7 = (f32[1024,64]{0,1:T(8,128)S(1)}, f32[1024,64]{0,1:T(8,128)S(1)}, u32[]{:S(2)}, u32[]{:S(2)}) collective-permute-start(f32[1024,64]{0,1:T(8,128)S(1)} %get-tuple-element.249), channel_id=1, source_target_pairs={{4,0},{8,4},{12,8},{16,12},{20,16},{24,20},{28,24},{0,28},{5,1},{9... | collective-permute-start | bytes 786440 | tf_op jit(solution)/shard_map/ppermute | solution.py:20
  165.9 0.8 copy-start.7
  171.1 2.5 %copy-start = (bf16[1024,1024]{1,0:T(8,128)(2,1)S(1)}, bf16[1024,1024]{1,0:T(8,128)(2,1)}, u32[]{:S(2)}) copy-start(bf16[1024,1024]{1,0:T(8,128)(2,1)} %get-tuple-element.92) | copy-start | bytes 6291460 | tf_op jit(solution)/shard_map/cond
  174.9 6.7 %collective-permute-start.15 = (f32[1024,64]{0,1:T(8,128)}, f32[1024,64]{0,1:T(8,128)}, u32[]{:S(2)}, u32[]{:S(2)}) collective-permute-start(f32[1024,64]{0,1:T(8,128)} %add.250), channel_id=1, source_target_pairs={{8,0},{12,4},{16,8},{20,12},{24,16},{28,20},{0,24},{4,28},{9,1},{1... | collective-permute-start | bytes 786440 | tf_op jit(solution)/shard_map/ppermute | solution.py:20
  175.8 14.4 %collective-permute-start.14 = (f32[1024,64]{0,1:T(8,128)S(1)}, f32[1024,64]{0,1:T(8,128)S(1)}, u32[]{:S(2)}, u32[]{:S(2)}) collective-permute-start(f32[1024,64]{0,1:T(8,128)S(1)} %add.248), channel_id=1, source_target_pairs={{28,0},{0,4},{4,8},{8,12},{12,16},{16,20},{20,24},{24,28},{29,1},{... | collective-permute-start | bytes 786440 | tf_op jit(solution)/shard_map/ppermute | solution.py:20
  194.0 3.8 %collective-permute-start.16 = (f32[34,128]{1,0:T(8,128)S(1)}, f32[34,128]{1,0:T(8,128)S(1)}, u32[]{:S(2)}, u32[]{:S(2)}) collective-permute-start(f32[34,128]{1,0:T(8,128)S(1)} %pad_maximum_fusion.11), channel_id=1, source_target_pairs={{0,4},{4,0},{8,12},{12,8},{16,20},{20,16},{24,28},{28,24},{1,5},{5... | collective-permute-start | bytes 52232 | tf_op jit(solution)/shard_map/ppermute | solution.py:196
  197.9 4.0 %collective-permute-start.17 = (f32[35,128]{1,0:T(8,128)S(1)}, f32[35,128]{1,0:T(8,128)S(1)}, u32[]{:S(2)}, u32[]{:S(2)}) collective-permute-start(f32[35,128]{1,0:T(8,128)S(1)} %pad_maximum_fusion.12), channel_id=1, source_target_pairs={{0,8},{4,12},{8,0},{12,4},{16,24},{20,28},{24,16},{28,20},{1,9},{5... | collective-permute-start | bytes 53768 | tf_op jit(solution)/shard_map/ppermute | solution.py:196
  202.0 4.7 %collective-permute-start.18 = (f32[37,128]{1,0:T(8,128)S(1)}, f32[37,128]{1,0:T(8,128)S(1)}, u32[]{:S(2)}, u32[]{:S(2)}) collective-permute-start(f32[37,128]{1,0:T(8,128)S(1)} %pad_maximum_fusion.13), channel_id=1, source_target_pairs={{0,16},{4,20},{8,24},{12,28},{16,0},{20,4},{24,8},{28,12},{1,17},{... | collective-permute-start | bytes 56840 | tf_op jit(solution)/shard_map/ppermute | solution.py:196
  206.8 1.3 collective-permute-start.19
  208.1 3.9 %collective-permute-start.20 = (f32[49,128]{1,0:T(8,128)S(1)}, f32[49,128]{1,0:T(8,128)S(1)}, u32[]{:S(2)}, u32[]{:S(2)}) collective-permute-start(f32[49,128]{1,0:T(8,128)S(1)} %pad_maximum_fusion.5), channel_id=1, source_target_pairs={{0,2},{1,3},{2,0},{3,1},{4,6},{5,7},{6,4},{7,5},{8,10},{9,11},{10,... | collective-permute-start | bytes 75272 | tf_op jit(solution)/shard_map/ppermute | solution.py:196

commit v17 on v13

--- a/solution.py
+++ b/solution.py
@@ -223,12 +223,12 @@
 
     def step(j, carry):
         remaining, inverse = carry
+        pivot_row = jnp.sum(jnp.where(rows == j, remaining, 0.0), axis=0, keepdims=True)
+        pivot = jnp.sum(jnp.where(cols[:1] == j, pivot_row, 0.0), axis=1, keepdims=True)
         column = jnp.sum(jnp.where(cols == j, remaining, 0.0), axis=1, keepdims=True)
-        pivot = jnp.sum(jnp.where(rows[:, :1] == j, column, 0.0), axis=0, keepdims=True)
         scale = lax.rsqrt(pivot)
         factor_column = jnp.where(rows[:, :1] >= j, column * scale, 0.0)
-        factor_row = jnp.sum(jnp.where(rows == j, remaining, 0.0), axis=0, keepdims=True)
-        factor_row = jnp.where(cols[:1] >= j, factor_row * scale, 0.0)
+        factor_row = jnp.where(cols[:1] >= j, pivot_row * scale, 0.0)
         remaining = remaining - factor_column * factor_row
         inverse_row = jnp.sum(jnp.where(rows == j, inverse, 0.0), axis=0, keepdims=True) * scale
         inverse = jnp.where(rows == j, inverse_row, inverse)

time: 220 us -> 219 us (level)
  matrix products: 30.8 us -> 60.8 us
  starting transfers between devices: 44.7 us -> 23.6 us
  local copies, waits for them, and re-layouts: 17.7 us -> 12.5 us
  waiting for transfers between devices: 80.9 us -> 77.2 us
    dot_general x3 -> x6, matrix products: 11.9 us -> 24 us  [scores_tile(): lax.dot_general(leftside_block, right_block, (((1,), (1,)), ((), ())), pr...]
    ppermute x11, starting transfers between devices: 31.3 us -> 20.2 us  [shifted(): return lax.ppermute(block, axis, route)]
    ppermute x10, starting transfers between devices: 13.4 us -> 3.47 us  [butterfly(): other = lax.ppermute(block, axis, route)]
    dot_general x5 -> x10, matrix products: 8.54 us -> 18 us  [row_product(): return jnp.dot(affinity, weights, preferred_element_type=jnp.float32)]
    ppermute x11, waiting for transfers between devices: 58.7 us -> 50.2 us  [shifted(): return lax.ppermute(block, axis, route)]
    dot_general x3 -> x8, matrix products: 3.62 us -> 12 us  [col_product(): lax.dot_general(affinity, weights, (((0,), (0,)), ((), ())), preferred_el...]
    another operation x18 -> x0, local copies, waits for them, and re-layouts: 5.21 us -> none
    ppermute x10, waiting for transfers between devices: 22.2 us -> 27 us  [butterfly(): other = lax.ppermute(block, axis, route)]
  transfers between devices with their start and end apart: 21 -> 21, of which waited for: 14 -> 13; matrix products, arithmetic and copies ran while one was open for 18% -> 27% of each run, Pallas kernels for 4% -> 4%
where the time goes in v17:
time: 219 us; the launch traced here: 218 us
  waiting for transfers between devices  77.2 us (35%)
  matrix products  60.8 us (28%)
  other arithmetic  23.9 us (11%)
  starting transfers between devices  23.6 us (11%)
  Pallas kernels  16.9 us (8%)
  local copies, waits for them, and re-layouts  12.5 us (6%)
  between operations  3.16 us (1%)
    ppermute x11, waiting for transfers between devices, shifted(): return lax.ppermute(block, axis, route)  50.2 us
    ppermute x10, waiting for transfers between devices, butterfly(): other = lax.ppermute(block, axis, route)  27 us
    dot_general x6, matrix products, scores_tile(): lax.dot_general(leftside_block, right_block, (((1,), (1,)), ((), ())), pr...  24 us
    ppermute x11, starting transfers between devices, shifted(): return lax.ppermute(block, axis, route)  20.2 us
    dot_general x10, matrix products, row_product(): return jnp.dot(affinity, weights, preferred_element_type=jnp.float32)  18 us
    pallas_call x2, Pallas kernels, factor_inverse(): pl.pallas_call(factor_kernel, out_shape=jax.ShapeDtypeStruct(gram_matrix....  16.9 us
    dot_general x8, matrix products, col_product(): lax.dot_general(affinity, weights, (((0,), (0,)), ((), ())), preferred_el...  12 us
    dot_general x8, matrix products, hdot(): jnp.dot(left, right, precision=lax.Precision.HIGHEST, preferred_element_t...  6.78 us
  transfers between devices with their start and end apart: 21, of which 13 were waited for; matrix products, arithmetic and copies ran while one was open for 27% of the time, Pallas kernels for 4%

profile of v17, /device:TPU:0, one launch (start us, length us, event | category | flops | bytes accessed | tf_op | source)
XLA Modules:
  0.0 218.2 jit_solution(17544038614199845783)
XLA Ops:
  0.6 3.1 %collective-permute-start.2 = (bf16[1024,768]{1,0:T(8,128)(2,1)}, bf16[1024,768]{1,0:T(8,128)(2,1)}, u32[]{:S(2)}, u32[]{:S(2)}) collective-permute-start(bf16[1024,768]{1,0:T(8,128)(2,1)} %param.21), channel_id=1, source_target_pairs={{24,0},{28,4},{0,8},{4,12},{8,16},{12,20},{16,24},{20,28},{25,1},{... | collective-permute-start | bytes 4718600 | tf_op jit(solution)/shard_map/ppermute | solution.py:20
  3.7 1.8 fusion.1
  6.0 1.1 copy-done.3
  7.1 1.1 fusion.45
  8.2 3.3 %collective-permute-start.3 = (bf16[512,768]{1,0:T(8,128)(2,1)S(1)}, bf16[512,768]{1,0:T(8,128)(2,1)}, u32[]{:S(2)}, u32[]{:S(2)}) collective-permute-start(bf16[512,768]{1,0:T(8,128)(2,1)S(1)} %get-tuple-element.255), channel_id=1, source_target_pairs={{4,0},{8,4},{12,8},{16,12},{20,16},{24,20},{28,24},{0,28},{5,1},{9... | collective-permute-start | bytes 2359304 | tf_op jit(solution)/shard_map/ppermute | solution.py:20
  12.7 5.0 %collective-permute-start = (bf16[512,768]{1,0:T(8,128)(2,1)}, bf16[512,768]{1,0:T(8,128)(2,1)}, u32[]{:S(2)}, u32[]{:S(2)}) collective-permute-start(bf16[512,768]{1,0:T(8,128)(2,1)} %get-tuple-element.256), channel_id=1, source_target_pairs={{4,0},{8,4},{12,8},{16,12},{20,16},{24,20},{28,24},{0,28},{5,1},{9... | collective-permute-start | bytes 2359304 | tf_op jit(solution)/shard_map/ppermute | solution.py:20
  17.7 4.4 %convert_reduce_fusion.10 = (f32[1024]{0:T(1024)}, bf16[1024,1024]{0,1:T(8,128)(2,1)S(1)}) fusion(bf16[1024,768]{1,0:T(8,128)(2,1)} %copy-done.3), kind=kOutput, calls=%fused_computation.15 | convolution fusion | flops 1616903168 | bytes 3674112 | tf_op jit(solution)/shard_map/dot_general | solution.py:55
  22.1 1.0 compare_reduce_fusion
  24.8 36.5 %collective-permute-done.1 = bf16[1024,64]{1,0:T(8,128)(2,1)} collective-permute-done((bf16[1024,64]{1,0:T(8,128)(2,1)}, bf16[1024,64]{1,0:T(8,128)(2,1)}, u32[]{:S(2)}, u32[]{:S(2)}) %collective-permute-start.1) | collective-permute-done | bytes 131104 | tf_op jit(solution)/shard_map/ppermute | solution.py:20
  62.3 8.3 %conditional.10 = (bf16[1024,512]{1,0:T(8,128)(2,1)}, f32[1024,64]{0,1:T(8,128)}, f32[1024]{0:T(1024)S(1)}, f32[512,64]{0,1:T(8,128)}, f32[512]{0:T(512)S(1)}) conditional(s32[]{:T(128)} %convert_element_type.80, () %tuple.85, (bf16[1024,768]{1,0:T(8,128)(2,1)}, bf16[512,768]{1,0:T(8,128)(2,1)}, bf16[512,64]{1,0:T(8,128)(2,1)S(1)}, ...), branch_computations={%region_8.9_spmd, %region_9.12_spmd} | conditional | flops 942144000 | bytes 6101032 | solution.py:166
  62.3 3.7 %convert_reduce_fusion.2 = (f32[512]{0:T(512)S(1)}, f32[1024]{0:T(1024)S(1)}, bf16[1024,512]{1,0:T(8,128)(2,1)}) fusion(bf16[1024,768]{1,0:T(8,128)(2,1)} %get-tuple-element.68, bf16[512,768]{1,0:T(8,128)(2,1)} %get-tuple-element.69), kind=kOutput, calls=%fused_computation.3 | convolution fusion | flops 807926272 | bytes 3414016 | tf_op jit(solution)/shard_map/cond/branch_1_fun/dot_general | solution.py:55
  66.0 2.4 %fusion.55 = f32[1024,64]{0,1:T(8,128)} fusion(bf16[1024,512]{1,0:T(8,128)(2,1)} %get-tuple-element.279, bf16[512,64]{1,0:T(8,128)(2,1)S(1)} %get-tuple-element.70), kind=kOutput, calls=%fused_computation.146 | convolution fusion | flops 67108864 | bytes 1376256 | tf_op jit(solution)/shard_map/cond/branch_1_fun/dot_general | solution.py:62
  68.4 2.2 fusion.56
  70.6 1.9 fusion.4
  72.5 3.0 %fusion.6 = bf16[1024,768]{1,0:T(8,128)(2,1)} fusion(bf16[1024,768]{1,0:T(8,128)(2,1)} %collective-permute-done.2, f32[1024]{0:T(1024)S(1)} %add_rsqrt_fusion), kind=kLoop, calls=%fused_computation.29 | loop fusion | flops 3145728 | bytes 3149824 | tf_op jit(solution)/shard_map/convert_element_type | solution.py:51
  75.5 7.1 %conditional.9 = (bf16[1024,1024]{1,0:T(8,128)(2,1)}, f32[1024,64]{0,1:T(8,128)S(1)}, f32[1024]{0:T(1024)S(1)}, f32[1024]{0:T(1024)S(1)}) conditional(s32[]{:T(128)} %convert_element_type.77, () %tuple.83, (bf16[1024,768]{1,0:T(8,128)(2,1)}, bf16[1024,768]{1,0:T(8,128)(2,1)S(1)}, bf16[1024,64]{0,1:T(8,128)(2,1)S(1)}) %tuple.159), branch_computations={%region_3.4_spmd, %region_4.0_spmd} | conditional | flops 1750071296 | bytes 7741472 | solution.py:125
  75.5 4.7 %convert_reduce_fusion = (f32[1024]{0:T(1024)S(1)}, f32[1024]{0:T(1024)S(1)}, bf16[1024,1024]{1,0:T(8,128)(2,1)}) fusion(bf16[1024,768]{1,0:T(8,128)(2,1)} %get-tuple-element.65, bf16[1024,768]{1,0:T(8,128)(2,1)S(1)} %get-tuple-element.66), kind=kOutput, calls=%fused_computation | convolution fusion | flops 1615853568 | bytes 5251072 | tf_op jit(solution)/shard_map/cond/branch_1_fun/dot_general | solution.py:55
  80.2 2.3 %fusion.54 = f32[1024,64]{0,1:T(8,128)S(1)} fusion(bf16[1024,1024]{1,0:T(8,128)(2,1)} %get-tuple-element.270, bf16[1024,64]{0,1:T(8,128)(2,1)S(1)} %get-tuple-element.211), kind=kOutput, calls=%fused_computation.145 | convolution fusion | flops 134217728 | bytes 2490368 | tf_op jit(solution)/shard_map/cond/branch_1_fun/dot_general | solution.py:62
  83.2 6.9 %conditional.11 = (bf16[1024,512]{1,0:T(8,128)(2,1)}, f32[1024,64]{0,1:T(8,128)S(1)}, f32[1024]{0:T(1024)S(1)}, f32[512,64]{0,1:T(8,128)S(1)}, f32[512]{0:T(512)S(1)}) conditional(s32[]{:T(128)} %convert_element_type.81, () %tuple.87, (bf16[1024,768]{1,0:T(8,128)(2,1)}, bf16[512,768]{1,0:T(8,128)(2,1)}, bf16[512,64]{1,0:T(8,128)(2,1)S(1)}, ...), branch_computations={%region_13.14_spmd, %region_14.17_spmd} | conditional | flops 942144000 | bytes 6101032 | solution.py:166
  83.2 3.7 %convert_reduce_fusion.4 = (f32[512]{0:T(512)S(1)}, f32[1024]{0:T(1024)S(1)}, bf16[1024,512]{1,0:T(8,128)(2,1)}) fusion(bf16[1024,768]{1,0:T(8,128)(2,1)} %get-tuple-element.72, bf16[512,768]{1,0:T(8,128)(2,1)} %get-tuple-element.73), kind=kOutput, calls=%fused_computation.6 | convolution fusion | flops 807926272 | bytes 3414016 | tf_op jit(solution)/shard_map/cond/branch_1_fun/dot_general | solution.py:55
  86.9 1.7 fusion.57
  88.6 1.6 fusion.58
  91.2 7.0 %conditional.14 = (bf16[1024,512]{1,0:T(8,128)(2,1)}, f32[1024,64]{0,1:T(8,128)S(1)}, f32[1024]{0:T(1024)S(1)}, f32[512,64]{0,1:T(8,128)S(1)}, f32[4,128]{1,0:T(4,128)S(1)}) conditional(s32[]{:T(128)} %convert_element_type.81, () %tuple.94, (bf16[1024,768]{1,0:T(8,128)(2,1)}, bf16[512,768]{1,0:T(8,128)(2,1)}, bf16[512,64]{1,0:T(8,128)(2,1)S(1)}, ...), branch_computations={%region_23.24_spmd, %region_24.0_spmd} | conditional | flops 942144000 | bytes 6101032 | solution.py:166
  91.2 3.8 %convert_reduce_fusion.8 = (f32[512]{0:T(512)S(1)}, f32[1024]{0:T(1024)S(1)}, bf16[1024,512]{1,0:T(8,128)(2,1)}) fusion(bf16[1024,768]{1,0:T(8,128)(2,1)} %get-tuple-element.82, bf16[512,768]{1,0:T(8,128)(2,1)} %get-tuple-element.83), kind=kOutput, calls=%fused_computation.12 | convolution fusion | flops 807926272 | bytes 3414016 | tf_op jit(solution)/shard_map/cond/branch_1_fun/dot_general | solution.py:55
  95.0 1.7 fusion.61
  96.7 1.6 fusion.62
  98.9 1.0 add_add_fusion
  101.0 3.8 %collective-permute-start.6 = (f32[520,128]{1,0:T(8,128)}, f32[520,128]{1,0:T(8,128)}, u32[]{:S(2)}, u32[]{:S(2)}) collective-permute-start(f32[520,128]{1,0:T(8,128)} %pad_maximum_fusion.3), channel_id=1, source_target_pairs={{8,0},{12,4},{16,8},{20,12},{24,16},{28,20},{0,24},{4,28},{9,1},{1... | collective-permute-start | bytes 798728 | tf_op jit(solution)/shard_map/ppermute | solution.py:20
  104.8 6.9 %conditional.12 = (bf16[1024,512]{1,0:T(8,128)(2,1)}, f32[1024,64]{0,1:T(8,128)S(1)}, f32[1024]{0:T(1024)S(1)}, f32[512,64]{0,1:T(8,128)S(1)}, f32[4,128]{1,0:T(4,128)S(1)}) conditional(s32[]{:T(128)} %convert_element_type.80, () %tuple.90, (bf16[1024,768]{1,0:T(8,128)(2,1)}, bf16[512,768]{1,0:T(8,128)(2,1)}, bf16[512,64]{1,0:T(8,128)(2,1)S(1)}, ...), branch_computations={%region_17.18_spmd, %region_18.21_spmd} | conditional | flops 942144000 | bytes 6101032 | solution.py:166
  104.8 3.7 %convert_reduce_fusion.6 = (f32[512]{0:T(512)S(1)}, f32[1024]{0:T(1024)S(1)}, bf16[1024,512]{1,0:T(8,128)(2,1)}) fusion(bf16[1024,768]{1,0:T(8,128)(2,1)} %get-tuple-element.76, bf16[512,768]{1,0:T(8,128)(2,1)} %get-tuple-element.77), kind=kOutput, calls=%fused_computation.9 | convolution fusion | flops 807926272 | bytes 3414016 | tf_op jit(solution)/shard_map/cond/branch_1_fun/dot_general | solution.py:55
  108.5 1.7 fusion.59
  110.1 1.5 fusion.60
  115.4 2.1 conditional.13
  115.4 2.1 fusion.47
  117.5 1.0 slice.185
  118.9 5.5 %collective-permute-done.5 = f32[520,128]{1,0:T(8,128)} collective-permute-done((f32[520,128]{1,0:T(8,128)}, f32[520,128]{1,0:T(8,128)}, u32[]{:S(2)}, u32[]{:S(2)}) %collective-permute-start.5) | collective-permute-done | bytes 266272 | tf_op jit(solution)/shard_map/ppermute | solution.py:20
  125.6 1.1 fusion.43
  126.8 1.3 broadcast_multiply_fusion
  130.6 1.2 collective-permute-done.9
  131.9 3.7 %collective-permute-done.10 = f32[35,128]{1,0:T(8,128)S(1)} collective-permute-done((f32[35,128]{1,0:T(8,128)S(1)}, f32[35,128]{1,0:T(8,128)S(1)}, u32[]{:S(2)}, u32[]{:S(2)}) %collective-permute-start.10) | collective-permute-done | bytes 17952 | tf_op jit(solution)/shard_map/ppermute | solution.py:196
  135.7 3.8 %collective-permute-done.11 = f32[37,128]{1,0:T(8,128)S(1)} collective-permute-done((f32[37,128]{1,0:T(8,128)S(1)}, f32[37,128]{1,0:T(8,128)S(1)}, u32[]{:S(2)}, u32[]{:S(2)}) %collective-permute-start.11) | collective-permute-done | bytes 18976 | tf_op jit(solution)/shard_map/ppermute | solution.py:196
  139.7 3.8 %collective-permute-done.12 = f32[41,128]{1,0:T(8,128)S(1)} collective-permute-done((f32[41,128]{1,0:T(8,128)S(1)}, f32[41,128]{1,0:T(8,128)S(1)}, u32[]{:S(2)}, u32[]{:S(2)}) %collective-permute-start.12) | collective-permute-done | bytes 21024 | tf_op jit(solution)/shard_map/ppermute | solution.py:196
  143.5 4.1 %pad_maximum_fusion = (bf16[1024,1024]{1,0:T(8,128)(2,1)S(1)}, bf16[1024,1024]{1,0:T(8,128)(2,1)}) fusion(bf16[1024,512]{1,0:T(8,128)(2,1)} %get-tuple-element.180, bf16[1024,512]{1,0:T(8,128)(2,1)} %get-tuple-element.179, bf16[1024,512]{1,0:T(8,128)(2,1)} %get-tuple-element.185, bf16[1024,512]{1,0:T(8,128)(2,1)} %get-tuple-element.184), kind=kLoop, calls=%fused_computation.30 | loop fusion | flops 8388608 | bytes 8388608 | tf_op jit(solution)/shard_map/concatenate | solution.py:379
  147.9 3.0 %collective-permute-start.7 = (f32[1024,64]{0,1:T(8,128)S(1)}, f32[1024,64]{0,1:T(8,128)S(1)}, u32[]{:S(2)}, u32[]{:S(2)}) collective-permute-start(f32[1024,64]{0,1:T(8,128)S(1)} %get-tuple-element.249), channel_id=1, source_target_pairs={{4,0},{8,4},{12,8},{16,12},{20,16},{24,20},{28,24},{0,28},{5,1},{9... | collective-permute-start | bytes 786440 | tf_op jit(solution)/shard_map/ppermute | solution.py:20
  153.5 8.4 %shard_map.50 = f32[64,64]{1,0:T(8,128)} custom-call(f32[64,64]{1,0:T(8,128)} %fusion.12.gram_ref), custom_call_target="tpu_custom_call" | custom-call | tf_op jit(solution)/shard_map/pallas_call | solution.py:244
  161.9 1.7 convolution_convert_fusion
  164.4 4.4 %conditional.16 = (f32[1024,64]{0,1:T(8,128)S(1)}, f32[1024,64]{0,1:T(8,128)S(1)}) conditional(s32[]{:T(128)} %convert_element_type.77, () %tuple.98, (bf16[1024,1024]{1,0:T(8,128)(2,1)}, bf16[1024,64]{0,1:T(8,128)(2,1)S(1)}, bf16[1024,64]{0,1:T(8,128)(2,1)S(1)}) %tuple.99), branch_computations={%region_34.35_spmd, %region_35.36_spmd} | conditional | flops 268435456 | bytes 4980752 | solution.py:180
  164.4 2.3 %fusion.50 = f32[1024,64]{0,1:T(8,128)S(1)} fusion(bf16[1024,1024]{1,0:T(8,128)(2,1)} %get-tuple-element.89, bf16[1024,64]{0,1:T(8,128)(2,1)S(1)} %get-tuple-element.224), kind=kOutput, calls=%fused_computation.141 | convolution fusion | flops 134217728 | bytes 2490368 | tf_op jit(solution)/shard_map/cond/branch_1_fun/dot_general | solution.py:62
  166.7 2.1 fusion.51
  168.8 3.0 %conditional.17 = (f32[1024,64]{0,1:T(8,128)S(1)}, f32[1024,64]{0,1:T(8,128)S(1)}) conditional(s32[]{:T(128)} %convert_element_type.81, () %tuple.100, (bf16[1024,1024]{1,0:T(8,128)(2,1)}, bf16[1024,64]{0,1:T(8,128)(2,1)S(1)}, bf16[1024,64]{0,1:T(8,128)(2,1)S(1)}) %tuple.101), branch_computations={%region_36.37_spmd, %region_37.38_spmd} | conditional | flops 268435456 | bytes 13369388 | solution.py:180
  168.8 2.5 %fusion.52 = f32[1024,64]{0,1:T(8,128)S(1)} fusion(bf16[1024,1024]{1,0:T(8,128)(2,1)} %get-tuple-element.92, bf16[1024,64]{0,1:T(8,128)(2,1)S(1)} %get-tuple-element.227), kind=kOutput, calls=%fused_computation.143 | convolution fusion | flops 134217728 | bytes 2490368 | tf_op jit(solution)/shard_map/cond/branch_1_fun/dot_general | solution.py:62
  173.2 1.2 conditional.15
  175.3 4.0 %collective-permute-done.15 = f32[1024,64]{0,1:T(8,128)} collective-permute-done((f32[1024,64]{0,1:T(8,128)}, f32[1024,64]{0,1:T(8,128)}, u32[]{:S(2)}, u32[]{:S(2)}) %collective-permute-start.15) | collective-permute-done | bytes 262176 | tf_op jit(solution)/shard_map/ppermute | solution.py:20
  179.3 4.3 %collective-permute-done.14 = f32[1024,64]{0,1:T(8,128)S(1)} collective-permute-done((f32[1024,64]{0,1:T(8,128)S(1)}, f32[1024,64]{0,1:T(8,128)S(1)}, u32[]{:S(2)}, u32[]{:S(2)}) %collective-permute-start.14) | collective-permute-done | bytes 262176 | tf_op jit(solution)/shard_map/ppermute | solution.py:20
  183.6 2.2 %fusion.40 = (f32[64]{0:T(128)S(1)}, f32[1024,64]{0,1:T(8,128)S(1)}) fusion(f32[1024]{0:T(1024)S(1)} %get-tuple-element.245, f32[1024,64]{0,1:T(8,128)} %collective-permute-done.15, f32[1024,64]{0,1:T(8,128)S(1)} %collective-permute-done.14, f32[1024,64]{0,1:T(8,128)S(1)} %get-tuple-element.181, f32[1024,64]{0,1:T(8,128)S(1)} %get-tuple-element.182, ...), kind=kOutput, calls=%fused_computation.132 | convolution fusion | flops 134610880 | bytes 3543296 | tf_op jit(solution)/shard_map/dot_general | solution.py:62
  187.5 1.2 collective-permute-done.16
  188.8 3.7 %collective-permute-done.17 = f32[35,128]{1,0:T(8,128)S(1)} collective-permute-done((f32[35,128]{1,0:T(8,128)S(1)}, f32[35,128]{1,0:T(8,128)S(1)}, u32[]{:S(2)}, u32[]{:S(2)}) %collective-permute-start.17) | collective-permute-done | bytes 17952 | tf_op jit(solution)/shard_map/ppermute | solution.py:196
  192.7 3.8 %collective-permute-done.18 = f32[37,128]{1,0:T(8,128)S(1)} collective-permute-done((f32[37,128]{1,0:T(8,128)S(1)}, f32[37,128]{1,0:T(8,128)S(1)}, u32[]{:S(2)}, u32[]{:S(2)}) %collective-permute-start.18) | collective-permute-done | bytes 18976 | tf_op jit(solution)/shard_map/ppermute | solution.py:196
  196.5 1.4 collective-permute-start.19
  197.9 2.5 %collective-permute-done.19 = f32[41,128]{1,0:T(8,128)S(1)} collective-permute-done((f32[41,128]{1,0:T(8,128)S(1)}, f32[41,128]{1,0:T(8,128)S(1)}, u32[]{:S(2)}, u32[]{:S(2)}) %collective-permute-start.19) | collective-permute-done | bytes 21024 | tf_op jit(solution)/shard_map/ppermute | solution.py:196
  200.4 1.5 collective-permute-start.20
  201.9 3.3 %collective-permute-done.20 = f32[49,128]{1,0:T(8,128)S(1)} collective-permute-done((f32[49,128]{1,0:T(8,128)S(1)}, f32[49,128]{1,0:T(8,128)S(1)}, u32[]{:S(2)}, u32[]{:S(2)}) %collective-permute-start.20) | collective-permute-done | bytes 25120 | tf_op jit(solution)/shard_map/ppermute | solution.py:196
  207.8 8.4 %shard_map.51 = f32[64,64]{1,0:T(8,128)} custom-call(f32[64,64]{1,0:T(8,128)} %fusion.10.gram_ref), custom_call_target="tpu_custom_call" | custom-call | tf_op jit(solution)/shard_map/pallas_call | solution.py:244
  216.2 1.9 fusion.18
  (152 shorter events, 25.9 us)
Async XLA Ops:
  0.6 4.9 %copy-start.2 = (bf16[1024,768]{1,0:T(8,128)(2,1)S(1)}, bf16[1024,768]{1,0:T(8,128)(2,1)}, u32[]{:S(2)}) copy-start(bf16[1024,768]{1,0:T(8,128)(2,1)} %param.21) | copy-start | bytes 4718596
  0.6 69.9 %collective-permute-start.2 = (bf16[1024,768]{1,0:T(8,128)(2,1)}, bf16[1024,768]{1,0:T(8,128)(2,1)}, u32[]{:S(2)}, u32[]{:S(2)}) collective-permute-start(bf16[1024,768]{1,0:T(8,128)(2,1)} %param.21), channel_id=1, source_target_pairs={{24,0},{28,4},{0,8},{4,12},{8,16},{12,20},{16,24},{20,28},{25,1},{... | collective-permute-start | bytes 4718600 | tf_op jit(solution)/shard_map/ppermute | solution.py:20
  6.0 1.2 copy-start.3
  7.1 4.4 %copy-start.5 = (bf16[1024,64]{0,1:T(8,128)(2,1)S(1)}, bf16[1024,64]{0,1:T(8,128)(2,1)}, u32[]{:S(2)}) copy-start(bf16[1024,64]{0,1:T(8,128)(2,1)} %param.22) | copy-start | bytes 393220
  8.2 54.0 %collective-permute-start.3 = (bf16[512,768]{1,0:T(8,128)(2,1)S(1)}, bf16[512,768]{1,0:T(8,128)(2,1)}, u32[]{:S(2)}, u32[]{:S(2)}) collective-permute-start(bf16[512,768]{1,0:T(8,128)(2,1)S(1)} %get-tuple-element.255), channel_id=1, source_target_pairs={{4,0},{8,4},{12,8},{16,12},{20,16},{24,20},{28,24},{0,28},{5,1},{9... | collective-permute-start | bytes 2359304 | tf_op jit(solution)/shard_map/ppermute | solution.py:20
  12.4 49.0 %collective-permute-start.1 = (bf16[1024,64]{1,0:T(8,128)(2,1)}, bf16[1024,64]{1,0:T(8,128)(2,1)}, u32[]{:S(2)}, u32[]{:S(2)}) collective-permute-start(bf16[1024,64]{1,0:T(8,128)(2,1)} %copy.18), channel_id=1, source_target_pairs={{4,0},{8,4},{12,8},{16,12},{20,16},{24,20},{28,24},{0,28},{5,1},{9... | collective-permute-start | bytes 393224 | tf_op jit(solution)/shard_map/ppermute | solution.py:20
  12.7 69.9 %collective-permute-start.4 = (bf16[1024,64]{1,0:T(8,128)(2,1)}, bf16[1024,64]{1,0:T(8,128)(2,1)S(1)}, u32[]{:S(2)}, u32[]{:S(2)}) collective-permute-start(bf16[1024,64]{1,0:T(8,128)(2,1)} %copy.18), channel_id=1, source_target_pairs={{24,0},{28,4},{0,8},{4,12},{8,16},{12,20},{16,24},{20,28},{25,1},{... | collective-permute-start | bytes 393224 | tf_op jit(solution)/shard_map/ppermute | solution.py:20
  12.7 9.4 %copy-start.15 = (s32[32,3]{0,1:T(4,128)S(1)}, s32[32,3]{0,1:T(4,128)}, u32[]{:S(2)}) copy-start(s32[32,3]{0,1:T(4,128)} %param.23) | copy-start | bytes 1156
  12.7 77.5 %collective-permute-start = (bf16[512,768]{1,0:T(8,128)(2,1)}, bf16[512,768]{1,0:T(8,128)(2,1)}, u32[]{:S(2)}, u32[]{:S(2)}) collective-permute-start(bf16[512,768]{1,0:T(8,128)(2,1)} %get-tuple-element.256), channel_id=1, source_target_pairs={{4,0},{8,4},{12,8},{16,12},{20,16},{24,20},{28,24},{0,28},{5,1},{9... | collective-permute-start | bytes 2359304 | tf_op jit(solution)/shard_map/ppermute | solution.py:20
  22.1 92.8 %copy-start.1 = (bf16[1024,1024]{0,1:T(8,128)(2,1)}, bf16[1024,1024]{0,1:T(8,128)(2,1)S(1)}, u32[]{:S(2)}) copy-start(bf16[1024,1024]{0,1:T(8,128)(2,1)S(1)} %get-tuple-element.261) | copy-start | bytes 6291460
  70.6 4.9 %copy-start.4 = (bf16[1024,768]{1,0:T(8,128)(2,1)S(1)}, bf16[1024,768]{1,0:T(8,128)(2,1)}, u32[]{:S(2)}) copy-start(bf16[1024,768]{1,0:T(8,128)(2,1)} %copy-done.3) | copy-start | bytes 4718596
  82.5 0.7 copy-start.6
  90.2 1.0 copy-start.8
  90.2 1.0 copy-start.12
  98.2 0.7 copy-start.10
  98.2 6.5 %copy-start.13 = (f32[4,128]{1,0:T(4,128)}, f32[4,128]{1,0:T(4,128)S(1)}, u32[]{:S(2)}) copy-start(f32[4,128]{1,0:T(4,128)S(1)} %get-tuple-element.169) | copy-start | bytes 6148
  101.0 11.2 %copy-start.9 = (f32[512,64]{0,1:T(8,128)S(1)}, f32[512,64]{0,1:T(8,128)}, u32[]{:S(2)}) copy-start(f32[512,64]{0,1:T(8,128)} %copy-done.8) | copy-start | bytes 393220
  101.0 11.2 %copy-start.11 = (f32[512,64]{0,1:T(8,128)S(1)}, f32[512,64]{0,1:T(8,128)}, u32[]{:S(2)}) copy-start(f32[512,64]{0,1:T(8,128)} %copy-done.10) | copy-start | bytes 393220
  101.0 16.5 %collective-permute-start.6 = (f32[520,128]{1,0:T(8,128)}, f32[520,128]{1,0:T(8,128)}, u32[]{:S(2)}, u32[]{:S(2)}) collective-permute-start(f32[520,128]{1,0:T(8,128)} %pad_maximum_fusion.3), channel_id=1, source_target_pairs={{8,0},{12,4},{16,8},{20,12},{24,16},{28,20},{0,24},{4,28},{9,1},{1... | collective-permute-start | bytes 798728 | tf_op jit(solution)/shard_map/ppermute | solution.py:20
  111.6 0.5 copy-start.14
  114.9 9.4 %collective-permute-start.5 = (f32[520,128]{1,0:T(8,128)}, f32[520,128]{1,0:T(8,128)}, u32[]{:S(2)}, u32[]{:S(2)}) collective-permute-start(f32[520,128]{1,0:T(8,128)} %pad_maximum_fusion.2), channel_id=1, source_target_pairs={{28,0},{0,4},{4,8},{8,12},{12,16},{16,20},{20,24},{24,28},{29,1},{... | collective-permute-start | bytes 798728 | tf_op jit(solution)/shard_map/ppermute | solution.py:20
  118.8 7.9 %copy-start.16 = (f32[1024]{0:T(1024)S(1)}, f32[1024]{0:T(1024)}, u32[]{:S(2)}) copy-start(f32[1024]{0:T(1024)} %get-tuple-element.260) | copy-start | bytes 12292
  130.5 1.3 collective-permute-start.9
  131.8 3.8 %collective-permute-start.10 = (f32[35,128]{1,0:T(8,128)S(1)}, f32[35,128]{1,0:T(8,128)S(1)}, u32[]{:S(2)}, u32[]{:S(2)}) collective-permute-start(f32[35,128]{1,0:T(8,128)S(1)} %pad_maximum_fusion.9), channel_id=1, source_target_pairs={{0,2},{1,3},{2,0},{3,1},{4,6},{5,7},{6,4},{7,5},{8,10},{9,11},{10,... | collective-permute-start | bytes 53768 | tf_op jit(solution)/shard_map/ppermute | solution.py:196
  135.7 3.8 %collective-permute-start.11 = (f32[37,128]{1,0:T(8,128)S(1)}, f32[37,128]{1,0:T(8,128)S(1)}, u32[]{:S(2)}, u32[]{:S(2)}) collective-permute-start(f32[37,128]{1,0:T(8,128)S(1)} %pad_maximum_fusion.10), channel_id=1, source_target_pairs={{0,4},{4,0},{8,12},{12,8},{16,20},{20,16},{24,28},{28,24},{1,5},{5... | collective-permute-start | bytes 56840 | tf_op jit(solution)/shard_map/ppermute | solution.py:196
  139.5 3.9 %collective-permute-start.12 = (f32[41,128]{1,0:T(8,128)S(1)}, f32[41,128]{1,0:T(8,128)S(1)}, u32[]{:S(2)}, u32[]{:S(2)}) collective-permute-start(f32[41,128]{1,0:T(8,128)S(1)} %pad_maximum_fusion.6), channel_id=1, source_target_pairs={{0,8},{4,12},{8,0},{12,4},{16,24},{20,28},{24,16},{28,20},{1,9},{5... | collective-permute-start | bytes 62984 | tf_op jit(solution)/shard_map/ppermute | solution.py:196
  143.5 7.4 %collective-permute-start.13 = (f32[49,128]{1,0:T(8,128)S(1)}, f32[49,128]{1,0:T(8,128)S(1)}, u32[]{:S(2)}, u32[]{:S(2)}) collective-permute-start(f32[49,128]{1,0:T(8,128)S(1)} %pad_maximum_fusion.4), channel_id=1, source_target_pairs={{0,16},{4,20},{8,24},{12,28},{16,0},{20,4},{24,8},{28,12},{1,17},{... | collective-permute-start | bytes 75272 | tf_op jit(solution)/shard_map/ppermute | solution.py:196
  147.6 14.3 %collective-permute-start.8 = (f32[1024,64]{0,1:T(8,128)S(1)}, f32[1024,64]{0,1:T(8,128)S(1)}, u32[]{:S(2)}, u32[]{:S(2)}) collective-permute-start(f32[1024,64]{0,1:T(8,128)S(1)} %get-tuple-element.249), channel_id=1, source_target_pairs={{24,0},{28,4},{0,8},{4,12},{8,16},{12,20},{16,24},{20,28},{25,1},{... | collective-permute-start | bytes 786440 | tf_op jit(solution)/shard_map/ppermute | solution.py:20
  147.9 14.0 %collective-permute-start.7 = (f32[1024,64]{0,1:T(8,128)S(1)}, f32[1024,64]{0,1:T(8,128)S(1)}, u32[]{:S(2)}, u32[]{:S(2)}) collective-permute-start(f32[1024,64]{0,1:T(8,128)S(1)} %get-tuple-element.249), channel_id=1, source_target_pairs={{4,0},{8,4},{12,8},{16,12},{20,16},{24,20},{28,24},{0,28},{5,1},{9... | collective-permute-start | bytes 786440 | tf_op jit(solution)/shard_map/ppermute | solution.py:20
  163.6 0.8 copy-start.7
  168.8 2.5 %copy-start = (bf16[1024,1024]{1,0:T(8,128)(2,1)S(1)}, bf16[1024,1024]{1,0:T(8,128)(2,1)}, u32[]{:S(2)}) copy-start(bf16[1024,1024]{1,0:T(8,128)(2,1)} %get-tuple-element.92) | copy-start | bytes 6291460 | tf_op jit(solution)/shard_map/cond
  172.6 6.7 %collective-permute-start.15 = (f32[1024,64]{0,1:T(8,128)}, f32[1024,64]{0,1:T(8,128)}, u32[]{:S(2)}, u32[]{:S(2)}) collective-permute-start(f32[1024,64]{0,1:T(8,128)} %add.250), channel_id=1, source_target_pairs={{8,0},{12,4},{16,8},{20,12},{24,16},{28,20},{0,24},{4,28},{9,1},{1... | collective-permute-start | bytes 786440 | tf_op jit(solution)/shard_map/ppermute | solution.py:20
  174.4 9.1 %collective-permute-start.14 = (f32[1024,64]{0,1:T(8,128)S(1)}, f32[1024,64]{0,1:T(8,128)S(1)}, u32[]{:S(2)}, u32[]{:S(2)}) collective-permute-start(f32[1024,64]{0,1:T(8,128)S(1)} %add.248), channel_id=1, source_target_pairs={{28,0},{0,4},{4,8},{8,12},{12,16},{16,20},{20,24},{24,28},{29,1},{... | collective-permute-start | bytes 786440 | tf_op jit(solution)/shard_map/ppermute | solution.py:20
  187.4 1.3 collective-permute-start.16
  188.7 3.8 %collective-permute-start.17 = (f32[35,128]{1,0:T(8,128)S(1)}, f32[35,128]{1,0:T(8,128)S(1)}, u32[]{:S(2)}, u32[]{:S(2)}) collective-permute-start(f32[35,128]{1,0:T(8,128)S(1)} %pad_maximum_fusion.12), channel_id=1, source_target_pairs={{0,2},{1,3},{2,0},{3,1},{4,6},{5,7},{6,4},{7,5},{8,10},{9,11},{10,... | collective-permute-start | bytes 53768 | tf_op jit(solution)/shard_map/ppermute | solution.py:196
  192.6 3.8 %collective-permute-start.18 = (f32[37,128]{1,0:T(8,128)S(1)}, f32[37,128]{1,0:T(8,128)S(1)}, u32[]{:S(2)}, u32[]{:S(2)}) collective-permute-start(f32[37,128]{1,0:T(8,128)S(1)} %pad_maximum_fusion.13), channel_id=1, source_target_pairs={{0,4},{4,0},{8,12},{12,8},{16,20},{20,16},{24,28},{28,24},{1,5},{5... | collective-permute-start | bytes 56840 | tf_op jit(solution)/shard_map/ppermute | solution.py:196
  196.5 3.9 %collective-permute-start.19 = (f32[41,128]{1,0:T(8,128)S(1)}, f32[41,128]{1,0:T(8,128)S(1)}, u32[]{:S(2)}, u32[]{:S(2)}) collective-permute-start(f32[41,128]{1,0:T(8,128)S(1)} %pad_maximum_fusion.7), channel_id=1, source_target_pairs={{0,8},{4,12},{8,0},{12,4},{16,24},{20,28},{24,16},{28,20},{1,9},{5... | collective-permute-start | bytes 62984 | tf_op jit(solution)/shard_map/ppermute | solution.py:196
  200.4 4.8 %collective-permute-start.20 = (f32[49,128]{1,0:T(8,128)S(1)}, f32[49,128]{1,0:T(8,128)S(1)}, u32[]{:S(2)}, u32[]{:S(2)}) collective-permute-start(f32[49,128]{1,0:T(8,128)S(1)} %pad_maximum_fusion.5), channel_id=1, source_target_pairs={{0,16},{4,20},{8,24},{12,28},{16,0},{20,4},{24,8},{28,12},{1,17},{... | collective-permute-start | bytes 75272 | tf_op jit(solution)/shard_map/ppermute | solution.py:196

commit v18 on v17

--- a/solution.py
+++ b/solution.py
@@ -217,26 +217,42 @@
 
 def factor_kernel(gram_ref, inverse_ref):
     size = gram_ref.shape[0]
-    rows = lax.broadcasted_iota(jnp.int32, (size, size), 0)
-    cols = lax.broadcasted_iota(jnp.int32, (size, size), 1)
+    rows = lax.broadcasted_iota(jnp.int32, (size, 1), 0)
+    cols = lax.broadcasted_iota(jnp.int32, (1, size), 1)
     eye = jnp.where(rows == cols, 1.0, 0.0).astype(jnp.float32)
 
-    def step(j, carry):
+    def pick_row(matrix, j):
+        return jnp.sum(jnp.where(rows == j, matrix, 0.0), axis=0, keepdims=True)
+
+    def pick_column(matrix, j):
+        return jnp.sum(jnp.where(cols == j, matrix, 0.0), axis=1, keepdims=True)
+
+    def invert(inverse, j, scale, factor_column):
+        inverse_row = pick_row(inverse, j) * scale
+        inverse = jnp.where(rows == j, inverse_row, inverse)
+        return inverse - jnp.where(rows > j, factor_column, 0.0) * inverse_row
+
+    def step(t, carry):
         remaining, inverse = carry
-        pivot_row = jnp.sum(jnp.where(rows == j, remaining, 0.0), axis=0, keepdims=True)
-        pivot = jnp.sum(jnp.where(cols[:1] == j, pivot_row, 0.0), axis=1, keepdims=True)
-        column = jnp.sum(jnp.where(cols == j, remaining, 0.0), axis=1, keepdims=True)
-        scale = lax.rsqrt(pivot)
-        factor_column = jnp.where(rows[:, :1] >= j, column * scale, 0.0)
-        factor_row = jnp.where(cols[:1] >= j, pivot_row * scale, 0.0)
-        remaining = remaining - factor_column * factor_row
-        inverse_row = jnp.sum(jnp.where(rows == j, inverse, 0.0), axis=0, keepdims=True) * scale
-        inverse = jnp.where(rows == j, inverse_row, inverse)
-        below = jnp.where(rows[:, :1] > j, factor_column, 0.0)
-        inverse = inverse - below * inverse_row
+        j = 2 * t
+        row0 = pick_row(remaining, j)
+        row1 = pick_row(remaining, j + 1)
+        column0 = pick_column(remaining, j)
+        column1 = pick_column(remaining, j + 1)
+        scale0 = lax.rsqrt(pick_column(row0, j))
+        factor_column0 = jnp.where(rows >= j, column0 * scale0, 0.0)
+        factor_row0 = jnp.where(cols >= j, row0 * scale0, 0.0)
+        row1 = row1 - pick_row(factor_column0, j + 1) * factor_row0
+        column1 = column1 - factor_column0 * pick_column(factor_row0, j + 1)
+        scale1 = lax.rsqrt(pick_column(row1, j + 1))
+        factor_column1 = jnp.where(rows >= j + 1, column1 * scale1, 0.0)
+        factor_row1 = jnp.where(cols >= j + 1, row1 * scale1, 0.0)
+        remaining = remaining - factor_column0 * factor_row0 - factor_column1 * factor_row1
+        inverse = invert(inverse, j, scale0, factor_column0)
+        inverse = invert(inverse, j + 1, scale1, factor_column1)
         return remaining, inverse
 
-    _, inverse = lax.fori_loop(0, size, step, (gram_ref[...], eye))
+    _, inverse = lax.fori_loop(0, size // 2, step, (gram_ref[...], eye))
     inverse_ref[...] = inverse
 
 

time: 219 us -> 220 us (level)
  no operation moved by 1% of the time
where the time goes in v18:
time: 220 us; the launch traced here: 218 us
  waiting for transfers between devices  75.8 us (34%)
  matrix products  60.8 us (28%)
  starting transfers between devices  25.1 us (11%)
  other arithmetic  23.9 us (11%)
  Pallas kernels  16.3 us (7%)
  local copies, waits for them, and re-layouts  12.5 us (6%)
  between operations  3.07 us (1%)
    ppermute x11, waiting for transfers between devices, shifted(): return lax.ppermute(block, axis, route)  49 us
    ppermute x10, waiting for transfers between devices, butterfly(): other = lax.ppermute(block, axis, route)  26.8 us
    dot_general x6, matrix products, scores_tile(): lax.dot_general(leftside_block, right_block, (((1,), (1,)), ((), ())), pr...  24 us
    ppermute x11, starting transfers between devices, shifted(): return lax.ppermute(block, axis, route)  20.8 us
    dot_general x10, matrix products, row_product(): return jnp.dot(affinity, weights, preferred_element_type=jnp.float32)  18 us
    pallas_call x2, Pallas kernels, factor_inverse(): pl.pallas_call(factor_kernel, out_shape=jax.ShapeDtypeStruct(gram_matrix....  16.3 us
    dot_general x8, matrix products, col_product(): lax.dot_general(affinity, weights, (((0,), (0,)), ((), ())), preferred_el...  12 us
    dot_general x8, matrix products, hdot(): jnp.dot(left, right, precision=lax.Precision.HIGHEST, preferred_element_t...  6.78 us
  transfers between devices with their start and end apart: 21, of which 13 were waited for; matrix products, arithmetic and copies ran while one was open for 27% of the time, Pallas kernels for 4%

profile of v18, /device:TPU:0, one launch (start us, length us, event | category | flops | bytes accessed | tf_op | source)
XLA Modules:
  0.0 217.7 jit_solution(13069146539611863627)
XLA Ops:
  0.6 3.1 %collective-permute-start.2 = (bf16[1024,768]{1,0:T(8,128)(2,1)}, bf16[1024,768]{1,0:T(8,128)(2,1)}, u32[]{:S(2)}, u32[]{:S(2)}) collective-permute-start(bf16[1024,768]{1,0:T(8,128)(2,1)} %param.21), channel_id=1, source_target_pairs={{24,0},{28,4},{0,8},{4,12},{8,16},{12,20},{16,24},{20,28},{25,1},{... | collective-permute-start | bytes 4718600 | tf_op jit(solution)/shard_map/ppermute | solution.py:20
  3.7 1.8 fusion.1
  6.0 1.1 copy-done.3
  7.1 1.1 fusion.45
  8.2 3.3 %collective-permute-start.3 = (bf16[512,768]{1,0:T(8,128)(2,1)S(1)}, bf16[512,768]{1,0:T(8,128)(2,1)}, u32[]{:S(2)}, u32[]{:S(2)}) collective-permute-start(bf16[512,768]{1,0:T(8,128)(2,1)S(1)} %get-tuple-element.255), channel_id=1, source_target_pairs={{4,0},{8,4},{12,8},{16,12},{20,16},{24,20},{28,24},{0,28},{5,1},{9... | collective-permute-start | bytes 2359304 | tf_op jit(solution)/shard_map/ppermute | solution.py:20
  12.7 5.0 %collective-permute-start = (bf16[512,768]{1,0:T(8,128)(2,1)}, bf16[512,768]{1,0:T(8,128)(2,1)}, u32[]{:S(2)}, u32[]{:S(2)}) collective-permute-start(bf16[512,768]{1,0:T(8,128)(2,1)} %get-tuple-element.256), channel_id=1, source_target_pairs={{4,0},{8,4},{12,8},{16,12},{20,16},{24,20},{28,24},{0,28},{5,1},{9... | collective-permute-start | bytes 2359304 | tf_op jit(solution)/shard_map/ppermute | solution.py:20
  17.7 4.4 %convert_reduce_fusion.10 = (f32[1024]{0:T(1024)}, bf16[1024,1024]{0,1:T(8,128)(2,1)S(1)}) fusion(bf16[1024,768]{1,0:T(8,128)(2,1)} %copy-done.3), kind=kOutput, calls=%fused_computation.15 | convolution fusion | flops 1616903168 | bytes 3674112 | tf_op jit(solution)/shard_map/dot_general | solution.py:55
  22.1 1.0 compare_reduce_fusion
  24.8 36.5 %collective-permute-done.1 = bf16[1024,64]{1,0:T(8,128)(2,1)} collective-permute-done((bf16[1024,64]{1,0:T(8,128)(2,1)}, bf16[1024,64]{1,0:T(8,128)(2,1)}, u32[]{:S(2)}, u32[]{:S(2)}) %collective-permute-start.1) | collective-permute-done | bytes 131104 | tf_op jit(solution)/shard_map/ppermute | solution.py:20
  62.3 8.3 %conditional.10 = (bf16[1024,512]{1,0:T(8,128)(2,1)}, f32[1024,64]{0,1:T(8,128)}, f32[1024]{0:T(1024)S(1)}, f32[512,64]{0,1:T(8,128)}, f32[512]{0:T(512)S(1)}) conditional(s32[]{:T(128)} %convert_element_type.80, () %tuple.85, (bf16[1024,768]{1,0:T(8,128)(2,1)}, bf16[512,768]{1,0:T(8,128)(2,1)}, bf16[512,64]{1,0:T(8,128)(2,1)S(1)}, ...), branch_computations={%region_8.9_spmd, %region_9.12_spmd} | conditional | flops 942144000 | bytes 6101032 | solution.py:166
  62.3 3.7 %convert_reduce_fusion.2 = (f32[512]{0:T(512)S(1)}, f32[1024]{0:T(1024)S(1)}, bf16[1024,512]{1,0:T(8,128)(2,1)}) fusion(bf16[1024,768]{1,0:T(8,128)(2,1)} %get-tuple-element.68, bf16[512,768]{1,0:T(8,128)(2,1)} %get-tuple-element.69), kind=kOutput, calls=%fused_computation.3 | convolution fusion | flops 807926272 | bytes 3414016 | tf_op jit(solution)/shard_map/cond/branch_1_fun/dot_general | solution.py:55
  66.0 2.4 %fusion.55 = f32[1024,64]{0,1:T(8,128)} fusion(bf16[1024,512]{1,0:T(8,128)(2,1)} %get-tuple-element.279, bf16[512,64]{1,0:T(8,128)(2,1)S(1)} %get-tuple-element.70), kind=kOutput, calls=%fused_computation.146 | convolution fusion | flops 67108864 | bytes 1376256 | tf_op jit(solution)/shard_map/cond/branch_1_fun/dot_general | solution.py:62
  68.4 2.2 fusion.56
  70.6 1.9 fusion.4
  72.5 3.0 %fusion.6 = bf16[1024,768]{1,0:T(8,128)(2,1)} fusion(bf16[1024,768]{1,0:T(8,128)(2,1)} %collective-permute-done.2, f32[1024]{0:T(1024)S(1)} %add_rsqrt_fusion), kind=kLoop, calls=%fused_computation.29 | loop fusion | flops 3145728 | bytes 3149824 | tf_op jit(solution)/shard_map/convert_element_type | solution.py:51
  75.5 7.1 %conditional.9 = (bf16[1024,1024]{1,0:T(8,128)(2,1)}, f32[1024,64]{0,1:T(8,128)S(1)}, f32[1024]{0:T(1024)S(1)}, f32[1024]{0:T(1024)S(1)}) conditional(s32[]{:T(128)} %convert_element_type.77, () %tuple.83, (bf16[1024,768]{1,0:T(8,128)(2,1)}, bf16[1024,768]{1,0:T(8,128)(2,1)S(1)}, bf16[1024,64]{0,1:T(8,128)(2,1)S(1)}) %tuple.159), branch_computations={%region_3.4_spmd, %region_4.0_spmd} | conditional | flops 1750071296 | bytes 7741472 | solution.py:125
  75.5 4.7 %convert_reduce_fusion = (f32[1024]{0:T(1024)S(1)}, f32[1024]{0:T(1024)S(1)}, bf16[1024,1024]{1,0:T(8,128)(2,1)}) fusion(bf16[1024,768]{1,0:T(8,128)(2,1)} %get-tuple-element.65, bf16[1024,768]{1,0:T(8,128)(2,1)S(1)} %get-tuple-element.66), kind=kOutput, calls=%fused_computation | convolution fusion | flops 1615853568 | bytes 5251072 | tf_op jit(solution)/shard_map/cond/branch_1_fun/dot_general | solution.py:55
  80.2 2.3 %fusion.54 = f32[1024,64]{0,1:T(8,128)S(1)} fusion(bf16[1024,1024]{1,0:T(8,128)(2,1)} %get-tuple-element.270, bf16[1024,64]{0,1:T(8,128)(2,1)S(1)} %get-tuple-element.211), kind=kOutput, calls=%fused_computation.145 | convolution fusion | flops 134217728 | bytes 2490368 | tf_op jit(solution)/shard_map/cond/branch_1_fun/dot_general | solution.py:62
  83.2 6.9 %conditional.11 = (bf16[1024,512]{1,0:T(8,128)(2,1)}, f32[1024,64]{0,1:T(8,128)S(1)}, f32[1024]{0:T(1024)S(1)}, f32[512,64]{0,1:T(8,128)S(1)}, f32[512]{0:T(512)S(1)}) conditional(s32[]{:T(128)} %convert_element_type.81, () %tuple.87, (bf16[1024,768]{1,0:T(8,128)(2,1)}, bf16[512,768]{1,0:T(8,128)(2,1)}, bf16[512,64]{1,0:T(8,128)(2,1)S(1)}, ...), branch_computations={%region_13.14_spmd, %region_14.17_spmd} | conditional | flops 942144000 | bytes 6101032 | solution.py:166
  83.2 3.7 %convert_reduce_fusion.4 = (f32[512]{0:T(512)S(1)}, f32[1024]{0:T(1024)S(1)}, bf16[1024,512]{1,0:T(8,128)(2,1)}) fusion(bf16[1024,768]{1,0:T(8,128)(2,1)} %get-tuple-element.72, bf16[512,768]{1,0:T(8,128)(2,1)} %get-tuple-element.73), kind=kOutput, calls=%fused_computation.6 | convolution fusion | flops 807926272 | bytes 3414016 | tf_op jit(solution)/shard_map/cond/branch_1_fun/dot_general | solution.py:55
  86.9 1.7 fusion.57
  88.6 1.6 fusion.58
  91.2 7.0 %conditional.14 = (bf16[1024,512]{1,0:T(8,128)(2,1)}, f32[1024,64]{0,1:T(8,128)S(1)}, f32[1024]{0:T(1024)S(1)}, f32[512,64]{0,1:T(8,128)S(1)}, f32[4,128]{1,0:T(4,128)S(1)}) conditional(s32[]{:T(128)} %convert_element_type.81, () %tuple.94, (bf16[1024,768]{1,0:T(8,128)(2,1)}, bf16[512,768]{1,0:T(8,128)(2,1)}, bf16[512,64]{1,0:T(8,128)(2,1)S(1)}, ...), branch_computations={%region_23.24_spmd, %region_24.0_spmd} | conditional | flops 942144000 | bytes 6101032 | solution.py:166
  91.2 3.8 %convert_reduce_fusion.8 = (f32[512]{0:T(512)S(1)}, f32[1024]{0:T(1024)S(1)}, bf16[1024,512]{1,0:T(8,128)(2,1)}) fusion(bf16[1024,768]{1,0:T(8,128)(2,1)} %get-tuple-element.82, bf16[512,768]{1,0:T(8,128)(2,1)} %get-tuple-element.83), kind=kOutput, calls=%fused_computation.12 | convolution fusion | flops 807926272 | bytes 3414016 | tf_op jit(solution)/shard_map/cond/branch_1_fun/dot_general | solution.py:55
  95.0 1.7 fusion.61
  96.7 1.6 fusion.62
  98.9 1.0 add_add_fusion
  101.0 7.0 %conditional.12 = (bf16[1024,512]{1,0:T(8,128)(2,1)}, f32[1024,64]{0,1:T(8,128)S(1)}, f32[1024]{0:T(1024)S(1)}, f32[512,64]{0,1:T(8,128)S(1)}, f32[4,128]{1,0:T(4,128)S(1)}) conditional(s32[]{:T(128)} %convert_element_type.80, () %tuple.90, (bf16[1024,768]{1,0:T(8,128)(2,1)}, bf16[512,768]{1,0:T(8,128)(2,1)}, bf16[512,64]{1,0:T(8,128)(2,1)S(1)}, ...), branch_computations={%region_17.18_spmd, %region_18.21_spmd} | conditional | flops 942144000 | bytes 6101032 | solution.py:166
  101.0 3.8 %convert_reduce_fusion.6 = (f32[512]{0:T(512)S(1)}, f32[1024]{0:T(1024)S(1)}, bf16[1024,512]{1,0:T(8,128)(2,1)}) fusion(bf16[1024,768]{1,0:T(8,128)(2,1)} %get-tuple-element.76, bf16[512,768]{1,0:T(8,128)(2,1)} %get-tuple-element.77), kind=kOutput, calls=%fused_computation.9 | convolution fusion | flops 807926272 | bytes 3414016 | tf_op jit(solution)/shard_map/cond/branch_1_fun/dot_general | solution.py:55
  104.8 1.7 fusion.59
  106.4 1.5 fusion.60
  111.2 4.0 %collective-permute-start.5 = (f32[520,128]{1,0:T(8,128)}, f32[520,128]{1,0:T(8,128)}, u32[]{:S(2)}, u32[]{:S(2)}) collective-permute-start(f32[520,128]{1,0:T(8,128)} %pad_maximum_fusion.2), channel_id=1, source_target_pairs={{28,0},{0,4},{4,8},{8,12},{12,16},{16,20},{20,24},{24,28},{29,1},{... | collective-permute-start | bytes 798728 | tf_op jit(solution)/shard_map/ppermute | solution.py:20
  115.6 2.1 conditional.13
  115.7 2.1 fusion.47
  117.8 1.0 slice.185
  119.1 3.5 %collective-permute-done.5 = f32[520,128]{1,0:T(8,128)} collective-permute-done((f32[520,128]{1,0:T(8,128)}, f32[520,128]{1,0:T(8,128)}, u32[]{:S(2)}, u32[]{:S(2)}) %collective-permute-start.5) | collective-permute-done | bytes 266272 | tf_op jit(solution)/shard_map/ppermute | solution.py:20
  123.9 1.1 fusion.43
  125.1 1.3 broadcast_multiply_fusion
  128.8 1.2 collective-permute-done.9
  130.1 3.7 %collective-permute-done.10 = f32[35,128]{1,0:T(8,128)S(1)} collective-permute-done((f32[35,128]{1,0:T(8,128)S(1)}, f32[35,128]{1,0:T(8,128)S(1)}, u32[]{:S(2)}, u32[]{:S(2)}) %collective-permute-start.10) | collective-permute-done | bytes 17952 | tf_op jit(solution)/shard_map/ppermute | solution.py:196
  133.9 1.0 collective-permute-start.11
  134.9 2.8 %collective-permute-done.11 = f32[37,128]{1,0:T(8,128)S(1)} collective-permute-done((f32[37,128]{1,0:T(8,128)S(1)}, f32[37,128]{1,0:T(8,128)S(1)}, u32[]{:S(2)}, u32[]{:S(2)}) %collective-permute-start.11) | collective-permute-done | bytes 18976 | tf_op jit(solution)/shard_map/ppermute | solution.py:196
  138.6 3.1 %collective-permute-done.12 = f32[41,128]{1,0:T(8,128)S(1)} collective-permute-done((f32[41,128]{1,0:T(8,128)S(1)}, f32[41,128]{1,0:T(8,128)S(1)}, u32[]{:S(2)}, u32[]{:S(2)}) %collective-permute-start.12) | collective-permute-done | bytes 21024 | tf_op jit(solution)/shard_map/ppermute | solution.py:196
  142.4 4.1 %pad_maximum_fusion = (bf16[1024,1024]{1,0:T(8,128)(2,1)S(1)}, bf16[1024,1024]{1,0:T(8,128)(2,1)}) fusion(bf16[1024,512]{1,0:T(8,128)(2,1)} %get-tuple-element.180, bf16[1024,512]{1,0:T(8,128)(2,1)} %get-tuple-element.179, bf16[1024,512]{1,0:T(8,128)(2,1)} %get-tuple-element.185, bf16[1024,512]{1,0:T(8,128)(2,1)} %get-tuple-element.184), kind=kLoop, calls=%fused_computation.30 | loop fusion | flops 8388608 | bytes 8388608 | tf_op jit(solution)/shard_map/concatenate | solution.py:395
  146.4 1.5 collective-permute-start.8
  147.9 3.6 %collective-permute-start.7 = (f32[1024,64]{0,1:T(8,128)S(1)}, f32[1024,64]{0,1:T(8,128)S(1)}, u32[]{:S(2)}, u32[]{:S(2)}) collective-permute-start(f32[1024,64]{0,1:T(8,128)S(1)} %get-tuple-element.249), channel_id=1, source_target_pairs={{4,0},{8,4},{12,8},{16,12},{20,16},{24,20},{28,24},{0,28},{5,1},{9... | collective-permute-start | bytes 786440 | tf_op jit(solution)/shard_map/ppermute | solution.py:20
  154.1 8.2 %shard_map.50 = f32[64,64]{1,0:T(8,128)} custom-call(f32[64,64]{1,0:T(8,128)} %fusion.12.gram_ref), custom_call_target="tpu_custom_call" | custom-call | tf_op jit(solution)/shard_map/pallas_call | solution.py:260
  162.3 1.7 convolution_convert_fusion
  164.7 4.4 %conditional.16 = (f32[1024,64]{0,1:T(8,128)S(1)}, f32[1024,64]{0,1:T(8,128)S(1)}) conditional(s32[]{:T(128)} %convert_element_type.77, () %tuple.98, (bf16[1024,1024]{1,0:T(8,128)(2,1)}, bf16[1024,64]{0,1:T(8,128)(2,1)S(1)}, bf16[1024,64]{0,1:T(8,128)(2,1)S(1)}) %tuple.99), branch_computations={%region_34.35_spmd, %region_35.36_spmd} | conditional | flops 268435456 | bytes 4980752 | solution.py:180
  164.7 2.3 %fusion.50 = f32[1024,64]{0,1:T(8,128)S(1)} fusion(bf16[1024,1024]{1,0:T(8,128)(2,1)} %get-tuple-element.89, bf16[1024,64]{0,1:T(8,128)(2,1)S(1)} %get-tuple-element.224), kind=kOutput, calls=%fused_computation.141 | convolution fusion | flops 134217728 | bytes 2490368 | tf_op jit(solution)/shard_map/cond/branch_1_fun/dot_general | solution.py:62
  167.1 2.1 fusion.51
  169.2 3.0 %conditional.17 = (f32[1024,64]{0,1:T(8,128)S(1)}, f32[1024,64]{0,1:T(8,128)S(1)}) conditional(s32[]{:T(128)} %convert_element_type.81, () %tuple.100, (bf16[1024,1024]{1,0:T(8,128)(2,1)}, bf16[1024,64]{0,1:T(8,128)(2,1)S(1)}, bf16[1024,64]{0,1:T(8,128)(2,1)S(1)}) %tuple.101), branch_computations={%region_36.37_spmd, %region_37.38_spmd} | conditional | flops 268435456 | bytes 13369388 | solution.py:180
  169.2 2.5 %fusion.52 = f32[1024,64]{0,1:T(8,128)S(1)} fusion(bf16[1024,1024]{1,0:T(8,128)(2,1)} %get-tuple-element.92, bf16[1024,64]{0,1:T(8,128)(2,1)S(1)} %get-tuple-element.227), kind=kOutput, calls=%fused_computation.143 | convolution fusion | flops 134217728 | bytes 2490368 | tf_op jit(solution)/shard_map/cond/branch_1_fun/dot_general | solution.py:62
  172.9 1.2 conditional.15
  174.3 5.3 %collective-permute-done.15 = f32[1024,64]{0,1:T(8,128)} collective-permute-done((f32[1024,64]{0,1:T(8,128)}, f32[1024,64]{0,1:T(8,128)}, u32[]{:S(2)}, u32[]{:S(2)}) %collective-permute-start.15) | collective-permute-done | bytes 262176 | tf_op jit(solution)/shard_map/ppermute | solution.py:20
  179.6 3.7 %collective-permute-done.14 = f32[1024,64]{0,1:T(8,128)S(1)} collective-permute-done((f32[1024,64]{0,1:T(8,128)S(1)}, f32[1024,64]{0,1:T(8,128)S(1)}, u32[]{:S(2)}, u32[]{:S(2)}) %collective-permute-start.14) | collective-permute-done | bytes 262176 | tf_op jit(solution)/shard_map/ppermute | solution.py:20
  183.3 2.2 %fusion.40 = (f32[64]{0:T(128)S(1)}, f32[1024,64]{0,1:T(8,128)S(1)}) fusion(f32[1024]{0:T(1024)S(1)} %get-tuple-element.245, f32[1024,64]{0,1:T(8,128)} %collective-permute-done.15, f32[1024,64]{0,1:T(8,128)S(1)} %collective-permute-done.14, f32[1024,64]{0,1:T(8,128)S(1)} %get-tuple-element.181, f32[1024,64]{0,1:T(8,128)S(1)} %get-tuple-element.182, ...), kind=kOutput, calls=%fused_computation.132 | convolution fusion | flops 134610880 | bytes 3543296 | tf_op jit(solution)/shard_map/dot_general | solution.py:62
  187.2 1.2 collective-permute-done.16
  189.4 2.9 %collective-permute-done.17 = f32[35,128]{1,0:T(8,128)S(1)} collective-permute-done((f32[35,128]{1,0:T(8,128)S(1)}, f32[35,128]{1,0:T(8,128)S(1)}, u32[]{:S(2)}, u32[]{:S(2)}) %collective-permute-start.17) | collective-permute-done | bytes 17952 | tf_op jit(solution)/shard_map/ppermute | solution.py:196
  192.4 3.8 %collective-permute-done.18 = f32[37,128]{1,0:T(8,128)S(1)} collective-permute-done((f32[37,128]{1,0:T(8,128)S(1)}, f32[37,128]{1,0:T(8,128)S(1)}, u32[]{:S(2)}, u32[]{:S(2)}) %collective-permute-start.18) | collective-permute-done | bytes 18976 | tf_op jit(solution)/shard_map/ppermute | solution.py:196
  196.5 3.6 %collective-permute-done.19 = f32[41,128]{1,0:T(8,128)S(1)} collective-permute-done((f32[41,128]{1,0:T(8,128)S(1)}, f32[41,128]{1,0:T(8,128)S(1)}, u32[]{:S(2)}, u32[]{:S(2)}) %collective-permute-start.19) | collective-permute-done | bytes 21024 | tf_op jit(solution)/shard_map/ppermute | solution.py:196
  200.6 4.5 %collective-permute-done.20 = f32[49,128]{1,0:T(8,128)S(1)} collective-permute-done((f32[49,128]{1,0:T(8,128)S(1)}, f32[49,128]{1,0:T(8,128)S(1)}, u32[]{:S(2)}, u32[]{:S(2)}) %collective-permute-start.20) | collective-permute-done | bytes 25120 | tf_op jit(solution)/shard_map/ppermute | solution.py:196
  207.6 8.2 %shard_map.51 = f32[64,64]{1,0:T(8,128)} custom-call(f32[64,64]{1,0:T(8,128)} %fusion.10.gram_ref), custom_call_target="tpu_custom_call" | custom-call | tf_op jit(solution)/shard_map/pallas_call | solution.py:260
  215.8 1.9 fusion.18
  (152 shorter events, 27.0 us)
Async XLA Ops:
  0.6 4.9 %copy-start.2 = (bf16[1024,768]{1,0:T(8,128)(2,1)S(1)}, bf16[1024,768]{1,0:T(8,128)(2,1)}, u32[]{:S(2)}) copy-start(bf16[1024,768]{1,0:T(8,128)(2,1)} %param.21) | copy-start | bytes 4718596
  0.6 69.9 %collective-permute-start.2 = (bf16[1024,768]{1,0:T(8,128)(2,1)}, bf16[1024,768]{1,0:T(8,128)(2,1)}, u32[]{:S(2)}, u32[]{:S(2)}) collective-permute-start(bf16[1024,768]{1,0:T(8,128)(2,1)} %param.21), channel_id=1, source_target_pairs={{24,0},{28,4},{0,8},{4,12},{8,16},{12,20},{16,24},{20,28},{25,1},{... | collective-permute-start | bytes 4718600 | tf_op jit(solution)/shard_map/ppermute | solution.py:20
  6.0 1.2 copy-start.3
  7.1 4.4 %copy-start.5 = (bf16[1024,64]{0,1:T(8,128)(2,1)S(1)}, bf16[1024,64]{0,1:T(8,128)(2,1)}, u32[]{:S(2)}) copy-start(bf16[1024,64]{0,1:T(8,128)(2,1)} %param.22) | copy-start | bytes 393220
  8.2 54.0 %collective-permute-start.3 = (bf16[512,768]{1,0:T(8,128)(2,1)S(1)}, bf16[512,768]{1,0:T(8,128)(2,1)}, u32[]{:S(2)}, u32[]{:S(2)}) collective-permute-start(bf16[512,768]{1,0:T(8,128)(2,1)S(1)} %get-tuple-element.255), channel_id=1, source_target_pairs={{4,0},{8,4},{12,8},{16,12},{20,16},{24,20},{28,24},{0,28},{5,1},{9... | collective-permute-start | bytes 2359304 | tf_op jit(solution)/shard_map/ppermute | solution.py:20
  12.4 49.0 %collective-permute-start.1 = (bf16[1024,64]{1,0:T(8,128)(2,1)}, bf16[1024,64]{1,0:T(8,128)(2,1)}, u32[]{:S(2)}, u32[]{:S(2)}) collective-permute-start(bf16[1024,64]{1,0:T(8,128)(2,1)} %copy.18), channel_id=1, source_target_pairs={{4,0},{8,4},{12,8},{16,12},{20,16},{24,20},{28,24},{0,28},{5,1},{9... | collective-permute-start | bytes 393224 | tf_op jit(solution)/shard_map/ppermute | solution.py:20
  12.7 69.9 %collective-permute-start.4 = (bf16[1024,64]{1,0:T(8,128)(2,1)}, bf16[1024,64]{1,0:T(8,128)(2,1)S(1)}, u32[]{:S(2)}, u32[]{:S(2)}) collective-permute-start(bf16[1024,64]{1,0:T(8,128)(2,1)} %copy.18), channel_id=1, source_target_pairs={{24,0},{28,4},{0,8},{4,12},{8,16},{12,20},{16,24},{20,28},{25,1},{... | collective-permute-start | bytes 393224 | tf_op jit(solution)/shard_map/ppermute | solution.py:20
  12.7 9.4 %copy-start.15 = (s32[32,3]{0,1:T(4,128)S(1)}, s32[32,3]{0,1:T(4,128)}, u32[]{:S(2)}) copy-start(s32[32,3]{0,1:T(4,128)} %param.23) | copy-start | bytes 1156
  12.7 77.5 %collective-permute-start = (bf16[512,768]{1,0:T(8,128)(2,1)}, bf16[512,768]{1,0:T(8,128)(2,1)}, u32[]{:S(2)}, u32[]{:S(2)}) collective-permute-start(bf16[512,768]{1,0:T(8,128)(2,1)} %get-tuple-element.256), channel_id=1, source_target_pairs={{4,0},{8,4},{12,8},{16,12},{20,16},{24,20},{28,24},{0,28},{5,1},{9... | collective-permute-start | bytes 2359304 | tf_op jit(solution)/shard_map/ppermute | solution.py:20
  22.1 93.1 %copy-start.1 = (bf16[1024,1024]{0,1:T(8,128)(2,1)}, bf16[1024,1024]{0,1:T(8,128)(2,1)S(1)}, u32[]{:S(2)}) copy-start(bf16[1024,1024]{0,1:T(8,128)(2,1)S(1)} %get-tuple-element.261) | copy-start | bytes 6291460
  70.6 4.9 %copy-start.4 = (bf16[1024,768]{1,0:T(8,128)(2,1)S(1)}, bf16[1024,768]{1,0:T(8,128)(2,1)}, u32[]{:S(2)}) copy-start(bf16[1024,768]{1,0:T(8,128)(2,1)} %copy-done.3) | copy-start | bytes 4718596
  82.5 0.7 copy-start.6
  90.2 1.0 copy-start.8
  90.2 1.0 copy-start.12
  98.2 0.7 copy-start.10
  98.2 2.7 %copy-start.13 = (f32[4,128]{1,0:T(4,128)}, f32[4,128]{1,0:T(4,128)S(1)}, u32[]{:S(2)}) copy-start(f32[4,128]{1,0:T(4,128)S(1)} %get-tuple-element.169) | copy-start | bytes 6148
  101.0 7.5 %copy-start.9 = (f32[512,64]{0,1:T(8,128)S(1)}, f32[512,64]{0,1:T(8,128)}, u32[]{:S(2)}) copy-start(f32[512,64]{0,1:T(8,128)} %copy-done.8) | copy-start | bytes 393220
  101.0 7.5 %copy-start.11 = (f32[512,64]{0,1:T(8,128)S(1)}, f32[512,64]{0,1:T(8,128)}, u32[]{:S(2)}) copy-start(f32[512,64]{0,1:T(8,128)} %copy-done.10) | copy-start | bytes 393220
  101.0 16.8 %collective-permute-start.6 = (f32[520,128]{1,0:T(8,128)}, f32[520,128]{1,0:T(8,128)}, u32[]{:S(2)}, u32[]{:S(2)}) collective-permute-start(f32[520,128]{1,0:T(8,128)} %pad_maximum_fusion.3), channel_id=1, source_target_pairs={{8,0},{12,4},{16,8},{20,12},{24,16},{28,20},{0,24},{4,28},{9,1},{1... | collective-permute-start | bytes 798728 | tf_op jit(solution)/shard_map/ppermute | solution.py:20
  107.9 0.5 copy-start.14
  111.2 11.4 %collective-permute-start.5 = (f32[520,128]{1,0:T(8,128)}, f32[520,128]{1,0:T(8,128)}, u32[]{:S(2)}, u32[]{:S(2)}) collective-permute-start(f32[520,128]{1,0:T(8,128)} %pad_maximum_fusion.2), channel_id=1, source_target_pairs={{28,0},{0,4},{4,8},{8,12},{12,16},{16,20},{20,24},{24,28},{29,1},{... | collective-permute-start | bytes 798728 | tf_op jit(solution)/shard_map/ppermute | solution.py:20
  119.1 5.9 %copy-start.16 = (f32[1024]{0:T(1024)S(1)}, f32[1024]{0:T(1024)}, u32[]{:S(2)}) copy-start(f32[1024]{0:T(1024)} %get-tuple-element.260) | copy-start | bytes 12292
  128.7 1.3 collective-permute-start.9
  130.0 3.8 %collective-permute-start.10 = (f32[35,128]{1,0:T(8,128)S(1)}, f32[35,128]{1,0:T(8,128)S(1)}, u32[]{:S(2)}, u32[]{:S(2)}) collective-permute-start(f32[35,128]{1,0:T(8,128)S(1)} %pad_maximum_fusion.9), channel_id=1, source_target_pairs={{0,2},{1,3},{2,0},{3,1},{4,6},{5,7},{6,4},{7,5},{8,10},{9,11},{10,... | collective-permute-start | bytes 53768 | tf_op jit(solution)/shard_map/ppermute | solution.py:196
  133.9 3.8 %collective-permute-start.11 = (f32[37,128]{1,0:T(8,128)S(1)}, f32[37,128]{1,0:T(8,128)S(1)}, u32[]{:S(2)}, u32[]{:S(2)}) collective-permute-start(f32[37,128]{1,0:T(8,128)S(1)} %pad_maximum_fusion.10), channel_id=1, source_target_pairs={{0,4},{4,0},{8,12},{12,8},{16,20},{20,16},{24,28},{28,24},{1,5},{5... | collective-permute-start | bytes 56840 | tf_op jit(solution)/shard_map/ppermute | solution.py:196
  137.8 3.9 %collective-permute-start.12 = (f32[41,128]{1,0:T(8,128)S(1)}, f32[41,128]{1,0:T(8,128)S(1)}, u32[]{:S(2)}, u32[]{:S(2)}) collective-permute-start(f32[41,128]{1,0:T(8,128)S(1)} %pad_maximum_fusion.6), channel_id=1, source_target_pairs={{0,8},{4,12},{8,0},{12,4},{16,24},{20,28},{24,16},{28,20},{1,9},{5... | collective-permute-start | bytes 62984 | tf_op jit(solution)/shard_map/ppermute | solution.py:196
  141.7 9.8 %collective-permute-start.13 = (f32[49,128]{1,0:T(8,128)S(1)}, f32[49,128]{1,0:T(8,128)S(1)}, u32[]{:S(2)}, u32[]{:S(2)}) collective-permute-start(f32[49,128]{1,0:T(8,128)S(1)} %pad_maximum_fusion.4), channel_id=1, source_target_pairs={{0,16},{4,20},{8,24},{12,28},{16,0},{20,4},{24,8},{28,12},{1,17},{... | collective-permute-start | bytes 75272 | tf_op jit(solution)/shard_map/ppermute | solution.py:196
  146.4 15.8 %collective-permute-start.8 = (f32[1024,64]{0,1:T(8,128)S(1)}, f32[1024,64]{0,1:T(8,128)S(1)}, u32[]{:S(2)}, u32[]{:S(2)}) collective-permute-start(f32[1024,64]{0,1:T(8,128)S(1)} %get-tuple-element.249), channel_id=1, source_target_pairs={{24,0},{28,4},{0,8},{4,12},{8,16},{12,20},{16,24},{20,28},{25,1},{... | collective-permute-start | bytes 786440 | tf_op jit(solution)/shard_map/ppermute | solution.py:20
  147.9 14.3 %collective-permute-start.7 = (f32[1024,64]{0,1:T(8,128)S(1)}, f32[1024,64]{0,1:T(8,128)S(1)}, u32[]{:S(2)}, u32[]{:S(2)}) collective-permute-start(f32[1024,64]{0,1:T(8,128)S(1)} %get-tuple-element.249), channel_id=1, source_target_pairs={{4,0},{8,4},{12,8},{16,12},{20,16},{24,20},{28,24},{0,28},{5,1},{9... | collective-permute-start | bytes 786440 | tf_op jit(solution)/shard_map/ppermute | solution.py:20
  164.0 0.8 copy-start.7
  169.2 2.5 %copy-start = (bf16[1024,1024]{1,0:T(8,128)(2,1)S(1)}, bf16[1024,1024]{1,0:T(8,128)(2,1)}, u32[]{:S(2)}) copy-start(bf16[1024,1024]{1,0:T(8,128)(2,1)} %get-tuple-element.92) | copy-start | bytes 6291460 | tf_op jit(solution)/shard_map/cond
  172.9 6.7 %collective-permute-start.15 = (f32[1024,64]{0,1:T(8,128)}, f32[1024,64]{0,1:T(8,128)}, u32[]{:S(2)}, u32[]{:S(2)}) collective-permute-start(f32[1024,64]{0,1:T(8,128)} %add.250), channel_id=1, source_target_pairs={{8,0},{12,4},{16,8},{20,12},{24,16},{28,20},{0,24},{4,28},{9,1},{1... | collective-permute-start | bytes 786440 | tf_op jit(solution)/shard_map/ppermute | solution.py:20
  174.2 9.1 %collective-permute-start.14 = (f32[1024,64]{0,1:T(8,128)S(1)}, f32[1024,64]{0,1:T(8,128)S(1)}, u32[]{:S(2)}, u32[]{:S(2)}) collective-permute-start(f32[1024,64]{0,1:T(8,128)S(1)} %add.248), channel_id=1, source_target_pairs={{28,0},{0,4},{4,8},{8,12},{12,16},{16,20},{20,24},{24,28},{29,1},{... | collective-permute-start | bytes 786440 | tf_op jit(solution)/shard_map/ppermute | solution.py:20
  187.2 1.3 collective-permute-start.16
  188.5 3.8 %collective-permute-start.17 = (f32[35,128]{1,0:T(8,128)S(1)}, f32[35,128]{1,0:T(8,128)S(1)}, u32[]{:S(2)}, u32[]{:S(2)}) collective-permute-start(f32[35,128]{1,0:T(8,128)S(1)} %pad_maximum_fusion.12), channel_id=1, source_target_pairs={{0,2},{1,3},{2,0},{3,1},{4,6},{5,7},{6,4},{7,5},{8,10},{9,11},{10,... | collective-permute-start | bytes 53768 | tf_op jit(solution)/shard_map/ppermute | solution.py:196
  192.4 3.8 %collective-permute-start.18 = (f32[37,128]{1,0:T(8,128)S(1)}, f32[37,128]{1,0:T(8,128)S(1)}, u32[]{:S(2)}, u32[]{:S(2)}) collective-permute-start(f32[37,128]{1,0:T(8,128)S(1)} %pad_maximum_fusion.13), channel_id=1, source_target_pairs={{0,4},{4,0},{8,12},{12,8},{16,20},{20,16},{24,28},{28,24},{1,5},{5... | collective-permute-start | bytes 56840 | tf_op jit(solution)/shard_map/ppermute | solution.py:196
  196.2 3.9 %collective-permute-start.19 = (f32[41,128]{1,0:T(8,128)S(1)}, f32[41,128]{1,0:T(8,128)S(1)}, u32[]{:S(2)}, u32[]{:S(2)}) collective-permute-start(f32[41,128]{1,0:T(8,128)S(1)} %pad_maximum_fusion.7), channel_id=1, source_target_pairs={{0,8},{4,12},{8,0},{12,4},{16,24},{20,28},{24,16},{28,20},{1,9},{5... | collective-permute-start | bytes 62984 | tf_op jit(solution)/shard_map/ppermute | solution.py:196
  200.2 4.9 %collective-permute-start.20 = (f32[49,128]{1,0:T(8,128)S(1)}, f32[49,128]{1,0:T(8,128)S(1)}, u32[]{:S(2)}, u32[]{:S(2)}) collective-permute-start(f32[49,128]{1,0:T(8,128)S(1)} %pad_maximum_fusion.5), channel_id=1, source_target_pairs={{0,16},{4,20},{8,24},{12,28},{16,0},{20,4},{24,8},{28,12},{1,17},{... | collective-permute-start | bytes 75272 | tf_op jit(solution)/shard_map/ppermute | solution.py:196

commit v19 on v17

--- a/solution.py
+++ b/solution.py
@@ -423,8 +423,11 @@
             weights[offset] = bases[position + 1].astype(jnp.bfloat16)
         current = weights[0]
         parts = {offset: zero_part for offset in units}
-        for (left, right), owned, affinity in zip(pair_plan, owned_list, tiles):
-            row_part, col_part = later_pass(owned, affinity, weights[left], weights[right])
+        first_return = fetch_offsets[0]
+        order = sorted(range(len(pair_plan)), key=lambda i: first_return not in pair_plan[i])
+        for i in order:
+            left, right = pair_plan[i]
+            row_part, col_part = later_pass(owned_list[i], tiles[i], weights[left], weights[right])
             parts[left] = parts[left] + row_part
             parts[right] = parts[right] + col_part
         product = row_product(near_tile, current) + parts[0]

time: 219 us -> 220 us (level)
  matrix products: 60.8 us -> 43.9 us
  starting transfers between devices: 23.6 us -> 37.6 us
  local copies, waits for them, and re-layouts: 12.5 us -> 14.8 us
    ppermute x11, starting transfers between devices: 20.2 us -> 33.3 us  [shifted(): return lax.ppermute(block, axis, route)]
    dot_general x6 -> x4, matrix products: 24 us -> 16.5 us  [scores_tile(): lax.dot_general(leftside_block, right_block, (((1,), (1,)), ((), ())), pr...]
    dot_general x10 -> x7, matrix products: 18 us -> 12.2 us  [row_product(): return jnp.dot(affinity, weights, preferred_element_type=jnp.float32)]
    dot_general x8 -> x5, matrix products: 12 us -> 8.35 us  [col_product(): lax.dot_general(affinity, weights, (((0,), (0,)), ((), ())), preferred_el...]
    ppermute x11, waiting for transfers between devices: 50.2 us -> 52.5 us  [shifted(): return lax.ppermute(block, axis, route)]
    another operation x0 -> x11, local copies, waits for them, and re-layouts: none -> 2.27 us
  transfers between devices with their start and end apart: 21 -> 21, of which waited for: 13 -> 13; matrix products, arithmetic and copies ran while one was open for 27% -> 24% of each run, Pallas kernels for 4% -> 4%
where the time goes in v19:
time: 220 us; the launch traced here: 219 us
  waiting for transfers between devices  78.9 us (36%)
  matrix products  43.9 us (20%)
  starting transfers between devices  37.6 us (17%)
  other arithmetic  23.9 us (11%)
  Pallas kernels  16.9 us (8%)
  local copies, waits for them, and re-layouts  14.8 us (7%)
  between operations  3.14 us (1%)
    ppermute x11, waiting for transfers between devices, shifted(): return lax.ppermute(block, axis, route)  52.5 us
    ppermute x11, starting transfers between devices, shifted(): return lax.ppermute(block, axis, route)  33.3 us
    ppermute x10, waiting for transfers between devices, butterfly(): other = lax.ppermute(block, axis, route)  26.3 us
    pallas_call x2, Pallas kernels, factor_inverse(): pl.pallas_call(factor_kernel, out_shape=jax.ShapeDtypeStruct(gram_matrix....  16.9 us
    dot_general x4, matrix products, scores_tile(): lax.dot_general(leftside_block, right_block, (((1,), (1,)), ((), ())), pr...  16.5 us
    dot_general x7, matrix products, row_product(): return jnp.dot(affinity, weights, preferred_element_type=jnp.float32)  12.2 us
    dot_general x5, matrix products, col_product(): lax.dot_general(affinity, weights, (((0,), (0,)), ((), ())), preferred_el...  8.35 us
    dot_general x8, matrix products, hdot(): jnp.dot(left, right, precision=lax.Precision.HIGHEST, preferred_element_t...  6.78 us
  transfers between devices with their start and end apart: 21, of which 13 were waited for; matrix products, arithmetic and copies ran while one was open for 24% of the time, Pallas kernels for 4%

profile of v19, /device:TPU:0, one launch (start us, length us, event | category | flops | bytes accessed | tf_op | source)
XLA Modules:
  0.0 219.2 jit_solution(15125218381831670039)
XLA Ops:
  0.6 3.1 %collective-permute-start.2 = (bf16[1024,768]{1,0:T(8,128)(2,1)}, bf16[1024,768]{1,0:T(8,128)(2,1)}, u32[]{:S(2)}, u32[]{:S(2)}) collective-permute-start(bf16[1024,768]{1,0:T(8,128)(2,1)} %param.21), channel_id=1, source_target_pairs={{24,0},{28,4},{0,8},{4,12},{8,16},{12,20},{16,24},{20,28},{25,1},{... | collective-permute-start | bytes 4718600 | tf_op jit(solution)/shard_map/ppermute | solution.py:20
  3.7 1.8 fusion.1
  6.0 1.1 copy-done.3
  7.1 1.1 fusion.45
  8.2 3.3 %collective-permute-start.3 = (bf16[512,768]{1,0:T(8,128)(2,1)S(1)}, bf16[512,768]{1,0:T(8,128)(2,1)}, u32[]{:S(2)}, u32[]{:S(2)}) collective-permute-start(bf16[512,768]{1,0:T(8,128)(2,1)S(1)} %get-tuple-element.255), channel_id=1, source_target_pairs={{4,0},{8,4},{12,8},{16,12},{20,16},{24,20},{28,24},{0,28},{5,1},{9... | collective-permute-start | bytes 2359304 | tf_op jit(solution)/shard_map/ppermute | solution.py:20
  12.7 5.0 %collective-permute-start = (bf16[512,768]{1,0:T(8,128)(2,1)}, bf16[512,768]{1,0:T(8,128)(2,1)}, u32[]{:S(2)}, u32[]{:S(2)}) collective-permute-start(bf16[512,768]{1,0:T(8,128)(2,1)} %get-tuple-element.256), channel_id=1, source_target_pairs={{4,0},{8,4},{12,8},{16,12},{20,16},{24,20},{28,24},{0,28},{5,1},{9... | collective-permute-start | bytes 2359304 | tf_op jit(solution)/shard_map/ppermute | solution.py:20
  17.7 4.4 %convert_reduce_fusion.10 = (f32[1024]{0:T(1024)}, bf16[1024,1024]{0,1:T(8,128)(2,1)S(1)}) fusion(bf16[1024,768]{1,0:T(8,128)(2,1)} %copy-done.3), kind=kOutput, calls=%fused_computation.15 | convolution fusion | flops 1616903168 | bytes 3674112 | tf_op jit(solution)/shard_map/dot_general | solution.py:55
  22.1 1.0 fusion.37
  24.9 36.5 %collective-permute-done.1 = bf16[1024,64]{1,0:T(8,128)(2,1)} collective-permute-done((bf16[1024,64]{1,0:T(8,128)(2,1)}, bf16[1024,64]{1,0:T(8,128)(2,1)}, u32[]{:S(2)}, u32[]{:S(2)}) %collective-permute-start.1) | collective-permute-done | bytes 131104 | tf_op jit(solution)/shard_map/ppermute | solution.py:20
  61.3 0.9 slice.183
  62.3 8.3 %conditional.10 = (bf16[1024,512]{1,0:T(8,128)(2,1)}, f32[1024,64]{0,1:T(8,128)}, f32[1024]{0:T(1024)S(1)}, f32[512,64]{0,1:T(8,128)}, f32[512]{0:T(512)S(1)}) conditional(s32[]{:T(128)} %convert_element_type.80, () %tuple.85, (bf16[1024,768]{1,0:T(8,128)(2,1)}, bf16[512,768]{1,0:T(8,128)(2,1)}, bf16[512,64]{1,0:T(8,128)(2,1)S(1)}, ...), branch_computations={%region_8.9_spmd, %region_9.12_spmd} | conditional | flops 942144000 | bytes 6101032 | solution.py:166
  62.3 3.7 %convert_reduce_fusion.2 = (f32[512]{0:T(512)S(1)}, f32[1024]{0:T(1024)S(1)}, bf16[1024,512]{1,0:T(8,128)(2,1)}) fusion(bf16[1024,768]{1,0:T(8,128)(2,1)} %get-tuple-element.68, bf16[512,768]{1,0:T(8,128)(2,1)} %get-tuple-element.69), kind=kOutput, calls=%fused_computation.3 | convolution fusion | flops 807926272 | bytes 3414016 | tf_op jit(solution)/shard_map/cond/branch_1_fun/dot_general | solution.py:55
  66.0 2.4 %fusion.55 = f32[1024,64]{0,1:T(8,128)} fusion(bf16[1024,512]{1,0:T(8,128)(2,1)} %get-tuple-element.279, bf16[512,64]{1,0:T(8,128)(2,1)S(1)} %get-tuple-element.70), kind=kOutput, calls=%fused_computation.146 | convolution fusion | flops 67108864 | bytes 1376256 | tf_op jit(solution)/shard_map/cond/branch_1_fun/dot_general | solution.py:62
  68.4 2.2 fusion.56
  70.6 1.9 fusion.4
  72.5 3.0 %fusion.6 = bf16[1024,768]{1,0:T(8,128)(2,1)} fusion(bf16[1024,768]{1,0:T(8,128)(2,1)} %collective-permute-done.2, f32[1024]{0:T(1024)S(1)} %add_rsqrt_fusion), kind=kLoop, calls=%fused_computation.29 | loop fusion | flops 3145728 | bytes 3149824 | tf_op jit(solution)/shard_map/convert_element_type | solution.py:51
  75.5 7.1 %conditional.9 = (bf16[1024,1024]{1,0:T(8,128)(2,1)}, f32[1024,64]{0,1:T(8,128)S(1)}, f32[1024]{0:T(1024)S(1)}, f32[1024]{0:T(1024)S(1)}) conditional(s32[]{:T(128)} %convert_element_type.77, () %tuple.83, (bf16[1024,768]{1,0:T(8,128)(2,1)}, bf16[1024,768]{1,0:T(8,128)(2,1)S(1)}, bf16[1024,64]{0,1:T(8,128)(2,1)S(1)}) %tuple.159), branch_computations={%region_3.4_spmd, %region_4.0_spmd} | conditional | flops 1750071296 | bytes 7741472 | solution.py:125
  75.5 4.7 %convert_reduce_fusion = (f32[1024]{0:T(1024)S(1)}, f32[1024]{0:T(1024)S(1)}, bf16[1024,1024]{1,0:T(8,128)(2,1)}) fusion(bf16[1024,768]{1,0:T(8,128)(2,1)} %get-tuple-element.65, bf16[1024,768]{1,0:T(8,128)(2,1)S(1)} %get-tuple-element.66), kind=kOutput, calls=%fused_computation | convolution fusion | flops 1615853568 | bytes 5251072 | tf_op jit(solution)/shard_map/cond/branch_1_fun/dot_general | solution.py:55
  80.2 2.3 %fusion.54 = f32[1024,64]{0,1:T(8,128)S(1)} fusion(bf16[1024,1024]{1,0:T(8,128)(2,1)} %get-tuple-element.270, bf16[1024,64]{0,1:T(8,128)(2,1)S(1)} %get-tuple-element.211), kind=kOutput, calls=%fused_computation.145 | convolution fusion | flops 134217728 | bytes 2490368 | tf_op jit(solution)/shard_map/cond/branch_1_fun/dot_general | solution.py:62
  83.2 1.1 conditional.11
  83.2 1.0 broadcast.154
  84.4 1.0 slice.141
  85.4 1.2 conditional.14
  85.4 1.1 broadcast.166
  87.2 1.0 add_add_fusion
  89.3 15.4 %collective-permute-start.6 = (f32[520,128]{1,0:T(8,128)}, f32[520,128]{1,0:T(8,128)}, u32[]{:S(2)}, u32[]{:S(2)}) collective-permute-start(f32[520,128]{1,0:T(8,128)} %pad_maximum_fusion.3), channel_id=1, source_target_pairs={{8,0},{12,4},{16,8},{20,12},{24,16},{28,20},{0,24},{4,28},{9,1},{1... | collective-permute-start | bytes 798728 | tf_op jit(solution)/shard_map/ppermute | solution.py:20
  104.8 6.9 %conditional.12 = (bf16[1024,512]{1,0:T(8,128)(2,1)}, f32[1024,64]{0,1:T(8,128)S(1)}, f32[1024]{0:T(1024)S(1)}, f32[512,64]{0,1:T(8,128)S(1)}, f32[4,128]{1,0:T(4,128)S(1)}) conditional(s32[]{:T(128)} %convert_element_type.80, () %tuple.90, (bf16[1024,768]{1,0:T(8,128)(2,1)}, bf16[512,768]{1,0:T(8,128)(2,1)}, bf16[512,64]{1,0:T(8,128)(2,1)S(1)}, ...), branch_computations={%region_17.18_spmd, %region_18.21_spmd} | conditional | flops 942144000 | bytes 6101032 | solution.py:166
  104.8 3.7 %convert_reduce_fusion.6 = (f32[512]{0:T(512)S(1)}, f32[1024]{0:T(1024)S(1)}, bf16[1024,512]{1,0:T(8,128)(2,1)}) fusion(bf16[1024,768]{1,0:T(8,128)(2,1)} %get-tuple-element.76, bf16[512,768]{1,0:T(8,128)(2,1)} %get-tuple-element.77), kind=kOutput, calls=%fused_computation.9 | convolution fusion | flops 807926272 | bytes 3414016 | tf_op jit(solution)/shard_map/cond/branch_1_fun/dot_general | solution.py:55
  108.5 1.7 fusion.59
  110.1 1.5 fusion.60
  112.2 0.9 maximum_add_fusion
  115.6 2.1 conditional.13
  115.7 2.1 fusion.47
  117.8 1.0 slice.185
  119.1 5.2 %collective-permute-done.5 = f32[520,128]{1,0:T(8,128)} collective-permute-done((f32[520,128]{1,0:T(8,128)}, f32[520,128]{1,0:T(8,128)}, u32[]{:S(2)}, u32[]{:S(2)}) %collective-permute-start.5) | collective-permute-done | bytes 266272 | tf_op jit(solution)/shard_map/ppermute | solution.py:20
  124.3 1.0 slice.184
  125.6 1.1 fusion.43
  126.8 1.3 broadcast_multiply_fusion
  130.6 1.2 collective-permute-done.9
  131.8 1.6 collective-permute-start.10
  133.3 2.3 %collective-permute-done.10 = f32[35,128]{1,0:T(8,128)S(1)} collective-permute-done((f32[35,128]{1,0:T(8,128)S(1)}, f32[35,128]{1,0:T(8,128)S(1)}, u32[]{:S(2)}, u32[]{:S(2)}) %collective-permute-start.10) | collective-permute-done | bytes 17952 | tf_op jit(solution)/shard_map/ppermute | solution.py:196
  135.7 3.8 %collective-permute-done.11 = f32[37,128]{1,0:T(8,128)S(1)} collective-permute-done((f32[37,128]{1,0:T(8,128)S(1)}, f32[37,128]{1,0:T(8,128)S(1)}, u32[]{:S(2)}, u32[]{:S(2)}) %collective-permute-start.11) | collective-permute-done | bytes 18976 | tf_op jit(solution)/shard_map/ppermute | solution.py:196
  139.7 3.8 %collective-permute-done.12 = f32[41,128]{1,0:T(8,128)S(1)} collective-permute-done((f32[41,128]{1,0:T(8,128)S(1)}, f32[41,128]{1,0:T(8,128)S(1)}, u32[]{:S(2)}, u32[]{:S(2)}) %collective-permute-start.12) | collective-permute-done | bytes 21024 | tf_op jit(solution)/shard_map/ppermute | solution.py:196
  143.5 4.1 %pad_maximum_fusion = (bf16[1024,1024]{1,0:T(8,128)(2,1)S(1)}, bf16[1024,1024]{1,0:T(8,128)(2,1)}) fusion(bf16[1024,512]{1,0:T(8,128)(2,1)} %get-tuple-element.180, bf16[1024,512]{1,0:T(8,128)(2,1)} %get-tuple-element.179, bf16[1024,512]{1,0:T(8,128)(2,1)} %get-tuple-element.185, bf16[1024,512]{1,0:T(8,128)(2,1)} %get-tuple-element.184), kind=kLoop, calls=%fused_computation.30 | loop fusion | flops 8388608 | bytes 8388608 | tf_op jit(solution)/shard_map/concatenate | solution.py:379
  147.9 3.0 %collective-permute-start.7 = (f32[1024,64]{0,1:T(8,128)S(1)}, f32[1024,64]{0,1:T(8,128)S(1)}, u32[]{:S(2)}, u32[]{:S(2)}) collective-permute-start(f32[1024,64]{0,1:T(8,128)S(1)} %get-tuple-element.249), channel_id=1, source_target_pairs={{4,0},{8,4},{12,8},{16,12},{20,16},{24,20},{28,24},{0,28},{5,1},{9... | collective-permute-start | bytes 786440 | tf_op jit(solution)/shard_map/ppermute | solution.py:20
  152.6 0.9 fusion.12.gram_ref
  153.5 8.4 %shard_map.50 = f32[64,64]{1,0:T(8,128)} custom-call(f32[64,64]{1,0:T(8,128)} %fusion.12.gram_ref), custom_call_target="tpu_custom_call" | custom-call | tf_op jit(solution)/shard_map/pallas_call | solution.py:244
  161.9 1.7 convolution_convert_fusion
  164.4 4.4 %conditional.16 = (f32[1024,64]{0,1:T(8,128)S(1)}, f32[1024,64]{0,1:T(8,128)S(1)}) conditional(s32[]{:T(128)} %convert_element_type.77, () %tuple.98, (bf16[1024,1024]{1,0:T(8,128)(2,1)}, bf16[1024,64]{0,1:T(8,128)(2,1)S(1)}, bf16[1024,64]{0,1:T(8,128)(2,1)S(1)}) %tuple.99), branch_computations={%region_34.35_spmd, %region_35.36_spmd} | conditional | flops 268435456 | bytes 4980752 | solution.py:180
  164.5 2.3 %fusion.50 = f32[1024,64]{0,1:T(8,128)S(1)} fusion(bf16[1024,1024]{1,0:T(8,128)(2,1)} %get-tuple-element.89, bf16[1024,64]{0,1:T(8,128)(2,1)S(1)} %get-tuple-element.224), kind=kOutput, calls=%fused_computation.141 | convolution fusion | flops 134217728 | bytes 2490368 | tf_op jit(solution)/shard_map/cond/branch_1_fun/dot_general | solution.py:62
  166.8 2.1 fusion.51
  169.6 1.2 conditional.15
  170.9 2.6 %collective-permute-start.14 = (f32[1024,64]{0,1:T(8,128)S(1)}, f32[1024,64]{0,1:T(8,128)S(1)}, u32[]{:S(2)}, u32[]{:S(2)}) collective-permute-start(f32[1024,64]{0,1:T(8,128)S(1)} %add.248), channel_id=1, source_target_pairs={{28,0},{0,4},{4,8},{8,12},{12,16},{16,20},{20,24},{24,28},{29,1},{... | collective-permute-start | bytes 786440 | tf_op jit(solution)/shard_map/ppermute | solution.py:20
  173.5 3.9 %collective-permute-done.15 = f32[1024,64]{0,1:T(8,128)} collective-permute-done((f32[1024,64]{0,1:T(8,128)}, f32[1024,64]{0,1:T(8,128)}, u32[]{:S(2)}, u32[]{:S(2)}) %collective-permute-start.15) | collective-permute-done | bytes 262176 | tf_op jit(solution)/shard_map/ppermute | solution.py:20
  177.4 7.0 %collective-permute-done.14 = f32[1024,64]{0,1:T(8,128)S(1)} collective-permute-done((f32[1024,64]{0,1:T(8,128)S(1)}, f32[1024,64]{0,1:T(8,128)S(1)}, u32[]{:S(2)}, u32[]{:S(2)}) %collective-permute-start.14) | collective-permute-done | bytes 262176 | tf_op jit(solution)/shard_map/ppermute | solution.py:20
  184.4 2.2 %fusion.40 = (f32[64]{0:T(128)S(1)}, f32[1024,64]{0,1:T(8,128)S(1)}) fusion(f32[1024]{0:T(1024)S(1)} %get-tuple-element.245, f32[1024,64]{0,1:T(8,128)} %collective-permute-done.15, f32[1024,64]{0,1:T(8,128)S(1)} %collective-permute-done.14, f32[1024,64]{0,1:T(8,128)S(1)} %get-tuple-element.181, f32[1024,64]{0,1:T(8,128)S(1)} %get-tuple-element.182, ...), kind=kOutput, calls=%fused_computation.132 | convolution fusion | flops 134610880 | bytes 3543296 | tf_op jit(solution)/shard_map/dot_general | solution.py:62
  188.3 1.2 collective-permute-done.16
  190.2 3.1 %collective-permute-done.17 = f32[35,128]{1,0:T(8,128)S(1)} collective-permute-done((f32[35,128]{1,0:T(8,128)S(1)}, f32[35,128]{1,0:T(8,128)S(1)}, u32[]{:S(2)}, u32[]{:S(2)}) %collective-permute-start.17) | collective-permute-done | bytes 17952 | tf_op jit(solution)/shard_map/ppermute | solution.py:196
  193.5 3.8 %collective-permute-done.18 = f32[37,128]{1,0:T(8,128)S(1)} collective-permute-done((f32[37,128]{1,0:T(8,128)S(1)}, f32[37,128]{1,0:T(8,128)S(1)}, u32[]{:S(2)}, u32[]{:S(2)}) %collective-permute-start.18) | collective-permute-done | bytes 18976 | tf_op jit(solution)/shard_map/ppermute | solution.py:196
  197.8 3.4 %collective-permute-done.19 = f32[41,128]{1,0:T(8,128)S(1)} collective-permute-done((f32[41,128]{1,0:T(8,128)S(1)}, f32[41,128]{1,0:T(8,128)S(1)}, u32[]{:S(2)}, u32[]{:S(2)}) %collective-permute-start.19) | collective-permute-done | bytes 21024 | tf_op jit(solution)/shard_map/ppermute | solution.py:196
  201.2 1.1 collective-permute-start.20
  202.4 3.9 %collective-permute-done.20 = f32[49,128]{1,0:T(8,128)S(1)} collective-permute-done((f32[49,128]{1,0:T(8,128)S(1)}, f32[49,128]{1,0:T(8,128)S(1)}, u32[]{:S(2)}, u32[]{:S(2)}) %collective-permute-start.20) | collective-permute-done | bytes 25120 | tf_op jit(solution)/shard_map/ppermute | solution.py:196
  208.8 8.4 %shard_map.51 = f32[64,64]{1,0:T(8,128)} custom-call(f32[64,64]{1,0:T(8,128)} %fusion.10.gram_ref), custom_call_target="tpu_custom_call" | custom-call | tf_op jit(solution)/shard_map/pallas_call | solution.py:244
  217.2 1.9 fusion.18
  (154 shorter events, 20.8 us)
Async XLA Ops:
  0.6 4.9 %copy-start.2 = (bf16[1024,768]{1,0:T(8,128)(2,1)S(1)}, bf16[1024,768]{1,0:T(8,128)(2,1)}, u32[]{:S(2)}) copy-start(bf16[1024,768]{1,0:T(8,128)(2,1)} %param.21) | copy-start | bytes 4718596
  0.6 69.9 %collective-permute-start.2 = (bf16[1024,768]{1,0:T(8,128)(2,1)}, bf16[1024,768]{1,0:T(8,128)(2,1)}, u32[]{:S(2)}, u32[]{:S(2)}) collective-permute-start(bf16[1024,768]{1,0:T(8,128)(2,1)} %param.21), channel_id=1, source_target_pairs={{24,0},{28,4},{0,8},{4,12},{8,16},{12,20},{16,24},{20,28},{25,1},{... | collective-permute-start | bytes 4718600 | tf_op jit(solution)/shard_map/ppermute | solution.py:20
  6.0 1.2 copy-start.3
  7.1 4.4 %copy-start.5 = (bf16[1024,64]{0,1:T(8,128)(2,1)S(1)}, bf16[1024,64]{0,1:T(8,128)(2,1)}, u32[]{:S(2)}) copy-start(bf16[1024,64]{0,1:T(8,128)(2,1)} %param.22) | copy-start | bytes 393220
  8.2 54.0 %collective-permute-start.3 = (bf16[512,768]{1,0:T(8,128)(2,1)S(1)}, bf16[512,768]{1,0:T(8,128)(2,1)}, u32[]{:S(2)}, u32[]{:S(2)}) collective-permute-start(bf16[512,768]{1,0:T(8,128)(2,1)S(1)} %get-tuple-element.255), channel_id=1, source_target_pairs={{4,0},{8,4},{12,8},{16,12},{20,16},{24,20},{28,24},{0,28},{5,1},{9... | collective-permute-start | bytes 2359304 | tf_op jit(solution)/shard_map/ppermute | solution.py:20
  12.4 49.0 %collective-permute-start.1 = (bf16[1024,64]{1,0:T(8,128)(2,1)}, bf16[1024,64]{1,0:T(8,128)(2,1)}, u32[]{:S(2)}, u32[]{:S(2)}) collective-permute-start(bf16[1024,64]{1,0:T(8,128)(2,1)} %copy.18), channel_id=1, source_target_pairs={{4,0},{8,4},{12,8},{16,12},{20,16},{24,20},{28,24},{0,28},{5,1},{9... | collective-permute-start | bytes 393224 | tf_op jit(solution)/shard_map/ppermute | solution.py:20
  12.7 69.9 %collective-permute-start.4 = (bf16[1024,64]{1,0:T(8,128)(2,1)}, bf16[1024,64]{1,0:T(8,128)(2,1)S(1)}, u32[]{:S(2)}, u32[]{:S(2)}) collective-permute-start(bf16[1024,64]{1,0:T(8,128)(2,1)} %copy.18), channel_id=1, source_target_pairs={{24,0},{28,4},{0,8},{4,12},{8,16},{12,20},{16,24},{20,28},{25,1},{... | collective-permute-start | bytes 393224 | tf_op jit(solution)/shard_map/ppermute | solution.py:20
  12.7 9.4 %copy-start.15 = (s32[32,3]{0,1:T(4,128)S(1)}, s32[32,3]{0,1:T(4,128)}, u32[]{:S(2)}) copy-start(s32[32,3]{0,1:T(4,128)} %param.23) | copy-start | bytes 1156
  12.7 71.7 %collective-permute-start = (bf16[512,768]{1,0:T(8,128)(2,1)}, bf16[512,768]{1,0:T(8,128)(2,1)}, u32[]{:S(2)}, u32[]{:S(2)}) collective-permute-start(bf16[512,768]{1,0:T(8,128)(2,1)} %get-tuple-element.256), channel_id=1, source_target_pairs={{4,0},{8,4},{12,8},{16,12},{20,16},{24,20},{28,24},{0,28},{5,1},{9... | collective-permute-start | bytes 2359304 | tf_op jit(solution)/shard_map/ppermute | solution.py:20
  22.1 93.1 %copy-start.1 = (bf16[1024,1024]{0,1:T(8,128)(2,1)}, bf16[1024,1024]{0,1:T(8,128)(2,1)S(1)}, u32[]{:S(2)}) copy-start(bf16[1024,1024]{0,1:T(8,128)(2,1)S(1)} %get-tuple-element.261) | copy-start | bytes 6291460
  70.6 4.9 %copy-start.4 = (bf16[1024,768]{1,0:T(8,128)(2,1)S(1)}, bf16[1024,768]{1,0:T(8,128)(2,1)}, u32[]{:S(2)}) copy-start(bf16[1024,768]{1,0:T(8,128)(2,1)} %copy-done.3) | copy-start | bytes 4718596
  82.5 0.7 copy-start.6
  84.4 1.0 copy-start.8
  84.4 1.0 copy-start.12
  86.6 0.7 copy-start.10
  86.6 18.2 %copy-start.13 = (f32[4,128]{1,0:T(4,128)}, f32[4,128]{1,0:T(4,128)S(1)}, u32[]{:S(2)}) copy-start(f32[4,128]{1,0:T(4,128)S(1)} %get-tuple-element.169) | copy-start | bytes 6148
  89.3 22.9 %copy-start.9 = (f32[512,64]{0,1:T(8,128)S(1)}, f32[512,64]{0,1:T(8,128)}, u32[]{:S(2)}) copy-start(f32[512,64]{0,1:T(8,128)} %copy-done.8) | copy-start | bytes 393220
  89.3 22.9 %copy-start.11 = (f32[512,64]{0,1:T(8,128)S(1)}, f32[512,64]{0,1:T(8,128)}, u32[]{:S(2)}) copy-start(f32[512,64]{0,1:T(8,128)} %copy-done.10) | copy-start | bytes 393220
  89.3 28.5 %collective-permute-start.6 = (f32[520,128]{1,0:T(8,128)}, f32[520,128]{1,0:T(8,128)}, u32[]{:S(2)}, u32[]{:S(2)}) collective-permute-start(f32[520,128]{1,0:T(8,128)} %pad_maximum_fusion.3), channel_id=1, source_target_pairs={{8,0},{12,4},{16,8},{20,12},{24,16},{28,20},{0,24},{4,28},{9,1},{1... | collective-permute-start | bytes 798728 | tf_op jit(solution)/shard_map/ppermute | solution.py:20
  111.6 0.5 copy-start.14
  114.9 9.4 %collective-permute-start.5 = (f32[520,128]{1,0:T(8,128)}, f32[520,128]{1,0:T(8,128)}, u32[]{:S(2)}, u32[]{:S(2)}) collective-permute-start(f32[520,128]{1,0:T(8,128)} %pad_maximum_fusion.2), channel_id=1, source_target_pairs={{28,0},{0,4},{4,8},{8,12},{12,16},{16,20},{20,24},{24,28},{29,1},{... | collective-permute-start | bytes 798728 | tf_op jit(solution)/shard_map/ppermute | solution.py:20
  119.1 7.7 %copy-start.16 = (f32[1024]{0:T(1024)S(1)}, f32[1024]{0:T(1024)}, u32[]{:S(2)}) copy-start(f32[1024]{0:T(1024)} %get-tuple-element.260) | copy-start | bytes 12292
  130.5 1.3 collective-permute-start.9
  131.8 3.8 %collective-permute-start.10 = (f32[35,128]{1,0:T(8,128)S(1)}, f32[35,128]{1,0:T(8,128)S(1)}, u32[]{:S(2)}, u32[]{:S(2)}) collective-permute-start(f32[35,128]{1,0:T(8,128)S(1)} %pad_maximum_fusion.9), channel_id=1, source_target_pairs={{0,2},{1,3},{2,0},{3,1},{4,6},{5,7},{6,4},{7,5},{8,10},{9,11},{10,... | collective-permute-start | bytes 53768 | tf_op jit(solution)/shard_map/ppermute | solution.py:196
  135.7 3.8 %collective-permute-start.11 = (f32[37,128]{1,0:T(8,128)S(1)}, f32[37,128]{1,0:T(8,128)S(1)}, u32[]{:S(2)}, u32[]{:S(2)}) collective-permute-start(f32[37,128]{1,0:T(8,128)S(1)} %pad_maximum_fusion.10), channel_id=1, source_target_pairs={{0,4},{4,0},{8,12},{12,8},{16,20},{20,16},{24,28},{28,24},{1,5},{5... | collective-permute-start | bytes 56840 | tf_op jit(solution)/shard_map/ppermute | solution.py:196
  139.5 3.9 %collective-permute-start.12 = (f32[41,128]{1,0:T(8,128)S(1)}, f32[41,128]{1,0:T(8,128)S(1)}, u32[]{:S(2)}, u32[]{:S(2)}) collective-permute-start(f32[41,128]{1,0:T(8,128)S(1)} %pad_maximum_fusion.6), channel_id=1, source_target_pairs={{0,8},{4,12},{8,0},{12,4},{16,24},{20,28},{24,16},{28,20},{1,9},{5... | collective-permute-start | bytes 62984 | tf_op jit(solution)/shard_map/ppermute | solution.py:196
  143.5 7.4 %collective-permute-start.13 = (f32[49,128]{1,0:T(8,128)S(1)}, f32[49,128]{1,0:T(8,128)S(1)}, u32[]{:S(2)}, u32[]{:S(2)}) collective-permute-start(f32[49,128]{1,0:T(8,128)S(1)} %pad_maximum_fusion.4), channel_id=1, source_target_pairs={{0,16},{4,20},{8,24},{12,28},{16,0},{20,4},{24,8},{28,12},{1,17},{... | collective-permute-start | bytes 75272 | tf_op jit(solution)/shard_map/ppermute | solution.py:196
  147.6 14.3 %collective-permute-start.8 = (f32[1024,64]{0,1:T(8,128)S(1)}, f32[1024,64]{0,1:T(8,128)S(1)}, u32[]{:S(2)}, u32[]{:S(2)}) collective-permute-start(f32[1024,64]{0,1:T(8,128)S(1)} %get-tuple-element.249), channel_id=1, source_target_pairs={{24,0},{28,4},{0,8},{4,12},{8,16},{12,20},{16,24},{20,28},{25,1},{... | collective-permute-start | bytes 786440 | tf_op jit(solution)/shard_map/ppermute | solution.py:20
  147.9 14.0 %collective-permute-start.7 = (f32[1024,64]{0,1:T(8,128)S(1)}, f32[1024,64]{0,1:T(8,128)S(1)}, u32[]{:S(2)}, u32[]{:S(2)}) collective-permute-start(f32[1024,64]{0,1:T(8,128)S(1)} %get-tuple-element.249), channel_id=1, source_target_pairs={{4,0},{8,4},{12,8},{16,12},{20,16},{24,20},{28,24},{0,28},{5,1},{9... | collective-permute-start | bytes 786440 | tf_op jit(solution)/shard_map/ppermute | solution.py:20
  163.6 0.8 copy-start.7
  169.6 7.8 %collective-permute-start.15 = (f32[1024,64]{0,1:T(8,128)}, f32[1024,64]{0,1:T(8,128)}, u32[]{:S(2)}, u32[]{:S(2)}) collective-permute-start(f32[1024,64]{0,1:T(8,128)} %add.250), channel_id=1, source_target_pairs={{8,0},{12,4},{16,8},{20,12},{24,16},{28,20},{0,24},{4,28},{9,1},{1... | collective-permute-start | bytes 786440 | tf_op jit(solution)/shard_map/ppermute | solution.py:20
  170.9 13.5 %collective-permute-start.14 = (f32[1024,64]{0,1:T(8,128)S(1)}, f32[1024,64]{0,1:T(8,128)S(1)}, u32[]{:S(2)}, u32[]{:S(2)}) collective-permute-start(f32[1024,64]{0,1:T(8,128)S(1)} %add.248), channel_id=1, source_target_pairs={{28,0},{0,4},{4,8},{8,12},{12,16},{16,20},{20,24},{24,28},{29,1},{... | collective-permute-start | bytes 786440 | tf_op jit(solution)/shard_map/ppermute | solution.py:20
  188.2 1.3 collective-permute-start.16
  189.5 3.8 %collective-permute-start.17 = (f32[35,128]{1,0:T(8,128)S(1)}, f32[35,128]{1,0:T(8,128)S(1)}, u32[]{:S(2)}, u32[]{:S(2)}) collective-permute-start(f32[35,128]{1,0:T(8,128)S(1)} %pad_maximum_fusion.12), channel_id=1, source_target_pairs={{0,2},{1,3},{2,0},{3,1},{4,6},{5,7},{6,4},{7,5},{8,10},{9,11},{10,... | collective-permute-start | bytes 53768 | tf_op jit(solution)/shard_map/ppermute | solution.py:196
  193.4 3.8 %collective-permute-start.18 = (f32[37,128]{1,0:T(8,128)S(1)}, f32[37,128]{1,0:T(8,128)S(1)}, u32[]{:S(2)}, u32[]{:S(2)}) collective-permute-start(f32[37,128]{1,0:T(8,128)S(1)} %pad_maximum_fusion.13), channel_id=1, source_target_pairs={{0,4},{4,0},{8,12},{12,8},{16,20},{20,16},{24,28},{28,24},{1,5},{5... | collective-permute-start | bytes 56840 | tf_op jit(solution)/shard_map/ppermute | solution.py:196
  197.3 3.9 %collective-permute-start.19 = (f32[41,128]{1,0:T(8,128)S(1)}, f32[41,128]{1,0:T(8,128)S(1)}, u32[]{:S(2)}, u32[]{:S(2)}) collective-permute-start(f32[41,128]{1,0:T(8,128)S(1)} %pad_maximum_fusion.7), channel_id=1, source_target_pairs={{0,8},{4,12},{8,0},{12,4},{16,24},{20,28},{24,16},{28,20},{1,9},{5... | collective-permute-start | bytes 62984 | tf_op jit(solution)/shard_map/ppermute | solution.py:196
  201.2 5.0 %collective-permute-start.20 = (f32[49,128]{1,0:T(8,128)S(1)}, f32[49,128]{1,0:T(8,128)S(1)}, u32[]{:S(2)}, u32[]{:S(2)}) collective-permute-start(f32[49,128]{1,0:T(8,128)S(1)} %pad_maximum_fusion.5), channel_id=1, source_target_pairs={{0,16},{4,20},{8,24},{12,28},{16,0},{20,4},{24,8},{28,12},{1,17},{... | collective-permute-start | bytes 75272 | tf_op jit(solution)/shard_map/ppermute | solution.py:196

commit v20 on v17

--- a/solution.py
+++ b/solution.py
@@ -180,28 +180,14 @@
     return lax.cond(owned, compute_pair, skip_pair)
 
 
-def butterfly(axis, summed_rows, block):
+def butterfly(axis, block):
     size = lax.axis_size(axis)
     if size & (size - 1):
-        return jnp.concatenate(
-            [
-                lax.psum(block[:summed_rows], axis),
-                lax.all_gather(block[summed_rows:], axis, tiled=True),
-            ]
-        )
-    index = lax.axis_index(axis)
+        return lax.psum(block, axis)
     step = 1
     while step < size:
         route = [(i, i ^ step) for i in range(size)]
-        other = lax.ppermute(block, axis, route)
-        summed = block[:summed_rows] + other[:summed_rows]
-        mine = block[summed_rows:]
-        theirs = other[summed_rows:]
-        upper = (index // step) % 2 == 1
-        gathered = jnp.where(
-            upper, jnp.concatenate([theirs, mine]), jnp.concatenate([mine, theirs])
-        )
-        block = jnp.concatenate([summed, gathered])
+        block = block + lax.ppermute(block, axis, route)
         step *= 2
     return block
 
@@ -261,10 +247,18 @@
         ]
     )
     summed_rows = summed.shape[0]
-    block = jnp.concatenate([summed, as_rows(jnp.concatenate([centre, local_drift]))])
-    gather_width = block.shape[0] - summed_rows
+    own_rows = as_rows(jnp.concatenate([centre, local_drift]))
+    gather_width = own_rows.shape[0]
+    device_count = lax.axis_size("wide") * lax.axis_size("narrow")
+    device_index = lax.axis_index("wide") * lax.axis_size("narrow") + lax.axis_index("narrow")
+    slots = lax.dynamic_update_slice(
+        jnp.zeros((device_count * gather_width, own_rows.shape[1]), jnp.float32),
+        own_rows,
+        (device_index * gather_width, 0),
+    )
+    block = jnp.concatenate([summed, slots])
     for axis in ("narrow", "wide"):
-        block = butterfly(axis, summed_rows, block)
+        block = butterfly(axis, block)
     totals = block[:summed_rows].reshape(-1)
     gram_sum = totals[: vector_count * vector_count].reshape(vector_count, vector_count)
     column_sums = totals[vector_count * vector_count : vector_count * vector_count + vector_count]

time: 219 us -> 220 us (level)
  matrix products: 60.8 us -> 30.8 us
  starting transfers between devices: 23.6 us -> 49.3 us
  local copies, waits for them, and re-layouts: 12.5 us -> 17.7 us
    ppermute x11, starting transfers between devices: 20.2 us -> 42.2 us  [shifted(): return lax.ppermute(block, axis, route)]
    dot_general x6 -> x3, matrix products: 24 us -> 11.9 us  [scores_tile(): lax.dot_general(leftside_block, right_block, (((1,), (1,)), ((), ())), pr...]
    dot_general x10 -> x5, matrix products: 18 us -> 8.54 us  [row_product(): return jnp.dot(affinity, weights, preferred_element_type=jnp.float32)]
    dot_general x8 -> x3, matrix products: 12 us -> 3.61 us  [col_product(): lax.dot_general(affinity, weights, (((0,), (0,)), ((), ())), preferred_el...]
    another operation x0 -> x20, local copies, waits for them, and re-layouts: none -> 5.22 us
    ppermute x10, starting transfers between devices: 3.47 us -> 7.09 us  [butterfly(): block = block + lax.ppermute(block, axis, route)]
  transfers between devices with their start and end apart: 21 -> 21, of which waited for: 13 -> 14; matrix products, arithmetic and copies ran while one was open for 27% -> 18% of each run, Pallas kernels for 4% -> 4%
where the time goes in v20:
time: 220 us; the launch traced here: 219 us
  waiting for transfers between devices  77.3 us (35%)
  starting transfers between devices  49.3 us (22%)
  matrix products  30.8 us (14%)
  other arithmetic  23.7 us (11%)
  local copies, waits for them, and re-layouts  17.7 us (8%)
  Pallas kernels  16.9 us (8%)
  between operations  2.94 us (1%)
    ppermute x11, waiting for transfers between devices, shifted(): return lax.ppermute(block, axis, route)  50.8 us
    ppermute x11, starting transfers between devices, shifted(): return lax.ppermute(block, axis, route)  42.2 us
    ppermute x10, waiting for transfers between devices, butterfly(): block = block + lax.ppermute(block, axis, route)  26.6 us
    pallas_call x2, Pallas kernels, factor_inverse(): pl.pallas_call(factor_kernel, out_shape=jax.ShapeDtypeStruct(gram_matrix....  16.9 us
    dot_general x3, matrix products, scores_tile(): lax.dot_general(leftside_block, right_block, (((1,), (1,)), ((), ())), pr...  11.9 us
    dot_general x5, matrix products, row_product(): return jnp.dot(affinity, weights, preferred_element_type=jnp.float32)  8.54 us
    ppermute x10, starting transfers between devices, butterfly(): block = block + lax.ppermute(block, axis, route)  7.09 us
    dot_general x8, matrix products, hdot(): jnp.dot(left, right, precision=lax.Precision.HIGHEST, preferred_element_t...  6.78 us
  transfers between devices with their start and end apart: 21, of which 14 were waited for; matrix products, arithmetic and copies ran while one was open for 18% of the time, Pallas kernels for 4%

profile of v20, /device:TPU:0, one launch (start us, length us, event | category | flops | bytes accessed | tf_op | source)
XLA Modules:
  0.0 218.9 jit_solution(18110856570624384568)
XLA Ops:
  0.6 3.1 %collective-permute-start.2 = (bf16[1024,768]{1,0:T(8,128)(2,1)}, bf16[1024,768]{1,0:T(8,128)(2,1)}, u32[]{:S(2)}, u32[]{:S(2)}) collective-permute-start(bf16[1024,768]{1,0:T(8,128)(2,1)} %param.21), channel_id=1, source_target_pairs={{24,0},{28,4},{0,8},{4,12},{8,16},{12,20},{16,24},{20,28},{25,1},{... | collective-permute-start | bytes 4718600 | tf_op jit(solution)/shard_map/ppermute | solution.py:20
  3.7 1.8 fusion.1
  6.0 1.1 copy-done.3
  7.1 1.1 fusion.47
  8.2 3.3 %collective-permute-start.3 = (bf16[512,768]{1,0:T(8,128)(2,1)S(1)}, bf16[512,768]{1,0:T(8,128)(2,1)}, u32[]{:S(2)}, u32[]{:S(2)}) collective-permute-start(bf16[512,768]{1,0:T(8,128)(2,1)S(1)} %get-tuple-element.255), channel_id=1, source_target_pairs={{4,0},{8,4},{12,8},{16,12},{20,16},{24,20},{28,24},{0,28},{5,1},{9... | collective-permute-start | bytes 2359304 | tf_op jit(solution)/shard_map/ppermute | solution.py:20
  12.7 5.0 %collective-permute-start = (bf16[512,768]{1,0:T(8,128)(2,1)}, bf16[512,768]{1,0:T(8,128)(2,1)}, u32[]{:S(2)}, u32[]{:S(2)}) collective-permute-start(bf16[512,768]{1,0:T(8,128)(2,1)} %get-tuple-element.256), channel_id=1, source_target_pairs={{4,0},{8,4},{12,8},{16,12},{20,16},{24,20},{28,24},{0,28},{5,1},{9... | collective-permute-start | bytes 2359304 | tf_op jit(solution)/shard_map/ppermute | solution.py:20
  17.7 4.4 %convert_reduce_fusion.10 = (f32[1024]{0:T(1024)}, bf16[1024,1024]{0,1:T(8,128)(2,1)S(1)}) fusion(bf16[1024,768]{1,0:T(8,128)(2,1)} %copy-done.3), kind=kOutput, calls=%fused_computation.15 | convolution fusion | flops 1616903168 | bytes 3674112 | tf_op jit(solution)/shard_map/dot_general | solution.py:55
  22.1 1.0 compare_reduce_fusion
  24.8 36.5 %collective-permute-done.1 = bf16[1024,64]{1,0:T(8,128)(2,1)} collective-permute-done((bf16[1024,64]{1,0:T(8,128)(2,1)}, bf16[1024,64]{1,0:T(8,128)(2,1)}, u32[]{:S(2)}, u32[]{:S(2)}) %collective-permute-start.1) | collective-permute-done | bytes 131104 | tf_op jit(solution)/shard_map/ppermute | solution.py:20
  61.3 0.9 slice.119
  62.3 2.5 %conditional.10 = (bf16[1024,512]{1,0:T(8,128)(2,1)}, f32[1024,64]{0,1:T(8,128)}, f32[1024]{0:T(1024)S(1)}, f32[512,64]{0,1:T(8,128)}, f32[512]{0:T(512)S(1)}) conditional(s32[]{:T(128)} %convert_element_type.80, () %tuple.85, (bf16[1024,768]{1,0:T(8,128)(2,1)}, bf16[512,768]{1,0:T(8,128)(2,1)}, bf16[512,64]{1,0:T(8,128)(2,1)S(1)}, ...), branch_computations={%region_8.9_spmd, %region_9.12_spmd} | conditional | flops 942144000 | bytes 6101032 | solution.py:166
  62.3 1.1 broadcast.140
  64.7 1.9 fusion.4
  66.7 3.0 %fusion.6 = bf16[1024,768]{1,0:T(8,128)(2,1)} fusion(bf16[1024,768]{1,0:T(8,128)(2,1)} %collective-permute-done.2, f32[1024]{0:T(1024)S(1)} %add_rsqrt_fusion), kind=kLoop, calls=%fused_computation.29 | loop fusion | flops 3145728 | bytes 3149824 | tf_op jit(solution)/shard_map/convert_element_type | solution.py:51
  69.7 1.6 conditional.9
  69.7 1.6 broadcast.136
  72.0 6.9 %conditional.11 = (bf16[1024,512]{1,0:T(8,128)(2,1)}, f32[1024,64]{0,1:T(8,128)S(1)}, f32[1024]{0:T(1024)S(1)}, f32[512,64]{0,1:T(8,128)S(1)}, f32[512]{0:T(512)S(1)}) conditional(s32[]{:T(128)} %convert_element_type.81, () %tuple.87, (bf16[1024,768]{1,0:T(8,128)(2,1)}, bf16[512,768]{1,0:T(8,128)(2,1)}, bf16[512,64]{1,0:T(8,128)(2,1)S(1)}, ...), branch_computations={%region_13.14_spmd, %region_14.17_spmd} | conditional | flops 942144000 | bytes 6101032 | solution.py:166
  72.0 3.7 %convert_reduce_fusion.4 = (f32[512]{0:T(512)S(1)}, f32[1024]{0:T(1024)S(1)}, bf16[1024,512]{1,0:T(8,128)(2,1)}) fusion(bf16[1024,768]{1,0:T(8,128)(2,1)} %get-tuple-element.72, bf16[512,768]{1,0:T(8,128)(2,1)} %get-tuple-element.73), kind=kOutput, calls=%fused_computation.6 | convolution fusion | flops 807926272 | bytes 3414016 | tf_op jit(solution)/shard_map/cond/branch_1_fun/dot_general | solution.py:55
  75.7 1.7 fusion.59
  77.4 1.6 fusion.60
  78.9 3.7 %collective-permute-done = bf16[512,768]{1,0:T(8,128)(2,1)} collective-permute-done((bf16[512,768]{1,0:T(8,128)(2,1)}, bf16[512,768]{1,0:T(8,128)(2,1)}, u32[]{:S(2)}, u32[]{:S(2)}) %collective-permute-start) | collective-permute-done | bytes 786464 | tf_op jit(solution)/shard_map/ppermute | solution.py:20
  82.7 0.9 slice.95
  83.6 7.0 %conditional.14 = (bf16[1024,512]{1,0:T(8,128)(2,1)}, f32[1024,64]{0,1:T(8,128)S(1)}, f32[1024]{0:T(1024)S(1)}, f32[512,64]{0,1:T(8,128)S(1)}, f32[4,128]{1,0:T(4,128)S(1)}) conditional(s32[]{:T(128)} %convert_element_type.81, () %tuple.94, (bf16[1024,768]{1,0:T(8,128)(2,1)}, bf16[512,768]{1,0:T(8,128)(2,1)}, bf16[512,64]{1,0:T(8,128)(2,1)S(1)}, ...), branch_computations={%region_23.24_spmd, %region_24.0_spmd} | conditional | flops 942144000 | bytes 6101032 | solution.py:166
  83.6 3.8 %convert_reduce_fusion.8 = (f32[512]{0:T(512)S(1)}, f32[1024]{0:T(1024)S(1)}, bf16[1024,512]{1,0:T(8,128)(2,1)}) fusion(bf16[1024,768]{1,0:T(8,128)(2,1)} %get-tuple-element.82, bf16[512,768]{1,0:T(8,128)(2,1)} %get-tuple-element.83), kind=kOutput, calls=%fused_computation.12 | convolution fusion | flops 807926272 | bytes 3414016 | tf_op jit(solution)/shard_map/cond/branch_1_fun/dot_general | solution.py:55
  87.4 1.7 fusion.63
  89.1 1.6 fusion.64
  91.3 1.0 add_add_fusion
  93.4 11.4 %collective-permute-start.6 = (f32[520,128]{1,0:T(8,128)}, f32[520,128]{1,0:T(8,128)}, u32[]{:S(2)}, u32[]{:S(2)}) collective-permute-start(f32[520,128]{1,0:T(8,128)} %pad_maximum_fusion.3), channel_id=1, source_target_pairs={{8,0},{12,4},{16,8},{20,12},{24,16},{28,20},{0,24},{4,28},{9,1},{1... | collective-permute-start | bytes 798728 | tf_op jit(solution)/shard_map/ppermute | solution.py:20
  104.8 1.1 conditional.12
  104.8 1.0 broadcast.152
  106.4 0.9 maximum_add_fusion
  109.1 7.7 %collective-permute-start.5 = (f32[520,128]{1,0:T(8,128)}, f32[520,128]{1,0:T(8,128)}, u32[]{:S(2)}, u32[]{:S(2)}) collective-permute-start(f32[520,128]{1,0:T(8,128)} %pad_maximum_fusion.2), channel_id=1, source_target_pairs={{28,0},{0,4},{4,8},{8,12},{12,16},{16,20},{20,24},{24,28},{29,1},{... | collective-permute-start | bytes 798728 | tf_op jit(solution)/shard_map/ppermute | solution.py:20
  117.4 1.0 slice.121
  118.7 2.5 %collective-permute-done.5 = f32[520,128]{1,0:T(8,128)} collective-permute-done((f32[520,128]{1,0:T(8,128)}, f32[520,128]{1,0:T(8,128)}, u32[]{:S(2)}, u32[]{:S(2)}) %collective-permute-start.5) | collective-permute-done | bytes 266272 | tf_op jit(solution)/shard_map/ppermute | solution.py:20
  121.2 1.0 slice.120
  122.5 1.1 fusion.45
  123.7 1.3 broadcast_multiply_fusion
  127.4 1.2 collective-permute-done.9
  128.7 3.9 %collective-permute-done.10 = f32[65,128]{1,0:T(8,128)S(1)} collective-permute-done((f32[65,128]{1,0:T(8,128)S(1)}, f32[65,128]{1,0:T(8,128)S(1)}, u32[]{:S(2)}, u32[]{:S(2)}) %collective-permute-start.10) | collective-permute-done | bytes 33312 | tf_op jit(solution)/shard_map/ppermute | solution.py:190
  132.7 2.4 %collective-permute-start.11 = (f32[65,128]{1,0:T(8,128)S(1)}, f32[65,128]{1,0:T(8,128)S(1)}, u32[]{:S(2)}, u32[]{:S(2)}) collective-permute-start(f32[65,128]{1,0:T(8,128)S(1)} %add.219), channel_id=1, source_target_pairs={{0,4},{4,0},{8,12},{12,8},{16,20},{20,16},{24,28},{28,24},{1,5},{5... | collective-permute-start | bytes 99848 | tf_op jit(solution)/shard_map/ppermute | solution.py:190
  135.1 1.9 collective-permute-done.11
  137.0 1.5 collective-permute-start.12
  138.5 2.5 %collective-permute-done.12 = f32[65,128]{1,0:T(8,128)S(1)} collective-permute-done((f32[65,128]{1,0:T(8,128)S(1)}, f32[65,128]{1,0:T(8,128)S(1)}, u32[]{:S(2)}, u32[]{:S(2)}) %collective-permute-start.12) | collective-permute-done | bytes 33312 | tf_op jit(solution)/shard_map/ppermute | solution.py:190
  141.0 1.6 collective-permute-start.13
  142.6 4.1 %pad_maximum_fusion = (bf16[1024,1024]{1,0:T(8,128)(2,1)S(1)}, bf16[1024,1024]{1,0:T(8,128)(2,1)}) fusion(bf16[1024,512]{1,0:T(8,128)(2,1)} %get-tuple-element.180, bf16[1024,512]{1,0:T(8,128)(2,1)} %get-tuple-element.179, bf16[1024,512]{1,0:T(8,128)(2,1)} %get-tuple-element.185, bf16[1024,512]{1,0:T(8,128)(2,1)} %get-tuple-element.184), kind=kLoop, calls=%fused_computation.30 | loop fusion | flops 8388608 | bytes 8388608 | tf_op jit(solution)/shard_map/concatenate | solution.py:373
  146.7 1.7 collective-permute-start.8
  148.4 3.5 %collective-permute-start.7 = (f32[1024,64]{0,1:T(8,128)S(1)}, f32[1024,64]{0,1:T(8,128)S(1)}, u32[]{:S(2)}, u32[]{:S(2)}) collective-permute-start(f32[1024,64]{0,1:T(8,128)S(1)} %get-tuple-element.249), channel_id=1, source_target_pairs={{4,0},{8,4},{12,8},{16,12},{20,16},{24,20},{28,24},{0,28},{5,1},{9... | collective-permute-start | bytes 786440 | tf_op jit(solution)/shard_map/ppermute | solution.py:20
  154.5 8.4 %shard_map.50 = f32[64,64]{1,0:T(8,128)} custom-call(f32[64,64]{1,0:T(8,128)} %fusion.26.gram_ref), custom_call_target="tpu_custom_call" | custom-call | tf_op jit(solution)/shard_map/pallas_call | solution.py:230
  163.0 1.7 convolution_convert_fusion
  165.5 3.0 %conditional.17 = (f32[1024,64]{0,1:T(8,128)S(1)}, f32[1024,64]{0,1:T(8,128)S(1)}) conditional(s32[]{:T(128)} %convert_element_type.81, () %tuple.100, (bf16[1024,1024]{1,0:T(8,128)(2,1)}, bf16[1024,64]{0,1:T(8,128)(2,1)S(1)}, bf16[1024,64]{0,1:T(8,128)(2,1)S(1)}) %tuple.101), branch_computations={%region_36.37_spmd, %region_37.38_spmd} | conditional | flops 268435456 | bytes 13369388 | solution.py:180
  165.5 2.5 %fusion.54 = f32[1024,64]{0,1:T(8,128)S(1)} fusion(bf16[1024,1024]{1,0:T(8,128)(2,1)} %get-tuple-element.92, bf16[1024,64]{0,1:T(8,128)(2,1)S(1)} %get-tuple-element.227), kind=kOutput, calls=%fused_computation.119 | convolution fusion | flops 134217728 | bytes 2490368 | tf_op jit(solution)/shard_map/cond/branch_1_fun/dot_general | solution.py:62
  169.4 6.2 %collective-permute-start.14 = (f32[1024,64]{0,1:T(8,128)S(1)}, f32[1024,64]{0,1:T(8,128)S(1)}, u32[]{:S(2)}, u32[]{:S(2)}) collective-permute-start(f32[1024,64]{0,1:T(8,128)S(1)} %add.228), channel_id=1, source_target_pairs={{28,0},{0,4},{4,8},{8,12},{12,16},{16,20},{20,24},{24,28},{29,1},{... | collective-permute-start | bytes 786440 | tf_op jit(solution)/shard_map/ppermute | solution.py:20
  175.5 1.0 collective-permute-done.15
  176.5 7.1 %collective-permute-done.14 = f32[1024,64]{0,1:T(8,128)S(1)} collective-permute-done((f32[1024,64]{0,1:T(8,128)S(1)}, f32[1024,64]{0,1:T(8,128)S(1)}, u32[]{:S(2)}, u32[]{:S(2)}) %collective-permute-start.14) | collective-permute-done | bytes 262176 | tf_op jit(solution)/shard_map/ppermute | solution.py:20
  183.6 2.2 %fusion.42 = (f32[64]{0:T(128)S(1)}, f32[1024,64]{0,1:T(8,128)S(1)}) fusion(f32[1024]{0:T(1024)S(1)} %get-tuple-element.245, f32[1024,64]{0,1:T(8,128)} %collective-permute-done.15, f32[1024,64]{0,1:T(8,128)S(1)} %collective-permute-done.14, f32[1024,64]{0,1:T(8,128)S(1)} %get-tuple-element.181, f32[1024,64]{0,1:T(8,128)S(1)} %get-tuple-element.182, ...), kind=kOutput, calls=%fused_computation.108 | convolution fusion | flops 134610880 | bytes 3543296 | tf_op jit(solution)/shard_map/dot_general | solution.py:62
  187.5 1.2 collective-permute-done.16
  188.8 3.9 %collective-permute-done.17 = f32[65,128]{1,0:T(8,128)S(1)} collective-permute-done((f32[65,128]{1,0:T(8,128)S(1)}, f32[65,128]{1,0:T(8,128)S(1)}, u32[]{:S(2)}, u32[]{:S(2)}) %collective-permute-start.17) | collective-permute-done | bytes 33312 | tf_op jit(solution)/shard_map/ppermute | solution.py:190
  192.8 3.9 %collective-permute-done.18 = f32[65,128]{1,0:T(8,128)S(1)} collective-permute-done((f32[65,128]{1,0:T(8,128)S(1)}, f32[65,128]{1,0:T(8,128)S(1)}, u32[]{:S(2)}, u32[]{:S(2)}) %collective-permute-start.18) | collective-permute-done | bytes 33312 | tf_op jit(solution)/shard_map/ppermute | solution.py:190
  197.1 3.6 %collective-permute-done.19 = f32[65,128]{1,0:T(8,128)S(1)} collective-permute-done((f32[65,128]{1,0:T(8,128)S(1)}, f32[65,128]{1,0:T(8,128)S(1)}, u32[]{:S(2)}, u32[]{:S(2)}) %collective-permute-start.19) | collective-permute-done | bytes 33312 | tf_op jit(solution)/shard_map/ppermute | solution.py:190
  200.7 1.0 collective-permute-start.20
  201.7 4.2 %collective-permute-done.20 = f32[65,128]{1,0:T(8,128)S(1)} collective-permute-done((f32[65,128]{1,0:T(8,128)S(1)}, f32[65,128]{1,0:T(8,128)S(1)}, u32[]{:S(2)}, u32[]{:S(2)}) %collective-permute-start.20) | collective-permute-done | bytes 33312 | tf_op jit(solution)/shard_map/ppermute | solution.py:190
  207.6 0.9 fusion.24.gram_ref
  208.5 8.4 %shard_map.51 = f32[64,64]{1,0:T(8,128)} custom-call(f32[64,64]{1,0:T(8,128)} %fusion.24.gram_ref), custom_call_target="tpu_custom_call" | custom-call | tf_op jit(solution)/shard_map/pallas_call | solution.py:230
  217.0 1.9 fusion.14
  (136 shorter events, 19.9 us)
Async XLA Ops:
  0.6 4.9 %copy-start.2 = (bf16[1024,768]{1,0:T(8,128)(2,1)S(1)}, bf16[1024,768]{1,0:T(8,128)(2,1)}, u32[]{:S(2)}) copy-start(bf16[1024,768]{1,0:T(8,128)(2,1)} %param.21) | copy-start | bytes 4718596
  0.6 64.1 %collective-permute-start.2 = (bf16[1024,768]{1,0:T(8,128)(2,1)}, bf16[1024,768]{1,0:T(8,128)(2,1)}, u32[]{:S(2)}, u32[]{:S(2)}) collective-permute-start(bf16[1024,768]{1,0:T(8,128)(2,1)} %param.21), channel_id=1, source_target_pairs={{24,0},{28,4},{0,8},{4,12},{8,16},{12,20},{16,24},{20,28},{25,1},{... | collective-permute-start | bytes 4718600 | tf_op jit(solution)/shard_map/ppermute | solution.py:20
  6.0 1.2 copy-start.3
  7.1 4.4 %copy-start.5 = (bf16[1024,64]{0,1:T(8,128)(2,1)S(1)}, bf16[1024,64]{0,1:T(8,128)(2,1)}, u32[]{:S(2)}) copy-start(bf16[1024,64]{0,1:T(8,128)(2,1)} %param.22) | copy-start | bytes 393220
  8.2 54.0 %collective-permute-start.3 = (bf16[512,768]{1,0:T(8,128)(2,1)S(1)}, bf16[512,768]{1,0:T(8,128)(2,1)}, u32[]{:S(2)}, u32[]{:S(2)}) collective-permute-start(bf16[512,768]{1,0:T(8,128)(2,1)S(1)} %get-tuple-element.255), channel_id=1, source_target_pairs={{4,0},{8,4},{12,8},{16,12},{20,16},{24,20},{28,24},{0,28},{5,1},{9... | collective-permute-start | bytes 2359304 | tf_op jit(solution)/shard_map/ppermute | solution.py:20
  12.4 49.0 %collective-permute-start.1 = (bf16[1024,64]{1,0:T(8,128)(2,1)}, bf16[1024,64]{1,0:T(8,128)(2,1)}, u32[]{:S(2)}, u32[]{:S(2)}) collective-permute-start(bf16[1024,64]{1,0:T(8,128)(2,1)} %copy.18), channel_id=1, source_target_pairs={{4,0},{8,4},{12,8},{16,12},{20,16},{24,20},{28,24},{0,28},{5,1},{9... | collective-permute-start | bytes 393224 | tf_op jit(solution)/shard_map/ppermute | solution.py:20
  12.7 58.7 %collective-permute-start.4 = (bf16[1024,64]{1,0:T(8,128)(2,1)}, bf16[1024,64]{1,0:T(8,128)(2,1)S(1)}, u32[]{:S(2)}, u32[]{:S(2)}) collective-permute-start(bf16[1024,64]{1,0:T(8,128)(2,1)} %copy.18), channel_id=1, source_target_pairs={{24,0},{28,4},{0,8},{4,12},{8,16},{12,20},{16,24},{20,28},{25,1},{... | collective-permute-start | bytes 393224 | tf_op jit(solution)/shard_map/ppermute | solution.py:20
  12.7 9.4 %copy-start.15 = (s32[32,3]{0,1:T(4,128)S(1)}, s32[32,3]{0,1:T(4,128)}, u32[]{:S(2)}) copy-start(s32[32,3]{0,1:T(4,128)} %param.23) | copy-start | bytes 1156
  12.7 70.0 %collective-permute-start = (bf16[512,768]{1,0:T(8,128)(2,1)}, bf16[512,768]{1,0:T(8,128)(2,1)}, u32[]{:S(2)}, u32[]{:S(2)}) collective-permute-start(bf16[512,768]{1,0:T(8,128)(2,1)} %get-tuple-element.256), channel_id=1, source_target_pairs={{4,0},{8,4},{12,8},{16,12},{20,16},{24,20},{28,24},{0,28},{5,1},{9... | collective-permute-start | bytes 2359304 | tf_op jit(solution)/shard_map/ppermute | solution.py:20
  22.1 94.8 %copy-start.1 = (bf16[1024,1024]{0,1:T(8,128)(2,1)}, bf16[1024,1024]{0,1:T(8,128)(2,1)S(1)}, u32[]{:S(2)}) copy-start(bf16[1024,1024]{0,1:T(8,128)(2,1)S(1)} %get-tuple-element.261) | copy-start | bytes 6291460
  64.7 4.9 %copy-start.4 = (bf16[1024,768]{1,0:T(8,128)(2,1)S(1)}, bf16[1024,768]{1,0:T(8,128)(2,1)}, u32[]{:S(2)}) copy-start(bf16[1024,768]{1,0:T(8,128)(2,1)} %copy-done.3) | copy-start | bytes 4718596
  71.3 0.7 copy-start.6
  78.9 4.7 %copy-start.8 = (f32[512,64]{0,1:T(8,128)}, f32[512,64]{0,1:T(8,128)S(1)}, u32[]{:S(2)}) copy-start(f32[512,64]{0,1:T(8,128)S(1)} %get-tuple-element.164) | copy-start | bytes 393220
  78.9 4.7 %copy-start.12 = (f32[512]{0:T(512)}, f32[512]{0:T(512)S(1)}, u32[]{:S(2)}) copy-start(f32[512]{0:T(512)S(1)} %get-tuple-element.168) | copy-start | bytes 6148
  90.7 0.7 copy-start.10
  90.7 14.1 %copy-start.13 = (f32[4,128]{1,0:T(4,128)}, f32[4,128]{1,0:T(4,128)S(1)}, u32[]{:S(2)}) copy-start(f32[4,128]{1,0:T(4,128)S(1)} %get-tuple-element.169) | copy-start | bytes 6148
  93.4 13.0 %copy-start.9 = (f32[512,64]{0,1:T(8,128)S(1)}, f32[512,64]{0,1:T(8,128)}, u32[]{:S(2)}) copy-start(f32[512,64]{0,1:T(8,128)} %copy-done.8) | copy-start | bytes 393220
  93.4 13.0 %copy-start.11 = (f32[512,64]{0,1:T(8,128)S(1)}, f32[512,64]{0,1:T(8,128)}, u32[]{:S(2)}) copy-start(f32[512,64]{0,1:T(8,128)} %copy-done.10) | copy-start | bytes 393220
  93.4 24.0 %collective-permute-start.6 = (f32[520,128]{1,0:T(8,128)}, f32[520,128]{1,0:T(8,128)}, u32[]{:S(2)}, u32[]{:S(2)}) collective-permute-start(f32[520,128]{1,0:T(8,128)} %pad_maximum_fusion.3), channel_id=1, source_target_pairs={{8,0},{12,4},{16,8},{20,12},{24,16},{28,20},{0,24},{4,28},{9,1},{1... | collective-permute-start | bytes 798728 | tf_op jit(solution)/shard_map/ppermute | solution.py:20
  105.9 0.5 copy-start.14
  109.1 12.1 %collective-permute-start.5 = (f32[520,128]{1,0:T(8,128)}, f32[520,128]{1,0:T(8,128)}, u32[]{:S(2)}, u32[]{:S(2)}) collective-permute-start(f32[520,128]{1,0:T(8,128)} %pad_maximum_fusion.2), channel_id=1, source_target_pairs={{28,0},{0,4},{4,8},{8,12},{12,16},{16,20},{20,24},{24,28},{29,1},{... | collective-permute-start | bytes 798728 | tf_op jit(solution)/shard_map/ppermute | solution.py:20
  118.7 4.9 %copy-start.16 = (f32[1024]{0:T(1024)S(1)}, f32[1024]{0:T(1024)}, u32[]{:S(2)}) copy-start(f32[1024]{0:T(1024)} %get-tuple-element.260) | copy-start | bytes 12292
  127.4 1.3 collective-permute-start.9
  128.7 4.0 %collective-permute-start.10 = (f32[65,128]{1,0:T(8,128)S(1)}, f32[65,128]{1,0:T(8,128)S(1)}, u32[]{:S(2)}, u32[]{:S(2)}) collective-permute-start(f32[65,128]{1,0:T(8,128)S(1)} %fusion.40), channel_id=1, source_target_pairs={{0,2},{1,3},{2,0},{3,1},{4,6},{5,7},{6,4},{7,5},{8,10},{9,11},{10,... | collective-permute-start | bytes 99848 | tf_op jit(solution)/shard_map/ppermute | solution.py:190
  132.7 4.3 %collective-permute-start.11 = (f32[65,128]{1,0:T(8,128)S(1)}, f32[65,128]{1,0:T(8,128)S(1)}, u32[]{:S(2)}, u32[]{:S(2)}) collective-permute-start(f32[65,128]{1,0:T(8,128)S(1)} %add.219), channel_id=1, source_target_pairs={{0,4},{4,0},{8,12},{12,8},{16,20},{20,16},{24,28},{28,24},{1,5},{5... | collective-permute-start | bytes 99848 | tf_op jit(solution)/shard_map/ppermute | solution.py:190
  137.0 4.0 %collective-permute-start.12 = (f32[65,128]{1,0:T(8,128)S(1)}, f32[65,128]{1,0:T(8,128)S(1)}, u32[]{:S(2)}, u32[]{:S(2)}) collective-permute-start(f32[65,128]{1,0:T(8,128)S(1)} %add.220), channel_id=1, source_target_pairs={{0,8},{4,12},{8,0},{12,4},{16,24},{20,28},{24,16},{28,20},{1,9},{5... | collective-permute-start | bytes 99848 | tf_op jit(solution)/shard_map/ppermute | solution.py:190
  141.0 11.0 %collective-permute-start.13 = (f32[65,128]{1,0:T(8,128)S(1)}, f32[65,128]{1,0:T(8,128)S(1)}, u32[]{:S(2)}, u32[]{:S(2)}) collective-permute-start(f32[65,128]{1,0:T(8,128)S(1)} %add.221), channel_id=1, source_target_pairs={{0,16},{4,20},{8,24},{12,28},{16,0},{20,4},{24,8},{28,12},{1,17},{... | collective-permute-start | bytes 99848 | tf_op jit(solution)/shard_map/ppermute | solution.py:190
  146.7 16.3 %collective-permute-start.8 = (f32[1024,64]{0,1:T(8,128)S(1)}, f32[1024,64]{0,1:T(8,128)S(1)}, u32[]{:S(2)}, u32[]{:S(2)}) collective-permute-start(f32[1024,64]{0,1:T(8,128)S(1)} %get-tuple-element.249), channel_id=1, source_target_pairs={{24,0},{28,4},{0,8},{4,12},{8,16},{12,20},{16,24},{20,28},{25,1},{... | collective-permute-start | bytes 786440 | tf_op jit(solution)/shard_map/ppermute | solution.py:20
  148.4 14.5 %collective-permute-start.7 = (f32[1024,64]{0,1:T(8,128)S(1)}, f32[1024,64]{0,1:T(8,128)S(1)}, u32[]{:S(2)}, u32[]{:S(2)}) collective-permute-start(f32[1024,64]{0,1:T(8,128)S(1)} %get-tuple-element.249), channel_id=1, source_target_pairs={{4,0},{8,4},{12,8},{16,12},{20,16},{24,20},{28,24},{0,28},{5,1},{9... | collective-permute-start | bytes 786440 | tf_op jit(solution)/shard_map/ppermute | solution.py:20
  164.7 0.8 copy-start.7
  165.5 2.5 %copy-start = (bf16[1024,1024]{1,0:T(8,128)(2,1)S(1)}, bf16[1024,1024]{1,0:T(8,128)(2,1)}, u32[]{:S(2)}) copy-start(bf16[1024,1024]{1,0:T(8,128)(2,1)} %get-tuple-element.92) | copy-start | bytes 6291460 | tf_op jit(solution)/shard_map/cond
  169.3 7.2 %collective-permute-start.15 = (f32[1024,64]{0,1:T(8,128)}, f32[1024,64]{0,1:T(8,128)}, u32[]{:S(2)}, u32[]{:S(2)}) collective-permute-start(f32[1024,64]{0,1:T(8,128)} %add.230), channel_id=1, source_target_pairs={{8,0},{12,4},{16,8},{20,12},{24,16},{28,20},{0,24},{4,28},{9,1},{1... | collective-permute-start | bytes 786440 | tf_op jit(solution)/shard_map/ppermute | solution.py:20
  169.4 14.2 %collective-permute-start.14 = (f32[1024,64]{0,1:T(8,128)S(1)}, f32[1024,64]{0,1:T(8,128)S(1)}, u32[]{:S(2)}, u32[]{:S(2)}) collective-permute-start(f32[1024,64]{0,1:T(8,128)S(1)} %add.228), channel_id=1, source_target_pairs={{28,0},{0,4},{4,8},{8,12},{12,16},{16,20},{20,24},{24,28},{29,1},{... | collective-permute-start | bytes 786440 | tf_op jit(solution)/shard_map/ppermute | solution.py:20
  187.5 1.3 collective-permute-start.16
  188.8 4.0 %collective-permute-start.17 = (f32[65,128]{1,0:T(8,128)S(1)}, f32[65,128]{1,0:T(8,128)S(1)}, u32[]{:S(2)}, u32[]{:S(2)}) collective-permute-start(f32[65,128]{1,0:T(8,128)S(1)} %fusion.39), channel_id=1, source_target_pairs={{0,2},{1,3},{2,0},{3,1},{4,6},{5,7},{6,4},{7,5},{8,10},{9,11},{10,... | collective-permute-start | bytes 99848 | tf_op jit(solution)/shard_map/ppermute | solution.py:190
  192.8 4.0 %collective-permute-start.18 = (f32[65,128]{1,0:T(8,128)S(1)}, f32[65,128]{1,0:T(8,128)S(1)}, u32[]{:S(2)}, u32[]{:S(2)}) collective-permute-start(f32[65,128]{1,0:T(8,128)S(1)} %add.233), channel_id=1, source_target_pairs={{0,4},{4,0},{8,12},{12,8},{16,20},{20,16},{24,28},{28,24},{1,5},{5... | collective-permute-start | bytes 99848 | tf_op jit(solution)/shard_map/ppermute | solution.py:190
  196.8 4.0 %collective-permute-start.19 = (f32[65,128]{1,0:T(8,128)S(1)}, f32[65,128]{1,0:T(8,128)S(1)}, u32[]{:S(2)}, u32[]{:S(2)}) collective-permute-start(f32[65,128]{1,0:T(8,128)S(1)} %add.234), channel_id=1, source_target_pairs={{0,8},{4,12},{8,0},{12,4},{16,24},{20,28},{24,16},{28,20},{1,9},{5... | collective-permute-start | bytes 99848 | tf_op jit(solution)/shard_map/ppermute | solution.py:190
  200.7 5.3 %collective-permute-start.20 = (f32[65,128]{1,0:T(8,128)S(1)}, f32[65,128]{1,0:T(8,128)S(1)}, u32[]{:S(2)}, u32[]{:S(2)}) collective-permute-start(f32[65,128]{1,0:T(8,128)S(1)} %add.235), channel_id=1, source_target_pairs={{0,16},{4,20},{8,24},{12,28},{16,0},{20,4},{24,8},{28,12},{1,17},{... | collective-permute-start | bytes 99848 | tf_op jit(solution)/shard_map/ppermute | solution.py:190

commit v21 on v17

--- a/solution.py
+++ b/solution.py
@@ -167,10 +167,18 @@
 
 
 def later_pass(owned, affinity, left_weights, right_weights):
-    block_rows = affinity.shape[0]
+    block_rows = left_weights.shape[0]
     vector_count = left_weights.shape[1]
 
     def compute_pair():
+        if isinstance(affinity, list):
+            width = affinity[0].shape[1]
+            row_part = sum(
+                row_product(piece, right_weights[h * width : (h + 1) * width])
+                for h, piece in enumerate(affinity)
+            )
+            col_part = jnp.concatenate([col_product(piece, left_weights) for piece in affinity])
+            return (row_part, col_part)
         return (row_product(affinity, right_weights), col_product(affinity, left_weights))
 
     def skip_pair():
@@ -376,7 +384,7 @@
         chunk_results[(i, 1)] = run_chunk(i, 1)
         left, right = pair_plan[i]
         first, second = chunk_results[(i, 0)], chunk_results[(i, 1)]
-        tiles[i] = jnp.concatenate([first[0], second[0]], axis=1)
+        tiles[i] = [first[0], second[0]]
         parts[left] = parts[left] + first[1] + second[1]
         sums[left] = sums[left] + first[2] + second[2]
         parts[right] = parts[right] + jnp.concatenate([first[3], second[3]])

time: 219 us -> 226 us (1.032)
  starting transfers between devices: 23.6 us -> 41 us
  matrix products: 60.8 us -> 47.9 us
  other arithmetic: 23.9 us -> 18.7 us
  local copies, waits for them, and re-layouts: 12.5 us -> 17.1 us
    ppermute x10, starting transfers between devices: 3.47 us -> 12.3 us  [butterfly(): other = lax.ppermute(block, axis, route)]
    ppermute x11, starting transfers between devices: 20.2 us -> 28.7 us  [shifted(): return lax.ppermute(block, axis, route)]
    dot_general x6 -> x4, matrix products: 24 us -> 16.5 us  [scores_tile(): lax.dot_general(leftside_block, right_block, (((1,), (1,)), ((), ())), pr...]
    dot_general x10 -> x8, matrix products: 18 us -> 13.5 us  [row_product(): return jnp.dot(affinity, weights, preferred_element_type=jnp.float32)]
    concatenate x1, other arithmetic: 4.08 us -> 0.02 us  [compute_pair(): jnp.concatenate([col_product(piece, left_weights) for piece in affinity])]
    another operation x0 -> x12, local copies, waits for them, and re-layouts: none -> 3.8 us
    dot_general x8 -> x6, matrix products: 12 us -> 11 us  [col_product(): lax.dot_general(affinity, weights, (((0,), (0,)), ((), ())), preferred_el...]
    unnamed x33 -> x39, local copies, waits for them, and re-layouts: 4.62 us -> 4.92 us
  transfers between devices with their start and end apart: 21 -> 21, of which waited for: 13 -> 14; matrix products, arithmetic and copies ran while one was open for 27% -> 19% of each run, Pallas kernels for 4% -> 4%
where the time goes in v21:
time: 226 us; the launch traced here: 224 us
  waiting for transfers between devices  79.2 us (35%)
  matrix products  47.9 us (21%)
  starting transfers between devices  41 us (18%)
  other arithmetic  18.7 us (8%)
  local copies, waits for them, and re-layouts  17.1 us (8%)
  Pallas kernels  16.9 us (7%)
  between operations  3.31 us (1%)
    ppermute x11, waiting for transfers between devices, shifted(): return lax.ppermute(block, axis, route)  51.9 us
    ppermute x11, starting transfers between devices, shifted(): return lax.ppermute(block, axis, route)  28.7 us
    ppermute x10, waiting for transfers between devices, butterfly(): other = lax.ppermute(block, axis, route)  27.3 us
    pallas_call x2, Pallas kernels, factor_inverse(): pl.pallas_call(factor_kernel, out_shape=jax.ShapeDtypeStruct(gram_matrix....  16.9 us
    dot_general x4, matrix products, scores_tile(): lax.dot_general(leftside_block, right_block, (((1,), (1,)), ((), ())), pr...  16.5 us
    dot_general x8, matrix products, row_product(): return jnp.dot(affinity, weights, preferred_element_type=jnp.float32)  13.5 us
    ppermute x10, starting transfers between devices, butterfly(): other = lax.ppermute(block, axis, route)  12.3 us
    dot_general x6, matrix products, col_product(): lax.dot_general(affinity, weights, (((0,), (0,)), ((), ())), preferred_el...  11 us
  transfers between devices with their start and end apart: 21, of which 14 were waited for; matrix products, arithmetic and copies ran while one was open for 19% of the time, Pallas kernels for 4%

profile of v21, /device:TPU:0, one launch (start us, length us, event | category | flops | bytes accessed | tf_op | source)
XLA Modules:
  0.0 224.2 jit_solution(8705113863101782101)
XLA Ops:
  0.6 3.1 %collective-permute-start.2 = (bf16[1024,768]{1,0:T(8,128)(2,1)}, bf16[1024,768]{1,0:T(8,128)(2,1)}, u32[]{:S(2)}, u32[]{:S(2)}) collective-permute-start(bf16[1024,768]{1,0:T(8,128)(2,1)} %param.21), channel_id=1, source_target_pairs={{24,0},{28,4},{0,8},{4,12},{8,16},{12,20},{16,24},{20,28},{25,1},{... | collective-permute-start | bytes 4718600 | tf_op jit(solution)/shard_map/ppermute | solution.py:20
  3.7 1.8 fusion.7
  6.0 1.1 copy-done.1
  7.1 1.0 fusion.51
  8.1 3.3 %collective-permute-start.3 = (bf16[512,768]{1,0:T(8,128)(2,1)S(1)}, bf16[512,768]{1,0:T(8,128)(2,1)}, u32[]{:S(2)}, u32[]{:S(2)}) collective-permute-start(bf16[512,768]{1,0:T(8,128)(2,1)S(1)} %get-tuple-element.265), channel_id=1, source_target_pairs={{4,0},{8,4},{12,8},{16,12},{20,16},{24,20},{28,24},{0,28},{5,1},{9... | collective-permute-start | bytes 2359304 | tf_op jit(solution)/shard_map/ppermute | solution.py:20
  12.6 5.0 %collective-permute-start = (bf16[512,768]{1,0:T(8,128)(2,1)}, bf16[512,768]{1,0:T(8,128)(2,1)}, u32[]{:S(2)}, u32[]{:S(2)}) collective-permute-start(bf16[512,768]{1,0:T(8,128)(2,1)} %get-tuple-element.266), channel_id=1, source_target_pairs={{4,0},{8,4},{12,8},{16,12},{20,16},{24,20},{28,24},{0,28},{5,1},{9... | collective-permute-start | bytes 2359304 | tf_op jit(solution)/shard_map/ppermute | solution.py:20
  17.6 4.4 %convert_reduce_fusion.10 = (f32[1024]{0:T(1024)}, bf16[1024,1024]{0,1:T(8,128)(2,1)S(1)}) fusion(bf16[1024,768]{1,0:T(8,128)(2,1)} %copy-done.1), kind=kOutput, calls=%fused_computation.25 | convolution fusion | flops 1616903168 | bytes 3674112 | tf_op jit(solution)/shard_map/dot_general | solution.py:55
  24.7 36.6 %collective-permute-done.1 = bf16[1024,64]{1,0:T(8,128)(2,1)} collective-permute-done((bf16[1024,64]{1,0:T(8,128)(2,1)}, bf16[1024,64]{1,0:T(8,128)(2,1)}, u32[]{:S(2)}, u32[]{:S(2)}) %collective-permute-start.1) | collective-permute-done | bytes 131104 | tf_op jit(solution)/shard_map/ppermute | solution.py:20
  62.3 1.8 conditional.10
  62.3 1.1 broadcast.148
  64.2 1.9 fusion.10
  66.1 3.0 %fusion.12 = bf16[1024,768]{1,0:T(8,128)(2,1)} fusion(bf16[1024,768]{1,0:T(8,128)(2,1)} %collective-permute-done.2, f32[1024]{0:T(1024)S(1)} %add_rsqrt_fusion), kind=kLoop, calls=%fused_computation.39 | loop fusion | flops 3145728 | bytes 3149824 | tf_op jit(solution)/shard_map/convert_element_type | solution.py:51
  69.1 7.1 %conditional.9 = (bf16[1024,1024]{1,0:T(8,128)(2,1)}, f32[1024,64]{0,1:T(8,128)S(1)}, f32[1024]{0:T(1024)S(1)}, f32[1024]{0:T(1024)S(1)}) conditional(s32[]{:T(128)} %convert_element_type.77, () %tuple.83, (bf16[1024,768]{1,0:T(8,128)(2,1)}, bf16[1024,768]{1,0:T(8,128)(2,1)S(1)}, bf16[1024,64]{0,1:T(8,128)(2,1)S(1)}) %tuple.159), branch_computations={%region_3.4_spmd, %region_4.0_spmd} | conditional | flops 1750071296 | bytes 7741472 | solution.py:125
  69.1 4.7 %convert_reduce_fusion = (f32[1024]{0:T(1024)S(1)}, f32[1024]{0:T(1024)S(1)}, bf16[1024,1024]{1,0:T(8,128)(2,1)}) fusion(bf16[1024,768]{1,0:T(8,128)(2,1)} %get-tuple-element.69, bf16[1024,768]{1,0:T(8,128)(2,1)S(1)} %get-tuple-element.70), kind=kOutput, calls=%fused_computation | convolution fusion | flops 1615853568 | bytes 5251072 | tf_op jit(solution)/shard_map/cond/branch_1_fun/dot_general | solution.py:55
  73.8 2.3 %fusion.56 = f32[1024,64]{0,1:T(8,128)S(1)} fusion(bf16[1024,1024]{1,0:T(8,128)(2,1)} %get-tuple-element.280, bf16[1024,64]{0,1:T(8,128)(2,1)S(1)} %get-tuple-element.219), kind=kOutput, calls=%fused_computation.149 | convolution fusion | flops 134217728 | bytes 2490368 | tf_op jit(solution)/shard_map/cond/branch_1_fun/dot_general | solution.py:62
  76.9 6.9 %conditional.11 = (bf16[1024,512]{1,0:T(8,128)(2,1)}, f32[1024,64]{0,1:T(8,128)S(1)}, f32[1024]{0:T(1024)S(1)}, f32[512,64]{0,1:T(8,128)S(1)}, f32[512]{0:T(512)S(1)}) conditional(s32[]{:T(128)} %convert_element_type.81, () %tuple.87, (bf16[1024,768]{1,0:T(8,128)(2,1)}, bf16[512,768]{1,0:T(8,128)(2,1)}, bf16[512,64]{1,0:T(8,128)(2,1)S(1)}, ...), branch_computations={%region_13.14_spmd, %region_14.17_spmd} | conditional | flops 942144000 | bytes 6101032 | solution.py:166
  76.9 3.7 %convert_reduce_fusion.4 = (f32[512]{0:T(512)S(1)}, f32[1024]{0:T(1024)S(1)}, bf16[1024,512]{1,0:T(8,128)(2,1)}) fusion(bf16[1024,768]{1,0:T(8,128)(2,1)} %get-tuple-element.76, bf16[512,768]{1,0:T(8,128)(2,1)} %get-tuple-element.77), kind=kOutput, calls=%fused_computation.6 | convolution fusion | flops 807926272 | bytes 3414016 | tf_op jit(solution)/shard_map/cond/branch_1_fun/dot_general | solution.py:55
  80.6 1.7 fusion.59
  82.2 1.6 fusion.60
  83.8 1.0 slice.153
  84.8 7.0 %conditional.14 = (bf16[1024,512]{1,0:T(8,128)(2,1)}, f32[1024,64]{0,1:T(8,128)S(1)}, f32[1024]{0:T(1024)S(1)}, f32[512,64]{0,1:T(8,128)S(1)}, f32[4,128]{1,0:T(4,128)S(1)}) conditional(s32[]{:T(128)} %convert_element_type.81, () %tuple.94, (bf16[1024,768]{1,0:T(8,128)(2,1)}, bf16[512,768]{1,0:T(8,128)(2,1)}, bf16[512,64]{1,0:T(8,128)(2,1)S(1)}, ...), branch_computations={%region_23.24_spmd, %region_24.0_spmd} | conditional | flops 942144000 | bytes 6101032 | solution.py:166
  84.8 3.7 %convert_reduce_fusion.8 = (f32[512]{0:T(512)S(1)}, f32[1024]{0:T(1024)S(1)}, bf16[1024,512]{1,0:T(8,128)(2,1)}) fusion(bf16[1024,768]{1,0:T(8,128)(2,1)} %get-tuple-element.86, bf16[512,768]{1,0:T(8,128)(2,1)} %get-tuple-element.87), kind=kOutput, calls=%fused_computation.12 | convolution fusion | flops 807926272 | bytes 3414016 | tf_op jit(solution)/shard_map/cond/branch_1_fun/dot_general | solution.py:55
  88.6 1.7 fusion.63
  90.2 1.6 fusion.64
  93.0 1.0 add_add_fusion
  95.1 10.2 %collective-permute-start.6 = (f32[520,128]{1,0:T(8,128)}, f32[520,128]{1,0:T(8,128)}, u32[]{:S(2)}, u32[]{:S(2)}) collective-permute-start(f32[520,128]{1,0:T(8,128)} %pad_maximum_fusion.3), channel_id=1, source_target_pairs={{8,0},{12,4},{16,8},{20,12},{24,16},{28,20},{0,24},{4,28},{9,1},{1... | collective-permute-start | bytes 798728 | tf_op jit(solution)/shard_map/ppermute | solution.py:20
  105.3 2.4 %conditional.12 = (bf16[1024,512]{1,0:T(8,128)(2,1)}, f32[1024,64]{0,1:T(8,128)}, f32[1024]{0:T(1024)S(1)}, f32[512,64]{0,1:T(8,128)S(1)}, f32[4,128]{1,0:T(4,128)}) conditional(s32[]{:T(128)} %convert_element_type.80, () %tuple.90, (bf16[1024,768]{1,0:T(8,128)(2,1)}, bf16[512,768]{1,0:T(8,128)(2,1)}, bf16[512,64]{1,0:T(8,128)(2,1)S(1)}, ...), branch_computations={%region_17.18_spmd, %region_18.21_spmd} | conditional | flops 942144000 | bytes 6101032 | solution.py:166
  105.3 1.0 broadcast.160
  110.5 2.8 %conditional.13 = (f32[1024,64]{0,1:T(8,128)}) conditional(s32[]{:T(128)} %convert_element_type.77, () %tuple.92, (bf16[1024,1024]{1,0:T(8,128)(2,1)}, bf16[1024,64]{1,0:T(8,128)(2,1)S(1)}) %tuple.93), branch_computations={%region_21.22_spmd, %region_22.23_spmd} | conditional | flops 134217728 | bytes 2490376 | solution.py:137
  110.5 2.8 %fusion.53 = f32[1024,64]{0,1:T(8,128)} fusion(bf16[1024,1024]{1,0:T(8,128)(2,1)} %get-tuple-element.84, bf16[1024,64]{1,0:T(8,128)(2,1)S(1)} %get-tuple-element.85), kind=kOutput, calls=%fused_computation.146 | convolution fusion | flops 134217728 | bytes 2490368 | tf_op jit(solution)/shard_map/cond/branch_1_fun/dot_general | solution.py:66
  113.3 1.0 slice.201
  114.6 6.9 %collective-permute-done.5 = f32[520,128]{1,0:T(8,128)} collective-permute-done((f32[520,128]{1,0:T(8,128)}, f32[520,128]{1,0:T(8,128)}, u32[]{:S(2)}, u32[]{:S(2)}) %collective-permute-start.5) | collective-permute-done | bytes 266272 | tf_op jit(solution)/shard_map/ppermute | solution.py:20
  121.6 1.0 slice.200
  122.9 1.3 fusion.49
  124.2 1.3 broadcast_multiply_fusion
  127.9 1.2 collective-permute-done.9
  129.1 5.0 %collective-permute-start.10 = (f32[35,128]{1,0:T(8,128)S(1)}, f32[35,128]{1,0:T(8,128)S(1)}, u32[]{:S(2)}, u32[]{:S(2)}) collective-permute-start(f32[35,128]{1,0:T(8,128)S(1)} %pad_maximum_fusion.9), channel_id=1, source_target_pairs={{0,2},{1,3},{2,0},{3,1},{4,6},{5,7},{6,4},{7,5},{8,10},{9,11},{10,... | collective-permute-start | bytes 53768 | tf_op jit(solution)/shard_map/ppermute | solution.py:204
  134.0 1.8 collective-permute-done.10
  135.9 3.8 %collective-permute-done.11 = f32[37,128]{1,0:T(8,128)S(1)} collective-permute-done((f32[37,128]{1,0:T(8,128)S(1)}, f32[37,128]{1,0:T(8,128)S(1)}, u32[]{:S(2)}, u32[]{:S(2)}) %collective-permute-start.11) | collective-permute-done | bytes 18976 | tf_op jit(solution)/shard_map/ppermute | solution.py:204
  139.8 3.8 %collective-permute-done.12 = f32[41,128]{1,0:T(8,128)S(1)} collective-permute-done((f32[41,128]{1,0:T(8,128)S(1)}, f32[41,128]{1,0:T(8,128)S(1)}, u32[]{:S(2)}, u32[]{:S(2)}) %collective-permute-start.12) | collective-permute-done | bytes 21024 | tf_op jit(solution)/shard_map/ppermute | solution.py:204
  143.9 3.6 %collective-permute-start.7 = (f32[1024,64]{0,1:T(8,128)S(1)}, f32[1024,64]{0,1:T(8,128)S(1)}, u32[]{:S(2)}, u32[]{:S(2)}) collective-permute-start(f32[1024,64]{0,1:T(8,128)S(1)} %get-tuple-element.259), channel_id=1, source_target_pairs={{4,0},{8,4},{12,8},{16,12},{20,16},{24,20},{28,24},{0,28},{5,1},{9... | collective-permute-start | bytes 786440 | tf_op jit(solution)/shard_map/ppermute | solution.py:20
  147.5 1.5 collective-permute-done.13
  151.6 8.4 %shard_map.50 = f32[64,64]{1,0:T(8,128)} custom-call(f32[64,64]{1,0:T(8,128)} %fusion.18.gram_ref), custom_call_target="tpu_custom_call" | custom-call | tf_op jit(solution)/shard_map/pallas_call | solution.py:252
  160.0 1.7 convolution_convert_fusion
  162.5 4.4 %conditional.16 = (f32[1024,64]{0,1:T(8,128)S(1)}, f32[1024,64]{0,1:T(8,128)S(1)}) conditional(s32[]{:T(128)} %convert_element_type.77, () %tuple.98, (bf16[1024,1024]{1,0:T(8,128)(2,1)}, bf16[1024,64]{0,1:T(8,128)(2,1)S(1)}, bf16[1024,64]{0,1:T(8,128)(2,1)S(1)}) %tuple.99), branch_computations={%region_34.35_spmd, %region_35.36_spmd} | conditional | flops 268435456 | bytes 4980752 | solution.py:188
  162.5 2.3 %fusion.54 = f32[1024,64]{0,1:T(8,128)S(1)} fusion(bf16[1024,1024]{1,0:T(8,128)(2,1)} %get-tuple-element.94, bf16[1024,64]{0,1:T(8,128)(2,1)S(1)} %get-tuple-element.233), kind=kOutput, calls=%fused_computation.147 | convolution fusion | flops 134217728 | bytes 2490368 | tf_op jit(solution)/shard_map/cond/branch_1_fun/dot_general | solution.py:62
  164.9 2.1 fusion.55
  167.0 6.6 %conditional.17 = (f32[1024,64]{0,1:T(8,128)S(1)}, f32[1024,64]{0,1:T(8,128)S(1)}) conditional(s32[]{:T(128)} %convert_element_type.81, () %tuple.100, (bf16[1024,64]{0,1:T(8,128)(2,1)S(1)}, bf16[1024,512]{1,0:T(8,128)(2,1)}, bf16[1024,512]{1,0:T(8,128)(2,1)}, bf16[1024,64]{0,1:T(8,128)(2,1)S(1)}) %tuple.101), branch_computations={%region_36.37_spmd, %region_37.38_spmd} | conditional | flops 268566528 | bytes 6553616 | solution.py:188
  167.2 1.7 fusion.4
  168.8 1.7 convolution_add_fusion.1
  170.5 1.5 fusion.68
  172.0 1.5 fusion.67
  174.4 2.8 %collective-permute-start.14 = (f32[1024,64]{0,1:T(8,128)S(1)}, f32[1024,64]{0,1:T(8,128)S(1)}, u32[]{:S(2)}, u32[]{:S(2)}) collective-permute-start(f32[1024,64]{0,1:T(8,128)S(1)} %add.254), channel_id=1, source_target_pairs={{28,0},{0,4},{4,8},{8,12},{12,16},{16,20},{20,24},{24,28},{29,1},{... | collective-permute-start | bytes 786440 | tf_op jit(solution)/shard_map/ppermute | solution.py:20
  177.3 3.7 %collective-permute-done.15 = f32[1024,64]{0,1:T(8,128)} collective-permute-done((f32[1024,64]{0,1:T(8,128)}, f32[1024,64]{0,1:T(8,128)}, u32[]{:S(2)}, u32[]{:S(2)}) %collective-permute-start.15) | collective-permute-done | bytes 262176 | tf_op jit(solution)/shard_map/ppermute | solution.py:20
  181.0 4.6 %collective-permute-done.14 = f32[1024,64]{0,1:T(8,128)S(1)} collective-permute-done((f32[1024,64]{0,1:T(8,128)S(1)}, f32[1024,64]{0,1:T(8,128)S(1)}, u32[]{:S(2)}, u32[]{:S(2)}) %collective-permute-start.14) | collective-permute-done | bytes 262176 | tf_op jit(solution)/shard_map/ppermute | solution.py:20
  185.6 1.7 fusion.46
  188.8 1.2 collective-permute-done.16
  190.0 6.5 %collective-permute-start.17 = (f32[35,128]{1,0:T(8,128)S(1)}, f32[35,128]{1,0:T(8,128)S(1)}, u32[]{:S(2)}, u32[]{:S(2)}) collective-permute-start(f32[35,128]{1,0:T(8,128)S(1)} %pad_maximum_fusion.12), channel_id=1, source_target_pairs={{0,2},{1,3},{2,0},{3,1},{4,6},{5,7},{6,4},{7,5},{8,10},{9,11},{10,... | collective-permute-start | bytes 53768 | tf_op jit(solution)/shard_map/ppermute | solution.py:204
  196.6 1.8 collective-permute-done.17
  198.5 3.8 %collective-permute-done.18 = f32[37,128]{1,0:T(8,128)S(1)} collective-permute-done((f32[37,128]{1,0:T(8,128)S(1)}, f32[37,128]{1,0:T(8,128)S(1)}, u32[]{:S(2)}, u32[]{:S(2)}) %collective-permute-start.18) | collective-permute-done | bytes 18976 | tf_op jit(solution)/shard_map/ppermute | solution.py:204
  202.6 3.6 %collective-permute-done.19 = f32[41,128]{1,0:T(8,128)S(1)} collective-permute-done((f32[41,128]{1,0:T(8,128)S(1)}, f32[41,128]{1,0:T(8,128)S(1)}, u32[]{:S(2)}, u32[]{:S(2)}) %collective-permute-start.19) | collective-permute-done | bytes 21024 | tf_op jit(solution)/shard_map/ppermute | solution.py:204
  206.3 5.0 %collective-permute-done.20 = f32[49,128]{1,0:T(8,128)S(1)} collective-permute-done((f32[49,128]{1,0:T(8,128)S(1)}, f32[49,128]{1,0:T(8,128)S(1)}, u32[]{:S(2)}, u32[]{:S(2)}) %collective-permute-start.20) | collective-permute-done | bytes 25120 | tf_op jit(solution)/shard_map/ppermute | solution.py:204
  213.8 8.4 %shard_map.51 = f32[64,64]{1,0:T(8,128)} custom-call(f32[64,64]{1,0:T(8,128)} %fusion.16.gram_ref), custom_call_target="tpu_custom_call" | custom-call | tf_op jit(solution)/shard_map/pallas_call | solution.py:252
  222.3 1.9 fusion.24
  (162 shorter events, 23.5 us)
Async XLA Ops:
  0.6 4.9 %copy-start = (bf16[1024,768]{1,0:T(8,128)(2,1)S(1)}, bf16[1024,768]{1,0:T(8,128)(2,1)}, u32[]{:S(2)}) copy-start(bf16[1024,768]{1,0:T(8,128)(2,1)} %param.21) | copy-start | bytes 4718596
  0.6 63.5 %collective-permute-start.2 = (bf16[1024,768]{1,0:T(8,128)(2,1)}, bf16[1024,768]{1,0:T(8,128)(2,1)}, u32[]{:S(2)}, u32[]{:S(2)}) collective-permute-start(bf16[1024,768]{1,0:T(8,128)(2,1)} %param.21), channel_id=1, source_target_pairs={{24,0},{28,4},{0,8},{4,12},{8,16},{12,20},{16,24},{20,28},{25,1},{... | collective-permute-start | bytes 4718600 | tf_op jit(solution)/shard_map/ppermute | solution.py:20
  6.0 1.1 copy-start.1
  7.1 4.3 %copy-start.3 = (bf16[1024,64]{0,1:T(8,128)(2,1)S(1)}, bf16[1024,64]{0,1:T(8,128)(2,1)}, u32[]{:S(2)}) copy-start(bf16[1024,64]{0,1:T(8,128)(2,1)} %param.22) | copy-start | bytes 393220
  8.1 54.1 %collective-permute-start.3 = (bf16[512,768]{1,0:T(8,128)(2,1)S(1)}, bf16[512,768]{1,0:T(8,128)(2,1)}, u32[]{:S(2)}, u32[]{:S(2)}) collective-permute-start(bf16[512,768]{1,0:T(8,128)(2,1)S(1)} %get-tuple-element.265), channel_id=1, source_target_pairs={{4,0},{8,4},{12,8},{16,12},{20,16},{24,20},{28,24},{0,28},{5,1},{9... | collective-permute-start | bytes 2359304 | tf_op jit(solution)/shard_map/ppermute | solution.py:20
  12.3 49.1 %collective-permute-start.1 = (bf16[1024,64]{1,0:T(8,128)(2,1)}, bf16[1024,64]{1,0:T(8,128)(2,1)}, u32[]{:S(2)}, u32[]{:S(2)}) collective-permute-start(bf16[1024,64]{1,0:T(8,128)(2,1)} %copy.18), channel_id=1, source_target_pairs={{4,0},{8,4},{12,8},{16,12},{20,16},{24,20},{28,24},{0,28},{5,1},{9... | collective-permute-start | bytes 393224 | tf_op jit(solution)/shard_map/ppermute | solution.py:20
  12.5 63.6 %collective-permute-start.4 = (bf16[1024,64]{1,0:T(8,128)(2,1)}, bf16[1024,64]{1,0:T(8,128)(2,1)S(1)}, u32[]{:S(2)}, u32[]{:S(2)}) collective-permute-start(bf16[1024,64]{1,0:T(8,128)(2,1)} %copy.18), channel_id=1, source_target_pairs={{24,0},{28,4},{0,8},{4,12},{8,16},{12,20},{16,24},{20,28},{25,1},{... | collective-permute-start | bytes 393224 | tf_op jit(solution)/shard_map/ppermute | solution.py:20
  12.6 9.4 %copy-start.17 = (s32[32,3]{0,1:T(4,128)S(1)}, s32[32,3]{0,1:T(4,128)}, u32[]{:S(2)}) copy-start(s32[32,3]{0,1:T(4,128)} %param.23) | copy-start | bytes 1156
  12.6 71.3 %collective-permute-start = (bf16[512,768]{1,0:T(8,128)(2,1)}, bf16[512,768]{1,0:T(8,128)(2,1)}, u32[]{:S(2)}, u32[]{:S(2)}) collective-permute-start(bf16[512,768]{1,0:T(8,128)(2,1)} %get-tuple-element.266), channel_id=1, source_target_pairs={{4,0},{8,4},{12,8},{16,12},{20,16},{24,20},{28,24},{0,28},{5,1},{9... | collective-permute-start | bytes 2359304 | tf_op jit(solution)/shard_map/ppermute | solution.py:20
  64.1 4.9 %copy-start.12 = (f32[512]{0:T(512)}, f32[512]{0:T(512)S(1)}, u32[]{:S(2)}) copy-start(f32[512]{0:T(512)S(1)} %get-tuple-element.172) | copy-start | bytes 6148
  64.1 4.9 %copy-start.2 = (bf16[1024,768]{1,0:T(8,128)(2,1)S(1)}, bf16[1024,768]{1,0:T(8,128)(2,1)}, u32[]{:S(2)}) copy-start(bf16[1024,768]{1,0:T(8,128)(2,1)} %copy-done.1) | copy-start | bytes 4718596
  76.1 0.6 copy-start.10
  76.1 0.7 copy-start.4
  83.8 1.0 copy-start.14
  83.8 1.0 copy-start.6
  91.8 0.6 copy-start.16
  92.4 0.6 copy-start.8
  95.1 12.6 %copy-start.7 = (f32[512,64]{0,1:T(8,128)S(1)}, f32[512,64]{0,1:T(8,128)}, u32[]{:S(2)}) copy-start(f32[512,64]{0,1:T(8,128)} %copy-done.6) | copy-start | bytes 393220
  95.1 12.6 %copy-start.9 = (f32[512,64]{0,1:T(8,128)S(1)}, f32[512,64]{0,1:T(8,128)}, u32[]{:S(2)}) copy-start(f32[512,64]{0,1:T(8,128)} %copy-done.8) | copy-start | bytes 393220
  95.1 18.2 %collective-permute-start.6 = (f32[520,128]{1,0:T(8,128)}, f32[520,128]{1,0:T(8,128)}, u32[]{:S(2)}, u32[]{:S(2)}) collective-permute-start(f32[520,128]{1,0:T(8,128)} %pad_maximum_fusion.3), channel_id=1, source_target_pairs={{8,0},{12,4},{16,8},{20,12},{24,16},{28,20},{0,24},{4,28},{9,1},{1... | collective-permute-start | bytes 798728 | tf_op jit(solution)/shard_map/ppermute | solution.py:20
  107.6 0.6 copy-start.13
  107.6 0.7 copy-start.15
  109.7 11.8 %collective-permute-start.5 = (f32[520,128]{1,0:T(8,128)}, f32[520,128]{1,0:T(8,128)}, u32[]{:S(2)}, u32[]{:S(2)}) collective-permute-start(f32[520,128]{1,0:T(8,128)} %pad_maximum_fusion.2), channel_id=1, source_target_pairs={{28,0},{0,4},{4,8},{8,12},{12,16},{16,20},{20,24},{24,28},{29,1},{... | collective-permute-start | bytes 798728 | tf_op jit(solution)/shard_map/ppermute | solution.py:20
  114.6 9.5 %copy-start.11 = (f32[1024]{0:T(1024)S(1)}, f32[1024]{0:T(1024)}, u32[]{:S(2)}) copy-start(f32[1024]{0:T(1024)} %copy-done.10) | copy-start | bytes 12292
  114.6 9.5 %copy-start.18 = (f32[1024]{0:T(1024)S(1)}, f32[1024]{0:T(1024)}, u32[]{:S(2)}) copy-start(f32[1024]{0:T(1024)} %get-tuple-element.270) | copy-start | bytes 12292
  127.8 1.3 collective-permute-start.9
  129.1 6.7 %collective-permute-start.10 = (f32[35,128]{1,0:T(8,128)S(1)}, f32[35,128]{1,0:T(8,128)S(1)}, u32[]{:S(2)}, u32[]{:S(2)}) collective-permute-start(f32[35,128]{1,0:T(8,128)S(1)} %pad_maximum_fusion.9), channel_id=1, source_target_pairs={{0,2},{1,3},{2,0},{3,1},{4,6},{5,7},{6,4},{7,5},{8,10},{9,11},{10,... | collective-permute-start | bytes 53768 | tf_op jit(solution)/shard_map/ppermute | solution.py:204
  135.8 3.8 %collective-permute-start.11 = (f32[37,128]{1,0:T(8,128)S(1)}, f32[37,128]{1,0:T(8,128)S(1)}, u32[]{:S(2)}, u32[]{:S(2)}) collective-permute-start(f32[37,128]{1,0:T(8,128)S(1)} %pad_maximum_fusion.10), channel_id=1, source_target_pairs={{0,4},{4,0},{8,12},{12,8},{16,20},{20,16},{24,28},{28,24},{1,5},{5... | collective-permute-start | bytes 56840 | tf_op jit(solution)/shard_map/ppermute | solution.py:204
  139.7 3.9 %collective-permute-start.12 = (f32[41,128]{1,0:T(8,128)S(1)}, f32[41,128]{1,0:T(8,128)S(1)}, u32[]{:S(2)}, u32[]{:S(2)}) collective-permute-start(f32[41,128]{1,0:T(8,128)S(1)} %pad_maximum_fusion.6), channel_id=1, source_target_pairs={{0,8},{4,12},{8,0},{12,4},{16,24},{20,28},{24,16},{28,20},{1,9},{5... | collective-permute-start | bytes 62984 | tf_op jit(solution)/shard_map/ppermute | solution.py:204
  143.7 5.4 %collective-permute-start.13 = (f32[49,128]{1,0:T(8,128)S(1)}, f32[49,128]{1,0:T(8,128)S(1)}, u32[]{:S(2)}, u32[]{:S(2)}) collective-permute-start(f32[49,128]{1,0:T(8,128)S(1)} %pad_maximum_fusion.4), channel_id=1, source_target_pairs={{0,16},{4,20},{8,24},{12,28},{16,0},{20,4},{24,8},{28,12},{1,17},{... | collective-permute-start | bytes 75272 | tf_op jit(solution)/shard_map/ppermute | solution.py:204
  143.8 16.3 %collective-permute-start.8 = (f32[1024,64]{0,1:T(8,128)S(1)}, f32[1024,64]{0,1:T(8,128)S(1)}, u32[]{:S(2)}, u32[]{:S(2)}) collective-permute-start(f32[1024,64]{0,1:T(8,128)S(1)} %get-tuple-element.259), channel_id=1, source_target_pairs={{24,0},{28,4},{0,8},{4,12},{8,16},{12,20},{16,24},{20,28},{25,1},{... | collective-permute-start | bytes 786440 | tf_op jit(solution)/shard_map/ppermute | solution.py:20
  143.9 16.2 %collective-permute-start.7 = (f32[1024,64]{0,1:T(8,128)S(1)}, f32[1024,64]{0,1:T(8,128)S(1)}, u32[]{:S(2)}, u32[]{:S(2)}) collective-permute-start(f32[1024,64]{0,1:T(8,128)S(1)} %get-tuple-element.259), channel_id=1, source_target_pairs={{4,0},{8,4},{12,8},{16,12},{20,16},{24,20},{28,24},{0,28},{5,1},{9... | collective-permute-start | bytes 786440 | tf_op jit(solution)/shard_map/ppermute | solution.py:20
  161.8 0.8 copy-start.5
  174.3 6.7 %collective-permute-start.15 = (f32[1024,64]{0,1:T(8,128)}, f32[1024,64]{0,1:T(8,128)}, u32[]{:S(2)}, u32[]{:S(2)}) collective-permute-start(f32[1024,64]{0,1:T(8,128)} %add.256), channel_id=1, source_target_pairs={{8,0},{12,4},{16,8},{20,12},{24,16},{28,20},{0,24},{4,28},{9,1},{1... | collective-permute-start | bytes 786440 | tf_op jit(solution)/shard_map/ppermute | solution.py:20
  174.4 11.2 %collective-permute-start.14 = (f32[1024,64]{0,1:T(8,128)S(1)}, f32[1024,64]{0,1:T(8,128)S(1)}, u32[]{:S(2)}, u32[]{:S(2)}) collective-permute-start(f32[1024,64]{0,1:T(8,128)S(1)} %add.254), channel_id=1, source_target_pairs={{28,0},{0,4},{4,8},{8,12},{12,16},{16,20},{20,24},{24,28},{29,1},{... | collective-permute-start | bytes 786440 | tf_op jit(solution)/shard_map/ppermute | solution.py:20
  188.8 1.2 collective-permute-start.16
  190.0 8.3 %collective-permute-start.17 = (f32[35,128]{1,0:T(8,128)S(1)}, f32[35,128]{1,0:T(8,128)S(1)}, u32[]{:S(2)}, u32[]{:S(2)}) collective-permute-start(f32[35,128]{1,0:T(8,128)S(1)} %pad_maximum_fusion.12), channel_id=1, source_target_pairs={{0,2},{1,3},{2,0},{3,1},{4,6},{5,7},{6,4},{7,5},{8,10},{9,11},{10,... | collective-permute-start | bytes 53768 | tf_op jit(solution)/shard_map/ppermute | solution.py:204
  198.4 3.8 %collective-permute-start.18 = (f32[37,128]{1,0:T(8,128)S(1)}, f32[37,128]{1,0:T(8,128)S(1)}, u32[]{:S(2)}, u32[]{:S(2)}) collective-permute-start(f32[37,128]{1,0:T(8,128)S(1)} %pad_maximum_fusion.13), channel_id=1, source_target_pairs={{0,4},{4,0},{8,12},{12,8},{16,20},{20,16},{24,28},{28,24},{1,5},{5... | collective-permute-start | bytes 56840 | tf_op jit(solution)/shard_map/ppermute | solution.py:204
  202.3 3.9 %collective-permute-start.19 = (f32[41,128]{1,0:T(8,128)S(1)}, f32[41,128]{1,0:T(8,128)S(1)}, u32[]{:S(2)}, u32[]{:S(2)}) collective-permute-start(f32[41,128]{1,0:T(8,128)S(1)} %pad_maximum_fusion.7), channel_id=1, source_target_pairs={{0,8},{4,12},{8,0},{12,4},{16,24},{20,28},{24,16},{28,20},{1,9},{5... | collective-permute-start | bytes 62984 | tf_op jit(solution)/shard_map/ppermute | solution.py:204
  206.2 5.1 %collective-permute-start.20 = (f32[49,128]{1,0:T(8,128)S(1)}, f32[49,128]{1,0:T(8,128)S(1)}, u32[]{:S(2)}, u32[]{:S(2)}) collective-permute-start(f32[49,128]{1,0:T(8,128)S(1)} %pad_maximum_fusion.5), channel_id=1, source_target_pairs={{0,16},{4,20},{8,24},{12,28},{16,0},{20,4},{24,8},{28,12},{1,17},{... | collective-permute-start | bytes 75272 | tf_op jit(solution)/shard_map/ppermute | solution.py:204
